TPU v7x, 32 devices: a whole 2x2x4 slice. The times are simulated.
32 devices in a mesh: timepoin: 2 (over y), tile: 4 (over z), view: 4 (over x, core).
Axes of the slice: x: 2, y: 2, z: 4, core: 2. Of those that a mesh axis runs over, the one named last changes fastest.
Arguments:
- acquired: bfloat16 [512, 128, 128], P(('timepoin', 'view'), 'tile'), parts along dimension 0, may hold values from 0.19921875 to 5
- psf_taps: float32 [2, 3, 31], replicated, may hold values from 0.1 to 1
- block_source: int32 [8, 32], P(('timepoin', 'view')), parts along dimension 0, may hold values from 0 to 31, as said below
Outputs:
- estimate: float32 [256, 128, 128], P(('timepoin', 'view'), 'tile'), parts along dimension 0
There are 2 independent parts, one for each index of `timepoin`. A program takes and returns all parts, laid end to end along the dimension named above; an argument that names none is the same for every part. Nothing has to cross between parts.
Inputs may be any that keep to these rules, and one draw needn't show every extreme that they name: `block_source`: entry (r, q) names the global view block of row r's stack that fills joined x-block q. With t the tile of q, blocks in the first half of tile t come from tile t or t - 1 and those in the second half from tile t or t + 1 (kept within the tiles), so at most 4 blocks of a tile come from one neighbouring tile; some tile takes exactly 4 from one neighbour.
All inputs are finite; a program needn't handle non-finite values.
Results may differ from a plain program's by a relative error of at most 0.00081.
Values may be sent and summed in bfloat16 or wider, within the bound.
No kernel may reach another device: no remote copies, remote signals or barrier semaphores. Data moves between devices by JAX's collectives and lax.ppermute only.
A program may use at most 64 MiB of HBM per device.

v0:
```python
import jax
import jax.numpy as jnp
from jax import lax
from jax.sharding import PartitionSpec as P

BX = 4
ITERS = 2


def shifted(block, axis, distance):
    devices = range(lax.axis_size(axis))
    route = [(i - distance, i) for i in devices if i - distance in devices]
    return lax.ppermute(block, axis, route)


def from_partner(block, axis, distance):
    count = lax.axis_size(axis)
    route = []
    for low in range(count):
        high = low | 1 << distance
        if high != low and high < count:
            route += [(low, high), (high, low)]
    return lax.ppermute(block, axis, route)


def extended_2(block, sides, width):
    for axis, dim in sides:
        count = lax.axis_size(axis)
        forward = [(i, i + 1) for i in range(count - 1)]
        backward = [(target, source) for source, target in forward]
        low = lax.ppermute(
            lax.slice_in_dim(block, block.shape[dim] - width, None, axis=dim), axis, forward
        )
        high = lax.ppermute(lax.slice_in_dim(block, 0, width, axis=dim), axis, backward)
        block = jnp.concatenate([low, block, high], axis=dim)
    return block


def band_matrix(kernel, row_count, col_count, base_shift):
    row_ids = lax.broadcasted_iota(jnp.int32, (row_count, col_count), 0)
    col_ids = lax.broadcasted_iota(jnp.int32, (row_count, col_count), 1)
    distance = row_ids - col_ids + base_shift
    taps = kernel.astype(jnp.float32)
    matrix = jnp.zeros((row_count, col_count), jnp.float32)
    for tap_index in range(kernel.shape[0]):
        matrix = matrix + jnp.where(distance == tap_index, taps[tap_index], jnp.float32(0.0))
    return matrix.astype(jnp.bfloat16)


def operators(kernels, plane_count, width_x, width_y):
    reach = kernels.shape[1] // 2
    return (
        band_matrix(kernels[0], width_x + 2 * reach, width_x, 0),
        band_matrix(kernels[1], width_y, width_y, reach),
        band_matrix(kernels[2], plane_count + 2 * reach, plane_count, 0),
    )


def along_z(volume, matrix, reach):
    below_rim = shifted(volume[volume.shape[0] - reach :], "view", 2)
    above_rim = shifted(volume[:reach], "view", -2)
    extended = jnp.concatenate([below_rim, volume, above_rim], axis=0)
    return jnp.einsum("axy,ap->pxy", extended, matrix, preferred_element_type=jnp.float32)


def separable(extended, matrices, reach):
    width_y = extended.shape[2]
    after_x = jnp.einsum(
        "zay,ap->zpy", extended, matrices[0], preferred_element_type=jnp.float32
    ).astype(jnp.bfloat16)
    after_y = jnp.dot(after_x.reshape(-1, width_y), matrices[1], preferred_element_type=jnp.float32)
    after_y = after_y.reshape(after_x.shape).astype(jnp.bfloat16)
    return along_z(after_y, matrices[2], reach)


def local(acquired, psf_taps, block_source):
    planes, width_x, width_y = acquired.shape
    block_count = width_x // BX
    capacity = block_count // 2
    reach = psf_taps.shape[2] // 2
    tile_index = lax.axis_index("tile")
    tile_total = lax.axis_size("tile")
    view_bit = lax.axis_index("view") % 2
    sources = block_source[0]
    blocks = acquired.reshape(planes, block_count, BX, width_y)
    wanted_here = lax.dynamic_slice_in_dim(sources, tile_index * block_count, block_count)
    source_tiles = wanted_here // block_count
    source_blocks = wanted_here % block_count
    parcels = []
    for offset in (1, -1):
        target = jnp.clip(tile_index + offset, 0, tile_total - 1)
        wanted = lax.dynamic_slice_in_dim(sources, target * block_count, block_count)
        matches = wanted // block_count == tile_index
        ranks = jnp.cumsum(matches.astype(jnp.int32)) - 1
        slot_ids = jnp.arange(capacity, dtype=jnp.int32)
        selected = jnp.where(
            matches[None, :] & (ranks[None, :] == slot_ids[:, None]),
            wanted[None, :] % block_count,
            0,
        )
        picked = jnp.sum(selected, axis=1)
        parcel = jnp.take(blocks, picked, axis=1)
        parcels.append(shifted(parcel, "tile", offset))
    candidates = jnp.concatenate([blocks, parcels[0], parcels[1]], axis=1)
    from_left = source_tiles == tile_index - 1
    from_right = source_tiles == tile_index + 1
    left_order = jnp.cumsum(from_left.astype(jnp.int32)) - 1
    right_order = jnp.cumsum(from_right.astype(jnp.int32)) - 1
    chosen = jnp.where(
        from_left,
        block_count + left_order,
        jnp.where(from_right, block_count + capacity + right_order, source_blocks),
    )
    measured = jnp.take(candidates, chosen, axis=1).reshape(planes, width_x, width_y)
    partner_view = from_partner(measured, "view", 0)
    measured_own = measured.astype(jnp.float32)
    estimate = 0.5 * (measured_own + partner_view.astype(jnp.float32))
    kernels = (psf_taps / jnp.sum(psf_taps, axis=2, keepdims=True)).astype(jnp.bfloat16)
    own_kernels = lax.dynamic_index_in_dim(kernels, view_bit, 0, keepdims=False)
    forward_ops = operators(own_kernels, planes, width_x, width_y)
    adjoint_ops = operators(own_kernels[:, ::-1], planes, width_x, width_y)
    half_rows = planes // 2
    for iteration in range(ITERS):
        estimate_low = estimate.astype(jnp.bfloat16)
        own_half = lax.dynamic_slice_in_dim(estimate_low, view_bit * half_rows, half_rows, 0)
        widened = extended_2(own_half, (("tile", 1),), reach)
        rim_stack = jnp.concatenate([widened[:, :reach], widened[:, reach + width_x :]], axis=1)
        partner_rims = from_partner(rim_stack, "view", 0)
        all_rims = jnp.where(
            view_bit == 0,
            jnp.concatenate([rim_stack, partner_rims], axis=0),
            jnp.concatenate([partner_rims, rim_stack], axis=0),
        )
        extended = jnp.concatenate([all_rims[:, :reach], estimate_low, all_rims[:, reach:]], axis=1)
        blurred = separable(extended, forward_ops, reach)
        quotient = (measured_own / blurred).astype(jnp.bfloat16)
        widened_quotient = extended_2(quotient, (("tile", 1),), reach)
        back_own = separable(widened_quotient, adjoint_ops, reach)
        back_partner = from_partner(back_own, "view", 0)
        estimate = estimate * (0.5 * (back_own + back_partner))
    return lax.dynamic_slice_in_dim(estimate, view_bit * half_rows, half_rows, 0)


def solution(mesh):
    in_specs = (P(("timepoin", "view"), "tile", None), P(), P(("timepoin", "view"), None))
    out_specs = P(("timepoin", "view"), "tile", None)
    return jax.shard_map(local, mesh=mesh, in_specs=in_specs, out_specs=out_specs, check_vma=False)
```

profile of v0, /device:TPU:0, one launch (start us, length us, event | category | flops | bytes accessed | tf_op | source)
XLA Modules:
  0.0 353.7 jit_solution(10702202787292051569)
XLA Ops:
  3.2 4.9 %collective-permute-start = (bf16[64,4,4,128]{3,0,2,1:T(8,128)(2,1)S(1)}, bf16[64,4,4,128]{3,0,2,1:T(8,128)(2,1)S(1)}, u32[]{:S(2)}, u32[]{:S(2)}) collective-permute-start(bf16[64,4,4,128]{3,0,2,1:T(8,128)(2,1)S(1)} %select_bitcast_fusion.1), channel_id=1, source_target_pairs={{0,4},{4,8},{8,12},{1,5},{5,9},{9,13},{2,6},{6,10},{10,14},{3,7},{... | collective-permute-start | bytes 786440 | tf_op jit(solution)/shard_map/ppermute | solution.py:13
  13.6 5.2 %collective-permute-done.1 = bf16[64,4,4,128]{3,0,2,1:T(8,128)(2,1)S(1)} collective-permute-done((bf16[64,4,4,128]{3,0,2,1:T(8,128)(2,1)S(1)}, bf16[64,4,4,128]{3,0,2,1:T(8,128)(2,1)S(1)}, u32[]{:S(2)}, u32[]{:S(2)}) %collective-permute-start.1) | collective-permute-done | bytes 262176 | tf_op jit(solution)/shard_map/ppermute | solution.py:13
  22.5 3.5 collective-permute-start.3
  29.0 4.1 %collective-permute-done.4 = bf16[32,15,128]{2,1,0:T(8,128)(2,1)S(1)} collective-permute-done((bf16[32,15,128]{2,1,0:T(8,128)(2,1)S(1)}, bf16[32,15,128]{2,1,0:T(8,128)(2,1)S(1)}, u32[]{:S(2)}, u32[]{:S(2)}) %collective-permute-start.4) | collective-permute-done | bytes 122912 | tf_op jit(solution)/shard_map/ppermute | solution.py:34
  35.7 39.4 %convolution_convert_fusion.7 = bf16[64,32,128]{2,1,0:T(8,128)(2,1)S(1)} fusion(bf16[64,15,128]{2,1,0:T(8,128)(2,1)S(1)} %get-tuple-element.33, bf16[64,32,128]{2,1,0:T(8,128)(2,1)S(1)} %fusion.47, bf16[64,15,128]{2,1,0:T(8,128)(2,1)S(1)} %get-tuple-element.32, f32[]{:T(128)} %bitcast.179, f32[]{:T(128)} %bitcast.178, f32[]{:T(128)} %bitcast.177, ...), kind=kOutput, calls=%fused_computation.13 | convolution fusion | flops 104929408 | bytes 1540344 | tf_op jit(solution)/shard_map/dot_general | solution.py:71
  75.2 3.4 collective-permute-start.6
  81.8 4.1 %collective-permute-done.7 = bf16[15,32,128]{2,1,0:T(8,128)(2,1)S(1)} collective-permute-done((bf16[15,32,128]{2,1,0:T(8,128)(2,1)S(1)}, bf16[15,32,128]{2,1,0:T(8,128)(2,1)S(1)}, u32[]{:S(2)}, u32[]{:S(2)}) %collective-permute-start.7) | collective-permute-done | bytes 122912 | tf_op jit(solution)/shard_map/ppermute | solution.py:13
  86.0 19.7 %fusion.54 = f32[64,32,128]{2,0,1:T(8,128)S(1)} fusion(bf16[94,32,128]{2,1,0:T(8,128)(2,1)S(1)} %pad_maximum_fusion.1, f32[]{:T(128)} %bitcast.114, f32[]{:T(128)} %bitcast.113, f32[]{:T(128)} %bitcast.112, f32[]{:T(128)} %bitcast.111, f32[]{:T(128)} %bitcast.110, f32[]{:T(128)} %bitcast.109, f32[]{:T(128)} %bitcast.108, f32[]{:T(128)} %bitcast.107, ...), kind=kOutput, calls=%fused_computation.50 | convolution fusion | flops 49848576 | bytes 1818748 | tf_op jit(solution)/shard_map/axy,ap->pxy/dot_general | solution.py:63
  106.5 3.5 collective-permute-start.8
  115.1 4.1 %collective-permute-done.9 = bf16[64,15,128]{2,1,0:T(8,128)(2,1)S(1)} collective-permute-done((bf16[64,15,128]{2,1,0:T(8,128)(2,1)S(1)}, bf16[64,15,128]{2,1,0:T(8,128)(2,1)S(1)}, u32[]{:S(2)}, u32[]{:S(2)}) %collective-permute-start.9) | collective-permute-done | bytes 245792 | tf_op jit(solution)/shard_map/ppermute | solution.py:34
  119.2 39.3 %convolution_convert_fusion.6 = bf16[64,32,128]{2,1,0:T(8,128)(2,1)S(1)} fusion(bf16[64,15,128]{2,1,0:T(8,128)(2,1)S(1)} %collective-permute-done.9, bf16[64,32,128]{2,1,0:T(8,128)(2,1)S(1)} %fusion.5, bf16[64,15,128]{2,1,0:T(8,128)(2,1)S(1)} %collective-permute-done.8, f32[]{:T(128)} %bitcast.213, f32[]{:T(128)} %bitcast.212, f32[]{:T(128)} %bitcast.211, ...), kind=kOutput, calls=%fused_computation.12 | convolution fusion | flops 104929408 | bytes 1540344 | tf_op jit(solution)/shard_map/dot_general | solution.py:71
  162.8 4.0 %collective-permute-done.11 = bf16[15,32,128]{2,1,0:T(8,128)(2,1)S(1)} collective-permute-done((bf16[15,32,128]{2,1,0:T(8,128)(2,1)S(1)}, bf16[15,32,128]{2,1,0:T(8,128)(2,1)S(1)}, u32[]{:S(2)}, u32[]{:S(2)}) %collective-permute-start.11) | collective-permute-done | bytes 122912 | tf_op jit(solution)/shard_map/ppermute | solution.py:13
  166.9 19.8 %fusion.52 = f32[64,32,128]{2,0,1:T(8,128)S(1)} fusion(bf16[94,32,128]{2,1,0:T(8,128)(2,1)S(1)} %pad_maximum_fusion.2, f32[]{:T(128)} %bitcast.49, f32[]{:T(128)} %bitcast.48, f32[]{:T(128)} %bitcast.47, f32[]{:T(128)} %bitcast.46, f32[]{:T(128)} %bitcast.45, f32[]{:T(128)} %bitcast.44, f32[]{:T(128)} %bitcast.43, f32[]{:T(128)} %bitcast.42, f32[]{:T(128)} %bitcast.41, ...), kind=kOutput, calls=%fused_computation.48 | convolution fusion | flops 49848576 | bytes 1818748 | tf_op jit(solution)/shard_map/axy,ap->pxy/dot_general | solution.py:63
  187.4 2.6 collective-permute-done.12
  196.2 4.1 %collective-permute-done.14 = bf16[32,15,128]{2,1,0:T(8,128)(2,1)S(1)} collective-permute-done((bf16[32,15,128]{2,1,0:T(8,128)(2,1)S(1)}, bf16[32,15,128]{2,1,0:T(8,128)(2,1)S(1)}, u32[]{:S(2)}, u32[]{:S(2)}) %collective-permute-start.14) | collective-permute-done | bytes 122912 | tf_op jit(solution)/shard_map/ppermute | solution.py:34
  202.3 39.4 %convolution_convert_fusion.5 = bf16[64,32,128]{2,1,0:T(8,128)(2,1)S(1)} fusion(bf16[64,15,128]{2,1,0:T(8,128)(2,1)S(1)} %get-tuple-element.23, bf16[64,32,128]{2,1,0:T(8,128)(2,1)S(1)} %get-tuple-element.6, bf16[64,15,128]{2,1,0:T(8,128)(2,1)S(1)} %get-tuple-element.22, f32[]{:T(128)} %bitcast.179, f32[]{:T(128)} %bitcast.178, f32[]{:T(128)} %bitcast.177, ...), kind=kOutput, calls=%fused_computation.11 | convolution fusion | flops 104929408 | bytes 1540344 | tf_op jit(solution)/shard_map/dot_general | solution.py:71
  246.1 4.1 %collective-permute-done.17 = bf16[15,32,128]{2,1,0:T(8,128)(2,1)S(1)} collective-permute-done((bf16[15,32,128]{2,1,0:T(8,128)(2,1)S(1)}, bf16[15,32,128]{2,1,0:T(8,128)(2,1)S(1)}, u32[]{:S(2)}, u32[]{:S(2)}) %collective-permute-start.17) | collective-permute-done | bytes 122912 | tf_op jit(solution)/shard_map/ppermute | solution.py:13
  250.4 19.7 %fusion.50 = f32[64,32,128]{2,0,1:T(8,128)S(1)} fusion(bf16[94,32,128]{2,1,0:T(8,128)(2,1)S(1)} %pad_maximum_fusion.3, f32[]{:T(128)} %bitcast.114, f32[]{:T(128)} %bitcast.113, f32[]{:T(128)} %bitcast.112, f32[]{:T(128)} %bitcast.111, f32[]{:T(128)} %bitcast.110, f32[]{:T(128)} %bitcast.109, f32[]{:T(128)} %bitcast.108, f32[]{:T(128)} %bitcast.107, ...), kind=kOutput, calls=%fused_computation.46 | convolution fusion | flops 49848576 | bytes 1818748 | tf_op jit(solution)/shard_map/axy,ap->pxy/dot_general | solution.py:63
  274.4 3.5 collective-permute-done.18
  277.8 4.1 %collective-permute-done.19 = bf16[64,15,128]{2,1,0:T(8,128)(2,1)S(1)} collective-permute-done((bf16[64,15,128]{2,1,0:T(8,128)(2,1)S(1)}, bf16[64,15,128]{2,1,0:T(8,128)(2,1)S(1)}, u32[]{:S(2)}, u32[]{:S(2)}) %collective-permute-start.19) | collective-permute-done | bytes 245792 | tf_op jit(solution)/shard_map/ppermute | solution.py:34
  282.0 39.3 %convolution_convert_fusion.4 = bf16[64,32,128]{2,1,0:T(8,128)(2,1)S(1)} fusion(bf16[64,15,128]{2,1,0:T(8,128)(2,1)S(1)} %collective-permute-done.19, bf16[64,32,128]{2,1,0:T(8,128)(2,1)S(1)} %fusion.6, bf16[64,15,128]{2,1,0:T(8,128)(2,1)S(1)} %collective-permute-done.18, f32[]{:T(128)} %bitcast.213, f32[]{:T(128)} %bitcast.212, f32[]{:T(128)} %bitcast.211, ...), kind=kOutput, calls=%fused_computation.10 | convolution fusion | flops 104929408 | bytes 1540344 | tf_op jit(solution)/shard_map/dot_general | solution.py:71
  325.2 4.4 %collective-permute-done.21 = bf16[15,32,128]{2,1,0:T(8,128)(2,1)S(1)} collective-permute-done((bf16[15,32,128]{2,1,0:T(8,128)(2,1)S(1)}, bf16[15,32,128]{2,1,0:T(8,128)(2,1)S(1)}, u32[]{:S(2)}, u32[]{:S(2)}) %collective-permute-start.21) | collective-permute-done | bytes 122912 | tf_op jit(solution)/shard_map/ppermute | solution.py:13
  329.7 19.8 %fusion.48 = f32[64,32,128]{2,0,1:T(8,128)S(1)} fusion(bf16[94,32,128]{2,1,0:T(8,128)(2,1)S(1)} %pad_maximum_fusion.4, f32[]{:T(128)} %bitcast.49, f32[]{:T(128)} %bitcast.48, f32[]{:T(128)} %bitcast.47, f32[]{:T(128)} %bitcast.46, f32[]{:T(128)} %bitcast.45, f32[]{:T(128)} %bitcast.44, f32[]{:T(128)} %bitcast.43, f32[]{:T(128)} %bitcast.42, f32[]{:T(128)} %bitcast.41, ...), kind=kOutput, calls=%fused_computation.44 | convolution fusion | flops 49848576 | bytes 1818748 | tf_op jit(solution)/shard_map/axy,ap->pxy/dot_general | solution.py:63
  350.1 2.6 collective-permute-done.22
  (111 shorter events, 54.4 us)
Async XLA Ops:
  2.4 8.8 %copy-start.1 = (f32[2,3,31]{2,0,1:T(2,128)S(1)}, f32[2,3,31]{2,0,1:T(2,128)}, u32[]{:S(2)}) copy-start(f32[2,3,31]{2,0,1:T(2,128)} %param.6) | copy-start | bytes 2236
  3.2 10.5 %collective-permute-start = (bf16[64,4,4,128]{3,0,2,1:T(8,128)(2,1)S(1)}, bf16[64,4,4,128]{3,0,2,1:T(8,128)(2,1)S(1)}, u32[]{:S(2)}, u32[]{:S(2)}) collective-permute-start(bf16[64,4,4,128]{3,0,2,1:T(8,128)(2,1)S(1)} %select_bitcast_fusion.1), channel_id=1, source_target_pairs={{0,4},{4,8},{8,12},{1,5},{5,9},{9,13},{2,6},{6,10},{10,14},{3,7},{... | collective-permute-start | bytes 786440 | tf_op jit(solution)/shard_map/ppermute | solution.py:13
  9.2 9.7 %collective-permute-start.1 = (bf16[64,4,4,128]{3,0,2,1:T(8,128)(2,1)S(1)}, bf16[64,4,4,128]{3,0,2,1:T(8,128)(2,1)S(1)}, u32[]{:S(2)}, u32[]{:S(2)}) collective-permute-start(bf16[64,4,4,128]{3,0,2,1:T(8,128)(2,1)S(1)} %select_bitcast_fusion), channel_id=1, source_target_pairs={{4,0},{8,4},{12,8},{5,1},{9,5},{13,9},{6,2},{10,6},{14,10},{7,3},{... | collective-permute-start | bytes 786440 | tf_op jit(solution)/shard_map/ppermute | solution.py:13
  20.1 2.0 collective-permute-start.2
  22.5 6.5 %collective-permute-start.3 = (bf16[32,15,128]{2,1,0:T(8,128)(2,1)S(1)}, bf16[32,15,128]{2,1,0:T(8,128)(2,1)S(1)}, u32[]{:S(2)}, u32[]{:S(2)}) collective-permute-start(bf16[32,15,128]{2,1,0:T(8,128)(2,1)S(1)} %get-tuple-element.34), channel_id=1, source_target_pairs={{0,4},{4,8},{8,12},{1,5},{5,9},{9,13},{2,6},{6,10},{10,14},{3,7},{... | collective-permute-start | bytes 368648 | tf_op jit(solution)/shard_map/ppermute | solution.py:31
  25.9 7.2 %collective-permute-start.4 = (bf16[32,15,128]{2,1,0:T(8,128)(2,1)S(1)}, bf16[32,15,128]{2,1,0:T(8,128)(2,1)S(1)}, u32[]{:S(2)}, u32[]{:S(2)}) collective-permute-start(bf16[32,15,128]{2,1,0:T(8,128)(2,1)S(1)} %get-tuple-element.35), channel_id=1, source_target_pairs={{4,0},{8,4},{12,8},{5,1},{9,5},{13,9},{6,2},{10,6},{14,10},{7,3},{... | collective-permute-start | bytes 368648 | tf_op jit(solution)/shard_map/ppermute | solution.py:34
  33.2 2.2 collective-permute-start.5
  75.2 6.6 %collective-permute-start.6 = (bf16[15,32,128]{2,1,0:T(8,128)(2,1)S(1)}, bf16[15,32,128]{2,1,0:T(8,128)(2,1)S(1)}, u32[]{:S(2)}, u32[]{:S(2)}) collective-permute-start(bf16[15,32,128]{2,1,0:T(8,128)(2,1)S(1)} %get-tuple-element.30), channel_id=1, source_target_pairs={{0,2},{1,3},{4,6},{5,7},{8,10},{9,11},{12,14},{13,15},{16,18},{17,... | collective-permute-start | bytes 368648 | tf_op jit(solution)/shard_map/ppermute | solution.py:13
  78.6 7.3 %collective-permute-start.7 = (bf16[15,32,128]{2,1,0:T(8,128)(2,1)S(1)}, bf16[15,32,128]{2,1,0:T(8,128)(2,1)S(1)}, u32[]{:S(2)}, u32[]{:S(2)}) collective-permute-start(bf16[15,32,128]{2,1,0:T(8,128)(2,1)S(1)} %get-tuple-element.31), channel_id=1, source_target_pairs={{2,0},{3,1},{6,4},{7,5},{10,8},{11,9},{14,12},{15,13},{18,16},{19,... | collective-permute-start | bytes 368648 | tf_op jit(solution)/shard_map/ppermute | solution.py:13
  106.5 8.6 %collective-permute-start.8 = (bf16[64,15,128]{2,1,0:T(8,128)(2,1)S(1)}, bf16[64,15,128]{2,1,0:T(8,128)(2,1)S(1)}, u32[]{:S(2)}, u32[]{:S(2)}) collective-permute-start(bf16[64,15,128]{2,1,0:T(8,128)(2,1)S(1)} %get-tuple-element.28), channel_id=1, source_target_pairs={{0,4},{4,8},{8,12},{1,5},{5,9},{9,13},{2,6},{6,10},{10,14},{3,7},{... | collective-permute-start | bytes 737288 | tf_op jit(solution)/shard_map/ppermute | solution.py:31
  110.0 9.2 %collective-permute-start.9 = (bf16[64,15,128]{2,1,0:T(8,128)(2,1)S(1)}, bf16[64,15,128]{2,1,0:T(8,128)(2,1)S(1)}, u32[]{:S(2)}, u32[]{:S(2)}) collective-permute-start(bf16[64,15,128]{2,1,0:T(8,128)(2,1)S(1)} %get-tuple-element.29), channel_id=1, source_target_pairs={{4,0},{8,4},{12,8},{5,1},{9,5},{13,9},{6,2},{10,6},{14,10},{7,3},{... | collective-permute-start | bytes 737288 | tf_op jit(solution)/shard_map/ppermute | solution.py:34
  158.6 4.2 %collective-permute-start.10 = (bf16[15,32,128]{2,1,0:T(8,128)(2,1)S(1)}, bf16[15,32,128]{2,1,0:T(8,128)(2,1)S(1)}, u32[]{:S(2)}, u32[]{:S(2)}) collective-permute-start(bf16[15,32,128]{2,1,0:T(8,128)(2,1)S(1)} %get-tuple-element.26), channel_id=1, source_target_pairs={{0,2},{1,3},{4,6},{5,7},{8,10},{9,11},{12,14},{13,15},{16,18},{17,... | collective-permute-start | bytes 368648 | tf_op jit(solution)/shard_map/ppermute | solution.py:13
  160.0 6.8 %collective-permute-start.11 = (bf16[15,32,128]{2,1,0:T(8,128)(2,1)S(1)}, bf16[15,32,128]{2,1,0:T(8,128)(2,1)S(1)}, u32[]{:S(2)}, u32[]{:S(2)}) collective-permute-start(bf16[15,32,128]{2,1,0:T(8,128)(2,1)S(1)} %get-tuple-element.27), channel_id=1, source_target_pairs={{2,0},{3,1},{6,4},{7,5},{10,8},{11,9},{14,12},{15,13},{18,16},{19,... | collective-permute-start | bytes 368648 | tf_op jit(solution)/shard_map/ppermute | solution.py:13
  187.3 2.7 collective-permute-start.12
  190.9 5.2 %collective-permute-start.13 = (bf16[32,15,128]{2,1,0:T(8,128)(2,1)S(1)}, bf16[32,15,128]{2,1,0:T(8,128)(2,1)S(1)}, u32[]{:S(2)}, u32[]{:S(2)}) collective-permute-start(bf16[32,15,128]{2,1,0:T(8,128)(2,1)S(1)} %get-tuple-element.24), channel_id=1, source_target_pairs={{0,4},{4,8},{8,12},{1,5},{5,9},{9,13},{2,6},{6,10},{10,14},{3,7},{... | collective-permute-start | bytes 368648 | tf_op jit(solution)/shard_map/ppermute | solution.py:31
  193.1 7.2 %collective-permute-start.14 = (bf16[32,15,128]{2,1,0:T(8,128)(2,1)S(1)}, bf16[32,15,128]{2,1,0:T(8,128)(2,1)S(1)}, u32[]{:S(2)}, u32[]{:S(2)}) collective-permute-start(bf16[32,15,128]{2,1,0:T(8,128)(2,1)S(1)} %get-tuple-element.25), channel_id=1, source_target_pairs={{4,0},{8,4},{12,8},{5,1},{9,5},{13,9},{6,2},{10,6},{14,10},{7,3},{... | collective-permute-start | bytes 368648 | tf_op jit(solution)/shard_map/ppermute | solution.py:34
  200.4 1.6 collective-permute-start.15
  241.7 4.4 %collective-permute-start.16 = (bf16[15,32,128]{2,1,0:T(8,128)(2,1)S(1)}, bf16[15,32,128]{2,1,0:T(8,128)(2,1)S(1)}, u32[]{:S(2)}, u32[]{:S(2)}) collective-permute-start(bf16[15,32,128]{2,1,0:T(8,128)(2,1)S(1)} %get-tuple-element.20), channel_id=1, source_target_pairs={{0,2},{1,3},{4,6},{5,7},{8,10},{9,11},{12,14},{13,15},{16,18},{17,... | collective-permute-start | bytes 368648 | tf_op jit(solution)/shard_map/ppermute | solution.py:13
  243.2 7.1 %collective-permute-start.17 = (bf16[15,32,128]{2,1,0:T(8,128)(2,1)S(1)}, bf16[15,32,128]{2,1,0:T(8,128)(2,1)S(1)}, u32[]{:S(2)}, u32[]{:S(2)}) collective-permute-start(bf16[15,32,128]{2,1,0:T(8,128)(2,1)S(1)} %get-tuple-element.21), channel_id=1, source_target_pairs={{2,0},{3,1},{6,4},{7,5},{10,8},{11,9},{14,12},{15,13},{18,16},{19,... | collective-permute-start | bytes 368648 | tf_op jit(solution)/shard_map/ppermute | solution.py:13
  270.9 7.0 %collective-permute-start.18 = (bf16[64,15,128]{2,1,0:T(8,128)(2,1)S(1)}, bf16[64,15,128]{2,1,0:T(8,128)(2,1)S(1)}, u32[]{:S(2)}, u32[]{:S(2)}) collective-permute-start(bf16[64,15,128]{2,1,0:T(8,128)(2,1)S(1)} %get-tuple-element.18), channel_id=1, source_target_pairs={{0,4},{4,8},{8,12},{1,5},{5,9},{9,13},{2,6},{6,10},{10,14},{3,7},{... | collective-permute-start | bytes 737288 | tf_op jit(solution)/shard_map/ppermute | solution.py:31
  273.1 8.9 %collective-permute-start.19 = (bf16[64,15,128]{2,1,0:T(8,128)(2,1)S(1)}, bf16[64,15,128]{2,1,0:T(8,128)(2,1)S(1)}, u32[]{:S(2)}, u32[]{:S(2)}) collective-permute-start(bf16[64,15,128]{2,1,0:T(8,128)(2,1)S(1)} %get-tuple-element.19), channel_id=1, source_target_pairs={{4,0},{8,4},{12,8},{5,1},{9,5},{13,9},{6,2},{10,6},{14,10},{7,3},{... | collective-permute-start | bytes 737288 | tf_op jit(solution)/shard_map/ppermute | solution.py:34
  321.3 3.9 %collective-permute-start.20 = (bf16[15,32,128]{2,1,0:T(8,128)(2,1)S(1)}, bf16[15,32,128]{2,1,0:T(8,128)(2,1)S(1)}, u32[]{:S(2)}, u32[]{:S(2)}) collective-permute-start(bf16[15,32,128]{2,1,0:T(8,128)(2,1)S(1)} %get-tuple-element.16), channel_id=1, source_target_pairs={{0,2},{1,3},{4,6},{5,7},{8,10},{9,11},{12,14},{13,15},{16,18},{17,... | collective-permute-start | bytes 368648 | tf_op jit(solution)/shard_map/ppermute | solution.py:13
  322.8 6.8 %collective-permute-start.21 = (bf16[15,32,128]{2,1,0:T(8,128)(2,1)S(1)}, bf16[15,32,128]{2,1,0:T(8,128)(2,1)S(1)}, u32[]{:S(2)}, u32[]{:S(2)}) collective-permute-start(bf16[15,32,128]{2,1,0:T(8,128)(2,1)S(1)} %get-tuple-element.17), channel_id=1, source_target_pairs={{2,0},{3,1},{6,4},{7,5},{10,8},{11,9},{14,12},{15,13},{18,16},{19,... | collective-permute-start | bytes 368648 | tf_op jit(solution)/shard_map/ppermute | solution.py:13
  350.1 2.7 collective-permute-start.22
  (1 other events, 8.0 us)
where the time goes:
time: 358 us; the launch traced here: 354 us
  matrix products  236 us (66%)
  waiting for transfers between devices  59.1 us (17%)
  starting transfers between devices  36.3 us (10%)
  local copies, waits for them, and re-layouts  14.4 us (4%)
  other arithmetic  7 us (2%)
    dot_general x4, matrix products, separable(): jnp.dot(after_x.reshape(-1, width_y), matrices[1], preferred_element_type...  157 us
    dot_general x4, matrix products, along_z(): jnp.einsum('axy,ap->pxy', extended, matrix, preferred_element_type=jnp.fl...  79 us
    ppermute x10, waiting for transfers between devices, shifted(): return lax.ppermute(block, axis, route)  27.2 us
    ppermute x10, starting transfers between devices, shifted(): return lax.ppermute(block, axis, route)  19.2 us
    ppermute x4, waiting for transfers between devices, extended_2(): lax.ppermute(lax.slice_in_dim(block, 0, width, axis=dim), axis, backward)  16.5 us
    ppermute x4, starting transfers between devices, extended_2(): lax.ppermute(lax.slice_in_dim(block, block.shape[dim] - width, None, axis...  11.4 us
    slice x12, local copies, waits for them, and re-layouts, band_matrix(): taps[tap_index]  8.46 us
    ppermute x5, waiting for transfers between devices, from_partner(): return lax.ppermute(block, axis, route)  8.45 us
  transfers between devices with their start and end apart: 23, of which 21 were waited for; matrix products, arithmetic and copies ran while one was open for 3% of the time, Pallas kernels for 0%

commit v1 on v0

--- a/solution.py
+++ b/solution.py
@@ -49,24 +49,29 @@
 
 def operators(kernels, plane_count, width_x, width_y):
     reach = kernels.shape[1] // 2
-    return (
-        band_matrix(kernels[0], width_x + 2 * reach, width_x, 0),
+    along_x = band_matrix(kernels[0], width_x + 2 * reach, width_x, 0).T
+    along_x = jnp.broadcast_to(along_x[None], (plane_count,) + along_x.shape)
+    return lax.optimization_barrier((
+        along_x,
         band_matrix(kernels[1], width_y, width_y, reach),
-        band_matrix(kernels[2], plane_count + 2 * reach, plane_count, 0),
-    )
+        band_matrix(kernels[2], plane_count + 2 * reach, plane_count, 0).T,
+    ))
 
 
 def along_z(volume, matrix, reach):
     below_rim = shifted(volume[volume.shape[0] - reach :], "view", 2)
     above_rim = shifted(volume[:reach], "view", -2)
     extended = jnp.concatenate([below_rim, volume, above_rim], axis=0)
-    return jnp.einsum("axy,ap->pxy", extended, matrix, preferred_element_type=jnp.float32)
+    planes = extended.shape[0]
+    flat = extended.reshape(planes, -1)
+    out = jnp.dot(matrix, flat, preferred_element_type=jnp.float32)
+    return out.reshape(volume.shape)
 
 
 def separable(extended, matrices, reach):
     width_y = extended.shape[2]
     after_x = jnp.einsum(
-        "zay,ap->zpy", extended, matrices[0], preferred_element_type=jnp.float32
+        "zpa,zay->zpy", matrices[0], extended, preferred_element_type=jnp.float32
     ).astype(jnp.bfloat16)
     after_y = jnp.dot(after_x.reshape(-1, width_y), matrices[1], preferred_element_type=jnp.float32)
     after_y = after_y.reshape(after_x.shape).astype(jnp.bfloat16)

time: 358 us -> 235 us (0.66)
  matrix products: 236 us -> 6.98 us
  other arithmetic: 7 us -> 123 us
  waiting for transfers between devices: 59.1 us -> 42.1 us
  starting transfers between devices: 36.3 us -> 44.2 us
    dot_general x4, matrix products: 157 us -> 5.34 us  [separable(): jnp.dot(after_x.reshape(-1, width_y), matrices[1], preferred_element_type...]
    convert_element_type x0 -> x7, other arithmetic: none -> 116 us  [the longest x6 116 us: band_matrix(): return matrix.astype(jnp.bfloat16)]
    dot_general x4, matrix products: 79 us -> 1.64 us  [along_z(): out = jnp.dot(matrix, flat, preferred_element_type=jnp.float32)]
    ppermute x4, waiting for transfers between devices: 16.5 us -> 8.36 us  [extended_2(): lax.ppermute(lax.slice_in_dim(block, 0, width, axis=dim), axis, backward)]
    ppermute x10, waiting for transfers between devices: 27.2 us -> 21.7 us  [shifted(): return lax.ppermute(block, axis, route)]
    ppermute x4, starting transfers between devices: 11.4 us -> 16 us  [extended_2(): lax.ppermute(lax.slice_in_dim(block, block.shape[dim] - width, None, axis...]
  transfers between devices with their start and end apart: 23 -> 23, of which waited for: 21 -> 14; matrix products, arithmetic and copies ran while one was open for 3% -> 55% of each run, Pallas kernels for 0% -> 0%
where the time goes in v1:
time: 235 us; the launch traced here: 233 us
  other arithmetic  123 us (52%)
  starting transfers between devices  44.2 us (19%)
  waiting for transfers between devices  42.1 us (18%)
  local copies, waits for them, and re-layouts  15.4 us (7%)
  matrix products  6.98 us (3%)
    convert_element_type x6, other arithmetic, band_matrix(): return matrix.astype(jnp.bfloat16)  116 us
    ppermute x10, starting transfers between devices, shifted(): return lax.ppermute(block, axis, route)  22.5 us
    ppermute x10, waiting for transfers between devices, shifted(): return lax.ppermute(block, axis, route)  21.7 us
    ppermute x4, starting transfers between devices, extended_2(): lax.ppermute(lax.slice_in_dim(block, block.shape[dim] - width, None, axis...  16 us
    slice x12, local copies, waits for them, and re-layouts, band_matrix(): taps[tap_index]  8.44 us
    ppermute x4, waiting for transfers between devices, extended_2(): lax.ppermute(lax.slice_in_dim(block, 0, width, axis=dim), axis, backward)  8.36 us
    ppermute x5, waiting for transfers between devices, from_partner(): return lax.ppermute(block, axis, route)  6.82 us
    dot_general x4, matrix products, separable(): jnp.dot(after_x.reshape(-1, width_y), matrices[1], preferred_element_type...  5.34 us
  transfers between devices with their start and end apart: 23, of which 14 were waited for; matrix products, arithmetic and copies ran while one was open for 55% of the time, Pallas kernels for 0%

profile of v1, /device:TPU:0, one launch (start us, length us, event | category | flops | bytes accessed | tf_op | source)
XLA Modules:
  0.0 232.6 jit_solution(8698964199770454531)
XLA Ops:
  3.2 4.9 %collective-permute-start = (bf16[64,4,4,128]{3,0,2,1:T(8,128)(2,1)S(1)}, bf16[64,4,4,128]{3,0,2,1:T(8,128)(2,1)S(1)}, u32[]{:S(2)}, u32[]{:S(2)}) collective-permute-start(bf16[64,4,4,128]{3,0,2,1:T(8,128)(2,1)S(1)} %select_bitcast_fusion.1), channel_id=1, source_target_pairs={{0,4},{4,8},{8,12},{1,5},{5,9},{9,13},{2,6},{6,10},{10,14},{3,7},{... | collective-permute-start | bytes 786440 | tf_op jit(solution)/shard_map/ppermute | solution.py:13
  13.8 5.0 %collective-permute-done.1 = bf16[64,4,4,128]{3,0,2,1:T(8,128)(2,1)S(1)} collective-permute-done((bf16[64,4,4,128]{3,0,2,1:T(8,128)(2,1)S(1)}, bf16[64,4,4,128]{3,0,2,1:T(8,128)(2,1)S(1)}, u32[]{:S(2)}, u32[]{:S(2)}) %collective-permute-start.1) | collective-permute-done | bytes 262176 | tf_op jit(solution)/shard_map/ppermute | solution.py:13
  22.3 19.4 %add_convert_fusion = bf16[128,128]{1,0:T(8,128)(2,1)S(1)} fusion(f32[]{:T(128)} %bitcast.176, f32[]{:T(128)} %bitcast.175, f32[]{:T(128)} %bitcast.174, f32[]{:T(128)} %bitcast.173, f32[]{:T(128)} %bitcast.172, f32[]{:T(128)} %bitcast.171, f32[]{:T(128)} %bitcast.170, f32[]{:T(128)} %bitcast.169, f32[]{:T(128)} %bitcast.168, f32[]{:T(128)} %bitcast.167, ...), kind=kLoop, calls=%fused_computation.66 | loop fusion | flops 1556480 | bytes 32892 | tf_op jit(solution)/shard_map/convert_element_type | solution.py:47
  42.8 3.5 %collective-permute-start.3 = (bf16[32,15,128]{2,1,0:T(8,128)(2,1)S(1)}, bf16[32,15,128]{2,1,0:T(8,128)(2,1)S(1)}, u32[]{:S(2)}, u32[]{:S(2)}) collective-permute-start(bf16[32,15,128]{2,1,0:T(8,128)(2,1)S(1)} %get-tuple-element.46), channel_id=1, source_target_pairs={{0,4},{4,8},{8,12},{1,5},{5,9},{9,13},{2,6},{6,10},{10,14},{3,7},{... | collective-permute-start | bytes 368648 | tf_op jit(solution)/shard_map/ppermute | solution.py:31
  47.6 19.3 %add_convert_fusion.2 = bf16[64,94]{1,0:T(8,128)(2,1)S(1)} fusion(f32[]{:T(128)} %bitcast.207, f32[]{:T(128)} %bitcast.206, f32[]{:T(128)} %bitcast.205, f32[]{:T(128)} %bitcast.204, f32[]{:T(128)} %bitcast.203, f32[]{:T(128)} %bitcast.202, f32[]{:T(128)} %bitcast.201, f32[]{:T(128)} %bitcast.200, f32[]{:T(128)} %bitcast.199, f32[]{:T(128)} %bitcast.198, ...), kind=kLoop, calls=%fused_computation.104 | loop fusion | flops 565504 | bytes 12156 | tf_op jit(solution)/shard_map/convert_element_type | solution.py:47
  68.0 19.3 %add_convert_fusion.4 = bf16[32,62]{1,0:T(8,128)(2,1)S(1)} fusion(f32[]{:T(128)} %bitcast.145, f32[]{:T(128)} %bitcast.144, f32[]{:T(128)} %bitcast.143, f32[]{:T(128)} %bitcast.142, f32[]{:T(128)} %bitcast.141, f32[]{:T(128)} %bitcast.140, f32[]{:T(128)} %bitcast.139, f32[]{:T(128)} %bitcast.138, f32[]{:T(128)} %bitcast.137, f32[]{:T(128)} %bitcast.136, ...), kind=kLoop, calls=%fused_computation.142 | loop fusion | flops 186496 | bytes 4092 | tf_op jit(solution)/shard_map/convert_element_type | solution.py:47
  89.8 3.4 %collective-permute-start.6 = (bf16[15,32,128]{2,1,0:T(8,128)(2,1)S(1)}, bf16[15,32,128]{2,1,0:T(8,128)(2,1)S(1)}, u32[]{:S(2)}, u32[]{:S(2)}) collective-permute-start(bf16[15,32,128]{2,1,0:T(8,128)(2,1)S(1)} %get-tuple-element.42), channel_id=1, source_target_pairs={{0,2},{1,3},{4,6},{5,7},{8,10},{9,11},{12,14},{13,15},{16,18},{17,... | collective-permute-start | bytes 368648 | tf_op jit(solution)/shard_map/ppermute | solution.py:13
  94.5 19.3 %add_convert_fusion.3 = bf16[64,94]{1,0:T(8,128)(2,1)S(1)} fusion(f32[]{:T(128)} %bitcast.113, f32[]{:T(128)} %bitcast.112, f32[]{:T(128)} %bitcast.111, f32[]{:T(128)} %bitcast.110, f32[]{:T(128)} %bitcast.109, f32[]{:T(128)} %bitcast.108, f32[]{:T(128)} %bitcast.107, f32[]{:T(128)} %bitcast.106, f32[]{:T(128)} %bitcast.105, f32[]{:T(128)} %bitcast.104, ...), kind=kLoop, calls=%fused_computation.105 | loop fusion | flops 565504 | bytes 12156 | tf_op jit(solution)/shard_map/convert_element_type | solution.py:47
  115.8 4.4 %collective-permute-start.8 = (bf16[64,15,128]{2,1,0:T(8,128)(2,1)S(1)}, bf16[64,15,128]{2,1,0:T(8,128)(2,1)S(1)}, u32[]{:S(2)}, u32[]{:S(2)}) collective-permute-start(bf16[64,15,128]{2,1,0:T(8,128)(2,1)S(1)} %get-tuple-element.40), channel_id=1, source_target_pairs={{0,4},{4,8},{8,12},{1,5},{5,9},{9,13},{2,6},{6,10},{10,14},{3,7},{... | collective-permute-start | bytes 737288 | tf_op jit(solution)/shard_map/ppermute | solution.py:31
  121.5 19.4 %add_convert_fusion.5 = bf16[32,62]{1,0:T(8,128)(2,1)S(1)} fusion(f32[]{:T(128)} %bitcast.49, f32[]{:T(128)} %bitcast.48, f32[]{:T(128)} %bitcast.47, f32[]{:T(128)} %bitcast.46, f32[]{:T(128)} %bitcast.45, f32[]{:T(128)} %bitcast.44, f32[]{:T(128)} %bitcast.43, f32[]{:T(128)} %bitcast.42, f32[]{:T(128)} %bitcast.41, f32[]{:T(128)} %bitcast.40, ...), kind=kLoop, calls=%fused_computation.143 | loop fusion | flops 186496 | bytes 4092 | tf_op jit(solution)/shard_map/convert_element_type | solution.py:47
  141.6 19.6 %add_convert_fusion.1 = bf16[128,128]{1,0:T(8,128)(2,1)S(1)} fusion(f32[]{:T(128)} %bitcast.81, f32[]{:T(128)} %bitcast.80, f32[]{:T(128)} %bitcast.79, f32[]{:T(128)} %bitcast.78, f32[]{:T(128)} %bitcast.77, f32[]{:T(128)} %bitcast.76, f32[]{:T(128)} %bitcast.75, f32[]{:T(128)} %bitcast.74, f32[]{:T(128)} %bitcast.73, f32[]{:T(128)} %bitcast.72, ...), kind=kLoop, calls=%fused_computation.67 | loop fusion | flops 1556480 | bytes 32892 | tf_op jit(solution)/shard_map/convert_element_type | solution.py:47
  161.3 1.7 convolution_convert_fusion.4
  163.1 4.6 %collective-permute-start.10 = (bf16[15,32,128]{2,1,0:T(8,128)(2,1)S(1)}, bf16[15,32,128]{2,1,0:T(8,128)(2,1)S(1)}, u32[]{:S(2)}, u32[]{:S(2)}) collective-permute-start(bf16[15,32,128]{2,1,0:T(8,128)(2,1)S(1)} %get-tuple-element.38), channel_id=1, source_target_pairs={{0,2},{1,3},{4,6},{5,7},{8,10},{9,11},{12,14},{13,15},{16,18},{17,... | collective-permute-start | bytes 368648 | tf_op jit(solution)/shard_map/ppermute | solution.py:13
  170.1 4.4 %collective-permute-done.11 = bf16[15,32,128]{2,1,0:T(8,128)(2,1)S(1)} collective-permute-done((bf16[15,32,128]{2,1,0:T(8,128)(2,1)S(1)}, bf16[15,32,128]{2,1,0:T(8,128)(2,1)S(1)}, u32[]{:S(2)}, u32[]{:S(2)}) %collective-permute-start.11) | collective-permute-done | bytes 122912 | tf_op jit(solution)/shard_map/ppermute | solution.py:13
  175.7 2.6 %collective-permute-done.12 = f32[64,32,128]{2,1,0:T(8,128)S(1)} collective-permute-done((f32[64,32,128]{2,1,0:T(8,128)S(1)}, f32[64,32,128]{2,1,0:T(8,128)S(1)}, u32[]{:S(2)}, u32[]{:S(2)}) %collective-permute-start.12) | collective-permute-done | bytes 1048608 | tf_op jit(solution)/shard_map/ppermute | solution.py:23
  179.2 4.6 %collective-permute-start.13 = (bf16[32,15,128]{2,1,0:T(8,128)(2,1)S(1)}, bf16[32,15,128]{2,1,0:T(8,128)(2,1)S(1)}, u32[]{:S(2)}, u32[]{:S(2)}) collective-permute-start(bf16[32,15,128]{2,1,0:T(8,128)(2,1)S(1)} %get-tuple-element.36), channel_id=1, source_target_pairs={{0,4},{4,8},{8,12},{1,5},{5,9},{9,13},{2,6},{6,10},{10,14},{3,7},{... | collective-permute-start | bytes 368648 | tf_op jit(solution)/shard_map/ppermute | solution.py:31
  185.1 1.7 collective-permute-done.13
  186.8 4.1 %collective-permute-done.14 = bf16[32,15,128]{2,1,0:T(8,128)(2,1)S(1)} collective-permute-done((bf16[32,15,128]{2,1,0:T(8,128)(2,1)S(1)}, bf16[32,15,128]{2,1,0:T(8,128)(2,1)S(1)}, u32[]{:S(2)}, u32[]{:S(2)}) %collective-permute-start.14) | collective-permute-done | bytes 122912 | tf_op jit(solution)/shard_map/ppermute | solution.py:34
  199.6 4.3 %collective-permute-done.17 = bf16[15,32,128]{2,1,0:T(8,128)(2,1)S(1)} collective-permute-done((bf16[15,32,128]{2,1,0:T(8,128)(2,1)S(1)}, bf16[15,32,128]{2,1,0:T(8,128)(2,1)S(1)}, u32[]{:S(2)}, u32[]{:S(2)}) %collective-permute-start.17) | collective-permute-done | bytes 122912 | tf_op jit(solution)/shard_map/ppermute | solution.py:13
  205.3 3.6 %collective-permute-start.18 = (bf16[64,15,128]{2,1,0:T(8,128)(2,1)S(1)}, bf16[64,15,128]{2,1,0:T(8,128)(2,1)S(1)}, u32[]{:S(2)}, u32[]{:S(2)}) collective-permute-start(bf16[64,15,128]{2,1,0:T(8,128)(2,1)S(1)} %get-tuple-element.30), channel_id=1, source_target_pairs={{0,4},{4,8},{8,12},{1,5},{5,9},{9,13},{2,6},{6,10},{10,14},{3,7},{... | collective-permute-start | bytes 737288 | tf_op jit(solution)/shard_map/ppermute | solution.py:31
  210.2 3.5 %collective-permute-done.18 = bf16[64,15,128]{2,1,0:T(8,128)(2,1)S(1)} collective-permute-done((bf16[64,15,128]{2,1,0:T(8,128)(2,1)S(1)}, bf16[64,15,128]{2,1,0:T(8,128)(2,1)S(1)}, u32[]{:S(2)}, u32[]{:S(2)}) %collective-permute-start.18) | collective-permute-done | bytes 245792 | tf_op jit(solution)/shard_map/ppermute | solution.py:31
  213.7 4.2 %collective-permute-done.19 = bf16[64,15,128]{2,1,0:T(8,128)(2,1)} collective-permute-done((bf16[64,15,128]{2,1,0:T(8,128)(2,1)S(1)}, bf16[64,15,128]{2,1,0:T(8,128)(2,1)}, u32[]{:S(2)}, u32[]{:S(2)}) %collective-permute-start.19) | collective-permute-done | bytes 245792 | tf_op jit(solution)/shard_map/ppermute | solution.py:34
  223.4 4.4 %collective-permute-done.21 = bf16[15,32,128]{2,1,0:T(8,128)(2,1)S(1)} collective-permute-done((bf16[15,32,128]{2,1,0:T(8,128)(2,1)S(1)}, bf16[15,32,128]{2,1,0:T(8,128)(2,1)S(1)}, u32[]{:S(2)}, u32[]{:S(2)}) %collective-permute-start.21) | collective-permute-done | bytes 122912 | tf_op jit(solution)/shard_map/ppermute | solution.py:13
  229.0 2.6 %collective-permute-done.22 = f32[64,32,128]{2,1,0:T(8,128)S(1)} collective-permute-done((f32[64,32,128]{2,1,0:T(8,128)S(1)}, f32[64,32,128]{2,1,0:T(8,128)S(1)}, u32[]{:S(2)}, u32[]{:S(2)}) %collective-permute-start.22) | collective-permute-done | bytes 1048608 | tf_op jit(solution)/shard_map/ppermute | solution.py:23
  (127 shorter events, 48.2 us)
Async XLA Ops:
  3.2 10.7 %collective-permute-start = (bf16[64,4,4,128]{3,0,2,1:T(8,128)(2,1)S(1)}, bf16[64,4,4,128]{3,0,2,1:T(8,128)(2,1)S(1)}, u32[]{:S(2)}, u32[]{:S(2)}) collective-permute-start(bf16[64,4,4,128]{3,0,2,1:T(8,128)(2,1)S(1)} %select_bitcast_fusion.1), channel_id=1, source_target_pairs={{0,4},{4,8},{8,12},{1,5},{5,9},{9,13},{2,6},{6,10},{10,14},{3,7},{... | collective-permute-start | bytes 786440 | tf_op jit(solution)/shard_map/ppermute | solution.py:13
  9.2 9.7 %collective-permute-start.1 = (bf16[64,4,4,128]{3,0,2,1:T(8,128)(2,1)S(1)}, bf16[64,4,4,128]{3,0,2,1:T(8,128)(2,1)S(1)}, u32[]{:S(2)}, u32[]{:S(2)}) collective-permute-start(bf16[64,4,4,128]{3,0,2,1:T(8,128)(2,1)S(1)} %select_bitcast_fusion), channel_id=1, source_target_pairs={{4,0},{8,4},{12,8},{5,1},{9,5},{13,9},{6,2},{10,6},{14,10},{7,3},{... | collective-permute-start | bytes 786440 | tf_op jit(solution)/shard_map/ppermute | solution.py:13
  20.1 22.3 %collective-permute-start.2 = (bf16[64,32,128]{2,1,0:T(8,128)(2,1)S(1)}, bf16[64,32,128]{2,1,0:T(8,128)(2,1)S(1)}, u32[]{:S(2)}, u32[]{:S(2)}) collective-permute-start(bf16[64,32,128]{2,1,0:T(8,128)(2,1)S(1)} %broadcast_select_fusion), channel_id=1, source_target_pairs={{0,1},{1,0},{2,3},{3,2},{4,5},{5,4},{6,7},{7,6},{8,9},{9,8},{10,11... | collective-permute-start | bytes 1572872 | tf_op jit(solution)/shard_map/ppermute | solution.py:23
  42.8 24.8 %collective-permute-start.3 = (bf16[32,15,128]{2,1,0:T(8,128)(2,1)S(1)}, bf16[32,15,128]{2,1,0:T(8,128)(2,1)S(1)}, u32[]{:S(2)}, u32[]{:S(2)}) collective-permute-start(bf16[32,15,128]{2,1,0:T(8,128)(2,1)S(1)} %get-tuple-element.46), channel_id=1, source_target_pairs={{0,4},{4,8},{8,12},{1,5},{5,9},{9,13},{2,6},{6,10},{10,14},{3,7},{... | collective-permute-start | bytes 368648 | tf_op jit(solution)/shard_map/ppermute | solution.py:31
  46.3 21.3 %collective-permute-start.4 = (bf16[32,15,128]{2,1,0:T(8,128)(2,1)S(1)}, bf16[32,15,128]{2,1,0:T(8,128)(2,1)S(1)}, u32[]{:S(2)}, u32[]{:S(2)}) collective-permute-start(bf16[32,15,128]{2,1,0:T(8,128)(2,1)S(1)} %get-tuple-element.47), channel_id=1, source_target_pairs={{4,0},{8,4},{12,8},{5,1},{9,5},{13,9},{6,2},{10,6},{14,10},{7,3},{... | collective-permute-start | bytes 368648 | tf_op jit(solution)/shard_map/ppermute | solution.py:34
  67.7 21.1 %collective-permute-start.5 = (bf16[32,30,128]{2,1,0:T(8,128)(2,1)S(1)}, bf16[32,30,128]{2,1,0:T(8,128)(2,1)S(1)}, u32[]{:S(2)}, u32[]{:S(2)}) collective-permute-start(bf16[32,30,128]{2,1,0:T(8,128)(2,1)S(1)} %pad_maximum_fusion.5), channel_id=1, source_target_pairs={{0,1},{1,0},{2,3},{3,2},{4,5},{5,4},{6,7},{7,6},{8,9},{9,8},{10,11... | collective-permute-start | bytes 737288 | tf_op jit(solution)/shard_map/ppermute | solution.py:23
  89.8 24.7 %collective-permute-start.6 = (bf16[15,32,128]{2,1,0:T(8,128)(2,1)S(1)}, bf16[15,32,128]{2,1,0:T(8,128)(2,1)S(1)}, u32[]{:S(2)}, u32[]{:S(2)}) collective-permute-start(bf16[15,32,128]{2,1,0:T(8,128)(2,1)S(1)} %get-tuple-element.42), channel_id=1, source_target_pairs={{0,2},{1,3},{4,6},{5,7},{8,10},{9,11},{12,14},{13,15},{16,18},{17,... | collective-permute-start | bytes 368648 | tf_op jit(solution)/shard_map/ppermute | solution.py:13
  93.2 21.3 %collective-permute-start.7 = (bf16[15,32,128]{2,1,0:T(8,128)(2,1)S(1)}, bf16[15,32,128]{2,1,0:T(8,128)(2,1)S(1)}, u32[]{:S(2)}, u32[]{:S(2)}) collective-permute-start(bf16[15,32,128]{2,1,0:T(8,128)(2,1)S(1)} %get-tuple-element.43), channel_id=1, source_target_pairs={{2,0},{3,1},{6,4},{7,5},{10,8},{11,9},{14,12},{15,13},{18,16},{19,... | collective-permute-start | bytes 368648 | tf_op jit(solution)/shard_map/ppermute | solution.py:13
  115.8 45.5 %collective-permute-start.8 = (bf16[64,15,128]{2,1,0:T(8,128)(2,1)S(1)}, bf16[64,15,128]{2,1,0:T(8,128)(2,1)S(1)}, u32[]{:S(2)}, u32[]{:S(2)}) collective-permute-start(bf16[64,15,128]{2,1,0:T(8,128)(2,1)S(1)} %get-tuple-element.40), channel_id=1, source_target_pairs={{0,4},{4,8},{8,12},{1,5},{5,9},{9,13},{2,6},{6,10},{10,14},{3,7},{... | collective-permute-start | bytes 737288 | tf_op jit(solution)/shard_map/ppermute | solution.py:31
  120.2 41.1 %collective-permute-start.9 = (bf16[64,15,128]{2,1,0:T(8,128)(2,1)S(1)}, bf16[64,15,128]{2,1,0:T(8,128)(2,1)}, u32[]{:S(2)}, u32[]{:S(2)}) collective-permute-start(bf16[64,15,128]{2,1,0:T(8,128)(2,1)S(1)} %get-tuple-element.41), channel_id=1, source_target_pairs={{4,0},{8,4},{12,8},{5,1},{9,5},{13,9},{6,2},{10,6},{14,10},{7,3},{... | collective-permute-start | bytes 737288 | tf_op jit(solution)/shard_map/ppermute | solution.py:34
  163.1 7.0 %collective-permute-start.10 = (bf16[15,32,128]{2,1,0:T(8,128)(2,1)S(1)}, bf16[15,32,128]{2,1,0:T(8,128)(2,1)S(1)}, u32[]{:S(2)}, u32[]{:S(2)}) collective-permute-start(bf16[15,32,128]{2,1,0:T(8,128)(2,1)S(1)} %get-tuple-element.38), channel_id=1, source_target_pairs={{0,2},{1,3},{4,6},{5,7},{8,10},{9,11},{12,14},{13,15},{16,18},{17,... | collective-permute-start | bytes 368648 | tf_op jit(solution)/shard_map/ppermute | solution.py:13
  167.7 6.8 %collective-permute-start.11 = (bf16[15,32,128]{2,1,0:T(8,128)(2,1)S(1)}, bf16[15,32,128]{2,1,0:T(8,128)(2,1)S(1)}, u32[]{:S(2)}, u32[]{:S(2)}) collective-permute-start(bf16[15,32,128]{2,1,0:T(8,128)(2,1)S(1)} %get-tuple-element.39), channel_id=1, source_target_pairs={{2,0},{3,1},{6,4},{7,5},{10,8},{11,9},{14,12},{15,13},{18,16},{19,... | collective-permute-start | bytes 368648 | tf_op jit(solution)/shard_map/ppermute | solution.py:13
  175.6 2.7 %collective-permute-start.12 = (f32[64,32,128]{2,1,0:T(8,128)S(1)}, f32[64,32,128]{2,1,0:T(8,128)S(1)}, u32[]{:S(2)}, u32[]{:S(2)}) collective-permute-start(f32[64,32,128]{2,1,0:T(8,128)S(1)} %copy.17), channel_id=1, source_target_pairs={{0,1},{1,0},{2,3},{3,2},{4,5},{5,4},{6,7},{7,6},{8,9},{9,8},{10,11... | collective-permute-start | bytes 3145736 | tf_op jit(solution)/shard_map/ppermute | solution.py:23
  179.2 7.6 %collective-permute-start.13 = (bf16[32,15,128]{2,1,0:T(8,128)(2,1)S(1)}, bf16[32,15,128]{2,1,0:T(8,128)(2,1)S(1)}, u32[]{:S(2)}, u32[]{:S(2)}) collective-permute-start(bf16[32,15,128]{2,1,0:T(8,128)(2,1)S(1)} %get-tuple-element.36), channel_id=1, source_target_pairs={{0,4},{4,8},{8,12},{1,5},{5,9},{9,13},{2,6},{6,10},{10,14},{3,7},{... | collective-permute-start | bytes 368648 | tf_op jit(solution)/shard_map/ppermute | solution.py:31
  183.8 7.2 %collective-permute-start.14 = (bf16[32,15,128]{2,1,0:T(8,128)(2,1)S(1)}, bf16[32,15,128]{2,1,0:T(8,128)(2,1)S(1)}, u32[]{:S(2)}, u32[]{:S(2)}) collective-permute-start(bf16[32,15,128]{2,1,0:T(8,128)(2,1)S(1)} %get-tuple-element.37), channel_id=1, source_target_pairs={{4,0},{8,4},{12,8},{5,1},{9,5},{13,9},{6,2},{10,6},{14,10},{7,3},{... | collective-permute-start | bytes 368648 | tf_op jit(solution)/shard_map/ppermute | solution.py:34
  191.0 1.6 collective-permute-start.15
  195.2 4.4 %collective-permute-start.16 = (bf16[15,32,128]{2,1,0:T(8,128)(2,1)S(1)}, bf16[15,32,128]{2,1,0:T(8,128)(2,1)S(1)}, u32[]{:S(2)}, u32[]{:S(2)}) collective-permute-start(bf16[15,32,128]{2,1,0:T(8,128)(2,1)S(1)} %get-tuple-element.32), channel_id=1, source_target_pairs={{0,2},{1,3},{4,6},{5,7},{8,10},{9,11},{12,14},{13,15},{16,18},{17,... | collective-permute-start | bytes 368648 | tf_op jit(solution)/shard_map/ppermute | solution.py:13
  196.9 7.1 %collective-permute-start.17 = (bf16[15,32,128]{2,1,0:T(8,128)(2,1)S(1)}, bf16[15,32,128]{2,1,0:T(8,128)(2,1)S(1)}, u32[]{:S(2)}, u32[]{:S(2)}) collective-permute-start(bf16[15,32,128]{2,1,0:T(8,128)(2,1)S(1)} %get-tuple-element.33), channel_id=1, source_target_pairs={{2,0},{3,1},{6,4},{7,5},{10,8},{11,9},{14,12},{15,13},{18,16},{19,... | collective-permute-start | bytes 368648 | tf_op jit(solution)/shard_map/ppermute | solution.py:13
  205.2 12.7 %copy-start.1 = (bf16[64,32,62]{2,1,0:T(8,128)(2,1)S(1)}, bf16[64,32,62]{2,1,0:T(8,128)(2,1)}, u32[]{:S(2)}) copy-start(bf16[64,32,62]{2,1,0:T(8,128)(2,1)} %copy-done) | copy-start | bytes 761860
  205.3 8.4 %collective-permute-start.18 = (bf16[64,15,128]{2,1,0:T(8,128)(2,1)S(1)}, bf16[64,15,128]{2,1,0:T(8,128)(2,1)S(1)}, u32[]{:S(2)}, u32[]{:S(2)}) collective-permute-start(bf16[64,15,128]{2,1,0:T(8,128)(2,1)S(1)} %get-tuple-element.30), channel_id=1, source_target_pairs={{0,4},{4,8},{8,12},{1,5},{5,9},{9,13},{2,6},{6,10},{10,14},{3,7},{... | collective-permute-start | bytes 737288 | tf_op jit(solution)/shard_map/ppermute | solution.py:31
  208.9 9.0 %collective-permute-start.19 = (bf16[64,15,128]{2,1,0:T(8,128)(2,1)S(1)}, bf16[64,15,128]{2,1,0:T(8,128)(2,1)}, u32[]{:S(2)}, u32[]{:S(2)}) collective-permute-start(bf16[64,15,128]{2,1,0:T(8,128)(2,1)S(1)} %get-tuple-element.31), channel_id=1, source_target_pairs={{4,0},{8,4},{12,8},{5,1},{9,5},{13,9},{6,2},{10,6},{14,10},{7,3},{... | collective-permute-start | bytes 737288 | tf_op jit(solution)/shard_map/ppermute | solution.py:34
  219.5 3.9 %collective-permute-start.20 = (bf16[15,32,128]{2,1,0:T(8,128)(2,1)S(1)}, bf16[15,32,128]{2,1,0:T(8,128)(2,1)S(1)}, u32[]{:S(2)}, u32[]{:S(2)}) collective-permute-start(bf16[15,32,128]{2,1,0:T(8,128)(2,1)S(1)} %get-tuple-element.28), channel_id=1, source_target_pairs={{0,2},{1,3},{4,6},{5,7},{8,10},{9,11},{12,14},{13,15},{16,18},{17,... | collective-permute-start | bytes 368648 | tf_op jit(solution)/shard_map/ppermute | solution.py:13
  220.9 6.8 %collective-permute-start.21 = (bf16[15,32,128]{2,1,0:T(8,128)(2,1)S(1)}, bf16[15,32,128]{2,1,0:T(8,128)(2,1)S(1)}, u32[]{:S(2)}, u32[]{:S(2)}) collective-permute-start(bf16[15,32,128]{2,1,0:T(8,128)(2,1)S(1)} %get-tuple-element.29), channel_id=1, source_target_pairs={{2,0},{3,1},{6,4},{7,5},{10,8},{11,9},{14,12},{15,13},{18,16},{19,... | collective-permute-start | bytes 368648 | tf_op jit(solution)/shard_map/ppermute | solution.py:13
  228.9 2.7 %collective-permute-start.22 = (f32[64,32,128]{2,1,0:T(8,128)S(1)}, f32[64,32,128]{2,1,0:T(8,128)S(1)}, u32[]{:S(2)}, u32[]{:S(2)}) collective-permute-start(f32[64,32,128]{2,1,0:T(8,128)S(1)} %copy.22), channel_id=1, source_target_pairs={{0,1},{1,0},{2,3},{3,2},{4,5},{5,4},{6,7},{7,6},{8,9},{9,8},{10,11... | collective-permute-start | bytes 3145736 | tf_op jit(solution)/shard_map/ppermute | solution.py:23
  (3 other events, 18.5 us)

commit v2 on v1

--- a/solution.py
+++ b/solution.py
@@ -37,13 +37,12 @@
 
 
 def band_matrix(kernel, row_count, col_count, base_shift):
-    row_ids = lax.broadcasted_iota(jnp.int32, (row_count, col_count), 0)
-    col_ids = lax.broadcasted_iota(jnp.int32, (row_count, col_count), 1)
-    distance = row_ids - col_ids + base_shift
-    taps = kernel.astype(jnp.float32)
-    matrix = jnp.zeros((row_count, col_count), jnp.float32)
-    for tap_index in range(kernel.shape[0]):
-        matrix = matrix + jnp.where(distance == tap_index, taps[tap_index], jnp.float32(0.0))
+    row_ids = lax.broadcasted_iota(jnp.int32, (row_count, col_count, 1), 0)
+    col_ids = lax.broadcasted_iota(jnp.int32, (row_count, col_count, 1), 1)
+    tap_ids = lax.broadcasted_iota(jnp.int32, (1, 1, kernel.shape[0]), 2)
+    hit = row_ids - col_ids + base_shift == tap_ids
+    taps = kernel.astype(jnp.float32)[None, None, :]
+    matrix = jnp.sum(jnp.where(hit, taps, jnp.float32(0.0)), axis=2)
     return matrix.astype(jnp.bfloat16)
 
 

time: 235 us -> 123 us (0.52)
  other arithmetic: 123 us -> 7.93 us
  waiting for transfers between devices: 42.1 us -> 65.3 us
  local copies, waits for them, and re-layouts: 15.4 us -> 6.95 us
  starting transfers between devices: 44.2 us -> 36.1 us
    convert_element_type x7 -> x3, other arithmetic: 116 us -> 0.01 us  [band_matrix(): taps = kernel.astype(jnp.float32)[None, None, :]]
    slice x12 -> x0, local copies, waits for them, and re-layouts: 8.44 us -> none  [band_matrix(): taps[tap_index]]
    ppermute x4, waiting for transfers between devices: 8.36 us -> 16.6 us  [extended_2(): lax.ppermute(lax.slice_in_dim(block, 0, width, axis=dim), axis, backward)]
    ppermute x10, waiting for transfers between devices: 21.7 us -> 29 us  [shifted(): return lax.ppermute(block, axis, route)]
    ppermute x4, waiting for transfers between devices: 5.2 us -> 10 us  [extended_2(): lax.ppermute(lax.slice_in_dim(block, block.shape[dim] - width, None, axis...]
    ppermute x4, starting transfers between devices: 16 us -> 11.5 us  [extended_2(): lax.ppermute(lax.slice_in_dim(block, block.shape[dim] - width, None, axis...]
    ppermute x10, starting transfers between devices: 22.5 us -> 19.1 us  [shifted(): return lax.ppermute(block, axis, route)]
    ppermute x5, waiting for transfers between devices: 6.82 us -> 9.68 us  [from_partner(): return lax.ppermute(block, axis, route)]
  transfers between devices with their start and end apart: 23 -> 23, of which waited for: 14 -> 23; matrix products, arithmetic and copies ran while one was open for 55% -> 3% of each run, Pallas kernels for 0% -> 0%
where the time goes in v2:
time: 123 us
  waiting for transfers between devices  65.3 us (53%)
  starting transfers between devices  36.1 us (29%)
  other arithmetic  7.93 us (6%)
  local copies, waits for them, and re-layouts  6.95 us (6%)
  matrix products  5.85 us (5%)
    ppermute x10, waiting for transfers between devices, shifted(): return lax.ppermute(block, axis, route)  29 us
    ppermute x10, starting transfers between devices, shifted(): return lax.ppermute(block, axis, route)  19.1 us
    ppermute x4, waiting for transfers between devices, extended_2(): lax.ppermute(lax.slice_in_dim(block, 0, width, axis=dim), axis, backward)  16.6 us
    ppermute x4, starting transfers between devices, extended_2(): lax.ppermute(lax.slice_in_dim(block, block.shape[dim] - width, None, axis...  11.5 us
    ppermute x4, waiting for transfers between devices, extended_2(): lax.ppermute(lax.slice_in_dim(block, block.shape[dim] - width, None, axis...  10 us
    ppermute x5, waiting for transfers between devices, from_partner(): return lax.ppermute(block, axis, route)  9.68 us
    ppermute x4, starting transfers between devices, extended_2(): lax.ppermute(lax.slice_in_dim(block, 0, width, axis=dim), axis, backward)  5.17 us
    dot_general x4, matrix products, separable(): jnp.dot(after_x.reshape(-1, width_y), matrices[1], preferred_element_type...  4.2 us
  transfers between devices with their start and end apart: 23, of which 23 were waited for; matrix products, arithmetic and copies ran while one was open for 3% of the time, Pallas kernels for 0%

profile of v2, /device:TPU:0, one launch (start us, length us, event | category | flops | bytes accessed | tf_op | source)
XLA Modules:
  0.0 122.8 jit_solution(2693400467156899794)
XLA Ops:
  3.2 4.9 %collective-permute-start = (bf16[64,4,4,128]{3,0,2,1:T(8,128)(2,1)S(1)}, bf16[64,4,4,128]{3,0,2,1:T(8,128)(2,1)S(1)}, u32[]{:S(2)}, u32[]{:S(2)}) collective-permute-start(bf16[64,4,4,128]{3,0,2,1:T(8,128)(2,1)S(1)} %select_bitcast_fusion.1), channel_id=1, source_target_pairs={{0,4},{4,8},{8,12},{1,5},{5,9},{9,13},{2,6},{6,10},{10,14},{3,7},{... | collective-permute-start | bytes 786440 | tf_op jit(solution)/shard_map/ppermute | solution.py:13
  13.6 5.2 %collective-permute-done.1 = bf16[64,4,4,128]{3,0,2,1:T(8,128)(2,1)S(1)} collective-permute-done((bf16[64,4,4,128]{3,0,2,1:T(8,128)(2,1)S(1)}, bf16[64,4,4,128]{3,0,2,1:T(8,128)(2,1)S(1)}, u32[]{:S(2)}, u32[]{:S(2)}) %collective-permute-start.1) | collective-permute-done | bytes 262176 | tf_op jit(solution)/shard_map/ppermute | solution.py:13
  20.2 1.9 %collective-permute-done.2 = bf16[64,32,128]{2,1,0:T(8,128)(2,1)S(1)} collective-permute-done((bf16[64,32,128]{2,1,0:T(8,128)(2,1)S(1)}, bf16[64,32,128]{2,1,0:T(8,128)(2,1)S(1)}, u32[]{:S(2)}, u32[]{:S(2)}) %collective-permute-start.2) | collective-permute-done | bytes 524320 | tf_op jit(solution)/shard_map/ppermute | solution.py:23
  22.5 3.5 %collective-permute-start.3 = (bf16[32,15,128]{2,1,0:T(8,128)(2,1)S(1)}, bf16[32,15,128]{2,1,0:T(8,128)(2,1)S(1)}, u32[]{:S(2)}, u32[]{:S(2)}) collective-permute-start(bf16[32,15,128]{2,1,0:T(8,128)(2,1)S(1)} %get-tuple-element.52), channel_id=1, source_target_pairs={{0,4},{4,8},{8,12},{1,5},{5,9},{9,13},{2,6},{6,10},{10,14},{3,7},{... | collective-permute-start | bytes 368648 | tf_op jit(solution)/shard_map/ppermute | solution.py:31
  27.4 1.5 %collective-permute-done.3 = bf16[32,15,128]{2,1,0:T(8,128)(2,1)S(1)} collective-permute-done((bf16[32,15,128]{2,1,0:T(8,128)(2,1)S(1)}, bf16[32,15,128]{2,1,0:T(8,128)(2,1)S(1)}, u32[]{:S(2)}, u32[]{:S(2)}) %collective-permute-start.3) | collective-permute-done | bytes 122912 | tf_op jit(solution)/shard_map/ppermute | solution.py:31
  29.0 4.1 %collective-permute-done.4 = bf16[32,15,128]{2,1,0:T(8,128)(2,1)S(1)} collective-permute-done((bf16[32,15,128]{2,1,0:T(8,128)(2,1)S(1)}, bf16[32,15,128]{2,1,0:T(8,128)(2,1)S(1)}, u32[]{:S(2)}, u32[]{:S(2)}) %collective-permute-start.4) | collective-permute-done | bytes 122912 | tf_op jit(solution)/shard_map/ppermute | solution.py:34
  35.7 3.4 %collective-permute-start.6 = (bf16[15,32,128]{2,1,0:T(8,128)(2,1)S(1)}, bf16[15,32,128]{2,1,0:T(8,128)(2,1)S(1)}, u32[]{:S(2)}, u32[]{:S(2)}) collective-permute-start(bf16[15,32,128]{2,1,0:T(8,128)(2,1)S(1)} %get-tuple-element.48), channel_id=1, source_target_pairs={{0,2},{1,3},{4,6},{5,7},{8,10},{9,11},{12,14},{13,15},{16,18},{17,... | collective-permute-start | bytes 368648 | tf_op jit(solution)/shard_map/ppermute | solution.py:13
  40.4 1.6 %collective-permute-done.6 = bf16[15,32,128]{2,1,0:T(8,128)(2,1)S(1)} collective-permute-done((bf16[15,32,128]{2,1,0:T(8,128)(2,1)S(1)}, bf16[15,32,128]{2,1,0:T(8,128)(2,1)S(1)}, u32[]{:S(2)}, u32[]{:S(2)}) %collective-permute-start.6) | collective-permute-done | bytes 122912 | tf_op jit(solution)/shard_map/ppermute | solution.py:13
  42.0 4.1 %collective-permute-done.7 = bf16[15,32,128]{2,1,0:T(8,128)(2,1)S(1)} collective-permute-done((bf16[15,32,128]{2,1,0:T(8,128)(2,1)S(1)}, bf16[15,32,128]{2,1,0:T(8,128)(2,1)S(1)}, u32[]{:S(2)}, u32[]{:S(2)}) %collective-permute-start.7) | collective-permute-done | bytes 122912 | tf_op jit(solution)/shard_map/ppermute | solution.py:13
  47.4 3.5 %collective-permute-start.8 = (bf16[64,15,128]{2,1,0:T(8,128)(2,1)S(1)}, bf16[64,15,128]{2,1,0:T(8,128)(2,1)S(1)}, u32[]{:S(2)}, u32[]{:S(2)}) collective-permute-start(bf16[64,15,128]{2,1,0:T(8,128)(2,1)S(1)} %get-tuple-element.46), channel_id=1, source_target_pairs={{0,4},{4,8},{8,12},{1,5},{5,9},{9,13},{2,6},{6,10},{10,14},{3,7},{... | collective-permute-start | bytes 737288 | tf_op jit(solution)/shard_map/ppermute | solution.py:31
  52.3 3.3 %collective-permute-done.8 = bf16[64,15,128]{2,1,0:T(8,128)(2,1)S(1)} collective-permute-done((bf16[64,15,128]{2,1,0:T(8,128)(2,1)S(1)}, bf16[64,15,128]{2,1,0:T(8,128)(2,1)S(1)}, u32[]{:S(2)}, u32[]{:S(2)}) %collective-permute-start.8) | collective-permute-done | bytes 245792 | tf_op jit(solution)/shard_map/ppermute | solution.py:31
  55.6 4.2 %collective-permute-done.9 = bf16[64,15,128]{2,1,0:T(8,128)(2,1)} collective-permute-done((bf16[64,15,128]{2,1,0:T(8,128)(2,1)S(1)}, bf16[64,15,128]{2,1,0:T(8,128)(2,1)}, u32[]{:S(2)}, u32[]{:S(2)}) %collective-permute-start.9) | collective-permute-done | bytes 245792 | tf_op jit(solution)/shard_map/ppermute | solution.py:34
  65.2 4.4 %collective-permute-done.11 = bf16[15,32,128]{2,1,0:T(8,128)(2,1)S(1)} collective-permute-done((bf16[15,32,128]{2,1,0:T(8,128)(2,1)S(1)}, bf16[15,32,128]{2,1,0:T(8,128)(2,1)S(1)}, u32[]{:S(2)}, u32[]{:S(2)}) %collective-permute-start.11) | collective-permute-done | bytes 122912 | tf_op jit(solution)/shard_map/ppermute | solution.py:13
  70.8 2.6 %collective-permute-done.12 = f32[64,32,128]{2,1,0:T(8,128)S(1)} collective-permute-done((f32[64,32,128]{2,1,0:T(8,128)S(1)}, f32[64,32,128]{2,1,0:T(8,128)S(1)}, u32[]{:S(2)}, u32[]{:S(2)}) %collective-permute-start.12) | collective-permute-done | bytes 1048608 | tf_op jit(solution)/shard_map/ppermute | solution.py:23
  74.4 2.2 %collective-permute-start.13 = (bf16[32,15,128]{2,1,0:T(8,128)(2,1)S(1)}, bf16[32,15,128]{2,1,0:T(8,128)(2,1)S(1)}, u32[]{:S(2)}, u32[]{:S(2)}) collective-permute-start(bf16[32,15,128]{2,1,0:T(8,128)(2,1)S(1)} %get-tuple-element.42), channel_id=1, source_target_pairs={{0,4},{4,8},{8,12},{1,5},{5,9},{9,13},{2,6},{6,10},{10,14},{3,7},{... | collective-permute-start | bytes 368648 | tf_op jit(solution)/shard_map/ppermute | solution.py:31
  77.9 1.7 %collective-permute-done.13 = bf16[32,15,128]{2,1,0:T(8,128)(2,1)S(1)} collective-permute-done((bf16[32,15,128]{2,1,0:T(8,128)(2,1)S(1)}, bf16[32,15,128]{2,1,0:T(8,128)(2,1)S(1)}, u32[]{:S(2)}, u32[]{:S(2)}) %collective-permute-start.13) | collective-permute-done | bytes 122912 | tf_op jit(solution)/shard_map/ppermute | solution.py:31
  79.6 4.1 %collective-permute-done.14 = bf16[32,15,128]{2,1,0:T(8,128)(2,1)S(1)} collective-permute-done((bf16[32,15,128]{2,1,0:T(8,128)(2,1)S(1)}, bf16[32,15,128]{2,1,0:T(8,128)(2,1)S(1)}, u32[]{:S(2)}, u32[]{:S(2)}) %collective-permute-start.14) | collective-permute-done | bytes 122912 | tf_op jit(solution)/shard_map/ppermute | solution.py:34
  90.8 1.6 %collective-permute-done.16 = bf16[15,32,128]{2,1,0:T(8,128)(2,1)S(1)} collective-permute-done((bf16[15,32,128]{2,1,0:T(8,128)(2,1)S(1)}, bf16[15,32,128]{2,1,0:T(8,128)(2,1)S(1)}, u32[]{:S(2)}, u32[]{:S(2)}) %collective-permute-start.16) | collective-permute-done | bytes 122912 | tf_op jit(solution)/shard_map/ppermute | solution.py:13
  92.4 4.1 %collective-permute-done.17 = bf16[15,32,128]{2,1,0:T(8,128)(2,1)S(1)} collective-permute-done((bf16[15,32,128]{2,1,0:T(8,128)(2,1)S(1)}, bf16[15,32,128]{2,1,0:T(8,128)(2,1)S(1)}, u32[]{:S(2)}, u32[]{:S(2)}) %collective-permute-start.17) | collective-permute-done | bytes 122912 | tf_op jit(solution)/shard_map/ppermute | solution.py:13
  97.9 2.3 %collective-permute-start.18 = (bf16[64,15,128]{2,1,0:T(8,128)(2,1)S(1)}, bf16[64,15,128]{2,1,0:T(8,128)(2,1)S(1)}, u32[]{:S(2)}, u32[]{:S(2)}) collective-permute-start(bf16[64,15,128]{2,1,0:T(8,128)(2,1)S(1)} %get-tuple-element.36), channel_id=1, source_target_pairs={{0,4},{4,8},{8,12},{1,5},{5,9},{9,13},{2,6},{6,10},{10,14},{3,7},{... | collective-permute-start | bytes 737288 | tf_op jit(solution)/shard_map/ppermute | solution.py:31
  101.5 3.5 %collective-permute-done.18 = bf16[64,15,128]{2,1,0:T(8,128)(2,1)S(1)} collective-permute-done((bf16[64,15,128]{2,1,0:T(8,128)(2,1)S(1)}, bf16[64,15,128]{2,1,0:T(8,128)(2,1)S(1)}, u32[]{:S(2)}, u32[]{:S(2)}) %collective-permute-start.18) | collective-permute-done | bytes 245792 | tf_op jit(solution)/shard_map/ppermute | solution.py:31
  105.0 4.1 %collective-permute-done.19 = bf16[64,15,128]{2,1,0:T(8,128)(2,1)S(1)} collective-permute-done((bf16[64,15,128]{2,1,0:T(8,128)(2,1)S(1)}, bf16[64,15,128]{2,1,0:T(8,128)(2,1)S(1)}, u32[]{:S(2)}, u32[]{:S(2)}) %collective-permute-start.19) | collective-permute-done | bytes 245792 | tf_op jit(solution)/shard_map/ppermute | solution.py:34
  113.6 4.4 %collective-permute-done.21 = bf16[15,32,128]{2,1,0:T(8,128)(2,1)S(1)} collective-permute-done((bf16[15,32,128]{2,1,0:T(8,128)(2,1)S(1)}, bf16[15,32,128]{2,1,0:T(8,128)(2,1)S(1)}, u32[]{:S(2)}, u32[]{:S(2)}) %collective-permute-start.21) | collective-permute-done | bytes 122912 | tf_op jit(solution)/shard_map/ppermute | solution.py:13
  119.2 2.6 %collective-permute-done.22 = f32[64,32,128]{2,1,0:T(8,128)S(1)} collective-permute-done((f32[64,32,128]{2,1,0:T(8,128)S(1)}, f32[64,32,128]{2,1,0:T(8,128)S(1)}, u32[]{:S(2)}, u32[]{:S(2)}) %collective-permute-start.22) | collective-permute-done | bytes 1048608 | tf_op jit(solution)/shard_map/ppermute | solution.py:23
  (118 shorter events, 43.2 us)
Async XLA Ops:
  3.2 10.5 %collective-permute-start = (bf16[64,4,4,128]{3,0,2,1:T(8,128)(2,1)S(1)}, bf16[64,4,4,128]{3,0,2,1:T(8,128)(2,1)S(1)}, u32[]{:S(2)}, u32[]{:S(2)}) collective-permute-start(bf16[64,4,4,128]{3,0,2,1:T(8,128)(2,1)S(1)} %select_bitcast_fusion.1), channel_id=1, source_target_pairs={{0,4},{4,8},{8,12},{1,5},{5,9},{9,13},{2,6},{6,10},{10,14},{3,7},{... | collective-permute-start | bytes 786440 | tf_op jit(solution)/shard_map/ppermute | solution.py:13
  9.2 9.7 %collective-permute-start.1 = (bf16[64,4,4,128]{3,0,2,1:T(8,128)(2,1)S(1)}, bf16[64,4,4,128]{3,0,2,1:T(8,128)(2,1)S(1)}, u32[]{:S(2)}, u32[]{:S(2)}) collective-permute-start(bf16[64,4,4,128]{3,0,2,1:T(8,128)(2,1)S(1)} %select_bitcast_fusion), channel_id=1, source_target_pairs={{4,0},{8,4},{12,8},{5,1},{9,5},{13,9},{6,2},{10,6},{14,10},{7,3},{... | collective-permute-start | bytes 786440 | tf_op jit(solution)/shard_map/ppermute | solution.py:13
  20.1 2.0 %collective-permute-start.2 = (bf16[64,32,128]{2,1,0:T(8,128)(2,1)S(1)}, bf16[64,32,128]{2,1,0:T(8,128)(2,1)S(1)}, u32[]{:S(2)}, u32[]{:S(2)}) collective-permute-start(bf16[64,32,128]{2,1,0:T(8,128)(2,1)S(1)} %broadcast_select_fusion), channel_id=1, source_target_pairs={{0,1},{1,0},{2,3},{3,2},{4,5},{5,4},{6,7},{7,6},{8,9},{9,8},{10,11... | collective-permute-start | bytes 1572872 | tf_op jit(solution)/shard_map/ppermute | solution.py:23
  22.5 6.5 %collective-permute-start.3 = (bf16[32,15,128]{2,1,0:T(8,128)(2,1)S(1)}, bf16[32,15,128]{2,1,0:T(8,128)(2,1)S(1)}, u32[]{:S(2)}, u32[]{:S(2)}) collective-permute-start(bf16[32,15,128]{2,1,0:T(8,128)(2,1)S(1)} %get-tuple-element.52), channel_id=1, source_target_pairs={{0,4},{4,8},{8,12},{1,5},{5,9},{9,13},{2,6},{6,10},{10,14},{3,7},{... | collective-permute-start | bytes 368648 | tf_op jit(solution)/shard_map/ppermute | solution.py:31
  25.9 7.2 %collective-permute-start.4 = (bf16[32,15,128]{2,1,0:T(8,128)(2,1)S(1)}, bf16[32,15,128]{2,1,0:T(8,128)(2,1)S(1)}, u32[]{:S(2)}, u32[]{:S(2)}) collective-permute-start(bf16[32,15,128]{2,1,0:T(8,128)(2,1)S(1)} %get-tuple-element.53), channel_id=1, source_target_pairs={{4,0},{8,4},{12,8},{5,1},{9,5},{13,9},{6,2},{10,6},{14,10},{7,3},{... | collective-permute-start | bytes 368648 | tf_op jit(solution)/shard_map/ppermute | solution.py:34
  33.2 1.6 %collective-permute-start.5 = (bf16[32,30,128]{2,1,0:T(8,128)(2,1)S(1)}, bf16[32,30,128]{2,1,0:T(8,128)(2,1)S(1)}, u32[]{:S(2)}, u32[]{:S(2)}) collective-permute-start(bf16[32,30,128]{2,1,0:T(8,128)(2,1)S(1)} %pad_maximum_fusion.5), channel_id=1, source_target_pairs={{0,1},{1,0},{2,3},{3,2},{4,5},{5,4},{6,7},{7,6},{8,9},{9,8},{10,11... | collective-permute-start | bytes 737288 | tf_op jit(solution)/shard_map/ppermute | solution.py:23
  35.7 6.3 %collective-permute-start.6 = (bf16[15,32,128]{2,1,0:T(8,128)(2,1)S(1)}, bf16[15,32,128]{2,1,0:T(8,128)(2,1)S(1)}, u32[]{:S(2)}, u32[]{:S(2)}) collective-permute-start(bf16[15,32,128]{2,1,0:T(8,128)(2,1)S(1)} %get-tuple-element.48), channel_id=1, source_target_pairs={{0,2},{1,3},{4,6},{5,7},{8,10},{9,11},{12,14},{13,15},{16,18},{17,... | collective-permute-start | bytes 368648 | tf_op jit(solution)/shard_map/ppermute | solution.py:13
  39.1 7.0 %collective-permute-start.7 = (bf16[15,32,128]{2,1,0:T(8,128)(2,1)S(1)}, bf16[15,32,128]{2,1,0:T(8,128)(2,1)S(1)}, u32[]{:S(2)}, u32[]{:S(2)}) collective-permute-start(bf16[15,32,128]{2,1,0:T(8,128)(2,1)S(1)} %get-tuple-element.49), channel_id=1, source_target_pairs={{2,0},{3,1},{6,4},{7,5},{10,8},{11,9},{14,12},{15,13},{18,16},{19,... | collective-permute-start | bytes 368648 | tf_op jit(solution)/shard_map/ppermute | solution.py:13
  47.4 8.2 %collective-permute-start.8 = (bf16[64,15,128]{2,1,0:T(8,128)(2,1)S(1)}, bf16[64,15,128]{2,1,0:T(8,128)(2,1)S(1)}, u32[]{:S(2)}, u32[]{:S(2)}) collective-permute-start(bf16[64,15,128]{2,1,0:T(8,128)(2,1)S(1)} %get-tuple-element.46), channel_id=1, source_target_pairs={{0,4},{4,8},{8,12},{1,5},{5,9},{9,13},{2,6},{6,10},{10,14},{3,7},{... | collective-permute-start | bytes 737288 | tf_op jit(solution)/shard_map/ppermute | solution.py:31
  50.9 8.9 %collective-permute-start.9 = (bf16[64,15,128]{2,1,0:T(8,128)(2,1)S(1)}, bf16[64,15,128]{2,1,0:T(8,128)(2,1)}, u32[]{:S(2)}, u32[]{:S(2)}) collective-permute-start(bf16[64,15,128]{2,1,0:T(8,128)(2,1)S(1)} %get-tuple-element.47), channel_id=1, source_target_pairs={{4,0},{8,4},{12,8},{5,1},{9,5},{13,9},{6,2},{10,6},{14,10},{7,3},{... | collective-permute-start | bytes 737288 | tf_op jit(solution)/shard_map/ppermute | solution.py:34
  61.4 3.7 %collective-permute-start.10 = (bf16[15,32,128]{2,1,0:T(8,128)(2,1)S(1)}, bf16[15,32,128]{2,1,0:T(8,128)(2,1)S(1)}, u32[]{:S(2)}, u32[]{:S(2)}) collective-permute-start(bf16[15,32,128]{2,1,0:T(8,128)(2,1)S(1)} %get-tuple-element.44), channel_id=1, source_target_pairs={{0,2},{1,3},{4,6},{5,7},{8,10},{9,11},{12,14},{13,15},{16,18},{17,... | collective-permute-start | bytes 368648 | tf_op jit(solution)/shard_map/ppermute | solution.py:13
  62.8 6.8 %collective-permute-start.11 = (bf16[15,32,128]{2,1,0:T(8,128)(2,1)S(1)}, bf16[15,32,128]{2,1,0:T(8,128)(2,1)S(1)}, u32[]{:S(2)}, u32[]{:S(2)}) collective-permute-start(bf16[15,32,128]{2,1,0:T(8,128)(2,1)S(1)} %get-tuple-element.45), channel_id=1, source_target_pairs={{2,0},{3,1},{6,4},{7,5},{10,8},{11,9},{14,12},{15,13},{18,16},{19,... | collective-permute-start | bytes 368648 | tf_op jit(solution)/shard_map/ppermute | solution.py:13
  70.7 2.7 %collective-permute-start.12 = (f32[64,32,128]{2,1,0:T(8,128)S(1)}, f32[64,32,128]{2,1,0:T(8,128)S(1)}, u32[]{:S(2)}, u32[]{:S(2)}) collective-permute-start(f32[64,32,128]{2,1,0:T(8,128)S(1)} %copy.21), channel_id=1, source_target_pairs={{0,1},{1,0},{2,3},{3,2},{4,5},{5,4},{6,7},{7,6},{8,9},{9,8},{10,11... | collective-permute-start | bytes 3145736 | tf_op jit(solution)/shard_map/ppermute | solution.py:23
  74.4 5.2 %collective-permute-start.13 = (bf16[32,15,128]{2,1,0:T(8,128)(2,1)S(1)}, bf16[32,15,128]{2,1,0:T(8,128)(2,1)S(1)}, u32[]{:S(2)}, u32[]{:S(2)}) collective-permute-start(bf16[32,15,128]{2,1,0:T(8,128)(2,1)S(1)} %get-tuple-element.42), channel_id=1, source_target_pairs={{0,4},{4,8},{8,12},{1,5},{5,9},{9,13},{2,6},{6,10},{10,14},{3,7},{... | collective-permute-start | bytes 368648 | tf_op jit(solution)/shard_map/ppermute | solution.py:31
  76.6 7.2 %collective-permute-start.14 = (bf16[32,15,128]{2,1,0:T(8,128)(2,1)S(1)}, bf16[32,15,128]{2,1,0:T(8,128)(2,1)S(1)}, u32[]{:S(2)}, u32[]{:S(2)}) collective-permute-start(bf16[32,15,128]{2,1,0:T(8,128)(2,1)S(1)} %get-tuple-element.43), channel_id=1, source_target_pairs={{4,0},{8,4},{12,8},{5,1},{9,5},{13,9},{6,2},{10,6},{14,10},{7,3},{... | collective-permute-start | bytes 368648 | tf_op jit(solution)/shard_map/ppermute | solution.py:34
  83.8 1.6 %collective-permute-start.15 = (bf16[32,30,128]{2,1,0:T(8,128)(2,1)S(1)}, bf16[32,30,128]{2,1,0:T(8,128)(2,1)S(1)}, u32[]{:S(2)}, u32[]{:S(2)}) collective-permute-start(bf16[32,30,128]{2,1,0:T(8,128)(2,1)S(1)} %pad_maximum_fusion.6), channel_id=1, source_target_pairs={{0,1},{1,0},{2,3},{3,2},{4,5},{5,4},{6,7},{7,6},{8,9},{9,8},{10,11... | collective-permute-start | bytes 737288 | tf_op jit(solution)/shard_map/ppermute | solution.py:23
  88.0 4.4 %collective-permute-start.16 = (bf16[15,32,128]{2,1,0:T(8,128)(2,1)S(1)}, bf16[15,32,128]{2,1,0:T(8,128)(2,1)S(1)}, u32[]{:S(2)}, u32[]{:S(2)}) collective-permute-start(bf16[15,32,128]{2,1,0:T(8,128)(2,1)S(1)} %get-tuple-element.38), channel_id=1, source_target_pairs={{0,2},{1,3},{4,6},{5,7},{8,10},{9,11},{12,14},{13,15},{16,18},{17,... | collective-permute-start | bytes 368648 | tf_op jit(solution)/shard_map/ppermute | solution.py:13
  89.5 7.1 %collective-permute-start.17 = (bf16[15,32,128]{2,1,0:T(8,128)(2,1)S(1)}, bf16[15,32,128]{2,1,0:T(8,128)(2,1)S(1)}, u32[]{:S(2)}, u32[]{:S(2)}) collective-permute-start(bf16[15,32,128]{2,1,0:T(8,128)(2,1)S(1)} %get-tuple-element.39), channel_id=1, source_target_pairs={{2,0},{3,1},{6,4},{7,5},{10,8},{11,9},{14,12},{15,13},{18,16},{19,... | collective-permute-start | bytes 368648 | tf_op jit(solution)/shard_map/ppermute | solution.py:13
  97.8 11.4 %copy-start.1 = (bf16[64,32,62]{2,1,0:T(8,128)(2,1)S(1)}, bf16[64,32,62]{2,1,0:T(8,128)(2,1)}, u32[]{:S(2)}) copy-start(bf16[64,32,62]{2,1,0:T(8,128)(2,1)} %copy-done) | copy-start | bytes 761860
  97.9 7.1 %collective-permute-start.18 = (bf16[64,15,128]{2,1,0:T(8,128)(2,1)S(1)}, bf16[64,15,128]{2,1,0:T(8,128)(2,1)S(1)}, u32[]{:S(2)}, u32[]{:S(2)}) collective-permute-start(bf16[64,15,128]{2,1,0:T(8,128)(2,1)S(1)} %get-tuple-element.36), channel_id=1, source_target_pairs={{0,4},{4,8},{8,12},{1,5},{5,9},{9,13},{2,6},{6,10},{10,14},{3,7},{... | collective-permute-start | bytes 737288 | tf_op jit(solution)/shard_map/ppermute | solution.py:31
  100.2 8.9 %collective-permute-start.19 = (bf16[64,15,128]{2,1,0:T(8,128)(2,1)S(1)}, bf16[64,15,128]{2,1,0:T(8,128)(2,1)S(1)}, u32[]{:S(2)}, u32[]{:S(2)}) collective-permute-start(bf16[64,15,128]{2,1,0:T(8,128)(2,1)S(1)} %get-tuple-element.37), channel_id=1, source_target_pairs={{4,0},{8,4},{12,8},{5,1},{9,5},{13,9},{6,2},{10,6},{14,10},{7,3},{... | collective-permute-start | bytes 737288 | tf_op jit(solution)/shard_map/ppermute | solution.py:34
  109.7 3.9 %collective-permute-start.20 = (bf16[15,32,128]{2,1,0:T(8,128)(2,1)S(1)}, bf16[15,32,128]{2,1,0:T(8,128)(2,1)S(1)}, u32[]{:S(2)}, u32[]{:S(2)}) collective-permute-start(bf16[15,32,128]{2,1,0:T(8,128)(2,1)S(1)} %get-tuple-element.34), channel_id=1, source_target_pairs={{0,2},{1,3},{4,6},{5,7},{8,10},{9,11},{12,14},{13,15},{16,18},{17,... | collective-permute-start | bytes 368648 | tf_op jit(solution)/shard_map/ppermute | solution.py:13
  111.2 6.8 %collective-permute-start.21 = (bf16[15,32,128]{2,1,0:T(8,128)(2,1)S(1)}, bf16[15,32,128]{2,1,0:T(8,128)(2,1)S(1)}, u32[]{:S(2)}, u32[]{:S(2)}) collective-permute-start(bf16[15,32,128]{2,1,0:T(8,128)(2,1)S(1)} %get-tuple-element.35), channel_id=1, source_target_pairs={{2,0},{3,1},{6,4},{7,5},{10,8},{11,9},{14,12},{15,13},{18,16},{19,... | collective-permute-start | bytes 368648 | tf_op jit(solution)/shard_map/ppermute | solution.py:13
  119.2 2.7 %collective-permute-start.22 = (f32[64,32,128]{2,1,0:T(8,128)S(1)}, f32[64,32,128]{2,1,0:T(8,128)S(1)}, u32[]{:S(2)}, u32[]{:S(2)}) collective-permute-start(f32[64,32,128]{2,1,0:T(8,128)S(1)} %copy.26), channel_id=1, source_target_pairs={{0,1},{1,0},{2,3},{3,2},{4,5},{5,4},{6,7},{7,6},{8,9},{9,8},{10,11... | collective-permute-start | bytes 3145736 | tf_op jit(solution)/shard_map/ppermute | solution.py:23
  (3 other events, 26.0 us)

commit v3 on v2

v3 whole, which is shorter than its diff:
```python
import jax
import jax.numpy as jnp
from jax import lax
from jax.sharding import PartitionSpec as P

BX = 4
ITERS = 2


def shifted(block, axis, distance):
    devices = range(lax.axis_size(axis))
    route = [(i - distance, i) for i in devices if i - distance in devices]
    return lax.ppermute(block, axis, route)


def from_partner(block, axis, distance):
    count = lax.axis_size(axis)
    route = []
    for low in range(count):
        high = low | 1 << distance
        if high != low and high < count:
            route += [(low, high), (high, low)]
    return lax.ppermute(block, axis, route)


def band_matrix(kernel, row_count, col_count, base_shift):
    row_ids = lax.broadcasted_iota(jnp.int32, (row_count, col_count, 1), 0)
    col_ids = lax.broadcasted_iota(jnp.int32, (row_count, col_count, 1), 1)
    tap_ids = lax.broadcasted_iota(jnp.int32, (1, 1, kernel.shape[0]), 2)
    hit = row_ids - col_ids + base_shift == tap_ids
    taps = kernel.astype(jnp.float32)[None, None, :]
    matrix = jnp.sum(jnp.where(hit, taps, jnp.float32(0.0)), axis=2)
    return matrix.astype(jnp.bfloat16)


def operators(kernels, x_planes, z_out, x_in, x_out, width_y):
    reach = kernels.shape[1] // 2
    along_x = band_matrix(kernels[0], x_in, x_out, 0).T
    along_x = jnp.broadcast_to(along_x[None], (x_planes,) + along_x.shape)
    return lax.optimization_barrier((
        along_x,
        band_matrix(kernels[1], width_y, width_y, reach),
        band_matrix(kernels[2], z_out + 2 * reach, z_out, 0).T,
    ))


def pass_xy(extended, matrices):
    width_y = extended.shape[2]
    after_x = jnp.einsum(
        "zpa,zay->zpy", matrices[0], extended, preferred_element_type=jnp.float32
    ).astype(jnp.bfloat16)
    after_y = jnp.dot(after_x.reshape(-1, width_y), matrices[1], preferred_element_type=jnp.float32)
    return after_y.reshape(after_x.shape).astype(jnp.bfloat16)


def pass_z(extended, matrix):
    planes = extended.shape[0]
    out = jnp.dot(matrix, extended.reshape(planes, -1), preferred_element_type=jnp.float32)
    return out.reshape((matrix.shape[0],) + extended.shape[1:])


def rims(block, axis, dim, width, distance):
    size = block.shape[dim]
    low = shifted(lax.slice_in_dim(block, size - width, size, axis=dim), axis, distance)
    high = shifted(lax.slice_in_dim(block, 0, width, axis=dim), axis, -distance)
    return low, high


def local(acquired, psf_taps, block_source):
    planes, width_x, width_y = acquired.shape
    block_count = width_x // BX
    capacity = block_count // 2
    reach = psf_taps.shape[2] // 2
    wide = 2 * reach
    tile_index = lax.axis_index("tile")
    tile_total = lax.axis_size("tile")
    view_index = lax.axis_index("view")
    view_total = lax.axis_size("view")
    view_bit = view_index % 2
    sources = block_source[0]
    blocks = acquired.reshape(planes, block_count, BX, width_y)
    wanted_here = lax.dynamic_slice_in_dim(sources, tile_index * block_count, block_count)
    source_tiles = wanted_here // block_count
    source_blocks = wanted_here % block_count
    parcels = []
    for offset in (1, -1):
        target = jnp.clip(tile_index + offset, 0, tile_total - 1)
        wanted = lax.dynamic_slice_in_dim(sources, target * block_count, block_count)
        matches = wanted // block_count == tile_index
        ranks = jnp.cumsum(matches.astype(jnp.int32)) - 1
        slot_ids = jnp.arange(capacity, dtype=jnp.int32)
        selected = jnp.where(
            matches[None, :] & (ranks[None, :] == slot_ids[:, None]),
            wanted[None, :] % block_count,
            0,
        )
        picked = jnp.sum(selected, axis=1)
        parcel = jnp.take(blocks, picked, axis=1)
        parcels.append(shifted(parcel, "tile", offset))
    candidates = jnp.concatenate([blocks, parcels[0], parcels[1]], axis=1)
    from_left = source_tiles == tile_index - 1
    from_right = source_tiles == tile_index + 1
    left_order = jnp.cumsum(from_left.astype(jnp.int32)) - 1
    right_order = jnp.cumsum(from_right.astype(jnp.int32)) - 1
    chosen = jnp.where(
        from_left,
        block_count + left_order,
        jnp.where(from_right, block_count + capacity + right_order, source_blocks),
    )
    measured = jnp.take(candidates, chosen, axis=1).reshape(planes, width_x, width_y)
    partner_view = from_partner(measured, "view", 0)
    measured_own = measured.astype(jnp.float32)
    estimate = 0.5 * (measured_own + partner_view.astype(jnp.float32))
    kernels = (psf_taps / jnp.sum(psf_taps, axis=2, keepdims=True)).astype(jnp.bfloat16)
    own_kernels = lax.dynamic_index_in_dim(kernels, view_bit, 0, keepdims=False)
    forward_ops = operators(
        own_kernels, planes, planes + wide, width_x + 2 * wide, width_x + wide, width_y
    )
    adjoint_ops = operators(
        own_kernels[:, ::-1], planes + wide, planes, width_x + wide, width_x, width_y
    )
    x_ids = tile_index * width_x + jnp.arange(-reach, width_x + reach)
    z_ids = (view_index // 2) * planes + jnp.arange(-reach, planes + reach)
    inside = (
        ((z_ids >= 0) & (z_ids < (view_total // 2) * planes))[:, None, None]
        & ((x_ids >= 0) & (x_ids < tile_total * width_x))[None, :, None]
    )
    measured_wide = None
    half_rows = planes // 2
    for iteration in range(ITERS):
        estimate_low = estimate.astype(jnp.bfloat16)
        if measured_wide is None:
            low, high = rims(jnp.stack([estimate_low, measured]), "tile", 2, wide, 1)
            est_x = jnp.concatenate([low[0], estimate_low, high[0]], axis=1)
            meas_x = jnp.concatenate([low[1][:, reach:], measured, high[1][:, :reach]], axis=1)
        else:
            low, high = rims(estimate_low, "tile", 1, wide, 1)
            est_x = jnp.concatenate([low, estimate_low, high], axis=1)
        after_xy = pass_xy(est_x, forward_ops)
        if measured_wide is None:
            below, above = rims(jnp.stack([after_xy, meas_x]), "view", 1, wide, 2)
            ext_z = jnp.concatenate([below[0], after_xy, above[0]], axis=0)
            measured_wide = jnp.concatenate(
                [below[1][reach:], meas_x, above[1][:reach]], axis=0
            ).astype(jnp.float32)
        else:
            below, above = rims(after_xy, "view", 0, wide, 2)
            ext_z = jnp.concatenate([below, after_xy, above], axis=0)
        blurred = pass_z(ext_z, forward_ops[2])
        quotient = jnp.where(inside, measured_wide / blurred, jnp.float32(0.0)).astype(jnp.bfloat16)
        back_own = pass_z(pass_xy(quotient, adjoint_ops), adjoint_ops[2])
        back_partner = from_partner(back_own, "view", 0)
        estimate = estimate * (0.5 * (back_own + back_partner))
    return lax.dynamic_slice_in_dim(estimate, view_bit * half_rows, half_rows, 0)


def solution(mesh):
    in_specs = (P(("timepoin", "view"), "tile", None), P(), P(("timepoin", "view"), None))
    out_specs = P(("timepoin", "view"), "tile", None)
    return jax.shard_map(local, mesh=mesh, in_specs=in_specs, out_specs=out_specs, check_vma=False)
```

time: 123 us -> 172 us (1.40)
  local copies, waits for them, and re-layouts: 6.95 us -> 36.3 us
  matrix products: 5.85 us -> 20.6 us
  other arithmetic: 7.93 us -> 16.3 us
  starting transfers between devices: 36.1 us -> 30.4 us
    ppermute x10, waiting for transfers between devices: 29 us -> 60.3 us  [shifted(): return lax.ppermute(block, axis, route)]
    ppermute x8 -> x0, waiting for transfers between devices: 26.6 us -> none  [the longest x4 16.6 us: extended_2(): lax.ppermute(lax.slice_in_dim(block, 0, width, axis=dim), axis, backward)]
    ppermute x8 -> x0, starting transfers between devices: 16.7 us -> none  [the longest x4 11.5 us: extended_2(): lax.ppermute(lax.slice_in_dim(block, block.shape[dim] - width, None, axis...]
    dot_general x8 -> x9, matrix products: 5.85 us -> 20.6 us  [the longest x4 14.4 us: pass_xy(): jnp.dot(after_x.reshape(-1, width_y), matrices[1], preferred_element_type...]
    slice x11 -> x15, local copies, waits for them, and re-layouts: 1.42 us -> 15 us  [the longest x2 5.11 us: local(): ext_z = jnp.concatenate([below[0], after_xy, above[0]], axis=0)]
    ppermute x10, starting transfers between devices: 19.1 us -> 30.2 us  [shifted(): return lax.ppermute(block, axis, route)]
    unnamed x9 -> x44, local copies, waits for them, and re-layouts: 1.27 us -> 7.43 us
    concatenate x0 -> x1, local copies, waits for them, and re-layouts: none -> 3.19 us  [local(): ext_z = jnp.concatenate([below, after_xy, above], axis=0)]
  transfers between devices with their start and end apart: 23 -> 13, of which waited for: 23 -> 12; matrix products, arithmetic and copies ran while one was open for 3% -> 12% of each run, Pallas kernels for 0% -> 0%
where the time goes in v3:
time: 172 us; the launch traced here: 171 us
  waiting for transfers between devices  67 us (39%)
  local copies, waits for them, and re-layouts  36.3 us (21%)
  starting transfers between devices  30.4 us (18%)
  matrix products  20.6 us (12%)
  other arithmetic  16.3 us (9%)
    ppermute x10, waiting for transfers between devices, shifted(): return lax.ppermute(block, axis, route)  60.3 us
    ppermute x10, starting transfers between devices, shifted(): return lax.ppermute(block, axis, route)  30.2 us
    dot_general x4, matrix products, pass_xy(): jnp.dot(after_x.reshape(-1, width_y), matrices[1], preferred_element_type...  14.4 us
    unnamed x44, local copies, waits for them, and re-layouts  7.43 us
    ppermute x3, waiting for transfers between devices, from_partner(): return lax.ppermute(block, axis, route)  6.73 us
    dot_general x4, matrix products, pass_z(): jnp.dot(matrix, extended.reshape(planes, -1), preferred_element_type=jnp....  5.65 us
    slice x2, local copies, waits for them, and re-layouts, local(): ext_z = jnp.concatenate([below[0], after_xy, above[0]], axis=0)  5.11 us
    dot_general x5, local copies, waits for them, and re-layouts, pass_z(): jnp.dot(matrix, extended.reshape(planes, -1), preferred_element_type=jnp....  4.51 us
  transfers between devices with their start and end apart: 13, of which 12 were waited for; matrix products, arithmetic and copies ran while one was open for 12% of the time, Pallas kernels for 0%

profile of v3, /device:TPU:0, one launch (start us, length us, event | category | flops | bytes accessed | tf_op | source)
XLA Modules:
  0.0 171.2 jit_solution(6974676822797289147)
XLA Ops:
  3.2 4.9 %collective-permute-start = (bf16[64,4,4,128]{3,0,2,1:T(8,128)(2,1)S(1)}, bf16[64,4,4,128]{3,0,2,1:T(8,128)(2,1)S(1)}, u32[]{:S(2)}, u32[]{:S(2)}) collective-permute-start(bf16[64,4,4,128]{3,0,2,1:T(8,128)(2,1)S(1)} %select_bitcast_fusion.1), channel_id=1, source_target_pairs={{0,4},{4,8},{8,12},{1,5},{5,9},{9,13},{2,6},{6,10},{10,14},{3,7},{... | collective-permute-start | bytes 786440 | tf_op jit(solution)/shard_map/ppermute | solution.py:13
  13.6 5.2 %collective-permute-done.1 = bf16[64,4,4,128]{3,0,2,1:T(8,128)(2,1)S(1)} collective-permute-done((bf16[64,4,4,128]{3,0,2,1:T(8,128)(2,1)S(1)}, bf16[64,4,4,128]{3,0,2,1:T(8,128)(2,1)S(1)}, u32[]{:S(2)}, u32[]{:S(2)}) %collective-permute-start.1) | collective-permute-done | bytes 262176 | tf_op jit(solution)/shard_map/ppermute | solution.py:13
  26.0 5.5 %collective-permute-start.3 = (bf16[2,64,30,128]{3,1,2,0:T(8,128)(2,1)}, bf16[2,64,30,128]{3,1,2,0:T(8,128)(2,1)}, u32[]{:S(2)}, u32[]{:S(2)}) collective-permute-start(bf16[2,64,30,128]{3,1,2,0:T(8,128)(2,1)} %copy.66), channel_id=1, source_target_pairs={{0,4},{4,8},{8,12},{1,5},{5,9},{9,13},{2,6},{6,10},{10,14},{3,7},{... | collective-permute-start | bytes 2949128 | tf_op jit(solution)/shard_map/ppermute | solution.py:13
  34.8 14.4 %collective-permute-done.4 = bf16[2,64,30,128]{3,1,2,0:T(8,128)(2,1)} collective-permute-done((bf16[2,64,30,128]{3,1,2,0:T(8,128)(2,1)S(1)}, bf16[2,64,30,128]{3,1,2,0:T(8,128)(2,1)}, u32[]{:S(2)}, u32[]{:S(2)}) %collective-permute-start.4) | collective-permute-done | bytes 983072 | tf_op jit(solution)/shard_map/ppermute | solution.py:13
  55.5 2.4 %convolution_convert_fusion = bf16[64,62,128]{2,1,0:T(8,128)(2,1)S(1)} fusion(bf16[64,62,92]{2,1,0:T(8,128)(2,1)} %broadcast_in_dim.196, bf16[64,30,128]{2,1,0:T(8,128)(2,1)} %bitcast.206, bf16[64,32,128]{2,1,0:T(8,128)(2,1)S(1)} %fusion.51, bf16[64,30,128]{2,1,0:T(8,128)(2,1)} %bitcast.207, bf16[128,128]{1,0:T(8,128)(2,1)S(1)} %get-tuple-element.15), kind=kOutput, calls=%fused_computation.37 | convolution fusion | flops 229015552 | bytes 3286016 | tf_op jit(solution)/shard_map/dot_general | solution.py:52
  65.6 4.8 %collective-permute-start.5 = (bf16[2,30,62,128]{3,0,2,1:T(2,128)(2,1)}, bf16[2,30,62,128]{3,0,2,1:T(2,128)(2,1)S(1)}, u32[]{:S(2)}, u32[]{:S(2)}) collective-permute-start(bf16[2,30,62,128]{3,0,2,1:T(2,128)(2,1)} %copy.74), channel_id=1, source_target_pairs={{0,2},{1,3},{4,6},{5,7},{8,10},{9,11},{12,14},{13,15},{16,18},{17,... | collective-permute-start | bytes 2856968 | tf_op jit(solution)/shard_map/ppermute | solution.py:13
  73.7 11.6 %collective-permute-done.6 = bf16[2,30,62,128]{3,0,2,1:T(2,128)(2,1)S(1)} collective-permute-done((bf16[2,30,62,128]{3,0,2,1:T(2,128)(2,1)}, bf16[2,30,62,128]{3,0,2,1:T(2,128)(2,1)S(1)}, u32[]{:S(2)}, u32[]{:S(2)}) %collective-permute-start.6) | collective-permute-done | bytes 952352 | tf_op jit(solution)/shard_map/ppermute | solution.py:13
  86.6 2.6 %slice_reduce_fusion = bf16[30,62,128]{2,1,0:T(8,128)(2,1)S(1)} fusion(bf16[2,30,62,128]{3,0,2,1:T(2,128)(2,1)S(1)} %collective-permute-done.6), kind=kLoop, calls=%fused_computation.59 | loop fusion | bytes 952320 | tf_op jit(solution)/shard_map/slice | solution.py:142
  91.3 2.6 %slice_reduce_fusion.1 = bf16[30,62,128]{2,1,0:T(8,128)(2,1)S(1)} fusion(bf16[2,30,62,128]{3,0,2,1:T(2,128)(2,1)S(1)} %collective-permute-done.5), kind=kLoop, calls=%fused_computation.60 | loop fusion | bytes 952320 | tf_op jit(solution)/shard_map/slice | solution.py:142
  96.0 3.2 %copy.78 = bf16[7936,124]{1,0:T(8,128)(2,1)S(1)} copy(bf16[7936,124]{0,1:T(8,128)(2,1)} %maximum_bitcast_fusion) | data formatting | bytes 3936256 | tf_op jit(solution)/shard_map/dot_general | solution.py:58
  99.2 2.4 %fusion.62 = f32[94,62,128]{2,0,1:T(8,128)} fusion(bf16[62,128,124]{2,1,0:T(8,128)(2,1)S(1)} %bitcast.191, bf16[94,124]{1,0:T(8,128)(2,1)S(1)} %bitcast.212), kind=kOutput, calls=%fused_computation.92 | convolution fusion | flops 185004032 | bytes 4975376 | tf_op jit(solution)/shard_map/dot_general | solution.py:58
  101.6 6.0 %fusion.36 = bf16[94,32,128]{2,1,0:T(8,128)(2,1)S(1)} fusion(bf16[94,32,62]{2,1,0:T(8,128)(2,1)} %broadcast_in_dim.186, f32[94,62,128]{2,0,1:T(8,128)} %fusion.62, pred[94,62]{1,0:T(8,128)(4,1)S(1)} %copy-done.13, bf16[128,128]{1,0:T(8,128)(2,1)S(1)} %copy-done.11, bf16[15,62,128]{2,1,0:T(8,128)(2,1)} %bitcast.208, bf16[64,15,128]{2,1,0:T(8,128)(2,1)S(1)} %copy-done.7, ...), kind=kOutput, calls=%fused_computation.41 | convolution fusion | flops 156776960 | bytes 5657540 | tf_op jit(solution)/shard_map/dot_general | solution.py:52
  108.8 2.6 %collective-permute-done.7 = f32[64,32,128]{2,1,0:T(8,128)S(1)} collective-permute-done((f32[64,32,128]{2,1,0:T(8,128)S(1)}, f32[64,32,128]{2,1,0:T(8,128)S(1)}, u32[]{:S(2)}, u32[]{:S(2)}) %collective-permute-start.7) | collective-permute-done | bytes 1048608 | tf_op jit(solution)/shard_map/ppermute | solution.py:23
  112.6 4.1 %collective-permute-start.8 = (bf16[64,30,128]{2,1,0:T(8,128)(2,1)S(1)}, bf16[64,30,128]{2,1,0:T(8,128)(2,1)S(1)}, u32[]{:S(2)}, u32[]{:S(2)}) collective-permute-start(bf16[64,30,128]{2,1,0:T(8,128)(2,1)S(1)} %get-tuple-element.40), channel_id=1, source_target_pairs={{0,4},{4,8},{8,12},{1,5},{5,9},{9,13},{2,6},{6,10},{10,14},{3,7},{... | collective-permute-start | bytes 1474568 | tf_op jit(solution)/shard_map/ppermute | solution.py:13
  118.0 10.1 %collective-permute-done.8 = bf16[64,30,128]{2,1,0:T(8,128)(2,1)S(1)} collective-permute-done((bf16[64,30,128]{2,1,0:T(8,128)(2,1)S(1)}, bf16[64,30,128]{2,1,0:T(8,128)(2,1)S(1)}, u32[]{:S(2)}, u32[]{:S(2)}) %collective-permute-start.8) | collective-permute-done | bytes 491552 | tf_op jit(solution)/shard_map/ppermute | solution.py:13
  128.1 4.2 %collective-permute-done.9 = bf16[64,30,128]{2,1,0:T(8,128)(2,1)S(1)} collective-permute-done((bf16[64,30,128]{2,1,0:T(8,128)(2,1)S(1)}, bf16[64,30,128]{2,1,0:T(8,128)(2,1)S(1)}, u32[]{:S(2)}, u32[]{:S(2)}) %collective-permute-start.9) | collective-permute-done | bytes 491552 | tf_op jit(solution)/shard_map/ppermute | solution.py:13
  133.9 4.3 %collective-permute-start.10 = (bf16[30,62,128]{2,0,1:T(8,128)(2,1)S(1)}, bf16[30,62,128]{2,0,1:T(8,128)(2,1)S(1)}, u32[]{:S(2)}, u32[]{:S(2)}) collective-permute-start(bf16[30,62,128]{2,0,1:T(8,128)(2,1)S(1)} %get-tuple-element.34), channel_id=1, source_target_pairs={{0,2},{1,3},{4,6},{5,7},{8,10},{9,11},{12,14},{13,15},{16,18},{17,... | collective-permute-start | bytes 1428488 | tf_op jit(solution)/shard_map/ppermute | solution.py:13
  139.5 8.6 %collective-permute-done.10 = bf16[30,62,128]{2,0,1:T(8,128)(2,1)S(1)} collective-permute-done((bf16[30,62,128]{2,0,1:T(8,128)(2,1)S(1)}, bf16[30,62,128]{2,0,1:T(8,128)(2,1)S(1)}, u32[]{:S(2)}, u32[]{:S(2)}) %collective-permute-start.10) | collective-permute-done | bytes 476192 | tf_op jit(solution)/shard_map/ppermute | solution.py:13
  148.1 4.1 %collective-permute-done.11 = bf16[30,62,128]{2,0,1:T(8,128)(2,1)S(1)} collective-permute-done((bf16[30,62,128]{2,0,1:T(8,128)(2,1)S(1)}, bf16[30,62,128]{2,0,1:T(8,128)(2,1)S(1)}, u32[]{:S(2)}, u32[]{:S(2)}) %collective-permute-start.11) | collective-permute-done | bytes 476192 | tf_op jit(solution)/shard_map/ppermute | solution.py:13
  152.3 2.1 %pad_maximum_fusion = bf16[124,62,128]{2,0,1:T(8,128)(2,1)} fusion(bf16[30,62,128]{2,0,1:T(8,128)(2,1)S(1)} %collective-permute-done.11, bf16[64,62,128]{2,0,1:T(8,128)(2,1)S(1)} %convolution_convert_fusion.1, bf16[30,62,128]{2,0,1:T(8,128)(2,1)S(1)} %collective-permute-done.10), kind=kLoop, calls=%fused_computation.10 | loop fusion | flops 5904384 | bytes 3936256 | tf_op jit(solution)/shard_map/concatenate | solution.py:148
  154.3 3.2 %copy.84 = bf16[124,62,128]{0,2,1:T(8,128)(2,1)S(1)} copy(bf16[124,62,128]{2,0,1:T(8,128)(2,1)} %pad_maximum_fusion) | data formatting | bytes 3936256 | tf_op jit(solution)/shard_map/concatenate | solution.py:148
  157.5 2.4 %fusion.4 = f32[94,62,128]{2,0,1:T(8,128)} fusion(bf16[124,62,128]{0,2,1:T(8,128)(2,1)S(1)} %copy.84, bf16[94,124]{1,0:T(8,128)(2,1)S(1)} %bitcast.213), kind=kOutput, calls=%fused_computation.11 | convolution fusion | flops 185004032 | bytes 4975376 | tf_op jit(solution)/shard_map/dot_general | solution.py:58
  159.9 5.4 %fusion.45 = bf16[94,32,128]{2,1,0:T(8,128)(2,1)S(1)} fusion(bf16[94,32,62]{2,1,0:T(8,128)(2,1)} %broadcast_in_dim.186, f32[94,62,128]{2,0,1:T(8,128)} %fusion.4, pred[94,62]{1,0:T(8,128)(4,1)S(1)} %copy-done.13, bf16[128,128]{1,0:T(8,128)(2,1)S(1)} %copy-done.11, bf16[15,62,128]{2,1,0:T(8,128)(2,1)} %bitcast.209, bf16[64,15,128]{2,1,0:T(8,128)(2,1)S(1)} %copy-done.7, ...), kind=kOutput, calls=%fused_computation.44 | convolution fusion | flops 156776960 | bytes 5657540 | tf_op jit(solution)/shard_map/dot_general | solution.py:52
  166.5 2.8 %collective-permute-done.12 = f32[64,32,128]{2,1,0:T(8,128)} collective-permute-done((f32[64,32,128]{2,1,0:T(8,128)S(1)}, f32[64,32,128]{2,1,0:T(8,128)}, u32[]{:S(2)}, u32[]{:S(2)}) %collective-permute-start.12) | collective-permute-done | bytes 1048608 | tf_op jit(solution)/shard_map/ppermute | solution.py:23
  (141 shorter events, 51.2 us)
Async XLA Ops:
  0.0 10.5 %copy-start.12 = (s32[1,32]{1,0:T(1,128)S(1)}, s32[1,32]{1,0:T(1,128)}, u32[]{:S(2)}) copy-start(s32[1,32]{1,0:T(1,128)} %param.7) | copy-start | bytes 388
  0.0 11.1 %copy-start.14 = (f32[2,3,31]{2,0,1:T(2,128)S(1)}, f32[2,3,31]{2,0,1:T(2,128)}, u32[]{:S(2)}) copy-start(f32[2,3,31]{2,0,1:T(2,128)} %param.6) | copy-start | bytes 2236
  3.2 10.5 %collective-permute-start = (bf16[64,4,4,128]{3,0,2,1:T(8,128)(2,1)S(1)}, bf16[64,4,4,128]{3,0,2,1:T(8,128)(2,1)S(1)}, u32[]{:S(2)}, u32[]{:S(2)}) collective-permute-start(bf16[64,4,4,128]{3,0,2,1:T(8,128)(2,1)S(1)} %select_bitcast_fusion.1), channel_id=1, source_target_pairs={{0,4},{4,8},{8,12},{1,5},{5,9},{9,13},{2,6},{6,10},{10,14},{3,7},{... | collective-permute-start | bytes 786440 | tf_op jit(solution)/shard_map/ppermute | solution.py:13
  9.2 9.7 %collective-permute-start.1 = (bf16[64,4,4,128]{3,0,2,1:T(8,128)(2,1)S(1)}, bf16[64,4,4,128]{3,0,2,1:T(8,128)(2,1)S(1)}, u32[]{:S(2)}, u32[]{:S(2)}) collective-permute-start(bf16[64,4,4,128]{3,0,2,1:T(8,128)(2,1)S(1)} %select_bitcast_fusion), channel_id=1, source_target_pairs={{4,0},{8,4},{12,8},{5,1},{9,5},{13,9},{6,2},{10,6},{14,10},{7,3},{... | collective-permute-start | bytes 786440 | tf_op jit(solution)/shard_map/ppermute | solution.py:13
  20.1 34.6 %copy-start.3 = (bf16[64,32,128]{2,1,0:T(8,128)(2,1)}, bf16[64,32,128]{2,1,0:T(8,128)(2,1)S(1)}, u32[]{:S(2)}) copy-start(bf16[64,32,128]{2,1,0:T(8,128)(2,1)S(1)} %broadcast_select_fusion.1) | copy-start | bytes 1572868
  20.1 2.0 %collective-permute-start.2 = (bf16[64,32,128]{2,1,0:T(8,128)(2,1)S(1)}, bf16[64,32,128]{2,1,0:T(8,128)(2,1)S(1)}, u32[]{:S(2)}, u32[]{:S(2)}) collective-permute-start(bf16[64,32,128]{2,1,0:T(8,128)(2,1)S(1)} %broadcast_select_fusion.1), channel_id=1, source_target_pairs={{0,1},{1,0},{2,3},{3,2},{4,5},{5,4},{6,7},{7,6},{8,9},{9,8},{10,11... | collective-permute-start | bytes 1572872 | tf_op jit(solution)/shard_map/ppermute | solution.py:23
  23.3 25.8 %collective-permute-start.4 = (bf16[2,64,30,128]{3,1,2,0:T(8,128)(2,1)S(1)}, bf16[2,64,30,128]{3,1,2,0:T(8,128)(2,1)}, u32[]{:S(2)}, u32[]{:S(2)}) collective-permute-start(bf16[2,64,30,128]{3,1,2,0:T(8,128)(2,1)S(1)} %copy.68), channel_id=1, source_target_pairs={{4,0},{8,4},{12,8},{5,1},{9,5},{13,9},{6,2},{10,6},{14,10},{7,3},{... | collective-permute-start | bytes 2949128 | tf_op jit(solution)/shard_map/ppermute | solution.py:13
  26.0 25.9 %collective-permute-start.3 = (bf16[2,64,30,128]{3,1,2,0:T(8,128)(2,1)}, bf16[2,64,30,128]{3,1,2,0:T(8,128)(2,1)}, u32[]{:S(2)}, u32[]{:S(2)}) collective-permute-start(bf16[2,64,30,128]{3,1,2,0:T(8,128)(2,1)} %copy.66), channel_id=1, source_target_pairs={{0,4},{4,8},{8,12},{1,5},{5,9},{9,13},{2,6},{6,10},{10,14},{3,7},{... | collective-permute-start | bytes 2949128 | tf_op jit(solution)/shard_map/ppermute | solution.py:13
  33.0 22.5 %copy-start.9 = (bf16[128,128]{1,0:T(8,128)(2,1)}, bf16[128,128]{1,0:T(8,128)(2,1)S(1)}, u32[]{:S(2)}) copy-start(bf16[128,128]{1,0:T(8,128)(2,1)S(1)} %get-tuple-element.15) | copy-start | bytes 98308
  51.9 2.9 %copy-start.6 = (bf16[64,15,128]{2,1,0:T(8,128)(2,1)}, bf16[64,15,128]{2,1,0:T(8,128)(2,1)S(1)}, u32[]{:S(2)}) copy-start(bf16[64,15,128]{2,1,0:T(8,128)(2,1)S(1)} %slice.142) | copy-start | bytes 737284
  57.8 4.4 %copy-start.15 = (f32[31]{0:T(128)S(1)}, f32[31]{0:T(128)}, u32[]{:S(2)}) copy-start(f32[31]{0:T(128)} %bitcast_convert_fusion.5) | copy-start | bytes 376
  59.0 4.7 %copy-start = (bf16[2,30,62,128]{3,2,1,0:T(8,128)(2,1)S(1)}, bf16[2,30,62,128]{3,2,1,0:T(8,128)(2,1)}, u32[]{:S(2)}) copy-start(bf16[2,30,62,128]{3,2,1,0:T(8,128)(2,1)} %get-tuple-element.30) | copy-start | bytes 2856964
  60.9 24.4 %collective-permute-start.6 = (bf16[2,30,62,128]{3,0,2,1:T(2,128)(2,1)}, bf16[2,30,62,128]{3,0,2,1:T(2,128)(2,1)S(1)}, u32[]{:S(2)}, u32[]{:S(2)}) collective-permute-start(bf16[2,30,62,128]{3,0,2,1:T(2,128)(2,1)} %copy.76), channel_id=1, source_target_pairs={{2,0},{3,1},{6,4},{7,5},{10,8},{11,9},{14,12},{15,13},{18,16},{19,... | collective-permute-start | bytes 2856968 | tf_op jit(solution)/shard_map/ppermute | solution.py:13
  65.6 24.4 %collective-permute-start.5 = (bf16[2,30,62,128]{3,0,2,1:T(2,128)(2,1)}, bf16[2,30,62,128]{3,0,2,1:T(2,128)(2,1)S(1)}, u32[]{:S(2)}, u32[]{:S(2)}) collective-permute-start(bf16[2,30,62,128]{3,0,2,1:T(2,128)(2,1)} %copy.74), channel_id=1, source_target_pairs={{0,2},{1,3},{4,6},{5,7},{8,10},{9,11},{12,14},{13,15},{16,18},{17,... | collective-permute-start | bytes 2856968 | tf_op jit(solution)/shard_map/ppermute | solution.py:13
  99.2 2.5 %copy-start.4 = (bf16[64,32,128]{2,1,0:T(8,128)(2,1)S(1)}, bf16[64,32,128]{2,1,0:T(8,128)(2,1)}, u32[]{:S(2)}) copy-start(bf16[64,32,128]{2,1,0:T(8,128)(2,1)} %copy-done.3) | copy-start | bytes 1572868
  107.7 3.8 %copy-start.2 = (bf16[64,32,128]{2,1,0:T(8,128)(2,1)S(1)}, bf16[64,32,128]{2,1,0:T(8,128)(2,1)}, u32[]{:S(2)}) copy-start(bf16[64,32,128]{2,1,0:T(8,128)(2,1)} %copy-done.1) | copy-start | bytes 1572868
  108.7 2.7 %collective-permute-start.7 = (f32[64,32,128]{2,1,0:T(8,128)S(1)}, f32[64,32,128]{2,1,0:T(8,128)S(1)}, u32[]{:S(2)}, u32[]{:S(2)}) collective-permute-start(f32[64,32,128]{2,1,0:T(8,128)S(1)} %copy.82), channel_id=1, source_target_pairs={{0,1},{1,0},{2,3},{3,2},{4,5},{5,4},{6,7},{7,6},{8,9},{9,8},{10,11... | collective-permute-start | bytes 3145736 | tf_op jit(solution)/shard_map/ppermute | solution.py:23
  112.3 20.0 %copy-start.5 = (bf16[64,62,92]{2,1,0:T(8,128)(2,1)S(1)}, bf16[64,62,92]{2,1,0:T(8,128)(2,1)}, u32[]{:S(2)}) copy-start(bf16[64,62,92]{2,1,0:T(8,128)(2,1)} %broadcast_in_dim.196) | copy-start | bytes 2190340
  112.6 15.6 %collective-permute-start.8 = (bf16[64,30,128]{2,1,0:T(8,128)(2,1)S(1)}, bf16[64,30,128]{2,1,0:T(8,128)(2,1)S(1)}, u32[]{:S(2)}, u32[]{:S(2)}) collective-permute-start(bf16[64,30,128]{2,1,0:T(8,128)(2,1)S(1)} %get-tuple-element.40), channel_id=1, source_target_pairs={{0,4},{4,8},{8,12},{1,5},{5,9},{9,13},{2,6},{6,10},{10,14},{3,7},{... | collective-permute-start | bytes 1474568 | tf_op jit(solution)/shard_map/ppermute | solution.py:13
  116.7 16.2 %copy-start.10 = (bf16[128,128]{1,0:T(8,128)(2,1)S(1)}, bf16[128,128]{1,0:T(8,128)(2,1)}, u32[]{:S(2)}) copy-start(bf16[128,128]{1,0:T(8,128)(2,1)} %copy-done.9) | copy-start | bytes 98308
  116.7 15.6 %collective-permute-start.9 = (bf16[64,30,128]{2,1,0:T(8,128)(2,1)S(1)}, bf16[64,30,128]{2,1,0:T(8,128)(2,1)S(1)}, u32[]{:S(2)}, u32[]{:S(2)}) collective-permute-start(bf16[64,30,128]{2,1,0:T(8,128)(2,1)S(1)} %get-tuple-element.41), channel_id=1, source_target_pairs={{4,0},{8,4},{12,8},{5,1},{9,5},{13,9},{6,2},{10,6},{14,10},{7,3},{... | collective-permute-start | bytes 1474568 | tf_op jit(solution)/shard_map/ppermute | solution.py:13
  133.9 14.2 %collective-permute-start.10 = (bf16[30,62,128]{2,0,1:T(8,128)(2,1)S(1)}, bf16[30,62,128]{2,0,1:T(8,128)(2,1)S(1)}, u32[]{:S(2)}, u32[]{:S(2)}) collective-permute-start(bf16[30,62,128]{2,0,1:T(8,128)(2,1)S(1)} %get-tuple-element.34), channel_id=1, source_target_pairs={{0,2},{1,3},{4,6},{5,7},{8,10},{9,11},{12,14},{13,15},{16,18},{17,... | collective-permute-start | bytes 1428488 | tf_op jit(solution)/shard_map/ppermute | solution.py:13
  138.2 14.1 %collective-permute-start.11 = (bf16[30,62,128]{2,0,1:T(8,128)(2,1)S(1)}, bf16[30,62,128]{2,0,1:T(8,128)(2,1)S(1)}, u32[]{:S(2)}, u32[]{:S(2)}) collective-permute-start(bf16[30,62,128]{2,0,1:T(8,128)(2,1)S(1)} %get-tuple-element.35), channel_id=1, source_target_pairs={{2,0},{3,1},{6,4},{7,5},{10,8},{11,9},{14,12},{15,13},{18,16},{19,... | collective-permute-start | bytes 1428488 | tf_op jit(solution)/shard_map/ppermute | solution.py:13
  166.4 2.9 %collective-permute-start.12 = (f32[64,32,128]{2,1,0:T(8,128)S(1)}, f32[64,32,128]{2,1,0:T(8,128)}, u32[]{:S(2)}, u32[]{:S(2)}) collective-permute-start(f32[64,32,128]{2,1,0:T(8,128)S(1)} %copy.88), channel_id=1, source_target_pairs={{0,1},{1,0},{2,3},{3,2},{4,5},{5,4},{6,7},{7,6},{8,9},{9,8},{10,11... | collective-permute-start | bytes 3145736 | tf_op jit(solution)/shard_map/ppermute | solution.py:23
  (5 other events, 8.8 us)

commit v4 on v2

--- a/solution.py
+++ b/solution.py
@@ -57,9 +57,30 @@
     ))
 
 
+def z_rims(volume, reach):
+    slabs = lax.axis_size("view") // 2
+    slab = lax.axis_index("view") // 2
+    planes = volume.shape[0]
+    below = jnp.zeros((reach,) + volume.shape[1:], volume.dtype)
+    above = below
+    for phase in (0, 1):
+        route = []
+        for low in range(phase, slabs - 1, 2):
+            for bit in (0, 1):
+                route += [(2 * low + bit, 2 * low + 2 + bit), (2 * low + 2 + bit, 2 * low + bit)]
+        if not route:
+            continue
+        is_lower = slab % 2 == phase
+        start = jnp.where(is_lower, planes - reach, 0)
+        payload = lax.dynamic_slice_in_dim(volume, start, reach, 0)
+        got = lax.ppermute(payload, "view", route)
+        below = jnp.where(is_lower, below, got)
+        above = jnp.where(is_lower, got, above)
+    return below, above
+
+
 def along_z(volume, matrix, reach):
-    below_rim = shifted(volume[volume.shape[0] - reach :], "view", 2)
-    above_rim = shifted(volume[:reach], "view", -2)
+    below_rim, above_rim = z_rims(volume, reach)
     extended = jnp.concatenate([below_rim, volume, above_rim], axis=0)
     planes = extended.shape[0]
     flat = extended.reshape(planes, -1)
@@ -140,9 +161,14 @@
         quotient = (measured_own / blurred).astype(jnp.bfloat16)
         widened_quotient = extended_2(quotient, (("tile", 1),), reach)
         back_own = separable(widened_quotient, adjoint_ops, reach)
+        if iteration == ITERS - 1:
+            partner_half = lax.dynamic_slice_in_dim(back_own, (1 - view_bit) * half_rows, half_rows, 0)
+            own_half = lax.dynamic_slice_in_dim(back_own, view_bit * half_rows, half_rows, 0)
+            back_partner = from_partner(partner_half, "view", 0)
+            kept = lax.dynamic_slice_in_dim(estimate, view_bit * half_rows, half_rows, 0)
+            return kept * (0.5 * (own_half + back_partner))
         back_partner = from_partner(back_own, "view", 0)
         estimate = estimate * (0.5 * (back_own + back_partner))
-    return lax.dynamic_slice_in_dim(estimate, view_bit * half_rows, half_rows, 0)
 
 
 def solution(mesh):

time: 123 us -> 109 us (0.89)
  waiting for transfers between devices: 65.3 us -> 57.2 us
  starting transfers between devices: 36.1 us -> 29.5 us
    ppermute x10 -> x2, waiting for transfers between devices: 29 us -> 6.65 us  [shifted(): return lax.ppermute(block, axis, route)]
    ppermute x0 -> x4, waiting for transfers between devices: none -> 14.5 us  [z_rims(): got = lax.ppermute(payload, 'view', route)]
    ppermute x10 -> x2, starting transfers between devices: 19.1 us -> 6.24 us  [shifted(): return lax.ppermute(block, axis, route)]
    ppermute x0 -> x4, starting transfers between devices: none -> 6.23 us  [z_rims(): got = lax.ppermute(payload, 'view', route)]
  transfers between devices with their start and end apart: 23 -> 19, of which waited for: 23 -> 19; matrix products, arithmetic and copies ran while one was open for 3% -> 3% of each run, Pallas kernels for 0% -> 0%
where the time goes in v4:
time: 109 us; the launch traced here: 108 us
  waiting for transfers between devices  57.2 us (52%)
  starting transfers between devices  29.5 us (27%)
  other arithmetic  8.23 us (8%)
  local copies, waits for them, and re-layouts  6.72 us (6%)
  matrix products  5.84 us (5%)
    ppermute x4, waiting for transfers between devices, extended_2(): lax.ppermute(lax.slice_in_dim(block, 0, width, axis=dim), axis, backward)  16.6 us
    ppermute x4, waiting for transfers between devices, z_rims(): got = lax.ppermute(payload, 'view', route)  14.5 us
    ppermute x4, starting transfers between devices, extended_2(): lax.ppermute(lax.slice_in_dim(block, block.shape[dim] - width, None, axis...  11.5 us
    ppermute x4, waiting for transfers between devices, extended_2(): lax.ppermute(lax.slice_in_dim(block, block.shape[dim] - width, None, axis...  10.6 us
    ppermute x5, waiting for transfers between devices, from_partner(): return lax.ppermute(block, axis, route)  8.89 us
    ppermute x2, waiting for transfers between devices, shifted(): return lax.ppermute(block, axis, route)  6.65 us
    ppermute x2, starting transfers between devices, shifted(): return lax.ppermute(block, axis, route)  6.24 us
    ppermute x4, starting transfers between devices, z_rims(): got = lax.ppermute(payload, 'view', route)  6.23 us
  transfers between devices with their start and end apart: 19, of which 19 were waited for; matrix products, arithmetic and copies ran while one was open for 3% of the time, Pallas kernels for 0%

profile of v4, /device:TPU:0, one launch (start us, length us, event | category | flops | bytes accessed | tf_op | source)
XLA Modules:
  0.0 108.2 jit_solution(1654519409860378448)
XLA Ops:
  3.2 4.9 %collective-permute-start = (bf16[64,4,4,128]{3,0,2,1:T(8,128)(2,1)S(1)}, bf16[64,4,4,128]{3,0,2,1:T(8,128)(2,1)S(1)}, u32[]{:S(2)}, u32[]{:S(2)}) collective-permute-start(bf16[64,4,4,128]{3,0,2,1:T(8,128)(2,1)S(1)} %select_bitcast_fusion.1), channel_id=1, source_target_pairs={{0,4},{4,8},{8,12},{1,5},{5,9},{9,13},{2,6},{6,10},{10,14},{3,7},{... | collective-permute-start | bytes 786440 | tf_op jit(solution)/shard_map/ppermute | solution.py:13
  13.6 5.2 %collective-permute-done.1 = bf16[64,4,4,128]{3,0,2,1:T(8,128)(2,1)S(1)} collective-permute-done((bf16[64,4,4,128]{3,0,2,1:T(8,128)(2,1)S(1)}, bf16[64,4,4,128]{3,0,2,1:T(8,128)(2,1)S(1)}, u32[]{:S(2)}, u32[]{:S(2)}) %collective-permute-start.1) | collective-permute-done | bytes 262176 | tf_op jit(solution)/shard_map/ppermute | solution.py:13
  20.2 1.9 %collective-permute-done.2 = bf16[64,32,128]{2,1,0:T(8,128)(2,1)S(1)} collective-permute-done((bf16[64,32,128]{2,1,0:T(8,128)(2,1)S(1)}, bf16[64,32,128]{2,1,0:T(8,128)(2,1)S(1)}, u32[]{:S(2)}, u32[]{:S(2)}) %collective-permute-start.2) | collective-permute-done | bytes 524320 | tf_op jit(solution)/shard_map/ppermute | solution.py:23
  22.5 3.5 %collective-permute-start.3 = (bf16[32,15,128]{2,1,0:T(8,128)(2,1)S(1)}, bf16[32,15,128]{2,1,0:T(8,128)(2,1)S(1)}, u32[]{:S(2)}, u32[]{:S(2)}) collective-permute-start(bf16[32,15,128]{2,1,0:T(8,128)(2,1)S(1)} %get-tuple-element.46), channel_id=1, source_target_pairs={{0,4},{4,8},{8,12},{1,5},{5,9},{9,13},{2,6},{6,10},{10,14},{3,7},{... | collective-permute-start | bytes 368648 | tf_op jit(solution)/shard_map/ppermute | solution.py:31
  29.0 4.1 %collective-permute-done.4 = bf16[32,15,128]{2,1,0:T(8,128)(2,1)S(1)} collective-permute-done((bf16[32,15,128]{2,1,0:T(8,128)(2,1)S(1)}, bf16[32,15,128]{2,1,0:T(8,128)(2,1)S(1)}, u32[]{:S(2)}, u32[]{:S(2)}) %collective-permute-start.4) | collective-permute-done | bytes 122912 | tf_op jit(solution)/shard_map/ppermute | solution.py:34
  35.7 1.6 %collective-permute-start.6 = (bf16[15,32,128]{2,1,0:T(8,128)(2,1)S(1)}, bf16[15,32,128]{2,1,0:T(8,128)(2,1)S(1)}, u32[]{:S(2)}, u32[]{:S(2)}) collective-permute-start(bf16[15,32,128]{2,1,0:T(8,128)(2,1)S(1)} %constant_dynamic-slice_fusion.9), channel_id=1, source_target_pairs={{0,2},{2,0},{1,3},{3,1},{4,6},{6,4},{5,7},{7,5},{8,10},{10,8},{9,1... | collective-permute-start | bytes 368648 | tf_op jit(solution)/shard_map/ppermute | solution.py:76
  37.2 3.9 %collective-permute-done.6 = bf16[15,32,128]{2,1,0:T(8,128)(2,1)S(1)} collective-permute-done((bf16[15,32,128]{2,1,0:T(8,128)(2,1)S(1)}, bf16[15,32,128]{2,1,0:T(8,128)(2,1)S(1)}, u32[]{:S(2)}, u32[]{:S(2)}) %collective-permute-start.6) | collective-permute-done | bytes 122912 | tf_op jit(solution)/shard_map/ppermute | solution.py:76
  42.5 3.5 %collective-permute-start.7 = (bf16[64,15,128]{2,1,0:T(8,128)(2,1)S(1)}, bf16[64,15,128]{2,1,0:T(8,128)(2,1)S(1)}, u32[]{:S(2)}, u32[]{:S(2)}) collective-permute-start(bf16[64,15,128]{2,1,0:T(8,128)(2,1)S(1)} %get-tuple-element.42), channel_id=1, source_target_pairs={{0,4},{4,8},{8,12},{1,5},{5,9},{9,13},{2,6},{6,10},{10,14},{3,7},{... | collective-permute-start | bytes 737288 | tf_op jit(solution)/shard_map/ppermute | solution.py:31
  47.4 3.6 %collective-permute-done.7 = bf16[64,15,128]{2,1,0:T(8,128)(2,1)S(1)} collective-permute-done((bf16[64,15,128]{2,1,0:T(8,128)(2,1)S(1)}, bf16[64,15,128]{2,1,0:T(8,128)(2,1)S(1)}, u32[]{:S(2)}, u32[]{:S(2)}) %collective-permute-start.7) | collective-permute-done | bytes 245792 | tf_op jit(solution)/shard_map/ppermute | solution.py:31
  51.0 4.2 %collective-permute-done.8 = bf16[64,15,128]{2,1,0:T(8,128)(2,1)} collective-permute-done((bf16[64,15,128]{2,1,0:T(8,128)(2,1)S(1)}, bf16[64,15,128]{2,1,0:T(8,128)(2,1)}, u32[]{:S(2)}, u32[]{:S(2)}) %collective-permute-start.8) | collective-permute-done | bytes 245792 | tf_op jit(solution)/shard_map/ppermute | solution.py:34
  56.8 1.6 %collective-permute-start.9 = (bf16[15,32,128]{2,1,0:T(8,128)(2,1)S(1)}, bf16[15,32,128]{2,1,0:T(8,128)(2,1)S(1)}, u32[]{:S(2)}, u32[]{:S(2)}) collective-permute-start(bf16[15,32,128]{2,1,0:T(8,128)(2,1)S(1)} %constant_dynamic-slice_fusion.8), channel_id=1, source_target_pairs={{0,2},{2,0},{1,3},{3,1},{4,6},{6,4},{5,7},{7,5},{8,10},{10,8},{9,1... | collective-permute-start | bytes 368648 | tf_op jit(solution)/shard_map/ppermute | solution.py:76
  58.4 3.4 %collective-permute-done.9 = bf16[15,32,128]{2,1,0:T(8,128)(2,1)S(1)} collective-permute-done((bf16[15,32,128]{2,1,0:T(8,128)(2,1)S(1)}, bf16[15,32,128]{2,1,0:T(8,128)(2,1)S(1)}, u32[]{:S(2)}, u32[]{:S(2)}) %collective-permute-start.9) | collective-permute-done | bytes 122912 | tf_op jit(solution)/shard_map/ppermute | solution.py:76
  63.1 2.6 %collective-permute-done.10 = f32[64,32,128]{2,1,0:T(8,128)S(1)} collective-permute-done((f32[64,32,128]{2,1,0:T(8,128)S(1)}, f32[64,32,128]{2,1,0:T(8,128)S(1)}, u32[]{:S(2)}, u32[]{:S(2)}) %collective-permute-start.10) | collective-permute-done | bytes 1048608 | tf_op jit(solution)/shard_map/ppermute | solution.py:23
  66.6 2.2 %collective-permute-start.11 = (bf16[32,15,128]{2,1,0:T(8,128)(2,1)S(1)}, bf16[32,15,128]{2,1,0:T(8,128)(2,1)S(1)}, u32[]{:S(2)}, u32[]{:S(2)}) collective-permute-start(bf16[32,15,128]{2,1,0:T(8,128)(2,1)S(1)} %get-tuple-element.40), channel_id=1, source_target_pairs={{0,4},{4,8},{8,12},{1,5},{5,9},{9,13},{2,6},{6,10},{10,14},{3,7},{... | collective-permute-start | bytes 368648 | tf_op jit(solution)/shard_map/ppermute | solution.py:31
  70.1 1.7 %collective-permute-done.11 = bf16[32,15,128]{2,1,0:T(8,128)(2,1)S(1)} collective-permute-done((bf16[32,15,128]{2,1,0:T(8,128)(2,1)S(1)}, bf16[32,15,128]{2,1,0:T(8,128)(2,1)S(1)}, u32[]{:S(2)}, u32[]{:S(2)}) %collective-permute-start.11) | collective-permute-done | bytes 122912 | tf_op jit(solution)/shard_map/ppermute | solution.py:31
  71.8 4.1 %collective-permute-done.12 = bf16[32,15,128]{2,1,0:T(8,128)(2,1)S(1)} collective-permute-done((bf16[32,15,128]{2,1,0:T(8,128)(2,1)S(1)}, bf16[32,15,128]{2,1,0:T(8,128)(2,1)S(1)}, u32[]{:S(2)}, u32[]{:S(2)}) %collective-permute-start.12) | collective-permute-done | bytes 122912 | tf_op jit(solution)/shard_map/ppermute | solution.py:34
  80.2 1.6 %collective-permute-start.14 = (bf16[15,32,128]{2,1,0:T(8,128)(2,1)S(1)}, bf16[15,32,128]{2,1,0:T(8,128)(2,1)S(1)}, u32[]{:S(2)}, u32[]{:S(2)}) collective-permute-start(bf16[15,32,128]{2,1,0:T(8,128)(2,1)S(1)} %constant_dynamic-slice_fusion.6), channel_id=1, source_target_pairs={{0,2},{2,0},{1,3},{3,1},{4,6},{6,4},{5,7},{7,5},{8,10},{10,8},{9,1... | collective-permute-start | bytes 368648 | tf_op jit(solution)/shard_map/ppermute | solution.py:76
  81.7 3.9 %collective-permute-done.14 = bf16[15,32,128]{2,1,0:T(8,128)(2,1)S(1)} collective-permute-done((bf16[15,32,128]{2,1,0:T(8,128)(2,1)S(1)}, bf16[15,32,128]{2,1,0:T(8,128)(2,1)S(1)}, u32[]{:S(2)}, u32[]{:S(2)}) %collective-permute-start.14) | collective-permute-done | bytes 122912 | tf_op jit(solution)/shard_map/ppermute | solution.py:76
  87.0 2.3 %collective-permute-start.15 = (bf16[64,15,128]{2,1,0:T(8,128)(2,1)S(1)}, bf16[64,15,128]{2,1,0:T(8,128)(2,1)S(1)}, u32[]{:S(2)}, u32[]{:S(2)}) collective-permute-start(bf16[64,15,128]{2,1,0:T(8,128)(2,1)S(1)} %get-tuple-element.36), channel_id=1, source_target_pairs={{0,4},{4,8},{8,12},{1,5},{5,9},{9,13},{2,6},{6,10},{10,14},{3,7},{... | collective-permute-start | bytes 737288 | tf_op jit(solution)/shard_map/ppermute | solution.py:31
  90.7 3.7 %collective-permute-done.15 = bf16[64,15,128]{2,1,0:T(8,128)(2,1)S(1)} collective-permute-done((bf16[64,15,128]{2,1,0:T(8,128)(2,1)S(1)}, bf16[64,15,128]{2,1,0:T(8,128)(2,1)S(1)}, u32[]{:S(2)}, u32[]{:S(2)}) %collective-permute-start.15) | collective-permute-done | bytes 245792 | tf_op jit(solution)/shard_map/ppermute | solution.py:31
  94.4 4.1 %collective-permute-done.16 = bf16[64,15,128]{2,1,0:T(8,128)(2,1)S(1)} collective-permute-done((bf16[64,15,128]{2,1,0:T(8,128)(2,1)S(1)}, bf16[64,15,128]{2,1,0:T(8,128)(2,1)S(1)}, u32[]{:S(2)}, u32[]{:S(2)}) %collective-permute-start.16) | collective-permute-done | bytes 245792 | tf_op jit(solution)/shard_map/ppermute | solution.py:34
  99.1 1.6 %collective-permute-start.17 = (bf16[15,32,128]{2,1,0:T(8,128)(2,1)S(1)}, bf16[15,32,128]{2,1,0:T(8,128)(2,1)S(1)}, u32[]{:S(2)}, u32[]{:S(2)}) collective-permute-start(bf16[15,32,128]{2,1,0:T(8,128)(2,1)S(1)} %constant_dynamic-slice_fusion.5), channel_id=1, source_target_pairs={{0,2},{2,0},{1,3},{3,1},{4,6},{6,4},{5,7},{7,5},{8,10},{10,8},{9,1... | collective-permute-start | bytes 368648 | tf_op jit(solution)/shard_map/ppermute | solution.py:76
  100.7 3.4 %collective-permute-done.17 = bf16[15,32,128]{2,1,0:T(8,128)(2,1)S(1)} collective-permute-done((bf16[15,32,128]{2,1,0:T(8,128)(2,1)S(1)}, bf16[15,32,128]{2,1,0:T(8,128)(2,1)S(1)}, u32[]{:S(2)}, u32[]{:S(2)}) %collective-permute-start.17) | collective-permute-done | bytes 122912 | tf_op jit(solution)/shard_map/ppermute | solution.py:76
  105.1 1.9 %collective-permute-done.18 = f32[32,32,128]{2,1,0:T(8,128)S(1)} collective-permute-done((f32[32,32,128]{2,1,0:T(8,128)S(1)}, f32[32,32,128]{2,1,0:T(8,128)S(1)}, u32[]{:S(2)}, u32[]{:S(2)}) %collective-permute-start.18) | collective-permute-done | bytes 524320 | tf_op jit(solution)/shard_map/ppermute | solution.py:23
  (115 shorter events, 33.1 us)
Async XLA Ops:
  2.4 8.0 %copy-start.2 = (s32[1,32]{1,0:T(1,128)S(1)}, s32[1,32]{1,0:T(1,128)}, u32[]{:S(2)}) copy-start(s32[1,32]{1,0:T(1,128)} %param.7) | copy-start | bytes 388
  2.4 8.9 %copy-start.3 = (f32[2,3,31]{2,0,1:T(2,128)S(1)}, f32[2,3,31]{2,0,1:T(2,128)}, u32[]{:S(2)}) copy-start(f32[2,3,31]{2,0,1:T(2,128)} %param.6) | copy-start | bytes 2236
  3.2 10.5 %collective-permute-start = (bf16[64,4,4,128]{3,0,2,1:T(8,128)(2,1)S(1)}, bf16[64,4,4,128]{3,0,2,1:T(8,128)(2,1)S(1)}, u32[]{:S(2)}, u32[]{:S(2)}) collective-permute-start(bf16[64,4,4,128]{3,0,2,1:T(8,128)(2,1)S(1)} %select_bitcast_fusion.1), channel_id=1, source_target_pairs={{0,4},{4,8},{8,12},{1,5},{5,9},{9,13},{2,6},{6,10},{10,14},{3,7},{... | collective-permute-start | bytes 786440 | tf_op jit(solution)/shard_map/ppermute | solution.py:13
  9.2 9.7 %collective-permute-start.1 = (bf16[64,4,4,128]{3,0,2,1:T(8,128)(2,1)S(1)}, bf16[64,4,4,128]{3,0,2,1:T(8,128)(2,1)S(1)}, u32[]{:S(2)}, u32[]{:S(2)}) collective-permute-start(bf16[64,4,4,128]{3,0,2,1:T(8,128)(2,1)S(1)} %select_bitcast_fusion), channel_id=1, source_target_pairs={{4,0},{8,4},{12,8},{5,1},{9,5},{13,9},{6,2},{10,6},{14,10},{7,3},{... | collective-permute-start | bytes 786440 | tf_op jit(solution)/shard_map/ppermute | solution.py:13
  20.1 2.0 %collective-permute-start.2 = (bf16[64,32,128]{2,1,0:T(8,128)(2,1)S(1)}, bf16[64,32,128]{2,1,0:T(8,128)(2,1)S(1)}, u32[]{:S(2)}, u32[]{:S(2)}) collective-permute-start(bf16[64,32,128]{2,1,0:T(8,128)(2,1)S(1)} %broadcast_select_fusion), channel_id=1, source_target_pairs={{0,1},{1,0},{2,3},{3,2},{4,5},{5,4},{6,7},{7,6},{8,9},{9,8},{10,11... | collective-permute-start | bytes 1572872 | tf_op jit(solution)/shard_map/ppermute | solution.py:23
  22.5 6.5 %collective-permute-start.3 = (bf16[32,15,128]{2,1,0:T(8,128)(2,1)S(1)}, bf16[32,15,128]{2,1,0:T(8,128)(2,1)S(1)}, u32[]{:S(2)}, u32[]{:S(2)}) collective-permute-start(bf16[32,15,128]{2,1,0:T(8,128)(2,1)S(1)} %get-tuple-element.46), channel_id=1, source_target_pairs={{0,4},{4,8},{8,12},{1,5},{5,9},{9,13},{2,6},{6,10},{10,14},{3,7},{... | collective-permute-start | bytes 368648 | tf_op jit(solution)/shard_map/ppermute | solution.py:31
  25.9 7.2 %collective-permute-start.4 = (bf16[32,15,128]{2,1,0:T(8,128)(2,1)S(1)}, bf16[32,15,128]{2,1,0:T(8,128)(2,1)S(1)}, u32[]{:S(2)}, u32[]{:S(2)}) collective-permute-start(bf16[32,15,128]{2,1,0:T(8,128)(2,1)S(1)} %get-tuple-element.47), channel_id=1, source_target_pairs={{4,0},{8,4},{12,8},{5,1},{9,5},{13,9},{6,2},{10,6},{14,10},{7,3},{... | collective-permute-start | bytes 368648 | tf_op jit(solution)/shard_map/ppermute | solution.py:34
  33.2 1.6 %collective-permute-start.5 = (bf16[32,30,128]{2,1,0:T(8,128)(2,1)S(1)}, bf16[32,30,128]{2,1,0:T(8,128)(2,1)S(1)}, u32[]{:S(2)}, u32[]{:S(2)}) collective-permute-start(bf16[32,30,128]{2,1,0:T(8,128)(2,1)S(1)} %pad_maximum_fusion.5), channel_id=1, source_target_pairs={{0,1},{1,0},{2,3},{3,2},{4,5},{5,4},{6,7},{7,6},{8,9},{9,8},{10,11... | collective-permute-start | bytes 737288 | tf_op jit(solution)/shard_map/ppermute | solution.py:23
  35.7 5.4 %collective-permute-start.6 = (bf16[15,32,128]{2,1,0:T(8,128)(2,1)S(1)}, bf16[15,32,128]{2,1,0:T(8,128)(2,1)S(1)}, u32[]{:S(2)}, u32[]{:S(2)}) collective-permute-start(bf16[15,32,128]{2,1,0:T(8,128)(2,1)S(1)} %constant_dynamic-slice_fusion.9), channel_id=1, source_target_pairs={{0,2},{2,0},{1,3},{3,1},{4,6},{6,4},{5,7},{7,5},{8,10},{10,8},{9,1... | collective-permute-start | bytes 368648 | tf_op jit(solution)/shard_map/ppermute | solution.py:76
  42.5 8.5 %collective-permute-start.7 = (bf16[64,15,128]{2,1,0:T(8,128)(2,1)S(1)}, bf16[64,15,128]{2,1,0:T(8,128)(2,1)S(1)}, u32[]{:S(2)}, u32[]{:S(2)}) collective-permute-start(bf16[64,15,128]{2,1,0:T(8,128)(2,1)S(1)} %get-tuple-element.42), channel_id=1, source_target_pairs={{0,4},{4,8},{8,12},{1,5},{5,9},{9,13},{2,6},{6,10},{10,14},{3,7},{... | collective-permute-start | bytes 737288 | tf_op jit(solution)/shard_map/ppermute | solution.py:31
  46.0 9.2 %collective-permute-start.8 = (bf16[64,15,128]{2,1,0:T(8,128)(2,1)S(1)}, bf16[64,15,128]{2,1,0:T(8,128)(2,1)}, u32[]{:S(2)}, u32[]{:S(2)}) collective-permute-start(bf16[64,15,128]{2,1,0:T(8,128)(2,1)S(1)} %get-tuple-element.43), channel_id=1, source_target_pairs={{4,0},{8,4},{12,8},{5,1},{9,5},{13,9},{6,2},{10,6},{14,10},{7,3},{... | collective-permute-start | bytes 737288 | tf_op jit(solution)/shard_map/ppermute | solution.py:34
  47.4 9.4 %copy-start = (bf16[64,32,62]{2,1,0:T(8,128)(2,1)}, bf16[64,32,62]{2,1,0:T(8,128)(2,1)S(1)}, u32[]{:S(2)}) copy-start(bf16[64,32,62]{2,1,0:T(8,128)(2,1)S(1)} %broadcast_in_dim.152) | copy-start | bytes 761860
  56.8 4.9 %collective-permute-start.9 = (bf16[15,32,128]{2,1,0:T(8,128)(2,1)S(1)}, bf16[15,32,128]{2,1,0:T(8,128)(2,1)S(1)}, u32[]{:S(2)}, u32[]{:S(2)}) collective-permute-start(bf16[15,32,128]{2,1,0:T(8,128)(2,1)S(1)} %constant_dynamic-slice_fusion.8), channel_id=1, source_target_pairs={{0,2},{2,0},{1,3},{3,1},{4,6},{6,4},{5,7},{7,5},{8,10},{10,8},{9,1... | collective-permute-start | bytes 368648 | tf_op jit(solution)/shard_map/ppermute | solution.py:76
  63.0 2.7 %collective-permute-start.10 = (f32[64,32,128]{2,1,0:T(8,128)S(1)}, f32[64,32,128]{2,1,0:T(8,128)S(1)}, u32[]{:S(2)}, u32[]{:S(2)}) collective-permute-start(f32[64,32,128]{2,1,0:T(8,128)S(1)} %copy.21), channel_id=1, source_target_pairs={{0,1},{1,0},{2,3},{3,2},{4,5},{5,4},{6,7},{7,6},{8,9},{9,8},{10,11... | collective-permute-start | bytes 3145736 | tf_op jit(solution)/shard_map/ppermute | solution.py:23
  66.6 5.2 %collective-permute-start.11 = (bf16[32,15,128]{2,1,0:T(8,128)(2,1)S(1)}, bf16[32,15,128]{2,1,0:T(8,128)(2,1)S(1)}, u32[]{:S(2)}, u32[]{:S(2)}) collective-permute-start(bf16[32,15,128]{2,1,0:T(8,128)(2,1)S(1)} %get-tuple-element.40), channel_id=1, source_target_pairs={{0,4},{4,8},{8,12},{1,5},{5,9},{9,13},{2,6},{6,10},{10,14},{3,7},{... | collective-permute-start | bytes 368648 | tf_op jit(solution)/shard_map/ppermute | solution.py:31
  68.8 7.2 %collective-permute-start.12 = (bf16[32,15,128]{2,1,0:T(8,128)(2,1)S(1)}, bf16[32,15,128]{2,1,0:T(8,128)(2,1)S(1)}, u32[]{:S(2)}, u32[]{:S(2)}) collective-permute-start(bf16[32,15,128]{2,1,0:T(8,128)(2,1)S(1)} %get-tuple-element.41), channel_id=1, source_target_pairs={{4,0},{8,4},{12,8},{5,1},{9,5},{13,9},{6,2},{10,6},{14,10},{7,3},{... | collective-permute-start | bytes 368648 | tf_op jit(solution)/shard_map/ppermute | solution.py:34
  76.0 1.6 %collective-permute-start.13 = (bf16[32,30,128]{2,1,0:T(8,128)(2,1)S(1)}, bf16[32,30,128]{2,1,0:T(8,128)(2,1)S(1)}, u32[]{:S(2)}, u32[]{:S(2)}) collective-permute-start(bf16[32,30,128]{2,1,0:T(8,128)(2,1)S(1)} %pad_maximum_fusion.6), channel_id=1, source_target_pairs={{0,1},{1,0},{2,3},{3,2},{4,5},{5,4},{6,7},{7,6},{8,9},{9,8},{10,11... | collective-permute-start | bytes 737288 | tf_op jit(solution)/shard_map/ppermute | solution.py:23
  80.2 5.4 %collective-permute-start.14 = (bf16[15,32,128]{2,1,0:T(8,128)(2,1)S(1)}, bf16[15,32,128]{2,1,0:T(8,128)(2,1)S(1)}, u32[]{:S(2)}, u32[]{:S(2)}) collective-permute-start(bf16[15,32,128]{2,1,0:T(8,128)(2,1)S(1)} %constant_dynamic-slice_fusion.6), channel_id=1, source_target_pairs={{0,2},{2,0},{1,3},{3,1},{4,6},{6,4},{5,7},{7,5},{8,10},{10,8},{9,1... | collective-permute-start | bytes 368648 | tf_op jit(solution)/shard_map/ppermute | solution.py:76
  86.9 11.6 %copy-start.1 = (bf16[64,32,62]{2,1,0:T(8,128)(2,1)S(1)}, bf16[64,32,62]{2,1,0:T(8,128)(2,1)}, u32[]{:S(2)}) copy-start(bf16[64,32,62]{2,1,0:T(8,128)(2,1)} %copy-done) | copy-start | bytes 761860
  87.0 7.3 %collective-permute-start.15 = (bf16[64,15,128]{2,1,0:T(8,128)(2,1)S(1)}, bf16[64,15,128]{2,1,0:T(8,128)(2,1)S(1)}, u32[]{:S(2)}, u32[]{:S(2)}) collective-permute-start(bf16[64,15,128]{2,1,0:T(8,128)(2,1)S(1)} %get-tuple-element.36), channel_id=1, source_target_pairs={{0,4},{4,8},{8,12},{1,5},{5,9},{9,13},{2,6},{6,10},{10,14},{3,7},{... | collective-permute-start | bytes 737288 | tf_op jit(solution)/shard_map/ppermute | solution.py:31
  89.4 9.1 %collective-permute-start.16 = (bf16[64,15,128]{2,1,0:T(8,128)(2,1)S(1)}, bf16[64,15,128]{2,1,0:T(8,128)(2,1)S(1)}, u32[]{:S(2)}, u32[]{:S(2)}) collective-permute-start(bf16[64,15,128]{2,1,0:T(8,128)(2,1)S(1)} %get-tuple-element.37), channel_id=1, source_target_pairs={{4,0},{8,4},{12,8},{5,1},{9,5},{13,9},{6,2},{10,6},{14,10},{7,3},{... | collective-permute-start | bytes 737288 | tf_op jit(solution)/shard_map/ppermute | solution.py:34
  99.1 4.9 %collective-permute-start.17 = (bf16[15,32,128]{2,1,0:T(8,128)(2,1)S(1)}, bf16[15,32,128]{2,1,0:T(8,128)(2,1)S(1)}, u32[]{:S(2)}, u32[]{:S(2)}) collective-permute-start(bf16[15,32,128]{2,1,0:T(8,128)(2,1)S(1)} %constant_dynamic-slice_fusion.5), channel_id=1, source_target_pairs={{0,2},{2,0},{1,3},{3,1},{4,6},{6,4},{5,7},{7,5},{8,10},{10,8},{9,1... | collective-permute-start | bytes 368648 | tf_op jit(solution)/shard_map/ppermute | solution.py:76
  105.1 2.0 %collective-permute-start.18 = (f32[32,32,128]{2,1,0:T(8,128)S(1)}, f32[32,32,128]{2,1,0:T(8,128)S(1)}, u32[]{:S(2)}, u32[]{:S(2)}) collective-permute-start(f32[32,32,128]{2,1,0:T(8,128)S(1)} %copy.28), channel_id=1, source_target_pairs={{0,1},{1,0},{2,3},{3,2},{4,5},{5,4},{6,7},{7,6},{8,9},{9,8},{10,11... | collective-permute-start | bytes 1572872 | tf_op jit(solution)/shard_map/ppermute | solution.py:23

commit v5 on v4

--- a/solution.py
+++ b/solution.py
@@ -34,6 +34,25 @@
         high = lax.ppermute(lax.slice_in_dim(block, 0, width, axis=dim), axis, backward)
         block = jnp.concatenate([low, block, high], axis=dim)
     return block
+
+
+def shared_x_rims(block, reach):
+    tiles = lax.axis_size("tile")
+    views = lax.axis_size("view")
+    route = []
+    for view in range(views):
+        for left in range(view % 2, tiles - 1, 2):
+            route += [(left * views + view, (left + 1) * views + view)]
+            route += [((left + 1) * views + view, left * views + view)]
+    is_left = lax.axis_index("tile") % 2 == lax.axis_index("view") % 2
+    width = block.shape[1]
+    start = jnp.where(is_left, width - reach, 0)
+    payload = lax.dynamic_slice_in_dim(block, start, reach, 1)
+    got = lax.ppermute(payload, ("tile", "view"), route)
+    other = from_partner(got, "view", 0)
+    low = jnp.where(is_left, other, got)
+    high = jnp.where(is_left, got, other)
+    return low, high
 
 
 def band_matrix(kernel, row_count, col_count, base_shift):
@@ -147,16 +166,8 @@
     half_rows = planes // 2
     for iteration in range(ITERS):
         estimate_low = estimate.astype(jnp.bfloat16)
-        own_half = lax.dynamic_slice_in_dim(estimate_low, view_bit * half_rows, half_rows, 0)
-        widened = extended_2(own_half, (("tile", 1),), reach)
-        rim_stack = jnp.concatenate([widened[:, :reach], widened[:, reach + width_x :]], axis=1)
-        partner_rims = from_partner(rim_stack, "view", 0)
-        all_rims = jnp.where(
-            view_bit == 0,
-            jnp.concatenate([rim_stack, partner_rims], axis=0),
-            jnp.concatenate([partner_rims, rim_stack], axis=0),
-        )
-        extended = jnp.concatenate([all_rims[:, :reach], estimate_low, all_rims[:, reach:]], axis=1)
+        low, high = shared_x_rims(estimate_low, reach)
+        extended = jnp.concatenate([low, estimate_low, high], axis=1)
         blurred = separable(extended, forward_ops, reach)
         quotient = (measured_own / blurred).astype(jnp.bfloat16)
         widened_quotient = extended_2(quotient, (("tile", 1),), reach)

time: 109 us -> 106 us (0.972)
  waiting for transfers between devices: 57.2 us -> 55.1 us
    ppermute x0 -> x2, waiting for transfers between devices: none -> 9.28 us  [shared_x_rims(): got = lax.ppermute(payload, ('tile', 'view'), route)]
    ppermute x4 -> x2, waiting for transfers between devices: 16.6 us -> 8.36 us  [extended_2(): lax.ppermute(lax.slice_in_dim(block, 0, width, axis=dim), axis, backward)]
    ppermute x0 -> x2, starting transfers between devices: none -> 6.95 us  [shared_x_rims(): got = lax.ppermute(payload, ('tile', 'view'), route)]
    ppermute x4 -> x2, starting transfers between devices: 11.5 us -> 7.1 us  [extended_2(): lax.ppermute(lax.slice_in_dim(block, block.shape[dim] - width, None, axis...]
    ppermute x4 -> x2, waiting for transfers between devices: 10.6 us -> 7.32 us  [extended_2(): lax.ppermute(lax.slice_in_dim(block, block.shape[dim] - width, None, axis...]
    ppermute x4 -> x2, starting transfers between devices: 5.17 us -> 2.58 us  [extended_2(): lax.ppermute(lax.slice_in_dim(block, 0, width, axis=dim), axis, backward)]
  transfers between devices with their start and end apart: 19 -> 17, of which waited for: 19 -> 17; matrix products, arithmetic and copies ran while one was open for 3% -> 3% of each run, Pallas kernels for 0% -> 0%
where the time goes in v5:
time: 106 us; the launch traced here: 105 us
  waiting for transfers between devices  55.1 us (52%)
  starting transfers between devices  29.3 us (28%)
  other arithmetic  8.46 us (8%)
  local copies, waits for them, and re-layouts  5.92 us (6%)
  matrix products  5.86 us (6%)
    ppermute x4, waiting for transfers between devices, z_rims(): got = lax.ppermute(payload, 'view', route)  14.5 us
    ppermute x2, waiting for transfers between devices, shared_x_rims(): got = lax.ppermute(payload, ('tile', 'view'), route)  9.28 us
    ppermute x5, waiting for transfers between devices, from_partner(): return lax.ppermute(block, axis, route)  8.5 us
    ppermute x2, waiting for transfers between devices, extended_2(): lax.ppermute(lax.slice_in_dim(block, 0, width, axis=dim), axis, backward)  8.36 us
    ppermute x2, waiting for transfers between devices, extended_2(): lax.ppermute(lax.slice_in_dim(block, block.shape[dim] - width, None, axis...  7.32 us
    ppermute x2, waiting for transfers between devices, shifted(): return lax.ppermute(block, axis, route)  7.15 us
    ppermute x2, starting transfers between devices, extended_2(): lax.ppermute(lax.slice_in_dim(block, block.shape[dim] - width, None, axis...  7.1 us
    ppermute x2, starting transfers between devices, shared_x_rims(): got = lax.ppermute(payload, ('tile', 'view'), route)  6.95 us
  transfers between devices with their start and end apart: 17, of which 17 were waited for; matrix products, arithmetic and copies ran while one was open for 3% of the time, Pallas kernels for 0%

profile of v5, /device:TPU:0, one launch (start us, length us, event | category | flops | bytes accessed | tf_op | source)
XLA Modules:
  0.0 105.3 jit_solution(17230743524313535139)
XLA Ops:
  3.2 4.9 %collective-permute-start = (bf16[64,4,4,128]{3,0,2,1:T(8,128)(2,1)S(1)}, bf16[64,4,4,128]{3,0,2,1:T(8,128)(2,1)S(1)}, u32[]{:S(2)}, u32[]{:S(2)}) collective-permute-start(bf16[64,4,4,128]{3,0,2,1:T(8,128)(2,1)S(1)} %select_bitcast_fusion.1), channel_id=1, source_target_pairs={{0,4},{4,8},{8,12},{1,5},{5,9},{9,13},{2,6},{6,10},{10,14},{3,7},{... | collective-permute-start | bytes 786440 | tf_op jit(solution)/shard_map/ppermute | solution.py:13
  11.7 2.0 %collective-permute-done = bf16[64,4,4,128]{3,0,2,1:T(8,128)(2,1)S(1)} collective-permute-done((bf16[64,4,4,128]{3,0,2,1:T(8,128)(2,1)S(1)}, bf16[64,4,4,128]{3,0,2,1:T(8,128)(2,1)S(1)}, u32[]{:S(2)}, u32[]{:S(2)}) %collective-permute-start) | collective-permute-done | bytes 262176 | tf_op jit(solution)/shard_map/ppermute | solution.py:13
  13.6 5.2 %collective-permute-done.1 = bf16[64,4,4,128]{3,0,2,1:T(8,128)(2,1)S(1)} collective-permute-done((bf16[64,4,4,128]{3,0,2,1:T(8,128)(2,1)S(1)}, bf16[64,4,4,128]{3,0,2,1:T(8,128)(2,1)S(1)}, u32[]{:S(2)}, u32[]{:S(2)}) %collective-permute-start.1) | collective-permute-done | bytes 262176 | tf_op jit(solution)/shard_map/ppermute | solution.py:13
  22.5 3.5 %collective-permute-start.3 = (bf16[64,15,128]{2,1,0:T(8,128)(2,1)S(1)}, bf16[64,15,128]{2,1,0:T(8,128)(2,1)S(1)}, u32[]{:S(2)}, u32[]{:S(2)}) collective-permute-start(bf16[64,15,128]{2,1,0:T(8,128)(2,1)S(1)} %constant_dynamic-slice_fusion.8), channel_id=1, source_target_pairs={{0,4},{4,0},{8,12},{12,8},{5,9},{9,5},{2,6},{6,2},{10,14},{14,10},... | collective-permute-start | bytes 737288 | tf_op jit(solution)/shard_map/ppermute | solution.py:51
  26.3 4.5 %collective-permute-done.3 = bf16[64,15,128]{2,1,0:T(8,128)(2,1)S(1)} collective-permute-done((bf16[64,15,128]{2,1,0:T(8,128)(2,1)S(1)}, bf16[64,15,128]{2,1,0:T(8,128)(2,1)S(1)}, u32[]{:S(2)}, u32[]{:S(2)}) %collective-permute-start.3) | collective-permute-done | bytes 245792 | tf_op jit(solution)/shard_map/ppermute | solution.py:51
  33.0 1.6 %collective-permute-start.5 = (bf16[15,32,128]{2,1,0:T(8,128)(2,1)S(1)}, bf16[15,32,128]{2,1,0:T(8,128)(2,1)S(1)}, u32[]{:S(2)}, u32[]{:S(2)}) collective-permute-start(bf16[15,32,128]{2,1,0:T(8,128)(2,1)S(1)} %constant_dynamic-slice_fusion.7), channel_id=1, source_target_pairs={{0,2},{2,0},{1,3},{3,1},{4,6},{6,4},{5,7},{7,5},{8,10},{10,8},{9,1... | collective-permute-start | bytes 368648 | tf_op jit(solution)/shard_map/ppermute | solution.py:95
  34.5 3.9 %collective-permute-done.5 = bf16[15,32,128]{2,1,0:T(8,128)(2,1)S(1)} collective-permute-done((bf16[15,32,128]{2,1,0:T(8,128)(2,1)S(1)}, bf16[15,32,128]{2,1,0:T(8,128)(2,1)S(1)}, u32[]{:S(2)}, u32[]{:S(2)}) %collective-permute-start.5) | collective-permute-done | bytes 122912 | tf_op jit(solution)/shard_map/ppermute | solution.py:95
  39.8 3.5 %collective-permute-start.6 = (bf16[64,15,128]{2,1,0:T(8,128)(2,1)S(1)}, bf16[64,15,128]{2,1,0:T(8,128)(2,1)S(1)}, u32[]{:S(2)}, u32[]{:S(2)}) collective-permute-start(bf16[64,15,128]{2,1,0:T(8,128)(2,1)S(1)} %get-tuple-element.40), channel_id=1, source_target_pairs={{0,4},{4,8},{8,12},{1,5},{5,9},{9,13},{2,6},{6,10},{10,14},{3,7},{... | collective-permute-start | bytes 737288 | tf_op jit(solution)/shard_map/ppermute | solution.py:31
  44.7 3.6 %collective-permute-done.6 = bf16[64,15,128]{2,1,0:T(8,128)(2,1)S(1)} collective-permute-done((bf16[64,15,128]{2,1,0:T(8,128)(2,1)S(1)}, bf16[64,15,128]{2,1,0:T(8,128)(2,1)S(1)}, u32[]{:S(2)}, u32[]{:S(2)}) %collective-permute-start.6) | collective-permute-done | bytes 245792 | tf_op jit(solution)/shard_map/ppermute | solution.py:31
  48.3 4.2 %collective-permute-done.7 = bf16[64,15,128]{2,1,0:T(8,128)(2,1)} collective-permute-done((bf16[64,15,128]{2,1,0:T(8,128)(2,1)S(1)}, bf16[64,15,128]{2,1,0:T(8,128)(2,1)}, u32[]{:S(2)}, u32[]{:S(2)}) %collective-permute-start.7) | collective-permute-done | bytes 245792 | tf_op jit(solution)/shard_map/ppermute | solution.py:34
  54.1 1.6 %collective-permute-start.8 = (bf16[15,32,128]{2,1,0:T(8,128)(2,1)S(1)}, bf16[15,32,128]{2,1,0:T(8,128)(2,1)S(1)}, u32[]{:S(2)}, u32[]{:S(2)}) collective-permute-start(bf16[15,32,128]{2,1,0:T(8,128)(2,1)S(1)} %constant_dynamic-slice_fusion.6), channel_id=1, source_target_pairs={{0,2},{2,0},{1,3},{3,1},{4,6},{6,4},{5,7},{7,5},{8,10},{10,8},{9,1... | collective-permute-start | bytes 368648 | tf_op jit(solution)/shard_map/ppermute | solution.py:95
  55.6 3.4 %collective-permute-done.8 = bf16[15,32,128]{2,1,0:T(8,128)(2,1)S(1)} collective-permute-done((bf16[15,32,128]{2,1,0:T(8,128)(2,1)S(1)}, bf16[15,32,128]{2,1,0:T(8,128)(2,1)S(1)}, u32[]{:S(2)}, u32[]{:S(2)}) %collective-permute-start.8) | collective-permute-done | bytes 122912 | tf_op jit(solution)/shard_map/ppermute | solution.py:95
  60.3 2.6 %collective-permute-done.9 = f32[64,32,128]{2,1,0:T(8,128)S(1)} collective-permute-done((f32[64,32,128]{2,1,0:T(8,128)S(1)}, f32[64,32,128]{2,1,0:T(8,128)S(1)}, u32[]{:S(2)}, u32[]{:S(2)}) %collective-permute-start.9) | collective-permute-done | bytes 1048608 | tf_op jit(solution)/shard_map/ppermute | solution.py:23
  63.9 3.5 %collective-permute-start.10 = (bf16[64,15,128]{2,1,0:T(8,128)(2,1)S(1)}, bf16[64,15,128]{2,1,0:T(8,128)(2,1)S(1)}, u32[]{:S(2)}, u32[]{:S(2)}) collective-permute-start(bf16[64,15,128]{2,1,0:T(8,128)(2,1)S(1)} %constant_dynamic-slice_fusion.5), channel_id=1, source_target_pairs={{0,4},{4,0},{8,12},{12,8},{5,9},{9,5},{2,6},{6,2},{10,14},{14,10},... | collective-permute-start | bytes 737288 | tf_op jit(solution)/shard_map/ppermute | solution.py:51
  67.4 4.8 %collective-permute-done.10 = bf16[64,15,128]{2,1,0:T(8,128)(2,1)S(1)} collective-permute-done((bf16[64,15,128]{2,1,0:T(8,128)(2,1)S(1)}, bf16[64,15,128]{2,1,0:T(8,128)(2,1)S(1)}, u32[]{:S(2)}, u32[]{:S(2)}) %collective-permute-start.10) | collective-permute-done | bytes 245792 | tf_op jit(solution)/shard_map/ppermute | solution.py:51
  72.2 1.5 %collective-permute-done.11 = bf16[64,15,128]{2,1,0:T(8,128)(2,1)S(1)} collective-permute-done((bf16[64,15,128]{2,1,0:T(8,128)(2,1)S(1)}, bf16[64,15,128]{2,1,0:T(8,128)(2,1)S(1)}, u32[]{:S(2)}, u32[]{:S(2)}) %collective-permute-start.11) | collective-permute-done | bytes 245792 | tf_op jit(solution)/shard_map/ppermute | solution.py:23
  76.0 1.6 %collective-permute-start.12 = (bf16[15,32,128]{2,1,0:T(8,128)(2,1)S(1)}, bf16[15,32,128]{2,1,0:T(8,128)(2,1)S(1)}, u32[]{:S(2)}, u32[]{:S(2)}) collective-permute-start(bf16[15,32,128]{2,1,0:T(8,128)(2,1)S(1)} %constant_dynamic-slice_fusion.4), channel_id=1, source_target_pairs={{0,2},{2,0},{1,3},{3,1},{4,6},{6,4},{5,7},{7,5},{8,10},{10,8},{9,1... | collective-permute-start | bytes 368648 | tf_op jit(solution)/shard_map/ppermute | solution.py:95
  77.6 3.9 %collective-permute-done.12 = bf16[15,32,128]{2,1,0:T(8,128)(2,1)S(1)} collective-permute-done((bf16[15,32,128]{2,1,0:T(8,128)(2,1)S(1)}, bf16[15,32,128]{2,1,0:T(8,128)(2,1)S(1)}, u32[]{:S(2)}, u32[]{:S(2)}) %collective-permute-start.12) | collective-permute-done | bytes 122912 | tf_op jit(solution)/shard_map/ppermute | solution.py:95
  82.8 3.6 %collective-permute-start.13 = (bf16[64,15,128]{2,1,0:T(8,128)(2,1)S(1)}, bf16[64,15,128]{2,1,0:T(8,128)(2,1)S(1)}, u32[]{:S(2)}, u32[]{:S(2)}) collective-permute-start(bf16[64,15,128]{2,1,0:T(8,128)(2,1)S(1)} %get-tuple-element.36), channel_id=1, source_target_pairs={{0,4},{4,8},{8,12},{1,5},{5,9},{9,13},{2,6},{6,10},{10,14},{3,7},{... | collective-permute-start | bytes 737288 | tf_op jit(solution)/shard_map/ppermute | solution.py:31
  87.8 3.7 %collective-permute-done.13 = bf16[64,15,128]{2,1,0:T(8,128)(2,1)S(1)} collective-permute-done((bf16[64,15,128]{2,1,0:T(8,128)(2,1)S(1)}, bf16[64,15,128]{2,1,0:T(8,128)(2,1)S(1)}, u32[]{:S(2)}, u32[]{:S(2)}) %collective-permute-start.13) | collective-permute-done | bytes 245792 | tf_op jit(solution)/shard_map/ppermute | solution.py:31
  91.5 4.1 %collective-permute-done.14 = bf16[64,15,128]{2,1,0:T(8,128)(2,1)S(1)} collective-permute-done((bf16[64,15,128]{2,1,0:T(8,128)(2,1)S(1)}, bf16[64,15,128]{2,1,0:T(8,128)(2,1)S(1)}, u32[]{:S(2)}, u32[]{:S(2)}) %collective-permute-start.14) | collective-permute-done | bytes 245792 | tf_op jit(solution)/shard_map/ppermute | solution.py:34
  96.2 1.6 %collective-permute-start.15 = (bf16[15,32,128]{2,1,0:T(8,128)(2,1)S(1)}, bf16[15,32,128]{2,1,0:T(8,128)(2,1)S(1)}, u32[]{:S(2)}, u32[]{:S(2)}) collective-permute-start(bf16[15,32,128]{2,1,0:T(8,128)(2,1)S(1)} %constant_dynamic-slice_fusion.3), channel_id=1, source_target_pairs={{0,2},{2,0},{1,3},{3,1},{4,6},{6,4},{5,7},{7,5},{8,10},{10,8},{9,1... | collective-permute-start | bytes 368648 | tf_op jit(solution)/shard_map/ppermute | solution.py:95
  97.8 3.4 %collective-permute-done.15 = bf16[15,32,128]{2,1,0:T(8,128)(2,1)S(1)} collective-permute-done((bf16[15,32,128]{2,1,0:T(8,128)(2,1)S(1)}, bf16[15,32,128]{2,1,0:T(8,128)(2,1)S(1)}, u32[]{:S(2)}, u32[]{:S(2)}) %collective-permute-start.15) | collective-permute-done | bytes 122912 | tf_op jit(solution)/shard_map/ppermute | solution.py:95
  102.3 1.9 %collective-permute-done.16 = f32[32,32,128]{2,1,0:T(8,128)S(1)} collective-permute-done((f32[32,32,128]{2,1,0:T(8,128)S(1)}, f32[32,32,128]{2,1,0:T(8,128)S(1)}, u32[]{:S(2)}, u32[]{:S(2)}) %collective-permute-start.16) | collective-permute-done | bytes 524320 | tf_op jit(solution)/shard_map/ppermute | solution.py:23
  (107 shorter events, 26.8 us)
Async XLA Ops:
  2.4 8.0 %copy-start.2 = (s32[1,32]{1,0:T(1,128)S(1)}, s32[1,32]{1,0:T(1,128)}, u32[]{:S(2)}) copy-start(s32[1,32]{1,0:T(1,128)} %param.7) | copy-start | bytes 388
  2.4 8.7 %copy-start.3 = (f32[2,3,31]{2,0,1:T(2,128)S(1)}, f32[2,3,31]{2,0,1:T(2,128)}, u32[]{:S(2)}) copy-start(f32[2,3,31]{2,0,1:T(2,128)} %param.6) | copy-start | bytes 2236
  3.2 10.5 %collective-permute-start = (bf16[64,4,4,128]{3,0,2,1:T(8,128)(2,1)S(1)}, bf16[64,4,4,128]{3,0,2,1:T(8,128)(2,1)S(1)}, u32[]{:S(2)}, u32[]{:S(2)}) collective-permute-start(bf16[64,4,4,128]{3,0,2,1:T(8,128)(2,1)S(1)} %select_bitcast_fusion.1), channel_id=1, source_target_pairs={{0,4},{4,8},{8,12},{1,5},{5,9},{9,13},{2,6},{6,10},{10,14},{3,7},{... | collective-permute-start | bytes 786440 | tf_op jit(solution)/shard_map/ppermute | solution.py:13
  9.2 9.7 %collective-permute-start.1 = (bf16[64,4,4,128]{3,0,2,1:T(8,128)(2,1)S(1)}, bf16[64,4,4,128]{3,0,2,1:T(8,128)(2,1)S(1)}, u32[]{:S(2)}, u32[]{:S(2)}) collective-permute-start(bf16[64,4,4,128]{3,0,2,1:T(8,128)(2,1)S(1)} %select_bitcast_fusion), channel_id=1, source_target_pairs={{4,0},{8,4},{12,8},{5,1},{9,5},{13,9},{6,2},{10,6},{14,10},{7,3},{... | collective-permute-start | bytes 786440 | tf_op jit(solution)/shard_map/ppermute | solution.py:13
  20.1 2.0 %collective-permute-start.2 = (bf16[64,32,128]{2,1,0:T(8,128)(2,1)S(1)}, bf16[64,32,128]{2,1,0:T(8,128)(2,1)S(1)}, u32[]{:S(2)}, u32[]{:S(2)}) collective-permute-start(bf16[64,32,128]{2,1,0:T(8,128)(2,1)S(1)} %broadcast_select_fusion), channel_id=1, source_target_pairs={{0,1},{1,0},{2,3},{3,2},{4,5},{5,4},{6,7},{7,6},{8,9},{9,8},{10,11... | collective-permute-start | bytes 1572872 | tf_op jit(solution)/shard_map/ppermute | solution.py:23
  22.5 8.3 %collective-permute-start.3 = (bf16[64,15,128]{2,1,0:T(8,128)(2,1)S(1)}, bf16[64,15,128]{2,1,0:T(8,128)(2,1)S(1)}, u32[]{:S(2)}, u32[]{:S(2)}) collective-permute-start(bf16[64,15,128]{2,1,0:T(8,128)(2,1)S(1)} %constant_dynamic-slice_fusion.8), channel_id=1, source_target_pairs={{0,4},{4,0},{8,12},{12,8},{5,9},{9,5},{2,6},{6,2},{10,14},{14,10},... | collective-permute-start | bytes 737288 | tf_op jit(solution)/shard_map/ppermute | solution.py:51
  30.8 1.5 %collective-permute-start.4 = (bf16[64,15,128]{2,1,0:T(8,128)(2,1)S(1)}, bf16[64,15,128]{2,1,0:T(8,128)(2,1)S(1)}, u32[]{:S(2)}, u32[]{:S(2)}) collective-permute-start(bf16[64,15,128]{2,1,0:T(8,128)(2,1)S(1)} %collective-permute-done.3), channel_id=1, source_target_pairs={{0,1},{1,0},{2,3},{3,2},{4,5},{5,4},{6,7},{7,6},{8,9},{9,8},{10,11... | collective-permute-start | bytes 737288 | tf_op jit(solution)/shard_map/ppermute | solution.py:23
  33.0 5.4 %collective-permute-start.5 = (bf16[15,32,128]{2,1,0:T(8,128)(2,1)S(1)}, bf16[15,32,128]{2,1,0:T(8,128)(2,1)S(1)}, u32[]{:S(2)}, u32[]{:S(2)}) collective-permute-start(bf16[15,32,128]{2,1,0:T(8,128)(2,1)S(1)} %constant_dynamic-slice_fusion.7), channel_id=1, source_target_pairs={{0,2},{2,0},{1,3},{3,1},{4,6},{6,4},{5,7},{7,5},{8,10},{10,8},{9,1... | collective-permute-start | bytes 368648 | tf_op jit(solution)/shard_map/ppermute | solution.py:95
  39.8 8.5 %collective-permute-start.6 = (bf16[64,15,128]{2,1,0:T(8,128)(2,1)S(1)}, bf16[64,15,128]{2,1,0:T(8,128)(2,1)S(1)}, u32[]{:S(2)}, u32[]{:S(2)}) collective-permute-start(bf16[64,15,128]{2,1,0:T(8,128)(2,1)S(1)} %get-tuple-element.40), channel_id=1, source_target_pairs={{0,4},{4,8},{8,12},{1,5},{5,9},{9,13},{2,6},{6,10},{10,14},{3,7},{... | collective-permute-start | bytes 737288 | tf_op jit(solution)/shard_map/ppermute | solution.py:31
  43.3 9.2 %collective-permute-start.7 = (bf16[64,15,128]{2,1,0:T(8,128)(2,1)S(1)}, bf16[64,15,128]{2,1,0:T(8,128)(2,1)}, u32[]{:S(2)}, u32[]{:S(2)}) collective-permute-start(bf16[64,15,128]{2,1,0:T(8,128)(2,1)S(1)} %get-tuple-element.41), channel_id=1, source_target_pairs={{4,0},{8,4},{12,8},{5,1},{9,5},{13,9},{6,2},{10,6},{14,10},{7,3},{... | collective-permute-start | bytes 737288 | tf_op jit(solution)/shard_map/ppermute | solution.py:34
  44.7 9.4 %copy-start = (bf16[64,32,62]{2,1,0:T(8,128)(2,1)}, bf16[64,32,62]{2,1,0:T(8,128)(2,1)S(1)}, u32[]{:S(2)}) copy-start(bf16[64,32,62]{2,1,0:T(8,128)(2,1)S(1)} %broadcast_in_dim.152) | copy-start | bytes 761860
  54.1 4.9 %collective-permute-start.8 = (bf16[15,32,128]{2,1,0:T(8,128)(2,1)S(1)}, bf16[15,32,128]{2,1,0:T(8,128)(2,1)S(1)}, u32[]{:S(2)}, u32[]{:S(2)}) collective-permute-start(bf16[15,32,128]{2,1,0:T(8,128)(2,1)S(1)} %constant_dynamic-slice_fusion.6), channel_id=1, source_target_pairs={{0,2},{2,0},{1,3},{3,1},{4,6},{6,4},{5,7},{7,5},{8,10},{10,8},{9,1... | collective-permute-start | bytes 368648 | tf_op jit(solution)/shard_map/ppermute | solution.py:95
  60.3 2.7 %collective-permute-start.9 = (f32[64,32,128]{2,1,0:T(8,128)S(1)}, f32[64,32,128]{2,1,0:T(8,128)S(1)}, u32[]{:S(2)}, u32[]{:S(2)}) collective-permute-start(f32[64,32,128]{2,1,0:T(8,128)S(1)} %copy.21), channel_id=1, source_target_pairs={{0,1},{1,0},{2,3},{3,2},{4,5},{5,4},{6,7},{7,6},{8,9},{9,8},{10,11... | collective-permute-start | bytes 3145736 | tf_op jit(solution)/shard_map/ppermute | solution.py:23
  63.9 8.3 %collective-permute-start.10 = (bf16[64,15,128]{2,1,0:T(8,128)(2,1)S(1)}, bf16[64,15,128]{2,1,0:T(8,128)(2,1)S(1)}, u32[]{:S(2)}, u32[]{:S(2)}) collective-permute-start(bf16[64,15,128]{2,1,0:T(8,128)(2,1)S(1)} %constant_dynamic-slice_fusion.5), channel_id=1, source_target_pairs={{0,4},{4,0},{8,12},{12,8},{5,9},{9,5},{2,6},{6,2},{10,14},{14,10},... | collective-permute-start | bytes 737288 | tf_op jit(solution)/shard_map/ppermute | solution.py:51
  72.2 1.5 %collective-permute-start.11 = (bf16[64,15,128]{2,1,0:T(8,128)(2,1)S(1)}, bf16[64,15,128]{2,1,0:T(8,128)(2,1)S(1)}, u32[]{:S(2)}, u32[]{:S(2)}) collective-permute-start(bf16[64,15,128]{2,1,0:T(8,128)(2,1)S(1)} %collective-permute-done.10), channel_id=1, source_target_pairs={{0,1},{1,0},{2,3},{3,2},{4,5},{5,4},{6,7},{7,6},{8,9},{9,8},{10,11... | collective-permute-start | bytes 737288 | tf_op jit(solution)/shard_map/ppermute | solution.py:23
  76.0 5.4 %collective-permute-start.12 = (bf16[15,32,128]{2,1,0:T(8,128)(2,1)S(1)}, bf16[15,32,128]{2,1,0:T(8,128)(2,1)S(1)}, u32[]{:S(2)}, u32[]{:S(2)}) collective-permute-start(bf16[15,32,128]{2,1,0:T(8,128)(2,1)S(1)} %constant_dynamic-slice_fusion.4), channel_id=1, source_target_pairs={{0,2},{2,0},{1,3},{3,1},{4,6},{6,4},{5,7},{7,5},{8,10},{10,8},{9,1... | collective-permute-start | bytes 368648 | tf_op jit(solution)/shard_map/ppermute | solution.py:95
  82.7 12.9 %copy-start.1 = (bf16[64,32,62]{2,1,0:T(8,128)(2,1)S(1)}, bf16[64,32,62]{2,1,0:T(8,128)(2,1)}, u32[]{:S(2)}) copy-start(bf16[64,32,62]{2,1,0:T(8,128)(2,1)} %copy-done) | copy-start | bytes 761860
  82.8 8.6 %collective-permute-start.13 = (bf16[64,15,128]{2,1,0:T(8,128)(2,1)S(1)}, bf16[64,15,128]{2,1,0:T(8,128)(2,1)S(1)}, u32[]{:S(2)}, u32[]{:S(2)}) collective-permute-start(bf16[64,15,128]{2,1,0:T(8,128)(2,1)S(1)} %get-tuple-element.36), channel_id=1, source_target_pairs={{0,4},{4,8},{8,12},{1,5},{5,9},{9,13},{2,6},{6,10},{10,14},{3,7},{... | collective-permute-start | bytes 737288 | tf_op jit(solution)/shard_map/ppermute | solution.py:31
  86.5 9.1 %collective-permute-start.14 = (bf16[64,15,128]{2,1,0:T(8,128)(2,1)S(1)}, bf16[64,15,128]{2,1,0:T(8,128)(2,1)S(1)}, u32[]{:S(2)}, u32[]{:S(2)}) collective-permute-start(bf16[64,15,128]{2,1,0:T(8,128)(2,1)S(1)} %get-tuple-element.37), channel_id=1, source_target_pairs={{4,0},{8,4},{12,8},{5,1},{9,5},{13,9},{6,2},{10,6},{14,10},{7,3},{... | collective-permute-start | bytes 737288 | tf_op jit(solution)/shard_map/ppermute | solution.py:34
  96.2 4.9 %collective-permute-start.15 = (bf16[15,32,128]{2,1,0:T(8,128)(2,1)S(1)}, bf16[15,32,128]{2,1,0:T(8,128)(2,1)S(1)}, u32[]{:S(2)}, u32[]{:S(2)}) collective-permute-start(bf16[15,32,128]{2,1,0:T(8,128)(2,1)S(1)} %constant_dynamic-slice_fusion.3), channel_id=1, source_target_pairs={{0,2},{2,0},{1,3},{3,1},{4,6},{6,4},{5,7},{7,5},{8,10},{10,8},{9,1... | collective-permute-start | bytes 368648 | tf_op jit(solution)/shard_map/ppermute | solution.py:95
  102.2 2.0 %collective-permute-start.16 = (f32[32,32,128]{2,1,0:T(8,128)S(1)}, f32[32,32,128]{2,1,0:T(8,128)S(1)}, u32[]{:S(2)}, u32[]{:S(2)}) collective-permute-start(f32[32,32,128]{2,1,0:T(8,128)S(1)} %copy.28), channel_id=1, source_target_pairs={{0,1},{1,0},{2,3},{3,2},{4,5},{5,4},{6,7},{7,6},{8,9},{9,8},{10,11... | collective-permute-start | bytes 1572872 | tf_op jit(solution)/shard_map/ppermute | solution.py:23

commit v6 on v2

--- a/solution.py
+++ b/solution.py
@@ -57,24 +57,63 @@
     ))
 
 
-def along_z(volume, matrix, reach):
-    below_rim = shifted(volume[volume.shape[0] - reach :], "view", 2)
-    above_rim = shifted(volume[:reach], "view", -2)
-    extended = jnp.concatenate([below_rim, volume, above_rim], axis=0)
-    planes = extended.shape[0]
-    flat = extended.reshape(planes, -1)
-    out = jnp.dot(matrix, flat, preferred_element_type=jnp.float32)
-    return out.reshape(volume.shape)
-
-
-def separable(extended, matrices, reach):
+def pass_xy(extended, matrices):
     width_y = extended.shape[2]
     after_x = jnp.einsum(
         "zpa,zay->zpy", matrices[0], extended, preferred_element_type=jnp.float32
     ).astype(jnp.bfloat16)
     after_y = jnp.dot(after_x.reshape(-1, width_y), matrices[1], preferred_element_type=jnp.float32)
-    after_y = after_y.reshape(after_x.shape).astype(jnp.bfloat16)
-    return along_z(after_y, matrices[2], reach)
+    return after_y.reshape(after_x.shape).astype(jnp.bfloat16)
+
+
+def pass_z(extended, matrix):
+    planes = extended.shape[0]
+    out = jnp.dot(matrix, extended.reshape(planes, -1), preferred_element_type=jnp.float32)
+    return out.reshape((matrix.shape[0],) + extended.shape[1:])
+
+
+def z_rims(volume, reach, axis):
+    slabs = lax.axis_size("view") // 2
+    slab = lax.axis_index("view") // 2
+    planes = volume.shape[axis]
+    shape = list(volume.shape)
+    shape[axis] = reach
+    below = jnp.zeros(shape, volume.dtype)
+    above = below
+    for phase in (0, 1):
+        route = []
+        for low in range(phase, slabs - 1, 2):
+            for bit in (0, 1):
+                route += [(2 * low + bit, 2 * low + 2 + bit), (2 * low + 2 + bit, 2 * low + bit)]
+        if not route:
+            continue
+        is_lower = slab % 2 == phase
+        start = jnp.where(is_lower, planes - reach, 0)
+        payload = lax.dynamic_slice_in_dim(volume, start, reach, axis)
+        got = lax.ppermute(payload, "view", route)
+        below = jnp.where(is_lower, below, got)
+        above = jnp.where(is_lower, got, above)
+    return below, above
+
+
+def x_rims(block, reach, axis):
+    tiles = lax.axis_size("tile")
+    views = lax.axis_size("view")
+    route = []
+    for tile in range(tiles - 1):
+        for slab in range(views // 2):
+            right_core = tile * views + 2 * slab + 1
+            left_core = (tile + 1) * views + 2 * slab
+            route += [(right_core, left_core), (left_core, right_core)]
+    first = lax.axis_index("view") % 2 == 0
+    width = block.shape[axis]
+    outward = lax.dynamic_slice_in_dim(block, jnp.where(first, 0, width - reach), reach, axis)
+    inward = lax.dynamic_slice_in_dim(block, jnp.where(first, width - reach, 0), reach, axis)
+    across = lax.ppermute(outward, ("tile", "view"), route)
+    beside = from_partner(inward, "view", 0)
+    low = jnp.where(first, across, beside)
+    high = jnp.where(first, beside, across)
+    return low, high
 
 
 def local(acquired, psf_taps, block_source):
@@ -116,33 +155,47 @@
         jnp.where(from_right, block_count + capacity + right_order, source_blocks),
     )
     measured = jnp.take(candidates, chosen, axis=1).reshape(planes, width_x, width_y)
-    partner_view = from_partner(measured, "view", 0)
-    measured_own = measured.astype(jnp.float32)
-    estimate = 0.5 * (measured_own + partner_view.astype(jnp.float32))
+    half_x = width_x // 2
+    half_rows = planes // 2
+    own_x = lax.dynamic_slice_in_dim(measured, view_bit * half_x, half_x, 1)
+    give_x = lax.dynamic_slice_in_dim(measured, (1 - view_bit) * half_x, half_x, 1)
+    got_x = from_partner(give_x, "view", 0)
+    views_measured = jnp.where(view_bit == 0, jnp.stack([own_x, got_x]), jnp.stack([got_x, own_x]))
+    observed = views_measured.astype(jnp.float32)
+    estimate = 0.5 * (observed[0] + observed[1])
     kernels = (psf_taps / jnp.sum(psf_taps, axis=2, keepdims=True)).astype(jnp.bfloat16)
-    own_kernels = lax.dynamic_index_in_dim(kernels, view_bit, 0, keepdims=False)
-    forward_ops = operators(own_kernels, planes, width_x, width_y)
-    adjoint_ops = operators(own_kernels[:, ::-1], planes, width_x, width_y)
-    half_rows = planes // 2
+    view_count = kernels.shape[0]
+    forward_ops = [operators(kernels[v], planes, half_x, width_y) for v in range(view_count)]
+    adjoint_ops = [operators(kernels[v][:, ::-1], planes, half_x, width_y) for v in range(view_count)]
     for iteration in range(ITERS):
         estimate_low = estimate.astype(jnp.bfloat16)
-        own_half = lax.dynamic_slice_in_dim(estimate_low, view_bit * half_rows, half_rows, 0)
-        widened = extended_2(own_half, (("tile", 1),), reach)
-        rim_stack = jnp.concatenate([widened[:, :reach], widened[:, reach + width_x :]], axis=1)
-        partner_rims = from_partner(rim_stack, "view", 0)
-        all_rims = jnp.where(
-            view_bit == 0,
-            jnp.concatenate([rim_stack, partner_rims], axis=0),
-            jnp.concatenate([partner_rims, rim_stack], axis=0),
-        )
-        extended = jnp.concatenate([all_rims[:, :reach], estimate_low, all_rims[:, reach:]], axis=1)
-        blurred = separable(extended, forward_ops, reach)
-        quotient = (measured_own / blurred).astype(jnp.bfloat16)
-        widened_quotient = extended_2(quotient, (("tile", 1),), reach)
-        back_own = separable(widened_quotient, adjoint_ops, reach)
-        back_partner = from_partner(back_own, "view", 0)
-        estimate = estimate * (0.5 * (back_own + back_partner))
-    return lax.dynamic_slice_in_dim(estimate, view_bit * half_rows, half_rows, 0)
+        low, high = x_rims(estimate_low, reach, 1)
+        extended = jnp.concatenate([low, estimate_low, high], axis=1)
+        after_xy = jnp.stack([pass_xy(extended, forward_ops[v]) for v in range(view_count)])
+        below, above = z_rims(after_xy, reach, 1)
+        quotients = []
+        for v in range(view_count):
+            widened = jnp.concatenate([below[v], after_xy[v], above[v]], axis=0)
+            blurred = pass_z(widened, forward_ops[v][2])
+            quotients.append((observed[v] / blurred).astype(jnp.bfloat16))
+        quotients = jnp.stack(quotients)
+        low, high = x_rims(quotients, reach, 2)
+        after_xy = jnp.stack([
+            pass_xy(jnp.concatenate([low[v], quotients[v], high[v]], axis=1), adjoint_ops[v])
+            for v in range(view_count)
+        ])
+        below, above = z_rims(after_xy, reach, 1)
+        backs = [
+            pass_z(jnp.concatenate([below[v], after_xy[v], above[v]], axis=0), adjoint_ops[v][2])
+            for v in range(view_count)
+        ]
+        estimate = estimate * (0.5 * (backs[0] + backs[1]))
+    keep = lax.dynamic_slice_in_dim(estimate, view_bit * half_rows, half_rows, 0)
+    give = lax.dynamic_slice_in_dim(estimate, (1 - view_bit) * half_rows, half_rows, 0)
+    got = from_partner(give, "view", 0)
+    return jnp.where(
+        view_bit == 0, jnp.concatenate([keep, got], axis=1), jnp.concatenate([got, keep], axis=1)
+    )
 
 
 def solution(mesh):

time: 123 us -> 101 us (0.82)
  waiting for transfers between devices: 65.3 us -> 24.9 us
  starting transfers between devices: 36.1 us -> 44.7 us
  other arithmetic: 7.93 us -> 11.4 us
  matrix products: 5.85 us -> 9.27 us
  local copies, waits for them, and re-layouts: 6.95 us -> 8.65 us
    ppermute x5 -> x6, starting transfers between devices: 0.36 us -> 29.4 us  [from_partner(): return lax.ppermute(block, axis, route)]
    ppermute x10 -> x2, waiting for transfers between devices: 29 us -> 6.2 us  [shifted(): return lax.ppermute(block, axis, route)]
    ppermute x8, waiting for transfers between devices: 26.6 us -> 13 us  [the longest x4 13 us: z_rims(): got = lax.ppermute(payload, 'view', route)]
    ppermute x10 -> x2, starting transfers between devices: 19.1 us -> 6.24 us  [shifted(): return lax.ppermute(block, axis, route)]
    ppermute x8, starting transfers between devices: 16.7 us -> 9.13 us  [the longest x4 6.22 us: z_rims(): got = lax.ppermute(payload, 'view', route)]
    ppermute x5 -> x6, waiting for transfers between devices: 9.68 us -> 5.72 us  [from_partner(): return lax.ppermute(block, axis, route)]
    dot_general x8 -> x16, matrix products: 5.85 us -> 9.27 us  [the longest x8 7.49 us: pass_xy(): jnp.dot(after_x.reshape(-1, width_y), matrices[1], preferred_element_type...]
    unnamed x9 -> x65, local copies, waits for them, and re-layouts: 1.27 us -> 3.87 us
  transfers between devices with their start and end apart: 23 -> 16, of which waited for: 23 -> 11; matrix products, arithmetic and copies ran while one was open for 3% -> 6% of each run, Pallas kernels for 0% -> 0%
where the time goes in v6:
time: 101 us; the launch traced here: 100 us
  starting transfers between devices  44.7 us (44%)
  waiting for transfers between devices  24.9 us (25%)
  other arithmetic  11.4 us (11%)
  matrix products  9.27 us (9%)
  local copies, waits for them, and re-layouts  8.65 us (9%)
  between operations  1.17 us (1%)
    ppermute x6, starting transfers between devices, from_partner(): return lax.ppermute(block, axis, route)  29.4 us
    ppermute x4, waiting for transfers between devices, z_rims(): got = lax.ppermute(payload, 'view', route)  13 us
    dot_general x8, matrix products, pass_xy(): jnp.dot(after_x.reshape(-1, width_y), matrices[1], preferred_element_type...  7.49 us
    ppermute x2, starting transfers between devices, shifted(): return lax.ppermute(block, axis, route)  6.24 us
    ppermute x4, starting transfers between devices, z_rims(): got = lax.ppermute(payload, 'view', route)  6.22 us
    ppermute x2, waiting for transfers between devices, shifted(): return lax.ppermute(block, axis, route)  6.2 us
    ppermute x6, waiting for transfers between devices, from_partner(): return lax.ppermute(block, axis, route)  5.72 us
    unnamed x65, local copies, waits for them, and re-layouts  3.87 us
  transfers between devices with their start and end apart: 16, of which 11 were waited for; matrix products, arithmetic and copies ran while one was open for 6% of the time, Pallas kernels for 0%

profile of v6, /device:TPU:0, one launch (start us, length us, event | category | flops | bytes accessed | tf_op | source)
XLA Modules:
  0.0 100.1 jit_solution(15074406408654327863)
XLA Ops:
  3.2 4.9 %collective-permute-start = (bf16[64,4,4,128]{3,0,2,1:T(8,128)(2,1)S(1)}, bf16[64,4,4,128]{3,0,2,1:T(8,128)(2,1)S(1)}, u32[]{:S(2)}, u32[]{:S(2)}) collective-permute-start(bf16[64,4,4,128]{3,0,2,1:T(8,128)(2,1)S(1)} %select_bitcast_fusion.1), channel_id=1, source_target_pairs={{0,4},{4,8},{8,12},{1,5},{5,9},{9,13},{2,6},{6,10},{10,14},{3,7},{... | collective-permute-start | bytes 786440 | tf_op jit(solution)/shard_map/ppermute | solution.py:13
  9.2 1.3 %collective-permute-start.1 = (bf16[64,4,4,128]{3,0,2,1:T(8,128)(2,1)S(1)}, bf16[64,4,4,128]{3,0,2,1:T(8,128)(2,1)S(1)}, u32[]{:S(2)}, u32[]{:S(2)}) collective-permute-start(bf16[64,4,4,128]{3,0,2,1:T(8,128)(2,1)S(1)} %select_bitcast_fusion), channel_id=1, source_target_pairs={{4,0},{8,4},{12,8},{5,1},{9,5},{13,9},{6,2},{10,6},{14,10},{7,3},{... | collective-permute-start | bytes 786440 | tf_op jit(solution)/shard_map/ppermute | solution.py:13
  13.6 5.2 %collective-permute-done.1 = bf16[64,4,4,128]{3,0,2,1:T(8,128)(2,1)S(1)} collective-permute-done((bf16[64,4,4,128]{3,0,2,1:T(8,128)(2,1)S(1)}, bf16[64,4,4,128]{3,0,2,1:T(8,128)(2,1)S(1)}, u32[]{:S(2)}, u32[]{:S(2)}) %collective-permute-start.1) | collective-permute-done | bytes 262176 | tf_op jit(solution)/shard_map/ppermute | solution.py:13
  20.5 1.3 %collective-permute-done.2 = bf16[64,16,128]{2,1,0:T(8,128)(2,1)S(1)} collective-permute-done((bf16[64,16,128]{2,1,0:T(8,128)(2,1)S(1)}, bf16[64,16,128]{2,1,0:T(8,128)(2,1)S(1)}, u32[]{:S(2)}, u32[]{:S(2)}) %collective-permute-start.2) | collective-permute-done | bytes 262176 | tf_op jit(solution)/shard_map/ppermute | solution.py:23
  22.9 3.0 %collective-permute-start.4 = (bf16[64,15,128]{2,1,0:T(8,128)(2,1)S(1)}, bf16[64,15,128]{2,1,0:T(8,128)(2,1)S(1)}, u32[]{:S(2)}, u32[]{:S(2)}) collective-permute-start(bf16[64,15,128]{2,1,0:T(8,128)(2,1)S(1)} %get-tuple-element.83), channel_id=1, source_target_pairs={{0,1},{1,0},{2,3},{3,2},{4,5},{5,4},{6,7},{7,6},{8,9},{9,8},{10,11... | collective-permute-start | bytes 737288 | tf_op jit(solution)/shard_map/ppermute | solution.py:23
  25.8 1.7 %select_reduce_fusion = (bf16[128,128]{1,0:T(8,128)(2,1)S(1)}, bf16[128,128]{1,0:T(8,128)(2,1)}, bf16[128,128]{1,0:T(8,128)(2,1)}, bf16[128,128]{1,0:T(8,128)(2,1)S(1)}) fusion(f32[31]{0:T(128)S(1)} %get-tuple-element.127, s32[128,128]{1,0:T(8,128)S(1)} %subtract_add_fusion, f32[31]{0:T(128)S(1)} %get-tuple-element.116, f32[31]{0:T(128)S(1)} %get-tuple-element.110, ...), kind=kLoop, calls=%fused_computation.3 | loop fusion | flops 4505600 | bytes 197104 | tf_op jit(solution)/shard_map/reduce_sum | solution.py:45
  29.6 1.6 %collective-permute-start.5 = (bf16[2,15,16,128]{3,2,1,0:T(8,128)(2,1)S(1)}, bf16[2,15,16,128]{3,2,1,0:T(8,128)(2,1)S(1)}, u32[]{:S(2)}, u32[]{:S(2)}) collective-permute-start(bf16[2,15,16,128]{3,2,1,0:T(8,128)(2,1)S(1)} %fusion.73), channel_id=1, source_target_pairs={{0,2},{2,0},{1,3},{3,1},{4,6},{6,4},{5,7},{7,5},{8,10},{10,8},{9,1... | collective-permute-start | bytes 368648 | tf_op jit(solution)/shard_map/ppermute | solution.py:93
  31.3 3.2 %collective-permute-done.5 = bf16[2,15,16,128]{3,2,1,0:T(8,128)(2,1)S(1)} collective-permute-done((bf16[2,15,16,128]{3,2,1,0:T(8,128)(2,1)S(1)}, bf16[2,15,16,128]{3,2,1,0:T(8,128)(2,1)S(1)}, u32[]{:S(2)}, u32[]{:S(2)}) %collective-permute-start.5) | collective-permute-done | bytes 122912 | tf_op jit(solution)/shard_map/ppermute | solution.py:93
  37.4 5.7 %collective-permute-start.7 = (bf16[2,64,15,128]{3,2,1,0:T(8,128)(2,1)S(1)}, bf16[2,64,15,128]{3,2,1,0:T(8,128)(2,1)S(1)}, u32[]{:S(2)}, u32[]{:S(2)}) collective-permute-start(bf16[2,64,15,128]{3,2,1,0:T(8,128)(2,1)S(1)} %get-tuple-element.75), channel_id=1, source_target_pairs={{0,1},{1,0},{2,3},{3,2},{4,5},{5,4},{6,7},{7,6},{8,9},{9,8},{10,11... | collective-permute-start | bytes 1474568 | tf_op jit(solution)/shard_map/ppermute | solution.py:23
  43.2 1.4 %collective-permute-done.7 = bf16[2,64,15,128]{3,2,1,0:T(8,128)(2,1)S(1)} collective-permute-done((bf16[2,64,15,128]{3,2,1,0:T(8,128)(2,1)S(1)}, bf16[2,64,15,128]{3,2,1,0:T(8,128)(2,1)S(1)}, u32[]{:S(2)}, u32[]{:S(2)}) %collective-permute-start.7) | collective-permute-done | bytes 491552 | tf_op jit(solution)/shard_map/ppermute | solution.py:23
  45.6 1.4 %convolution_convert_fusion.4 = bf16[64,16,128]{2,1,0:T(8,128)(2,1)S(1)} fusion(bf16[64,16,46]{2,1,0:T(8,128)(2,1)S(1)} %broadcast_in_dim.247, bf16[64,15,128]{2,1,0:T(8,128)(2,1)} %get-tuple-element.72, bf16[64,16,128]{2,1,0:T(8,128)(2,1)S(1)} %get-tuple-element.58, bf16[64,15,128]{2,1,0:T(8,128)(2,1)S(1)} %get-tuple-element.70, ...), kind=kOutput, calls=%fused_computation.12 | convolution fusion | flops 48136192 | bytes 1142784 | tf_op jit(solution)/shard_map/dot_general | solution.py:65
  47.0 1.4 %convolution_convert_fusion.5 = bf16[64,16,128]{2,1,0:T(8,128)(2,1)S(1)} fusion(bf16[64,16,46]{2,1,0:T(8,128)(2,1)S(1)} %broadcast_in_dim.221, bf16[64,15,128]{2,1,0:T(8,128)(2,1)} %get-tuple-element.73, bf16[64,16,128]{2,1,0:T(8,128)(2,1)S(1)} %get-tuple-element.59, bf16[64,15,128]{2,1,0:T(8,128)(2,1)S(1)} %get-tuple-element.71, ...), kind=kOutput, calls=%fused_computation.13 | convolution fusion | flops 48136192 | bytes 1142784 | tf_op jit(solution)/shard_map/dot_general | solution.py:65
  48.5 1.6 %collective-permute-start.8 = (bf16[2,15,16,128]{3,2,1,0:T(8,128)(2,1)S(1)}, bf16[2,15,16,128]{3,2,1,0:T(8,128)(2,1)S(1)}, u32[]{:S(2)}, u32[]{:S(2)}) collective-permute-start(bf16[2,15,16,128]{3,2,1,0:T(8,128)(2,1)S(1)} %fusion.72), channel_id=1, source_target_pairs={{0,2},{2,0},{1,3},{3,1},{4,6},{6,4},{5,7},{7,5},{8,10},{10,8},{9,1... | collective-permute-start | bytes 368648 | tf_op jit(solution)/shard_map/ppermute | solution.py:93
  50.2 3.2 %collective-permute-done.8 = bf16[2,15,16,128]{3,2,1,0:T(8,128)(2,1)S(1)} collective-permute-done((bf16[2,15,16,128]{3,2,1,0:T(8,128)(2,1)S(1)}, bf16[2,15,16,128]{3,2,1,0:T(8,128)(2,1)S(1)}, u32[]{:S(2)}, u32[]{:S(2)}) %collective-permute-start.8) | collective-permute-done | bytes 122912 | tf_op jit(solution)/shard_map/ppermute | solution.py:93
  55.4 4.2 %collective-permute-start.10 = (bf16[64,15,128]{2,1,0:T(8,128)(2,1)S(1)}, bf16[64,15,128]{2,1,0:T(8,128)(2,1)S(1)}, u32[]{:S(2)}, u32[]{:S(2)}) collective-permute-start(bf16[64,15,128]{2,1,0:T(8,128)(2,1)S(1)} %get-tuple-element.81), channel_id=1, source_target_pairs={{0,1},{1,0},{2,3},{3,2},{4,5},{5,4},{6,7},{7,6},{8,9},{9,8},{10,11... | collective-permute-start | bytes 737288 | tf_op jit(solution)/shard_map/ppermute | solution.py:23
  61.5 1.4 %convolution_convert_fusion.2 = bf16[64,16,128]{2,1,0:T(8,128)(2,1)S(1)} fusion(bf16[64,16,46]{2,1,0:T(8,128)(2,1)S(1)} %broadcast_in_dim.239, bf16[64,15,128]{2,1,0:T(8,128)(2,1)} %get-tuple-element.69, bf16[64,16,128]{2,1,0:T(8,128)(2,1)S(1)} %get-tuple-element.42, bf16[64,15,128]{2,1,0:T(8,128)(2,1)S(1)} %get-tuple-element.68, ...), kind=kOutput, calls=%fused_computation.10 | convolution fusion | flops 48136192 | bytes 1142784 | tf_op jit(solution)/shard_map/dot_general | solution.py:65
  62.9 1.4 %convolution_convert_fusion.3 = bf16[64,16,128]{2,1,0:T(8,128)(2,1)S(1)} fusion(bf16[64,16,46]{2,1,0:T(8,128)(2,1)S(1)} %broadcast_in_dim.229, bf16[64,15,128]{2,1,0:T(8,128)(2,1)} %get-tuple-element.69, bf16[64,16,128]{2,1,0:T(8,128)(2,1)S(1)} %get-tuple-element.42, bf16[64,15,128]{2,1,0:T(8,128)(2,1)S(1)} %get-tuple-element.68, ...), kind=kOutput, calls=%fused_computation.11 | convolution fusion | flops 48136192 | bytes 1142784 | tf_op jit(solution)/shard_map/dot_general | solution.py:65
  64.4 1.6 %collective-permute-start.11 = (bf16[2,15,16,128]{3,2,1,0:T(8,128)(2,1)S(1)}, bf16[2,15,16,128]{3,2,1,0:T(8,128)(2,1)S(1)}, u32[]{:S(2)}, u32[]{:S(2)}) collective-permute-start(bf16[2,15,16,128]{3,2,1,0:T(8,128)(2,1)S(1)} %fusion.71), channel_id=1, source_target_pairs={{0,2},{2,0},{1,3},{3,1},{4,6},{6,4},{5,7},{7,5},{8,10},{10,8},{9,1... | collective-permute-start | bytes 368648 | tf_op jit(solution)/shard_map/ppermute | solution.py:93
  66.1 3.2 %collective-permute-done.11 = bf16[2,15,16,128]{3,2,1,0:T(8,128)(2,1)S(1)} collective-permute-done((bf16[2,15,16,128]{3,2,1,0:T(8,128)(2,1)S(1)}, bf16[2,15,16,128]{3,2,1,0:T(8,128)(2,1)S(1)}, u32[]{:S(2)}, u32[]{:S(2)}) %collective-permute-start.11) | collective-permute-done | bytes 122912 | tf_op jit(solution)/shard_map/ppermute | solution.py:93
  72.2 12.0 %collective-permute-start.13 = (bf16[2,64,15,128]{3,2,1,0:T(8,128)(2,1)S(1)}, bf16[2,64,15,128]{3,2,1,0:T(8,128)(2,1)S(1)}, u32[]{:S(2)}, u32[]{:S(2)}) collective-permute-start(bf16[2,64,15,128]{3,2,1,0:T(8,128)(2,1)S(1)} %get-tuple-element.67), channel_id=1, source_target_pairs={{0,1},{1,0},{2,3},{3,2},{4,5},{5,4},{6,7},{7,6},{8,9},{9,8},{10,11... | collective-permute-start | bytes 1474568 | tf_op jit(solution)/shard_map/ppermute | solution.py:23
  84.2 1.5 %collective-permute-done.13 = bf16[2,64,15,128]{3,2,1,0:T(8,128)(2,1)S(1)} collective-permute-done((bf16[2,64,15,128]{3,2,1,0:T(8,128)(2,1)S(1)}, bf16[2,64,15,128]{3,2,1,0:T(8,128)(2,1)S(1)}, u32[]{:S(2)}, u32[]{:S(2)}) %collective-permute-start.13) | collective-permute-done | bytes 491552 | tf_op jit(solution)/shard_map/ppermute | solution.py:23
  86.9 1.6 %collective-permute-start.14 = (bf16[2,15,16,128]{3,2,1,0:T(8,128)(2,1)S(1)}, bf16[2,15,16,128]{3,2,1,0:T(8,128)(2,1)S(1)}, u32[]{:S(2)}, u32[]{:S(2)}) collective-permute-start(bf16[2,15,16,128]{3,2,1,0:T(8,128)(2,1)S(1)} %fusion.70), channel_id=1, source_target_pairs={{0,2},{2,0},{1,3},{3,1},{4,6},{6,4},{5,7},{7,5},{8,10},{10,8},{9,1... | collective-permute-start | bytes 368648 | tf_op jit(solution)/shard_map/ppermute | solution.py:93
  88.6 3.2 %collective-permute-done.14 = bf16[2,15,16,128]{3,2,1,0:T(8,128)(2,1)S(1)} collective-permute-done((bf16[2,15,16,128]{3,2,1,0:T(8,128)(2,1)S(1)}, bf16[2,15,16,128]{3,2,1,0:T(8,128)(2,1)S(1)}, u32[]{:S(2)}, u32[]{:S(2)}) %collective-permute-start.14) | collective-permute-done | bytes 122912 | tf_op jit(solution)/shard_map/ppermute | solution.py:93
  93.6 4.5 %collective-permute-start.15 = (f32[32,16,128]{2,1,0:T(8,128)S(1)}, f32[32,16,128]{2,1,0:T(8,128)S(1)}, u32[]{:S(2)}, u32[]{:S(2)}) collective-permute-start(f32[32,16,128]{2,1,0:T(8,128)S(1)} %get-tuple-element.61), channel_id=1, source_target_pairs={{0,1},{1,0},{2,3},{3,2},{4,5},{5,4},{6,7},{7,6},{8,9},{9,8},{10,11... | collective-permute-start | bytes 786440 | tf_op jit(solution)/shard_map/ppermute | solution.py:23
  (188 shorter events, 27.5 us)
Async XLA Ops:
  2.4 8.0 %copy-start.2 = (s32[1,32]{1,0:T(1,128)S(1)}, s32[1,32]{1,0:T(1,128)}, u32[]{:S(2)}) copy-start(s32[1,32]{1,0:T(1,128)} %param.7) | copy-start | bytes 388
  2.4 8.9 %copy-start.3 = (f32[2,3,31]{2,0,1:T(2,128)S(1)}, f32[2,3,31]{2,0,1:T(2,128)}, u32[]{:S(2)}) copy-start(f32[2,3,31]{2,0,1:T(2,128)} %param.6) | copy-start | bytes 2236
  3.2 10.5 %collective-permute-start = (bf16[64,4,4,128]{3,0,2,1:T(8,128)(2,1)S(1)}, bf16[64,4,4,128]{3,0,2,1:T(8,128)(2,1)S(1)}, u32[]{:S(2)}, u32[]{:S(2)}) collective-permute-start(bf16[64,4,4,128]{3,0,2,1:T(8,128)(2,1)S(1)} %select_bitcast_fusion.1), channel_id=1, source_target_pairs={{0,4},{4,8},{8,12},{1,5},{5,9},{9,13},{2,6},{6,10},{10,14},{3,7},{... | collective-permute-start | bytes 786440 | tf_op jit(solution)/shard_map/ppermute | solution.py:13
  9.2 9.7 %collective-permute-start.1 = (bf16[64,4,4,128]{3,0,2,1:T(8,128)(2,1)S(1)}, bf16[64,4,4,128]{3,0,2,1:T(8,128)(2,1)S(1)}, u32[]{:S(2)}, u32[]{:S(2)}) collective-permute-start(bf16[64,4,4,128]{3,0,2,1:T(8,128)(2,1)S(1)} %select_bitcast_fusion), channel_id=1, source_target_pairs={{4,0},{8,4},{12,8},{5,1},{9,5},{13,9},{6,2},{10,6},{14,10},{7,3},{... | collective-permute-start | bytes 786440 | tf_op jit(solution)/shard_map/ppermute | solution.py:13
  20.2 1.6 %collective-permute-start.2 = (bf16[64,16,128]{2,1,0:T(8,128)(2,1)S(1)}, bf16[64,16,128]{2,1,0:T(8,128)(2,1)S(1)}, u32[]{:S(2)}, u32[]{:S(2)}) collective-permute-start(bf16[64,16,128]{2,1,0:T(8,128)(2,1)S(1)} %get-tuple-element.79), channel_id=1, source_target_pairs={{0,1},{1,0},{2,3},{3,2},{4,5},{5,4},{6,7},{7,6},{8,9},{9,8},{10,11... | collective-permute-start | bytes 786440 | tf_op jit(solution)/shard_map/ppermute | solution.py:23
  22.2 5.4 %collective-permute-start.3 = (bf16[64,15,128]{2,1,0:T(8,128)(2,1)S(1)}, bf16[64,15,128]{2,1,0:T(8,128)(2,1)S(1)}, u32[]{:S(2)}, u32[]{:S(2)}) collective-permute-start(bf16[64,15,128]{2,1,0:T(8,128)(2,1)S(1)} %get-tuple-element.82), channel_id=1, source_target_pairs={{1,4},{4,1},{3,6},{6,3},{5,8},{8,5},{7,10},{10,7},{9,12},{12,9},{1... | collective-permute-start | bytes 737288 | tf_op jit(solution)/shard_map/ppermute | solution.py:112
  22.9 4.8 %collective-permute-start.4 = (bf16[64,15,128]{2,1,0:T(8,128)(2,1)S(1)}, bf16[64,15,128]{2,1,0:T(8,128)(2,1)S(1)}, u32[]{:S(2)}, u32[]{:S(2)}) collective-permute-start(bf16[64,15,128]{2,1,0:T(8,128)(2,1)S(1)} %get-tuple-element.83), channel_id=1, source_target_pairs={{0,1},{1,0},{2,3},{3,2},{4,5},{5,4},{6,7},{7,6},{8,9},{9,8},{10,11... | collective-permute-start | bytes 737288 | tf_op jit(solution)/shard_map/ppermute | solution.py:23
  27.6 0.8 copy-start.1
  28.4 0.8 copy-start
  29.6 4.9 %collective-permute-start.5 = (bf16[2,15,16,128]{3,2,1,0:T(8,128)(2,1)S(1)}, bf16[2,15,16,128]{3,2,1,0:T(8,128)(2,1)S(1)}, u32[]{:S(2)}, u32[]{:S(2)}) collective-permute-start(bf16[2,15,16,128]{3,2,1,0:T(8,128)(2,1)S(1)} %fusion.73), channel_id=1, source_target_pairs={{0,2},{2,0},{1,3},{3,1},{4,6},{6,4},{5,7},{7,5},{8,10},{10,8},{9,1... | collective-permute-start | bytes 368648 | tf_op jit(solution)/shard_map/ppermute | solution.py:93
  36.7 6.5 %collective-permute-start.6 = (bf16[2,64,15,128]{3,2,1,0:T(8,128)(2,1)S(1)}, bf16[2,64,15,128]{3,2,1,0:T(8,128)(2,1)S(1)}, u32[]{:S(2)}, u32[]{:S(2)}) collective-permute-start(bf16[2,64,15,128]{3,2,1,0:T(8,128)(2,1)S(1)} %get-tuple-element.74), channel_id=1, source_target_pairs={{1,4},{4,1},{3,6},{6,3},{5,8},{8,5},{7,10},{10,7},{9,12},{12,9},{1... | collective-permute-start | bytes 1474568 | tf_op jit(solution)/shard_map/ppermute | solution.py:112
  37.4 7.2 %collective-permute-start.7 = (bf16[2,64,15,128]{3,2,1,0:T(8,128)(2,1)S(1)}, bf16[2,64,15,128]{3,2,1,0:T(8,128)(2,1)S(1)}, u32[]{:S(2)}, u32[]{:S(2)}) collective-permute-start(bf16[2,64,15,128]{3,2,1,0:T(8,128)(2,1)S(1)} %get-tuple-element.75), channel_id=1, source_target_pairs={{0,1},{1,0},{2,3},{3,2},{4,5},{5,4},{6,7},{7,6},{8,9},{9,8},{10,11... | collective-permute-start | bytes 1474568 | tf_op jit(solution)/shard_map/ppermute | solution.py:23
  48.5 4.9 %collective-permute-start.8 = (bf16[2,15,16,128]{3,2,1,0:T(8,128)(2,1)S(1)}, bf16[2,15,16,128]{3,2,1,0:T(8,128)(2,1)S(1)}, u32[]{:S(2)}, u32[]{:S(2)}) collective-permute-start(bf16[2,15,16,128]{3,2,1,0:T(8,128)(2,1)S(1)} %fusion.72), channel_id=1, source_target_pairs={{0,2},{2,0},{1,3},{3,1},{4,6},{6,4},{5,7},{7,5},{8,10},{10,8},{9,1... | collective-permute-start | bytes 368648 | tf_op jit(solution)/shard_map/ppermute | solution.py:93
  55.4 5.3 %collective-permute-start.10 = (bf16[64,15,128]{2,1,0:T(8,128)(2,1)S(1)}, bf16[64,15,128]{2,1,0:T(8,128)(2,1)S(1)}, u32[]{:S(2)}, u32[]{:S(2)}) collective-permute-start(bf16[64,15,128]{2,1,0:T(8,128)(2,1)S(1)} %get-tuple-element.81), channel_id=1, source_target_pairs={{0,1},{1,0},{2,3},{3,2},{4,5},{5,4},{6,7},{7,6},{8,9},{9,8},{10,11... | collective-permute-start | bytes 737288 | tf_op jit(solution)/shard_map/ppermute | solution.py:23
  59.6 1.2 %collective-permute-start.9 = (bf16[64,15,128]{2,1,0:T(8,128)(2,1)S(1)}, bf16[64,15,128]{2,1,0:T(8,128)(2,1)S(1)}, u32[]{:S(2)}, u32[]{:S(2)}) collective-permute-start(bf16[64,15,128]{2,1,0:T(8,128)(2,1)S(1)} %get-tuple-element.80), channel_id=1, source_target_pairs={{1,4},{4,1},{3,6},{6,3},{5,8},{8,5},{7,10},{10,7},{9,12},{12,9},{1... | collective-permute-start | bytes 737288 | tf_op jit(solution)/shard_map/ppermute | solution.py:112
  64.4 4.9 %collective-permute-start.11 = (bf16[2,15,16,128]{3,2,1,0:T(8,128)(2,1)S(1)}, bf16[2,15,16,128]{3,2,1,0:T(8,128)(2,1)S(1)}, u32[]{:S(2)}, u32[]{:S(2)}) collective-permute-start(bf16[2,15,16,128]{3,2,1,0:T(8,128)(2,1)S(1)} %fusion.71), channel_id=1, source_target_pairs={{0,2},{2,0},{1,3},{3,1},{4,6},{6,4},{5,7},{7,5},{8,10},{10,8},{9,1... | collective-permute-start | bytes 368648 | tf_op jit(solution)/shard_map/ppermute | solution.py:93
  71.5 12.7 %collective-permute-start.12 = (bf16[2,64,15,128]{3,2,1,0:T(8,128)(2,1)S(1)}, bf16[2,64,15,128]{3,2,1,0:T(8,128)(2,1)S(1)}, u32[]{:S(2)}, u32[]{:S(2)}) collective-permute-start(bf16[2,64,15,128]{3,2,1,0:T(8,128)(2,1)S(1)} %get-tuple-element.66), channel_id=1, source_target_pairs={{1,4},{4,1},{3,6},{6,3},{5,8},{8,5},{7,10},{10,7},{9,12},{12,9},{1... | collective-permute-start | bytes 1474568 | tf_op jit(solution)/shard_map/ppermute | solution.py:112
  72.2 13.5 %collective-permute-start.13 = (bf16[2,64,15,128]{3,2,1,0:T(8,128)(2,1)S(1)}, bf16[2,64,15,128]{3,2,1,0:T(8,128)(2,1)S(1)}, u32[]{:S(2)}, u32[]{:S(2)}) collective-permute-start(bf16[2,64,15,128]{3,2,1,0:T(8,128)(2,1)S(1)} %get-tuple-element.67), channel_id=1, source_target_pairs={{0,1},{1,0},{2,3},{3,2},{4,5},{5,4},{6,7},{7,6},{8,9},{9,8},{10,11... | collective-permute-start | bytes 1474568 | tf_op jit(solution)/shard_map/ppermute | solution.py:23
  86.9 4.9 %collective-permute-start.14 = (bf16[2,15,16,128]{3,2,1,0:T(8,128)(2,1)S(1)}, bf16[2,15,16,128]{3,2,1,0:T(8,128)(2,1)S(1)}, u32[]{:S(2)}, u32[]{:S(2)}) collective-permute-start(bf16[2,15,16,128]{3,2,1,0:T(8,128)(2,1)S(1)} %fusion.70), channel_id=1, source_target_pairs={{0,2},{2,0},{1,3},{3,1},{4,6},{6,4},{5,7},{7,5},{8,10},{10,8},{9,1... | collective-permute-start | bytes 368648 | tf_op jit(solution)/shard_map/ppermute | solution.py:93
  93.6 5.6 %collective-permute-start.15 = (f32[32,16,128]{2,1,0:T(8,128)S(1)}, f32[32,16,128]{2,1,0:T(8,128)S(1)}, u32[]{:S(2)}, u32[]{:S(2)}) collective-permute-start(f32[32,16,128]{2,1,0:T(8,128)S(1)} %get-tuple-element.61), channel_id=1, source_target_pairs={{0,1},{1,0},{2,3},{3,2},{4,5},{5,4},{6,7},{7,6},{8,9},{9,8},{10,11... | collective-permute-start | bytes 786440 | tf_op jit(solution)/shard_map/ppermute | solution.py:23

commit v7 on v6

--- a/solution.py
+++ b/solution.py
@@ -70,6 +70,34 @@
     planes = extended.shape[0]
     out = jnp.dot(matrix, extended.reshape(planes, -1), preferred_element_type=jnp.float32)
     return out.reshape((matrix.shape[0],) + extended.shape[1:])
+
+
+def stacked_operators(kernels, plane_count, width_x, width_y):
+    reach = kernels.shape[2] // 2
+    views = range(kernels.shape[0])
+    along_x = jnp.stack([band_matrix(kernels[v, 0], width_x + 2 * reach, width_x, 0).T for v in views])
+    along_x = jnp.broadcast_to(along_x[:, None], (along_x.shape[0], plane_count) + along_x.shape[1:])
+    return lax.optimization_barrier((
+        along_x,
+        jnp.stack([band_matrix(kernels[v, 1], width_y, width_y, reach) for v in views]),
+        jnp.stack([band_matrix(kernels[v, 2], plane_count + 2 * reach, plane_count, 0).T for v in views]),
+    ))
+
+
+def pass_y_views(after_x, matrices):
+    shape = after_x.shape
+    flat = after_x.reshape(shape[0], -1, shape[-1])
+    after_y = jnp.einsum("vmy,vyq->vmq", flat, matrices, preferred_element_type=jnp.float32)
+    return after_y.reshape(shape).astype(jnp.bfloat16)
+
+
+def pass_z_views(after_y, matrices, reach):
+    below, above = z_rims(after_y, reach, 1)
+    widened = jnp.concatenate([below, after_y, above], axis=1)
+    shape = widened.shape
+    flat = widened.reshape(shape[0], shape[1], -1)
+    out = jnp.einsum("vpa,vam->vpm", matrices, flat, preferred_element_type=jnp.float32)
+    return out.reshape((shape[0], matrices.shape[1]) + shape[2:])
 
 
 def z_rims(volume, reach, axis):
@@ -165,30 +193,23 @@
     estimate = 0.5 * (observed[0] + observed[1])
     kernels = (psf_taps / jnp.sum(psf_taps, axis=2, keepdims=True)).astype(jnp.bfloat16)
     view_count = kernels.shape[0]
-    forward_ops = [operators(kernels[v], planes, half_x, width_y) for v in range(view_count)]
-    adjoint_ops = [operators(kernels[v][:, ::-1], planes, half_x, width_y) for v in range(view_count)]
+    forward_ops = stacked_operators(kernels, planes, half_x, width_y)
+    adjoint_ops = stacked_operators(kernels[:, :, ::-1], planes, half_x, width_y)
     for iteration in range(ITERS):
         estimate_low = estimate.astype(jnp.bfloat16)
         low, high = x_rims(estimate_low, reach, 1)
         extended = jnp.concatenate([low, estimate_low, high], axis=1)
-        after_xy = jnp.stack([pass_xy(extended, forward_ops[v]) for v in range(view_count)])
-        below, above = z_rims(after_xy, reach, 1)
-        quotients = []
-        for v in range(view_count):
-            widened = jnp.concatenate([below[v], after_xy[v], above[v]], axis=0)
-            blurred = pass_z(widened, forward_ops[v][2])
-            quotients.append((observed[v] / blurred).astype(jnp.bfloat16))
-        quotients = jnp.stack(quotients)
+        after_x = jnp.einsum(
+            "vzpa,zay->vzpy", forward_ops[0], extended, preferred_element_type=jnp.float32
+        ).astype(jnp.bfloat16)
+        blurred = pass_z_views(pass_y_views(after_x, forward_ops[1]), forward_ops[2], reach)
+        quotients = (observed / blurred).astype(jnp.bfloat16)
         low, high = x_rims(quotients, reach, 2)
-        after_xy = jnp.stack([
-            pass_xy(jnp.concatenate([low[v], quotients[v], high[v]], axis=1), adjoint_ops[v])
-            for v in range(view_count)
-        ])
-        below, above = z_rims(after_xy, reach, 1)
-        backs = [
-            pass_z(jnp.concatenate([below[v], after_xy[v], above[v]], axis=0), adjoint_ops[v][2])
-            for v in range(view_count)
-        ]
+        widened = jnp.concatenate([low, quotients, high], axis=2)
+        after_x = jnp.einsum(
+            "vzpa,vzay->vzpy", adjoint_ops[0], widened, preferred_element_type=jnp.float32
+        ).astype(jnp.bfloat16)
+        backs = pass_z_views(pass_y_views(after_x, adjoint_ops[1]), adjoint_ops[2], reach)
         estimate = estimate * (0.5 * (backs[0] + backs[1]))
     keep = lax.dynamic_slice_in_dim(estimate, view_bit * half_rows, half_rows, 0)
     give = lax.dynamic_slice_in_dim(estimate, (1 - view_bit) * half_rows, half_rows, 0)

time: 101 us -> 94.8 us (0.939)
  matrix products: 9.27 us -> 4.15 us
  other arithmetic: 11.4 us -> 7.52 us
  local copies, waits for them, and re-layouts: 8.65 us -> 10.6 us
    dot_general x16 -> x12, matrix products: 9.27 us -> 4.15 us  [the longest x2 1.15 us: local(): jnp.einsum('vzpa,vzay->vzpy', adjoint_ops[0], widened, preferred_element_...]
    reshape x0 -> x4, local copies, waits for them, and re-layouts: none -> 1.51 us  [pass_z_views(): flat = widened.reshape(shape[0], shape[1], -1)]
    unnamed x65 -> x31, local copies, waits for them, and re-layouts: 3.87 us -> 4.43 us
  transfers between devices with their start and end apart: 16 -> 16, of which waited for: 11 -> 11; matrix products, arithmetic and copies ran while one was open for 6% -> 5% of each run, Pallas kernels for 0% -> 0%
where the time goes in v7:
time: 94.8 us; the launch traced here: 93.7 us
  starting transfers between devices  45.7 us (48%)
  waiting for transfers between devices  24.9 us (26%)
  local copies, waits for them, and re-layouts  10.6 us (11%)
  other arithmetic  7.52 us (8%)
  matrix products  4.15 us (4%)
    ppermute x6, starting transfers between devices, from_partner(): return lax.ppermute(block, axis, route)  30.3 us
    ppermute x4, waiting for transfers between devices, z_rims(): got = lax.ppermute(payload, 'view', route)  13.6 us
    ppermute x2, starting transfers between devices, shifted(): return lax.ppermute(block, axis, route)  6.24 us
    ppermute x4, starting transfers between devices, z_rims(): got = lax.ppermute(payload, 'view', route)  6.23 us
    ppermute x2, waiting for transfers between devices, shifted(): return lax.ppermute(block, axis, route)  5.97 us
    ppermute x6, waiting for transfers between devices, from_partner(): return lax.ppermute(block, axis, route)  5.39 us
    unnamed x31, local copies, waits for them, and re-layouts  4.43 us
    ppermute x4, starting transfers between devices, x_rims(): across = lax.ppermute(outward, ('tile', 'view'), route)  2.91 us
  transfers between devices with their start and end apart: 16, of which 11 were waited for; matrix products, arithmetic and copies ran while one was open for 5% of the time, Pallas kernels for 0%

profile of v7, /device:TPU:0, one launch (start us, length us, event | category | flops | bytes accessed | tf_op | source)
XLA Modules:
  0.0 93.7 jit_solution(13961654897619590244)
XLA Ops:
  1.2 1.2 %copy.8 = bf16[64,32,128]{2,0,1:T(8,128)(2,1)S(1)} copy(bf16[64,32,128]{2,1,0:T(8,128)(2,1)} %param.5) | data formatting | bytes 1048576 | tf_op args[0]
  3.2 4.9 %collective-permute-start = (bf16[64,4,4,128]{3,0,2,1:T(8,128)(2,1)S(1)}, bf16[64,4,4,128]{3,0,2,1:T(8,128)(2,1)S(1)}, u32[]{:S(2)}, u32[]{:S(2)}) collective-permute-start(bf16[64,4,4,128]{3,0,2,1:T(8,128)(2,1)S(1)} %select_bitcast_fusion.1), channel_id=1, source_target_pairs={{0,4},{4,8},{8,12},{1,5},{5,9},{9,13},{2,6},{6,10},{10,14},{3,7},{... | collective-permute-start | bytes 786440 | tf_op jit(solution)/shard_map/ppermute | solution.py:13
  9.2 1.3 %collective-permute-start.1 = (bf16[64,4,4,128]{3,0,2,1:T(8,128)(2,1)S(1)}, bf16[64,4,4,128]{3,0,2,1:T(8,128)(2,1)S(1)}, u32[]{:S(2)}, u32[]{:S(2)}) collective-permute-start(bf16[64,4,4,128]{3,0,2,1:T(8,128)(2,1)S(1)} %select_bitcast_fusion), channel_id=1, source_target_pairs={{4,0},{8,4},{12,8},{5,1},{9,5},{13,9},{6,2},{10,6},{14,10},{7,3},{... | collective-permute-start | bytes 786440 | tf_op jit(solution)/shard_map/ppermute | solution.py:13
  13.6 5.2 %collective-permute-done.1 = bf16[64,4,4,128]{3,0,2,1:T(8,128)(2,1)S(1)} collective-permute-done((bf16[64,4,4,128]{3,0,2,1:T(8,128)(2,1)S(1)}, bf16[64,4,4,128]{3,0,2,1:T(8,128)(2,1)S(1)}, u32[]{:S(2)}, u32[]{:S(2)}) %collective-permute-start.1) | collective-permute-done | bytes 262176 | tf_op jit(solution)/shard_map/ppermute | solution.py:13
  20.3 1.6 %select_reduce_fusion.1 = (bf16[128,128]{1,0:T(8,128)(2,1)S(1)}, bf16[128,128]{1,0:T(8,128)(2,1)S(1)}, bf16[128,128]{1,0:T(8,128)(2,1)}, bf16[128,128]{1,0:T(8,128)(2,1)}) fusion(f32[31]{0:T(128)S(1)} %get-tuple-element.69, s32[128,128]{1,0:T(8,128)S(1)} %subtract_add_fusion, f32[31]{0:T(128)S(1)} %get-tuple-element.70, f32[31]{0:T(128)S(1)} %get-tuple-element.83, ...), kind=kLoop, calls=%fused_computation.4 | loop fusion | flops 4505600 | bytes 197104 | tf_op jit(solution)/shard_map/reduce_sum | solution.py:45
  23.7 3.0 %collective-permute-start.4 = (bf16[64,15,128]{2,1,0:T(8,128)(2,1)S(1)}, bf16[64,15,128]{2,1,0:T(8,128)(2,1)S(1)}, u32[]{:S(2)}, u32[]{:S(2)}) collective-permute-start(bf16[64,15,128]{2,1,0:T(8,128)(2,1)S(1)} %get-tuple-element.57), channel_id=1, source_target_pairs={{0,1},{1,0},{2,3},{3,2},{4,5},{5,4},{6,7},{7,6},{8,9},{9,8},{10,11... | collective-permute-start | bytes 737288 | tf_op jit(solution)/shard_map/ppermute | solution.py:23
  26.8 1.0 %collective-permute-done.4 = bf16[64,15,128]{2,1,0:T(8,128)(2,1)S(1)} collective-permute-done((bf16[64,15,128]{2,1,0:T(8,128)(2,1)S(1)}, bf16[64,15,128]{2,1,0:T(8,128)(2,1)S(1)}, u32[]{:S(2)}, u32[]{:S(2)}) %collective-permute-start.4) | collective-permute-done | bytes 245792 | tf_op jit(solution)/shard_map/ppermute | solution.py:23
  28.6 1.6 %collective-permute-start.5 = (bf16[2,15,16,128]{3,2,1,0:T(8,128)(2,1)S(1)}, bf16[2,15,16,128]{3,2,1,0:T(8,128)(2,1)S(1)}, u32[]{:S(2)}, u32[]{:S(2)}) collective-permute-start(bf16[2,15,16,128]{3,2,1,0:T(8,128)(2,1)S(1)} %constant_dynamic-slice_fusion.11), channel_id=1, source_target_pairs={{0,2},{2,0},{1,3},{3,1},{4,6},{6,4},{5,7},{7,5},{8,10},{10,8},{9,1... | collective-permute-start | bytes 368648 | tf_op jit(solution)/shard_map/ppermute | solution.py:121
  30.2 3.4 %collective-permute-done.5 = bf16[2,15,16,128]{3,2,1,0:T(8,128)(2,1)S(1)} collective-permute-done((bf16[2,15,16,128]{3,2,1,0:T(8,128)(2,1)S(1)}, bf16[2,15,16,128]{3,2,1,0:T(8,128)(2,1)S(1)}, u32[]{:S(2)}, u32[]{:S(2)}) %collective-permute-start.5) | collective-permute-done | bytes 122912 | tf_op jit(solution)/shard_map/ppermute | solution.py:121
  36.7 6.7 %collective-permute-start.7 = (bf16[2,64,15,128]{3,2,1,0:T(8,128)(2,1)S(1)}, bf16[2,64,15,128]{3,2,1,0:T(8,128)(2,1)S(1)}, u32[]{:S(2)}, u32[]{:S(2)}) collective-permute-start(bf16[2,64,15,128]{3,2,1,0:T(8,128)(2,1)S(1)} %get-tuple-element.49), channel_id=1, source_target_pairs={{0,1},{1,0},{2,3},{3,2},{4,5},{5,4},{6,7},{7,6},{8,9},{9,8},{10,11... | collective-permute-start | bytes 1474568 | tf_op jit(solution)/shard_map/ppermute | solution.py:23
  43.5 1.4 %collective-permute-done.7 = bf16[2,64,15,128]{3,2,1,0:T(8,128)(2,1)S(1)} collective-permute-done((bf16[2,64,15,128]{3,2,1,0:T(8,128)(2,1)S(1)}, bf16[2,64,15,128]{3,2,1,0:T(8,128)(2,1)S(1)}, u32[]{:S(2)}, u32[]{:S(2)}) %collective-permute-start.7) | collective-permute-done | bytes 491552 | tf_op jit(solution)/shard_map/ppermute | solution.py:23
  45.9 1.6 %collective-permute-start.8 = (bf16[2,15,16,128]{3,2,1,0:T(8,128)(2,1)S(1)}, bf16[2,15,16,128]{3,2,1,0:T(8,128)(2,1)S(1)}, u32[]{:S(2)}, u32[]{:S(2)}) collective-permute-start(bf16[2,15,16,128]{3,2,1,0:T(8,128)(2,1)S(1)} %constant_dynamic-slice_fusion.8), channel_id=1, source_target_pairs={{0,2},{2,0},{1,3},{3,1},{4,6},{6,4},{5,7},{7,5},{8,10},{10,8},{9,1... | collective-permute-start | bytes 368648 | tf_op jit(solution)/shard_map/ppermute | solution.py:121
  47.4 3.4 %collective-permute-done.8 = bf16[2,15,16,128]{3,2,1,0:T(8,128)(2,1)S(1)} collective-permute-done((bf16[2,15,16,128]{3,2,1,0:T(8,128)(2,1)S(1)}, bf16[2,15,16,128]{3,2,1,0:T(8,128)(2,1)S(1)}, u32[]{:S(2)}, u32[]{:S(2)}) %collective-permute-start.8) | collective-permute-done | bytes 122912 | tf_op jit(solution)/shard_map/ppermute | solution.py:121
  52.1 4.5 %collective-permute-start.10 = (bf16[64,15,128]{2,1,0:T(8,128)(2,1)S(1)}, bf16[64,15,128]{2,1,0:T(8,128)(2,1)S(1)}, u32[]{:S(2)}, u32[]{:S(2)}) collective-permute-start(bf16[64,15,128]{2,1,0:T(8,128)(2,1)S(1)} %get-tuple-element.55), channel_id=1, source_target_pairs={{0,1},{1,0},{2,3},{3,2},{4,5},{5,4},{6,7},{7,6},{8,9},{9,8},{10,11... | collective-permute-start | bytes 737288 | tf_op jit(solution)/shard_map/ppermute | solution.py:23
  56.6 0.8 collective-permute-start.9
  58.5 1.6 %collective-permute-start.11 = (bf16[2,15,16,128]{3,2,1,0:T(8,128)(2,1)S(1)}, bf16[2,15,16,128]{3,2,1,0:T(8,128)(2,1)S(1)}, u32[]{:S(2)}, u32[]{:S(2)}) collective-permute-start(bf16[2,15,16,128]{3,2,1,0:T(8,128)(2,1)S(1)} %constant_dynamic-slice_fusion.5), channel_id=1, source_target_pairs={{0,2},{2,0},{1,3},{3,1},{4,6},{6,4},{5,7},{7,5},{8,10},{10,8},{9,1... | collective-permute-start | bytes 368648 | tf_op jit(solution)/shard_map/ppermute | solution.py:121
  60.1 3.4 %collective-permute-done.11 = bf16[2,15,16,128]{3,2,1,0:T(8,128)(2,1)S(1)} collective-permute-done((bf16[2,15,16,128]{3,2,1,0:T(8,128)(2,1)S(1)}, bf16[2,15,16,128]{3,2,1,0:T(8,128)(2,1)S(1)}, u32[]{:S(2)}, u32[]{:S(2)}) %collective-permute-start.11) | collective-permute-done | bytes 122912 | tf_op jit(solution)/shard_map/ppermute | solution.py:121
  67.0 11.7 %collective-permute-start.13 = (bf16[2,64,15,128]{3,2,1,0:T(8,128)(2,1)S(1)}, bf16[2,64,15,128]{3,2,1,0:T(8,128)(2,1)S(1)}, u32[]{:S(2)}, u32[]{:S(2)}) collective-permute-start(bf16[2,64,15,128]{3,2,1,0:T(8,128)(2,1)S(1)} %get-tuple-element.45), channel_id=1, source_target_pairs={{0,1},{1,0},{2,3},{3,2},{4,5},{5,4},{6,7},{7,6},{8,9},{9,8},{10,11... | collective-permute-start | bytes 1474568 | tf_op jit(solution)/shard_map/ppermute | solution.py:23
  78.7 1.5 %collective-permute-done.13 = bf16[2,64,15,128]{3,2,1,0:T(8,128)(2,1)S(1)} collective-permute-done((bf16[2,64,15,128]{3,2,1,0:T(8,128)(2,1)S(1)}, bf16[2,64,15,128]{3,2,1,0:T(8,128)(2,1)S(1)}, u32[]{:S(2)}, u32[]{:S(2)}) %collective-permute-start.13) | collective-permute-done | bytes 491552 | tf_op jit(solution)/shard_map/ppermute | solution.py:23
  81.2 1.6 %collective-permute-start.14 = (bf16[2,15,16,128]{3,2,1,0:T(8,128)(2,1)S(1)}, bf16[2,15,16,128]{3,2,1,0:T(8,128)(2,1)S(1)}, u32[]{:S(2)}, u32[]{:S(2)}) collective-permute-start(bf16[2,15,16,128]{3,2,1,0:T(8,128)(2,1)S(1)} %constant_dynamic-slice_fusion.2), channel_id=1, source_target_pairs={{0,2},{2,0},{1,3},{3,1},{4,6},{6,4},{5,7},{7,5},{8,10},{10,8},{9,1... | collective-permute-start | bytes 368648 | tf_op jit(solution)/shard_map/ppermute | solution.py:121
  82.7 3.4 %collective-permute-done.14 = bf16[2,15,16,128]{3,2,1,0:T(8,128)(2,1)S(1)} collective-permute-done((bf16[2,15,16,128]{3,2,1,0:T(8,128)(2,1)S(1)}, bf16[2,15,16,128]{3,2,1,0:T(8,128)(2,1)S(1)}, u32[]{:S(2)}, u32[]{:S(2)}) %collective-permute-start.14) | collective-permute-done | bytes 122912 | tf_op jit(solution)/shard_map/ppermute | solution.py:121
  87.3 4.5 %collective-permute-start.15 = (f32[32,16,128]{2,1,0:T(8,128)S(1)}, f32[32,16,128]{2,1,0:T(8,128)S(1)}, u32[]{:S(2)}, u32[]{:S(2)}) collective-permute-start(f32[32,16,128]{2,1,0:T(8,128)S(1)} %get-tuple-element.43), channel_id=1, source_target_pairs={{0,1},{1,0},{2,3},{3,2},{4,5},{5,4},{6,7},{7,6},{8,9},{9,8},{10,11... | collective-permute-start | bytes 786440 | tf_op jit(solution)/shard_map/ppermute | solution.py:23
  91.7 1.2 %collective-permute-done.15 = f32[32,16,128]{2,1,0:T(8,128)S(1)} collective-permute-done((f32[32,16,128]{2,1,0:T(8,128)S(1)}, f32[32,16,128]{2,1,0:T(8,128)S(1)}, u32[]{:S(2)}, u32[]{:S(2)}) %collective-permute-start.15) | collective-permute-done | bytes 262176 | tf_op jit(solution)/shard_map/ppermute | solution.py:23
  92.9 0.8 maximum_select_fusion.1
  (146 shorter events, 21.8 us)
Async XLA Ops:
  2.4 8.0 %copy-start.11 = (s32[1,32]{1,0:T(1,128)S(1)}, s32[1,32]{1,0:T(1,128)}, u32[]{:S(2)}) copy-start(s32[1,32]{1,0:T(1,128)} %param.7) | copy-start | bytes 388
  2.4 8.7 %copy-start.12 = (f32[2,3,31]{2,0,1:T(2,128)S(1)}, f32[2,3,31]{2,0,1:T(2,128)}, u32[]{:S(2)}) copy-start(f32[2,3,31]{2,0,1:T(2,128)} %param.6) | copy-start | bytes 2236
  3.2 10.5 %collective-permute-start = (bf16[64,4,4,128]{3,0,2,1:T(8,128)(2,1)S(1)}, bf16[64,4,4,128]{3,0,2,1:T(8,128)(2,1)S(1)}, u32[]{:S(2)}, u32[]{:S(2)}) collective-permute-start(bf16[64,4,4,128]{3,0,2,1:T(8,128)(2,1)S(1)} %select_bitcast_fusion.1), channel_id=1, source_target_pairs={{0,4},{4,8},{8,12},{1,5},{5,9},{9,13},{2,6},{6,10},{10,14},{3,7},{... | collective-permute-start | bytes 786440 | tf_op jit(solution)/shard_map/ppermute | solution.py:13
  9.2 9.7 %collective-permute-start.1 = (bf16[64,4,4,128]{3,0,2,1:T(8,128)(2,1)S(1)}, bf16[64,4,4,128]{3,0,2,1:T(8,128)(2,1)S(1)}, u32[]{:S(2)}, u32[]{:S(2)}) collective-permute-start(bf16[64,4,4,128]{3,0,2,1:T(8,128)(2,1)S(1)} %select_bitcast_fusion), channel_id=1, source_target_pairs={{4,0},{8,4},{12,8},{5,1},{9,5},{13,9},{6,2},{10,6},{14,10},{7,3},{... | collective-permute-start | bytes 786440 | tf_op jit(solution)/shard_map/ppermute | solution.py:13
  20.2 1.7 %collective-permute-start.2 = (bf16[64,16,128]{2,1,0:T(8,128)(2,1)S(1)}, bf16[64,16,128]{2,1,0:T(8,128)(2,1)S(1)}, u32[]{:S(2)}, u32[]{:S(2)}) collective-permute-start(bf16[64,16,128]{2,1,0:T(8,128)(2,1)S(1)} %get-tuple-element.53), channel_id=1, source_target_pairs={{0,1},{1,0},{2,3},{3,2},{4,5},{5,4},{6,7},{7,6},{8,9},{9,8},{10,11... | collective-permute-start | bytes 786440 | tf_op jit(solution)/shard_map/ppermute | solution.py:23
  23.0 3.8 %collective-permute-start.3 = (bf16[64,15,128]{2,1,0:T(8,128)(2,1)S(1)}, bf16[64,15,128]{2,1,0:T(8,128)(2,1)S(1)}, u32[]{:S(2)}, u32[]{:S(2)}) collective-permute-start(bf16[64,15,128]{2,1,0:T(8,128)(2,1)S(1)} %get-tuple-element.56), channel_id=1, source_target_pairs={{1,4},{4,1},{3,6},{6,3},{5,8},{8,5},{7,10},{10,7},{9,12},{12,9},{1... | collective-permute-start | bytes 737288 | tf_op jit(solution)/shard_map/ppermute | solution.py:140
  23.7 4.1 %collective-permute-start.4 = (bf16[64,15,128]{2,1,0:T(8,128)(2,1)S(1)}, bf16[64,15,128]{2,1,0:T(8,128)(2,1)S(1)}, u32[]{:S(2)}, u32[]{:S(2)}) collective-permute-start(bf16[64,15,128]{2,1,0:T(8,128)(2,1)S(1)} %get-tuple-element.57), channel_id=1, source_target_pairs={{0,1},{1,0},{2,3},{3,2},{4,5},{5,4},{6,7},{7,6},{8,9},{9,8},{10,11... | collective-permute-start | bytes 737288 | tf_op jit(solution)/shard_map/ppermute | solution.py:23
  26.7 7.4 %copy-start.7 = (bf16[2,64,94]{2,1,0:T(8,128)(2,1)}, bf16[2,64,94]{2,1,0:T(8,128)(2,1)S(1)}, u32[]{:S(2)}) copy-start(bf16[2,64,94]{2,1,0:T(8,128)(2,1)S(1)} %pad_maximum_fusion.8) | copy-start | bytes 72196
  28.6 4.9 %collective-permute-start.5 = (bf16[2,15,16,128]{3,2,1,0:T(8,128)(2,1)S(1)}, bf16[2,15,16,128]{3,2,1,0:T(8,128)(2,1)S(1)}, u32[]{:S(2)}, u32[]{:S(2)}) collective-permute-start(bf16[2,15,16,128]{3,2,1,0:T(8,128)(2,1)S(1)} %constant_dynamic-slice_fusion.11), channel_id=1, source_target_pairs={{0,2},{2,0},{1,3},{3,1},{4,6},{6,4},{5,7},{7,5},{8,10},{10,8},{9,1... | collective-permute-start | bytes 368648 | tf_op jit(solution)/shard_map/ppermute | solution.py:121
  35.5 7.9 %copy-start.9 = (bf16[128,128]{1,0:T(8,128)(2,1)S(1)}, bf16[128,128]{1,0:T(8,128)(2,1)}, u32[]{:S(2)}) copy-start(bf16[128,128]{1,0:T(8,128)(2,1)} %get-tuple-element.20) | copy-start | bytes 98308
  35.5 7.9 %copy-start.10 = (bf16[128,128]{1,0:T(8,128)(2,1)S(1)}, bf16[128,128]{1,0:T(8,128)(2,1)}, u32[]{:S(2)}) copy-start(bf16[128,128]{1,0:T(8,128)(2,1)} %get-tuple-element.21) | copy-start | bytes 98308
  36.0 7.5 %collective-permute-start.6 = (bf16[2,64,15,128]{3,2,1,0:T(8,128)(2,1)S(1)}, bf16[2,64,15,128]{3,2,1,0:T(8,128)(2,1)S(1)}, u32[]{:S(2)}, u32[]{:S(2)}) collective-permute-start(bf16[2,64,15,128]{3,2,1,0:T(8,128)(2,1)S(1)} %get-tuple-element.48), channel_id=1, source_target_pairs={{1,4},{4,1},{3,6},{6,3},{5,8},{8,5},{7,10},{10,7},{9,12},{12,9},{1... | collective-permute-start | bytes 1474568 | tf_op jit(solution)/shard_map/ppermute | solution.py:140
  36.7 8.2 %collective-permute-start.7 = (bf16[2,64,15,128]{3,2,1,0:T(8,128)(2,1)S(1)}, bf16[2,64,15,128]{3,2,1,0:T(8,128)(2,1)S(1)}, u32[]{:S(2)}, u32[]{:S(2)}) collective-permute-start(bf16[2,64,15,128]{3,2,1,0:T(8,128)(2,1)S(1)} %get-tuple-element.49), channel_id=1, source_target_pairs={{0,1},{1,0},{2,3},{3,2},{4,5},{5,4},{6,7},{7,6},{8,9},{9,8},{10,11... | collective-permute-start | bytes 1474568 | tf_op jit(solution)/shard_map/ppermute | solution.py:23
  43.5 1.5 %copy-start.5 = (bf16[2,64,16,46]{3,2,1,0:T(8,128)(2,1)}, bf16[2,64,16,46]{3,2,1,0:T(8,128)(2,1)S(1)}, u32[]{:S(2)}) copy-start(bf16[2,64,16,46]{3,2,1,0:T(8,128)(2,1)S(1)} %broadcast_in_dim.244) | copy-start | bytes 565252
  45.9 4.9 %collective-permute-start.8 = (bf16[2,15,16,128]{3,2,1,0:T(8,128)(2,1)S(1)}, bf16[2,15,16,128]{3,2,1,0:T(8,128)(2,1)S(1)}, u32[]{:S(2)}, u32[]{:S(2)}) collective-permute-start(bf16[2,15,16,128]{3,2,1,0:T(8,128)(2,1)S(1)} %constant_dynamic-slice_fusion.8), channel_id=1, source_target_pairs={{0,2},{2,0},{1,3},{3,1},{4,6},{6,4},{5,7},{7,5},{8,10},{10,8},{9,1... | collective-permute-start | bytes 368648 | tf_op jit(solution)/shard_map/ppermute | solution.py:121
  51.9 5.9 %copy-start.4 = (bf16[2,64,16,46]{3,2,0,1:T(8,128)(2,1)S(1)}, bf16[2,64,16,46]{3,2,0,1:T(8,128)(2,1)}, u32[]{:S(2)}) copy-start(bf16[2,64,16,46]{3,2,0,1:T(8,128)(2,1)} %copy-done.3) | copy-start | bytes 565252
  52.1 5.6 %collective-permute-start.10 = (bf16[64,15,128]{2,1,0:T(8,128)(2,1)S(1)}, bf16[64,15,128]{2,1,0:T(8,128)(2,1)S(1)}, u32[]{:S(2)}, u32[]{:S(2)}) collective-permute-start(bf16[64,15,128]{2,1,0:T(8,128)(2,1)S(1)} %get-tuple-element.55), channel_id=1, source_target_pairs={{0,1},{1,0},{2,3},{3,2},{4,5},{5,4},{6,7},{7,6},{8,9},{9,8},{10,11... | collective-permute-start | bytes 737288 | tf_op jit(solution)/shard_map/ppermute | solution.py:23
  56.6 1.2 %collective-permute-start.9 = (bf16[64,15,128]{2,1,0:T(8,128)(2,1)S(1)}, bf16[64,15,128]{2,1,0:T(8,128)(2,1)S(1)}, u32[]{:S(2)}, u32[]{:S(2)}) collective-permute-start(bf16[64,15,128]{2,1,0:T(8,128)(2,1)S(1)} %get-tuple-element.54), channel_id=1, source_target_pairs={{1,4},{4,1},{3,6},{6,3},{5,8},{8,5},{7,10},{10,7},{9,12},{12,9},{1... | collective-permute-start | bytes 737288 | tf_op jit(solution)/shard_map/ppermute | solution.py:140
  58.5 4.9 %collective-permute-start.11 = (bf16[2,15,16,128]{3,2,1,0:T(8,128)(2,1)S(1)}, bf16[2,15,16,128]{3,2,1,0:T(8,128)(2,1)S(1)}, u32[]{:S(2)}, u32[]{:S(2)}) collective-permute-start(bf16[2,15,16,128]{3,2,1,0:T(8,128)(2,1)S(1)} %constant_dynamic-slice_fusion.5), channel_id=1, source_target_pairs={{0,2},{2,0},{1,3},{3,1},{4,6},{6,4},{5,7},{7,5},{8,10},{10,8},{9,1... | collective-permute-start | bytes 368648 | tf_op jit(solution)/shard_map/ppermute | solution.py:121
  66.2 12.4 %collective-permute-start.12 = (bf16[2,64,15,128]{3,2,1,0:T(8,128)(2,1)S(1)}, bf16[2,64,15,128]{3,2,1,0:T(8,128)(2,1)S(1)}, u32[]{:S(2)}, u32[]{:S(2)}) collective-permute-start(bf16[2,64,15,128]{3,2,1,0:T(8,128)(2,1)S(1)} %get-tuple-element.44), channel_id=1, source_target_pairs={{1,4},{4,1},{3,6},{6,3},{5,8},{8,5},{7,10},{10,7},{9,12},{12,9},{1... | collective-permute-start | bytes 1474568 | tf_op jit(solution)/shard_map/ppermute | solution.py:140
  66.9 13.3 %copy-start.6 = (bf16[2,64,16,46]{3,2,1,0:T(8,128)(2,1)S(1)}, bf16[2,64,16,46]{3,2,1,0:T(8,128)(2,1)}, u32[]{:S(2)}) copy-start(bf16[2,64,16,46]{3,2,1,0:T(8,128)(2,1)} %copy-done.5) | copy-start | bytes 565252
  67.0 13.2 %collective-permute-start.13 = (bf16[2,64,15,128]{3,2,1,0:T(8,128)(2,1)S(1)}, bf16[2,64,15,128]{3,2,1,0:T(8,128)(2,1)S(1)}, u32[]{:S(2)}, u32[]{:S(2)}) collective-permute-start(bf16[2,64,15,128]{3,2,1,0:T(8,128)(2,1)S(1)} %get-tuple-element.45), channel_id=1, source_target_pairs={{0,1},{1,0},{2,3},{3,2},{4,5},{5,4},{6,7},{7,6},{8,9},{9,8},{10,11... | collective-permute-start | bytes 1474568 | tf_op jit(solution)/shard_map/ppermute | solution.py:23
  81.2 4.9 %collective-permute-start.14 = (bf16[2,15,16,128]{3,2,1,0:T(8,128)(2,1)S(1)}, bf16[2,15,16,128]{3,2,1,0:T(8,128)(2,1)S(1)}, u32[]{:S(2)}, u32[]{:S(2)}) collective-permute-start(bf16[2,15,16,128]{3,2,1,0:T(8,128)(2,1)S(1)} %constant_dynamic-slice_fusion.2), channel_id=1, source_target_pairs={{0,2},{2,0},{1,3},{3,1},{4,6},{6,4},{5,7},{7,5},{8,10},{10,8},{9,1... | collective-permute-start | bytes 368648 | tf_op jit(solution)/shard_map/ppermute | solution.py:121
  87.3 5.6 %collective-permute-start.15 = (f32[32,16,128]{2,1,0:T(8,128)S(1)}, f32[32,16,128]{2,1,0:T(8,128)S(1)}, u32[]{:S(2)}, u32[]{:S(2)}) collective-permute-start(f32[32,16,128]{2,1,0:T(8,128)S(1)} %get-tuple-element.43), channel_id=1, source_target_pairs={{0,1},{1,0},{2,3},{3,2},{4,5},{5,4},{6,7},{7,6},{8,9},{9,8},{10,11... | collective-permute-start | bytes 786440 | tf_op jit(solution)/shard_map/ppermute | solution.py:23
  (5 other events, 4.8 us)

commit v8 on v7

--- a/solution.py
+++ b/solution.py
@@ -154,41 +154,36 @@
     view_bit = lax.axis_index("view") % 2
     sources = block_source[0]
     blocks = acquired.reshape(planes, block_count, BX, width_y)
-    wanted_here = lax.dynamic_slice_in_dim(sources, tile_index * block_count, block_count)
-    source_tiles = wanted_here // block_count
-    source_blocks = wanted_here % block_count
-    parcels = []
-    for offset in (1, -1):
-        target = jnp.clip(tile_index + offset, 0, tile_total - 1)
-        wanted = lax.dynamic_slice_in_dim(sources, target * block_count, block_count)
-        matches = wanted // block_count == tile_index
-        ranks = jnp.cumsum(matches.astype(jnp.int32)) - 1
-        slot_ids = jnp.arange(capacity, dtype=jnp.int32)
-        selected = jnp.where(
-            matches[None, :] & (ranks[None, :] == slot_ids[:, None]),
-            wanted[None, :] % block_count,
-            0,
-        )
-        picked = jnp.sum(selected, axis=1)
-        parcel = jnp.take(blocks, picked, axis=1)
-        parcels.append(shifted(parcel, "tile", offset))
-    candidates = jnp.concatenate([blocks, parcels[0], parcels[1]], axis=1)
-    from_left = source_tiles == tile_index - 1
-    from_right = source_tiles == tile_index + 1
-    left_order = jnp.cumsum(from_left.astype(jnp.int32)) - 1
-    right_order = jnp.cumsum(from_right.astype(jnp.int32)) - 1
-    chosen = jnp.where(
-        from_left,
-        block_count + left_order,
-        jnp.where(from_right, block_count + capacity + right_order, source_blocks),
-    )
-    measured = jnp.take(candidates, chosen, axis=1).reshape(planes, width_x, width_y)
     half_x = width_x // 2
     half_rows = planes // 2
-    own_x = lax.dynamic_slice_in_dim(measured, view_bit * half_x, half_x, 1)
-    give_x = lax.dynamic_slice_in_dim(measured, (1 - view_bit) * half_x, half_x, 1)
-    got_x = from_partner(give_x, "view", 0)
-    views_measured = jnp.where(view_bit == 0, jnp.stack([own_x, got_x]), jnp.stack([got_x, own_x]))
+    half_blocks = block_count // 2
+    first = view_bit == 0
+    starts = []
+    for target, half in ((tile_index, 0), (tile_index, 1), (tile_index + 1, 0), (tile_index - 1, 1)):
+        target = jnp.clip(target, 0, tile_total - 1)
+        starts.append(target * block_count + half * half_blocks)
+    slots = jnp.concatenate([lax.dynamic_slice_in_dim(sources, st, half_blocks) for st in starts])
+    picked = jnp.take(blocks, slots % block_count, axis=1)
+    mine = (slots // block_count == tile_index)[None, :, None, None]
+    partials = jnp.where(mine, picked, jnp.zeros((), picked.dtype))
+    partials = partials.reshape(planes, 4, half_x, width_y)
+    own_keep = jnp.where(first, partials[:, 0], partials[:, 1])
+    own_give = jnp.where(first, partials[:, 1], partials[:, 0])
+    cross_keep = jnp.where(first, partials[:, 3], partials[:, 2])
+    cross_pass = jnp.where(first, partials[:, 2], partials[:, 3])
+    got = from_partner(jnp.stack([own_give, cross_pass]), "view", 0)
+    tiles = lax.axis_size("tile")
+    views = lax.axis_size("view")
+    route = []
+    for tile in range(tiles - 1):
+        for slab in range(views // 2):
+            right_core = tile * views + 2 * slab + 1
+            left_core = (tile + 1) * views + 2 * slab
+            route += [(right_core, left_core), (left_core, right_core)]
+    outgoing = jnp.where(first, jnp.stack([cross_keep, got[1]]), jnp.stack([got[1], cross_keep]))
+    incoming = lax.ppermute(outgoing, ("tile", "view"), route)
+    own_parts = jnp.where(first, jnp.stack([own_keep, got[0]]), jnp.stack([got[0], own_keep]))
+    views_measured = own_parts + incoming
     observed = views_measured.astype(jnp.float32)
     estimate = 0.5 * (observed[0] + observed[1])
     kernels = (psf_taps / jnp.sum(psf_taps, axis=2, keepdims=True)).astype(jnp.bfloat16)

time: 94.8 us -> 95.8 us (1.011)
  waiting for transfers between devices: 24.9 us -> 18.8 us
  other arithmetic: 7.52 us -> 11.9 us
  starting transfers between devices: 45.7 us -> 47.8 us
  local copies, waits for them, and re-layouts: 10.6 us -> 11.9 us
    ppermute x6, starting transfers between devices: 30.3 us -> 37.3 us  [from_partner(): return lax.ppermute(block, axis, route)]
    ppermute x2 -> x1, waiting for transfers between devices: 5.97 us -> 0.01 us  [local(): incoming = lax.ppermute(outgoing, ('tile', 'view'), route)]
    ppermute x2 -> x1, starting transfers between devices: 6.24 us -> 0.69 us  [local(): incoming = lax.ppermute(outgoing, ('tile', 'view'), route)]
    reshape x4, local copies, waits for them, and re-layouts: 1.51 us -> 4.89 us  [pass_z_views(): flat = widened.reshape(shape[0], shape[1], -1)]
    concatenate x4, other arithmetic: 0.38 us -> 3.02 us  [pass_z_views(): widened = jnp.concatenate([below, after_y, above], axis=1)]
    unnamed x31 -> x25, local copies, waits for them, and re-layouts: 4.43 us -> 1.95 us
    gather x4 -> x1, local copies, waits for them, and re-layouts: 2.25 us -> 0.75 us  [local(): picked = jnp.take(blocks, slots % block_count, axis=1)]
    reduce_sum x3, other arithmetic: 2.33 us -> 3.55 us  [band_matrix(): matrix = jnp.sum(jnp.where(hit, taps, jnp.float32(0.0)), axis=2)]
  transfers between devices with their start and end apart: 16 -> 15, of which waited for: 11 -> 8; matrix products, arithmetic and copies ran while one was open for 5% -> 6% of each run, Pallas kernels for 0% -> 0%
where the time goes in v8:
time: 95.8 us; the launch traced here: 95.2 us
  starting transfers between devices  47.8 us (50%)
  waiting for transfers between devices  18.8 us (20%)
  local copies, waits for them, and re-layouts  11.9 us (12%)
  other arithmetic  11.9 us (12%)
  matrix products  4.14 us (4%)
    ppermute x6, starting transfers between devices, from_partner(): return lax.ppermute(block, axis, route)  37.3 us
    ppermute x4, waiting for transfers between devices, z_rims(): got = lax.ppermute(payload, 'view', route)  13.6 us
    ppermute x4, starting transfers between devices, z_rims(): got = lax.ppermute(payload, 'view', route)  6.22 us
    ppermute x6, waiting for transfers between devices, from_partner(): return lax.ppermute(block, axis, route)  5.22 us
    reshape x4, local copies, waits for them, and re-layouts, pass_z_views(): flat = widened.reshape(shape[0], shape[1], -1)  4.89 us
    ppermute x4, starting transfers between devices, x_rims(): across = lax.ppermute(outward, ('tile', 'view'), route)  3.61 us
    reduce_sum x3, other arithmetic, band_matrix(): matrix = jnp.sum(jnp.where(hit, taps, jnp.float32(0.0)), axis=2)  3.55 us
    concatenate x4, other arithmetic, pass_z_views(): widened = jnp.concatenate([below, after_y, above], axis=1)  3.02 us
  transfers between devices with their start and end apart: 15, of which 8 were waited for; matrix products, arithmetic and copies ran while one was open for 6% of the time, Pallas kernels for 0%

profile of v8, /device:TPU:0, one launch (start us, length us, event | category | flops | bytes accessed | tf_op | source)
XLA Modules:
  0.0 95.2 jit_solution(4876885716256130927)
XLA Ops:
  1.0 1.2 %copy.11 = bf16[64,32,128]{2,0,1:T(8,128)(2,1)S(1)} copy(bf16[64,32,128]{2,1,0:T(8,128)(2,1)} %param.3) | data formatting | bytes 1048576 | tf_op args[0]
  8.7 1.6 %select_reduce_fusion.1 = (bf16[128,128]{1,0:T(8,128)(2,1)S(1)}, bf16[128,128]{1,0:T(8,128)(2,1)S(1)}, bf16[128,128]{1,0:T(8,128)(2,1)}, bf16[128,128]{1,0:T(8,128)(2,1)}) fusion(f32[31]{0:T(128)S(1)} %get-tuple-element.64, s32[128,128]{1,0:T(8,128)S(1)} %subtract_add_fusion, f32[31]{0:T(128)S(1)} %get-tuple-element.65, f32[31]{0:T(128)S(1)} %get-tuple-element.89, ...), kind=kLoop, calls=%fused_computation.2 | loop fusion | flops 4505600 | bytes 197104 | tf_op jit(solution)/shard_map/reduce_sum | solution.py:45
  10.8 1.4 %collective-permute-start.2 = (bf16[64,15,128]{2,1,0:T(8,128)(2,1)S(1)}, bf16[64,15,128]{2,1,0:T(8,128)(2,1)}, u32[]{:S(2)}, u32[]{:S(2)}) collective-permute-start(bf16[64,15,128]{2,1,0:T(8,128)(2,1)S(1)} %get-tuple-element.51), channel_id=1, source_target_pairs={{1,4},{4,1},{3,6},{6,3},{5,8},{8,5},{7,10},{10,7},{9,12},{12,9},{1... | collective-permute-start | bytes 737288 | tf_op jit(solution)/shard_map/ppermute | solution.py:140
  12.1 11.7 %collective-permute-start.3 = (bf16[64,15,128]{2,1,0:T(8,128)(2,1)S(1)}, bf16[64,15,128]{2,1,0:T(8,128)(2,1)}, u32[]{:S(2)}, u32[]{:S(2)}) collective-permute-start(bf16[64,15,128]{2,1,0:T(8,128)(2,1)S(1)} %get-tuple-element.52), channel_id=1, source_target_pairs={{0,1},{1,0},{2,3},{3,2},{4,5},{5,4},{6,7},{7,6},{8,9},{9,8},{10,11... | collective-permute-start | bytes 737288 | tf_op jit(solution)/shard_map/ppermute | solution.py:23
  25.2 1.2 %broadcast_select_fusion.7 = (bf16[64,15,128]{2,1,0:T(8,128)(2,1)S(1)}, bf16[64,15,128]{2,1,0:T(8,128)(2,1)S(1)}) fusion(bf16[64,15,128]{2,1,0:T(8,128)(2,1)} %collective-permute-done.2, bf16[64,15,128]{2,1,0:T(8,128)(2,1)} %collective-permute-done.3, pred[]{:T(512)S(6)} %eq.96), kind=kLoop, calls=%fused_computation.81 | loop fusion | flops 245760 | bytes 983041 | tf_op jit(solution)/shard_map/jit(_where)/select_n | solution.py:142
  27.2 1.6 %collective-permute-start.4 = (bf16[2,15,16,128]{3,2,1,0:T(8,128)(2,1)S(1)}, bf16[2,15,16,128]{3,2,1,0:T(8,128)(2,1)S(1)}, u32[]{:S(2)}, u32[]{:S(2)}) collective-permute-start(bf16[2,15,16,128]{3,2,1,0:T(8,128)(2,1)S(1)} %constant_dynamic-slice_fusion.11), channel_id=1, source_target_pairs={{0,2},{2,0},{1,3},{3,1},{4,6},{6,4},{5,7},{7,5},{8,10},{10,8},{9,1... | collective-permute-start | bytes 368648 | tf_op jit(solution)/shard_map/ppermute | solution.py:121
  28.8 3.4 %collective-permute-done.4 = bf16[2,15,16,128]{3,2,1,0:T(8,128)(2,1)S(1)} collective-permute-done((bf16[2,15,16,128]{3,2,1,0:T(8,128)(2,1)S(1)}, bf16[2,15,16,128]{3,2,1,0:T(8,128)(2,1)S(1)}, u32[]{:S(2)}, u32[]{:S(2)}) %collective-permute-start.4) | collective-permute-done | bytes 122912 | tf_op jit(solution)/shard_map/ppermute | solution.py:121
  33.2 1.5 %reshape.519 = bf16[2,94,2048]{2,1,0:T(8,128)(2,1)S(1)} reshape(bf16[2,94,16,128]{3,2,1,0:T(8,128)(2,1)} %pad_maximum_fusion) | data formatting | bytes 1540096 | tf_op jit(solution)/shard_map/reshape | solution.py:98
  36.6 6.0 %collective-permute-start.6 = (bf16[2,64,15,128]{3,2,1,0:T(8,128)(2,1)S(1)}, bf16[2,64,15,128]{3,2,1,0:T(8,128)(2,1)S(1)}, u32[]{:S(2)}, u32[]{:S(2)}) collective-permute-start(bf16[2,64,15,128]{3,2,1,0:T(8,128)(2,1)S(1)} %get-tuple-element.44), channel_id=1, source_target_pairs={{0,1},{1,0},{2,3},{3,2},{4,5},{5,4},{6,7},{7,6},{8,9},{9,8},{10,11... | collective-permute-start | bytes 1474568 | tf_op jit(solution)/shard_map/ppermute | solution.py:23
  42.7 1.4 %collective-permute-done.6 = bf16[2,64,15,128]{3,2,1,0:T(8,128)(2,1)S(1)} collective-permute-done((bf16[2,64,15,128]{3,2,1,0:T(8,128)(2,1)S(1)}, bf16[2,64,15,128]{3,2,1,0:T(8,128)(2,1)S(1)}, u32[]{:S(2)}, u32[]{:S(2)}) %collective-permute-start.6) | collective-permute-done | bytes 491552 | tf_op jit(solution)/shard_map/ppermute | solution.py:23
  45.1 1.6 %collective-permute-start.7 = (bf16[2,15,16,128]{3,2,1,0:T(8,128)(2,1)S(1)}, bf16[2,15,16,128]{3,2,1,0:T(8,128)(2,1)S(1)}, u32[]{:S(2)}, u32[]{:S(2)}) collective-permute-start(bf16[2,15,16,128]{3,2,1,0:T(8,128)(2,1)S(1)} %constant_dynamic-slice_fusion.8), channel_id=1, source_target_pairs={{0,2},{2,0},{1,3},{3,1},{4,6},{6,4},{5,7},{7,5},{8,10},{10,8},{9,1... | collective-permute-start | bytes 368648 | tf_op jit(solution)/shard_map/ppermute | solution.py:121
  46.6 3.4 %collective-permute-done.7 = bf16[2,15,16,128]{3,2,1,0:T(8,128)(2,1)S(1)} collective-permute-done((bf16[2,15,16,128]{3,2,1,0:T(8,128)(2,1)S(1)}, bf16[2,15,16,128]{3,2,1,0:T(8,128)(2,1)S(1)}, u32[]{:S(2)}, u32[]{:S(2)}) %collective-permute-start.7) | collective-permute-done | bytes 122912 | tf_op jit(solution)/shard_map/ppermute | solution.py:121
  51.0 1.5 %reshape.522 = bf16[2,94,2048]{2,1,0:T(8,128)(2,1)S(1)} reshape(bf16[2,94,16,128]{3,2,1,0:T(8,128)(2,1)} %pad_maximum_fusion.1) | data formatting | bytes 1540096 | tf_op jit(solution)/shard_map/reshape | solution.py:98
  54.2 8.7 %collective-permute-start.9 = (bf16[64,15,128]{2,1,0:T(8,128)(2,1)S(1)}, bf16[64,15,128]{2,1,0:T(8,128)(2,1)S(1)}, u32[]{:S(2)}, u32[]{:S(2)}) collective-permute-start(bf16[64,15,128]{2,1,0:T(8,128)(2,1)S(1)} %get-tuple-element.50), channel_id=1, source_target_pairs={{0,1},{1,0},{2,3},{3,2},{4,5},{5,4},{6,7},{7,6},{8,9},{9,8},{10,11... | collective-permute-start | bytes 737288 | tf_op jit(solution)/shard_map/ppermute | solution.py:23
  62.9 1.2 %collective-permute-done.9 = bf16[64,15,128]{2,1,0:T(8,128)(2,1)S(1)} collective-permute-done((bf16[64,15,128]{2,1,0:T(8,128)(2,1)S(1)}, bf16[64,15,128]{2,1,0:T(8,128)(2,1)S(1)}, u32[]{:S(2)}, u32[]{:S(2)}) %collective-permute-start.9) | collective-permute-done | bytes 245792 | tf_op jit(solution)/shard_map/ppermute | solution.py:23
  64.9 1.6 %collective-permute-start.10 = (bf16[2,15,16,128]{3,2,1,0:T(8,128)(2,1)S(1)}, bf16[2,15,16,128]{3,2,1,0:T(8,128)(2,1)S(1)}, u32[]{:S(2)}, u32[]{:S(2)}) collective-permute-start(bf16[2,15,16,128]{3,2,1,0:T(8,128)(2,1)S(1)} %constant_dynamic-slice_fusion.5), channel_id=1, source_target_pairs={{0,2},{2,0},{1,3},{3,1},{4,6},{6,4},{5,7},{7,5},{8,10},{10,8},{9,1... | collective-permute-start | bytes 368648 | tf_op jit(solution)/shard_map/ppermute | solution.py:121
  66.4 3.4 %collective-permute-done.10 = bf16[2,15,16,128]{3,2,1,0:T(8,128)(2,1)S(1)} collective-permute-done((bf16[2,15,16,128]{3,2,1,0:T(8,128)(2,1)S(1)}, bf16[2,15,16,128]{3,2,1,0:T(8,128)(2,1)S(1)}, u32[]{:S(2)}, u32[]{:S(2)}) %collective-permute-start.10) | collective-permute-done | bytes 122912 | tf_op jit(solution)/shard_map/ppermute | solution.py:121
  70.8 1.5 %reshape.524 = bf16[2,94,2048]{2,1,0:T(8,128)(2,1)S(1)} reshape(bf16[2,94,16,128]{3,2,1,0:T(8,128)(2,1)} %pad_maximum_fusion.2) | data formatting | bytes 1540096 | tf_op jit(solution)/shard_map/reshape | solution.py:98
  74.2 5.9 %collective-permute-start.12 = (bf16[2,64,15,128]{3,2,1,0:T(8,128)(2,1)S(1)}, bf16[2,64,15,128]{3,2,1,0:T(8,128)(2,1)S(1)}, u32[]{:S(2)}, u32[]{:S(2)}) collective-permute-start(bf16[2,64,15,128]{3,2,1,0:T(8,128)(2,1)S(1)} %get-tuple-element.40), channel_id=1, source_target_pairs={{0,1},{1,0},{2,3},{3,2},{4,5},{5,4},{6,7},{7,6},{8,9},{9,8},{10,11... | collective-permute-start | bytes 1474568 | tf_op jit(solution)/shard_map/ppermute | solution.py:23
  80.1 1.5 %collective-permute-done.12 = bf16[2,64,15,128]{3,2,1,0:T(8,128)(2,1)S(1)} collective-permute-done((bf16[2,64,15,128]{3,2,1,0:T(8,128)(2,1)S(1)}, bf16[2,64,15,128]{3,2,1,0:T(8,128)(2,1)S(1)}, u32[]{:S(2)}, u32[]{:S(2)}) %collective-permute-start.12) | collective-permute-done | bytes 491552 | tf_op jit(solution)/shard_map/ppermute | solution.py:23
  82.6 1.6 %collective-permute-start.13 = (bf16[2,15,16,128]{3,2,1,0:T(8,128)(2,1)S(1)}, bf16[2,15,16,128]{3,2,1,0:T(8,128)(2,1)S(1)}, u32[]{:S(2)}, u32[]{:S(2)}) collective-permute-start(bf16[2,15,16,128]{3,2,1,0:T(8,128)(2,1)S(1)} %constant_dynamic-slice_fusion.2), channel_id=1, source_target_pairs={{0,2},{2,0},{1,3},{3,1},{4,6},{6,4},{5,7},{7,5},{8,10},{10,8},{9,1... | collective-permute-start | bytes 368648 | tf_op jit(solution)/shard_map/ppermute | solution.py:121
  84.2 3.4 %collective-permute-done.13 = bf16[2,15,16,128]{3,2,1,0:T(8,128)(2,1)S(1)} collective-permute-done((bf16[2,15,16,128]{3,2,1,0:T(8,128)(2,1)S(1)}, bf16[2,15,16,128]{3,2,1,0:T(8,128)(2,1)S(1)}, u32[]{:S(2)}, u32[]{:S(2)}) %collective-permute-start.13) | collective-permute-done | bytes 122912 | tf_op jit(solution)/shard_map/ppermute | solution.py:121
  88.7 4.5 %collective-permute-start.14 = (f32[32,16,128]{2,1,0:T(8,128)S(1)}, f32[32,16,128]{2,1,0:T(8,128)S(1)}, u32[]{:S(2)}, u32[]{:S(2)}) collective-permute-start(f32[32,16,128]{2,1,0:T(8,128)S(1)} %get-tuple-element.38), channel_id=1, source_target_pairs={{0,1},{1,0},{2,3},{3,2},{4,5},{5,4},{6,7},{7,6},{8,9},{9,8},{10,11... | collective-permute-start | bytes 786440 | tf_op jit(solution)/shard_map/ppermute | solution.py:23
  93.2 1.2 %collective-permute-done.14 = f32[32,16,128]{2,1,0:T(8,128)S(1)} collective-permute-done((f32[32,16,128]{2,1,0:T(8,128)S(1)}, f32[32,16,128]{2,1,0:T(8,128)S(1)}, u32[]{:S(2)}, u32[]{:S(2)}) %collective-permute-start.14) | collective-permute-done | bytes 262176 | tf_op jit(solution)/shard_map/ppermute | solution.py:23
  (123 shorter events, 22.8 us)
Async XLA Ops:
  4.5 3.1 %collective-permute-start = (bf16[2,64,16,128]{3,2,1,0:T(8,128)(2,1)S(1)}, bf16[2,64,16,128]{3,2,1,0:T(8,128)(2,1)S(1)}, u32[]{:S(2)}, u32[]{:S(2)}) collective-permute-start(bf16[2,64,16,128]{3,2,1,0:T(8,128)(2,1)S(1)} %pad_maximum_fusion.4), channel_id=1, source_target_pairs={{0,1},{1,0},{2,3},{3,2},{4,5},{5,4},{6,7},{7,6},{8,9},{9,8},{10,11... | collective-permute-start | bytes 1572872 | tf_op jit(solution)/shard_map/ppermute | solution.py:23
  7.8 2.6 %collective-permute-start.1 = (bf16[2,64,16,128]{3,2,1,0:T(8,128)(2,1)S(1)}, bf16[2,64,16,128]{3,2,1,0:T(8,128)(2,1)S(1)}, u32[]{:S(2)}, u32[]{:S(2)}) collective-permute-start(bf16[2,64,16,128]{3,2,1,0:T(8,128)(2,1)S(1)} %maximum_select_fusion.1), channel_id=1, source_target_pairs={{1,4},{4,1},{3,6},{6,3},{5,8},{8,5},{7,10},{10,7},{9,12},{12,9},{1... | collective-permute-start | bytes 1572872 | tf_op jit(solution)/shard_map/ppermute | solution.py:184
  10.8 14.5 %collective-permute-start.2 = (bf16[64,15,128]{2,1,0:T(8,128)(2,1)S(1)}, bf16[64,15,128]{2,1,0:T(8,128)(2,1)}, u32[]{:S(2)}, u32[]{:S(2)}) collective-permute-start(bf16[64,15,128]{2,1,0:T(8,128)(2,1)S(1)} %get-tuple-element.51), channel_id=1, source_target_pairs={{1,4},{4,1},{3,6},{6,3},{5,8},{8,5},{7,10},{10,7},{9,12},{12,9},{1... | collective-permute-start | bytes 737288 | tf_op jit(solution)/shard_map/ppermute | solution.py:140
  12.1 13.1 %collective-permute-start.3 = (bf16[64,15,128]{2,1,0:T(8,128)(2,1)S(1)}, bf16[64,15,128]{2,1,0:T(8,128)(2,1)}, u32[]{:S(2)}, u32[]{:S(2)}) collective-permute-start(bf16[64,15,128]{2,1,0:T(8,128)(2,1)S(1)} %get-tuple-element.52), channel_id=1, source_target_pairs={{0,1},{1,0},{2,3},{3,2},{4,5},{5,4},{6,7},{7,6},{8,9},{9,8},{10,11... | collective-permute-start | bytes 737288 | tf_op jit(solution)/shard_map/ppermute | solution.py:23
  25.2 1.7 %copy-start = (bf16[2,64,16,46]{3,2,0,1:T(8,128)(2,1)}, bf16[2,64,16,46]{3,2,0,1:T(8,128)(2,1)S(1)}, u32[]{:S(2)}) copy-start(bf16[2,64,16,46]{3,2,0,1:T(8,128)(2,1)S(1)} %broadcast_in_dim.242) | copy-start | bytes 565252
  27.2 4.9 %collective-permute-start.4 = (bf16[2,15,16,128]{3,2,1,0:T(8,128)(2,1)S(1)}, bf16[2,15,16,128]{3,2,1,0:T(8,128)(2,1)S(1)}, u32[]{:S(2)}, u32[]{:S(2)}) collective-permute-start(bf16[2,15,16,128]{3,2,1,0:T(8,128)(2,1)S(1)} %constant_dynamic-slice_fusion.11), channel_id=1, source_target_pairs={{0,2},{2,0},{1,3},{3,1},{4,6},{6,4},{5,7},{7,5},{8,10},{10,8},{9,1... | collective-permute-start | bytes 368648 | tf_op jit(solution)/shard_map/ppermute | solution.py:121
  35.4 7.2 %copy-start.7 = (bf16[46,16]{0,1:T(8,128)(2,1)S(1)}, bf16[46,16]{0,1:T(8,128)(2,1)}, u32[]{:S(2)}) copy-start(bf16[46,16]{0,1:T(8,128)(2,1)} %get-tuple-element.27) | copy-start | bytes 4420
  35.4 7.2 %copy-start.8 = (bf16[46,16]{0,1:T(8,128)(2,1)S(1)}, bf16[46,16]{0,1:T(8,128)(2,1)}, u32[]{:S(2)}) copy-start(bf16[46,16]{0,1:T(8,128)(2,1)} %get-tuple-element.28) | copy-start | bytes 4420
  35.4 7.2 %copy-start.6 = (bf16[94,64]{0,1:T(8,128)(2,1)S(1)}, bf16[94,64]{0,1:T(8,128)(2,1)}, u32[]{:S(2)}) copy-start(bf16[94,64]{0,1:T(8,128)(2,1)} %get-tuple-element.24) | copy-start | bytes 36100
  35.4 7.2 %copy-start.4 = (bf16[128,128]{1,0:T(8,128)(2,1)S(1)}, bf16[128,128]{1,0:T(8,128)(2,1)}, u32[]{:S(2)}) copy-start(bf16[128,128]{1,0:T(8,128)(2,1)} %get-tuple-element.19) | copy-start | bytes 98308
  35.4 7.2 %copy-start.5 = (bf16[128,128]{1,0:T(8,128)(2,1)S(1)}, bf16[128,128]{1,0:T(8,128)(2,1)}, u32[]{:S(2)}) copy-start(bf16[128,128]{1,0:T(8,128)(2,1)} %get-tuple-element.20) | copy-start | bytes 98308
  35.9 6.8 %collective-permute-start.5 = (bf16[2,64,15,128]{3,2,1,0:T(8,128)(2,1)S(1)}, bf16[2,64,15,128]{3,2,1,0:T(8,128)(2,1)S(1)}, u32[]{:S(2)}, u32[]{:S(2)}) collective-permute-start(bf16[2,64,15,128]{3,2,1,0:T(8,128)(2,1)S(1)} %get-tuple-element.43), channel_id=1, source_target_pairs={{1,4},{4,1},{3,6},{6,3},{5,8},{8,5},{7,10},{10,7},{9,12},{12,9},{1... | collective-permute-start | bytes 1474568 | tf_op jit(solution)/shard_map/ppermute | solution.py:140
  36.6 7.5 %collective-permute-start.6 = (bf16[2,64,15,128]{3,2,1,0:T(8,128)(2,1)S(1)}, bf16[2,64,15,128]{3,2,1,0:T(8,128)(2,1)S(1)}, u32[]{:S(2)}, u32[]{:S(2)}) collective-permute-start(bf16[2,64,15,128]{3,2,1,0:T(8,128)(2,1)S(1)} %get-tuple-element.44), channel_id=1, source_target_pairs={{0,1},{1,0},{2,3},{3,2},{4,5},{5,4},{6,7},{7,6},{8,9},{9,8},{10,11... | collective-permute-start | bytes 1474568 | tf_op jit(solution)/shard_map/ppermute | solution.py:23
  42.7 1.5 %copy-start.2 = (bf16[2,64,16,46]{3,2,1,0:T(8,128)(2,1)}, bf16[2,64,16,46]{3,2,1,0:T(8,128)(2,1)S(1)}, u32[]{:S(2)}) copy-start(bf16[2,64,16,46]{3,2,1,0:T(8,128)(2,1)S(1)} %broadcast_in_dim.221) | copy-start | bytes 565252
  45.1 4.9 %collective-permute-start.7 = (bf16[2,15,16,128]{3,2,1,0:T(8,128)(2,1)S(1)}, bf16[2,15,16,128]{3,2,1,0:T(8,128)(2,1)S(1)}, u32[]{:S(2)}, u32[]{:S(2)}) collective-permute-start(bf16[2,15,16,128]{3,2,1,0:T(8,128)(2,1)S(1)} %constant_dynamic-slice_fusion.8), channel_id=1, source_target_pairs={{0,2},{2,0},{1,3},{3,1},{4,6},{6,4},{5,7},{7,5},{8,10},{10,8},{9,1... | collective-permute-start | bytes 368648 | tf_op jit(solution)/shard_map/ppermute | solution.py:121
  53.1 11.0 %copy-start.1 = (bf16[2,64,16,46]{3,2,0,1:T(8,128)(2,1)S(1)}, bf16[2,64,16,46]{3,2,0,1:T(8,128)(2,1)}, u32[]{:S(2)}) copy-start(bf16[2,64,16,46]{3,2,0,1:T(8,128)(2,1)} %copy-done) | copy-start | bytes 565252
  53.3 9.6 %collective-permute-start.8 = (bf16[64,15,128]{2,1,0:T(8,128)(2,1)S(1)}, bf16[64,15,128]{2,1,0:T(8,128)(2,1)S(1)}, u32[]{:S(2)}, u32[]{:S(2)}) collective-permute-start(bf16[64,15,128]{2,1,0:T(8,128)(2,1)S(1)} %get-tuple-element.49), channel_id=1, source_target_pairs={{1,4},{4,1},{3,6},{6,3},{5,8},{8,5},{7,10},{10,7},{9,12},{12,9},{1... | collective-permute-start | bytes 737288 | tf_op jit(solution)/shard_map/ppermute | solution.py:140
  54.2 9.9 %collective-permute-start.9 = (bf16[64,15,128]{2,1,0:T(8,128)(2,1)S(1)}, bf16[64,15,128]{2,1,0:T(8,128)(2,1)S(1)}, u32[]{:S(2)}, u32[]{:S(2)}) collective-permute-start(bf16[64,15,128]{2,1,0:T(8,128)(2,1)S(1)} %get-tuple-element.50), channel_id=1, source_target_pairs={{0,1},{1,0},{2,3},{3,2},{4,5},{5,4},{6,7},{7,6},{8,9},{9,8},{10,11... | collective-permute-start | bytes 737288 | tf_op jit(solution)/shard_map/ppermute | solution.py:23
  64.9 4.9 %collective-permute-start.10 = (bf16[2,15,16,128]{3,2,1,0:T(8,128)(2,1)S(1)}, bf16[2,15,16,128]{3,2,1,0:T(8,128)(2,1)S(1)}, u32[]{:S(2)}, u32[]{:S(2)}) collective-permute-start(bf16[2,15,16,128]{3,2,1,0:T(8,128)(2,1)S(1)} %constant_dynamic-slice_fusion.5), channel_id=1, source_target_pairs={{0,2},{2,0},{1,3},{3,1},{4,6},{6,4},{5,7},{7,5},{8,10},{10,8},{9,1... | collective-permute-start | bytes 368648 | tf_op jit(solution)/shard_map/ppermute | solution.py:121
  73.5 6.6 %collective-permute-start.11 = (bf16[2,64,15,128]{3,2,1,0:T(8,128)(2,1)S(1)}, bf16[2,64,15,128]{3,2,1,0:T(8,128)(2,1)S(1)}, u32[]{:S(2)}, u32[]{:S(2)}) collective-permute-start(bf16[2,64,15,128]{3,2,1,0:T(8,128)(2,1)S(1)} %get-tuple-element.39), channel_id=1, source_target_pairs={{1,4},{4,1},{3,6},{6,3},{5,8},{8,5},{7,10},{10,7},{9,12},{12,9},{1... | collective-permute-start | bytes 1474568 | tf_op jit(solution)/shard_map/ppermute | solution.py:140
  74.2 7.5 %copy-start.3 = (bf16[2,64,16,46]{3,2,1,0:T(8,128)(2,1)S(1)}, bf16[2,64,16,46]{3,2,1,0:T(8,128)(2,1)}, u32[]{:S(2)}) copy-start(bf16[2,64,16,46]{3,2,1,0:T(8,128)(2,1)} %copy-done.2) | copy-start | bytes 565252
  74.2 7.5 %collective-permute-start.12 = (bf16[2,64,15,128]{3,2,1,0:T(8,128)(2,1)S(1)}, bf16[2,64,15,128]{3,2,1,0:T(8,128)(2,1)S(1)}, u32[]{:S(2)}, u32[]{:S(2)}) collective-permute-start(bf16[2,64,15,128]{3,2,1,0:T(8,128)(2,1)S(1)} %get-tuple-element.40), channel_id=1, source_target_pairs={{0,1},{1,0},{2,3},{3,2},{4,5},{5,4},{6,7},{7,6},{8,9},{9,8},{10,11... | collective-permute-start | bytes 1474568 | tf_op jit(solution)/shard_map/ppermute | solution.py:23
  82.6 4.9 %collective-permute-start.13 = (bf16[2,15,16,128]{3,2,1,0:T(8,128)(2,1)S(1)}, bf16[2,15,16,128]{3,2,1,0:T(8,128)(2,1)S(1)}, u32[]{:S(2)}, u32[]{:S(2)}) collective-permute-start(bf16[2,15,16,128]{3,2,1,0:T(8,128)(2,1)S(1)} %constant_dynamic-slice_fusion.2), channel_id=1, source_target_pairs={{0,2},{2,0},{1,3},{3,1},{4,6},{6,4},{5,7},{7,5},{8,10},{10,8},{9,1... | collective-permute-start | bytes 368648 | tf_op jit(solution)/shard_map/ppermute | solution.py:121
  88.7 5.6 %collective-permute-start.14 = (f32[32,16,128]{2,1,0:T(8,128)S(1)}, f32[32,16,128]{2,1,0:T(8,128)S(1)}, u32[]{:S(2)}, u32[]{:S(2)}) collective-permute-start(f32[32,16,128]{2,1,0:T(8,128)S(1)} %get-tuple-element.38), channel_id=1, source_target_pairs={{0,1},{1,0},{2,3},{3,2},{4,5},{5,4},{6,7},{7,6},{8,9},{9,8},{10,11... | collective-permute-start | bytes 786440 | tf_op jit(solution)/shard_map/ppermute | solution.py:23
  (1 other events, 0.7 us)

commit v9 on v8

--- a/solution.py
+++ b/solution.py
@@ -94,10 +94,7 @@
 def pass_z_views(after_y, matrices, reach):
     below, above = z_rims(after_y, reach, 1)
     widened = jnp.concatenate([below, after_y, above], axis=1)
-    shape = widened.shape
-    flat = widened.reshape(shape[0], shape[1], -1)
-    out = jnp.einsum("vpa,vam->vpm", matrices, flat, preferred_element_type=jnp.float32)
-    return out.reshape((shape[0], matrices.shape[1]) + shape[2:])
+    return jnp.einsum("vpa,vaxy->vpxy", matrices, widened, preferred_element_type=jnp.float32)
 
 
 def z_rims(volume, reach, axis):

time: 95.8 us -> 91.6 us (0.956)
  local copies, waits for them, and re-layouts: 11.9 us -> 7.28 us
  other arithmetic: 11.9 us -> 10.7 us
  starting transfers between devices: 47.8 us -> 48.8 us
    reshape x4 -> x0, local copies, waits for them, and re-layouts: 4.89 us -> none  [pass_z_views(): flat = widened.reshape(shape[0], shape[1], -1)]
    concatenate x4 -> x0, other arithmetic: 3.02 us -> none  [pass_z_views(): widened = jnp.concatenate([below, after_y, above], axis=1)]
    ppermute x6, starting transfers between devices: 37.3 us -> 39 us  [from_partner(): return lax.ppermute(block, axis, route)]
    convert_element_type x2, other arithmetic: 0.45 us -> 1.47 us  [local(): quotients = (observed / blurred).astype(jnp.bfloat16)]
    unnamed x25 -> x11, local copies, waits for them, and re-layouts: 1.95 us -> 1.34 us
where the time goes in v9:
time: 91.6 us; the launch traced here: 91.1 us
  starting transfers between devices  48.8 us (53%)
  waiting for transfers between devices  19.2 us (21%)
  other arithmetic  10.7 us (12%)
  local copies, waits for them, and re-layouts  7.28 us (8%)
  matrix products  4.6 us (5%)
    ppermute x6, starting transfers between devices, from_partner(): return lax.ppermute(block, axis, route)  39 us
    ppermute x4, waiting for transfers between devices, z_rims(): got = lax.ppermute(payload, 'view', route)  13.9 us
    ppermute x4, starting transfers between devices, z_rims(): got = lax.ppermute(payload, 'view', route)  6.22 us
    ppermute x6, waiting for transfers between devices, from_partner(): return lax.ppermute(block, axis, route)  5.25 us
    ppermute x4, starting transfers between devices, x_rims(): across = lax.ppermute(outward, ('tile', 'view'), route)  2.92 us
    reduce_sum x3, other arithmetic, band_matrix(): matrix = jnp.sum(jnp.where(hit, taps, jnp.float32(0.0)), axis=2)  2.88 us
  transfers between devices with their start and end apart: 15, of which 8 were waited for; matrix products, arithmetic and copies ran while one was open for 6% of the time, Pallas kernels for 0%

profile of v9, /device:TPU:0, one launch (start us, length us, event | category | flops | bytes accessed | tf_op | source)
XLA Modules:
  0.0 91.1 jit_solution(13988995696133294602)
XLA Ops:
  0.0 0.9 fusion.83
  1.0 1.2 %copy.47 = bf16[64,32,128]{2,0,1:T(8,128)(2,1)S(1)} copy(bf16[64,32,128]{2,1,0:T(8,128)(2,1)} %param.3) | data formatting | bytes 1048576 | tf_op args[0]
  5.5 1.1 %select_reduce_fusion.5 = (bf16[94,64]{0,1:T(8,128)(2,1)S(1)}, bf16[94,64]{0,1:T(8,128)(2,1)S(1)}, bf16[94,64]{0,1:T(8,128)(2,1)S(1)}, bf16[94,64]{0,1:T(8,128)(2,1)}) fusion(f32[31]{0:T(128)S(1)} %get-tuple-element.72, s32[94,64]{0,1:T(8,128)S(1)} %iota_subtract_fusion, f32[31]{0:T(128)S(1)} %get-tuple-element.73, f32[31]{0:T(128)S(1)} %get-tuple-element.97, ...), kind=kLoop, calls=%fused_computation.35 | loop fusion | flops 1654400 | bytes 72688 | tf_op jit(solution)/shard_map/reduce_sum | solution.py:45
  7.5 1.0 %select_reduce_fusion.1 = (bf16[128,128]{1,0:T(8,128)(2,1)S(1)}, bf16[128,128]{1,0:T(8,128)(2,1)S(1)}, bf16[128,128]{1,0:T(8,128)(2,1)S(1)}, bf16[128,128]{1,0:T(8,128)(2,1)S(1)}) fusion(f32[31]{0:T(128)S(1)} %get-tuple-element.70, s32[128,128]{1,0:T(8,128)S(1)} %subtract_add_fusion, f32[31]{0:T(128)S(1)} %get-tuple-element.71, f32[31]{0:T(128)S(1)} %get-tuple-element.95, ...), kind=kLoop, calls=%fused_computation.2 | loop fusion | flops 4505600 | bytes 197104 | tf_op jit(solution)/shard_map/reduce_sum | solution.py:45
  11.4 13.2 %collective-permute-start.3 = (bf16[64,15,128]{2,1,0:T(8,128)(2,1)S(1)}, bf16[64,15,128]{2,1,0:T(8,128)(2,1)}, u32[]{:S(2)}, u32[]{:S(2)}) collective-permute-start(bf16[64,15,128]{2,1,0:T(8,128)(2,1)S(1)} %get-tuple-element.58), channel_id=1, source_target_pairs={{0,1},{1,0},{2,3},{3,2},{4,5},{5,4},{6,7},{7,6},{8,9},{9,8},{10,11... | collective-permute-start | bytes 737288 | tf_op jit(solution)/shard_map/ppermute | solution.py:23
  26.1 1.0 %broadcast_select_fusion.7 = (bf16[64,15,128]{2,1,0:T(8,128)(2,1)S(1)}, bf16[64,15,128]{2,1,0:T(8,128)(2,1)S(1)}) fusion(bf16[64,15,128]{2,1,0:T(8,128)(2,1)S(1)} %collective-permute-done.2, bf16[64,15,128]{2,1,0:T(8,128)(2,1)} %collective-permute-done.3, pred[]{:T(512)S(6)} %eq.96), kind=kLoop, calls=%fused_computation.104 | loop fusion | flops 245760 | bytes 983041 | tf_op jit(solution)/shard_map/jit(_where)/select_n | solution.py:139
  28.1 1.6 %collective-permute-start.4 = (bf16[2,15,16,128]{3,1,2,0:T(8,128)(2,1)S(1)}, bf16[2,15,16,128]{3,1,2,0:T(8,128)(2,1)S(1)}, u32[]{:S(2)}, u32[]{:S(2)}) collective-permute-start(bf16[2,15,16,128]{3,1,2,0:T(8,128)(2,1)S(1)} %constant_dynamic-slice_fusion.7), channel_id=1, source_target_pairs={{0,2},{2,0},{1,3},{3,1},{4,6},{6,4},{5,7},{7,5},{8,10},{10,8},{9,1... | collective-permute-start | bytes 368648 | tf_op jit(solution)/shard_map/ppermute | solution.py:118
  29.6 3.5 %collective-permute-done.4 = bf16[2,15,16,128]{3,1,2,0:T(8,128)(2,1)S(1)} collective-permute-done((bf16[2,15,16,128]{3,1,2,0:T(8,128)(2,1)S(1)}, bf16[2,15,16,128]{3,1,2,0:T(8,128)(2,1)S(1)}, u32[]{:S(2)}, u32[]{:S(2)}) %collective-permute-start.4) | collective-permute-done | bytes 122912 | tf_op jit(solution)/shard_map/ppermute | solution.py:118
  35.4 6.1 %collective-permute-start.6 = (bf16[2,64,15,128]{3,2,1,0:T(8,128)(2,1)S(1)}, bf16[2,64,15,128]{3,2,1,0:T(8,128)(2,1)S(1)}, u32[]{:S(2)}, u32[]{:S(2)}) collective-permute-start(bf16[2,64,15,128]{3,2,1,0:T(8,128)(2,1)S(1)} %get-tuple-element.50), channel_id=1, source_target_pairs={{0,1},{1,0},{2,3},{3,2},{4,5},{5,4},{6,7},{7,6},{8,9},{9,8},{10,11... | collective-permute-start | bytes 1474568 | tf_op jit(solution)/shard_map/ppermute | solution.py:23
  41.7 1.4 %collective-permute-done.6 = bf16[2,64,15,128]{3,2,1,0:T(8,128)(2,1)S(1)} collective-permute-done((bf16[2,64,15,128]{3,2,1,0:T(8,128)(2,1)S(1)}, bf16[2,64,15,128]{3,2,1,0:T(8,128)(2,1)S(1)}, u32[]{:S(2)}, u32[]{:S(2)}) %collective-permute-start.6) | collective-permute-done | bytes 491552 | tf_op jit(solution)/shard_map/ppermute | solution.py:23
  44.2 1.6 %collective-permute-start.7 = (bf16[2,15,16,128]{3,1,2,0:T(8,128)(2,1)S(1)}, bf16[2,15,16,128]{3,1,2,0:T(8,128)(2,1)S(1)}, u32[]{:S(2)}, u32[]{:S(2)}) collective-permute-start(bf16[2,15,16,128]{3,1,2,0:T(8,128)(2,1)S(1)} %constant_dynamic-slice_fusion.4), channel_id=1, source_target_pairs={{0,2},{2,0},{1,3},{3,1},{4,6},{6,4},{5,7},{7,5},{8,10},{10,8},{9,1... | collective-permute-start | bytes 368648 | tf_op jit(solution)/shard_map/ppermute | solution.py:118
  45.7 3.5 %collective-permute-done.7 = bf16[2,15,16,128]{3,1,2,0:T(8,128)(2,1)S(1)} collective-permute-done((bf16[2,15,16,128]{3,1,2,0:T(8,128)(2,1)S(1)}, bf16[2,15,16,128]{3,1,2,0:T(8,128)(2,1)S(1)}, u32[]{:S(2)}, u32[]{:S(2)}) %collective-permute-start.7) | collective-permute-done | bytes 122912 | tf_op jit(solution)/shard_map/ppermute | solution.py:118
  50.6 0.9 collective-permute-start.8
  51.5 8.8 %collective-permute-start.9 = (bf16[64,15,128]{2,1,0:T(8,128)(2,1)S(1)}, bf16[64,15,128]{2,1,0:T(8,128)(2,1)S(1)}, u32[]{:S(2)}, u32[]{:S(2)}) collective-permute-start(bf16[64,15,128]{2,1,0:T(8,128)(2,1)S(1)} %get-tuple-element.56), channel_id=1, source_target_pairs={{0,1},{1,0},{2,3},{3,2},{4,5},{5,4},{6,7},{7,6},{8,9},{9,8},{10,11... | collective-permute-start | bytes 737288 | tf_op jit(solution)/shard_map/ppermute | solution.py:23
  60.3 1.2 %collective-permute-done.9 = bf16[64,15,128]{2,1,0:T(8,128)(2,1)S(1)} collective-permute-done((bf16[64,15,128]{2,1,0:T(8,128)(2,1)S(1)}, bf16[64,15,128]{2,1,0:T(8,128)(2,1)S(1)}, u32[]{:S(2)}, u32[]{:S(2)}) %collective-permute-start.9) | collective-permute-done | bytes 245792 | tf_op jit(solution)/shard_map/ppermute | solution.py:23
  62.5 1.5 %collective-permute-start.10 = (bf16[2,15,16,128]{3,1,2,0:T(8,128)(2,1)S(1)}, bf16[2,15,16,128]{3,1,2,0:T(8,128)(2,1)S(1)}, u32[]{:S(2)}, u32[]{:S(2)}) collective-permute-start(bf16[2,15,16,128]{3,1,2,0:T(8,128)(2,1)S(1)} %constant_dynamic-slice_fusion.3), channel_id=1, source_target_pairs={{0,2},{2,0},{1,3},{3,1},{4,6},{6,4},{5,7},{7,5},{8,10},{10,8},{9,1... | collective-permute-start | bytes 368648 | tf_op jit(solution)/shard_map/ppermute | solution.py:118
  64.0 3.5 %collective-permute-done.10 = bf16[2,15,16,128]{3,1,2,0:T(8,128)(2,1)S(1)} collective-permute-done((bf16[2,15,16,128]{3,1,2,0:T(8,128)(2,1)S(1)}, bf16[2,15,16,128]{3,1,2,0:T(8,128)(2,1)S(1)}, u32[]{:S(2)}, u32[]{:S(2)}) %collective-permute-start.10) | collective-permute-done | bytes 122912 | tf_op jit(solution)/shard_map/ppermute | solution.py:118
  69.8 5.9 %collective-permute-start.12 = (bf16[2,64,15,128]{3,2,1,0:T(8,128)(2,1)S(1)}, bf16[2,64,15,128]{3,2,1,0:T(8,128)(2,1)S(1)}, u32[]{:S(2)}, u32[]{:S(2)}) collective-permute-start(bf16[2,64,15,128]{3,2,1,0:T(8,128)(2,1)S(1)} %get-tuple-element.46), channel_id=1, source_target_pairs={{0,1},{1,0},{2,3},{3,2},{4,5},{5,4},{6,7},{7,6},{8,9},{9,8},{10,11... | collective-permute-start | bytes 1474568 | tf_op jit(solution)/shard_map/ppermute | solution.py:23
  75.8 1.5 %collective-permute-done.12 = bf16[2,64,15,128]{3,2,1,0:T(8,128)(2,1)S(1)} collective-permute-done((bf16[2,64,15,128]{3,2,1,0:T(8,128)(2,1)S(1)}, bf16[2,64,15,128]{3,2,1,0:T(8,128)(2,1)S(1)}, u32[]{:S(2)}, u32[]{:S(2)}) %collective-permute-start.12) | collective-permute-done | bytes 491552 | tf_op jit(solution)/shard_map/ppermute | solution.py:23
  78.4 1.6 %collective-permute-start.13 = (bf16[2,15,16,128]{3,1,2,0:T(8,128)(2,1)S(1)}, bf16[2,15,16,128]{3,1,2,0:T(8,128)(2,1)S(1)}, u32[]{:S(2)}, u32[]{:S(2)}) collective-permute-start(bf16[2,15,16,128]{3,1,2,0:T(8,128)(2,1)S(1)} %constant_dynamic-slice_fusion), channel_id=1, source_target_pairs={{0,2},{2,0},{1,3},{3,1},{4,6},{6,4},{5,7},{7,5},{8,10},{10,8},{9,1... | collective-permute-start | bytes 368648 | tf_op jit(solution)/shard_map/ppermute | solution.py:118
  80.0 3.5 %collective-permute-done.13 = bf16[2,15,16,128]{3,1,2,0:T(8,128)(2,1)S(1)} collective-permute-done((bf16[2,15,16,128]{3,1,2,0:T(8,128)(2,1)S(1)}, bf16[2,15,16,128]{3,1,2,0:T(8,128)(2,1)S(1)}, u32[]{:S(2)}, u32[]{:S(2)}) %collective-permute-start.13) | collective-permute-done | bytes 122912 | tf_op jit(solution)/shard_map/ppermute | solution.py:118
  84.7 4.5 %collective-permute-start.14 = (f32[32,16,128]{2,1,0:T(8,128)S(1)}, f32[32,16,128]{2,1,0:T(8,128)S(1)}, u32[]{:S(2)}, u32[]{:S(2)}) collective-permute-start(f32[32,16,128]{2,1,0:T(8,128)S(1)} %get-tuple-element.44), channel_id=1, source_target_pairs={{0,1},{1,0},{2,3},{3,2},{4,5},{5,4},{6,7},{7,6},{8,9},{9,8},{10,11... | collective-permute-start | bytes 786440 | tf_op jit(solution)/shard_map/ppermute | solution.py:23
  89.1 1.2 %collective-permute-done.14 = f32[32,16,128]{2,1,0:T(8,128)S(1)} collective-permute-done((f32[32,16,128]{2,1,0:T(8,128)S(1)}, f32[32,16,128]{2,1,0:T(8,128)S(1)}, u32[]{:S(2)}, u32[]{:S(2)}) %collective-permute-start.14) | collective-permute-done | bytes 262176 | tf_op jit(solution)/shard_map/ppermute | solution.py:23
  90.3 0.8 maximum_select_fusion.2
  (106 shorter events, 19.8 us)
Async XLA Ops:
  4.5 0.7 copy-start.4
  4.5 3.9 %collective-permute-start = (bf16[2,64,16,128]{3,2,1,0:T(8,128)(2,1)S(1)}, bf16[2,64,16,128]{3,2,1,0:T(8,128)(2,1)S(1)}, u32[]{:S(2)}, u32[]{:S(2)}) collective-permute-start(bf16[2,64,16,128]{3,2,1,0:T(8,128)(2,1)S(1)} %pad_maximum_fusion), channel_id=1, source_target_pairs={{0,1},{1,0},{2,3},{3,2},{4,5},{5,4},{6,7},{7,6},{8,9},{9,8},{10,11... | collective-permute-start | bytes 1572872 | tf_op jit(solution)/shard_map/ppermute | solution.py:23
  8.6 1.7 %collective-permute-start.1 = (bf16[2,64,16,128]{3,2,1,0:T(8,128)(2,1)S(1)}, bf16[2,64,16,128]{3,2,1,0:T(8,128)(2,1)S(1)}, u32[]{:S(2)}, u32[]{:S(2)}) collective-permute-start(bf16[2,64,16,128]{3,2,1,0:T(8,128)(2,1)S(1)} %maximum_select_fusion.1), channel_id=1, source_target_pairs={{1,4},{4,1},{3,6},{6,3},{5,8},{8,5},{7,10},{10,7},{9,12},{12,9},{1... | collective-permute-start | bytes 1572872 | tf_op jit(solution)/shard_map/ppermute | solution.py:181
  10.7 15.4 %collective-permute-start.2 = (bf16[64,15,128]{2,1,0:T(8,128)(2,1)S(1)}, bf16[64,15,128]{2,1,0:T(8,128)(2,1)S(1)}, u32[]{:S(2)}, u32[]{:S(2)}) collective-permute-start(bf16[64,15,128]{2,1,0:T(8,128)(2,1)S(1)} %get-tuple-element.57), channel_id=1, source_target_pairs={{1,4},{4,1},{3,6},{6,3},{5,8},{8,5},{7,10},{10,7},{9,12},{12,9},{1... | collective-permute-start | bytes 737288 | tf_op jit(solution)/shard_map/ppermute | solution.py:137
  11.4 14.7 %collective-permute-start.3 = (bf16[64,15,128]{2,1,0:T(8,128)(2,1)S(1)}, bf16[64,15,128]{2,1,0:T(8,128)(2,1)}, u32[]{:S(2)}, u32[]{:S(2)}) collective-permute-start(bf16[64,15,128]{2,1,0:T(8,128)(2,1)S(1)} %get-tuple-element.58), channel_id=1, source_target_pairs={{0,1},{1,0},{2,3},{3,2},{4,5},{5,4},{6,7},{7,6},{8,9},{9,8},{10,11... | collective-permute-start | bytes 737288 | tf_op jit(solution)/shard_map/ppermute | solution.py:23
  27.8 5.3 %copy-start.1 = (bf16[2,64,94]{2,1,0:T(8,128)(2,1)S(1)}, bf16[2,64,94]{2,1,0:T(8,128)(2,1)}, u32[]{:S(2)}) copy-start(bf16[2,64,94]{2,1,0:T(8,128)(2,1)} %pad_maximum_fusion.4) | copy-start | bytes 72196
  28.1 5.0 %collective-permute-start.4 = (bf16[2,15,16,128]{3,1,2,0:T(8,128)(2,1)S(1)}, bf16[2,15,16,128]{3,1,2,0:T(8,128)(2,1)S(1)}, u32[]{:S(2)}, u32[]{:S(2)}) collective-permute-start(bf16[2,15,16,128]{3,1,2,0:T(8,128)(2,1)S(1)} %constant_dynamic-slice_fusion.7), channel_id=1, source_target_pairs={{0,2},{2,0},{1,3},{3,1},{4,6},{6,4},{5,7},{7,5},{8,10},{10,8},{9,1... | collective-permute-start | bytes 368648 | tf_op jit(solution)/shard_map/ppermute | solution.py:118
  34.3 7.2 %copy-start.2 = (bf16[46,16]{0,1:T(8,128)(2,1)S(1)}, bf16[46,16]{0,1:T(8,128)(2,1)}, u32[]{:S(2)}) copy-start(bf16[46,16]{0,1:T(8,128)(2,1)} %get-tuple-element.27) | copy-start | bytes 4420
  34.3 7.2 %copy-start.3 = (bf16[46,16]{0,1:T(8,128)(2,1)S(1)}, bf16[46,16]{0,1:T(8,128)(2,1)}, u32[]{:S(2)}) copy-start(bf16[46,16]{0,1:T(8,128)(2,1)} %get-tuple-element.28) | copy-start | bytes 4420
  34.3 7.2 %copy-start = (bf16[94,64]{0,1:T(8,128)(2,1)S(1)}, bf16[94,64]{0,1:T(8,128)(2,1)}, u32[]{:S(2)}) copy-start(bf16[94,64]{0,1:T(8,128)(2,1)} %get-tuple-element.24) | copy-start | bytes 36100
  34.7 6.9 %collective-permute-start.5 = (bf16[2,64,15,128]{3,2,1,0:T(8,128)(2,1)S(1)}, bf16[2,64,15,128]{3,2,1,0:T(8,128)(2,1)S(1)}, u32[]{:S(2)}, u32[]{:S(2)}) collective-permute-start(bf16[2,64,15,128]{3,2,1,0:T(8,128)(2,1)S(1)} %get-tuple-element.49), channel_id=1, source_target_pairs={{1,4},{4,1},{3,6},{6,3},{5,8},{8,5},{7,10},{10,7},{9,12},{12,9},{1... | collective-permute-start | bytes 1474568 | tf_op jit(solution)/shard_map/ppermute | solution.py:137
  35.4 7.6 %collective-permute-start.6 = (bf16[2,64,15,128]{3,2,1,0:T(8,128)(2,1)S(1)}, bf16[2,64,15,128]{3,2,1,0:T(8,128)(2,1)S(1)}, u32[]{:S(2)}, u32[]{:S(2)}) collective-permute-start(bf16[2,64,15,128]{3,2,1,0:T(8,128)(2,1)S(1)} %get-tuple-element.50), channel_id=1, source_target_pairs={{0,1},{1,0},{2,3},{3,2},{4,5},{5,4},{6,7},{7,6},{8,9},{9,8},{10,11... | collective-permute-start | bytes 1474568 | tf_op jit(solution)/shard_map/ppermute | solution.py:23
  44.2 5.0 %collective-permute-start.7 = (bf16[2,15,16,128]{3,1,2,0:T(8,128)(2,1)S(1)}, bf16[2,15,16,128]{3,1,2,0:T(8,128)(2,1)S(1)}, u32[]{:S(2)}, u32[]{:S(2)}) collective-permute-start(bf16[2,15,16,128]{3,1,2,0:T(8,128)(2,1)S(1)} %constant_dynamic-slice_fusion.4), channel_id=1, source_target_pairs={{0,2},{2,0},{1,3},{3,1},{4,6},{6,4},{5,7},{7,5},{8,10},{10,8},{9,1... | collective-permute-start | bytes 368648 | tf_op jit(solution)/shard_map/ppermute | solution.py:118
  50.6 9.7 %collective-permute-start.8 = (bf16[64,15,128]{2,1,0:T(8,128)(2,1)S(1)}, bf16[64,15,128]{2,1,0:T(8,128)(2,1)S(1)}, u32[]{:S(2)}, u32[]{:S(2)}) collective-permute-start(bf16[64,15,128]{2,1,0:T(8,128)(2,1)S(1)} %get-tuple-element.55), channel_id=1, source_target_pairs={{1,4},{4,1},{3,6},{6,3},{5,8},{8,5},{7,10},{10,7},{9,12},{12,9},{1... | collective-permute-start | bytes 737288 | tf_op jit(solution)/shard_map/ppermute | solution.py:137
  51.5 10.0 %collective-permute-start.9 = (bf16[64,15,128]{2,1,0:T(8,128)(2,1)S(1)}, bf16[64,15,128]{2,1,0:T(8,128)(2,1)S(1)}, u32[]{:S(2)}, u32[]{:S(2)}) collective-permute-start(bf16[64,15,128]{2,1,0:T(8,128)(2,1)S(1)} %get-tuple-element.56), channel_id=1, source_target_pairs={{0,1},{1,0},{2,3},{3,2},{4,5},{5,4},{6,7},{7,6},{8,9},{9,8},{10,11... | collective-permute-start | bytes 737288 | tf_op jit(solution)/shard_map/ppermute | solution.py:23
  62.5 5.0 %collective-permute-start.10 = (bf16[2,15,16,128]{3,1,2,0:T(8,128)(2,1)S(1)}, bf16[2,15,16,128]{3,1,2,0:T(8,128)(2,1)S(1)}, u32[]{:S(2)}, u32[]{:S(2)}) collective-permute-start(bf16[2,15,16,128]{3,1,2,0:T(8,128)(2,1)S(1)} %constant_dynamic-slice_fusion.3), channel_id=1, source_target_pairs={{0,2},{2,0},{1,3},{3,1},{4,6},{6,4},{5,7},{7,5},{8,10},{10,8},{9,1... | collective-permute-start | bytes 368648 | tf_op jit(solution)/shard_map/ppermute | solution.py:118
  69.1 6.6 %collective-permute-start.11 = (bf16[2,64,15,128]{3,2,1,0:T(8,128)(2,1)S(1)}, bf16[2,64,15,128]{3,2,1,0:T(8,128)(2,1)S(1)}, u32[]{:S(2)}, u32[]{:S(2)}) collective-permute-start(bf16[2,64,15,128]{3,2,1,0:T(8,128)(2,1)S(1)} %get-tuple-element.45), channel_id=1, source_target_pairs={{1,4},{4,1},{3,6},{6,3},{5,8},{8,5},{7,10},{10,7},{9,12},{12,9},{1... | collective-permute-start | bytes 1474568 | tf_op jit(solution)/shard_map/ppermute | solution.py:137
  69.8 7.5 %collective-permute-start.12 = (bf16[2,64,15,128]{3,2,1,0:T(8,128)(2,1)S(1)}, bf16[2,64,15,128]{3,2,1,0:T(8,128)(2,1)S(1)}, u32[]{:S(2)}, u32[]{:S(2)}) collective-permute-start(bf16[2,64,15,128]{3,2,1,0:T(8,128)(2,1)S(1)} %get-tuple-element.46), channel_id=1, source_target_pairs={{0,1},{1,0},{2,3},{3,2},{4,5},{5,4},{6,7},{7,6},{8,9},{9,8},{10,11... | collective-permute-start | bytes 1474568 | tf_op jit(solution)/shard_map/ppermute | solution.py:23
  78.4 5.0 %collective-permute-start.13 = (bf16[2,15,16,128]{3,1,2,0:T(8,128)(2,1)S(1)}, bf16[2,15,16,128]{3,1,2,0:T(8,128)(2,1)S(1)}, u32[]{:S(2)}, u32[]{:S(2)}) collective-permute-start(bf16[2,15,16,128]{3,1,2,0:T(8,128)(2,1)S(1)} %constant_dynamic-slice_fusion), channel_id=1, source_target_pairs={{0,2},{2,0},{1,3},{3,1},{4,6},{6,4},{5,7},{7,5},{8,10},{10,8},{9,1... | collective-permute-start | bytes 368648 | tf_op jit(solution)/shard_map/ppermute | solution.py:118
  84.7 5.6 %collective-permute-start.14 = (f32[32,16,128]{2,1,0:T(8,128)S(1)}, f32[32,16,128]{2,1,0:T(8,128)S(1)}, u32[]{:S(2)}, u32[]{:S(2)}) collective-permute-start(f32[32,16,128]{2,1,0:T(8,128)S(1)} %get-tuple-element.44), channel_id=1, source_target_pairs={{0,1},{1,0},{2,3},{3,2},{4,5},{5,4},{6,7},{7,6},{8,9},{9,8},{10,11... | collective-permute-start | bytes 786440 | tf_op jit(solution)/shard_map/ppermute | solution.py:23

commit v10 on v9

--- a/solution.py
+++ b/solution.py
@@ -160,8 +160,11 @@
         target = jnp.clip(target, 0, tile_total - 1)
         starts.append(target * block_count + half * half_blocks)
     slots = jnp.concatenate([lax.dynamic_slice_in_dim(sources, st, half_blocks) for st in starts])
-    picked = jnp.take(blocks, slots % block_count, axis=1)
-    mine = (slots // block_count == tile_index)[None, :, None, None]
+    picked = jnp.concatenate(
+        [lax.dynamic_slice_in_dim(acquired, (slots[i] % block_count) * BX, BX, 1) for i in range(slots.shape[0])],
+        axis=1,
+    )
+    mine = jnp.repeat(slots // block_count == tile_index, BX)[None, :, None]
     partials = jnp.where(mine, picked, jnp.zeros((), picked.dtype))
     partials = partials.reshape(planes, 4, half_x, width_y)
     own_keep = jnp.where(first, partials[:, 0], partials[:, 1])
@@ -186,7 +189,7 @@
     kernels = (psf_taps / jnp.sum(psf_taps, axis=2, keepdims=True)).astype(jnp.bfloat16)
     view_count = kernels.shape[0]
     forward_ops = stacked_operators(kernels, planes, half_x, width_y)
-    adjoint_ops = stacked_operators(kernels[:, :, ::-1], planes, half_x, width_y)
+    adjoint_ops = tuple(jnp.flip(m, axis=(-2, -1)) for m in forward_ops)
     for iteration in range(ITERS):
         estimate_low = estimate.astype(jnp.bfloat16)
         low, high = x_rims(estimate_low, reach, 1)

time: 91.6 us -> 126 us (1.38)
  between operations: 0.56 us -> 30.9 us
  local copies, waits for them, and re-layouts: 7.28 us -> 11.5 us
  other arithmetic: 10.7 us -> 8.66 us
    rev x0 -> x3, local copies, waits for them, and re-layouts: none -> 2.74 us  [local(): adjoint_ops = tuple((jnp.flip(m, axis=(-2, -1)) for m in forward_ops))]
    reduce_sum x3, other arithmetic: 2.88 us -> 0.84 us  [band_matrix(): matrix = jnp.sum(jnp.where(hit, taps, jnp.float32(0.0)), axis=2)]
    dynamic_slice x0 -> x2, local copies, waits for them, and re-layouts: none -> 1.67 us  [the longest x1 0.87 us: local(): lax.dynamic_slice_in_dim(sources, st, half_blocks)]
    ppermute x4, waiting for transfers between devices: 13.9 us -> 12.5 us  [z_rims(): got = lax.ppermute(payload, 'view', route)]
  transfers between devices with their start and end apart: 15 -> 15, of which waited for: 8 -> 10; matrix products, arithmetic and copies ran while one was open for 6% -> 3% of each run, Pallas kernels for 0% -> 0%
where the time goes in v10:
time: 126 us; the launch traced here: 125 us
  starting transfers between devices  49.3 us (39%)
  between operations  30.9 us (25%)
  waiting for transfers between devices  18.9 us (15%)
  local copies, waits for them, and re-layouts  11.5 us (9%)
  other arithmetic  8.66 us (7%)
  matrix products  5.36 us (4%)
    ppermute x6, starting transfers between devices, from_partner(): return lax.ppermute(block, axis, route)  38.7 us
    ppermute x4, waiting for transfers between devices, z_rims(): got = lax.ppermute(payload, 'view', route)  12.5 us
    ppermute x6, waiting for transfers between devices, from_partner(): return lax.ppermute(block, axis, route)  6.42 us
    ppermute x4, starting transfers between devices, z_rims(): got = lax.ppermute(payload, 'view', route)  6.21 us
    ppermute x4, starting transfers between devices, x_rims(): across = lax.ppermute(outward, ('tile', 'view'), route)  3.68 us
    rev x3, local copies, waits for them, and re-layouts, local(): adjoint_ops = tuple((jnp.flip(m, axis=(-2, -1)) for m in forward_ops))  2.74 us
  transfers between devices with their start and end apart: 15, of which 10 were waited for; matrix products, arithmetic and copies ran while one was open for 3% of the time, Pallas kernels for 0%

profile of v10, /device:TPU:0, one launch (start us, length us, event | category | flops | bytes accessed | tf_op | source)
XLA Modules:
  0.0 124.7 jit_solution(15722687784676952265)
XLA Ops:
  39.6 13.6 %collective-permute-start.3 = (bf16[64,15,128]{2,1,0:T(8,128)(2,1)S(1)}, bf16[64,15,128]{2,1,0:T(8,128)(2,1)}, u32[]{:S(2)}, u32[]{:S(2)}) collective-permute-start(bf16[64,15,128]{2,1,0:T(8,128)(2,1)S(1)} %get-tuple-element.62), channel_id=1, source_target_pairs={{0,1},{1,0},{2,3},{3,2},{4,5},{5,4},{6,7},{7,6},{8,9},{9,8},{10,11... | collective-permute-start | bytes 737288 | tf_op jit(solution)/shard_map/ppermute | solution.py:23
  53.4 1.1 collective-permute-done.3
  56.4 1.5 %collective-permute-start.4 = (bf16[2,15,16,128]{3,1,2,0:T(8,128)(2,1)S(1)}, bf16[2,15,16,128]{3,1,2,0:T(8,128)(2,1)S(1)}, u32[]{:S(2)}, u32[]{:S(2)}) collective-permute-start(bf16[2,15,16,128]{3,1,2,0:T(8,128)(2,1)S(1)} %constant_dynamic-slice_fusion.7), channel_id=1, source_target_pairs={{0,2},{2,0},{1,3},{3,1},{4,6},{6,4},{5,7},{7,5},{8,10},{10,8},{9,1... | collective-permute-start | bytes 368648 | tf_op jit(solution)/shard_map/ppermute | solution.py:118
  57.9 3.5 %collective-permute-done.4 = bf16[2,15,16,128]{3,1,2,0:T(8,128)(2,1)S(1)} collective-permute-done((bf16[2,15,16,128]{3,1,2,0:T(8,128)(2,1)S(1)}, bf16[2,15,16,128]{3,1,2,0:T(8,128)(2,1)S(1)}, u32[]{:S(2)}, u32[]{:S(2)}) %collective-permute-start.4) | collective-permute-done | bytes 122912 | tf_op jit(solution)/shard_map/ppermute | solution.py:118
  62.6 1.5 %constant_dynamic-slice_fusion.6 = (bf16[2,64,15,128]{3,2,1,0:T(8,128)(2,1)}, bf16[2,64,15,128]{3,2,1,0:T(8,128)(2,1)}) fusion(bf16[2,64,16,128]{3,2,1,0:T(8,128)(2,1)S(1)} %fusion.21, s32[]{:T(128)S(6)} %select_n.444, s32[]{:T(128)S(6)} %select_n.445), kind=kLoop, calls=%fused_computation.131 | loop fusion | bytes 1966088 | tf_op jit(solution)/shard_map/dynamic_slice | solution.py:135
  64.1 1.4 %collective-permute-start.5 = (bf16[2,64,15,128]{3,2,1,0:T(8,128)(2,1)}, bf16[2,64,15,128]{3,2,1,0:T(8,128)(2,1)}, u32[]{:S(2)}, u32[]{:S(2)}) collective-permute-start(bf16[2,64,15,128]{3,2,1,0:T(8,128)(2,1)} %get-tuple-element.37), channel_id=1, source_target_pairs={{1,4},{4,1},{3,6},{6,3},{5,8},{8,5},{7,10},{10,7},{9,12},{12,9},{1... | collective-permute-start | bytes 1474568 | tf_op jit(solution)/shard_map/ppermute | solution.py:137
  65.5 5.5 %collective-permute-start.6 = (bf16[2,64,15,128]{3,2,1,0:T(8,128)(2,1)}, bf16[2,64,15,128]{3,2,1,0:T(8,128)(2,1)}, u32[]{:S(2)}, u32[]{:S(2)}) collective-permute-start(bf16[2,64,15,128]{3,2,1,0:T(8,128)(2,1)} %get-tuple-element.38), channel_id=1, source_target_pairs={{0,1},{1,0},{2,3},{3,2},{4,5},{5,4},{6,7},{7,6},{8,9},{9,8},{10,11... | collective-permute-start | bytes 1474568 | tf_op jit(solution)/shard_map/ppermute | solution.py:23
  71.0 1.1 rev.13
  72.9 1.3 %broadcast_select_fusion.3 = (bf16[2,64,15,128]{3,2,1,0:T(8,128)(2,1)S(1)}, bf16[2,64,15,128]{3,2,1,0:T(8,128)(2,1)S(1)}) fusion(bf16[2,64,15,128]{3,2,1,0:T(8,128)(2,1)} %collective-permute-done.5, bf16[2,64,15,128]{3,2,1,0:T(8,128)(2,1)} %collective-permute-done.6, pred[]{:T(512)S(6)} %eq.125), kind=kLoop, calls=%fused_computation.84 | loop fusion | flops 491520 | bytes 1966081 | tf_op jit(solution)/shard_map/jit(_where)/select_n | solution.py:139
  75.3 1.6 %collective-permute-start.7 = (bf16[2,15,16,128]{3,1,2,0:T(8,128)(2,1)S(1)}, bf16[2,15,16,128]{3,1,2,0:T(8,128)(2,1)S(1)}, u32[]{:S(2)}, u32[]{:S(2)}) collective-permute-start(bf16[2,15,16,128]{3,1,2,0:T(8,128)(2,1)S(1)} %constant_dynamic-slice_fusion.4), channel_id=1, source_target_pairs={{0,2},{2,0},{1,3},{3,1},{4,6},{6,4},{5,7},{7,5},{8,10},{10,8},{9,1... | collective-permute-start | bytes 368648 | tf_op jit(solution)/shard_map/ppermute | solution.py:118
  76.8 1.5 %rev.12 = bf16[2,64,94]{2,1,0:T(8,128)(2,1)} reverse(bf16[2,64,94]{2,1,0:T(8,128)(2,1)} %copy-done.4), dimensions={1,2} | reverse | bytes 48128 | tf_op jit(solution)/shard_map/jit(_flip)/rev | solution.py:192
  78.3 2.0 %collective-permute-done.7 = bf16[2,15,16,128]{3,1,2,0:T(8,128)(2,1)S(1)} collective-permute-done((bf16[2,15,16,128]{3,1,2,0:T(8,128)(2,1)S(1)}, bf16[2,15,16,128]{3,1,2,0:T(8,128)(2,1)S(1)}, u32[]{:S(2)}, u32[]{:S(2)}) %collective-permute-start.7) | collective-permute-done | bytes 122912 | tf_op jit(solution)/shard_map/ppermute | solution.py:118
  80.3 1.2 fusion.32
  81.6 1.5 %fusion.85 = (bf16[1,64,16,128]{3,2,1,0:T(8,128)(2,1)S(1)}, f32[1,64,16,128]{3,2,1,0:T(8,128)}) fusion(f32[1,64,16,128]{3,1,2,0:T(8,128)S(1)} %get-tuple-element.24, f32[1,64,16,128]{3,1,2,0:T(8,128)S(1)} %get-tuple-element.23, f32[2,64,16,128]{3,2,1,0:T(8,128)S(1)} %fusion.56), kind=kLoop, calls=%fused_computation.187 | loop fusion | flops 786432 | bytes 2883584 | tf_op jit(solution)/shard_map/convert_element_type | solution.py:194
  84.1 8.8 %collective-permute-start.9 = (bf16[64,15,128]{2,1,0:T(8,128)(2,1)S(1)}, bf16[64,15,128]{2,1,0:T(8,128)(2,1)S(1)}, u32[]{:S(2)}, u32[]{:S(2)}) collective-permute-start(bf16[64,15,128]{2,1,0:T(8,128)(2,1)S(1)} %get-tuple-element.60), channel_id=1, source_target_pairs={{0,1},{1,0},{2,3},{3,2},{4,5},{5,4},{6,7},{7,6},{8,9},{9,8},{10,11... | collective-permute-start | bytes 737288 | tf_op jit(solution)/shard_map/ppermute | solution.py:23
  92.9 1.2 collective-permute-done.9
  95.1 1.6 %collective-permute-start.10 = (bf16[2,15,16,128]{3,1,2,0:T(8,128)(2,1)S(1)}, bf16[2,15,16,128]{3,1,2,0:T(8,128)(2,1)S(1)}, u32[]{:S(2)}, u32[]{:S(2)}) collective-permute-start(bf16[2,15,16,128]{3,1,2,0:T(8,128)(2,1)S(1)} %constant_dynamic-slice_fusion.3), channel_id=1, source_target_pairs={{0,2},{2,0},{1,3},{3,1},{4,6},{6,4},{5,7},{7,5},{8,10},{10,8},{9,1... | collective-permute-start | bytes 368648 | tf_op jit(solution)/shard_map/ppermute | solution.py:118
  96.6 3.5 %collective-permute-done.10 = bf16[2,15,16,128]{3,1,2,0:T(8,128)(2,1)S(1)} collective-permute-done((bf16[2,15,16,128]{3,1,2,0:T(8,128)(2,1)S(1)}, bf16[2,15,16,128]{3,1,2,0:T(8,128)(2,1)S(1)}, u32[]{:S(2)}, u32[]{:S(2)}) %collective-permute-start.10) | collective-permute-done | bytes 122912 | tf_op jit(solution)/shard_map/ppermute | solution.py:118
  102.4 5.9 %collective-permute-start.12 = (bf16[2,64,15,128]{3,2,1,0:T(8,128)(2,1)S(1)}, bf16[2,64,15,128]{3,2,1,0:T(8,128)(2,1)S(1)}, u32[]{:S(2)}, u32[]{:S(2)}) collective-permute-start(bf16[2,64,15,128]{3,2,1,0:T(8,128)(2,1)S(1)} %get-tuple-element.34), channel_id=1, source_target_pairs={{0,1},{1,0},{2,3},{3,2},{4,5},{5,4},{6,7},{7,6},{8,9},{9,8},{10,11... | collective-permute-start | bytes 1474568 | tf_op jit(solution)/shard_map/ppermute | solution.py:23
  108.4 1.5 %collective-permute-done.12 = bf16[2,64,15,128]{3,2,1,0:T(8,128)(2,1)S(1)} collective-permute-done((bf16[2,64,15,128]{3,2,1,0:T(8,128)(2,1)S(1)}, bf16[2,64,15,128]{3,2,1,0:T(8,128)(2,1)S(1)}, u32[]{:S(2)}, u32[]{:S(2)}) %collective-permute-start.12) | collective-permute-done | bytes 491552 | tf_op jit(solution)/shard_map/ppermute | solution.py:23
  111.1 1.5 %collective-permute-start.13 = (bf16[2,15,16,128]{3,1,2,0:T(8,128)(2,1)S(1)}, bf16[2,15,16,128]{3,1,2,0:T(8,128)(2,1)S(1)}, u32[]{:S(2)}, u32[]{:S(2)}) collective-permute-start(bf16[2,15,16,128]{3,1,2,0:T(8,128)(2,1)S(1)} %constant_dynamic-slice_fusion), channel_id=1, source_target_pairs={{0,2},{2,0},{1,3},{3,1},{4,6},{6,4},{5,7},{7,5},{8,10},{10,8},{9,1... | collective-permute-start | bytes 368648 | tf_op jit(solution)/shard_map/ppermute | solution.py:118
  112.6 3.5 %collective-permute-done.13 = bf16[2,15,16,128]{3,1,2,0:T(8,128)(2,1)S(1)} collective-permute-done((bf16[2,15,16,128]{3,1,2,0:T(8,128)(2,1)S(1)}, bf16[2,15,16,128]{3,1,2,0:T(8,128)(2,1)S(1)}, u32[]{:S(2)}, u32[]{:S(2)}) %collective-permute-start.13) | collective-permute-done | bytes 122912 | tf_op jit(solution)/shard_map/ppermute | solution.py:118
  118.3 4.4 %collective-permute-start.14 = (f32[32,16,128]{2,1,0:T(8,128)S(1)}, f32[32,16,128]{2,1,0:T(8,128)S(1)}, u32[]{:S(2)}, u32[]{:S(2)}) collective-permute-start(f32[32,16,128]{2,1,0:T(8,128)S(1)} %get-tuple-element.32), channel_id=1, source_target_pairs={{0,1},{1,0},{2,3},{3,2},{4,5},{5,4},{6,7},{7,6},{8,9},{9,8},{10,11... | collective-permute-start | bytes 786440 | tf_op jit(solution)/shard_map/ppermute | solution.py:23
  122.7 1.2 collective-permute-done.14
  (98 shorter events, 22.6 us)
Async XLA Ops:
  0.0 32.9 %copy-start = (bf16[64,32,128]{2,1,0:T(8,128)(2,1)S(1)}, bf16[64,32,128]{2,1,0:T(8,128)(2,1)}, u32[]{:S(2)}) copy-start(bf16[64,32,128]{2,1,0:T(8,128)(2,1)} %param.3) | copy-start | bytes 1572868
  35.0 0.7 copy-start.7
  35.1 2.1 %collective-permute-start = (bf16[2,64,16,128]{3,2,1,0:T(8,128)(2,1)S(1)}, bf16[2,64,16,128]{3,2,1,0:T(8,128)(2,1)S(1)}, u32[]{:S(2)}, u32[]{:S(2)}) collective-permute-start(bf16[2,64,16,128]{3,2,1,0:T(8,128)(2,1)S(1)} %pad_maximum_fusion), channel_id=1, source_target_pairs={{0,1},{1,0},{2,3},{3,2},{4,5},{5,4},{6,7},{7,6},{8,9},{9,8},{10,11... | collective-permute-start | bytes 1572872 | tf_op jit(solution)/shard_map/ppermute | solution.py:23
  36.2 25.3 %copy-start.4 = (bf16[2,64,94]{2,1,0:T(8,128)(2,1)}, bf16[2,64,94]{2,1,0:T(8,128)(2,1)S(1)}, u32[]{:S(2)}) copy-start(bf16[2,64,94]{2,1,0:T(8,128)(2,1)S(1)} %pad_maximum_fusion.2) | copy-start | bytes 72196
  37.2 1.3 %collective-permute-start.1 = (bf16[2,64,16,128]{3,2,1,0:T(8,128)(2,1)S(1)}, bf16[2,64,16,128]{3,2,1,0:T(8,128)(2,1)S(1)}, u32[]{:S(2)}, u32[]{:S(2)}) collective-permute-start(bf16[2,64,16,128]{3,2,1,0:T(8,128)(2,1)S(1)} %maximum_select_fusion.1), channel_id=1, source_target_pairs={{1,4},{4,1},{3,6},{6,3},{5,8},{8,5},{7,10},{10,7},{9,12},{12,9},{1... | collective-permute-start | bytes 1572872 | tf_op jit(solution)/shard_map/ppermute | solution.py:184
  38.9 14.4 %collective-permute-start.2 = (bf16[64,15,128]{2,1,0:T(8,128)(2,1)S(1)}, bf16[64,15,128]{2,1,0:T(8,128)(2,1)S(1)}, u32[]{:S(2)}, u32[]{:S(2)}) collective-permute-start(bf16[64,15,128]{2,1,0:T(8,128)(2,1)S(1)} %get-tuple-element.61), channel_id=1, source_target_pairs={{1,4},{4,1},{3,6},{6,3},{5,8},{8,5},{7,10},{10,7},{9,12},{12,9},{1... | collective-permute-start | bytes 737288 | tf_op jit(solution)/shard_map/ppermute | solution.py:137
  39.6 14.8 %collective-permute-start.3 = (bf16[64,15,128]{2,1,0:T(8,128)(2,1)S(1)}, bf16[64,15,128]{2,1,0:T(8,128)(2,1)}, u32[]{:S(2)}, u32[]{:S(2)}) collective-permute-start(bf16[64,15,128]{2,1,0:T(8,128)(2,1)S(1)} %get-tuple-element.62), channel_id=1, source_target_pairs={{0,1},{1,0},{2,3},{3,2},{4,5},{5,4},{6,7},{7,6},{8,9},{9,8},{10,11... | collective-permute-start | bytes 737288 | tf_op jit(solution)/shard_map/ppermute | solution.py:23
  56.4 5.0 %collective-permute-start.4 = (bf16[2,15,16,128]{3,1,2,0:T(8,128)(2,1)S(1)}, bf16[2,15,16,128]{3,1,2,0:T(8,128)(2,1)S(1)}, u32[]{:S(2)}, u32[]{:S(2)}) collective-permute-start(bf16[2,15,16,128]{3,1,2,0:T(8,128)(2,1)S(1)} %constant_dynamic-slice_fusion.7), channel_id=1, source_target_pairs={{0,2},{2,0},{1,3},{3,1},{4,6},{6,4},{5,7},{7,5},{8,10},{10,8},{9,1... | collective-permute-start | bytes 368648 | tf_op jit(solution)/shard_map/ppermute | solution.py:118
  64.1 8.3 %collective-permute-start.5 = (bf16[2,64,15,128]{3,2,1,0:T(8,128)(2,1)}, bf16[2,64,15,128]{3,2,1,0:T(8,128)(2,1)}, u32[]{:S(2)}, u32[]{:S(2)}) collective-permute-start(bf16[2,64,15,128]{3,2,1,0:T(8,128)(2,1)} %get-tuple-element.37), channel_id=1, source_target_pairs={{1,4},{4,1},{3,6},{6,3},{5,8},{8,5},{7,10},{10,7},{9,12},{12,9},{1... | collective-permute-start | bytes 1474568 | tf_op jit(solution)/shard_map/ppermute | solution.py:137
  65.5 7.4 %collective-permute-start.6 = (bf16[2,64,15,128]{3,2,1,0:T(8,128)(2,1)}, bf16[2,64,15,128]{3,2,1,0:T(8,128)(2,1)}, u32[]{:S(2)}, u32[]{:S(2)}) collective-permute-start(bf16[2,64,15,128]{3,2,1,0:T(8,128)(2,1)} %get-tuple-element.38), channel_id=1, source_target_pairs={{0,1},{1,0},{2,3},{3,2},{4,5},{5,4},{6,7},{7,6},{8,9},{9,8},{10,11... | collective-permute-start | bytes 1474568 | tf_op jit(solution)/shard_map/ppermute | solution.py:23
  72.3 1.9 %copy-start.2 = (bf16[2,64,16,46]{3,2,1,0:T(8,128)(2,1)S(1)}, bf16[2,64,16,46]{3,2,1,0:T(8,128)(2,1)}, u32[]{:S(2)}) copy-start(bf16[2,64,16,46]{3,2,1,0:T(8,128)(2,1)} %rev.13) | copy-start | bytes 565252
  75.3 5.0 %collective-permute-start.7 = (bf16[2,15,16,128]{3,1,2,0:T(8,128)(2,1)S(1)}, bf16[2,15,16,128]{3,1,2,0:T(8,128)(2,1)S(1)}, u32[]{:S(2)}, u32[]{:S(2)}) collective-permute-start(bf16[2,15,16,128]{3,1,2,0:T(8,128)(2,1)S(1)} %constant_dynamic-slice_fusion.4), channel_id=1, source_target_pairs={{0,2},{2,0},{1,3},{3,1},{4,6},{6,4},{5,7},{7,5},{8,10},{10,8},{9,1... | collective-permute-start | bytes 368648 | tf_op jit(solution)/shard_map/ppermute | solution.py:118
  83.2 9.7 %collective-permute-start.8 = (bf16[64,15,128]{2,1,0:T(8,128)(2,1)S(1)}, bf16[64,15,128]{2,1,0:T(8,128)(2,1)S(1)}, u32[]{:S(2)}, u32[]{:S(2)}) collective-permute-start(bf16[64,15,128]{2,1,0:T(8,128)(2,1)S(1)} %get-tuple-element.59), channel_id=1, source_target_pairs={{1,4},{4,1},{3,6},{6,3},{5,8},{8,5},{7,10},{10,7},{9,12},{12,9},{1... | collective-permute-start | bytes 737288 | tf_op jit(solution)/shard_map/ppermute | solution.py:137
  84.1 10.0 %collective-permute-start.9 = (bf16[64,15,128]{2,1,0:T(8,128)(2,1)S(1)}, bf16[64,15,128]{2,1,0:T(8,128)(2,1)S(1)}, u32[]{:S(2)}, u32[]{:S(2)}) collective-permute-start(bf16[64,15,128]{2,1,0:T(8,128)(2,1)S(1)} %get-tuple-element.60), channel_id=1, source_target_pairs={{0,1},{1,0},{2,3},{3,2},{4,5},{5,4},{6,7},{7,6},{8,9},{9,8},{10,11... | collective-permute-start | bytes 737288 | tf_op jit(solution)/shard_map/ppermute | solution.py:23
  94.8 5.3 %copy-start.5 = (bf16[2,64,94]{2,1,0:T(8,128)(2,1)S(1)}, bf16[2,64,94]{2,1,0:T(8,128)(2,1)}, u32[]{:S(2)}) copy-start(bf16[2,64,94]{2,1,0:T(8,128)(2,1)} %copy-done.4) | copy-start | bytes 72196
  95.1 5.0 %collective-permute-start.10 = (bf16[2,15,16,128]{3,1,2,0:T(8,128)(2,1)S(1)}, bf16[2,15,16,128]{3,1,2,0:T(8,128)(2,1)S(1)}, u32[]{:S(2)}, u32[]{:S(2)}) collective-permute-start(bf16[2,15,16,128]{3,1,2,0:T(8,128)(2,1)S(1)} %constant_dynamic-slice_fusion.3), channel_id=1, source_target_pairs={{0,2},{2,0},{1,3},{3,1},{4,6},{6,4},{5,7},{7,5},{8,10},{10,8},{9,1... | collective-permute-start | bytes 368648 | tf_op jit(solution)/shard_map/ppermute | solution.py:118
  101.7 6.6 %collective-permute-start.11 = (bf16[2,64,15,128]{3,2,1,0:T(8,128)(2,1)S(1)}, bf16[2,64,15,128]{3,2,1,0:T(8,128)(2,1)S(1)}, u32[]{:S(2)}, u32[]{:S(2)}) collective-permute-start(bf16[2,64,15,128]{3,2,1,0:T(8,128)(2,1)S(1)} %get-tuple-element.33), channel_id=1, source_target_pairs={{1,4},{4,1},{3,6},{6,3},{5,8},{8,5},{7,10},{10,7},{9,12},{12,9},{1... | collective-permute-start | bytes 1474568 | tf_op jit(solution)/shard_map/ppermute | solution.py:137
  102.4 7.6 %copy-start.3 = (bf16[2,64,16,46]{3,2,1,0:T(8,128)(2,1)S(1)}, bf16[2,64,16,46]{3,2,1,0:T(8,128)(2,1)}, u32[]{:S(2)}) copy-start(bf16[2,64,16,46]{3,2,1,0:T(8,128)(2,1)} %rev.13) | copy-start | bytes 565252
  102.4 7.5 %collective-permute-start.12 = (bf16[2,64,15,128]{3,2,1,0:T(8,128)(2,1)S(1)}, bf16[2,64,15,128]{3,2,1,0:T(8,128)(2,1)S(1)}, u32[]{:S(2)}, u32[]{:S(2)}) collective-permute-start(bf16[2,64,15,128]{3,2,1,0:T(8,128)(2,1)S(1)} %get-tuple-element.34), channel_id=1, source_target_pairs={{0,1},{1,0},{2,3},{3,2},{4,5},{5,4},{6,7},{7,6},{8,9},{9,8},{10,11... | collective-permute-start | bytes 1474568 | tf_op jit(solution)/shard_map/ppermute | solution.py:23
  110.9 5.3 %copy-start.6 = (bf16[2,64,94]{2,1,0:T(8,128)(2,1)S(1)}, bf16[2,64,94]{2,1,0:T(8,128)(2,1)}, u32[]{:S(2)}) copy-start(bf16[2,64,94]{2,1,0:T(8,128)(2,1)} %rev.12) | copy-start | bytes 72196
  111.1 5.0 %collective-permute-start.13 = (bf16[2,15,16,128]{3,1,2,0:T(8,128)(2,1)S(1)}, bf16[2,15,16,128]{3,1,2,0:T(8,128)(2,1)S(1)}, u32[]{:S(2)}, u32[]{:S(2)}) collective-permute-start(bf16[2,15,16,128]{3,1,2,0:T(8,128)(2,1)S(1)} %constant_dynamic-slice_fusion), channel_id=1, source_target_pairs={{0,2},{2,0},{1,3},{3,1},{4,6},{6,4},{5,7},{7,5},{8,10},{10,8},{9,1... | collective-permute-start | bytes 368648 | tf_op jit(solution)/shard_map/ppermute | solution.py:118
  116.6 1.0 copy-start.1
  118.3 5.6 %collective-permute-start.14 = (f32[32,16,128]{2,1,0:T(8,128)S(1)}, f32[32,16,128]{2,1,0:T(8,128)S(1)}, u32[]{:S(2)}, u32[]{:S(2)}) collective-permute-start(f32[32,16,128]{2,1,0:T(8,128)S(1)} %get-tuple-element.32), channel_id=1, source_target_pairs={{0,1},{1,0},{2,3},{3,2},{4,5},{5,4},{6,7},{7,6},{8,9},{9,8},{10,11... | collective-permute-start | bytes 786440 | tf_op jit(solution)/shard_map/ppermute | solution.py:23

commit v11 on v10

--- a/solution.py
+++ b/solution.py
@@ -189,7 +189,7 @@
     kernels = (psf_taps / jnp.sum(psf_taps, axis=2, keepdims=True)).astype(jnp.bfloat16)
     view_count = kernels.shape[0]
     forward_ops = stacked_operators(kernels, planes, half_x, width_y)
-    adjoint_ops = tuple(jnp.flip(m, axis=(-2, -1)) for m in forward_ops)
+    adjoint_ops = stacked_operators(kernels[:, :, ::-1], planes, half_x, width_y)
     for iteration in range(ITERS):
         estimate_low = estimate.astype(jnp.bfloat16)
         low, high = x_rims(estimate_low, reach, 1)

time: 126 us -> 122 us (0.968)
  local copies, waits for them, and re-layouts: 11.5 us -> 8.15 us
  other arithmetic: 8.66 us -> 9.94 us
    rev x3 -> x0, local copies, waits for them, and re-layouts: 2.74 us -> none  [local(): adjoint_ops = tuple((jnp.flip(m, axis=(-2, -1)) for m in forward_ops))]
    reduce_sum x3, other arithmetic: 0.84 us -> 2.88 us  [band_matrix(): matrix = jnp.sum(jnp.where(hit, taps, jnp.float32(0.0)), axis=2)]
    ppermute x4, waiting for transfers between devices: 12.5 us -> 13.9 us  [z_rims(): got = lax.ppermute(payload, 'view', route)]
  transfers between devices with their start and end apart: 15 -> 15, of which waited for: 10 -> 8; matrix products, arithmetic and copies ran while one was open for 3% -> 5% of each run, Pallas kernels for 0% -> 0%
where the time goes in v11:
time: 122 us; the launch traced here: 121 us
  starting transfers between devices  48.8 us (40%)
  between operations  30.5 us (25%)
  waiting for transfers between devices  19.2 us (16%)
  other arithmetic  9.94 us (8%)
  local copies, waits for them, and re-layouts  8.15 us (7%)
  matrix products  4.6 us (4%)
    ppermute x6, starting transfers between devices, from_partner(): return lax.ppermute(block, axis, route)  39 us
    ppermute x4, waiting for transfers between devices, z_rims(): got = lax.ppermute(payload, 'view', route)  13.9 us
    ppermute x4, starting transfers between devices, z_rims(): got = lax.ppermute(payload, 'view', route)  6.2 us
    ppermute x6, waiting for transfers between devices, from_partner(): return lax.ppermute(block, axis, route)  5.25 us
    ppermute x4, starting transfers between devices, x_rims(): across = lax.ppermute(outward, ('tile', 'view'), route)  2.92 us
    reduce_sum x3, other arithmetic, band_matrix(): matrix = jnp.sum(jnp.where(hit, taps, jnp.float32(0.0)), axis=2)  2.88 us
  transfers between devices with their start and end apart: 15, of which 8 were waited for; matrix products, arithmetic and copies ran while one was open for 5% of the time, Pallas kernels for 0%

profile of v11, /device:TPU:0, one launch (start us, length us, event | category | flops | bytes accessed | tf_op | source)
XLA Modules:
  0.0 121.2 jit_solution(7324432930327118751)
XLA Ops:
  0.0 0.9 constant_dynamic-slice_fusion.24
  33.3 1.0 concatenate.42
  35.6 1.1 select_reduce_fusion.5
  37.5 1.0 select_reduce_fusion.1
  41.5 13.2 %collective-permute-start.3 = (bf16[64,15,128]{2,1,0:T(8,128)(2,1)S(1)}, bf16[64,15,128]{2,1,0:T(8,128)(2,1)}, u32[]{:S(2)}, u32[]{:S(2)}) collective-permute-start(bf16[64,15,128]{2,1,0:T(8,128)(2,1)S(1)} %get-tuple-element.74), channel_id=1, source_target_pairs={{0,1},{1,0},{2,3},{3,2},{4,5},{5,4},{6,7},{7,6},{8,9},{9,8},{10,11... | collective-permute-start | bytes 737288 | tf_op jit(solution)/shard_map/ppermute | solution.py:23
  56.2 1.0 broadcast_select_fusion.7
  58.1 1.5 %collective-permute-start.4 = (bf16[2,15,16,128]{3,1,2,0:T(8,128)(2,1)S(1)}, bf16[2,15,16,128]{3,1,2,0:T(8,128)(2,1)S(1)}, u32[]{:S(2)}, u32[]{:S(2)}) collective-permute-start(bf16[2,15,16,128]{3,1,2,0:T(8,128)(2,1)S(1)} %constant_dynamic-slice_fusion.7), channel_id=1, source_target_pairs={{0,2},{2,0},{1,3},{3,1},{4,6},{6,4},{5,7},{7,5},{8,10},{10,8},{9,1... | collective-permute-start | bytes 368648 | tf_op jit(solution)/shard_map/ppermute | solution.py:118
  59.6 3.5 %collective-permute-done.4 = bf16[2,15,16,128]{3,1,2,0:T(8,128)(2,1)S(1)} collective-permute-done((bf16[2,15,16,128]{3,1,2,0:T(8,128)(2,1)S(1)}, bf16[2,15,16,128]{3,1,2,0:T(8,128)(2,1)S(1)}, u32[]{:S(2)}, u32[]{:S(2)}) %collective-permute-start.4) | collective-permute-done | bytes 122912 | tf_op jit(solution)/shard_map/ppermute | solution.py:118
  65.5 6.1 %collective-permute-start.6 = (bf16[2,64,15,128]{3,2,1,0:T(8,128)(2,1)S(1)}, bf16[2,64,15,128]{3,2,1,0:T(8,128)(2,1)S(1)}, u32[]{:S(2)}, u32[]{:S(2)}) collective-permute-start(bf16[2,64,15,128]{3,2,1,0:T(8,128)(2,1)S(1)} %get-tuple-element.50), channel_id=1, source_target_pairs={{0,1},{1,0},{2,3},{3,2},{4,5},{5,4},{6,7},{7,6},{8,9},{9,8},{10,11... | collective-permute-start | bytes 1474568 | tf_op jit(solution)/shard_map/ppermute | solution.py:23
  71.7 1.4 %collective-permute-done.6 = bf16[2,64,15,128]{3,2,1,0:T(8,128)(2,1)S(1)} collective-permute-done((bf16[2,64,15,128]{3,2,1,0:T(8,128)(2,1)S(1)}, bf16[2,64,15,128]{3,2,1,0:T(8,128)(2,1)S(1)}, u32[]{:S(2)}, u32[]{:S(2)}) %collective-permute-start.6) | collective-permute-done | bytes 491552 | tf_op jit(solution)/shard_map/ppermute | solution.py:23
  74.2 1.6 %collective-permute-start.7 = (bf16[2,15,16,128]{3,1,2,0:T(8,128)(2,1)S(1)}, bf16[2,15,16,128]{3,1,2,0:T(8,128)(2,1)S(1)}, u32[]{:S(2)}, u32[]{:S(2)}) collective-permute-start(bf16[2,15,16,128]{3,1,2,0:T(8,128)(2,1)S(1)} %constant_dynamic-slice_fusion.4), channel_id=1, source_target_pairs={{0,2},{2,0},{1,3},{3,1},{4,6},{6,4},{5,7},{7,5},{8,10},{10,8},{9,1... | collective-permute-start | bytes 368648 | tf_op jit(solution)/shard_map/ppermute | solution.py:118
  75.8 3.5 %collective-permute-done.7 = bf16[2,15,16,128]{3,1,2,0:T(8,128)(2,1)S(1)} collective-permute-done((bf16[2,15,16,128]{3,1,2,0:T(8,128)(2,1)S(1)}, bf16[2,15,16,128]{3,1,2,0:T(8,128)(2,1)S(1)}, u32[]{:S(2)}, u32[]{:S(2)}) %collective-permute-start.7) | collective-permute-done | bytes 122912 | tf_op jit(solution)/shard_map/ppermute | solution.py:118
  80.7 0.9 collective-permute-start.8
  81.5 8.8 %collective-permute-start.9 = (bf16[64,15,128]{2,1,0:T(8,128)(2,1)S(1)}, bf16[64,15,128]{2,1,0:T(8,128)(2,1)S(1)}, u32[]{:S(2)}, u32[]{:S(2)}) collective-permute-start(bf16[64,15,128]{2,1,0:T(8,128)(2,1)S(1)} %get-tuple-element.72), channel_id=1, source_target_pairs={{0,1},{1,0},{2,3},{3,2},{4,5},{5,4},{6,7},{7,6},{8,9},{9,8},{10,11... | collective-permute-start | bytes 737288 | tf_op jit(solution)/shard_map/ppermute | solution.py:23
  90.4 1.2 collective-permute-done.9
  92.5 1.6 %collective-permute-start.10 = (bf16[2,15,16,128]{3,1,2,0:T(8,128)(2,1)S(1)}, bf16[2,15,16,128]{3,1,2,0:T(8,128)(2,1)S(1)}, u32[]{:S(2)}, u32[]{:S(2)}) collective-permute-start(bf16[2,15,16,128]{3,1,2,0:T(8,128)(2,1)S(1)} %constant_dynamic-slice_fusion.3), channel_id=1, source_target_pairs={{0,2},{2,0},{1,3},{3,1},{4,6},{6,4},{5,7},{7,5},{8,10},{10,8},{9,1... | collective-permute-start | bytes 368648 | tf_op jit(solution)/shard_map/ppermute | solution.py:118
  94.1 3.5 %collective-permute-done.10 = bf16[2,15,16,128]{3,1,2,0:T(8,128)(2,1)S(1)} collective-permute-done((bf16[2,15,16,128]{3,1,2,0:T(8,128)(2,1)S(1)}, bf16[2,15,16,128]{3,1,2,0:T(8,128)(2,1)S(1)}, u32[]{:S(2)}, u32[]{:S(2)}) %collective-permute-start.10) | collective-permute-done | bytes 122912 | tf_op jit(solution)/shard_map/ppermute | solution.py:118
  99.9 5.9 %collective-permute-start.12 = (bf16[2,64,15,128]{3,2,1,0:T(8,128)(2,1)S(1)}, bf16[2,64,15,128]{3,2,1,0:T(8,128)(2,1)S(1)}, u32[]{:S(2)}, u32[]{:S(2)}) collective-permute-start(bf16[2,64,15,128]{3,2,1,0:T(8,128)(2,1)S(1)} %get-tuple-element.46), channel_id=1, source_target_pairs={{0,1},{1,0},{2,3},{3,2},{4,5},{5,4},{6,7},{7,6},{8,9},{9,8},{10,11... | collective-permute-start | bytes 1474568 | tf_op jit(solution)/shard_map/ppermute | solution.py:23
  105.8 1.5 %collective-permute-done.12 = bf16[2,64,15,128]{3,2,1,0:T(8,128)(2,1)S(1)} collective-permute-done((bf16[2,64,15,128]{3,2,1,0:T(8,128)(2,1)S(1)}, bf16[2,64,15,128]{3,2,1,0:T(8,128)(2,1)S(1)}, u32[]{:S(2)}, u32[]{:S(2)}) %collective-permute-start.12) | collective-permute-done | bytes 491552 | tf_op jit(solution)/shard_map/ppermute | solution.py:23
  108.5 1.5 %collective-permute-start.13 = (bf16[2,15,16,128]{3,1,2,0:T(8,128)(2,1)S(1)}, bf16[2,15,16,128]{3,1,2,0:T(8,128)(2,1)S(1)}, u32[]{:S(2)}, u32[]{:S(2)}) collective-permute-start(bf16[2,15,16,128]{3,1,2,0:T(8,128)(2,1)S(1)} %constant_dynamic-slice_fusion), channel_id=1, source_target_pairs={{0,2},{2,0},{1,3},{3,1},{4,6},{6,4},{5,7},{7,5},{8,10},{10,8},{9,1... | collective-permute-start | bytes 368648 | tf_op jit(solution)/shard_map/ppermute | solution.py:118
  110.0 3.5 %collective-permute-done.13 = bf16[2,15,16,128]{3,1,2,0:T(8,128)(2,1)S(1)} collective-permute-done((bf16[2,15,16,128]{3,1,2,0:T(8,128)(2,1)S(1)}, bf16[2,15,16,128]{3,1,2,0:T(8,128)(2,1)S(1)}, u32[]{:S(2)}, u32[]{:S(2)}) %collective-permute-start.13) | collective-permute-done | bytes 122912 | tf_op jit(solution)/shard_map/ppermute | solution.py:118
  114.7 4.5 %collective-permute-start.14 = (f32[32,16,128]{2,1,0:T(8,128)S(1)}, f32[32,16,128]{2,1,0:T(8,128)S(1)}, u32[]{:S(2)}, u32[]{:S(2)}) collective-permute-start(f32[32,16,128]{2,1,0:T(8,128)S(1)} %get-tuple-element.44), channel_id=1, source_target_pairs={{0,1},{1,0},{2,3},{3,2},{4,5},{5,4},{6,7},{7,6},{8,9},{9,8},{10,11... | collective-permute-start | bytes 786440 | tf_op jit(solution)/shard_map/ppermute | solution.py:23
  119.2 1.2 collective-permute-done.14
  120.3 0.8 maximum_select_fusion.2
  (104 shorter events, 20.2 us)
Async XLA Ops:
  0.0 32.5 %copy-start = (bf16[64,32,128]{2,1,0:T(8,128)(2,1)S(1)}, bf16[64,32,128]{2,1,0:T(8,128)(2,1)}, u32[]{:S(2)}) copy-start(bf16[64,32,128]{2,1,0:T(8,128)(2,1)} %param.3) | copy-start | bytes 1572868
  34.5 0.7 copy-start.5
  34.6 3.9 %collective-permute-start = (bf16[2,64,16,128]{3,2,1,0:T(8,128)(2,1)S(1)}, bf16[2,64,16,128]{3,2,1,0:T(8,128)(2,1)S(1)}, u32[]{:S(2)}, u32[]{:S(2)}) collective-permute-start(bf16[2,64,16,128]{3,2,1,0:T(8,128)(2,1)S(1)} %pad_maximum_fusion), channel_id=1, source_target_pairs={{0,1},{1,0},{2,3},{3,2},{4,5},{5,4},{6,7},{7,6},{8,9},{9,8},{10,11... | collective-permute-start | bytes 1572872 | tf_op jit(solution)/shard_map/ppermute | solution.py:23
  38.6 1.7 %collective-permute-start.1 = (bf16[2,64,16,128]{3,2,1,0:T(8,128)(2,1)S(1)}, bf16[2,64,16,128]{3,2,1,0:T(8,128)(2,1)S(1)}, u32[]{:S(2)}, u32[]{:S(2)}) collective-permute-start(bf16[2,64,16,128]{3,2,1,0:T(8,128)(2,1)S(1)} %maximum_select_fusion.1), channel_id=1, source_target_pairs={{1,4},{4,1},{3,6},{6,3},{5,8},{8,5},{7,10},{10,7},{9,12},{12,9},{1... | collective-permute-start | bytes 1572872 | tf_op jit(solution)/shard_map/ppermute | solution.py:184
  40.8 15.4 %collective-permute-start.2 = (bf16[64,15,128]{2,1,0:T(8,128)(2,1)S(1)}, bf16[64,15,128]{2,1,0:T(8,128)(2,1)S(1)}, u32[]{:S(2)}, u32[]{:S(2)}) collective-permute-start(bf16[64,15,128]{2,1,0:T(8,128)(2,1)S(1)} %get-tuple-element.73), channel_id=1, source_target_pairs={{1,4},{4,1},{3,6},{6,3},{5,8},{8,5},{7,10},{10,7},{9,12},{12,9},{1... | collective-permute-start | bytes 737288 | tf_op jit(solution)/shard_map/ppermute | solution.py:137
  41.5 14.7 %collective-permute-start.3 = (bf16[64,15,128]{2,1,0:T(8,128)(2,1)S(1)}, bf16[64,15,128]{2,1,0:T(8,128)(2,1)}, u32[]{:S(2)}, u32[]{:S(2)}) collective-permute-start(bf16[64,15,128]{2,1,0:T(8,128)(2,1)S(1)} %get-tuple-element.74), channel_id=1, source_target_pairs={{0,1},{1,0},{2,3},{3,2},{4,5},{5,4},{6,7},{7,6},{8,9},{9,8},{10,11... | collective-permute-start | bytes 737288 | tf_op jit(solution)/shard_map/ppermute | solution.py:23
  57.9 5.3 %copy-start.2 = (bf16[2,64,94]{2,1,0:T(8,128)(2,1)S(1)}, bf16[2,64,94]{2,1,0:T(8,128)(2,1)}, u32[]{:S(2)}) copy-start(bf16[2,64,94]{2,1,0:T(8,128)(2,1)} %pad_maximum_fusion.4) | copy-start | bytes 72196
  58.1 5.0 %collective-permute-start.4 = (bf16[2,15,16,128]{3,1,2,0:T(8,128)(2,1)S(1)}, bf16[2,15,16,128]{3,1,2,0:T(8,128)(2,1)S(1)}, u32[]{:S(2)}, u32[]{:S(2)}) collective-permute-start(bf16[2,15,16,128]{3,1,2,0:T(8,128)(2,1)S(1)} %constant_dynamic-slice_fusion.7), channel_id=1, source_target_pairs={{0,2},{2,0},{1,3},{3,1},{4,6},{6,4},{5,7},{7,5},{8,10},{10,8},{9,1... | collective-permute-start | bytes 368648 | tf_op jit(solution)/shard_map/ppermute | solution.py:118
  64.3 7.3 %copy-start.3 = (bf16[46,16]{0,1:T(8,128)(2,1)S(1)}, bf16[46,16]{0,1:T(8,128)(2,1)}, u32[]{:S(2)}) copy-start(bf16[46,16]{0,1:T(8,128)(2,1)} %get-tuple-element.27) | copy-start | bytes 4420
  64.3 7.2 %copy-start.4 = (bf16[46,16]{0,1:T(8,128)(2,1)S(1)}, bf16[46,16]{0,1:T(8,128)(2,1)}, u32[]{:S(2)}) copy-start(bf16[46,16]{0,1:T(8,128)(2,1)} %get-tuple-element.28) | copy-start | bytes 4420
  64.3 7.2 %copy-start.1 = (bf16[94,64]{0,1:T(8,128)(2,1)S(1)}, bf16[94,64]{0,1:T(8,128)(2,1)}, u32[]{:S(2)}) copy-start(bf16[94,64]{0,1:T(8,128)(2,1)} %get-tuple-element.24) | copy-start | bytes 36100
  64.8 6.9 %collective-permute-start.5 = (bf16[2,64,15,128]{3,2,1,0:T(8,128)(2,1)S(1)}, bf16[2,64,15,128]{3,2,1,0:T(8,128)(2,1)S(1)}, u32[]{:S(2)}, u32[]{:S(2)}) collective-permute-start(bf16[2,64,15,128]{3,2,1,0:T(8,128)(2,1)S(1)} %get-tuple-element.49), channel_id=1, source_target_pairs={{1,4},{4,1},{3,6},{6,3},{5,8},{8,5},{7,10},{10,7},{9,12},{12,9},{1... | collective-permute-start | bytes 1474568 | tf_op jit(solution)/shard_map/ppermute | solution.py:137
  65.5 7.6 %collective-permute-start.6 = (bf16[2,64,15,128]{3,2,1,0:T(8,128)(2,1)S(1)}, bf16[2,64,15,128]{3,2,1,0:T(8,128)(2,1)S(1)}, u32[]{:S(2)}, u32[]{:S(2)}) collective-permute-start(bf16[2,64,15,128]{3,2,1,0:T(8,128)(2,1)S(1)} %get-tuple-element.50), channel_id=1, source_target_pairs={{0,1},{1,0},{2,3},{3,2},{4,5},{5,4},{6,7},{7,6},{8,9},{9,8},{10,11... | collective-permute-start | bytes 1474568 | tf_op jit(solution)/shard_map/ppermute | solution.py:23
  74.2 5.0 %collective-permute-start.7 = (bf16[2,15,16,128]{3,1,2,0:T(8,128)(2,1)S(1)}, bf16[2,15,16,128]{3,1,2,0:T(8,128)(2,1)S(1)}, u32[]{:S(2)}, u32[]{:S(2)}) collective-permute-start(bf16[2,15,16,128]{3,1,2,0:T(8,128)(2,1)S(1)} %constant_dynamic-slice_fusion.4), channel_id=1, source_target_pairs={{0,2},{2,0},{1,3},{3,1},{4,6},{6,4},{5,7},{7,5},{8,10},{10,8},{9,1... | collective-permute-start | bytes 368648 | tf_op jit(solution)/shard_map/ppermute | solution.py:118
  80.7 9.7 %collective-permute-start.8 = (bf16[64,15,128]{2,1,0:T(8,128)(2,1)S(1)}, bf16[64,15,128]{2,1,0:T(8,128)(2,1)S(1)}, u32[]{:S(2)}, u32[]{:S(2)}) collective-permute-start(bf16[64,15,128]{2,1,0:T(8,128)(2,1)S(1)} %get-tuple-element.71), channel_id=1, source_target_pairs={{1,4},{4,1},{3,6},{6,3},{5,8},{8,5},{7,10},{10,7},{9,12},{12,9},{1... | collective-permute-start | bytes 737288 | tf_op jit(solution)/shard_map/ppermute | solution.py:137
  81.5 10.0 %collective-permute-start.9 = (bf16[64,15,128]{2,1,0:T(8,128)(2,1)S(1)}, bf16[64,15,128]{2,1,0:T(8,128)(2,1)S(1)}, u32[]{:S(2)}, u32[]{:S(2)}) collective-permute-start(bf16[64,15,128]{2,1,0:T(8,128)(2,1)S(1)} %get-tuple-element.72), channel_id=1, source_target_pairs={{0,1},{1,0},{2,3},{3,2},{4,5},{5,4},{6,7},{7,6},{8,9},{9,8},{10,11... | collective-permute-start | bytes 737288 | tf_op jit(solution)/shard_map/ppermute | solution.py:23
  92.5 5.0 %collective-permute-start.10 = (bf16[2,15,16,128]{3,1,2,0:T(8,128)(2,1)S(1)}, bf16[2,15,16,128]{3,1,2,0:T(8,128)(2,1)S(1)}, u32[]{:S(2)}, u32[]{:S(2)}) collective-permute-start(bf16[2,15,16,128]{3,1,2,0:T(8,128)(2,1)S(1)} %constant_dynamic-slice_fusion.3), channel_id=1, source_target_pairs={{0,2},{2,0},{1,3},{3,1},{4,6},{6,4},{5,7},{7,5},{8,10},{10,8},{9,1... | collective-permute-start | bytes 368648 | tf_op jit(solution)/shard_map/ppermute | solution.py:118
  99.2 6.6 %collective-permute-start.11 = (bf16[2,64,15,128]{3,2,1,0:T(8,128)(2,1)S(1)}, bf16[2,64,15,128]{3,2,1,0:T(8,128)(2,1)S(1)}, u32[]{:S(2)}, u32[]{:S(2)}) collective-permute-start(bf16[2,64,15,128]{3,2,1,0:T(8,128)(2,1)S(1)} %get-tuple-element.45), channel_id=1, source_target_pairs={{1,4},{4,1},{3,6},{6,3},{5,8},{8,5},{7,10},{10,7},{9,12},{12,9},{1... | collective-permute-start | bytes 1474568 | tf_op jit(solution)/shard_map/ppermute | solution.py:137
  99.9 7.5 %collective-permute-start.12 = (bf16[2,64,15,128]{3,2,1,0:T(8,128)(2,1)S(1)}, bf16[2,64,15,128]{3,2,1,0:T(8,128)(2,1)S(1)}, u32[]{:S(2)}, u32[]{:S(2)}) collective-permute-start(bf16[2,64,15,128]{3,2,1,0:T(8,128)(2,1)S(1)} %get-tuple-element.46), channel_id=1, source_target_pairs={{0,1},{1,0},{2,3},{3,2},{4,5},{5,4},{6,7},{7,6},{8,9},{9,8},{10,11... | collective-permute-start | bytes 1474568 | tf_op jit(solution)/shard_map/ppermute | solution.py:23
  108.5 5.0 %collective-permute-start.13 = (bf16[2,15,16,128]{3,1,2,0:T(8,128)(2,1)S(1)}, bf16[2,15,16,128]{3,1,2,0:T(8,128)(2,1)S(1)}, u32[]{:S(2)}, u32[]{:S(2)}) collective-permute-start(bf16[2,15,16,128]{3,1,2,0:T(8,128)(2,1)S(1)} %constant_dynamic-slice_fusion), channel_id=1, source_target_pairs={{0,2},{2,0},{1,3},{3,1},{4,6},{6,4},{5,7},{7,5},{8,10},{10,8},{9,1... | collective-permute-start | bytes 368648 | tf_op jit(solution)/shard_map/ppermute | solution.py:118
  114.7 5.6 %collective-permute-start.14 = (f32[32,16,128]{2,1,0:T(8,128)S(1)}, f32[32,16,128]{2,1,0:T(8,128)S(1)}, u32[]{:S(2)}, u32[]{:S(2)}) collective-permute-start(f32[32,16,128]{2,1,0:T(8,128)S(1)} %get-tuple-element.44), channel_id=1, source_target_pairs={{0,1},{1,0},{2,3},{3,2},{4,5},{5,4},{6,7},{7,6},{8,9},{9,8},{10,11... | collective-permute-start | bytes 786440 | tf_op jit(solution)/shard_map/ppermute | solution.py:23

commit v12 on v9

--- a/solution.py
+++ b/solution.py
@@ -178,6 +178,7 @@
             left_core = (tile + 1) * views + 2 * slab
             route += [(right_core, left_core), (left_core, right_core)]
     outgoing = jnp.where(first, jnp.stack([cross_keep, got[1]]), jnp.stack([got[1], cross_keep]))
+    outgoing, psf_taps = lax.optimization_barrier((outgoing, psf_taps))
     incoming = lax.ppermute(outgoing, ("tile", "view"), route)
     own_parts = jnp.where(first, jnp.stack([own_keep, got[0]]), jnp.stack([got[0], own_keep]))
     views_measured = own_parts + incoming

time: 91.6 us -> 88.6 us (0.967)
  other arithmetic: 10.7 us -> 7.37 us
  waiting for transfers between devices: 19.2 us -> 21.7 us
  starting transfers between devices: 48.8 us -> 47.6 us
    ppermute x6, waiting for transfers between devices: 5.25 us -> 7.75 us  [from_partner(): return lax.ppermute(block, axis, route)]
    ppermute x6, starting transfers between devices: 39 us -> 37.7 us  [from_partner(): return lax.ppermute(block, axis, route)]
    reduce_sum x3, other arithmetic: 2.88 us -> 1.66 us  [band_matrix(): matrix = jnp.sum(jnp.where(hit, taps, jnp.float32(0.0)), axis=2)]
    select_n x4, other arithmetic: 1.2 us -> 0.28 us  [x_rims(): low = jnp.where(first, across, beside)]
  transfers between devices with their start and end apart: 15 -> 15, of which waited for: 8 -> 10; matrix products, arithmetic and copies ran while one was open for 6% -> 3% of each run, Pallas kernels for 0% -> 0%
where the time goes in v12:
time: 88.6 us; the launch traced here: 88.3 us
  starting transfers between devices  47.6 us (54%)
  waiting for transfers between devices  21.7 us (24%)
  other arithmetic  7.37 us (8%)
  local copies, waits for them, and re-layouts  6.53 us (7%)
  matrix products  4.61 us (5%)
    ppermute x6, starting transfers between devices, from_partner(): return lax.ppermute(block, axis, route)  37.7 us
    ppermute x4, waiting for transfers between devices, z_rims(): got = lax.ppermute(payload, 'view', route)  13.9 us
    ppermute x6, waiting for transfers between devices, from_partner(): return lax.ppermute(block, axis, route)  7.75 us
    ppermute x4, starting transfers between devices, z_rims(): got = lax.ppermute(payload, 'view', route)  6.23 us
    ppermute x4, starting transfers between devices, x_rims(): across = lax.ppermute(outward, ('tile', 'view'), route)  2.92 us
  transfers between devices with their start and end apart: 15, of which 10 were waited for; matrix products, arithmetic and copies ran while one was open for 3% of the time, Pallas kernels for 0%

profile of v12, /device:TPU:0, one launch (start us, length us, event | category | flops | bytes accessed | tf_op | source)
XLA Modules:
  0.0 88.3 jit_solution(8782488178689272615)
XLA Ops:
  0.0 0.9 fusion.83
  1.0 1.2 %copy.47 = bf16[64,32,128]{2,0,1:T(8,128)(2,1)S(1)} copy(bf16[64,32,128]{2,1,0:T(8,128)(2,1)} %param.3) | data formatting | bytes 1048576 | tf_op args[0]
  5.1 1.5 %collective-permute-done = bf16[2,64,16,128]{3,2,1,0:T(8,128)(2,1)S(1)} collective-permute-done((bf16[2,64,16,128]{3,2,1,0:T(8,128)(2,1)S(1)}, bf16[2,64,16,128]{3,2,1,0:T(8,128)(2,1)S(1)}, u32[]{:S(2)}, u32[]{:S(2)}) %collective-permute-start) | collective-permute-done | bytes 524320 | tf_op jit(solution)/shard_map/ppermute | solution.py:23
  8.6 1.0 %select_reduce_fusion.1 = (bf16[128,128]{1,0:T(8,128)(2,1)S(1)}, bf16[128,128]{1,0:T(8,128)(2,1)S(1)}, bf16[128,128]{1,0:T(8,128)(2,1)S(1)}, bf16[128,128]{1,0:T(8,128)(2,1)S(1)}) fusion(f32[31]{0:T(128)S(1)} %get-tuple-element.74, s32[128,128]{1,0:T(8,128)S(1)} %subtract_add_fusion, f32[31]{0:T(128)S(1)} %get-tuple-element.75, ...), kind=kLoop, calls=%fused_computation.2 | loop fusion | flops 4505600 | bytes 197104 | tf_op jit(solution)/shard_map/reduce_sum | solution.py:45
  11.0 11.6 %collective-permute-start.3 = (bf16[64,15,128]{2,1,0:T(8,128)(2,1)S(1)}, bf16[64,15,128]{2,1,0:T(8,128)(2,1)S(1)}, u32[]{:S(2)}, u32[]{:S(2)}) collective-permute-start(bf16[64,15,128]{2,1,0:T(8,128)(2,1)S(1)} %get-tuple-element.62), channel_id=1, source_target_pairs={{0,1},{1,0},{2,3},{3,2},{4,5},{5,4},{6,7},{7,6},{8,9},{9,8},{10,11... | collective-permute-start | bytes 737288 | tf_op jit(solution)/shard_map/ppermute | solution.py:23
  22.8 1.0 %collective-permute-done.3 = bf16[64,15,128]{2,1,0:T(8,128)(2,1)S(1)} collective-permute-done((bf16[64,15,128]{2,1,0:T(8,128)(2,1)S(1)}, bf16[64,15,128]{2,1,0:T(8,128)(2,1)S(1)}, u32[]{:S(2)}, u32[]{:S(2)}) %collective-permute-start.3) | collective-permute-done | bytes 245792 | tf_op jit(solution)/shard_map/ppermute | solution.py:23
  24.8 1.6 %collective-permute-start.4 = (bf16[2,15,16,128]{3,1,2,0:T(8,128)(2,1)S(1)}, bf16[2,15,16,128]{3,1,2,0:T(8,128)(2,1)S(1)}, u32[]{:S(2)}, u32[]{:S(2)}) collective-permute-start(bf16[2,15,16,128]{3,1,2,0:T(8,128)(2,1)S(1)} %constant_dynamic-slice_fusion.7), channel_id=1, source_target_pairs={{0,2},{2,0},{1,3},{3,1},{4,6},{6,4},{5,7},{7,5},{8,10},{10,8},{9,1... | collective-permute-start | bytes 368648 | tf_op jit(solution)/shard_map/ppermute | solution.py:118
  26.3 3.5 %collective-permute-done.4 = bf16[2,15,16,128]{3,1,2,0:T(8,128)(2,1)S(1)} collective-permute-done((bf16[2,15,16,128]{3,1,2,0:T(8,128)(2,1)S(1)}, bf16[2,15,16,128]{3,1,2,0:T(8,128)(2,1)S(1)}, u32[]{:S(2)}, u32[]{:S(2)}) %collective-permute-start.4) | collective-permute-done | bytes 122912 | tf_op jit(solution)/shard_map/ppermute | solution.py:118
  32.1 6.4 %collective-permute-start.6 = (bf16[2,64,15,128]{3,2,1,0:T(8,128)(2,1)S(1)}, bf16[2,64,15,128]{3,2,1,0:T(8,128)(2,1)S(1)}, u32[]{:S(2)}, u32[]{:S(2)}) collective-permute-start(bf16[2,64,15,128]{3,2,1,0:T(8,128)(2,1)S(1)} %get-tuple-element.54), channel_id=1, source_target_pairs={{0,1},{1,0},{2,3},{3,2},{4,5},{5,4},{6,7},{7,6},{8,9},{9,8},{10,11... | collective-permute-start | bytes 1474568 | tf_op jit(solution)/shard_map/ppermute | solution.py:23
  38.7 1.4 %collective-permute-done.6 = bf16[2,64,15,128]{3,2,1,0:T(8,128)(2,1)S(1)} collective-permute-done((bf16[2,64,15,128]{3,2,1,0:T(8,128)(2,1)S(1)}, bf16[2,64,15,128]{3,2,1,0:T(8,128)(2,1)S(1)}, u32[]{:S(2)}, u32[]{:S(2)}) %collective-permute-start.6) | collective-permute-done | bytes 491552 | tf_op jit(solution)/shard_map/ppermute | solution.py:23
  41.3 1.6 %collective-permute-start.7 = (bf16[2,15,16,128]{3,1,2,0:T(8,128)(2,1)S(1)}, bf16[2,15,16,128]{3,1,2,0:T(8,128)(2,1)S(1)}, u32[]{:S(2)}, u32[]{:S(2)}) collective-permute-start(bf16[2,15,16,128]{3,1,2,0:T(8,128)(2,1)S(1)} %constant_dynamic-slice_fusion.4), channel_id=1, source_target_pairs={{0,2},{2,0},{1,3},{3,1},{4,6},{6,4},{5,7},{7,5},{8,10},{10,8},{9,1... | collective-permute-start | bytes 368648 | tf_op jit(solution)/shard_map/ppermute | solution.py:118
  42.8 3.5 %collective-permute-done.7 = bf16[2,15,16,128]{3,1,2,0:T(8,128)(2,1)S(1)} collective-permute-done((bf16[2,15,16,128]{3,1,2,0:T(8,128)(2,1)S(1)}, bf16[2,15,16,128]{3,1,2,0:T(8,128)(2,1)S(1)}, u32[]{:S(2)}, u32[]{:S(2)}) %collective-permute-start.7) | collective-permute-done | bytes 122912 | tf_op jit(solution)/shard_map/ppermute | solution.py:118
  47.8 0.9 collective-permute-start.8
  48.6 8.8 %collective-permute-start.9 = (bf16[64,15,128]{2,1,0:T(8,128)(2,1)S(1)}, bf16[64,15,128]{2,1,0:T(8,128)(2,1)S(1)}, u32[]{:S(2)}, u32[]{:S(2)}) collective-permute-start(bf16[64,15,128]{2,1,0:T(8,128)(2,1)S(1)} %get-tuple-element.60), channel_id=1, source_target_pairs={{0,1},{1,0},{2,3},{3,2},{4,5},{5,4},{6,7},{7,6},{8,9},{9,8},{10,11... | collective-permute-start | bytes 737288 | tf_op jit(solution)/shard_map/ppermute | solution.py:23
  57.4 1.2 %collective-permute-done.9 = bf16[64,15,128]{2,1,0:T(8,128)(2,1)S(1)} collective-permute-done((bf16[64,15,128]{2,1,0:T(8,128)(2,1)S(1)}, bf16[64,15,128]{2,1,0:T(8,128)(2,1)S(1)}, u32[]{:S(2)}, u32[]{:S(2)}) %collective-permute-start.9) | collective-permute-done | bytes 245792 | tf_op jit(solution)/shard_map/ppermute | solution.py:23
  59.6 1.6 %collective-permute-start.10 = (bf16[2,15,16,128]{3,1,2,0:T(8,128)(2,1)S(1)}, bf16[2,15,16,128]{3,1,2,0:T(8,128)(2,1)S(1)}, u32[]{:S(2)}, u32[]{:S(2)}) collective-permute-start(bf16[2,15,16,128]{3,1,2,0:T(8,128)(2,1)S(1)} %constant_dynamic-slice_fusion.3), channel_id=1, source_target_pairs={{0,2},{2,0},{1,3},{3,1},{4,6},{6,4},{5,7},{7,5},{8,10},{10,8},{9,1... | collective-permute-start | bytes 368648 | tf_op jit(solution)/shard_map/ppermute | solution.py:118
  61.1 3.5 %collective-permute-done.10 = bf16[2,15,16,128]{3,1,2,0:T(8,128)(2,1)S(1)} collective-permute-done((bf16[2,15,16,128]{3,1,2,0:T(8,128)(2,1)S(1)}, bf16[2,15,16,128]{3,1,2,0:T(8,128)(2,1)S(1)}, u32[]{:S(2)}, u32[]{:S(2)}) %collective-permute-start.10) | collective-permute-done | bytes 122912 | tf_op jit(solution)/shard_map/ppermute | solution.py:118
  66.9 5.9 %collective-permute-start.12 = (bf16[2,64,15,128]{3,2,1,0:T(8,128)(2,1)S(1)}, bf16[2,64,15,128]{3,2,1,0:T(8,128)(2,1)S(1)}, u32[]{:S(2)}, u32[]{:S(2)}) collective-permute-start(bf16[2,64,15,128]{3,2,1,0:T(8,128)(2,1)S(1)} %get-tuple-element.50), channel_id=1, source_target_pairs={{0,1},{1,0},{2,3},{3,2},{4,5},{5,4},{6,7},{7,6},{8,9},{9,8},{10,11... | collective-permute-start | bytes 1474568 | tf_op jit(solution)/shard_map/ppermute | solution.py:23
  72.9 1.5 %collective-permute-done.12 = bf16[2,64,15,128]{3,2,1,0:T(8,128)(2,1)S(1)} collective-permute-done((bf16[2,64,15,128]{3,2,1,0:T(8,128)(2,1)S(1)}, bf16[2,64,15,128]{3,2,1,0:T(8,128)(2,1)S(1)}, u32[]{:S(2)}, u32[]{:S(2)}) %collective-permute-start.12) | collective-permute-done | bytes 491552 | tf_op jit(solution)/shard_map/ppermute | solution.py:23
  75.5 1.6 %collective-permute-start.13 = (bf16[2,15,16,128]{3,1,2,0:T(8,128)(2,1)S(1)}, bf16[2,15,16,128]{3,1,2,0:T(8,128)(2,1)S(1)}, u32[]{:S(2)}, u32[]{:S(2)}) collective-permute-start(bf16[2,15,16,128]{3,1,2,0:T(8,128)(2,1)S(1)} %constant_dynamic-slice_fusion), channel_id=1, source_target_pairs={{0,2},{2,0},{1,3},{3,1},{4,6},{6,4},{5,7},{7,5},{8,10},{10,8},{9,1... | collective-permute-start | bytes 368648 | tf_op jit(solution)/shard_map/ppermute | solution.py:118
  77.1 3.5 %collective-permute-done.13 = bf16[2,15,16,128]{3,1,2,0:T(8,128)(2,1)S(1)} collective-permute-done((bf16[2,15,16,128]{3,1,2,0:T(8,128)(2,1)S(1)}, bf16[2,15,16,128]{3,1,2,0:T(8,128)(2,1)S(1)}, u32[]{:S(2)}, u32[]{:S(2)}) %collective-permute-start.13) | collective-permute-done | bytes 122912 | tf_op jit(solution)/shard_map/ppermute | solution.py:118
  81.8 4.5 %collective-permute-start.14 = (f32[32,16,128]{2,1,0:T(8,128)S(1)}, f32[32,16,128]{2,1,0:T(8,128)S(1)}, u32[]{:S(2)}, u32[]{:S(2)}) collective-permute-start(f32[32,16,128]{2,1,0:T(8,128)S(1)} %get-tuple-element.48), channel_id=1, source_target_pairs={{0,1},{1,0},{2,3},{3,2},{4,5},{5,4},{6,7},{7,6},{8,9},{9,8},{10,11... | collective-permute-start | bytes 786440 | tf_op jit(solution)/shard_map/ppermute | solution.py:23
  86.3 1.2 %collective-permute-done.14 = f32[32,16,128]{2,1,0:T(8,128)S(1)} collective-permute-done((f32[32,16,128]{2,1,0:T(8,128)S(1)}, f32[32,16,128]{2,1,0:T(8,128)S(1)}, u32[]{:S(2)}, u32[]{:S(2)}) %collective-permute-start.14) | collective-permute-done | bytes 262176 | tf_op jit(solution)/shard_map/ppermute | solution.py:23
  87.4 0.8 maximum_select_fusion.2
  (101 shorter events, 17.9 us)
Async XLA Ops:
  4.5 2.1 %collective-permute-start = (bf16[2,64,16,128]{3,2,1,0:T(8,128)(2,1)S(1)}, bf16[2,64,16,128]{3,2,1,0:T(8,128)(2,1)S(1)}, u32[]{:S(2)}, u32[]{:S(2)}) collective-permute-start(bf16[2,64,16,128]{3,2,1,0:T(8,128)(2,1)S(1)} %pad_maximum_fusion), channel_id=1, source_target_pairs={{0,1},{1,0},{2,3},{3,2},{4,5},{5,4},{6,7},{7,6},{8,9},{9,8},{10,11... | collective-permute-start | bytes 1572872 | tf_op jit(solution)/shard_map/ppermute | solution.py:23
  5.1 2.3 %copy-start = (f32[2,3,31]{2,0,1:T(2,128)S(1)}, f32[2,3,31]{2,0,1:T(2,128)}, u32[]{:S(2)}) copy-start(f32[2,3,31]{2,0,1:T(2,128)} %param.4) | copy-start | bytes 2236
  6.7 3.2 %collective-permute-start.1 = (bf16[2,64,16,128]{3,2,1,0:T(8,128)(2,1)S(1)}, bf16[2,64,16,128]{3,2,1,0:T(8,128)(2,1)S(1)}, u32[]{:S(2)}, u32[]{:S(2)}) collective-permute-start(bf16[2,64,16,128]{3,2,1,0:T(8,128)(2,1)S(1)} %maximum_select_fusion.1), channel_id=1, source_target_pairs={{1,4},{4,1},{3,6},{6,3},{5,8},{8,5},{7,10},{10,7},{9,12},{12,9},{1... | collective-permute-start | bytes 1572872 | tf_op jit(solution)/shard_map/ppermute | solution.py:182
  10.4 12.5 %collective-permute-start.2 = (bf16[64,15,128]{2,1,0:T(8,128)(2,1)S(1)}, bf16[64,15,128]{2,1,0:T(8,128)(2,1)S(1)}, u32[]{:S(2)}, u32[]{:S(2)}) collective-permute-start(bf16[64,15,128]{2,1,0:T(8,128)(2,1)S(1)} %get-tuple-element.61), channel_id=1, source_target_pairs={{1,4},{4,1},{3,6},{6,3},{5,8},{8,5},{7,10},{10,7},{9,12},{12,9},{1... | collective-permute-start | bytes 737288 | tf_op jit(solution)/shard_map/ppermute | solution.py:137
  11.0 12.8 %collective-permute-start.3 = (bf16[64,15,128]{2,1,0:T(8,128)(2,1)S(1)}, bf16[64,15,128]{2,1,0:T(8,128)(2,1)S(1)}, u32[]{:S(2)}, u32[]{:S(2)}) collective-permute-start(bf16[64,15,128]{2,1,0:T(8,128)(2,1)S(1)} %get-tuple-element.62), channel_id=1, source_target_pairs={{0,1},{1,0},{2,3},{3,2},{4,5},{5,4},{6,7},{7,6},{8,9},{9,8},{10,11... | collective-permute-start | bytes 737288 | tf_op jit(solution)/shard_map/ppermute | solution.py:23
  24.8 5.0 %collective-permute-start.4 = (bf16[2,15,16,128]{3,1,2,0:T(8,128)(2,1)S(1)}, bf16[2,15,16,128]{3,1,2,0:T(8,128)(2,1)S(1)}, u32[]{:S(2)}, u32[]{:S(2)}) collective-permute-start(bf16[2,15,16,128]{3,1,2,0:T(8,128)(2,1)S(1)} %constant_dynamic-slice_fusion.7), channel_id=1, source_target_pairs={{0,2},{2,0},{1,3},{3,1},{4,6},{6,4},{5,7},{7,5},{8,10},{10,8},{9,1... | collective-permute-start | bytes 368648 | tf_op jit(solution)/shard_map/ppermute | solution.py:118
  31.4 7.2 %collective-permute-start.5 = (bf16[2,64,15,128]{3,2,1,0:T(8,128)(2,1)S(1)}, bf16[2,64,15,128]{3,2,1,0:T(8,128)(2,1)S(1)}, u32[]{:S(2)}, u32[]{:S(2)}) collective-permute-start(bf16[2,64,15,128]{3,2,1,0:T(8,128)(2,1)S(1)} %get-tuple-element.53), channel_id=1, source_target_pairs={{1,4},{4,1},{3,6},{6,3},{5,8},{8,5},{7,10},{10,7},{9,12},{12,9},{1... | collective-permute-start | bytes 1474568 | tf_op jit(solution)/shard_map/ppermute | solution.py:137
  32.1 7.9 %collective-permute-start.6 = (bf16[2,64,15,128]{3,2,1,0:T(8,128)(2,1)S(1)}, bf16[2,64,15,128]{3,2,1,0:T(8,128)(2,1)S(1)}, u32[]{:S(2)}, u32[]{:S(2)}) collective-permute-start(bf16[2,64,15,128]{3,2,1,0:T(8,128)(2,1)S(1)} %get-tuple-element.54), channel_id=1, source_target_pairs={{0,1},{1,0},{2,3},{3,2},{4,5},{5,4},{6,7},{7,6},{8,9},{9,8},{10,11... | collective-permute-start | bytes 1474568 | tf_op jit(solution)/shard_map/ppermute | solution.py:23
  41.3 5.0 %collective-permute-start.7 = (bf16[2,15,16,128]{3,1,2,0:T(8,128)(2,1)S(1)}, bf16[2,15,16,128]{3,1,2,0:T(8,128)(2,1)S(1)}, u32[]{:S(2)}, u32[]{:S(2)}) collective-permute-start(bf16[2,15,16,128]{3,1,2,0:T(8,128)(2,1)S(1)} %constant_dynamic-slice_fusion.4), channel_id=1, source_target_pairs={{0,2},{2,0},{1,3},{3,1},{4,6},{6,4},{5,7},{7,5},{8,10},{10,8},{9,1... | collective-permute-start | bytes 368648 | tf_op jit(solution)/shard_map/ppermute | solution.py:118
  47.8 9.7 %collective-permute-start.8 = (bf16[64,15,128]{2,1,0:T(8,128)(2,1)S(1)}, bf16[64,15,128]{2,1,0:T(8,128)(2,1)S(1)}, u32[]{:S(2)}, u32[]{:S(2)}) collective-permute-start(bf16[64,15,128]{2,1,0:T(8,128)(2,1)S(1)} %get-tuple-element.59), channel_id=1, source_target_pairs={{1,4},{4,1},{3,6},{6,3},{5,8},{8,5},{7,10},{10,7},{9,12},{12,9},{1... | collective-permute-start | bytes 737288 | tf_op jit(solution)/shard_map/ppermute | solution.py:137
  48.6 10.0 %collective-permute-start.9 = (bf16[64,15,128]{2,1,0:T(8,128)(2,1)S(1)}, bf16[64,15,128]{2,1,0:T(8,128)(2,1)S(1)}, u32[]{:S(2)}, u32[]{:S(2)}) collective-permute-start(bf16[64,15,128]{2,1,0:T(8,128)(2,1)S(1)} %get-tuple-element.60), channel_id=1, source_target_pairs={{0,1},{1,0},{2,3},{3,2},{4,5},{5,4},{6,7},{7,6},{8,9},{9,8},{10,11... | collective-permute-start | bytes 737288 | tf_op jit(solution)/shard_map/ppermute | solution.py:23
  59.6 5.0 %collective-permute-start.10 = (bf16[2,15,16,128]{3,1,2,0:T(8,128)(2,1)S(1)}, bf16[2,15,16,128]{3,1,2,0:T(8,128)(2,1)S(1)}, u32[]{:S(2)}, u32[]{:S(2)}) collective-permute-start(bf16[2,15,16,128]{3,1,2,0:T(8,128)(2,1)S(1)} %constant_dynamic-slice_fusion.3), channel_id=1, source_target_pairs={{0,2},{2,0},{1,3},{3,1},{4,6},{6,4},{5,7},{7,5},{8,10},{10,8},{9,1... | collective-permute-start | bytes 368648 | tf_op jit(solution)/shard_map/ppermute | solution.py:118
  66.2 6.6 %collective-permute-start.11 = (bf16[2,64,15,128]{3,2,1,0:T(8,128)(2,1)S(1)}, bf16[2,64,15,128]{3,2,1,0:T(8,128)(2,1)S(1)}, u32[]{:S(2)}, u32[]{:S(2)}) collective-permute-start(bf16[2,64,15,128]{3,2,1,0:T(8,128)(2,1)S(1)} %get-tuple-element.49), channel_id=1, source_target_pairs={{1,4},{4,1},{3,6},{6,3},{5,8},{8,5},{7,10},{10,7},{9,12},{12,9},{1... | collective-permute-start | bytes 1474568 | tf_op jit(solution)/shard_map/ppermute | solution.py:137
  66.9 7.4 %collective-permute-start.12 = (bf16[2,64,15,128]{3,2,1,0:T(8,128)(2,1)S(1)}, bf16[2,64,15,128]{3,2,1,0:T(8,128)(2,1)S(1)}, u32[]{:S(2)}, u32[]{:S(2)}) collective-permute-start(bf16[2,64,15,128]{3,2,1,0:T(8,128)(2,1)S(1)} %get-tuple-element.50), channel_id=1, source_target_pairs={{0,1},{1,0},{2,3},{3,2},{4,5},{5,4},{6,7},{7,6},{8,9},{9,8},{10,11... | collective-permute-start | bytes 1474568 | tf_op jit(solution)/shard_map/ppermute | solution.py:23
  75.5 5.0 %collective-permute-start.13 = (bf16[2,15,16,128]{3,1,2,0:T(8,128)(2,1)S(1)}, bf16[2,15,16,128]{3,1,2,0:T(8,128)(2,1)S(1)}, u32[]{:S(2)}, u32[]{:S(2)}) collective-permute-start(bf16[2,15,16,128]{3,1,2,0:T(8,128)(2,1)S(1)} %constant_dynamic-slice_fusion), channel_id=1, source_target_pairs={{0,2},{2,0},{1,3},{3,1},{4,6},{6,4},{5,7},{7,5},{8,10},{10,8},{9,1... | collective-permute-start | bytes 368648 | tf_op jit(solution)/shard_map/ppermute | solution.py:118
  81.8 5.6 %collective-permute-start.14 = (f32[32,16,128]{2,1,0:T(8,128)S(1)}, f32[32,16,128]{2,1,0:T(8,128)S(1)}, u32[]{:S(2)}, u32[]{:S(2)}) collective-permute-start(f32[32,16,128]{2,1,0:T(8,128)S(1)} %get-tuple-element.48), channel_id=1, source_target_pairs={{0,1},{1,0},{2,3},{3,2},{4,5},{5,4},{6,7},{7,6},{8,9},{9,8},{10,11... | collective-permute-start | bytes 786440 | tf_op jit(solution)/shard_map/ppermute | solution.py:23

commit v13 on v12

--- a/solution.py
+++ b/solution.py
@@ -160,7 +160,10 @@
         target = jnp.clip(target, 0, tile_total - 1)
         starts.append(target * block_count + half * half_blocks)
     slots = jnp.concatenate([lax.dynamic_slice_in_dim(sources, st, half_blocks) for st in starts])
-    picked = jnp.take(blocks, slots % block_count, axis=1)
+    picked = jnp.zeros((planes, slots.shape[0], BX, width_y), acquired.dtype)
+    for block in range(block_count):
+        hit = (slots % block_count == block)[None, :, None, None]
+        picked = jnp.where(hit, blocks[:, block : block + 1], picked)
     mine = (slots // block_count == tile_index)[None, :, None, None]
     partials = jnp.where(mine, picked, jnp.zeros((), picked.dtype))
     partials = partials.reshape(planes, 4, half_x, width_y)

time: 88.6 us -> 97.5 us (1.10)
  other arithmetic: 7.37 us -> 13.7 us
  local copies, waits for them, and re-layouts: 6.53 us -> 8.94 us
    select_n x1, other arithmetic: 0.69 us -> 7.18 us  [local(): partials = jnp.where(mine, picked, jnp.zeros((), picked.dtype))]
    broadcast_in_dim x2 -> x28, local copies, waits for them, and re-layouts: 0.16 us -> 3.37 us  [local(): picked = jnp.where(hit, blocks[:, block:block + 1], picked)]
    slice x0 -> x1, local copies, waits for them, and re-layouts: none -> 1.29 us  [local(): picked = jnp.where(hit, blocks[:, block:block + 1], picked)]
    unnamed x3 -> x2, local copies, waits for them, and re-layouts: 1.26 us -> 0.01 us
where the time goes in v13:
time: 97.5 us; the launch traced here: 97.1 us
  starting transfers between devices  47.6 us (49%)
  waiting for transfers between devices  21.7 us (22%)
  other arithmetic  13.7 us (14%)
  local copies, waits for them, and re-layouts  8.94 us (9%)
  matrix products  4.6 us (5%)
    ppermute x6, starting transfers between devices, from_partner(): return lax.ppermute(block, axis, route)  37.7 us
    ppermute x4, waiting for transfers between devices, z_rims(): got = lax.ppermute(payload, 'view', route)  13.9 us
    ppermute x6, waiting for transfers between devices, from_partner(): return lax.ppermute(block, axis, route)  7.75 us
    select_n x1, other arithmetic, local(): partials = jnp.where(mine, picked, jnp.zeros((), picked.dtype))  7.18 us
    ppermute x4, starting transfers between devices, z_rims(): got = lax.ppermute(payload, 'view', route)  6.23 us
    broadcast_in_dim x28, local copies, waits for them, and re-layouts, local(): picked = jnp.where(hit, blocks[:, block:block + 1], picked)  3.37 us
    ppermute x4, starting transfers between devices, x_rims(): across = lax.ppermute(outward, ('tile', 'view'), route)  2.92 us
  transfers between devices with their start and end apart: 15, of which 10 were waited for; matrix products, arithmetic and copies ran while one was open for 3% of the time, Pallas kernels for 0%

profile of v13, /device:TPU:0, one launch (start us, length us, event | category | flops | bytes accessed | tf_op | source)
XLA Modules:
  0.0 97.1 jit_solution(16011856313777932138)
XLA Ops:
  0.0 0.9 fusion.69
  2.6 1.3 %fusion.86 = (bf16[64,1,4,128]{3,2,1,0:T(4,128)(2,1)S(1)}, bf16[64,1,4,128]{3,2,1,0:T(4,128)(2,1)S(1)}, bf16[64,1,4,128]{3,2,1,0:T(4,128)(2,1)S(1)}, bf16[64,1,4...) fusion(bf16[64,8,4,128]{3,2,1,0:T(4,128)(2,1)} %bitcast.207), kind=kLoop, calls=%fused_computation.217 | loop fusion | bytes 1048576 | tf_op jit(solution)/shard_map/slice | solution.py:166
  6.0 7.2 %fusion.22 = bf16[64,4,16,128]{3,2,0,1:T(8,128)(2,1)S(1)} fusion(bf16[64,4,16,128]{3,0,2,1:T(8,128)(2,1)S(1)} %bitcast.198, bf16[64,4,16,128]{3,0,2,1:T(8,128)(2,1)S(1)} %bitcast.199, bf16[64,4,16,128]{3,0,2,1:T(8,128)(2,1)S(1)} %bitcast.192, bf16[64,4,16,128]{3,0,2,1:T(8,128)(2,1)S(1)} %bitcast.193, bf16[64,4,16,128]{3,0,2,1:T(8,128)(2,1)S(1)} %bitcast.194, ...), kind=kLoop, calls=%fused_computation.32 | loop fusion | flops 4718592 | bytes 9437760 | tf_op jit(solution)/shard_map/jit(_where)/select_n | solution.py:168
  13.9 1.5 %collective-permute-done = bf16[2,64,16,128]{3,2,1,0:T(8,128)(2,1)S(1)} collective-permute-done((bf16[2,64,16,128]{3,2,1,0:T(8,128)(2,1)S(1)}, bf16[2,64,16,128]{3,2,1,0:T(8,128)(2,1)S(1)}, u32[]{:S(2)}, u32[]{:S(2)}) %collective-permute-start) | collective-permute-done | bytes 524320 | tf_op jit(solution)/shard_map/ppermute | solution.py:23
  17.5 1.0 select_reduce_fusion.1
  19.9 11.6 %collective-permute-start.3 = (bf16[64,15,128]{2,1,0:T(8,128)(2,1)S(1)}, bf16[64,15,128]{2,1,0:T(8,128)(2,1)S(1)}, u32[]{:S(2)}, u32[]{:S(2)}) collective-permute-start(bf16[64,15,128]{2,1,0:T(8,128)(2,1)S(1)} %get-tuple-element.72), channel_id=1, source_target_pairs={{0,1},{1,0},{2,3},{3,2},{4,5},{5,4},{6,7},{7,6},{8,9},{9,8},{10,11... | collective-permute-start | bytes 737288 | tf_op jit(solution)/shard_map/ppermute | solution.py:23
  31.7 1.0 %collective-permute-done.3 = bf16[64,15,128]{2,1,0:T(8,128)(2,1)S(1)} collective-permute-done((bf16[64,15,128]{2,1,0:T(8,128)(2,1)S(1)}, bf16[64,15,128]{2,1,0:T(8,128)(2,1)S(1)}, u32[]{:S(2)}, u32[]{:S(2)}) %collective-permute-start.3) | collective-permute-done | bytes 245792 | tf_op jit(solution)/shard_map/ppermute | solution.py:23
  33.6 1.6 %collective-permute-start.4 = (bf16[2,15,16,128]{3,1,2,0:T(8,128)(2,1)S(1)}, bf16[2,15,16,128]{3,1,2,0:T(8,128)(2,1)S(1)}, u32[]{:S(2)}, u32[]{:S(2)}) collective-permute-start(bf16[2,15,16,128]{3,1,2,0:T(8,128)(2,1)S(1)} %constant_dynamic-slice_fusion.7), channel_id=1, source_target_pairs={{0,2},{2,0},{1,3},{3,1},{4,6},{6,4},{5,7},{7,5},{8,10},{10,8},{9,1... | collective-permute-start | bytes 368648 | tf_op jit(solution)/shard_map/ppermute | solution.py:118
  35.2 3.5 %collective-permute-done.4 = bf16[2,15,16,128]{3,1,2,0:T(8,128)(2,1)S(1)} collective-permute-done((bf16[2,15,16,128]{3,1,2,0:T(8,128)(2,1)S(1)}, bf16[2,15,16,128]{3,1,2,0:T(8,128)(2,1)S(1)}, u32[]{:S(2)}, u32[]{:S(2)}) %collective-permute-start.4) | collective-permute-done | bytes 122912 | tf_op jit(solution)/shard_map/ppermute | solution.py:118
  40.3 0.9 collective-permute-start.5
  41.2 6.4 %collective-permute-start.6 = (bf16[2,64,15,128]{3,2,1,0:T(8,128)(2,1)S(1)}, bf16[2,64,15,128]{3,2,1,0:T(8,128)(2,1)S(1)}, u32[]{:S(2)}, u32[]{:S(2)}) collective-permute-start(bf16[2,64,15,128]{3,2,1,0:T(8,128)(2,1)S(1)} %get-tuple-element.56), channel_id=1, source_target_pairs={{0,1},{1,0},{2,3},{3,2},{4,5},{5,4},{6,7},{7,6},{8,9},{9,8},{10,11... | collective-permute-start | bytes 1474568 | tf_op jit(solution)/shard_map/ppermute | solution.py:23
  47.7 1.4 %collective-permute-done.6 = bf16[2,64,15,128]{3,2,1,0:T(8,128)(2,1)S(1)} collective-permute-done((bf16[2,64,15,128]{3,2,1,0:T(8,128)(2,1)S(1)}, bf16[2,64,15,128]{3,2,1,0:T(8,128)(2,1)S(1)}, u32[]{:S(2)}, u32[]{:S(2)}) %collective-permute-start.6) | collective-permute-done | bytes 491552 | tf_op jit(solution)/shard_map/ppermute | solution.py:23
  50.3 1.6 %collective-permute-start.7 = (bf16[2,15,16,128]{3,1,2,0:T(8,128)(2,1)S(1)}, bf16[2,15,16,128]{3,1,2,0:T(8,128)(2,1)S(1)}, u32[]{:S(2)}, u32[]{:S(2)}) collective-permute-start(bf16[2,15,16,128]{3,1,2,0:T(8,128)(2,1)S(1)} %constant_dynamic-slice_fusion.4), channel_id=1, source_target_pairs={{0,2},{2,0},{1,3},{3,1},{4,6},{6,4},{5,7},{7,5},{8,10},{10,8},{9,1... | collective-permute-start | bytes 368648 | tf_op jit(solution)/shard_map/ppermute | solution.py:118
  51.9 3.5 %collective-permute-done.7 = bf16[2,15,16,128]{3,1,2,0:T(8,128)(2,1)S(1)} collective-permute-done((bf16[2,15,16,128]{3,1,2,0:T(8,128)(2,1)S(1)}, bf16[2,15,16,128]{3,1,2,0:T(8,128)(2,1)S(1)}, u32[]{:S(2)}, u32[]{:S(2)}) %collective-permute-start.7) | collective-permute-done | bytes 122912 | tf_op jit(solution)/shard_map/ppermute | solution.py:118
  57.5 8.6 %collective-permute-start.9 = (bf16[64,15,128]{2,1,0:T(8,128)(2,1)S(1)}, bf16[64,15,128]{2,1,0:T(8,128)(2,1)S(1)}, u32[]{:S(2)}, u32[]{:S(2)}) collective-permute-start(bf16[64,15,128]{2,1,0:T(8,128)(2,1)S(1)} %get-tuple-element.70), channel_id=1, source_target_pairs={{0,1},{1,0},{2,3},{3,2},{4,5},{5,4},{6,7},{7,6},{8,9},{9,8},{10,11... | collective-permute-start | bytes 737288 | tf_op jit(solution)/shard_map/ppermute | solution.py:23
  66.1 1.2 %collective-permute-done.9 = bf16[64,15,128]{2,1,0:T(8,128)(2,1)S(1)} collective-permute-done((bf16[64,15,128]{2,1,0:T(8,128)(2,1)S(1)}, bf16[64,15,128]{2,1,0:T(8,128)(2,1)S(1)}, u32[]{:S(2)}, u32[]{:S(2)}) %collective-permute-start.9) | collective-permute-done | bytes 245792 | tf_op jit(solution)/shard_map/ppermute | solution.py:23
  68.2 1.6 %collective-permute-start.10 = (bf16[2,15,16,128]{3,1,2,0:T(8,128)(2,1)S(1)}, bf16[2,15,16,128]{3,1,2,0:T(8,128)(2,1)S(1)}, u32[]{:S(2)}, u32[]{:S(2)}) collective-permute-start(bf16[2,15,16,128]{3,1,2,0:T(8,128)(2,1)S(1)} %constant_dynamic-slice_fusion.3), channel_id=1, source_target_pairs={{0,2},{2,0},{1,3},{3,1},{4,6},{6,4},{5,7},{7,5},{8,10},{10,8},{9,1... | collective-permute-start | bytes 368648 | tf_op jit(solution)/shard_map/ppermute | solution.py:118
  69.8 3.5 %collective-permute-done.10 = bf16[2,15,16,128]{3,1,2,0:T(8,128)(2,1)S(1)} collective-permute-done((bf16[2,15,16,128]{3,1,2,0:T(8,128)(2,1)S(1)}, bf16[2,15,16,128]{3,1,2,0:T(8,128)(2,1)S(1)}, u32[]{:S(2)}, u32[]{:S(2)}) %collective-permute-start.10) | collective-permute-done | bytes 122912 | tf_op jit(solution)/shard_map/ppermute | solution.py:118
  75.6 6.1 %collective-permute-start.12 = (bf16[2,64,15,128]{3,2,1,0:T(8,128)(2,1)S(1)}, bf16[2,64,15,128]{3,2,1,0:T(8,128)(2,1)S(1)}, u32[]{:S(2)}, u32[]{:S(2)}) collective-permute-start(bf16[2,64,15,128]{3,2,1,0:T(8,128)(2,1)S(1)} %get-tuple-element.52), channel_id=1, source_target_pairs={{0,1},{1,0},{2,3},{3,2},{4,5},{5,4},{6,7},{7,6},{8,9},{9,8},{10,11... | collective-permute-start | bytes 1474568 | tf_op jit(solution)/shard_map/ppermute | solution.py:23
  81.7 1.5 %collective-permute-done.12 = bf16[2,64,15,128]{3,2,1,0:T(8,128)(2,1)S(1)} collective-permute-done((bf16[2,64,15,128]{3,2,1,0:T(8,128)(2,1)S(1)}, bf16[2,64,15,128]{3,2,1,0:T(8,128)(2,1)S(1)}, u32[]{:S(2)}, u32[]{:S(2)}) %collective-permute-start.12) | collective-permute-done | bytes 491552 | tf_op jit(solution)/shard_map/ppermute | solution.py:23
  84.4 1.6 %collective-permute-start.13 = (bf16[2,15,16,128]{3,1,2,0:T(8,128)(2,1)S(1)}, bf16[2,15,16,128]{3,1,2,0:T(8,128)(2,1)S(1)}, u32[]{:S(2)}, u32[]{:S(2)}) collective-permute-start(bf16[2,15,16,128]{3,1,2,0:T(8,128)(2,1)S(1)} %constant_dynamic-slice_fusion), channel_id=1, source_target_pairs={{0,2},{2,0},{1,3},{3,1},{4,6},{6,4},{5,7},{7,5},{8,10},{10,8},{9,1... | collective-permute-start | bytes 368648 | tf_op jit(solution)/shard_map/ppermute | solution.py:118
  85.9 3.5 %collective-permute-done.13 = bf16[2,15,16,128]{3,1,2,0:T(8,128)(2,1)S(1)} collective-permute-done((bf16[2,15,16,128]{3,1,2,0:T(8,128)(2,1)S(1)}, bf16[2,15,16,128]{3,1,2,0:T(8,128)(2,1)S(1)}, u32[]{:S(2)}, u32[]{:S(2)}) %collective-permute-start.13) | collective-permute-done | bytes 122912 | tf_op jit(solution)/shard_map/ppermute | solution.py:118
  90.6 4.5 %collective-permute-start.14 = (f32[32,16,128]{2,1,0:T(8,128)S(1)}, f32[32,16,128]{2,1,0:T(8,128)S(1)}, u32[]{:S(2)}, u32[]{:S(2)}) collective-permute-start(f32[32,16,128]{2,1,0:T(8,128)S(1)} %get-tuple-element.50), channel_id=1, source_target_pairs={{0,1},{1,0},{2,3},{3,2},{4,5},{5,4},{6,7},{7,6},{8,9},{9,8},{10,11... | collective-permute-start | bytes 786440 | tf_op jit(solution)/shard_map/ppermute | solution.py:23
  95.1 1.2 %collective-permute-done.14 = f32[32,16,128]{2,1,0:T(8,128)S(1)} collective-permute-done((f32[32,16,128]{2,1,0:T(8,128)S(1)}, f32[32,16,128]{2,1,0:T(8,128)S(1)}, u32[]{:S(2)}, u32[]{:S(2)}) %collective-permute-start.14) | collective-permute-done | bytes 262176 | tf_op jit(solution)/shard_map/ppermute | solution.py:23
  (123 shorter events, 20.2 us)
Async XLA Ops:
  13.4 2.1 %collective-permute-start = (bf16[2,64,16,128]{3,2,1,0:T(8,128)(2,1)S(1)}, bf16[2,64,16,128]{3,2,1,0:T(8,128)(2,1)S(1)}, u32[]{:S(2)}, u32[]{:S(2)}) collective-permute-start(bf16[2,64,16,128]{3,2,1,0:T(8,128)(2,1)S(1)} %pad_maximum_fusion), channel_id=1, source_target_pairs={{0,1},{1,0},{2,3},{3,2},{4,5},{5,4},{6,7},{7,6},{8,9},{9,8},{10,11... | collective-permute-start | bytes 1572872 | tf_op jit(solution)/shard_map/ppermute | solution.py:23
  13.9 2.3 %copy-start = (f32[2,3,31]{2,0,1:T(2,128)S(1)}, f32[2,3,31]{2,0,1:T(2,128)}, u32[]{:S(2)}) copy-start(f32[2,3,31]{2,0,1:T(2,128)} %param.4) | copy-start | bytes 2236
  15.5 3.2 %collective-permute-start.1 = (bf16[2,64,16,128]{3,2,1,0:T(8,128)(2,1)S(1)}, bf16[2,64,16,128]{3,2,1,0:T(8,128)(2,1)S(1)}, u32[]{:S(2)}, u32[]{:S(2)}) collective-permute-start(bf16[2,64,16,128]{3,2,1,0:T(8,128)(2,1)S(1)} %maximum_select_fusion.1), channel_id=1, source_target_pairs={{1,4},{4,1},{3,6},{6,3},{5,8},{8,5},{7,10},{10,7},{9,12},{12,9},{1... | collective-permute-start | bytes 1572872 | tf_op jit(solution)/shard_map/ppermute | solution.py:185
  19.2 12.5 %collective-permute-start.2 = (bf16[64,15,128]{2,1,0:T(8,128)(2,1)S(1)}, bf16[64,15,128]{2,1,0:T(8,128)(2,1)S(1)}, u32[]{:S(2)}, u32[]{:S(2)}) collective-permute-start(bf16[64,15,128]{2,1,0:T(8,128)(2,1)S(1)} %get-tuple-element.71), channel_id=1, source_target_pairs={{1,4},{4,1},{3,6},{6,3},{5,8},{8,5},{7,10},{10,7},{9,12},{12,9},{1... | collective-permute-start | bytes 737288 | tf_op jit(solution)/shard_map/ppermute | solution.py:137
  19.9 12.8 %collective-permute-start.3 = (bf16[64,15,128]{2,1,0:T(8,128)(2,1)S(1)}, bf16[64,15,128]{2,1,0:T(8,128)(2,1)S(1)}, u32[]{:S(2)}, u32[]{:S(2)}) collective-permute-start(bf16[64,15,128]{2,1,0:T(8,128)(2,1)S(1)} %get-tuple-element.72), channel_id=1, source_target_pairs={{0,1},{1,0},{2,3},{3,2},{4,5},{5,4},{6,7},{7,6},{8,9},{9,8},{10,11... | collective-permute-start | bytes 737288 | tf_op jit(solution)/shard_map/ppermute | solution.py:23
  33.6 5.0 %collective-permute-start.4 = (bf16[2,15,16,128]{3,1,2,0:T(8,128)(2,1)S(1)}, bf16[2,15,16,128]{3,1,2,0:T(8,128)(2,1)S(1)}, u32[]{:S(2)}, u32[]{:S(2)}) collective-permute-start(bf16[2,15,16,128]{3,1,2,0:T(8,128)(2,1)S(1)} %constant_dynamic-slice_fusion.7), channel_id=1, source_target_pairs={{0,2},{2,0},{1,3},{3,1},{4,6},{6,4},{5,7},{7,5},{8,10},{10,8},{9,1... | collective-permute-start | bytes 368648 | tf_op jit(solution)/shard_map/ppermute | solution.py:118
  40.3 7.4 %collective-permute-start.5 = (bf16[2,64,15,128]{3,2,1,0:T(8,128)(2,1)S(1)}, bf16[2,64,15,128]{3,2,1,0:T(8,128)(2,1)S(1)}, u32[]{:S(2)}, u32[]{:S(2)}) collective-permute-start(bf16[2,64,15,128]{3,2,1,0:T(8,128)(2,1)S(1)} %get-tuple-element.55), channel_id=1, source_target_pairs={{1,4},{4,1},{3,6},{6,3},{5,8},{8,5},{7,10},{10,7},{9,12},{12,9},{1... | collective-permute-start | bytes 1474568 | tf_op jit(solution)/shard_map/ppermute | solution.py:137
  41.2 7.9 %collective-permute-start.6 = (bf16[2,64,15,128]{3,2,1,0:T(8,128)(2,1)S(1)}, bf16[2,64,15,128]{3,2,1,0:T(8,128)(2,1)S(1)}, u32[]{:S(2)}, u32[]{:S(2)}) collective-permute-start(bf16[2,64,15,128]{3,2,1,0:T(8,128)(2,1)S(1)} %get-tuple-element.56), channel_id=1, source_target_pairs={{0,1},{1,0},{2,3},{3,2},{4,5},{5,4},{6,7},{7,6},{8,9},{9,8},{10,11... | collective-permute-start | bytes 1474568 | tf_op jit(solution)/shard_map/ppermute | solution.py:23
  50.3 5.0 %collective-permute-start.7 = (bf16[2,15,16,128]{3,1,2,0:T(8,128)(2,1)S(1)}, bf16[2,15,16,128]{3,1,2,0:T(8,128)(2,1)S(1)}, u32[]{:S(2)}, u32[]{:S(2)}) collective-permute-start(bf16[2,15,16,128]{3,1,2,0:T(8,128)(2,1)S(1)} %constant_dynamic-slice_fusion.4), channel_id=1, source_target_pairs={{0,2},{2,0},{1,3},{3,1},{4,6},{6,4},{5,7},{7,5},{8,10},{10,8},{9,1... | collective-permute-start | bytes 368648 | tf_op jit(solution)/shard_map/ppermute | solution.py:118
  56.8 9.3 %collective-permute-start.8 = (bf16[64,15,128]{2,1,0:T(8,128)(2,1)S(1)}, bf16[64,15,128]{2,1,0:T(8,128)(2,1)S(1)}, u32[]{:S(2)}, u32[]{:S(2)}) collective-permute-start(bf16[64,15,128]{2,1,0:T(8,128)(2,1)S(1)} %get-tuple-element.69), channel_id=1, source_target_pairs={{1,4},{4,1},{3,6},{6,3},{5,8},{8,5},{7,10},{10,7},{9,12},{12,9},{1... | collective-permute-start | bytes 737288 | tf_op jit(solution)/shard_map/ppermute | solution.py:137
  57.5 9.8 %collective-permute-start.9 = (bf16[64,15,128]{2,1,0:T(8,128)(2,1)S(1)}, bf16[64,15,128]{2,1,0:T(8,128)(2,1)S(1)}, u32[]{:S(2)}, u32[]{:S(2)}) collective-permute-start(bf16[64,15,128]{2,1,0:T(8,128)(2,1)S(1)} %get-tuple-element.70), channel_id=1, source_target_pairs={{0,1},{1,0},{2,3},{3,2},{4,5},{5,4},{6,7},{7,6},{8,9},{9,8},{10,11... | collective-permute-start | bytes 737288 | tf_op jit(solution)/shard_map/ppermute | solution.py:23
  68.2 5.0 %collective-permute-start.10 = (bf16[2,15,16,128]{3,1,2,0:T(8,128)(2,1)S(1)}, bf16[2,15,16,128]{3,1,2,0:T(8,128)(2,1)S(1)}, u32[]{:S(2)}, u32[]{:S(2)}) collective-permute-start(bf16[2,15,16,128]{3,1,2,0:T(8,128)(2,1)S(1)} %constant_dynamic-slice_fusion.3), channel_id=1, source_target_pairs={{0,2},{2,0},{1,3},{3,1},{4,6},{6,4},{5,7},{7,5},{8,10},{10,8},{9,1... | collective-permute-start | bytes 368648 | tf_op jit(solution)/shard_map/ppermute | solution.py:118
  74.9 6.8 %collective-permute-start.11 = (bf16[2,64,15,128]{3,2,1,0:T(8,128)(2,1)S(1)}, bf16[2,64,15,128]{3,2,1,0:T(8,128)(2,1)S(1)}, u32[]{:S(2)}, u32[]{:S(2)}) collective-permute-start(bf16[2,64,15,128]{3,2,1,0:T(8,128)(2,1)S(1)} %get-tuple-element.51), channel_id=1, source_target_pairs={{1,4},{4,1},{3,6},{6,3},{5,8},{8,5},{7,10},{10,7},{9,12},{12,9},{1... | collective-permute-start | bytes 1474568 | tf_op jit(solution)/shard_map/ppermute | solution.py:137
  75.6 7.6 %collective-permute-start.12 = (bf16[2,64,15,128]{3,2,1,0:T(8,128)(2,1)S(1)}, bf16[2,64,15,128]{3,2,1,0:T(8,128)(2,1)S(1)}, u32[]{:S(2)}, u32[]{:S(2)}) collective-permute-start(bf16[2,64,15,128]{3,2,1,0:T(8,128)(2,1)S(1)} %get-tuple-element.52), channel_id=1, source_target_pairs={{0,1},{1,0},{2,3},{3,2},{4,5},{5,4},{6,7},{7,6},{8,9},{9,8},{10,11... | collective-permute-start | bytes 1474568 | tf_op jit(solution)/shard_map/ppermute | solution.py:23
  84.4 5.0 %collective-permute-start.13 = (bf16[2,15,16,128]{3,1,2,0:T(8,128)(2,1)S(1)}, bf16[2,15,16,128]{3,1,2,0:T(8,128)(2,1)S(1)}, u32[]{:S(2)}, u32[]{:S(2)}) collective-permute-start(bf16[2,15,16,128]{3,1,2,0:T(8,128)(2,1)S(1)} %constant_dynamic-slice_fusion), channel_id=1, source_target_pairs={{0,2},{2,0},{1,3},{3,1},{4,6},{6,4},{5,7},{7,5},{8,10},{10,8},{9,1... | collective-permute-start | bytes 368648 | tf_op jit(solution)/shard_map/ppermute | solution.py:118
  90.6 5.6 %collective-permute-start.14 = (f32[32,16,128]{2,1,0:T(8,128)S(1)}, f32[32,16,128]{2,1,0:T(8,128)S(1)}, u32[]{:S(2)}, u32[]{:S(2)}) collective-permute-start(f32[32,16,128]{2,1,0:T(8,128)S(1)} %get-tuple-element.50), channel_id=1, source_target_pairs={{0,1},{1,0},{2,3},{3,2},{4,5},{5,4},{6,7},{7,6},{8,9},{9,8},{10,11... | collective-permute-start | bytes 786440 | tf_op jit(solution)/shard_map/ppermute | solution.py:23

commit v14 on v12

--- a/solution.py
+++ b/solution.py
@@ -121,7 +121,7 @@
     return below, above
 
 
-def x_rims(block, reach, axis):
+def x_rims(block, reach, axis, across=None):
     tiles = lax.axis_size("tile")
     views = lax.axis_size("view")
     route = []
@@ -134,7 +134,8 @@
     width = block.shape[axis]
     outward = lax.dynamic_slice_in_dim(block, jnp.where(first, 0, width - reach), reach, axis)
     inward = lax.dynamic_slice_in_dim(block, jnp.where(first, width - reach, 0), reach, axis)
-    across = lax.ppermute(outward, ("tile", "view"), route)
+    if across is None:
+        across = lax.ppermute(outward, ("tile", "view"), route)
     beside = from_partner(inward, "view", 0)
     low = jnp.where(first, across, beside)
     high = jnp.where(first, beside, across)
@@ -179,9 +180,19 @@
             route += [(right_core, left_core), (left_core, right_core)]
     outgoing = jnp.where(first, jnp.stack([cross_keep, got[1]]), jnp.stack([got[1], cross_keep]))
     outgoing, psf_taps = lax.optimization_barrier((outgoing, psf_taps))
-    incoming = lax.ppermute(outgoing, ("tile", "view"), route)
     own_parts = jnp.where(first, jnp.stack([own_keep, got[0]]), jnp.stack([got[0], own_keep]))
+    arrived = lax.ppermute(jnp.stack([outgoing, own_parts]), ("tile", "view"), route)
+    incoming = arrived[0]
     views_measured = own_parts + incoming
+    neighbour_low = (
+        0.5 * ((arrived[1][0] + outgoing[0]).astype(jnp.float32) + (arrived[1][1] + outgoing[1]).astype(jnp.float32))
+    ).astype(jnp.bfloat16)
+    has_neighbour = jnp.where(first, tile_index > 0, tile_index < tile_total - 1)
+    across_first = jnp.where(
+        has_neighbour,
+        lax.dynamic_slice_in_dim(neighbour_low, jnp.where(first, 1, 0), reach, 1),
+        jnp.zeros((), neighbour_low.dtype),
+    )
     observed = views_measured.astype(jnp.float32)
     estimate = 0.5 * (observed[0] + observed[1])
     kernels = (psf_taps / jnp.sum(psf_taps, axis=2, keepdims=True)).astype(jnp.bfloat16)
@@ -190,7 +201,7 @@
     adjoint_ops = stacked_operators(kernels[:, :, ::-1], planes, half_x, width_y)
     for iteration in range(ITERS):
         estimate_low = estimate.astype(jnp.bfloat16)
-        low, high = x_rims(estimate_low, reach, 1)
+        low, high = x_rims(estimate_low, reach, 1, across_first if iteration == 0 else None)
         extended = jnp.concatenate([low, estimate_low, high], axis=1)
         after_x = jnp.einsum(
             "vzpa,zay->vzpy", forward_ops[0], extended, preferred_element_type=jnp.float32

time: 88.6 us -> 91.3 us (1.030)
  other arithmetic: 7.37 us -> 10.7 us
  starting transfers between devices: 47.6 us -> 45 us
    ppermute x6, starting transfers between devices: 37.7 us -> 35.7 us  [from_partner(): return lax.ppermute(block, axis, route)]
    reduce_sum x3, other arithmetic: 1.66 us -> 2.88 us  [band_matrix(): matrix = jnp.sum(jnp.where(hit, taps, jnp.float32(0.0)), axis=2)]
    another operation x0 -> x1, other arithmetic: none -> 1.06 us  [local(): jnp.stack([outgoing, own_parts])]
    ppermute x4 -> x3, starting transfers between devices: 2.92 us -> 2.25 us  [x_rims(): across = lax.ppermute(outward, ('tile', 'view'), route)]
  transfers between devices with their start and end apart: 15 -> 14, of which waited for: 10 -> 10; matrix products, arithmetic and copies ran while one was open for 3% -> 5% of each run, Pallas kernels for 0% -> 0%
where the time goes in v14:
time: 91.3 us; the launch traced here: 90.6 us
  starting transfers between devices  45 us (49%)
  waiting for transfers between devices  22.3 us (24%)
  other arithmetic  10.7 us (12%)
  local copies, waits for them, and re-layouts  6.56 us (7%)
  matrix products  5.34 us (6%)
    ppermute x6, starting transfers between devices, from_partner(): return lax.ppermute(block, axis, route)  35.7 us
    ppermute x4, waiting for transfers between devices, z_rims(): got = lax.ppermute(payload, 'view', route)  14.5 us
    ppermute x6, waiting for transfers between devices, from_partner(): return lax.ppermute(block, axis, route)  7.8 us
    ppermute x4, starting transfers between devices, z_rims(): got = lax.ppermute(payload, 'view', route)  6.42 us
    reduce_sum x3, other arithmetic, band_matrix(): matrix = jnp.sum(jnp.where(hit, taps, jnp.float32(0.0)), axis=2)  2.88 us
    dot_general x4, matrix products, pass_z_views(): jnp.einsum('vpa,vaxy->vpxy', matrices, widened, preferred_element_type=jn...  2.35 us
    ppermute x3, starting transfers between devices, x_rims(): across = lax.ppermute(outward, ('tile', 'view'), route)  2.25 us
  transfers between devices with their start and end apart: 14, of which 10 were waited for; matrix products, arithmetic and copies ran while one was open for 5% of the time, Pallas kernels for 0%

profile of v14, /device:TPU:0, one launch (start us, length us, event | category | flops | bytes accessed | tf_op | source)
XLA Modules:
  0.0 90.6 jit_solution(4010012191754453020)
XLA Ops:
  1.0 1.2 %copy.47 = bf16[64,32,128]{2,0,1:T(8,128)(2,1)S(1)} copy(bf16[64,32,128]{2,1,0:T(8,128)(2,1)} %param.3) | data formatting | bytes 1048576 | tf_op args[0]
  5.1 1.5 %collective-permute-done = bf16[2,64,16,128]{3,2,1,0:T(8,128)(2,1)S(1)} collective-permute-done((bf16[2,64,16,128]{3,2,1,0:T(8,128)(2,1)S(1)}, bf16[2,64,16,128]{3,2,1,0:T(8,128)(2,1)S(1)}, u32[]{:S(2)}, u32[]{:S(2)}) %collective-permute-start) | collective-permute-done | bytes 524320 | tf_op jit(solution)/shard_map/ppermute | solution.py:23
  6.9 1.1 %pad_maximum_fusion = bf16[2,2,64,16,128]{4,3,2,1,0:T(8,128)(2,1)} fusion(bf16[1,2,64,16,128]{4,3,2,1,0:T(8,128)(2,1)S(1)} %maximum_select_fusion.2, bf16[1,2,64,16,128]{4,3,2,1,0:T(8,128)(2,1)S(1)} %bitcast.211), kind=kLoop, calls=%fused_computation.28 | loop fusion | flops 524288 | bytes 2097152 | tf_op jit(solution)/shard_map/stack | solution.py:184
  9.5 1.1 %select_reduce_fusion.5 = (bf16[94,64]{0,1:T(8,128)(2,1)S(1)}, bf16[94,64]{0,1:T(8,128)(2,1)S(1)}, bf16[94,64]{0,1:T(8,128)(2,1)S(1)}, bf16[94,64]{0,1:T(8,128)(2,1)}) fusion(f32[31]{0:T(128)S(1)} %get-tuple-element.80, s32[94,64]{0,1:T(8,128)S(1)} %iota_subtract_fusion, f32[31]{0:T(128)S(1)} %get-tuple-element.81, f32[31]{0:T(128)S(1)} %bitcast_convert_fusion.6, ...), kind=kLoop, calls=%fused_computation.36 | loop fusion | flops 1654400 | bytes 72688 | tf_op jit(solution)/shard_map/reduce_sum | solution.py:45
  12.0 1.0 %select_reduce_fusion.1 = (bf16[128,128]{1,0:T(8,128)(2,1)S(1)}, bf16[128,128]{1,0:T(8,128)(2,1)S(1)}, bf16[128,128]{1,0:T(8,128)(2,1)S(1)}, bf16[128,128]{1,0:T(8,128)(2,1)S(1)}) fusion(f32[31]{0:T(128)S(1)} %get-tuple-element.78, s32[128,128]{1,0:T(8,128)S(1)} %subtract_add_fusion, f32[31]{0:T(128)S(1)} %get-tuple-element.79, ...), kind=kLoop, calls=%fused_computation.2 | loop fusion | flops 4505600 | bytes 197104 | tf_op jit(solution)/shard_map/reduce_sum | solution.py:45
  13.5 12.5 %collective-permute-start.2 = (bf16[64,15,128]{2,1,0:T(8,128)(2,1)S(1)}, bf16[64,15,128]{2,1,0:T(8,128)(2,1)S(1)}, u32[]{:S(2)}, u32[]{:S(2)}) collective-permute-start(bf16[64,15,128]{2,1,0:T(8,128)(2,1)S(1)} %dynamic-slice_bitcast_fusion.4), channel_id=1, source_target_pairs={{0,1},{1,0},{2,3},{3,2},{4,5},{5,4},{6,7},{7,6},{8,9},{9,8},{10,11... | collective-permute-start | bytes 737288 | tf_op jit(solution)/shard_map/ppermute | solution.py:23
  26.1 1.0 %collective-permute-done.2 = bf16[64,15,128]{2,1,0:T(8,128)(2,1)S(1)} collective-permute-done((bf16[64,15,128]{2,1,0:T(8,128)(2,1)S(1)}, bf16[64,15,128]{2,1,0:T(8,128)(2,1)S(1)}, u32[]{:S(2)}, u32[]{:S(2)}) %collective-permute-start.2) | collective-permute-done | bytes 245792 | tf_op jit(solution)/shard_map/ppermute | solution.py:23
  28.5 1.8 %collective-permute-start.3 = (bf16[2,15,16,128]{3,1,2,0:T(8,128)(2,1)S(1)}, bf16[2,15,16,128]{3,1,2,0:T(8,128)(2,1)S(1)}, u32[]{:S(2)}, u32[]{:S(2)}) collective-permute-start(bf16[2,15,16,128]{3,1,2,0:T(8,128)(2,1)S(1)} %constant_dynamic-slice_fusion.7), channel_id=1, source_target_pairs={{0,2},{2,0},{1,3},{3,1},{4,6},{6,4},{5,7},{7,5},{8,10},{10,8},{9,1... | collective-permute-start | bytes 368648 | tf_op jit(solution)/shard_map/ppermute | solution.py:118
  30.3 4.1 %collective-permute-done.3 = bf16[2,15,16,128]{3,1,2,0:T(8,128)(2,1)S(1)} collective-permute-done((bf16[2,15,16,128]{3,1,2,0:T(8,128)(2,1)S(1)}, bf16[2,15,16,128]{3,1,2,0:T(8,128)(2,1)S(1)}, u32[]{:S(2)}, u32[]{:S(2)}) %collective-permute-start.3) | collective-permute-done | bytes 122912 | tf_op jit(solution)/shard_map/ppermute | solution.py:118
  34.4 1.2 %fusion.27 = f32[2,64,16,128]{3,1,2,0:T(8,128)S(1)} fusion(bf16[2,15,16,128]{3,1,2,0:T(8,128)(2,1)S(1)} %get-tuple-element.74, bf16[2,64,16,128]{3,1,2,0:T(8,128)(2,1)S(1)} %copy.50, bf16[2,15,16,128]{3,1,2,0:T(8,128)(2,1)S(1)} %get-tuple-element.73, bf16[2,64,94]{2,1,0:T(8,128)(2,1)} %pad_maximum_fusion.5), kind=kOutput, calls=%fused_computation.45 | convolution fusion | flops 51593216 | bytes 1842688 | tf_op jit(solution)/shard_map/vpa,vaxy->vpxy/dot_general | solution.py:97
  37.5 3.1 %collective-permute-start.5 = (bf16[2,64,15,128]{3,2,1,0:T(8,128)(2,1)S(1)}, bf16[2,64,15,128]{3,2,1,0:T(8,128)(2,1)S(1)}, u32[]{:S(2)}, u32[]{:S(2)}) collective-permute-start(bf16[2,64,15,128]{3,2,1,0:T(8,128)(2,1)S(1)} %get-tuple-element.59), channel_id=1, source_target_pairs={{0,1},{1,0},{2,3},{3,2},{4,5},{5,4},{6,7},{7,6},{8,9},{9,8},{10,11... | collective-permute-start | bytes 1474568 | tf_op jit(solution)/shard_map/ppermute | solution.py:23
  40.8 1.4 %collective-permute-done.5 = bf16[2,64,15,128]{3,2,1,0:T(8,128)(2,1)S(1)} collective-permute-done((bf16[2,64,15,128]{3,2,1,0:T(8,128)(2,1)S(1)}, bf16[2,64,15,128]{3,2,1,0:T(8,128)(2,1)S(1)}, u32[]{:S(2)}, u32[]{:S(2)}) %collective-permute-start.5) | collective-permute-done | bytes 491552 | tf_op jit(solution)/shard_map/ppermute | solution.py:23
  43.3 1.5 %collective-permute-start.6 = (bf16[2,15,16,128]{3,1,2,0:T(8,128)(2,1)S(1)}, bf16[2,15,16,128]{3,1,2,0:T(8,128)(2,1)S(1)}, u32[]{:S(2)}, u32[]{:S(2)}) collective-permute-start(bf16[2,15,16,128]{3,1,2,0:T(8,128)(2,1)S(1)} %constant_dynamic-slice_fusion.4), channel_id=1, source_target_pairs={{0,2},{2,0},{1,3},{3,1},{4,6},{6,4},{5,7},{7,5},{8,10},{10,8},{9,1... | collective-permute-start | bytes 368648 | tf_op jit(solution)/shard_map/ppermute | solution.py:118
  44.9 3.5 %collective-permute-done.6 = bf16[2,15,16,128]{3,1,2,0:T(8,128)(2,1)S(1)} collective-permute-done((bf16[2,15,16,128]{3,1,2,0:T(8,128)(2,1)S(1)}, bf16[2,15,16,128]{3,1,2,0:T(8,128)(2,1)S(1)}, u32[]{:S(2)}, u32[]{:S(2)}) %collective-permute-start.6) | collective-permute-done | bytes 122912 | tf_op jit(solution)/shard_map/ppermute | solution.py:118
  50.6 8.8 %collective-permute-start.8 = (bf16[64,15,128]{2,1,0:T(8,128)(2,1)S(1)}, bf16[64,15,128]{2,1,0:T(8,128)(2,1)S(1)}, u32[]{:S(2)}, u32[]{:S(2)}) collective-permute-start(bf16[64,15,128]{2,1,0:T(8,128)(2,1)S(1)} %get-tuple-element.66), channel_id=1, source_target_pairs={{0,1},{1,0},{2,3},{3,2},{4,5},{5,4},{6,7},{7,6},{8,9},{9,8},{10,11... | collective-permute-start | bytes 737288 | tf_op jit(solution)/shard_map/ppermute | solution.py:23
  59.5 1.2 %collective-permute-done.8 = bf16[64,15,128]{2,1,0:T(8,128)(2,1)S(1)} collective-permute-done((bf16[64,15,128]{2,1,0:T(8,128)(2,1)S(1)}, bf16[64,15,128]{2,1,0:T(8,128)(2,1)S(1)}, u32[]{:S(2)}, u32[]{:S(2)}) %collective-permute-start.8) | collective-permute-done | bytes 245792 | tf_op jit(solution)/shard_map/ppermute | solution.py:23
  61.6 1.6 %collective-permute-start.9 = (bf16[2,15,16,128]{3,1,2,0:T(8,128)(2,1)S(1)}, bf16[2,15,16,128]{3,1,2,0:T(8,128)(2,1)S(1)}, u32[]{:S(2)}, u32[]{:S(2)}) collective-permute-start(bf16[2,15,16,128]{3,1,2,0:T(8,128)(2,1)S(1)} %constant_dynamic-slice_fusion.3), channel_id=1, source_target_pairs={{0,2},{2,0},{1,3},{3,1},{4,6},{6,4},{5,7},{7,5},{8,10},{10,8},{9,1... | collective-permute-start | bytes 368648 | tf_op jit(solution)/shard_map/ppermute | solution.py:118
  63.2 3.5 %collective-permute-done.9 = bf16[2,15,16,128]{3,1,2,0:T(8,128)(2,1)S(1)} collective-permute-done((bf16[2,15,16,128]{3,1,2,0:T(8,128)(2,1)S(1)}, bf16[2,15,16,128]{3,1,2,0:T(8,128)(2,1)S(1)}, u32[]{:S(2)}, u32[]{:S(2)}) %collective-permute-start.9) | collective-permute-done | bytes 122912 | tf_op jit(solution)/shard_map/ppermute | solution.py:118
  69.0 6.2 %collective-permute-start.11 = (bf16[2,64,15,128]{3,2,1,0:T(8,128)(2,1)S(1)}, bf16[2,64,15,128]{3,2,1,0:T(8,128)(2,1)S(1)}, u32[]{:S(2)}, u32[]{:S(2)}) collective-permute-start(bf16[2,64,15,128]{3,2,1,0:T(8,128)(2,1)S(1)} %get-tuple-element.55), channel_id=1, source_target_pairs={{0,1},{1,0},{2,3},{3,2},{4,5},{5,4},{6,7},{7,6},{8,9},{9,8},{10,11... | collective-permute-start | bytes 1474568 | tf_op jit(solution)/shard_map/ppermute | solution.py:23
  75.2 1.5 %collective-permute-done.11 = bf16[2,64,15,128]{3,2,1,0:T(8,128)(2,1)S(1)} collective-permute-done((bf16[2,64,15,128]{3,2,1,0:T(8,128)(2,1)S(1)}, bf16[2,64,15,128]{3,2,1,0:T(8,128)(2,1)S(1)}, u32[]{:S(2)}, u32[]{:S(2)}) %collective-permute-start.11) | collective-permute-done | bytes 491552 | tf_op jit(solution)/shard_map/ppermute | solution.py:23
  77.9 1.6 %collective-permute-start.12 = (bf16[2,15,16,128]{3,1,2,0:T(8,128)(2,1)S(1)}, bf16[2,15,16,128]{3,1,2,0:T(8,128)(2,1)S(1)}, u32[]{:S(2)}, u32[]{:S(2)}) collective-permute-start(bf16[2,15,16,128]{3,1,2,0:T(8,128)(2,1)S(1)} %constant_dynamic-slice_fusion), channel_id=1, source_target_pairs={{0,2},{2,0},{1,3},{3,1},{4,6},{6,4},{5,7},{7,5},{8,10},{10,8},{9,1... | collective-permute-start | bytes 368648 | tf_op jit(solution)/shard_map/ppermute | solution.py:118
  79.4 3.5 %collective-permute-done.12 = bf16[2,15,16,128]{3,1,2,0:T(8,128)(2,1)S(1)} collective-permute-done((bf16[2,15,16,128]{3,1,2,0:T(8,128)(2,1)S(1)}, bf16[2,15,16,128]{3,1,2,0:T(8,128)(2,1)S(1)}, u32[]{:S(2)}, u32[]{:S(2)}) %collective-permute-start.12) | collective-permute-done | bytes 122912 | tf_op jit(solution)/shard_map/ppermute | solution.py:118
  84.1 4.5 %collective-permute-start.13 = (f32[32,16,128]{2,1,0:T(8,128)S(1)}, f32[32,16,128]{2,1,0:T(8,128)S(1)}, u32[]{:S(2)}, u32[]{:S(2)}) collective-permute-start(f32[32,16,128]{2,1,0:T(8,128)S(1)} %get-tuple-element.53), channel_id=1, source_target_pairs={{0,1},{1,0},{2,3},{3,2},{4,5},{5,4},{6,7},{7,6},{8,9},{9,8},{10,11... | collective-permute-start | bytes 786440 | tf_op jit(solution)/shard_map/ppermute | solution.py:23
  88.6 1.2 %collective-permute-done.13 = f32[32,16,128]{2,1,0:T(8,128)S(1)} collective-permute-done((f32[32,16,128]{2,1,0:T(8,128)S(1)}, f32[32,16,128]{2,1,0:T(8,128)S(1)}, u32[]{:S(2)}, u32[]{:S(2)}) %collective-permute-start.13) | collective-permute-done | bytes 262176 | tf_op jit(solution)/shard_map/ppermute | solution.py:23
  (116 shorter events, 20.5 us)
Async XLA Ops:
  4.5 2.1 %collective-permute-start = (bf16[2,64,16,128]{3,2,1,0:T(8,128)(2,1)S(1)}, bf16[2,64,16,128]{3,2,1,0:T(8,128)(2,1)S(1)}, u32[]{:S(2)}, u32[]{:S(2)}) collective-permute-start(bf16[2,64,16,128]{3,2,1,0:T(8,128)(2,1)S(1)} %pad_maximum_fusion.1), channel_id=1, source_target_pairs={{0,1},{1,0},{2,3},{3,2},{4,5},{5,4},{6,7},{7,6},{8,9},{9,8},{10,11... | collective-permute-start | bytes 1572872 | tf_op jit(solution)/shard_map/ppermute | solution.py:23
  6.9 1.8 %copy-start.6 = (f32[2,3,31]{2,0,1:T(2,128)S(1)}, f32[2,3,31]{2,0,1:T(2,128)}, u32[]{:S(2)}) copy-start(f32[2,3,31]{2,0,1:T(2,128)} %param.4) | copy-start | bytes 2236
  7.9 5.2 %collective-permute-start.1 = (bf16[2,2,64,16,128]{4,3,2,1,0:T(8,128)(2,1)}, bf16[2,2,64,16,128]{4,3,2,1,0:T(8,128)(2,1)S(1)}, u32[]{:S(2)}, u32[]{:S(2)}) collective-permute-start(bf16[2,2,64,16,128]{4,3,2,1,0:T(8,128)(2,1)} %pad_maximum_fusion), channel_id=1, source_target_pairs={{1,4},{4,1},{3,6},{6,3},{5,8},{8,5},{7,10},{10,7},{9,12},{12,9},{1... | collective-permute-start | bytes 3145736 | tf_op jit(solution)/shard_map/ppermute | solution.py:184
  13.1 14.5 %copy-start = (bf16[2,64,16,46]{3,2,0,1:T(8,128)(2,1)}, bf16[2,64,16,46]{3,2,0,1:T(8,128)(2,1)S(1)}, u32[]{:S(2)}) copy-start(bf16[2,64,16,46]{3,2,0,1:T(8,128)(2,1)S(1)} %broadcast_in_dim.246) | copy-start | bytes 565252
  13.5 13.7 %collective-permute-start.2 = (bf16[64,15,128]{2,1,0:T(8,128)(2,1)S(1)}, bf16[64,15,128]{2,1,0:T(8,128)(2,1)S(1)}, u32[]{:S(2)}, u32[]{:S(2)}) collective-permute-start(bf16[64,15,128]{2,1,0:T(8,128)(2,1)S(1)} %dynamic-slice_bitcast_fusion.4), channel_id=1, source_target_pairs={{0,1},{1,0},{2,3},{3,2},{4,5},{5,4},{6,7},{7,6},{8,9},{9,8},{10,11... | collective-permute-start | bytes 737288 | tf_op jit(solution)/shard_map/ppermute | solution.py:23
  28.5 5.8 %collective-permute-start.3 = (bf16[2,15,16,128]{3,1,2,0:T(8,128)(2,1)S(1)}, bf16[2,15,16,128]{3,1,2,0:T(8,128)(2,1)S(1)}, u32[]{:S(2)}, u32[]{:S(2)}) collective-permute-start(bf16[2,15,16,128]{3,1,2,0:T(8,128)(2,1)S(1)} %constant_dynamic-slice_fusion.7), channel_id=1, source_target_pairs={{0,2},{2,0},{1,3},{3,1},{4,6},{6,4},{5,7},{7,5},{8,10},{10,8},{9,1... | collective-permute-start | bytes 368648 | tf_op jit(solution)/shard_map/ppermute | solution.py:118
  36.3 4.3 %copy-start.4 = (bf16[46,16]{0,1:T(8,128)(2,1)S(1)}, bf16[46,16]{0,1:T(8,128)(2,1)}, u32[]{:S(2)}) copy-start(bf16[46,16]{0,1:T(8,128)(2,1)} %get-tuple-element.31) | copy-start | bytes 4420
  36.3 4.3 %copy-start.5 = (bf16[46,16]{0,1:T(8,128)(2,1)S(1)}, bf16[46,16]{0,1:T(8,128)(2,1)}, u32[]{:S(2)}) copy-start(bf16[46,16]{0,1:T(8,128)(2,1)} %get-tuple-element.32) | copy-start | bytes 4420
  36.3 4.3 %copy-start.2 = (bf16[94,64]{0,1:T(8,128)(2,1)S(1)}, bf16[94,64]{0,1:T(8,128)(2,1)}, u32[]{:S(2)}) copy-start(bf16[94,64]{0,1:T(8,128)(2,1)} %get-tuple-element.28) | copy-start | bytes 36100
  36.8 4.0 %collective-permute-start.4 = (bf16[2,64,15,128]{3,2,1,0:T(8,128)(2,1)S(1)}, bf16[2,64,15,128]{3,2,1,0:T(8,128)(2,1)S(1)}, u32[]{:S(2)}, u32[]{:S(2)}) collective-permute-start(bf16[2,64,15,128]{3,2,1,0:T(8,128)(2,1)S(1)} %get-tuple-element.58), channel_id=1, source_target_pairs={{1,4},{4,1},{3,6},{6,3},{5,8},{8,5},{7,10},{10,7},{9,12},{12,9},{1... | collective-permute-start | bytes 1474568 | tf_op jit(solution)/shard_map/ppermute | solution.py:138
  37.5 4.7 %collective-permute-start.5 = (bf16[2,64,15,128]{3,2,1,0:T(8,128)(2,1)S(1)}, bf16[2,64,15,128]{3,2,1,0:T(8,128)(2,1)S(1)}, u32[]{:S(2)}, u32[]{:S(2)}) collective-permute-start(bf16[2,64,15,128]{3,2,1,0:T(8,128)(2,1)S(1)} %get-tuple-element.59), channel_id=1, source_target_pairs={{0,1},{1,0},{2,3},{3,2},{4,5},{5,4},{6,7},{7,6},{8,9},{9,8},{10,11... | collective-permute-start | bytes 1474568 | tf_op jit(solution)/shard_map/ppermute | solution.py:23
  43.3 5.0 %collective-permute-start.6 = (bf16[2,15,16,128]{3,1,2,0:T(8,128)(2,1)S(1)}, bf16[2,15,16,128]{3,1,2,0:T(8,128)(2,1)S(1)}, u32[]{:S(2)}, u32[]{:S(2)}) collective-permute-start(bf16[2,15,16,128]{3,1,2,0:T(8,128)(2,1)S(1)} %constant_dynamic-slice_fusion.4), channel_id=1, source_target_pairs={{0,2},{2,0},{1,3},{3,1},{4,6},{6,4},{5,7},{7,5},{8,10},{10,8},{9,1... | collective-permute-start | bytes 368648 | tf_op jit(solution)/shard_map/ppermute | solution.py:118
  49.5 11.1 %copy-start.1 = (bf16[2,64,16,46]{3,2,0,1:T(8,128)(2,1)S(1)}, bf16[2,64,16,46]{3,2,0,1:T(8,128)(2,1)}, u32[]{:S(2)}) copy-start(bf16[2,64,16,46]{3,2,0,1:T(8,128)(2,1)} %copy-done) | copy-start | bytes 565252
  49.8 9.7 %collective-permute-start.7 = (bf16[64,15,128]{2,1,0:T(8,128)(2,1)S(1)}, bf16[64,15,128]{2,1,0:T(8,128)(2,1)S(1)}, u32[]{:S(2)}, u32[]{:S(2)}) collective-permute-start(bf16[64,15,128]{2,1,0:T(8,128)(2,1)S(1)} %get-tuple-element.65), channel_id=1, source_target_pairs={{1,4},{4,1},{3,6},{6,3},{5,8},{8,5},{7,10},{10,7},{9,12},{12,9},{1... | collective-permute-start | bytes 737288 | tf_op jit(solution)/shard_map/ppermute | solution.py:138
  50.6 10.0 %collective-permute-start.8 = (bf16[64,15,128]{2,1,0:T(8,128)(2,1)S(1)}, bf16[64,15,128]{2,1,0:T(8,128)(2,1)S(1)}, u32[]{:S(2)}, u32[]{:S(2)}) collective-permute-start(bf16[64,15,128]{2,1,0:T(8,128)(2,1)S(1)} %get-tuple-element.66), channel_id=1, source_target_pairs={{0,1},{1,0},{2,3},{3,2},{4,5},{5,4},{6,7},{7,6},{8,9},{9,8},{10,11... | collective-permute-start | bytes 737288 | tf_op jit(solution)/shard_map/ppermute | solution.py:23
  61.4 5.3 %copy-start.3 = (bf16[2,64,94]{2,1,0:T(8,128)(2,1)S(1)}, bf16[2,64,94]{2,1,0:T(8,128)(2,1)}, u32[]{:S(2)}) copy-start(bf16[2,64,94]{2,1,0:T(8,128)(2,1)} %pad_maximum_fusion.5) | copy-start | bytes 72196
  61.6 5.0 %collective-permute-start.9 = (bf16[2,15,16,128]{3,1,2,0:T(8,128)(2,1)S(1)}, bf16[2,15,16,128]{3,1,2,0:T(8,128)(2,1)S(1)}, u32[]{:S(2)}, u32[]{:S(2)}) collective-permute-start(bf16[2,15,16,128]{3,1,2,0:T(8,128)(2,1)S(1)} %constant_dynamic-slice_fusion.3), channel_id=1, source_target_pairs={{0,2},{2,0},{1,3},{3,1},{4,6},{6,4},{5,7},{7,5},{8,10},{10,8},{9,1... | collective-permute-start | bytes 368648 | tf_op jit(solution)/shard_map/ppermute | solution.py:118
  68.3 6.9 %collective-permute-start.10 = (bf16[2,64,15,128]{3,2,1,0:T(8,128)(2,1)S(1)}, bf16[2,64,15,128]{3,2,1,0:T(8,128)(2,1)S(1)}, u32[]{:S(2)}, u32[]{:S(2)}) collective-permute-start(bf16[2,64,15,128]{3,2,1,0:T(8,128)(2,1)S(1)} %get-tuple-element.54), channel_id=1, source_target_pairs={{1,4},{4,1},{3,6},{6,3},{5,8},{8,5},{7,10},{10,7},{9,12},{12,9},{1... | collective-permute-start | bytes 1474568 | tf_op jit(solution)/shard_map/ppermute | solution.py:138
  69.0 7.7 %collective-permute-start.11 = (bf16[2,64,15,128]{3,2,1,0:T(8,128)(2,1)S(1)}, bf16[2,64,15,128]{3,2,1,0:T(8,128)(2,1)S(1)}, u32[]{:S(2)}, u32[]{:S(2)}) collective-permute-start(bf16[2,64,15,128]{3,2,1,0:T(8,128)(2,1)S(1)} %get-tuple-element.55), channel_id=1, source_target_pairs={{0,1},{1,0},{2,3},{3,2},{4,5},{5,4},{6,7},{7,6},{8,9},{9,8},{10,11... | collective-permute-start | bytes 1474568 | tf_op jit(solution)/shard_map/ppermute | solution.py:23
  77.9 5.0 %collective-permute-start.12 = (bf16[2,15,16,128]{3,1,2,0:T(8,128)(2,1)S(1)}, bf16[2,15,16,128]{3,1,2,0:T(8,128)(2,1)S(1)}, u32[]{:S(2)}, u32[]{:S(2)}) collective-permute-start(bf16[2,15,16,128]{3,1,2,0:T(8,128)(2,1)S(1)} %constant_dynamic-slice_fusion), channel_id=1, source_target_pairs={{0,2},{2,0},{1,3},{3,1},{4,6},{6,4},{5,7},{7,5},{8,10},{10,8},{9,1... | collective-permute-start | bytes 368648 | tf_op jit(solution)/shard_map/ppermute | solution.py:118
  84.1 5.6 %collective-permute-start.13 = (f32[32,16,128]{2,1,0:T(8,128)S(1)}, f32[32,16,128]{2,1,0:T(8,128)S(1)}, u32[]{:S(2)}, u32[]{:S(2)}) collective-permute-start(f32[32,16,128]{2,1,0:T(8,128)S(1)} %get-tuple-element.53), channel_id=1, source_target_pairs={{0,1},{1,0},{2,3},{3,2},{4,5},{5,4},{6,7},{7,6},{8,9},{9,8},{10,11... | collective-permute-start | bytes 786440 | tf_op jit(solution)/shard_map/ppermute | solution.py:23

commit v15 on v12

--- a/solution.py
+++ b/solution.py
@@ -132,8 +132,10 @@
             route += [(right_core, left_core), (left_core, right_core)]
     first = lax.axis_index("view") % 2 == 0
     width = block.shape[axis]
-    outward = lax.dynamic_slice_in_dim(block, jnp.where(first, 0, width - reach), reach, axis)
-    inward = lax.dynamic_slice_in_dim(block, jnp.where(first, width - reach, 0), reach, axis)
+    front = lax.slice_in_dim(block, 0, reach, axis=axis)
+    back = lax.slice_in_dim(block, width - reach, width, axis=axis)
+    outward = jnp.where(first, front, back)
+    inward = jnp.where(first, back, front)
     across = lax.ppermute(outward, ("tile", "view"), route)
     beside = from_partner(inward, "view", 0)
     low = jnp.where(first, across, beside)
@@ -207,9 +209,9 @@
     keep = lax.dynamic_slice_in_dim(estimate, view_bit * half_rows, half_rows, 0)
     give = lax.dynamic_slice_in_dim(estimate, (1 - view_bit) * half_rows, half_rows, 0)
     got = from_partner(give, "view", 0)
-    return jnp.where(
-        view_bit == 0, jnp.concatenate([keep, got], axis=1), jnp.concatenate([got, keep], axis=1)
-    )
+    first_half = jnp.where(view_bit == 0, keep, got)
+    second_half = jnp.where(view_bit == 0, got, keep)
+    return jnp.concatenate([first_half, second_half], axis=1)
 
 
 def solution(mesh):

time: 88.6 us -> 87.9 us (level)
  local copies, waits for them, and re-layouts: 6.53 us -> 5.19 us
    dynamic_slice x5 -> x1, local copies, waits for them, and re-layouts: 1.35 us -> 0.03 us  [local(): lax.dynamic_slice_in_dim(estimate, (1 - view_bit) * half_rows, half_rows, 0)]
where the time goes in v15:
time: 87.9 us; the launch traced here: 87.5 us
  starting transfers between devices  47.6 us (54%)
  waiting for transfers between devices  21.7 us (25%)
  other arithmetic  7.9 us (9%)
  local copies, waits for them, and re-layouts  5.19 us (6%)
  matrix products  4.61 us (5%)
    ppermute x6, starting transfers between devices, from_partner(): return lax.ppermute(block, axis, route)  37.7 us
    ppermute x4, waiting for transfers between devices, z_rims(): got = lax.ppermute(payload, 'view', route)  13.9 us
    ppermute x6, waiting for transfers between devices, from_partner(): return lax.ppermute(block, axis, route)  7.8 us
    ppermute x4, starting transfers between devices, z_rims(): got = lax.ppermute(payload, 'view', route)  6.23 us
    ppermute x4, starting transfers between devices, x_rims(): across = lax.ppermute(outward, ('tile', 'view'), route)  2.92 us
  transfers between devices with their start and end apart: 15, of which 10 were waited for; matrix products, arithmetic and copies ran while one was open for 3% of the time, Pallas kernels for 0%

profile of v15, /device:TPU:0, one launch (start us, length us, event | category | flops | bytes accessed | tf_op | source)
XLA Modules:
  0.0 87.5 jit_solution(2615332660588220068)
XLA Ops:
  0.0 0.9 fusion.82
  1.0 1.2 %copy.47 = bf16[64,32,128]{2,0,1:T(8,128)(2,1)S(1)} copy(bf16[64,32,128]{2,1,0:T(8,128)(2,1)} %param.3) | data formatting | bytes 1048576 | tf_op args[0]
  5.1 1.5 %collective-permute-done = bf16[2,64,16,128]{3,2,1,0:T(8,128)(2,1)S(1)} collective-permute-done((bf16[2,64,16,128]{3,2,1,0:T(8,128)(2,1)S(1)}, bf16[2,64,16,128]{3,2,1,0:T(8,128)(2,1)S(1)}, u32[]{:S(2)}, u32[]{:S(2)}) %collective-permute-start) | collective-permute-done | bytes 524320 | tf_op jit(solution)/shard_map/ppermute | solution.py:23
  8.9 1.0 %select_reduce_fusion.1 = (bf16[128,128]{1,0:T(8,128)(2,1)S(1)}, bf16[128,128]{1,0:T(8,128)(2,1)S(1)}, bf16[128,128]{1,0:T(8,128)(2,1)S(1)}, bf16[128,128]{1,0:T(8,128)(2,1)S(1)}) fusion(f32[31]{0:T(128)S(1)} %get-tuple-element.74, s32[128,128]{1,0:T(8,128)S(1)} %subtract_add_fusion, f32[31]{0:T(128)S(1)} %get-tuple-element.75, ...), kind=kLoop, calls=%fused_computation.2 | loop fusion | flops 4505600 | bytes 197104 | tf_op jit(solution)/shard_map/reduce_sum | solution.py:45
  10.9 11.6 %collective-permute-start.3 = (bf16[64,15,128]{2,1,0:T(8,128)(2,1)S(1)}, bf16[64,15,128]{2,1,0:T(8,128)(2,1)S(1)}, u32[]{:S(2)}, u32[]{:S(2)}) collective-permute-start(bf16[64,15,128]{2,1,0:T(8,128)(2,1)S(1)} %get-tuple-element.62), channel_id=1, source_target_pairs={{0,1},{1,0},{2,3},{3,2},{4,5},{5,4},{6,7},{7,6},{8,9},{9,8},{10,11... | collective-permute-start | bytes 737288 | tf_op jit(solution)/shard_map/ppermute | solution.py:23
  22.6 1.0 %collective-permute-done.3 = bf16[64,15,128]{2,1,0:T(8,128)(2,1)S(1)} collective-permute-done((bf16[64,15,128]{2,1,0:T(8,128)(2,1)S(1)}, bf16[64,15,128]{2,1,0:T(8,128)(2,1)S(1)}, u32[]{:S(2)}, u32[]{:S(2)}) %collective-permute-start.3) | collective-permute-done | bytes 245792 | tf_op jit(solution)/shard_map/ppermute | solution.py:23
  24.7 1.6 %collective-permute-start.4 = (bf16[2,15,16,128]{3,1,2,0:T(8,128)(2,1)S(1)}, bf16[2,15,16,128]{3,1,2,0:T(8,128)(2,1)S(1)}, u32[]{:S(2)}, u32[]{:S(2)}) collective-permute-start(bf16[2,15,16,128]{3,1,2,0:T(8,128)(2,1)S(1)} %constant_dynamic-slice_fusion.3), channel_id=1, source_target_pairs={{0,2},{2,0},{1,3},{3,1},{4,6},{6,4},{5,7},{7,5},{8,10},{10,8},{9,1... | collective-permute-start | bytes 368648 | tf_op jit(solution)/shard_map/ppermute | solution.py:118
  26.2 3.5 %collective-permute-done.4 = bf16[2,15,16,128]{3,1,2,0:T(8,128)(2,1)S(1)} collective-permute-done((bf16[2,15,16,128]{3,1,2,0:T(8,128)(2,1)S(1)}, bf16[2,15,16,128]{3,1,2,0:T(8,128)(2,1)S(1)}, u32[]{:S(2)}, u32[]{:S(2)}) %collective-permute-start.4) | collective-permute-done | bytes 122912 | tf_op jit(solution)/shard_map/ppermute | solution.py:118
  31.7 6.4 %collective-permute-start.6 = (bf16[2,64,15,128]{3,2,1,0:T(8,128)(2,1)S(1)}, bf16[2,64,15,128]{3,2,1,0:T(8,128)(2,1)S(1)}, u32[]{:S(2)}, u32[]{:S(2)}) collective-permute-start(bf16[2,64,15,128]{3,2,1,0:T(8,128)(2,1)S(1)} %get-tuple-element.54), channel_id=1, source_target_pairs={{0,1},{1,0},{2,3},{3,2},{4,5},{5,4},{6,7},{7,6},{8,9},{9,8},{10,11... | collective-permute-start | bytes 1474568 | tf_op jit(solution)/shard_map/ppermute | solution.py:23
  38.2 1.4 %collective-permute-done.6 = bf16[2,64,15,128]{3,2,1,0:T(8,128)(2,1)S(1)} collective-permute-done((bf16[2,64,15,128]{3,2,1,0:T(8,128)(2,1)S(1)}, bf16[2,64,15,128]{3,2,1,0:T(8,128)(2,1)S(1)}, u32[]{:S(2)}, u32[]{:S(2)}) %collective-permute-start.6) | collective-permute-done | bytes 491552 | tf_op jit(solution)/shard_map/ppermute | solution.py:23
  40.9 1.6 %collective-permute-start.7 = (bf16[2,15,16,128]{3,1,2,0:T(8,128)(2,1)S(1)}, bf16[2,15,16,128]{3,1,2,0:T(8,128)(2,1)S(1)}, u32[]{:S(2)}, u32[]{:S(2)}) collective-permute-start(bf16[2,15,16,128]{3,1,2,0:T(8,128)(2,1)S(1)} %constant_dynamic-slice_fusion.2), channel_id=1, source_target_pairs={{0,2},{2,0},{1,3},{3,1},{4,6},{6,4},{5,7},{7,5},{8,10},{10,8},{9,1... | collective-permute-start | bytes 368648 | tf_op jit(solution)/shard_map/ppermute | solution.py:118
  42.4 3.5 %collective-permute-done.7 = bf16[2,15,16,128]{3,1,2,0:T(8,128)(2,1)S(1)} collective-permute-done((bf16[2,15,16,128]{3,1,2,0:T(8,128)(2,1)S(1)}, bf16[2,15,16,128]{3,1,2,0:T(8,128)(2,1)S(1)}, u32[]{:S(2)}, u32[]{:S(2)}) %collective-permute-start.7) | collective-permute-done | bytes 122912 | tf_op jit(solution)/shard_map/ppermute | solution.py:118
  47.9 8.8 %collective-permute-start.9 = (bf16[64,15,128]{2,1,0:T(8,128)(2,1)S(1)}, bf16[64,15,128]{2,1,0:T(8,128)(2,1)S(1)}, u32[]{:S(2)}, u32[]{:S(2)}) collective-permute-start(bf16[64,15,128]{2,1,0:T(8,128)(2,1)S(1)} %get-tuple-element.60), channel_id=1, source_target_pairs={{0,1},{1,0},{2,3},{3,2},{4,5},{5,4},{6,7},{7,6},{8,9},{9,8},{10,11... | collective-permute-start | bytes 737288 | tf_op jit(solution)/shard_map/ppermute | solution.py:23
  56.7 1.2 %collective-permute-done.9 = bf16[64,15,128]{2,1,0:T(8,128)(2,1)S(1)} collective-permute-done((bf16[64,15,128]{2,1,0:T(8,128)(2,1)S(1)}, bf16[64,15,128]{2,1,0:T(8,128)(2,1)S(1)}, u32[]{:S(2)}, u32[]{:S(2)}) %collective-permute-start.9) | collective-permute-done | bytes 245792 | tf_op jit(solution)/shard_map/ppermute | solution.py:23
  58.9 1.6 %collective-permute-start.10 = (bf16[2,15,16,128]{3,1,2,0:T(8,128)(2,1)S(1)}, bf16[2,15,16,128]{3,1,2,0:T(8,128)(2,1)S(1)}, u32[]{:S(2)}, u32[]{:S(2)}) collective-permute-start(bf16[2,15,16,128]{3,1,2,0:T(8,128)(2,1)S(1)} %constant_dynamic-slice_fusion.1), channel_id=1, source_target_pairs={{0,2},{2,0},{1,3},{3,1},{4,6},{6,4},{5,7},{7,5},{8,10},{10,8},{9,1... | collective-permute-start | bytes 368648 | tf_op jit(solution)/shard_map/ppermute | solution.py:118
  60.4 3.5 %collective-permute-done.10 = bf16[2,15,16,128]{3,1,2,0:T(8,128)(2,1)S(1)} collective-permute-done((bf16[2,15,16,128]{3,1,2,0:T(8,128)(2,1)S(1)}, bf16[2,15,16,128]{3,1,2,0:T(8,128)(2,1)S(1)}, u32[]{:S(2)}, u32[]{:S(2)}) %collective-permute-start.10) | collective-permute-done | bytes 122912 | tf_op jit(solution)/shard_map/ppermute | solution.py:118
  65.2 0.9 collective-permute-start.11
  66.1 6.1 %collective-permute-start.12 = (bf16[2,64,15,128]{3,2,1,0:T(8,128)(2,1)S(1)}, bf16[2,64,15,128]{3,2,1,0:T(8,128)(2,1)S(1)}, u32[]{:S(2)}, u32[]{:S(2)}) collective-permute-start(bf16[2,64,15,128]{3,2,1,0:T(8,128)(2,1)S(1)} %get-tuple-element.50), channel_id=1, source_target_pairs={{0,1},{1,0},{2,3},{3,2},{4,5},{5,4},{6,7},{7,6},{8,9},{9,8},{10,11... | collective-permute-start | bytes 1474568 | tf_op jit(solution)/shard_map/ppermute | solution.py:23
  72.2 1.5 %collective-permute-done.12 = bf16[2,64,15,128]{3,2,1,0:T(8,128)(2,1)S(1)} collective-permute-done((bf16[2,64,15,128]{3,2,1,0:T(8,128)(2,1)S(1)}, bf16[2,64,15,128]{3,2,1,0:T(8,128)(2,1)S(1)}, u32[]{:S(2)}, u32[]{:S(2)}) %collective-permute-start.12) | collective-permute-done | bytes 491552 | tf_op jit(solution)/shard_map/ppermute | solution.py:23
  74.9 1.6 %collective-permute-start.13 = (bf16[2,15,16,128]{3,1,2,0:T(8,128)(2,1)S(1)}, bf16[2,15,16,128]{3,1,2,0:T(8,128)(2,1)S(1)}, u32[]{:S(2)}, u32[]{:S(2)}) collective-permute-start(bf16[2,15,16,128]{3,1,2,0:T(8,128)(2,1)S(1)} %constant_dynamic-slice_fusion), channel_id=1, source_target_pairs={{0,2},{2,0},{1,3},{3,1},{4,6},{6,4},{5,7},{7,5},{8,10},{10,8},{9,1... | collective-permute-start | bytes 368648 | tf_op jit(solution)/shard_map/ppermute | solution.py:118
  76.5 3.5 %collective-permute-done.13 = bf16[2,15,16,128]{3,1,2,0:T(8,128)(2,1)S(1)} collective-permute-done((bf16[2,15,16,128]{3,1,2,0:T(8,128)(2,1)S(1)}, bf16[2,15,16,128]{3,1,2,0:T(8,128)(2,1)S(1)}, u32[]{:S(2)}, u32[]{:S(2)}) %collective-permute-start.13) | collective-permute-done | bytes 122912 | tf_op jit(solution)/shard_map/ppermute | solution.py:118
  81.2 4.3 %collective-permute-start.14 = (f32[32,16,128]{2,1,0:T(8,128)S(1)}, f32[32,16,128]{2,1,0:T(8,128)S(1)}, u32[]{:S(2)}, u32[]{:S(2)}) collective-permute-start(f32[32,16,128]{2,1,0:T(8,128)S(1)} %dynamic-slice_bitcast_fusion), channel_id=1, source_target_pairs={{0,1},{1,0},{2,3},{3,2},{4,5},{5,4},{6,7},{7,6},{8,9},{9,8},{10,11... | collective-permute-start | bytes 786440 | tf_op jit(solution)/shard_map/ppermute | solution.py:23
  85.4 1.2 %collective-permute-done.14 = f32[32,16,128]{2,1,0:T(8,128)S(1)} collective-permute-done((f32[32,16,128]{2,1,0:T(8,128)S(1)}, f32[32,16,128]{2,1,0:T(8,128)S(1)}, u32[]{:S(2)}, u32[]{:S(2)}) %collective-permute-start.14) | collective-permute-done | bytes 262176 | tf_op jit(solution)/shard_map/ppermute | solution.py:23
  86.6 0.9 pad_maximum_fusion.1
  (101 shorter events, 17.0 us)
Async XLA Ops:
  4.5 2.1 %collective-permute-start = (bf16[2,64,16,128]{3,2,1,0:T(8,128)(2,1)S(1)}, bf16[2,64,16,128]{3,2,1,0:T(8,128)(2,1)S(1)}, u32[]{:S(2)}, u32[]{:S(2)}) collective-permute-start(bf16[2,64,16,128]{3,2,1,0:T(8,128)(2,1)S(1)} %pad_maximum_fusion), channel_id=1, source_target_pairs={{0,1},{1,0},{2,3},{3,2},{4,5},{5,4},{6,7},{7,6},{8,9},{9,8},{10,11... | collective-permute-start | bytes 1572872 | tf_op jit(solution)/shard_map/ppermute | solution.py:23
  5.1 2.3 %copy-start = (f32[2,3,31]{2,0,1:T(2,128)S(1)}, f32[2,3,31]{2,0,1:T(2,128)}, u32[]{:S(2)}) copy-start(f32[2,3,31]{2,0,1:T(2,128)} %param.4) | copy-start | bytes 2236
  6.7 3.2 %collective-permute-start.1 = (bf16[2,64,16,128]{3,2,1,0:T(8,128)(2,1)S(1)}, bf16[2,64,16,128]{3,2,1,0:T(8,128)(2,1)S(1)}, u32[]{:S(2)}, u32[]{:S(2)}) collective-permute-start(bf16[2,64,16,128]{3,2,1,0:T(8,128)(2,1)S(1)} %maximum_select_fusion.1), channel_id=1, source_target_pairs={{1,4},{4,1},{3,6},{6,3},{5,8},{8,5},{7,10},{10,7},{9,12},{12,9},{1... | collective-permute-start | bytes 1572872 | tf_op jit(solution)/shard_map/ppermute | solution.py:184
  10.2 12.4 %collective-permute-start.2 = (bf16[64,15,128]{2,1,0:T(8,128)(2,1)S(1)}, bf16[64,15,128]{2,1,0:T(8,128)(2,1)S(1)}, u32[]{:S(2)}, u32[]{:S(2)}) collective-permute-start(bf16[64,15,128]{2,1,0:T(8,128)(2,1)S(1)} %get-tuple-element.61), channel_id=1, source_target_pairs={{1,4},{4,1},{3,6},{6,3},{5,8},{8,5},{7,10},{10,7},{9,12},{12,9},{1... | collective-permute-start | bytes 737288 | tf_op jit(solution)/shard_map/ppermute | solution.py:139
  10.9 12.8 %collective-permute-start.3 = (bf16[64,15,128]{2,1,0:T(8,128)(2,1)S(1)}, bf16[64,15,128]{2,1,0:T(8,128)(2,1)S(1)}, u32[]{:S(2)}, u32[]{:S(2)}) collective-permute-start(bf16[64,15,128]{2,1,0:T(8,128)(2,1)S(1)} %get-tuple-element.62), channel_id=1, source_target_pairs={{0,1},{1,0},{2,3},{3,2},{4,5},{5,4},{6,7},{7,6},{8,9},{9,8},{10,11... | collective-permute-start | bytes 737288 | tf_op jit(solution)/shard_map/ppermute | solution.py:23
  24.7 5.0 %collective-permute-start.4 = (bf16[2,15,16,128]{3,1,2,0:T(8,128)(2,1)S(1)}, bf16[2,15,16,128]{3,1,2,0:T(8,128)(2,1)S(1)}, u32[]{:S(2)}, u32[]{:S(2)}) collective-permute-start(bf16[2,15,16,128]{3,1,2,0:T(8,128)(2,1)S(1)} %constant_dynamic-slice_fusion.3), channel_id=1, source_target_pairs={{0,2},{2,0},{1,3},{3,1},{4,6},{6,4},{5,7},{7,5},{8,10},{10,8},{9,1... | collective-permute-start | bytes 368648 | tf_op jit(solution)/shard_map/ppermute | solution.py:118
  31.0 7.2 %collective-permute-start.5 = (bf16[2,64,15,128]{3,2,1,0:T(8,128)(2,1)S(1)}, bf16[2,64,15,128]{3,2,1,0:T(8,128)(2,1)S(1)}, u32[]{:S(2)}, u32[]{:S(2)}) collective-permute-start(bf16[2,64,15,128]{3,2,1,0:T(8,128)(2,1)S(1)} %get-tuple-element.53), channel_id=1, source_target_pairs={{1,4},{4,1},{3,6},{6,3},{5,8},{8,5},{7,10},{10,7},{9,12},{12,9},{1... | collective-permute-start | bytes 1474568 | tf_op jit(solution)/shard_map/ppermute | solution.py:139
  31.7 7.9 %collective-permute-start.6 = (bf16[2,64,15,128]{3,2,1,0:T(8,128)(2,1)S(1)}, bf16[2,64,15,128]{3,2,1,0:T(8,128)(2,1)S(1)}, u32[]{:S(2)}, u32[]{:S(2)}) collective-permute-start(bf16[2,64,15,128]{3,2,1,0:T(8,128)(2,1)S(1)} %get-tuple-element.54), channel_id=1, source_target_pairs={{0,1},{1,0},{2,3},{3,2},{4,5},{5,4},{6,7},{7,6},{8,9},{9,8},{10,11... | collective-permute-start | bytes 1474568 | tf_op jit(solution)/shard_map/ppermute | solution.py:23
  40.9 5.0 %collective-permute-start.7 = (bf16[2,15,16,128]{3,1,2,0:T(8,128)(2,1)S(1)}, bf16[2,15,16,128]{3,1,2,0:T(8,128)(2,1)S(1)}, u32[]{:S(2)}, u32[]{:S(2)}) collective-permute-start(bf16[2,15,16,128]{3,1,2,0:T(8,128)(2,1)S(1)} %constant_dynamic-slice_fusion.2), channel_id=1, source_target_pairs={{0,2},{2,0},{1,3},{3,1},{4,6},{6,4},{5,7},{7,5},{8,10},{10,8},{9,1... | collective-permute-start | bytes 368648 | tf_op jit(solution)/shard_map/ppermute | solution.py:118
  47.2 9.5 %collective-permute-start.8 = (bf16[64,15,128]{2,1,0:T(8,128)(2,1)S(1)}, bf16[64,15,128]{2,1,0:T(8,128)(2,1)S(1)}, u32[]{:S(2)}, u32[]{:S(2)}) collective-permute-start(bf16[64,15,128]{2,1,0:T(8,128)(2,1)S(1)} %get-tuple-element.59), channel_id=1, source_target_pairs={{1,4},{4,1},{3,6},{6,3},{5,8},{8,5},{7,10},{10,7},{9,12},{12,9},{1... | collective-permute-start | bytes 737288 | tf_op jit(solution)/shard_map/ppermute | solution.py:139
  47.9 10.0 %collective-permute-start.9 = (bf16[64,15,128]{2,1,0:T(8,128)(2,1)S(1)}, bf16[64,15,128]{2,1,0:T(8,128)(2,1)S(1)}, u32[]{:S(2)}, u32[]{:S(2)}) collective-permute-start(bf16[64,15,128]{2,1,0:T(8,128)(2,1)S(1)} %get-tuple-element.60), channel_id=1, source_target_pairs={{0,1},{1,0},{2,3},{3,2},{4,5},{5,4},{6,7},{7,6},{8,9},{9,8},{10,11... | collective-permute-start | bytes 737288 | tf_op jit(solution)/shard_map/ppermute | solution.py:23
  58.9 5.0 %collective-permute-start.10 = (bf16[2,15,16,128]{3,1,2,0:T(8,128)(2,1)S(1)}, bf16[2,15,16,128]{3,1,2,0:T(8,128)(2,1)S(1)}, u32[]{:S(2)}, u32[]{:S(2)}) collective-permute-start(bf16[2,15,16,128]{3,1,2,0:T(8,128)(2,1)S(1)} %constant_dynamic-slice_fusion.1), channel_id=1, source_target_pairs={{0,2},{2,0},{1,3},{3,1},{4,6},{6,4},{5,7},{7,5},{8,10},{10,8},{9,1... | collective-permute-start | bytes 368648 | tf_op jit(solution)/shard_map/ppermute | solution.py:118
  65.2 7.0 %collective-permute-start.11 = (bf16[2,64,15,128]{3,2,1,0:T(8,128)(2,1)S(1)}, bf16[2,64,15,128]{3,2,1,0:T(8,128)(2,1)S(1)}, u32[]{:S(2)}, u32[]{:S(2)}) collective-permute-start(bf16[2,64,15,128]{3,2,1,0:T(8,128)(2,1)S(1)} %get-tuple-element.49), channel_id=1, source_target_pairs={{1,4},{4,1},{3,6},{6,3},{5,8},{8,5},{7,10},{10,7},{9,12},{12,9},{1... | collective-permute-start | bytes 1474568 | tf_op jit(solution)/shard_map/ppermute | solution.py:139
  66.1 7.6 %collective-permute-start.12 = (bf16[2,64,15,128]{3,2,1,0:T(8,128)(2,1)S(1)}, bf16[2,64,15,128]{3,2,1,0:T(8,128)(2,1)S(1)}, u32[]{:S(2)}, u32[]{:S(2)}) collective-permute-start(bf16[2,64,15,128]{3,2,1,0:T(8,128)(2,1)S(1)} %get-tuple-element.50), channel_id=1, source_target_pairs={{0,1},{1,0},{2,3},{3,2},{4,5},{5,4},{6,7},{7,6},{8,9},{9,8},{10,11... | collective-permute-start | bytes 1474568 | tf_op jit(solution)/shard_map/ppermute | solution.py:23
  74.9 5.0 %collective-permute-start.13 = (bf16[2,15,16,128]{3,1,2,0:T(8,128)(2,1)S(1)}, bf16[2,15,16,128]{3,1,2,0:T(8,128)(2,1)S(1)}, u32[]{:S(2)}, u32[]{:S(2)}) collective-permute-start(bf16[2,15,16,128]{3,1,2,0:T(8,128)(2,1)S(1)} %constant_dynamic-slice_fusion), channel_id=1, source_target_pairs={{0,2},{2,0},{1,3},{3,1},{4,6},{6,4},{5,7},{7,5},{8,10},{10,8},{9,1... | collective-permute-start | bytes 368648 | tf_op jit(solution)/shard_map/ppermute | solution.py:118
  81.2 5.4 %collective-permute-start.14 = (f32[32,16,128]{2,1,0:T(8,128)S(1)}, f32[32,16,128]{2,1,0:T(8,128)S(1)}, u32[]{:S(2)}, u32[]{:S(2)}) collective-permute-start(f32[32,16,128]{2,1,0:T(8,128)S(1)} %dynamic-slice_bitcast_fusion), channel_id=1, source_target_pairs={{0,1},{1,0},{2,3},{3,2},{4,5},{5,4},{6,7},{7,6},{8,9},{9,8},{10,11... | collective-permute-start | bytes 786440 | tf_op jit(solution)/shard_map/ppermute | solution.py:23

commit v16 on v15

--- a/solution.py
+++ b/solution.py
@@ -162,9 +162,16 @@
         target = jnp.clip(target, 0, tile_total - 1)
         starts.append(target * block_count + half * half_blocks)
     slots = jnp.concatenate([lax.dynamic_slice_in_dim(sources, st, half_blocks) for st in starts])
-    picked = jnp.take(blocks, slots % block_count, axis=1)
-    mine = (slots // block_count == tile_index)[None, :, None, None]
-    partials = jnp.where(mine, picked, jnp.zeros((), picked.dtype))
+    row_ids = jnp.arange(slots.shape[0] * BX, dtype=jnp.int32)
+    row_slots = slots[row_ids // BX]
+    source_x = (row_slots % block_count) * BX + row_ids % BX
+    chosen_rows = (row_slots // block_count == tile_index)[:, None] & (
+        source_x[:, None] == jnp.arange(width_x, dtype=jnp.int32)[None, :]
+    )
+    selection = jnp.broadcast_to(chosen_rows.astype(acquired.dtype)[None], (planes,) + chosen_rows.shape)
+    partials = jnp.einsum(
+        "zrx,zxy->zry", selection, acquired, preferred_element_type=jnp.float32
+    ).astype(acquired.dtype)
     partials = partials.reshape(planes, 4, half_x, width_y)
     own_keep = jnp.where(first, partials[:, 0], partials[:, 1])
     own_give = jnp.where(first, partials[:, 1], partials[:, 0])

time: 87.9 us -> 85.8 us (0.976)
  local copies, waits for them, and re-layouts: 5.19 us -> 3.49 us
    unnamed x3 -> x4, local copies, waits for them, and re-layouts: 1.26 us -> 0.01 us
    concatenate x3 -> x0, local copies, waits for them, and re-layouts: 1.04 us -> none  [local(): jnp.concatenate([lax.dynamic_slice_in_dim(sources, st, half_blocks) for s...]
    dynamic_slice x0 -> x1, local copies, waits for them, and re-layouts: none -> 0.89 us  [local(): lax.dynamic_slice_in_dim(sources, st, half_blocks)]
where the time goes in v16:
time: 85.8 us; the launch traced here: 85.5 us
  starting transfers between devices  47.6 us (55%)
  waiting for transfers between devices  21.7 us (25%)
  other arithmetic  7.04 us (8%)
  matrix products  5.1 us (6%)
  local copies, waits for them, and re-layouts  3.49 us (4%)
    ppermute x6, starting transfers between devices, from_partner(): return lax.ppermute(block, axis, route)  37.8 us
    ppermute x4, waiting for transfers between devices, z_rims(): got = lax.ppermute(payload, 'view', route)  13.9 us
    ppermute x6, waiting for transfers between devices, from_partner(): return lax.ppermute(block, axis, route)  7.8 us
    ppermute x4, starting transfers between devices, z_rims(): got = lax.ppermute(payload, 'view', route)  6.22 us
    ppermute x4, starting transfers between devices, x_rims(): across = lax.ppermute(outward, ('tile', 'view'), route)  2.92 us
  transfers between devices with their start and end apart: 15, of which 10 were waited for; matrix products, arithmetic and copies ran while one was open for 3% of the time, Pallas kernels for 0%

profile of v16, /device:TPU:0, one launch (start us, length us, event | category | flops | bytes accessed | tf_op | source)
XLA Modules:
  0.0 85.5 jit_solution(5008036340788404592)
XLA Ops:
  0.0 0.9 %fusion.71 = (s32[4]{0:T(128)S(1)}, s32[4]{0:T(128)S(1)}, s32[4]{0:T(128)S(1)}, s32[4]{0:T(128)S(1)}) fusion(s32[1,32]{1,0:T(1,128)} %param.5, s32[]{:T(128)S(6)} %select_n.343, s32[]{:T(128)S(6)} %select_n.344, s32[]{:T(128)S(6)} %select_n.346, s32[]{:T(128)S(6)} %select_n.345), kind=kLoop, calls=%fused_computation.181 | loop fusion | bytes 144 | tf_op jit(solution)/shard_map/dynamic_slice | solution.py:164
  1.0 0.8 gather_fusion
  3.0 1.5 %collective-permute-done = bf16[2,64,16,128]{3,2,1,0:T(8,128)(2,1)S(1)} collective-permute-done((bf16[2,64,16,128]{3,2,1,0:T(8,128)(2,1)S(1)}, bf16[2,64,16,128]{3,2,1,0:T(8,128)(2,1)S(1)}, u32[]{:S(2)}, u32[]{:S(2)}) %collective-permute-start) | collective-permute-done | bytes 524320 | tf_op jit(solution)/shard_map/ppermute | solution.py:23
  6.9 1.0 %select_reduce_fusion.1 = (bf16[128,128]{1,0:T(8,128)(2,1)S(1)}, bf16[128,128]{1,0:T(8,128)(2,1)S(1)}, bf16[128,128]{1,0:T(8,128)(2,1)S(1)}, bf16[128,128]{1,0:T(8,128)(2,1)S(1)}) fusion(f32[31]{0:T(128)S(1)} %get-tuple-element.74, s32[128,128]{1,0:T(8,128)S(1)} %subtract_add_fusion, f32[31]{0:T(128)S(1)} %get-tuple-element.75, f32[31]{0:T(128)S(1)} %get-tuple-element.89, ...), kind=kLoop, calls=%fused_computation.2 | loop fusion | flops 4505600 | bytes 197104 | tf_op jit(solution)/shard_map/reduce_sum | solution.py:45
  8.8 11.7 %collective-permute-start.3 = (bf16[64,15,128]{2,1,0:T(8,128)(2,1)S(1)}, bf16[64,15,128]{2,1,0:T(8,128)(2,1)S(1)}, u32[]{:S(2)}, u32[]{:S(2)}) collective-permute-start(bf16[64,15,128]{2,1,0:T(8,128)(2,1)S(1)} %get-tuple-element.62), channel_id=1, source_target_pairs={{0,1},{1,0},{2,3},{3,2},{4,5},{5,4},{6,7},{7,6},{8,9},{9,8},{10,11... | collective-permute-start | bytes 737288 | tf_op jit(solution)/shard_map/ppermute | solution.py:23
  20.6 1.0 %collective-permute-done.3 = bf16[64,15,128]{2,1,0:T(8,128)(2,1)S(1)} collective-permute-done((bf16[64,15,128]{2,1,0:T(8,128)(2,1)S(1)}, bf16[64,15,128]{2,1,0:T(8,128)(2,1)S(1)}, u32[]{:S(2)}, u32[]{:S(2)}) %collective-permute-start.3) | collective-permute-done | bytes 245792 | tf_op jit(solution)/shard_map/ppermute | solution.py:23
  22.6 1.6 %collective-permute-start.4 = (bf16[2,15,16,128]{3,1,2,0:T(8,128)(2,1)S(1)}, bf16[2,15,16,128]{3,1,2,0:T(8,128)(2,1)S(1)}, u32[]{:S(2)}, u32[]{:S(2)}) collective-permute-start(bf16[2,15,16,128]{3,1,2,0:T(8,128)(2,1)S(1)} %constant_dynamic-slice_fusion.3), channel_id=1, source_target_pairs={{0,2},{2,0},{1,3},{3,1},{4,6},{6,4},{5,7},{7,5},{8,10},{10,8},{9,1... | collective-permute-start | bytes 368648 | tf_op jit(solution)/shard_map/ppermute | solution.py:118
  24.2 3.5 %collective-permute-done.4 = bf16[2,15,16,128]{3,1,2,0:T(8,128)(2,1)S(1)} collective-permute-done((bf16[2,15,16,128]{3,1,2,0:T(8,128)(2,1)S(1)}, bf16[2,15,16,128]{3,1,2,0:T(8,128)(2,1)S(1)}, u32[]{:S(2)}, u32[]{:S(2)}) %collective-permute-start.4) | collective-permute-done | bytes 122912 | tf_op jit(solution)/shard_map/ppermute | solution.py:118
  29.7 6.4 %collective-permute-start.6 = (bf16[2,64,15,128]{3,2,1,0:T(8,128)(2,1)S(1)}, bf16[2,64,15,128]{3,2,1,0:T(8,128)(2,1)S(1)}, u32[]{:S(2)}, u32[]{:S(2)}) collective-permute-start(bf16[2,64,15,128]{3,2,1,0:T(8,128)(2,1)S(1)} %get-tuple-element.54), channel_id=1, source_target_pairs={{0,1},{1,0},{2,3},{3,2},{4,5},{5,4},{6,7},{7,6},{8,9},{9,8},{10,11... | collective-permute-start | bytes 1474568 | tf_op jit(solution)/shard_map/ppermute | solution.py:23
  36.2 1.4 %collective-permute-done.6 = bf16[2,64,15,128]{3,2,1,0:T(8,128)(2,1)S(1)} collective-permute-done((bf16[2,64,15,128]{3,2,1,0:T(8,128)(2,1)S(1)}, bf16[2,64,15,128]{3,2,1,0:T(8,128)(2,1)S(1)}, u32[]{:S(2)}, u32[]{:S(2)}) %collective-permute-start.6) | collective-permute-done | bytes 491552 | tf_op jit(solution)/shard_map/ppermute | solution.py:23
  38.8 1.6 %collective-permute-start.7 = (bf16[2,15,16,128]{3,1,2,0:T(8,128)(2,1)S(1)}, bf16[2,15,16,128]{3,1,2,0:T(8,128)(2,1)S(1)}, u32[]{:S(2)}, u32[]{:S(2)}) collective-permute-start(bf16[2,15,16,128]{3,1,2,0:T(8,128)(2,1)S(1)} %constant_dynamic-slice_fusion.2), channel_id=1, source_target_pairs={{0,2},{2,0},{1,3},{3,1},{4,6},{6,4},{5,7},{7,5},{8,10},{10,8},{9,1... | collective-permute-start | bytes 368648 | tf_op jit(solution)/shard_map/ppermute | solution.py:118
  40.4 3.5 %collective-permute-done.7 = bf16[2,15,16,128]{3,1,2,0:T(8,128)(2,1)S(1)} collective-permute-done((bf16[2,15,16,128]{3,1,2,0:T(8,128)(2,1)S(1)}, bf16[2,15,16,128]{3,1,2,0:T(8,128)(2,1)S(1)}, u32[]{:S(2)}, u32[]{:S(2)}) %collective-permute-start.7) | collective-permute-done | bytes 122912 | tf_op jit(solution)/shard_map/ppermute | solution.py:118
  45.8 8.8 %collective-permute-start.9 = (bf16[64,15,128]{2,1,0:T(8,128)(2,1)S(1)}, bf16[64,15,128]{2,1,0:T(8,128)(2,1)S(1)}, u32[]{:S(2)}, u32[]{:S(2)}) collective-permute-start(bf16[64,15,128]{2,1,0:T(8,128)(2,1)S(1)} %get-tuple-element.60), channel_id=1, source_target_pairs={{0,1},{1,0},{2,3},{3,2},{4,5},{5,4},{6,7},{7,6},{8,9},{9,8},{10,11... | collective-permute-start | bytes 737288 | tf_op jit(solution)/shard_map/ppermute | solution.py:23
  54.7 1.2 %collective-permute-done.9 = bf16[64,15,128]{2,1,0:T(8,128)(2,1)S(1)} collective-permute-done((bf16[64,15,128]{2,1,0:T(8,128)(2,1)S(1)}, bf16[64,15,128]{2,1,0:T(8,128)(2,1)S(1)}, u32[]{:S(2)}, u32[]{:S(2)}) %collective-permute-start.9) | collective-permute-done | bytes 245792 | tf_op jit(solution)/shard_map/ppermute | solution.py:23
  56.8 1.6 %collective-permute-start.10 = (bf16[2,15,16,128]{3,1,2,0:T(8,128)(2,1)S(1)}, bf16[2,15,16,128]{3,1,2,0:T(8,128)(2,1)S(1)}, u32[]{:S(2)}, u32[]{:S(2)}) collective-permute-start(bf16[2,15,16,128]{3,1,2,0:T(8,128)(2,1)S(1)} %constant_dynamic-slice_fusion.1), channel_id=1, source_target_pairs={{0,2},{2,0},{1,3},{3,1},{4,6},{6,4},{5,7},{7,5},{8,10},{10,8},{9,1... | collective-permute-start | bytes 368648 | tf_op jit(solution)/shard_map/ppermute | solution.py:118
  58.4 3.5 %collective-permute-done.10 = bf16[2,15,16,128]{3,1,2,0:T(8,128)(2,1)S(1)} collective-permute-done((bf16[2,15,16,128]{3,1,2,0:T(8,128)(2,1)S(1)}, bf16[2,15,16,128]{3,1,2,0:T(8,128)(2,1)S(1)}, u32[]{:S(2)}, u32[]{:S(2)}) %collective-permute-start.10) | collective-permute-done | bytes 122912 | tf_op jit(solution)/shard_map/ppermute | solution.py:118
  63.2 0.9 %collective-permute-start.11 = (bf16[2,64,15,128]{3,2,1,0:T(8,128)(2,1)S(1)}, bf16[2,64,15,128]{3,2,1,0:T(8,128)(2,1)S(1)}, u32[]{:S(2)}, u32[]{:S(2)}) collective-permute-start(bf16[2,64,15,128]{3,2,1,0:T(8,128)(2,1)S(1)} %get-tuple-element.49), channel_id=1, source_target_pairs={{1,4},{4,1},{3,6},{6,3},{5,8},{8,5},{7,10},{10,7},{9,12},{12,9},{1... | collective-permute-start | bytes 1474568 | tf_op jit(solution)/shard_map/ppermute | solution.py:139
  64.1 6.1 %collective-permute-start.12 = (bf16[2,64,15,128]{3,2,1,0:T(8,128)(2,1)S(1)}, bf16[2,64,15,128]{3,2,1,0:T(8,128)(2,1)S(1)}, u32[]{:S(2)}, u32[]{:S(2)}) collective-permute-start(bf16[2,64,15,128]{3,2,1,0:T(8,128)(2,1)S(1)} %get-tuple-element.50), channel_id=1, source_target_pairs={{0,1},{1,0},{2,3},{3,2},{4,5},{5,4},{6,7},{7,6},{8,9},{9,8},{10,11... | collective-permute-start | bytes 1474568 | tf_op jit(solution)/shard_map/ppermute | solution.py:23
  70.2 1.5 %collective-permute-done.12 = bf16[2,64,15,128]{3,2,1,0:T(8,128)(2,1)S(1)} collective-permute-done((bf16[2,64,15,128]{3,2,1,0:T(8,128)(2,1)S(1)}, bf16[2,64,15,128]{3,2,1,0:T(8,128)(2,1)S(1)}, u32[]{:S(2)}, u32[]{:S(2)}) %collective-permute-start.12) | collective-permute-done | bytes 491552 | tf_op jit(solution)/shard_map/ppermute | solution.py:23
  72.9 1.6 %collective-permute-start.13 = (bf16[2,15,16,128]{3,1,2,0:T(8,128)(2,1)S(1)}, bf16[2,15,16,128]{3,1,2,0:T(8,128)(2,1)S(1)}, u32[]{:S(2)}, u32[]{:S(2)}) collective-permute-start(bf16[2,15,16,128]{3,1,2,0:T(8,128)(2,1)S(1)} %constant_dynamic-slice_fusion), channel_id=1, source_target_pairs={{0,2},{2,0},{1,3},{3,1},{4,6},{6,4},{5,7},{7,5},{8,10},{10,8},{9,1... | collective-permute-start | bytes 368648 | tf_op jit(solution)/shard_map/ppermute | solution.py:118
  74.5 3.5 %collective-permute-done.13 = bf16[2,15,16,128]{3,1,2,0:T(8,128)(2,1)S(1)} collective-permute-done((bf16[2,15,16,128]{3,1,2,0:T(8,128)(2,1)S(1)}, bf16[2,15,16,128]{3,1,2,0:T(8,128)(2,1)S(1)}, u32[]{:S(2)}, u32[]{:S(2)}) %collective-permute-start.13) | collective-permute-done | bytes 122912 | tf_op jit(solution)/shard_map/ppermute | solution.py:118
  79.1 4.3 %collective-permute-start.14 = (f32[32,16,128]{2,1,0:T(8,128)S(1)}, f32[32,16,128]{2,1,0:T(8,128)S(1)}, u32[]{:S(2)}, u32[]{:S(2)}) collective-permute-start(f32[32,16,128]{2,1,0:T(8,128)S(1)} %dynamic-slice_bitcast_fusion), channel_id=1, source_target_pairs={{0,1},{1,0},{2,3},{3,2},{4,5},{5,4},{6,7},{7,6},{8,9},{9,8},{10,11... | collective-permute-start | bytes 786440 | tf_op jit(solution)/shard_map/ppermute | solution.py:23
  83.4 1.2 %collective-permute-done.14 = f32[32,16,128]{2,1,0:T(8,128)S(1)} collective-permute-done((f32[32,16,128]{2,1,0:T(8,128)S(1)}, f32[32,16,128]{2,1,0:T(8,128)S(1)}, u32[]{:S(2)}, u32[]{:S(2)}) %collective-permute-start.14) | collective-permute-done | bytes 262176 | tf_op jit(solution)/shard_map/ppermute | solution.py:23
  84.6 0.9 pad_maximum_fusion.1
  (94 shorter events, 15.4 us)
Async XLA Ops:
  0.0 1.8 %copy-start = (bf16[64,32,128]{2,1,0:T(8,128)(2,1)S(1)}, bf16[64,32,128]{2,1,0:T(8,128)(2,1)}, u32[]{:S(2)}) copy-start(bf16[64,32,128]{2,1,0:T(8,128)(2,1)} %param.3) | copy-start | bytes 1572868
  2.5 2.1 %collective-permute-start = (bf16[2,64,16,128]{3,2,1,0:T(8,128)(2,1)S(1)}, bf16[2,64,16,128]{3,2,1,0:T(8,128)(2,1)S(1)}, u32[]{:S(2)}, u32[]{:S(2)}) collective-permute-start(bf16[2,64,16,128]{3,2,1,0:T(8,128)(2,1)S(1)} %pad_maximum_fusion), channel_id=1, source_target_pairs={{0,1},{1,0},{2,3},{3,2},{4,5},{5,4},{6,7},{7,6},{8,9},{9,8},{10,11... | collective-permute-start | bytes 1572872 | tf_op jit(solution)/shard_map/ppermute | solution.py:23
  3.0 2.3 %copy-start.1 = (f32[2,3,31]{2,0,1:T(2,128)S(1)}, f32[2,3,31]{2,0,1:T(2,128)}, u32[]{:S(2)}) copy-start(f32[2,3,31]{2,0,1:T(2,128)} %param.4) | copy-start | bytes 2236
  4.7 3.2 %collective-permute-start.1 = (bf16[2,64,16,128]{3,2,1,0:T(8,128)(2,1)S(1)}, bf16[2,64,16,128]{3,2,1,0:T(8,128)(2,1)S(1)}, u32[]{:S(2)}, u32[]{:S(2)}) collective-permute-start(bf16[2,64,16,128]{3,2,1,0:T(8,128)(2,1)S(1)} %maximum_select_fusion.1), channel_id=1, source_target_pairs={{1,4},{4,1},{3,6},{6,3},{5,8},{8,5},{7,10},{10,7},{9,12},{12,9},{1... | collective-permute-start | bytes 1572872 | tf_op jit(solution)/shard_map/ppermute | solution.py:191
  8.1 12.5 %collective-permute-start.2 = (bf16[64,15,128]{2,1,0:T(8,128)(2,1)S(1)}, bf16[64,15,128]{2,1,0:T(8,128)(2,1)S(1)}, u32[]{:S(2)}, u32[]{:S(2)}) collective-permute-start(bf16[64,15,128]{2,1,0:T(8,128)(2,1)S(1)} %get-tuple-element.61), channel_id=1, source_target_pairs={{1,4},{4,1},{3,6},{6,3},{5,8},{8,5},{7,10},{10,7},{9,12},{12,9},{1... | collective-permute-start | bytes 737288 | tf_op jit(solution)/shard_map/ppermute | solution.py:139
  8.8 12.8 %collective-permute-start.3 = (bf16[64,15,128]{2,1,0:T(8,128)(2,1)S(1)}, bf16[64,15,128]{2,1,0:T(8,128)(2,1)S(1)}, u32[]{:S(2)}, u32[]{:S(2)}) collective-permute-start(bf16[64,15,128]{2,1,0:T(8,128)(2,1)S(1)} %get-tuple-element.62), channel_id=1, source_target_pairs={{0,1},{1,0},{2,3},{3,2},{4,5},{5,4},{6,7},{7,6},{8,9},{9,8},{10,11... | collective-permute-start | bytes 737288 | tf_op jit(solution)/shard_map/ppermute | solution.py:23
  22.6 5.0 %collective-permute-start.4 = (bf16[2,15,16,128]{3,1,2,0:T(8,128)(2,1)S(1)}, bf16[2,15,16,128]{3,1,2,0:T(8,128)(2,1)S(1)}, u32[]{:S(2)}, u32[]{:S(2)}) collective-permute-start(bf16[2,15,16,128]{3,1,2,0:T(8,128)(2,1)S(1)} %constant_dynamic-slice_fusion.3), channel_id=1, source_target_pairs={{0,2},{2,0},{1,3},{3,1},{4,6},{6,4},{5,7},{7,5},{8,10},{10,8},{9,1... | collective-permute-start | bytes 368648 | tf_op jit(solution)/shard_map/ppermute | solution.py:118
  29.0 7.2 %collective-permute-start.5 = (bf16[2,64,15,128]{3,2,1,0:T(8,128)(2,1)S(1)}, bf16[2,64,15,128]{3,2,1,0:T(8,128)(2,1)S(1)}, u32[]{:S(2)}, u32[]{:S(2)}) collective-permute-start(bf16[2,64,15,128]{3,2,1,0:T(8,128)(2,1)S(1)} %get-tuple-element.53), channel_id=1, source_target_pairs={{1,4},{4,1},{3,6},{6,3},{5,8},{8,5},{7,10},{10,7},{9,12},{12,9},{1... | collective-permute-start | bytes 1474568 | tf_op jit(solution)/shard_map/ppermute | solution.py:139
  29.7 7.9 %collective-permute-start.6 = (bf16[2,64,15,128]{3,2,1,0:T(8,128)(2,1)S(1)}, bf16[2,64,15,128]{3,2,1,0:T(8,128)(2,1)S(1)}, u32[]{:S(2)}, u32[]{:S(2)}) collective-permute-start(bf16[2,64,15,128]{3,2,1,0:T(8,128)(2,1)S(1)} %get-tuple-element.54), channel_id=1, source_target_pairs={{0,1},{1,0},{2,3},{3,2},{4,5},{5,4},{6,7},{7,6},{8,9},{9,8},{10,11... | collective-permute-start | bytes 1474568 | tf_op jit(solution)/shard_map/ppermute | solution.py:23
  38.8 5.0 %collective-permute-start.7 = (bf16[2,15,16,128]{3,1,2,0:T(8,128)(2,1)S(1)}, bf16[2,15,16,128]{3,1,2,0:T(8,128)(2,1)S(1)}, u32[]{:S(2)}, u32[]{:S(2)}) collective-permute-start(bf16[2,15,16,128]{3,1,2,0:T(8,128)(2,1)S(1)} %constant_dynamic-slice_fusion.2), channel_id=1, source_target_pairs={{0,2},{2,0},{1,3},{3,1},{4,6},{6,4},{5,7},{7,5},{8,10},{10,8},{9,1... | collective-permute-start | bytes 368648 | tf_op jit(solution)/shard_map/ppermute | solution.py:118
  45.2 9.5 %collective-permute-start.8 = (bf16[64,15,128]{2,1,0:T(8,128)(2,1)S(1)}, bf16[64,15,128]{2,1,0:T(8,128)(2,1)S(1)}, u32[]{:S(2)}, u32[]{:S(2)}) collective-permute-start(bf16[64,15,128]{2,1,0:T(8,128)(2,1)S(1)} %get-tuple-element.59), channel_id=1, source_target_pairs={{1,4},{4,1},{3,6},{6,3},{5,8},{8,5},{7,10},{10,7},{9,12},{12,9},{1... | collective-permute-start | bytes 737288 | tf_op jit(solution)/shard_map/ppermute | solution.py:139
  45.8 10.0 %collective-permute-start.9 = (bf16[64,15,128]{2,1,0:T(8,128)(2,1)S(1)}, bf16[64,15,128]{2,1,0:T(8,128)(2,1)S(1)}, u32[]{:S(2)}, u32[]{:S(2)}) collective-permute-start(bf16[64,15,128]{2,1,0:T(8,128)(2,1)S(1)} %get-tuple-element.60), channel_id=1, source_target_pairs={{0,1},{1,0},{2,3},{3,2},{4,5},{5,4},{6,7},{7,6},{8,9},{9,8},{10,11... | collective-permute-start | bytes 737288 | tf_op jit(solution)/shard_map/ppermute | solution.py:23
  56.8 5.0 %collective-permute-start.10 = (bf16[2,15,16,128]{3,1,2,0:T(8,128)(2,1)S(1)}, bf16[2,15,16,128]{3,1,2,0:T(8,128)(2,1)S(1)}, u32[]{:S(2)}, u32[]{:S(2)}) collective-permute-start(bf16[2,15,16,128]{3,1,2,0:T(8,128)(2,1)S(1)} %constant_dynamic-slice_fusion.1), channel_id=1, source_target_pairs={{0,2},{2,0},{1,3},{3,1},{4,6},{6,4},{5,7},{7,5},{8,10},{10,8},{9,1... | collective-permute-start | bytes 368648 | tf_op jit(solution)/shard_map/ppermute | solution.py:118
  63.2 7.0 %collective-permute-start.11 = (bf16[2,64,15,128]{3,2,1,0:T(8,128)(2,1)S(1)}, bf16[2,64,15,128]{3,2,1,0:T(8,128)(2,1)S(1)}, u32[]{:S(2)}, u32[]{:S(2)}) collective-permute-start(bf16[2,64,15,128]{3,2,1,0:T(8,128)(2,1)S(1)} %get-tuple-element.49), channel_id=1, source_target_pairs={{1,4},{4,1},{3,6},{6,3},{5,8},{8,5},{7,10},{10,7},{9,12},{12,9},{1... | collective-permute-start | bytes 1474568 | tf_op jit(solution)/shard_map/ppermute | solution.py:139
  64.1 7.6 %collective-permute-start.12 = (bf16[2,64,15,128]{3,2,1,0:T(8,128)(2,1)S(1)}, bf16[2,64,15,128]{3,2,1,0:T(8,128)(2,1)S(1)}, u32[]{:S(2)}, u32[]{:S(2)}) collective-permute-start(bf16[2,64,15,128]{3,2,1,0:T(8,128)(2,1)S(1)} %get-tuple-element.50), channel_id=1, source_target_pairs={{0,1},{1,0},{2,3},{3,2},{4,5},{5,4},{6,7},{7,6},{8,9},{9,8},{10,11... | collective-permute-start | bytes 1474568 | tf_op jit(solution)/shard_map/ppermute | solution.py:23
  72.9 5.0 %collective-permute-start.13 = (bf16[2,15,16,128]{3,1,2,0:T(8,128)(2,1)S(1)}, bf16[2,15,16,128]{3,1,2,0:T(8,128)(2,1)S(1)}, u32[]{:S(2)}, u32[]{:S(2)}) collective-permute-start(bf16[2,15,16,128]{3,1,2,0:T(8,128)(2,1)S(1)} %constant_dynamic-slice_fusion), channel_id=1, source_target_pairs={{0,2},{2,0},{1,3},{3,1},{4,6},{6,4},{5,7},{7,5},{8,10},{10,8},{9,1... | collective-permute-start | bytes 368648 | tf_op jit(solution)/shard_map/ppermute | solution.py:118
  79.1 5.4 %collective-permute-start.14 = (f32[32,16,128]{2,1,0:T(8,128)S(1)}, f32[32,16,128]{2,1,0:T(8,128)S(1)}, u32[]{:S(2)}, u32[]{:S(2)}) collective-permute-start(f32[32,16,128]{2,1,0:T(8,128)S(1)} %dynamic-slice_bitcast_fusion), channel_id=1, source_target_pairs={{0,1},{1,0},{2,3},{3,2},{4,5},{5,4},{6,7},{7,6},{8,9},{9,8},{10,11... | collective-permute-start | bytes 786440 | tf_op jit(solution)/shard_map/ppermute | solution.py:23

commit v17 on v16

--- a/solution.py
+++ b/solution.py
@@ -157,13 +157,11 @@
     half_rows = planes // 2
     half_blocks = block_count // 2
     first = view_bit == 0
-    starts = []
-    for target, half in ((tile_index, 0), (tile_index, 1), (tile_index + 1, 0), (tile_index - 1, 1)):
-        target = jnp.clip(target, 0, tile_total - 1)
-        starts.append(target * block_count + half * half_blocks)
-    slots = jnp.concatenate([lax.dynamic_slice_in_dim(sources, st, half_blocks) for st in starts])
+    table = jnp.pad(sources.reshape(tile_total, block_count), ((1, 1), (0, 0)))
+    near = lax.dynamic_slice_in_dim(table, tile_index, 3, 0)
+    slots = jnp.concatenate([near[1], near[2, :half_blocks], near[0, half_blocks:]])
     row_ids = jnp.arange(slots.shape[0] * BX, dtype=jnp.int32)
-    row_slots = slots[row_ids // BX]
+    row_slots = jnp.repeat(slots, BX)
     source_x = (row_slots % block_count) * BX + row_ids % BX
     chosen_rows = (row_slots // block_count == tile_index)[:, None] & (
         source_x[:, None] == jnp.arange(width_x, dtype=jnp.int32)[None, :]

time: 85.8 us -> 86.3 us (level)
  other arithmetic: 7.04 us -> 8.35 us
    unnamed x0 -> x1, other arithmetic: none -> 1.32 us
    dynamic_slice x1, local copies, waits for them, and re-layouts: 0.89 us -> 0.01 us  [local(): near = lax.dynamic_slice_in_dim(table, tile_index, 3, 0)]
where the time goes in v17:
time: 86.3 us; the launch traced here: 86 us
  starting transfers between devices  47.6 us (55%)
  waiting for transfers between devices  21.7 us (25%)
  other arithmetic  8.35 us (10%)
  matrix products  5.1 us (6%)
  local copies, waits for them, and re-layouts  2.67 us (3%)
    ppermute x6, starting transfers between devices, from_partner(): return lax.ppermute(block, axis, route)  37.8 us
    ppermute x4, waiting for transfers between devices, z_rims(): got = lax.ppermute(payload, 'view', route)  13.9 us
    ppermute x6, waiting for transfers between devices, from_partner(): return lax.ppermute(block, axis, route)  7.8 us
    ppermute x4, starting transfers between devices, z_rims(): got = lax.ppermute(payload, 'view', route)  6.22 us
    ppermute x4, starting transfers between devices, x_rims(): across = lax.ppermute(outward, ('tile', 'view'), route)  2.92 us
  transfers between devices with their start and end apart: 15, of which 10 were waited for; matrix products, arithmetic and copies ran while one was open for 3% of the time, Pallas kernels for 0%

profile of v17, /device:TPU:0, one launch (start us, length us, event | category | flops | bytes accessed | tf_op | source)
XLA Modules:
  0.0 86.0 jit_solution(12094803669642445135)
XLA Ops:
  0.5 1.3 %reduce.3 = s32[32]{0:T(128)S(1)} reduce(s32[1,32]{1,0:T(1,128)} %param.5, s32[]{:T(128)} %broadcast.198), dimensions={0}, to_apply=%param.5.reduce_sub_computation.3 | reduce | bytes 260 | tf_op args[2]
  3.5 1.5 %collective-permute-done = bf16[2,64,16,128]{3,2,1,0:T(8,128)(2,1)S(1)} collective-permute-done((bf16[2,64,16,128]{3,2,1,0:T(8,128)(2,1)S(1)}, bf16[2,64,16,128]{3,2,1,0:T(8,128)(2,1)S(1)}, u32[]{:S(2)}, u32[]{:S(2)}) %collective-permute-start) | collective-permute-done | bytes 524320 | tf_op jit(solution)/shard_map/ppermute | solution.py:23
  7.3 1.0 %select_reduce_fusion.1 = (bf16[128,128]{1,0:T(8,128)(2,1)S(1)}, bf16[128,128]{1,0:T(8,128)(2,1)S(1)}, bf16[128,128]{1,0:T(8,128)(2,1)S(1)}, bf16[128,128]{1,0:T(8,128)(2,1)S(1)}) fusion(f32[31]{0:T(128)S(1)} %get-tuple-element.76, s32[128,128]{1,0:T(8,128)S(1)} %subtract_add_fusion, f32[31]{0:T(128)S(1)} %get-tuple-element.77, f32[31]{0:T(128)S(1)} %get-tuple-element.87, ...), kind=kLoop, calls=%fused_computation.1 | loop fusion | flops 4505600 | bytes 197104 | tf_op jit(solution)/shard_map/reduce_sum | solution.py:45
  9.3 11.7 %collective-permute-start.3 = (bf16[64,15,128]{2,1,0:T(8,128)(2,1)S(1)}, bf16[64,15,128]{2,1,0:T(8,128)(2,1)S(1)}, u32[]{:S(2)}, u32[]{:S(2)}) collective-permute-start(bf16[64,15,128]{2,1,0:T(8,128)(2,1)S(1)} %get-tuple-element.62), channel_id=1, source_target_pairs={{0,1},{1,0},{2,3},{3,2},{4,5},{5,4},{6,7},{7,6},{8,9},{9,8},{10,11... | collective-permute-start | bytes 737288 | tf_op jit(solution)/shard_map/ppermute | solution.py:23
  21.1 1.0 %collective-permute-done.3 = bf16[64,15,128]{2,1,0:T(8,128)(2,1)S(1)} collective-permute-done((bf16[64,15,128]{2,1,0:T(8,128)(2,1)S(1)}, bf16[64,15,128]{2,1,0:T(8,128)(2,1)S(1)}, u32[]{:S(2)}, u32[]{:S(2)}) %collective-permute-start.3) | collective-permute-done | bytes 245792 | tf_op jit(solution)/shard_map/ppermute | solution.py:23
  23.1 1.6 %collective-permute-start.4 = (bf16[2,15,16,128]{3,1,2,0:T(8,128)(2,1)S(1)}, bf16[2,15,16,128]{3,1,2,0:T(8,128)(2,1)S(1)}, u32[]{:S(2)}, u32[]{:S(2)}) collective-permute-start(bf16[2,15,16,128]{3,1,2,0:T(8,128)(2,1)S(1)} %constant_dynamic-slice_fusion.3), channel_id=1, source_target_pairs={{0,2},{2,0},{1,3},{3,1},{4,6},{6,4},{5,7},{7,5},{8,10},{10,8},{9,1... | collective-permute-start | bytes 368648 | tf_op jit(solution)/shard_map/ppermute | solution.py:118
  24.7 3.5 %collective-permute-done.4 = bf16[2,15,16,128]{3,1,2,0:T(8,128)(2,1)S(1)} collective-permute-done((bf16[2,15,16,128]{3,1,2,0:T(8,128)(2,1)S(1)}, bf16[2,15,16,128]{3,1,2,0:T(8,128)(2,1)S(1)}, u32[]{:S(2)}, u32[]{:S(2)}) %collective-permute-start.4) | collective-permute-done | bytes 122912 | tf_op jit(solution)/shard_map/ppermute | solution.py:118
  28.6 0.7 fusion.21
  30.2 6.4 %collective-permute-start.6 = (bf16[2,64,15,128]{3,2,1,0:T(8,128)(2,1)S(1)}, bf16[2,64,15,128]{3,2,1,0:T(8,128)(2,1)S(1)}, u32[]{:S(2)}, u32[]{:S(2)}) collective-permute-start(bf16[2,64,15,128]{3,2,1,0:T(8,128)(2,1)S(1)} %get-tuple-element.54), channel_id=1, source_target_pairs={{0,1},{1,0},{2,3},{3,2},{4,5},{5,4},{6,7},{7,6},{8,9},{9,8},{10,11... | collective-permute-start | bytes 1474568 | tf_op jit(solution)/shard_map/ppermute | solution.py:23
  36.7 1.4 %collective-permute-done.6 = bf16[2,64,15,128]{3,2,1,0:T(8,128)(2,1)S(1)} collective-permute-done((bf16[2,64,15,128]{3,2,1,0:T(8,128)(2,1)S(1)}, bf16[2,64,15,128]{3,2,1,0:T(8,128)(2,1)S(1)}, u32[]{:S(2)}, u32[]{:S(2)}) %collective-permute-start.6) | collective-permute-done | bytes 491552 | tf_op jit(solution)/shard_map/ppermute | solution.py:23
  39.3 1.6 %collective-permute-start.7 = (bf16[2,15,16,128]{3,1,2,0:T(8,128)(2,1)S(1)}, bf16[2,15,16,128]{3,1,2,0:T(8,128)(2,1)S(1)}, u32[]{:S(2)}, u32[]{:S(2)}) collective-permute-start(bf16[2,15,16,128]{3,1,2,0:T(8,128)(2,1)S(1)} %constant_dynamic-slice_fusion.2), channel_id=1, source_target_pairs={{0,2},{2,0},{1,3},{3,1},{4,6},{6,4},{5,7},{7,5},{8,10},{10,8},{9,1... | collective-permute-start | bytes 368648 | tf_op jit(solution)/shard_map/ppermute | solution.py:118
  40.9 3.5 %collective-permute-done.7 = bf16[2,15,16,128]{3,1,2,0:T(8,128)(2,1)S(1)} collective-permute-done((bf16[2,15,16,128]{3,1,2,0:T(8,128)(2,1)S(1)}, bf16[2,15,16,128]{3,1,2,0:T(8,128)(2,1)S(1)}, u32[]{:S(2)}, u32[]{:S(2)}) %collective-permute-start.7) | collective-permute-done | bytes 122912 | tf_op jit(solution)/shard_map/ppermute | solution.py:118
  46.3 8.8 %collective-permute-start.9 = (bf16[64,15,128]{2,1,0:T(8,128)(2,1)S(1)}, bf16[64,15,128]{2,1,0:T(8,128)(2,1)S(1)}, u32[]{:S(2)}, u32[]{:S(2)}) collective-permute-start(bf16[64,15,128]{2,1,0:T(8,128)(2,1)S(1)} %get-tuple-element.60), channel_id=1, source_target_pairs={{0,1},{1,0},{2,3},{3,2},{4,5},{5,4},{6,7},{7,6},{8,9},{9,8},{10,11... | collective-permute-start | bytes 737288 | tf_op jit(solution)/shard_map/ppermute | solution.py:23
  55.2 1.2 %collective-permute-done.9 = bf16[64,15,128]{2,1,0:T(8,128)(2,1)S(1)} collective-permute-done((bf16[64,15,128]{2,1,0:T(8,128)(2,1)S(1)}, bf16[64,15,128]{2,1,0:T(8,128)(2,1)S(1)}, u32[]{:S(2)}, u32[]{:S(2)}) %collective-permute-start.9) | collective-permute-done | bytes 245792 | tf_op jit(solution)/shard_map/ppermute | solution.py:23
  57.3 1.6 %collective-permute-start.10 = (bf16[2,15,16,128]{3,1,2,0:T(8,128)(2,1)S(1)}, bf16[2,15,16,128]{3,1,2,0:T(8,128)(2,1)S(1)}, u32[]{:S(2)}, u32[]{:S(2)}) collective-permute-start(bf16[2,15,16,128]{3,1,2,0:T(8,128)(2,1)S(1)} %constant_dynamic-slice_fusion.1), channel_id=1, source_target_pairs={{0,2},{2,0},{1,3},{3,1},{4,6},{6,4},{5,7},{7,5},{8,10},{10,8},{9,1... | collective-permute-start | bytes 368648 | tf_op jit(solution)/shard_map/ppermute | solution.py:118
  58.9 3.5 %collective-permute-done.10 = bf16[2,15,16,128]{3,1,2,0:T(8,128)(2,1)S(1)} collective-permute-done((bf16[2,15,16,128]{3,1,2,0:T(8,128)(2,1)S(1)}, bf16[2,15,16,128]{3,1,2,0:T(8,128)(2,1)S(1)}, u32[]{:S(2)}, u32[]{:S(2)}) %collective-permute-start.10) | collective-permute-done | bytes 122912 | tf_op jit(solution)/shard_map/ppermute | solution.py:118
  63.7 0.9 %collective-permute-start.11 = (bf16[2,64,15,128]{3,2,1,0:T(8,128)(2,1)S(1)}, bf16[2,64,15,128]{3,2,1,0:T(8,128)(2,1)S(1)}, u32[]{:S(2)}, u32[]{:S(2)}) collective-permute-start(bf16[2,64,15,128]{3,2,1,0:T(8,128)(2,1)S(1)} %get-tuple-element.49), channel_id=1, source_target_pairs={{1,4},{4,1},{3,6},{6,3},{5,8},{8,5},{7,10},{10,7},{9,12},{12,9},{1... | collective-permute-start | bytes 1474568 | tf_op jit(solution)/shard_map/ppermute | solution.py:139
  64.6 6.1 %collective-permute-start.12 = (bf16[2,64,15,128]{3,2,1,0:T(8,128)(2,1)S(1)}, bf16[2,64,15,128]{3,2,1,0:T(8,128)(2,1)S(1)}, u32[]{:S(2)}, u32[]{:S(2)}) collective-permute-start(bf16[2,64,15,128]{3,2,1,0:T(8,128)(2,1)S(1)} %get-tuple-element.50), channel_id=1, source_target_pairs={{0,1},{1,0},{2,3},{3,2},{4,5},{5,4},{6,7},{7,6},{8,9},{9,8},{10,11... | collective-permute-start | bytes 1474568 | tf_op jit(solution)/shard_map/ppermute | solution.py:23
  70.6 1.5 %collective-permute-done.12 = bf16[2,64,15,128]{3,2,1,0:T(8,128)(2,1)S(1)} collective-permute-done((bf16[2,64,15,128]{3,2,1,0:T(8,128)(2,1)S(1)}, bf16[2,64,15,128]{3,2,1,0:T(8,128)(2,1)S(1)}, u32[]{:S(2)}, u32[]{:S(2)}) %collective-permute-start.12) | collective-permute-done | bytes 491552 | tf_op jit(solution)/shard_map/ppermute | solution.py:23
  73.4 1.6 %collective-permute-start.13 = (bf16[2,15,16,128]{3,1,2,0:T(8,128)(2,1)S(1)}, bf16[2,15,16,128]{3,1,2,0:T(8,128)(2,1)S(1)}, u32[]{:S(2)}, u32[]{:S(2)}) collective-permute-start(bf16[2,15,16,128]{3,1,2,0:T(8,128)(2,1)S(1)} %constant_dynamic-slice_fusion), channel_id=1, source_target_pairs={{0,2},{2,0},{1,3},{3,1},{4,6},{6,4},{5,7},{7,5},{8,10},{10,8},{9,1... | collective-permute-start | bytes 368648 | tf_op jit(solution)/shard_map/ppermute | solution.py:118
  75.0 3.5 %collective-permute-done.13 = bf16[2,15,16,128]{3,1,2,0:T(8,128)(2,1)S(1)} collective-permute-done((bf16[2,15,16,128]{3,1,2,0:T(8,128)(2,1)S(1)}, bf16[2,15,16,128]{3,1,2,0:T(8,128)(2,1)S(1)}, u32[]{:S(2)}, u32[]{:S(2)}) %collective-permute-start.13) | collective-permute-done | bytes 122912 | tf_op jit(solution)/shard_map/ppermute | solution.py:118
  79.6 4.3 %collective-permute-start.14 = (f32[32,16,128]{2,1,0:T(8,128)S(1)}, f32[32,16,128]{2,1,0:T(8,128)S(1)}, u32[]{:S(2)}, u32[]{:S(2)}) collective-permute-start(f32[32,16,128]{2,1,0:T(8,128)S(1)} %dynamic-slice_bitcast_fusion), channel_id=1, source_target_pairs={{0,1},{1,0},{2,3},{3,2},{4,5},{5,4},{6,7},{7,6},{8,9},{9,8},{10,11... | collective-permute-start | bytes 786440 | tf_op jit(solution)/shard_map/ppermute | solution.py:23
  83.9 1.2 %collective-permute-done.14 = f32[32,16,128]{2,1,0:T(8,128)S(1)} collective-permute-done((f32[32,16,128]{2,1,0:T(8,128)S(1)}, f32[32,16,128]{2,1,0:T(8,128)S(1)}, u32[]{:S(2)}, u32[]{:S(2)}) %collective-permute-start.14) | collective-permute-done | bytes 262176 | tf_op jit(solution)/shard_map/ppermute | solution.py:23
  85.1 0.9 pad_maximum_fusion.1
  (98 shorter events, 15.5 us)
Async XLA Ops:
  0.0 2.3 %copy-start = (bf16[64,32,128]{2,1,0:T(8,128)(2,1)S(1)}, bf16[64,32,128]{2,1,0:T(8,128)(2,1)}, u32[]{:S(2)}) copy-start(bf16[64,32,128]{2,1,0:T(8,128)(2,1)} %param.3) | copy-start | bytes 1572868
  3.0 2.1 %collective-permute-start = (bf16[2,64,16,128]{3,2,1,0:T(8,128)(2,1)S(1)}, bf16[2,64,16,128]{3,2,1,0:T(8,128)(2,1)S(1)}, u32[]{:S(2)}, u32[]{:S(2)}) collective-permute-start(bf16[2,64,16,128]{3,2,1,0:T(8,128)(2,1)S(1)} %pad_maximum_fusion), channel_id=1, source_target_pairs={{0,1},{1,0},{2,3},{3,2},{4,5},{5,4},{6,7},{7,6},{8,9},{9,8},{10,11... | collective-permute-start | bytes 1572872 | tf_op jit(solution)/shard_map/ppermute | solution.py:23
  3.5 2.3 %copy-start.1 = (f32[2,3,31]{2,0,1:T(2,128)S(1)}, f32[2,3,31]{2,0,1:T(2,128)}, u32[]{:S(2)}) copy-start(f32[2,3,31]{2,0,1:T(2,128)} %param.4) | copy-start | bytes 2236
  5.1 3.2 %collective-permute-start.1 = (bf16[2,64,16,128]{3,2,1,0:T(8,128)(2,1)S(1)}, bf16[2,64,16,128]{3,2,1,0:T(8,128)(2,1)S(1)}, u32[]{:S(2)}, u32[]{:S(2)}) collective-permute-start(bf16[2,64,16,128]{3,2,1,0:T(8,128)(2,1)S(1)} %maximum_select_fusion.1), channel_id=1, source_target_pairs={{1,4},{4,1},{3,6},{6,3},{5,8},{8,5},{7,10},{10,7},{9,12},{12,9},{1... | collective-permute-start | bytes 1572872 | tf_op jit(solution)/shard_map/ppermute | solution.py:189
  8.6 12.5 %collective-permute-start.2 = (bf16[64,15,128]{2,1,0:T(8,128)(2,1)S(1)}, bf16[64,15,128]{2,1,0:T(8,128)(2,1)S(1)}, u32[]{:S(2)}, u32[]{:S(2)}) collective-permute-start(bf16[64,15,128]{2,1,0:T(8,128)(2,1)S(1)} %get-tuple-element.61), channel_id=1, source_target_pairs={{1,4},{4,1},{3,6},{6,3},{5,8},{8,5},{7,10},{10,7},{9,12},{12,9},{1... | collective-permute-start | bytes 737288 | tf_op jit(solution)/shard_map/ppermute | solution.py:139
  9.3 12.8 %collective-permute-start.3 = (bf16[64,15,128]{2,1,0:T(8,128)(2,1)S(1)}, bf16[64,15,128]{2,1,0:T(8,128)(2,1)S(1)}, u32[]{:S(2)}, u32[]{:S(2)}) collective-permute-start(bf16[64,15,128]{2,1,0:T(8,128)(2,1)S(1)} %get-tuple-element.62), channel_id=1, source_target_pairs={{0,1},{1,0},{2,3},{3,2},{4,5},{5,4},{6,7},{7,6},{8,9},{9,8},{10,11... | collective-permute-start | bytes 737288 | tf_op jit(solution)/shard_map/ppermute | solution.py:23
  23.1 5.0 %collective-permute-start.4 = (bf16[2,15,16,128]{3,1,2,0:T(8,128)(2,1)S(1)}, bf16[2,15,16,128]{3,1,2,0:T(8,128)(2,1)S(1)}, u32[]{:S(2)}, u32[]{:S(2)}) collective-permute-start(bf16[2,15,16,128]{3,1,2,0:T(8,128)(2,1)S(1)} %constant_dynamic-slice_fusion.3), channel_id=1, source_target_pairs={{0,2},{2,0},{1,3},{3,1},{4,6},{6,4},{5,7},{7,5},{8,10},{10,8},{9,1... | collective-permute-start | bytes 368648 | tf_op jit(solution)/shard_map/ppermute | solution.py:118
  29.5 7.2 %collective-permute-start.5 = (bf16[2,64,15,128]{3,2,1,0:T(8,128)(2,1)S(1)}, bf16[2,64,15,128]{3,2,1,0:T(8,128)(2,1)S(1)}, u32[]{:S(2)}, u32[]{:S(2)}) collective-permute-start(bf16[2,64,15,128]{3,2,1,0:T(8,128)(2,1)S(1)} %get-tuple-element.53), channel_id=1, source_target_pairs={{1,4},{4,1},{3,6},{6,3},{5,8},{8,5},{7,10},{10,7},{9,12},{12,9},{1... | collective-permute-start | bytes 1474568 | tf_op jit(solution)/shard_map/ppermute | solution.py:139
  30.2 7.9 %collective-permute-start.6 = (bf16[2,64,15,128]{3,2,1,0:T(8,128)(2,1)S(1)}, bf16[2,64,15,128]{3,2,1,0:T(8,128)(2,1)S(1)}, u32[]{:S(2)}, u32[]{:S(2)}) collective-permute-start(bf16[2,64,15,128]{3,2,1,0:T(8,128)(2,1)S(1)} %get-tuple-element.54), channel_id=1, source_target_pairs={{0,1},{1,0},{2,3},{3,2},{4,5},{5,4},{6,7},{7,6},{8,9},{9,8},{10,11... | collective-permute-start | bytes 1474568 | tf_op jit(solution)/shard_map/ppermute | solution.py:23
  39.3 5.0 %collective-permute-start.7 = (bf16[2,15,16,128]{3,1,2,0:T(8,128)(2,1)S(1)}, bf16[2,15,16,128]{3,1,2,0:T(8,128)(2,1)S(1)}, u32[]{:S(2)}, u32[]{:S(2)}) collective-permute-start(bf16[2,15,16,128]{3,1,2,0:T(8,128)(2,1)S(1)} %constant_dynamic-slice_fusion.2), channel_id=1, source_target_pairs={{0,2},{2,0},{1,3},{3,1},{4,6},{6,4},{5,7},{7,5},{8,10},{10,8},{9,1... | collective-permute-start | bytes 368648 | tf_op jit(solution)/shard_map/ppermute | solution.py:118
  45.7 9.5 %collective-permute-start.8 = (bf16[64,15,128]{2,1,0:T(8,128)(2,1)S(1)}, bf16[64,15,128]{2,1,0:T(8,128)(2,1)S(1)}, u32[]{:S(2)}, u32[]{:S(2)}) collective-permute-start(bf16[64,15,128]{2,1,0:T(8,128)(2,1)S(1)} %get-tuple-element.59), channel_id=1, source_target_pairs={{1,4},{4,1},{3,6},{6,3},{5,8},{8,5},{7,10},{10,7},{9,12},{12,9},{1... | collective-permute-start | bytes 737288 | tf_op jit(solution)/shard_map/ppermute | solution.py:139
  46.3 10.0 %collective-permute-start.9 = (bf16[64,15,128]{2,1,0:T(8,128)(2,1)S(1)}, bf16[64,15,128]{2,1,0:T(8,128)(2,1)S(1)}, u32[]{:S(2)}, u32[]{:S(2)}) collective-permute-start(bf16[64,15,128]{2,1,0:T(8,128)(2,1)S(1)} %get-tuple-element.60), channel_id=1, source_target_pairs={{0,1},{1,0},{2,3},{3,2},{4,5},{5,4},{6,7},{7,6},{8,9},{9,8},{10,11... | collective-permute-start | bytes 737288 | tf_op jit(solution)/shard_map/ppermute | solution.py:23
  57.3 5.0 %collective-permute-start.10 = (bf16[2,15,16,128]{3,1,2,0:T(8,128)(2,1)S(1)}, bf16[2,15,16,128]{3,1,2,0:T(8,128)(2,1)S(1)}, u32[]{:S(2)}, u32[]{:S(2)}) collective-permute-start(bf16[2,15,16,128]{3,1,2,0:T(8,128)(2,1)S(1)} %constant_dynamic-slice_fusion.1), channel_id=1, source_target_pairs={{0,2},{2,0},{1,3},{3,1},{4,6},{6,4},{5,7},{7,5},{8,10},{10,8},{9,1... | collective-permute-start | bytes 368648 | tf_op jit(solution)/shard_map/ppermute | solution.py:118
  63.7 7.0 %collective-permute-start.11 = (bf16[2,64,15,128]{3,2,1,0:T(8,128)(2,1)S(1)}, bf16[2,64,15,128]{3,2,1,0:T(8,128)(2,1)S(1)}, u32[]{:S(2)}, u32[]{:S(2)}) collective-permute-start(bf16[2,64,15,128]{3,2,1,0:T(8,128)(2,1)S(1)} %get-tuple-element.49), channel_id=1, source_target_pairs={{1,4},{4,1},{3,6},{6,3},{5,8},{8,5},{7,10},{10,7},{9,12},{12,9},{1... | collective-permute-start | bytes 1474568 | tf_op jit(solution)/shard_map/ppermute | solution.py:139
  64.6 7.6 %collective-permute-start.12 = (bf16[2,64,15,128]{3,2,1,0:T(8,128)(2,1)S(1)}, bf16[2,64,15,128]{3,2,1,0:T(8,128)(2,1)S(1)}, u32[]{:S(2)}, u32[]{:S(2)}) collective-permute-start(bf16[2,64,15,128]{3,2,1,0:T(8,128)(2,1)S(1)} %get-tuple-element.50), channel_id=1, source_target_pairs={{0,1},{1,0},{2,3},{3,2},{4,5},{5,4},{6,7},{7,6},{8,9},{9,8},{10,11... | collective-permute-start | bytes 1474568 | tf_op jit(solution)/shard_map/ppermute | solution.py:23
  73.4 5.0 %collective-permute-start.13 = (bf16[2,15,16,128]{3,1,2,0:T(8,128)(2,1)S(1)}, bf16[2,15,16,128]{3,1,2,0:T(8,128)(2,1)S(1)}, u32[]{:S(2)}, u32[]{:S(2)}) collective-permute-start(bf16[2,15,16,128]{3,1,2,0:T(8,128)(2,1)S(1)} %constant_dynamic-slice_fusion), channel_id=1, source_target_pairs={{0,2},{2,0},{1,3},{3,1},{4,6},{6,4},{5,7},{7,5},{8,10},{10,8},{9,1... | collective-permute-start | bytes 368648 | tf_op jit(solution)/shard_map/ppermute | solution.py:118
  79.6 5.4 %collective-permute-start.14 = (f32[32,16,128]{2,1,0:T(8,128)S(1)}, f32[32,16,128]{2,1,0:T(8,128)S(1)}, u32[]{:S(2)}, u32[]{:S(2)}) collective-permute-start(f32[32,16,128]{2,1,0:T(8,128)S(1)} %dynamic-slice_bitcast_fusion), channel_id=1, source_target_pairs={{0,1},{1,0},{2,3},{3,2},{4,5},{5,4},{6,7},{7,6},{8,9},{9,8},{10,11... | collective-permute-start | bytes 786440 | tf_op jit(solution)/shard_map/ppermute | solution.py:23

commit v18 on v16

--- a/solution.py
+++ b/solution.py
@@ -177,7 +177,7 @@
     own_give = jnp.where(first, partials[:, 1], partials[:, 0])
     cross_keep = jnp.where(first, partials[:, 3], partials[:, 2])
     cross_pass = jnp.where(first, partials[:, 2], partials[:, 3])
-    got = from_partner(jnp.stack([own_give, cross_pass]), "view", 0)
+    got_pass = from_partner(cross_pass, "view", 0)
     tiles = lax.axis_size("tile")
     views = lax.axis_size("view")
     route = []
@@ -186,10 +186,11 @@
             right_core = tile * views + 2 * slab + 1
             left_core = (tile + 1) * views + 2 * slab
             route += [(right_core, left_core), (left_core, right_core)]
-    outgoing = jnp.where(first, jnp.stack([cross_keep, got[1]]), jnp.stack([got[1], cross_keep]))
-    outgoing, psf_taps = lax.optimization_barrier((outgoing, psf_taps))
+    outgoing = jnp.where(first, jnp.stack([cross_keep, got_pass]), jnp.stack([got_pass, cross_keep]))
+    outgoing, psf_taps, own_give = lax.optimization_barrier((outgoing, psf_taps, own_give))
     incoming = lax.ppermute(outgoing, ("tile", "view"), route)
-    own_parts = jnp.where(first, jnp.stack([own_keep, got[0]]), jnp.stack([got[0], own_keep]))
+    got_own = from_partner(own_give, "view", 0)
+    own_parts = jnp.where(first, jnp.stack([own_keep, got_own]), jnp.stack([got_own, own_keep]))
     views_measured = own_parts + incoming
     observed = views_measured.astype(jnp.float32)
     estimate = 0.5 * (observed[0] + observed[1])

time: 85.8 us -> 86.5 us (level)
  starting transfers between devices: 47.6 us -> 49 us
  waiting for transfers between devices: 21.7 us -> 20.7 us
    ppermute x6 -> x7, starting transfers between devices: 37.8 us -> 39.2 us  [from_partner(): return lax.ppermute(block, axis, route)]
    ppermute x6 -> x7, waiting for transfers between devices: 7.8 us -> 6.77 us  [from_partner(): return lax.ppermute(block, axis, route)]
  transfers between devices with their start and end apart: 15 -> 16, of which waited for: 10 -> 10; matrix products, arithmetic and copies ran while one was open for 3% -> 3% of each run, Pallas kernels for 0% -> 0%
where the time goes in v18:
time: 86.5 us; the launch traced here: 85.8 us
  starting transfers between devices  49 us (57%)
  waiting for transfers between devices  20.7 us (24%)
  other arithmetic  6.99 us (8%)
  matrix products  5.1 us (6%)
  local copies, waits for them, and re-layouts  3.45 us (4%)
    ppermute x7, starting transfers between devices, from_partner(): return lax.ppermute(block, axis, route)  39.2 us
    ppermute x4, waiting for transfers between devices, z_rims(): got = lax.ppermute(payload, 'view', route)  13.9 us
    ppermute x7, waiting for transfers between devices, from_partner(): return lax.ppermute(block, axis, route)  6.77 us
    ppermute x4, starting transfers between devices, z_rims(): got = lax.ppermute(payload, 'view', route)  6.21 us
    ppermute x4, starting transfers between devices, x_rims(): across = lax.ppermute(outward, ('tile', 'view'), route)  2.91 us
  transfers between devices with their start and end apart: 16, of which 10 were waited for; matrix products, arithmetic and copies ran while one was open for 3% of the time, Pallas kernels for 0%

profile of v18, /device:TPU:0, one launch (start us, length us, event | category | flops | bytes accessed | tf_op | source)
XLA Modules:
  0.0 85.8 jit_solution(11374634764191098475)
XLA Ops:
  0.0 0.9 %fusion.71 = (s32[4]{0:T(128)S(1)}, s32[4]{0:T(128)S(1)}, s32[4]{0:T(128)S(1)}, s32[4]{0:T(128)S(1)}) fusion(s32[1,32]{1,0:T(1,128)} %param.5, s32[]{:T(128)S(6)} %select_n.329, s32[]{:T(128)S(6)} %select_n.330, s32[]{:T(128)S(6)} %select_n.332, s32[]{:T(128)S(6)} %select_n.331), kind=kLoop, calls=%fused_computation.180 | loop fusion | bytes 144 | tf_op jit(solution)/shard_map/dynamic_slice | solution.py:164
  1.0 0.8 gather_fusion
  3.0 1.1 %collective-permute-done = bf16[64,16,128]{2,1,0:T(8,128)(2,1)S(1)} collective-permute-done((bf16[64,16,128]{2,1,0:T(8,128)(2,1)S(1)}, bf16[64,16,128]{2,1,0:T(8,128)(2,1)S(1)}, u32[]{:S(2)}, u32[]{:S(2)}) %collective-permute-start) | collective-permute-done | bytes 262176 | tf_op jit(solution)/shard_map/ppermute | solution.py:23
  4.9 4.3 %collective-permute-start.1 = (bf16[64,16,128]{2,1,0:T(8,128)(2,1)S(1)}, bf16[64,16,128]{2,1,0:T(8,128)(2,1)S(1)}, u32[]{:S(2)}, u32[]{:S(2)}) collective-permute-start(bf16[64,16,128]{2,1,0:T(8,128)(2,1)S(1)} %get-tuple-element.14), channel_id=1, source_target_pairs={{0,1},{1,0},{2,3},{3,2},{4,5},{5,4},{6,7},{7,6},{8,9},{9,8},{10,11... | collective-permute-start | bytes 786440 | tf_op jit(solution)/shard_map/ppermute | solution.py:23
  10.7 1.0 %select_reduce_fusion.1 = (bf16[128,128]{1,0:T(8,128)(2,1)S(1)}, bf16[128,128]{1,0:T(8,128)(2,1)S(1)}, bf16[128,128]{1,0:T(8,128)(2,1)S(1)}, bf16[128,128]{1,0:T(8,128)(2,1)S(1)}) fusion(f32[31]{0:T(128)S(1)} %get-tuple-element.74, s32[128,128]{1,0:T(8,128)S(1)} %subtract_add_fusion, f32[31]{0:T(128)S(1)} %get-tuple-element.75, f32[31]{0:T(128)S(1)} %get-tuple-element.89, ...), kind=kLoop, calls=%fused_computation.2 | loop fusion | flops 4505600 | bytes 197104 | tf_op jit(solution)/shard_map/reduce_sum | solution.py:45
  12.7 7.3 %collective-permute-start.4 = (bf16[64,15,128]{2,1,0:T(8,128)(2,1)S(1)}, bf16[64,15,128]{2,1,0:T(8,128)(2,1)S(1)}, u32[]{:S(2)}, u32[]{:S(2)}) collective-permute-start(bf16[64,15,128]{2,1,0:T(8,128)(2,1)S(1)} %get-tuple-element.62), channel_id=1, source_target_pairs={{0,1},{1,0},{2,3},{3,2},{4,5},{5,4},{6,7},{7,6},{8,9},{9,8},{10,11... | collective-permute-start | bytes 737288 | tf_op jit(solution)/shard_map/ppermute | solution.py:23
  20.1 1.0 %collective-permute-done.4 = bf16[64,15,128]{2,1,0:T(8,128)(2,1)S(1)} collective-permute-done((bf16[64,15,128]{2,1,0:T(8,128)(2,1)S(1)}, bf16[64,15,128]{2,1,0:T(8,128)(2,1)S(1)}, u32[]{:S(2)}, u32[]{:S(2)}) %collective-permute-start.4) | collective-permute-done | bytes 245792 | tf_op jit(solution)/shard_map/ppermute | solution.py:23
  22.1 1.6 %collective-permute-start.5 = (bf16[2,15,16,128]{3,1,2,0:T(8,128)(2,1)S(1)}, bf16[2,15,16,128]{3,1,2,0:T(8,128)(2,1)S(1)}, u32[]{:S(2)}, u32[]{:S(2)}) collective-permute-start(bf16[2,15,16,128]{3,1,2,0:T(8,128)(2,1)S(1)} %constant_dynamic-slice_fusion.3), channel_id=1, source_target_pairs={{0,2},{2,0},{1,3},{3,1},{4,6},{6,4},{5,7},{7,5},{8,10},{10,8},{9,1... | collective-permute-start | bytes 368648 | tf_op jit(solution)/shard_map/ppermute | solution.py:118
  23.7 3.5 %collective-permute-done.5 = bf16[2,15,16,128]{3,1,2,0:T(8,128)(2,1)S(1)} collective-permute-done((bf16[2,15,16,128]{3,1,2,0:T(8,128)(2,1)S(1)}, bf16[2,15,16,128]{3,1,2,0:T(8,128)(2,1)S(1)}, u32[]{:S(2)}, u32[]{:S(2)}) %collective-permute-start.5) | collective-permute-done | bytes 122912 | tf_op jit(solution)/shard_map/ppermute | solution.py:118
  29.2 6.4 %collective-permute-start.7 = (bf16[2,64,15,128]{3,2,1,0:T(8,128)(2,1)S(1)}, bf16[2,64,15,128]{3,2,1,0:T(8,128)(2,1)S(1)}, u32[]{:S(2)}, u32[]{:S(2)}) collective-permute-start(bf16[2,64,15,128]{3,2,1,0:T(8,128)(2,1)S(1)} %get-tuple-element.56), channel_id=1, source_target_pairs={{0,1},{1,0},{2,3},{3,2},{4,5},{5,4},{6,7},{7,6},{8,9},{9,8},{10,11... | collective-permute-start | bytes 1474568 | tf_op jit(solution)/shard_map/ppermute | solution.py:23
  35.7 1.4 %collective-permute-done.7 = bf16[2,64,15,128]{3,2,1,0:T(8,128)(2,1)S(1)} collective-permute-done((bf16[2,64,15,128]{3,2,1,0:T(8,128)(2,1)S(1)}, bf16[2,64,15,128]{3,2,1,0:T(8,128)(2,1)S(1)}, u32[]{:S(2)}, u32[]{:S(2)}) %collective-permute-start.7) | collective-permute-done | bytes 491552 | tf_op jit(solution)/shard_map/ppermute | solution.py:23
  38.4 1.6 %collective-permute-start.8 = (bf16[2,15,16,128]{3,1,2,0:T(8,128)(2,1)S(1)}, bf16[2,15,16,128]{3,1,2,0:T(8,128)(2,1)S(1)}, u32[]{:S(2)}, u32[]{:S(2)}) collective-permute-start(bf16[2,15,16,128]{3,1,2,0:T(8,128)(2,1)S(1)} %constant_dynamic-slice_fusion.2), channel_id=1, source_target_pairs={{0,2},{2,0},{1,3},{3,1},{4,6},{6,4},{5,7},{7,5},{8,10},{10,8},{9,1... | collective-permute-start | bytes 368648 | tf_op jit(solution)/shard_map/ppermute | solution.py:118
  39.9 3.5 %collective-permute-done.8 = bf16[2,15,16,128]{3,1,2,0:T(8,128)(2,1)S(1)} collective-permute-done((bf16[2,15,16,128]{3,1,2,0:T(8,128)(2,1)S(1)}, bf16[2,15,16,128]{3,1,2,0:T(8,128)(2,1)S(1)}, u32[]{:S(2)}, u32[]{:S(2)}) %collective-permute-start.8) | collective-permute-done | bytes 122912 | tf_op jit(solution)/shard_map/ppermute | solution.py:118
  44.7 4.5 %collective-permute-start.10 = (bf16[64,15,128]{2,1,0:T(8,128)(2,1)S(1)}, bf16[64,15,128]{2,1,0:T(8,128)(2,1)S(1)}, u32[]{:S(2)}, u32[]{:S(2)}) collective-permute-start(bf16[64,15,128]{2,1,0:T(8,128)(2,1)S(1)} %get-tuple-element.60), channel_id=1, source_target_pairs={{0,1},{1,0},{2,3},{3,2},{4,5},{5,4},{6,7},{7,6},{8,9},{9,8},{10,11... | collective-permute-start | bytes 737288 | tf_op jit(solution)/shard_map/ppermute | solution.py:23
  51.3 1.5 %collective-permute-start.11 = (bf16[2,15,16,128]{3,1,2,0:T(8,128)(2,1)S(1)}, bf16[2,15,16,128]{3,1,2,0:T(8,128)(2,1)S(1)}, u32[]{:S(2)}, u32[]{:S(2)}) collective-permute-start(bf16[2,15,16,128]{3,1,2,0:T(8,128)(2,1)S(1)} %constant_dynamic-slice_fusion.1), channel_id=1, source_target_pairs={{0,2},{2,0},{1,3},{3,1},{4,6},{6,4},{5,7},{7,5},{8,10},{10,8},{9,1... | collective-permute-start | bytes 368648 | tf_op jit(solution)/shard_map/ppermute | solution.py:118
  52.9 3.5 %collective-permute-done.11 = bf16[2,15,16,128]{3,1,2,0:T(8,128)(2,1)S(1)} collective-permute-done((bf16[2,15,16,128]{3,1,2,0:T(8,128)(2,1)S(1)}, bf16[2,15,16,128]{3,1,2,0:T(8,128)(2,1)S(1)}, u32[]{:S(2)}, u32[]{:S(2)}) %collective-permute-start.11) | collective-permute-done | bytes 122912 | tf_op jit(solution)/shard_map/ppermute | solution.py:118
  57.7 0.9 %collective-permute-start.12 = (bf16[2,64,15,128]{3,2,1,0:T(8,128)(2,1)S(1)}, bf16[2,64,15,128]{3,2,1,0:T(8,128)(2,1)S(1)}, u32[]{:S(2)}, u32[]{:S(2)}) collective-permute-start(bf16[2,64,15,128]{3,2,1,0:T(8,128)(2,1)S(1)} %get-tuple-element.51), channel_id=1, source_target_pairs={{1,4},{4,1},{3,6},{6,3},{5,8},{8,5},{7,10},{10,7},{9,12},{12,9},{1... | collective-permute-start | bytes 1474568 | tf_op jit(solution)/shard_map/ppermute | solution.py:139
  58.6 11.9 %collective-permute-start.13 = (bf16[2,64,15,128]{3,2,1,0:T(8,128)(2,1)S(1)}, bf16[2,64,15,128]{3,2,1,0:T(8,128)(2,1)S(1)}, u32[]{:S(2)}, u32[]{:S(2)}) collective-permute-start(bf16[2,64,15,128]{3,2,1,0:T(8,128)(2,1)S(1)} %get-tuple-element.52), channel_id=1, source_target_pairs={{0,1},{1,0},{2,3},{3,2},{4,5},{5,4},{6,7},{7,6},{8,9},{9,8},{10,11... | collective-permute-start | bytes 1474568 | tf_op jit(solution)/shard_map/ppermute | solution.py:23
  70.4 1.5 %collective-permute-done.13 = bf16[2,64,15,128]{3,2,1,0:T(8,128)(2,1)S(1)} collective-permute-done((bf16[2,64,15,128]{3,2,1,0:T(8,128)(2,1)S(1)}, bf16[2,64,15,128]{3,2,1,0:T(8,128)(2,1)S(1)}, u32[]{:S(2)}, u32[]{:S(2)}) %collective-permute-start.13) | collective-permute-done | bytes 491552 | tf_op jit(solution)/shard_map/ppermute | solution.py:23
  73.2 1.6 %collective-permute-start.14 = (bf16[2,15,16,128]{3,1,2,0:T(8,128)(2,1)S(1)}, bf16[2,15,16,128]{3,1,2,0:T(8,128)(2,1)S(1)}, u32[]{:S(2)}, u32[]{:S(2)}) collective-permute-start(bf16[2,15,16,128]{3,1,2,0:T(8,128)(2,1)S(1)} %constant_dynamic-slice_fusion), channel_id=1, source_target_pairs={{0,2},{2,0},{1,3},{3,1},{4,6},{6,4},{5,7},{7,5},{8,10},{10,8},{9,1... | collective-permute-start | bytes 368648 | tf_op jit(solution)/shard_map/ppermute | solution.py:118
  74.7 3.5 %collective-permute-done.14 = bf16[2,15,16,128]{3,1,2,0:T(8,128)(2,1)S(1)} collective-permute-done((bf16[2,15,16,128]{3,1,2,0:T(8,128)(2,1)S(1)}, bf16[2,15,16,128]{3,1,2,0:T(8,128)(2,1)S(1)}, u32[]{:S(2)}, u32[]{:S(2)}) %collective-permute-start.14) | collective-permute-done | bytes 122912 | tf_op jit(solution)/shard_map/ppermute | solution.py:118
  79.4 4.3 %collective-permute-start.15 = (f32[32,16,128]{2,1,0:T(8,128)S(1)}, f32[32,16,128]{2,1,0:T(8,128)S(1)}, u32[]{:S(2)}, u32[]{:S(2)}) collective-permute-start(f32[32,16,128]{2,1,0:T(8,128)S(1)} %dynamic-slice_bitcast_fusion), channel_id=1, source_target_pairs={{0,1},{1,0},{2,3},{3,2},{4,5},{5,4},{6,7},{7,6},{8,9},{9,8},{10,11... | collective-permute-start | bytes 786440 | tf_op jit(solution)/shard_map/ppermute | solution.py:23
  83.7 1.2 %collective-permute-done.15 = f32[32,16,128]{2,1,0:T(8,128)S(1)} collective-permute-done((f32[32,16,128]{2,1,0:T(8,128)S(1)}, f32[32,16,128]{2,1,0:T(8,128)S(1)}, u32[]{:S(2)}, u32[]{:S(2)}) %collective-permute-start.15) | collective-permute-done | bytes 262176 | tf_op jit(solution)/shard_map/ppermute | solution.py:23
  84.9 0.9 pad_maximum_fusion
  (94 shorter events, 15.8 us)
Async XLA Ops:
  0.0 1.8 %copy-start = (bf16[64,32,128]{2,1,0:T(8,128)(2,1)S(1)}, bf16[64,32,128]{2,1,0:T(8,128)(2,1)}, u32[]{:S(2)}) copy-start(bf16[64,32,128]{2,1,0:T(8,128)(2,1)} %param.3) | copy-start | bytes 1572868
  2.4 6.8 %copy-start.1 = (f32[2,3,31]{2,0,1:T(2,128)S(1)}, f32[2,3,31]{2,0,1:T(2,128)}, u32[]{:S(2)}) copy-start(f32[2,3,31]{2,0,1:T(2,128)} %param.4) | copy-start | bytes 2236
  2.4 1.7 %collective-permute-start = (bf16[64,16,128]{2,1,0:T(8,128)(2,1)S(1)}, bf16[64,16,128]{2,1,0:T(8,128)(2,1)S(1)}, u32[]{:S(2)}, u32[]{:S(2)}) collective-permute-start(bf16[64,16,128]{2,1,0:T(8,128)(2,1)S(1)} %get-tuple-element.47), channel_id=1, source_target_pairs={{0,1},{1,0},{2,3},{3,2},{4,5},{5,4},{6,7},{7,6},{8,9},{9,8},{10,11... | collective-permute-start | bytes 786440 | tf_op jit(solution)/shard_map/ppermute | solution.py:23
  4.2 7.5 %collective-permute-start.2 = (bf16[2,64,16,128]{3,2,1,0:T(8,128)(2,1)S(1)}, bf16[2,64,16,128]{3,2,1,0:T(8,128)(2,1)S(1)}, u32[]{:S(2)}, u32[]{:S(2)}) collective-permute-start(bf16[2,64,16,128]{3,2,1,0:T(8,128)(2,1)S(1)} %maximum_select_fusion), channel_id=1, source_target_pairs={{1,4},{4,1},{3,6},{6,3},{5,8},{8,5},{7,10},{10,7},{9,12},{12,9},{1... | collective-permute-start | bytes 1572872 | tf_op jit(solution)/shard_map/ppermute | solution.py:191
  4.9 6.8 %collective-permute-start.1 = (bf16[64,16,128]{2,1,0:T(8,128)(2,1)S(1)}, bf16[64,16,128]{2,1,0:T(8,128)(2,1)S(1)}, u32[]{:S(2)}, u32[]{:S(2)}) collective-permute-start(bf16[64,16,128]{2,1,0:T(8,128)(2,1)S(1)} %get-tuple-element.14), channel_id=1, source_target_pairs={{0,1},{1,0},{2,3},{3,2},{4,5},{5,4},{6,7},{7,6},{8,9},{9,8},{10,11... | collective-permute-start | bytes 786440 | tf_op jit(solution)/shard_map/ppermute | solution.py:23
  12.0 8.1 %collective-permute-start.3 = (bf16[64,15,128]{2,1,0:T(8,128)(2,1)S(1)}, bf16[64,15,128]{2,1,0:T(8,128)(2,1)S(1)}, u32[]{:S(2)}, u32[]{:S(2)}) collective-permute-start(bf16[64,15,128]{2,1,0:T(8,128)(2,1)S(1)} %get-tuple-element.61), channel_id=1, source_target_pairs={{1,4},{4,1},{3,6},{6,3},{5,8},{8,5},{7,10},{10,7},{9,12},{12,9},{1... | collective-permute-start | bytes 737288 | tf_op jit(solution)/shard_map/ppermute | solution.py:139
  12.7 8.5 %collective-permute-start.4 = (bf16[64,15,128]{2,1,0:T(8,128)(2,1)S(1)}, bf16[64,15,128]{2,1,0:T(8,128)(2,1)S(1)}, u32[]{:S(2)}, u32[]{:S(2)}) collective-permute-start(bf16[64,15,128]{2,1,0:T(8,128)(2,1)S(1)} %get-tuple-element.62), channel_id=1, source_target_pairs={{0,1},{1,0},{2,3},{3,2},{4,5},{5,4},{6,7},{7,6},{8,9},{9,8},{10,11... | collective-permute-start | bytes 737288 | tf_op jit(solution)/shard_map/ppermute | solution.py:23
  22.1 5.0 %collective-permute-start.5 = (bf16[2,15,16,128]{3,1,2,0:T(8,128)(2,1)S(1)}, bf16[2,15,16,128]{3,1,2,0:T(8,128)(2,1)S(1)}, u32[]{:S(2)}, u32[]{:S(2)}) collective-permute-start(bf16[2,15,16,128]{3,1,2,0:T(8,128)(2,1)S(1)} %constant_dynamic-slice_fusion.3), channel_id=1, source_target_pairs={{0,2},{2,0},{1,3},{3,1},{4,6},{6,4},{5,7},{7,5},{8,10},{10,8},{9,1... | collective-permute-start | bytes 368648 | tf_op jit(solution)/shard_map/ppermute | solution.py:118
  28.5 7.2 %collective-permute-start.6 = (bf16[2,64,15,128]{3,2,1,0:T(8,128)(2,1)S(1)}, bf16[2,64,15,128]{3,2,1,0:T(8,128)(2,1)S(1)}, u32[]{:S(2)}, u32[]{:S(2)}) collective-permute-start(bf16[2,64,15,128]{3,2,1,0:T(8,128)(2,1)S(1)} %get-tuple-element.55), channel_id=1, source_target_pairs={{1,4},{4,1},{3,6},{6,3},{5,8},{8,5},{7,10},{10,7},{9,12},{12,9},{1... | collective-permute-start | bytes 1474568 | tf_op jit(solution)/shard_map/ppermute | solution.py:139
  29.2 7.9 %collective-permute-start.7 = (bf16[2,64,15,128]{3,2,1,0:T(8,128)(2,1)S(1)}, bf16[2,64,15,128]{3,2,1,0:T(8,128)(2,1)S(1)}, u32[]{:S(2)}, u32[]{:S(2)}) collective-permute-start(bf16[2,64,15,128]{3,2,1,0:T(8,128)(2,1)S(1)} %get-tuple-element.56), channel_id=1, source_target_pairs={{0,1},{1,0},{2,3},{3,2},{4,5},{5,4},{6,7},{7,6},{8,9},{9,8},{10,11... | collective-permute-start | bytes 1474568 | tf_op jit(solution)/shard_map/ppermute | solution.py:23
  38.4 5.0 %collective-permute-start.8 = (bf16[2,15,16,128]{3,1,2,0:T(8,128)(2,1)S(1)}, bf16[2,15,16,128]{3,1,2,0:T(8,128)(2,1)S(1)}, u32[]{:S(2)}, u32[]{:S(2)}) collective-permute-start(bf16[2,15,16,128]{3,1,2,0:T(8,128)(2,1)S(1)} %constant_dynamic-slice_fusion.2), channel_id=1, source_target_pairs={{0,2},{2,0},{1,3},{3,1},{4,6},{6,4},{5,7},{7,5},{8,10},{10,8},{9,1... | collective-permute-start | bytes 368648 | tf_op jit(solution)/shard_map/ppermute | solution.py:118
  44.7 5.6 %collective-permute-start.10 = (bf16[64,15,128]{2,1,0:T(8,128)(2,1)S(1)}, bf16[64,15,128]{2,1,0:T(8,128)(2,1)S(1)}, u32[]{:S(2)}, u32[]{:S(2)}) collective-permute-start(bf16[64,15,128]{2,1,0:T(8,128)(2,1)S(1)} %get-tuple-element.60), channel_id=1, source_target_pairs={{0,1},{1,0},{2,3},{3,2},{4,5},{5,4},{6,7},{7,6},{8,9},{9,8},{10,11... | collective-permute-start | bytes 737288 | tf_op jit(solution)/shard_map/ppermute | solution.py:23
  49.2 1.2 %collective-permute-start.9 = (bf16[64,15,128]{2,1,0:T(8,128)(2,1)S(1)}, bf16[64,15,128]{2,1,0:T(8,128)(2,1)S(1)}, u32[]{:S(2)}, u32[]{:S(2)}) collective-permute-start(bf16[64,15,128]{2,1,0:T(8,128)(2,1)S(1)} %get-tuple-element.59), channel_id=1, source_target_pairs={{1,4},{4,1},{3,6},{6,3},{5,8},{8,5},{7,10},{10,7},{9,12},{12,9},{1... | collective-permute-start | bytes 737288 | tf_op jit(solution)/shard_map/ppermute | solution.py:139
  51.3 5.0 %collective-permute-start.11 = (bf16[2,15,16,128]{3,1,2,0:T(8,128)(2,1)S(1)}, bf16[2,15,16,128]{3,1,2,0:T(8,128)(2,1)S(1)}, u32[]{:S(2)}, u32[]{:S(2)}) collective-permute-start(bf16[2,15,16,128]{3,1,2,0:T(8,128)(2,1)S(1)} %constant_dynamic-slice_fusion.1), channel_id=1, source_target_pairs={{0,2},{2,0},{1,3},{3,1},{4,6},{6,4},{5,7},{7,5},{8,10},{10,8},{9,1... | collective-permute-start | bytes 368648 | tf_op jit(solution)/shard_map/ppermute | solution.py:118
  57.7 12.8 %collective-permute-start.12 = (bf16[2,64,15,128]{3,2,1,0:T(8,128)(2,1)S(1)}, bf16[2,64,15,128]{3,2,1,0:T(8,128)(2,1)S(1)}, u32[]{:S(2)}, u32[]{:S(2)}) collective-permute-start(bf16[2,64,15,128]{3,2,1,0:T(8,128)(2,1)S(1)} %get-tuple-element.51), channel_id=1, source_target_pairs={{1,4},{4,1},{3,6},{6,3},{5,8},{8,5},{7,10},{10,7},{9,12},{12,9},{1... | collective-permute-start | bytes 1474568 | tf_op jit(solution)/shard_map/ppermute | solution.py:139
  58.6 13.4 %collective-permute-start.13 = (bf16[2,64,15,128]{3,2,1,0:T(8,128)(2,1)S(1)}, bf16[2,64,15,128]{3,2,1,0:T(8,128)(2,1)S(1)}, u32[]{:S(2)}, u32[]{:S(2)}) collective-permute-start(bf16[2,64,15,128]{3,2,1,0:T(8,128)(2,1)S(1)} %get-tuple-element.52), channel_id=1, source_target_pairs={{0,1},{1,0},{2,3},{3,2},{4,5},{5,4},{6,7},{7,6},{8,9},{9,8},{10,11... | collective-permute-start | bytes 1474568 | tf_op jit(solution)/shard_map/ppermute | solution.py:23
  73.2 5.0 %collective-permute-start.14 = (bf16[2,15,16,128]{3,1,2,0:T(8,128)(2,1)S(1)}, bf16[2,15,16,128]{3,1,2,0:T(8,128)(2,1)S(1)}, u32[]{:S(2)}, u32[]{:S(2)}) collective-permute-start(bf16[2,15,16,128]{3,1,2,0:T(8,128)(2,1)S(1)} %constant_dynamic-slice_fusion), channel_id=1, source_target_pairs={{0,2},{2,0},{1,3},{3,1},{4,6},{6,4},{5,7},{7,5},{8,10},{10,8},{9,1... | collective-permute-start | bytes 368648 | tf_op jit(solution)/shard_map/ppermute | solution.py:118
  79.4 5.5 %collective-permute-start.15 = (f32[32,16,128]{2,1,0:T(8,128)S(1)}, f32[32,16,128]{2,1,0:T(8,128)S(1)}, u32[]{:S(2)}, u32[]{:S(2)}) collective-permute-start(f32[32,16,128]{2,1,0:T(8,128)S(1)} %dynamic-slice_bitcast_fusion), channel_id=1, source_target_pairs={{0,1},{1,0},{2,3},{3,2},{4,5},{5,4},{6,7},{7,6},{8,9},{9,8},{10,11... | collective-permute-start | bytes 786440 | tf_op jit(solution)/shard_map/ppermute | solution.py:23

commit v19 on v16

--- a/solution.py
+++ b/solution.py
@@ -132,14 +132,10 @@
             route += [(right_core, left_core), (left_core, right_core)]
     first = lax.axis_index("view") % 2 == 0
     width = block.shape[axis]
-    front = lax.slice_in_dim(block, 0, reach, axis=axis)
-    back = lax.slice_in_dim(block, width - reach, width, axis=axis)
-    outward = jnp.where(first, front, back)
-    inward = jnp.where(first, back, front)
-    across = lax.ppermute(outward, ("tile", "view"), route)
-    beside = from_partner(inward, "view", 0)
-    low = jnp.where(first, across, beside)
-    high = jnp.where(first, beside, across)
+    across = lax.ppermute(block, ("tile", "view"), route)
+    beside = from_partner(block, "view", 0)
+    low = lax.slice_in_dim(jnp.where(first, across, beside), width - reach, width, axis=axis)
+    high = lax.slice_in_dim(jnp.where(first, beside, across), 0, reach, axis=axis)
     return low, high
 
 

time: 85.8 us -> 85.8 us (level)
  no operation moved by 1% of the time
where the time goes in v19:
time: 85.8 us; the launch traced here: 85.5 us
  starting transfers between devices  47.6 us (55%)
  waiting for transfers between devices  21.7 us (25%)
  other arithmetic  7.05 us (8%)
  matrix products  5.09 us (6%)
  local copies, waits for them, and re-layouts  3.49 us (4%)
    ppermute x6, starting transfers between devices, from_partner(): return lax.ppermute(block, axis, route)  37.8 us
    ppermute x4, waiting for transfers between devices, z_rims(): got = lax.ppermute(payload, 'view', route)  13.9 us
    ppermute x6, waiting for transfers between devices, from_partner(): return lax.ppermute(block, axis, route)  7.8 us
    ppermute x4, starting transfers between devices, z_rims(): got = lax.ppermute(payload, 'view', route)  6.24 us
    ppermute x4, starting transfers between devices, x_rims(): across = lax.ppermute(block, ('tile', 'view'), route)  2.92 us
  transfers between devices with their start and end apart: 15, of which 10 were waited for; matrix products, arithmetic and copies ran while one was open for 3% of the time, Pallas kernels for 0%

profile of v19, /device:TPU:0, one launch (start us, length us, event | category | flops | bytes accessed | tf_op | source)
XLA Modules:
  0.0 85.5 jit_solution(9888724947801843726)
XLA Ops:
  0.0 0.9 %fusion.71 = (s32[4]{0:T(128)S(1)}, s32[4]{0:T(128)S(1)}, s32[4]{0:T(128)S(1)}, s32[4]{0:T(128)S(1)}) fusion(s32[1,32]{1,0:T(1,128)} %param.5, s32[]{:T(128)S(6)} %select_n.305, s32[]{:T(128)S(6)} %select_n.306, s32[]{:T(128)S(6)} %select_n.308, s32[]{:T(128)S(6)} %select_n.307), kind=kLoop, calls=%fused_computation.173 | loop fusion | bytes 144 | tf_op jit(solution)/shard_map/dynamic_slice | solution.py:160
  1.0 0.8 gather_fusion
  3.0 1.5 %collective-permute-done = bf16[2,64,16,128]{3,2,1,0:T(8,128)(2,1)S(1)} collective-permute-done((bf16[2,64,16,128]{3,2,1,0:T(8,128)(2,1)S(1)}, bf16[2,64,16,128]{3,2,1,0:T(8,128)(2,1)S(1)}, u32[]{:S(2)}, u32[]{:S(2)}) %collective-permute-start) | collective-permute-done | bytes 524320 | tf_op jit(solution)/shard_map/ppermute | solution.py:23
  6.8 1.0 %select_reduce_fusion.1 = (bf16[128,128]{1,0:T(8,128)(2,1)S(1)}, bf16[128,128]{1,0:T(8,128)(2,1)S(1)}, bf16[128,128]{1,0:T(8,128)(2,1)S(1)}, bf16[128,128]{1,0:T(8,128)(2,1)S(1)}) fusion(f32[31]{0:T(128)S(1)} %get-tuple-element.66, s32[128,128]{1,0:T(8,128)S(1)} %subtract_add_fusion, f32[31]{0:T(128)S(1)} %get-tuple-element.67, f32[31]{0:T(128)S(1)} %get-tuple-element.81, ...), kind=kLoop, calls=%fused_computation.2 | loop fusion | flops 4505600 | bytes 197104 | tf_op jit(solution)/shard_map/reduce_sum | solution.py:45
  8.7 11.7 %collective-permute-start.3 = (bf16[64,16,128]{2,1,0:T(8,128)(2,1)S(1)}, bf16[64,16,128]{2,1,0:T(8,128)(2,1)S(1)}, u32[]{:S(2)}, u32[]{:S(2)}) collective-permute-start(bf16[64,16,128]{2,1,0:T(8,128)(2,1)S(1)} %convert_bitcast_fusion.1), channel_id=1, source_target_pairs={{0,1},{1,0},{2,3},{3,2},{4,5},{5,4},{6,7},{7,6},{8,9},{9,8},{10,11... | collective-permute-start | bytes 786440 | tf_op jit(solution)/shard_map/ppermute | solution.py:23
  20.5 1.0 %collective-permute-done.3 = bf16[64,16,128]{2,1,0:T(8,128)(2,1)S(1)} collective-permute-done((bf16[64,16,128]{2,1,0:T(8,128)(2,1)S(1)}, bf16[64,16,128]{2,1,0:T(8,128)(2,1)S(1)}, u32[]{:S(2)}, u32[]{:S(2)}) %collective-permute-start.3) | collective-permute-done | bytes 262176 | tf_op jit(solution)/shard_map/ppermute | solution.py:23
  22.6 1.6 %collective-permute-start.4 = (bf16[2,15,16,128]{3,1,2,0:T(8,128)(2,1)S(1)}, bf16[2,15,16,128]{3,1,2,0:T(8,128)(2,1)S(1)}, u32[]{:S(2)}, u32[]{:S(2)}) collective-permute-start(bf16[2,15,16,128]{3,1,2,0:T(8,128)(2,1)S(1)} %constant_dynamic-slice_fusion.3), channel_id=1, source_target_pairs={{0,2},{2,0},{1,3},{3,1},{4,6},{6,4},{5,7},{7,5},{8,10},{10,8},{9,1... | collective-permute-start | bytes 368648 | tf_op jit(solution)/shard_map/ppermute | solution.py:118
  24.2 3.5 %collective-permute-done.4 = bf16[2,15,16,128]{3,1,2,0:T(8,128)(2,1)S(1)} collective-permute-done((bf16[2,15,16,128]{3,1,2,0:T(8,128)(2,1)S(1)}, bf16[2,15,16,128]{3,1,2,0:T(8,128)(2,1)S(1)}, u32[]{:S(2)}, u32[]{:S(2)}) %collective-permute-start.4) | collective-permute-done | bytes 122912 | tf_op jit(solution)/shard_map/ppermute | solution.py:118
  29.5 6.4 %collective-permute-start.6 = (bf16[2,64,16,128]{3,2,1,0:T(8,128)(2,1)S(1)}, bf16[2,64,16,128]{3,2,1,0:T(8,128)(2,1)S(1)}, u32[]{:S(2)}, u32[]{:S(2)}) collective-permute-start(bf16[2,64,16,128]{3,2,1,0:T(8,128)(2,1)S(1)} %fusion.21), channel_id=1, source_target_pairs={{0,1},{1,0},{2,3},{3,2},{4,5},{5,4},{6,7},{7,6},{8,9},{9,8},{10,11... | collective-permute-start | bytes 1572872 | tf_op jit(solution)/shard_map/ppermute | solution.py:23
  36.0 1.4 %collective-permute-done.6 = bf16[2,64,16,128]{3,2,1,0:T(8,128)(2,1)S(1)} collective-permute-done((bf16[2,64,16,128]{3,2,1,0:T(8,128)(2,1)S(1)}, bf16[2,64,16,128]{3,2,1,0:T(8,128)(2,1)S(1)}, u32[]{:S(2)}, u32[]{:S(2)}) %collective-permute-start.6) | collective-permute-done | bytes 524320 | tf_op jit(solution)/shard_map/ppermute | solution.py:23
  38.8 1.6 %collective-permute-start.7 = (bf16[2,15,16,128]{3,1,2,0:T(8,128)(2,1)S(1)}, bf16[2,15,16,128]{3,1,2,0:T(8,128)(2,1)S(1)}, u32[]{:S(2)}, u32[]{:S(2)}) collective-permute-start(bf16[2,15,16,128]{3,1,2,0:T(8,128)(2,1)S(1)} %constant_dynamic-slice_fusion.2), channel_id=1, source_target_pairs={{0,2},{2,0},{1,3},{3,1},{4,6},{6,4},{5,7},{7,5},{8,10},{10,8},{9,1... | collective-permute-start | bytes 368648 | tf_op jit(solution)/shard_map/ppermute | solution.py:118
  40.4 3.5 %collective-permute-done.7 = bf16[2,15,16,128]{3,1,2,0:T(8,128)(2,1)S(1)} collective-permute-done((bf16[2,15,16,128]{3,1,2,0:T(8,128)(2,1)S(1)}, bf16[2,15,16,128]{3,1,2,0:T(8,128)(2,1)S(1)}, u32[]{:S(2)}, u32[]{:S(2)}) %collective-permute-start.7) | collective-permute-done | bytes 122912 | tf_op jit(solution)/shard_map/ppermute | solution.py:118
  45.7 8.8 %collective-permute-start.9 = (bf16[64,16,128]{2,1,0:T(8,128)(2,1)S(1)}, bf16[64,16,128]{2,1,0:T(8,128)(2,1)S(1)}, u32[]{:S(2)}, u32[]{:S(2)}) collective-permute-start(bf16[64,16,128]{2,1,0:T(8,128)(2,1)S(1)} %get-tuple-element.33), channel_id=1, source_target_pairs={{0,1},{1,0},{2,3},{3,2},{4,5},{5,4},{6,7},{7,6},{8,9},{9,8},{10,11... | collective-permute-start | bytes 786440 | tf_op jit(solution)/shard_map/ppermute | solution.py:23
  54.6 1.2 %collective-permute-done.9 = bf16[64,16,128]{2,1,0:T(8,128)(2,1)S(1)} collective-permute-done((bf16[64,16,128]{2,1,0:T(8,128)(2,1)S(1)}, bf16[64,16,128]{2,1,0:T(8,128)(2,1)S(1)}, u32[]{:S(2)}, u32[]{:S(2)}) %collective-permute-start.9) | collective-permute-done | bytes 262176 | tf_op jit(solution)/shard_map/ppermute | solution.py:23
  56.8 1.6 %collective-permute-start.10 = (bf16[2,15,16,128]{3,1,2,0:T(8,128)(2,1)S(1)}, bf16[2,15,16,128]{3,1,2,0:T(8,128)(2,1)S(1)}, u32[]{:S(2)}, u32[]{:S(2)}) collective-permute-start(bf16[2,15,16,128]{3,1,2,0:T(8,128)(2,1)S(1)} %constant_dynamic-slice_fusion.1), channel_id=1, source_target_pairs={{0,2},{2,0},{1,3},{3,1},{4,6},{6,4},{5,7},{7,5},{8,10},{10,8},{9,1... | collective-permute-start | bytes 368648 | tf_op jit(solution)/shard_map/ppermute | solution.py:118
  58.4 3.5 %collective-permute-done.10 = bf16[2,15,16,128]{3,1,2,0:T(8,128)(2,1)S(1)} collective-permute-done((bf16[2,15,16,128]{3,1,2,0:T(8,128)(2,1)S(1)}, bf16[2,15,16,128]{3,1,2,0:T(8,128)(2,1)S(1)}, u32[]{:S(2)}, u32[]{:S(2)}) %collective-permute-start.10) | collective-permute-done | bytes 122912 | tf_op jit(solution)/shard_map/ppermute | solution.py:118
  63.0 0.9 %collective-permute-start.11 = (bf16[2,64,16,128]{3,2,1,0:T(8,128)(2,1)S(1)}, bf16[2,64,16,128]{3,2,1,0:T(8,128)(2,1)S(1)}, u32[]{:S(2)}, u32[]{:S(2)}) collective-permute-start(bf16[2,64,16,128]{3,2,1,0:T(8,128)(2,1)S(1)} %fusion.20), channel_id=1, source_target_pairs={{1,4},{4,1},{3,6},{6,3},{5,8},{8,5},{7,10},{10,7},{9,12},{12,9},{1... | collective-permute-start | bytes 1572872 | tf_op jit(solution)/shard_map/ppermute | solution.py:135
  63.9 6.1 %collective-permute-start.12 = (bf16[2,64,16,128]{3,2,1,0:T(8,128)(2,1)S(1)}, bf16[2,64,16,128]{3,2,1,0:T(8,128)(2,1)S(1)}, u32[]{:S(2)}, u32[]{:S(2)}) collective-permute-start(bf16[2,64,16,128]{3,2,1,0:T(8,128)(2,1)S(1)} %fusion.20), channel_id=1, source_target_pairs={{0,1},{1,0},{2,3},{3,2},{4,5},{5,4},{6,7},{7,6},{8,9},{9,8},{10,11... | collective-permute-start | bytes 1572872 | tf_op jit(solution)/shard_map/ppermute | solution.py:23
  70.0 1.5 %collective-permute-done.12 = bf16[2,64,16,128]{3,2,1,0:T(8,128)(2,1)S(1)} collective-permute-done((bf16[2,64,16,128]{3,2,1,0:T(8,128)(2,1)S(1)}, bf16[2,64,16,128]{3,2,1,0:T(8,128)(2,1)S(1)}, u32[]{:S(2)}, u32[]{:S(2)}) %collective-permute-start.12) | collective-permute-done | bytes 524320 | tf_op jit(solution)/shard_map/ppermute | solution.py:23
  72.9 1.6 %collective-permute-start.13 = (bf16[2,15,16,128]{3,1,2,0:T(8,128)(2,1)S(1)}, bf16[2,15,16,128]{3,1,2,0:T(8,128)(2,1)S(1)}, u32[]{:S(2)}, u32[]{:S(2)}) collective-permute-start(bf16[2,15,16,128]{3,1,2,0:T(8,128)(2,1)S(1)} %constant_dynamic-slice_fusion), channel_id=1, source_target_pairs={{0,2},{2,0},{1,3},{3,1},{4,6},{6,4},{5,7},{7,5},{8,10},{10,8},{9,1... | collective-permute-start | bytes 368648 | tf_op jit(solution)/shard_map/ppermute | solution.py:118
  74.4 3.5 %collective-permute-done.13 = bf16[2,15,16,128]{3,1,2,0:T(8,128)(2,1)S(1)} collective-permute-done((bf16[2,15,16,128]{3,1,2,0:T(8,128)(2,1)S(1)}, bf16[2,15,16,128]{3,1,2,0:T(8,128)(2,1)S(1)}, u32[]{:S(2)}, u32[]{:S(2)}) %collective-permute-start.13) | collective-permute-done | bytes 122912 | tf_op jit(solution)/shard_map/ppermute | solution.py:118
  79.1 4.3 %collective-permute-start.14 = (f32[32,16,128]{2,1,0:T(8,128)S(1)}, f32[32,16,128]{2,1,0:T(8,128)S(1)}, u32[]{:S(2)}, u32[]{:S(2)}) collective-permute-start(f32[32,16,128]{2,1,0:T(8,128)S(1)} %dynamic-slice_bitcast_fusion), channel_id=1, source_target_pairs={{0,1},{1,0},{2,3},{3,2},{4,5},{5,4},{6,7},{7,6},{8,9},{9,8},{10,11... | collective-permute-start | bytes 786440 | tf_op jit(solution)/shard_map/ppermute | solution.py:23
  83.4 1.2 %collective-permute-done.14 = f32[32,16,128]{2,1,0:T(8,128)S(1)} collective-permute-done((f32[32,16,128]{2,1,0:T(8,128)S(1)}, f32[32,16,128]{2,1,0:T(8,128)S(1)}, u32[]{:S(2)}, u32[]{:S(2)}) %collective-permute-start.14) | collective-permute-done | bytes 262176 | tf_op jit(solution)/shard_map/ppermute | solution.py:23
  84.6 0.9 pad_maximum_fusion.1
  (90 shorter events, 15.4 us)
Async XLA Ops:
  0.0 1.8 %copy-start = (bf16[64,32,128]{2,1,0:T(8,128)(2,1)S(1)}, bf16[64,32,128]{2,1,0:T(8,128)(2,1)}, u32[]{:S(2)}) copy-start(bf16[64,32,128]{2,1,0:T(8,128)(2,1)} %param.3) | copy-start | bytes 1572868
  2.5 2.1 %collective-permute-start = (bf16[2,64,16,128]{3,2,1,0:T(8,128)(2,1)S(1)}, bf16[2,64,16,128]{3,2,1,0:T(8,128)(2,1)S(1)}, u32[]{:S(2)}, u32[]{:S(2)}) collective-permute-start(bf16[2,64,16,128]{3,2,1,0:T(8,128)(2,1)S(1)} %pad_maximum_fusion), channel_id=1, source_target_pairs={{0,1},{1,0},{2,3},{3,2},{4,5},{5,4},{6,7},{7,6},{8,9},{9,8},{10,11... | collective-permute-start | bytes 1572872 | tf_op jit(solution)/shard_map/ppermute | solution.py:23
  3.0 2.3 %copy-start.1 = (f32[2,3,31]{2,0,1:T(2,128)S(1)}, f32[2,3,31]{2,0,1:T(2,128)}, u32[]{:S(2)}) copy-start(f32[2,3,31]{2,0,1:T(2,128)} %param.4) | copy-start | bytes 2236
  4.7 3.2 %collective-permute-start.1 = (bf16[2,64,16,128]{3,2,1,0:T(8,128)(2,1)S(1)}, bf16[2,64,16,128]{3,2,1,0:T(8,128)(2,1)S(1)}, u32[]{:S(2)}, u32[]{:S(2)}) collective-permute-start(bf16[2,64,16,128]{3,2,1,0:T(8,128)(2,1)S(1)} %maximum_select_fusion.1), channel_id=1, source_target_pairs={{1,4},{4,1},{3,6},{6,3},{5,8},{8,5},{7,10},{10,7},{9,12},{12,9},{1... | collective-permute-start | bytes 1572872 | tf_op jit(solution)/shard_map/ppermute | solution.py:187
  8.0 12.5 %collective-permute-start.2 = (bf16[64,16,128]{2,1,0:T(8,128)(2,1)S(1)}, bf16[64,16,128]{2,1,0:T(8,128)(2,1)S(1)}, u32[]{:S(2)}, u32[]{:S(2)}) collective-permute-start(bf16[64,16,128]{2,1,0:T(8,128)(2,1)S(1)} %convert_bitcast_fusion.1), channel_id=1, source_target_pairs={{1,4},{4,1},{3,6},{6,3},{5,8},{8,5},{7,10},{10,7},{9,12},{12,9},{1... | collective-permute-start | bytes 786440 | tf_op jit(solution)/shard_map/ppermute | solution.py:135
  8.7 12.8 %collective-permute-start.3 = (bf16[64,16,128]{2,1,0:T(8,128)(2,1)S(1)}, bf16[64,16,128]{2,1,0:T(8,128)(2,1)S(1)}, u32[]{:S(2)}, u32[]{:S(2)}) collective-permute-start(bf16[64,16,128]{2,1,0:T(8,128)(2,1)S(1)} %convert_bitcast_fusion.1), channel_id=1, source_target_pairs={{0,1},{1,0},{2,3},{3,2},{4,5},{5,4},{6,7},{7,6},{8,9},{9,8},{10,11... | collective-permute-start | bytes 786440 | tf_op jit(solution)/shard_map/ppermute | solution.py:23
  22.6 5.0 %collective-permute-start.4 = (bf16[2,15,16,128]{3,1,2,0:T(8,128)(2,1)S(1)}, bf16[2,15,16,128]{3,1,2,0:T(8,128)(2,1)S(1)}, u32[]{:S(2)}, u32[]{:S(2)}) collective-permute-start(bf16[2,15,16,128]{3,1,2,0:T(8,128)(2,1)S(1)} %constant_dynamic-slice_fusion.3), channel_id=1, source_target_pairs={{0,2},{2,0},{1,3},{3,1},{4,6},{6,4},{5,7},{7,5},{8,10},{10,8},{9,1... | collective-permute-start | bytes 368648 | tf_op jit(solution)/shard_map/ppermute | solution.py:118
  28.8 7.2 %collective-permute-start.5 = (bf16[2,64,16,128]{3,2,1,0:T(8,128)(2,1)S(1)}, bf16[2,64,16,128]{3,2,1,0:T(8,128)(2,1)S(1)}, u32[]{:S(2)}, u32[]{:S(2)}) collective-permute-start(bf16[2,64,16,128]{3,2,1,0:T(8,128)(2,1)S(1)} %fusion.21), channel_id=1, source_target_pairs={{1,4},{4,1},{3,6},{6,3},{5,8},{8,5},{7,10},{10,7},{9,12},{12,9},{1... | collective-permute-start | bytes 1572872 | tf_op jit(solution)/shard_map/ppermute | solution.py:135
  29.5 7.9 %collective-permute-start.6 = (bf16[2,64,16,128]{3,2,1,0:T(8,128)(2,1)S(1)}, bf16[2,64,16,128]{3,2,1,0:T(8,128)(2,1)S(1)}, u32[]{:S(2)}, u32[]{:S(2)}) collective-permute-start(bf16[2,64,16,128]{3,2,1,0:T(8,128)(2,1)S(1)} %fusion.21), channel_id=1, source_target_pairs={{0,1},{1,0},{2,3},{3,2},{4,5},{5,4},{6,7},{7,6},{8,9},{9,8},{10,11... | collective-permute-start | bytes 1572872 | tf_op jit(solution)/shard_map/ppermute | solution.py:23
  38.8 5.0 %collective-permute-start.7 = (bf16[2,15,16,128]{3,1,2,0:T(8,128)(2,1)S(1)}, bf16[2,15,16,128]{3,1,2,0:T(8,128)(2,1)S(1)}, u32[]{:S(2)}, u32[]{:S(2)}) collective-permute-start(bf16[2,15,16,128]{3,1,2,0:T(8,128)(2,1)S(1)} %constant_dynamic-slice_fusion.2), channel_id=1, source_target_pairs={{0,2},{2,0},{1,3},{3,1},{4,6},{6,4},{5,7},{7,5},{8,10},{10,8},{9,1... | collective-permute-start | bytes 368648 | tf_op jit(solution)/shard_map/ppermute | solution.py:118
  45.1 9.5 %collective-permute-start.8 = (bf16[64,16,128]{2,1,0:T(8,128)(2,1)S(1)}, bf16[64,16,128]{2,1,0:T(8,128)(2,1)S(1)}, u32[]{:S(2)}, u32[]{:S(2)}) collective-permute-start(bf16[64,16,128]{2,1,0:T(8,128)(2,1)S(1)} %get-tuple-element.33), channel_id=1, source_target_pairs={{1,4},{4,1},{3,6},{6,3},{5,8},{8,5},{7,10},{10,7},{9,12},{12,9},{1... | collective-permute-start | bytes 786440 | tf_op jit(solution)/shard_map/ppermute | solution.py:135
  45.7 10.0 %collective-permute-start.9 = (bf16[64,16,128]{2,1,0:T(8,128)(2,1)S(1)}, bf16[64,16,128]{2,1,0:T(8,128)(2,1)S(1)}, u32[]{:S(2)}, u32[]{:S(2)}) collective-permute-start(bf16[64,16,128]{2,1,0:T(8,128)(2,1)S(1)} %get-tuple-element.33), channel_id=1, source_target_pairs={{0,1},{1,0},{2,3},{3,2},{4,5},{5,4},{6,7},{7,6},{8,9},{9,8},{10,11... | collective-permute-start | bytes 786440 | tf_op jit(solution)/shard_map/ppermute | solution.py:23
  56.8 5.0 %collective-permute-start.10 = (bf16[2,15,16,128]{3,1,2,0:T(8,128)(2,1)S(1)}, bf16[2,15,16,128]{3,1,2,0:T(8,128)(2,1)S(1)}, u32[]{:S(2)}, u32[]{:S(2)}) collective-permute-start(bf16[2,15,16,128]{3,1,2,0:T(8,128)(2,1)S(1)} %constant_dynamic-slice_fusion.1), channel_id=1, source_target_pairs={{0,2},{2,0},{1,3},{3,1},{4,6},{6,4},{5,7},{7,5},{8,10},{10,8},{9,1... | collective-permute-start | bytes 368648 | tf_op jit(solution)/shard_map/ppermute | solution.py:118
  63.0 7.0 %collective-permute-start.11 = (bf16[2,64,16,128]{3,2,1,0:T(8,128)(2,1)S(1)}, bf16[2,64,16,128]{3,2,1,0:T(8,128)(2,1)S(1)}, u32[]{:S(2)}, u32[]{:S(2)}) collective-permute-start(bf16[2,64,16,128]{3,2,1,0:T(8,128)(2,1)S(1)} %fusion.20), channel_id=1, source_target_pairs={{1,4},{4,1},{3,6},{6,3},{5,8},{8,5},{7,10},{10,7},{9,12},{12,9},{1... | collective-permute-start | bytes 1572872 | tf_op jit(solution)/shard_map/ppermute | solution.py:135
  63.9 7.6 %collective-permute-start.12 = (bf16[2,64,16,128]{3,2,1,0:T(8,128)(2,1)S(1)}, bf16[2,64,16,128]{3,2,1,0:T(8,128)(2,1)S(1)}, u32[]{:S(2)}, u32[]{:S(2)}) collective-permute-start(bf16[2,64,16,128]{3,2,1,0:T(8,128)(2,1)S(1)} %fusion.20), channel_id=1, source_target_pairs={{0,1},{1,0},{2,3},{3,2},{4,5},{5,4},{6,7},{7,6},{8,9},{9,8},{10,11... | collective-permute-start | bytes 1572872 | tf_op jit(solution)/shard_map/ppermute | solution.py:23
  72.9 5.0 %collective-permute-start.13 = (bf16[2,15,16,128]{3,1,2,0:T(8,128)(2,1)S(1)}, bf16[2,15,16,128]{3,1,2,0:T(8,128)(2,1)S(1)}, u32[]{:S(2)}, u32[]{:S(2)}) collective-permute-start(bf16[2,15,16,128]{3,1,2,0:T(8,128)(2,1)S(1)} %constant_dynamic-slice_fusion), channel_id=1, source_target_pairs={{0,2},{2,0},{1,3},{3,1},{4,6},{6,4},{5,7},{7,5},{8,10},{10,8},{9,1... | collective-permute-start | bytes 368648 | tf_op jit(solution)/shard_map/ppermute | solution.py:118
  79.1 5.5 %collective-permute-start.14 = (f32[32,16,128]{2,1,0:T(8,128)S(1)}, f32[32,16,128]{2,1,0:T(8,128)S(1)}, u32[]{:S(2)}, u32[]{:S(2)}) collective-permute-start(f32[32,16,128]{2,1,0:T(8,128)S(1)} %dynamic-slice_bitcast_fusion), channel_id=1, source_target_pairs={{0,1},{1,0},{2,3},{3,2},{4,5},{5,4},{6,7},{7,6},{8,9},{9,8},{10,11... | collective-permute-start | bytes 786440 | tf_op jit(solution)/shard_map/ppermute | solution.py:23

commit v20 on v16

--- a/solution.py
+++ b/solution.py
@@ -136,7 +136,10 @@
     back = lax.slice_in_dim(block, width - reach, width, axis=axis)
     outward = jnp.where(first, front, back)
     inward = jnp.where(first, back, front)
-    across = lax.ppermute(outward, ("tile", "view"), route)
+    if outward.ndim == 4:
+        across = jnp.stack([lax.ppermute(outward[v], ("tile", "view"), route) for v in range(outward.shape[0])])
+    else:
+        across = lax.ppermute(outward, ("tile", "view"), route)
     beside = from_partner(inward, "view", 0)
     low = jnp.where(first, across, beside)
     high = jnp.where(first, beside, across)
@@ -188,7 +191,7 @@
             route += [(right_core, left_core), (left_core, right_core)]
     outgoing = jnp.where(first, jnp.stack([cross_keep, got[1]]), jnp.stack([got[1], cross_keep]))
     outgoing, psf_taps = lax.optimization_barrier((outgoing, psf_taps))
-    incoming = lax.ppermute(outgoing, ("tile", "view"), route)
+    incoming = jnp.stack([lax.ppermute(outgoing[v], ("tile", "view"), route) for v in range(outgoing.shape[0])])
     own_parts = jnp.where(first, jnp.stack([own_keep, got[0]]), jnp.stack([got[0], own_keep]))
     views_measured = own_parts + incoming
     observed = views_measured.astype(jnp.float32)

time: 85.8 us -> 88.9 us (1.036)
  starting transfers between devices: 47.6 us -> 52.8 us
  waiting for transfers between devices: 21.7 us -> 18.8 us
    ppermute x1 -> x6, starting transfers between devices: 0.69 us -> 4.24 us  [the longest x4 2.89 us: x_rims(): lax.ppermute(outward[v], ('tile', 'view'), route)]
    ppermute x6, starting transfers between devices: 37.8 us -> 41 us  [from_partner(): return lax.ppermute(block, axis, route)]
    ppermute x6, waiting for transfers between devices: 7.8 us -> 4.87 us  [from_partner(): return lax.ppermute(block, axis, route)]
    ppermute x4 -> x2, starting transfers between devices: 2.92 us -> 1.35 us  [x_rims(): across = lax.ppermute(outward, ('tile', 'view'), route)]
  transfers between devices with their start and end apart: 15 -> 18, of which waited for: 10 -> 8; matrix products, arithmetic and copies ran while one was open for 3% -> 3% of each run, Pallas kernels for 0% -> 0%
where the time goes in v20:
time: 88.9 us; the launch traced here: 88.1 us
  starting transfers between devices  52.8 us (59%)
  waiting for transfers between devices  18.8 us (21%)
  other arithmetic  7.14 us (8%)
  matrix products  5.09 us (6%)
  local copies, waits for them, and re-layouts  3.59 us (4%)
    ppermute x6, starting transfers between devices, from_partner(): return lax.ppermute(block, axis, route)  41 us
    ppermute x4, waiting for transfers between devices, z_rims(): got = lax.ppermute(payload, 'view', route)  13.9 us
    ppermute x4, starting transfers between devices, z_rims(): got = lax.ppermute(payload, 'view', route)  6.22 us
    ppermute x6, waiting for transfers between devices, from_partner(): return lax.ppermute(block, axis, route)  4.87 us
    ppermute x4, starting transfers between devices, x_rims(): lax.ppermute(outward[v], ('tile', 'view'), route)  2.89 us
  transfers between devices with their start and end apart: 18, of which 8 were waited for; matrix products, arithmetic and copies ran while one was open for 3% of the time, Pallas kernels for 0%

profile of v20, /device:TPU:0, one launch (start us, length us, event | category | flops | bytes accessed | tf_op | source)
XLA Modules:
  0.0 88.1 jit_solution(55142148009491118)
XLA Ops:
  0.0 0.9 %fusion.71 = (s32[4]{0:T(128)S(1)}, s32[4]{0:T(128)S(1)}, s32[4]{0:T(128)S(1)}, s32[4]{0:T(128)S(1)}) fusion(s32[1,32]{1,0:T(1,128)} %param.5, s32[]{:T(128)S(6)} %select_n.343, s32[]{:T(128)S(6)} %select_n.344, s32[]{:T(128)S(6)} %select_n.346, s32[]{:T(128)S(6)} %select_n.345), kind=kLoop, calls=%fused_computation.189 | loop fusion | bytes 144 | tf_op jit(solution)/shard_map/dynamic_slice | solution.py:167
  1.0 0.8 gather_fusion
  3.0 1.5 %collective-permute-done = bf16[2,64,16,128]{3,2,1,0:T(8,128)(2,1)S(1)} collective-permute-done((bf16[2,64,16,128]{3,2,1,0:T(8,128)(2,1)S(1)}, bf16[2,64,16,128]{3,2,1,0:T(8,128)(2,1)S(1)}, u32[]{:S(2)}, u32[]{:S(2)}) %collective-permute-start) | collective-permute-done | bytes 524320 | tf_op jit(solution)/shard_map/ppermute | solution.py:23
  7.6 1.0 %select_reduce_fusion.1 = (bf16[128,128]{1,0:T(8,128)(2,1)S(1)}, bf16[128,128]{1,0:T(8,128)(2,1)S(1)}, bf16[128,128]{1,0:T(8,128)(2,1)S(1)}, bf16[128,128]{1,0:T(8,128)(2,1)S(1)}) fusion(f32[31]{0:T(128)S(1)} %get-tuple-element.80, s32[128,128]{1,0:T(8,128)S(1)} %subtract_add_fusion, f32[31]{0:T(128)S(1)} %get-tuple-element.81, f32[31]{0:T(128)S(1)} %get-tuple-element.95, ...), kind=kLoop, calls=%fused_computation.2 | loop fusion | flops 4505600 | bytes 197104 | tf_op jit(solution)/shard_map/reduce_sum | solution.py:45
  9.6 11.0 %collective-permute-start.4 = (bf16[64,15,128]{2,1,0:T(8,128)(2,1)S(1)}, bf16[64,15,128]{2,1,0:T(8,128)(2,1)S(1)}, u32[]{:S(2)}, u32[]{:S(2)}) collective-permute-start(bf16[64,15,128]{2,1,0:T(8,128)(2,1)S(1)} %get-tuple-element.68), channel_id=1, source_target_pairs={{0,1},{1,0},{2,3},{3,2},{4,5},{5,4},{6,7},{7,6},{8,9},{9,8},{10,11... | collective-permute-start | bytes 737288 | tf_op jit(solution)/shard_map/ppermute | solution.py:23
  20.7 1.0 %collective-permute-done.4 = bf16[64,15,128]{2,1,0:T(8,128)(2,1)S(1)} collective-permute-done((bf16[64,15,128]{2,1,0:T(8,128)(2,1)S(1)}, bf16[64,15,128]{2,1,0:T(8,128)(2,1)S(1)}, u32[]{:S(2)}, u32[]{:S(2)}) %collective-permute-start.4) | collective-permute-done | bytes 245792 | tf_op jit(solution)/shard_map/ppermute | solution.py:23
  22.7 1.6 %collective-permute-start.5 = (bf16[2,15,16,128]{3,1,2,0:T(8,128)(2,1)S(1)}, bf16[2,15,16,128]{3,1,2,0:T(8,128)(2,1)S(1)}, u32[]{:S(2)}, u32[]{:S(2)}) collective-permute-start(bf16[2,15,16,128]{3,1,2,0:T(8,128)(2,1)S(1)} %constant_dynamic-slice_fusion.3), channel_id=1, source_target_pairs={{0,2},{2,0},{1,3},{3,1},{4,6},{6,4},{5,7},{7,5},{8,10},{10,8},{9,1... | collective-permute-start | bytes 368648 | tf_op jit(solution)/shard_map/ppermute | solution.py:118
  24.2 3.5 %collective-permute-done.5 = bf16[2,15,16,128]{3,1,2,0:T(8,128)(2,1)S(1)} collective-permute-done((bf16[2,15,16,128]{3,1,2,0:T(8,128)(2,1)S(1)}, bf16[2,15,16,128]{3,1,2,0:T(8,128)(2,1)S(1)}, u32[]{:S(2)}, u32[]{:S(2)}) %collective-permute-start.5) | collective-permute-done | bytes 122912 | tf_op jit(solution)/shard_map/ppermute | solution.py:118
  28.1 0.8 fusion.21
  29.1 2.6 %collective-permute-start.8 = (bf16[2,64,15,128]{3,2,1,0:T(8,128)(2,1)S(1)}, bf16[2,64,15,128]{3,2,1,0:T(8,128)(2,1)S(1)}, u32[]{:S(2)}, u32[]{:S(2)}) collective-permute-start(bf16[2,64,15,128]{3,2,1,0:T(8,128)(2,1)S(1)} %get-tuple-element.58), channel_id=1, source_target_pairs={{0,1},{1,0},{2,3},{3,2},{4,5},{5,4},{6,7},{7,6},{8,9},{9,8},{10,11... | collective-permute-start | bytes 1474568 | tf_op jit(solution)/shard_map/ppermute | solution.py:23
  34.4 1.6 %collective-permute-start.9 = (bf16[2,15,16,128]{3,1,2,0:T(8,128)(2,1)S(1)}, bf16[2,15,16,128]{3,1,2,0:T(8,128)(2,1)S(1)}, u32[]{:S(2)}, u32[]{:S(2)}) collective-permute-start(bf16[2,15,16,128]{3,1,2,0:T(8,128)(2,1)S(1)} %constant_dynamic-slice_fusion.2), channel_id=1, source_target_pairs={{0,2},{2,0},{1,3},{3,1},{4,6},{6,4},{5,7},{7,5},{8,10},{10,8},{9,1... | collective-permute-start | bytes 368648 | tf_op jit(solution)/shard_map/ppermute | solution.py:118
  36.0 3.5 %collective-permute-done.9 = bf16[2,15,16,128]{3,1,2,0:T(8,128)(2,1)S(1)} collective-permute-done((bf16[2,15,16,128]{3,1,2,0:T(8,128)(2,1)S(1)}, bf16[2,15,16,128]{3,1,2,0:T(8,128)(2,1)S(1)}, u32[]{:S(2)}, u32[]{:S(2)}) %collective-permute-start.9) | collective-permute-done | bytes 122912 | tf_op jit(solution)/shard_map/ppermute | solution.py:118
  41.5 14.8 %collective-permute-start.11 = (bf16[64,15,128]{2,1,0:T(8,128)(2,1)S(1)}, bf16[64,15,128]{2,1,0:T(8,128)(2,1)S(1)}, u32[]{:S(2)}, u32[]{:S(2)}) collective-permute-start(bf16[64,15,128]{2,1,0:T(8,128)(2,1)S(1)} %get-tuple-element.66), channel_id=1, source_target_pairs={{0,1},{1,0},{2,3},{3,2},{4,5},{5,4},{6,7},{7,6},{8,9},{9,8},{10,11... | collective-permute-start | bytes 737288 | tf_op jit(solution)/shard_map/ppermute | solution.py:23
  56.3 1.2 %collective-permute-done.11 = bf16[64,15,128]{2,1,0:T(8,128)(2,1)S(1)} collective-permute-done((bf16[64,15,128]{2,1,0:T(8,128)(2,1)S(1)}, bf16[64,15,128]{2,1,0:T(8,128)(2,1)S(1)}, u32[]{:S(2)}, u32[]{:S(2)}) %collective-permute-start.11) | collective-permute-done | bytes 245792 | tf_op jit(solution)/shard_map/ppermute | solution.py:23
  58.4 1.6 %collective-permute-start.12 = (bf16[2,15,16,128]{3,1,2,0:T(8,128)(2,1)S(1)}, bf16[2,15,16,128]{3,1,2,0:T(8,128)(2,1)S(1)}, u32[]{:S(2)}, u32[]{:S(2)}) collective-permute-start(bf16[2,15,16,128]{3,1,2,0:T(8,128)(2,1)S(1)} %constant_dynamic-slice_fusion.1), channel_id=1, source_target_pairs={{0,2},{2,0},{1,3},{3,1},{4,6},{6,4},{5,7},{7,5},{8,10},{10,8},{9,1... | collective-permute-start | bytes 368648 | tf_op jit(solution)/shard_map/ppermute | solution.py:118
  60.0 3.5 %collective-permute-done.12 = bf16[2,15,16,128]{3,1,2,0:T(8,128)(2,1)S(1)} collective-permute-done((bf16[2,15,16,128]{3,1,2,0:T(8,128)(2,1)S(1)}, bf16[2,15,16,128]{3,1,2,0:T(8,128)(2,1)S(1)}, u32[]{:S(2)}, u32[]{:S(2)}) %collective-permute-start.12) | collective-permute-done | bytes 122912 | tf_op jit(solution)/shard_map/ppermute | solution.py:118
  63.9 0.8 fusion.20
  64.8 1.7 %collective-permute-start.15 = (bf16[2,64,15,128]{3,2,1,0:T(8,128)(2,1)S(1)}, bf16[2,64,15,128]{3,2,1,0:T(8,128)(2,1)S(1)}, u32[]{:S(2)}, u32[]{:S(2)}) collective-permute-start(bf16[2,64,15,128]{3,2,1,0:T(8,128)(2,1)S(1)} %get-tuple-element.52), channel_id=1, source_target_pairs={{0,1},{1,0},{2,3},{3,2},{4,5},{5,4},{6,7},{7,6},{8,9},{9,8},{10,11... | collective-permute-start | bytes 1474568 | tf_op jit(solution)/shard_map/ppermute | solution.py:23
  67.2 0.9 collective-permute-start.14
  69.4 1.6 %collective-permute-start.16 = (bf16[2,15,16,128]{3,1,2,0:T(8,128)(2,1)S(1)}, bf16[2,15,16,128]{3,1,2,0:T(8,128)(2,1)S(1)}, u32[]{:S(2)}, u32[]{:S(2)}) collective-permute-start(bf16[2,15,16,128]{3,1,2,0:T(8,128)(2,1)S(1)} %constant_dynamic-slice_fusion), channel_id=1, source_target_pairs={{0,2},{2,0},{1,3},{3,1},{4,6},{6,4},{5,7},{7,5},{8,10},{10,8},{9,1... | collective-permute-start | bytes 368648 | tf_op jit(solution)/shard_map/ppermute | solution.py:118
  70.9 3.5 %collective-permute-done.16 = bf16[2,15,16,128]{3,1,2,0:T(8,128)(2,1)S(1)} collective-permute-done((bf16[2,15,16,128]{3,1,2,0:T(8,128)(2,1)S(1)}, bf16[2,15,16,128]{3,1,2,0:T(8,128)(2,1)S(1)}, u32[]{:S(2)}, u32[]{:S(2)}) %collective-permute-start.16) | collective-permute-done | bytes 122912 | tf_op jit(solution)/shard_map/ppermute | solution.py:118
  75.6 10.4 %collective-permute-start.17 = (f32[32,16,128]{2,1,0:T(8,128)S(1)}, f32[32,16,128]{2,1,0:T(8,128)S(1)}, u32[]{:S(2)}, u32[]{:S(2)}) collective-permute-start(f32[32,16,128]{2,1,0:T(8,128)S(1)} %dynamic-slice_bitcast_fusion), channel_id=1, source_target_pairs={{0,1},{1,0},{2,3},{3,2},{4,5},{5,4},{6,7},{7,6},{8,9},{9,8},{10,11... | collective-permute-start | bytes 786440 | tf_op jit(solution)/shard_map/ppermute | solution.py:23
  86.0 1.2 %collective-permute-done.17 = f32[32,16,128]{2,1,0:T(8,128)S(1)} collective-permute-done((f32[32,16,128]{2,1,0:T(8,128)S(1)}, f32[32,16,128]{2,1,0:T(8,128)S(1)}, u32[]{:S(2)}, u32[]{:S(2)}) %collective-permute-start.17) | collective-permute-done | bytes 262176 | tf_op jit(solution)/shard_map/ppermute | solution.py:23
  87.2 0.9 pad_maximum_fusion.3
  (103 shorter events, 16.1 us)
Async XLA Ops:
  0.0 1.8 %copy-start = (bf16[64,32,128]{2,1,0:T(8,128)(2,1)S(1)}, bf16[64,32,128]{2,1,0:T(8,128)(2,1)}, u32[]{:S(2)}) copy-start(bf16[64,32,128]{2,1,0:T(8,128)(2,1)} %param.3) | copy-start | bytes 1572868
  2.5 2.1 %collective-permute-start = (bf16[2,64,16,128]{3,2,1,0:T(8,128)(2,1)S(1)}, bf16[2,64,16,128]{3,2,1,0:T(8,128)(2,1)S(1)}, u32[]{:S(2)}, u32[]{:S(2)}) collective-permute-start(bf16[2,64,16,128]{3,2,1,0:T(8,128)(2,1)S(1)} %pad_maximum_fusion), channel_id=1, source_target_pairs={{0,1},{1,0},{2,3},{3,2},{4,5},{5,4},{6,7},{7,6},{8,9},{9,8},{10,11... | collective-permute-start | bytes 1572872 | tf_op jit(solution)/shard_map/ppermute | solution.py:23
  4.6 1.5 %copy-start.1 = (f32[2,3,31]{2,0,1:T(2,128)S(1)}, f32[2,3,31]{2,0,1:T(2,128)}, u32[]{:S(2)}) copy-start(f32[2,3,31]{2,0,1:T(2,128)} %param.4) | copy-start | bytes 2236
  4.7 3.9 %collective-permute-start.1 = (bf16[64,16,128]{2,1,0:T(8,128)(2,1)S(1)}, bf16[64,16,128]{2,1,0:T(8,128)(2,1)S(1)}, u32[]{:S(2)}, u32[]{:S(2)}) collective-permute-start(bf16[64,16,128]{2,1,0:T(8,128)(2,1)S(1)} %get-tuple-element.61), channel_id=1, source_target_pairs={{1,4},{4,1},{3,6},{6,3},{5,8},{8,5},{7,10},{10,7},{9,12},{12,9},{1... | collective-permute-start | bytes 786440 | tf_op jit(solution)/shard_map/ppermute | solution.py:194
  5.4 3.2 %collective-permute-start.2 = (bf16[64,16,128]{2,1,0:T(8,128)(2,1)S(1)}, bf16[64,16,128]{2,1,0:T(8,128)(2,1)S(1)}, u32[]{:S(2)}, u32[]{:S(2)}) collective-permute-start(bf16[64,16,128]{2,1,0:T(8,128)(2,1)S(1)} %get-tuple-element.62), channel_id=1, source_target_pairs={{1,4},{4,1},{3,6},{6,3},{5,8},{8,5},{7,10},{10,7},{9,12},{12,9},{1... | collective-permute-start | bytes 786440 | tf_op jit(solution)/shard_map/ppermute | solution.py:194
  8.9 11.8 %collective-permute-start.3 = (bf16[64,15,128]{2,1,0:T(8,128)(2,1)S(1)}, bf16[64,15,128]{2,1,0:T(8,128)(2,1)S(1)}, u32[]{:S(2)}, u32[]{:S(2)}) collective-permute-start(bf16[64,15,128]{2,1,0:T(8,128)(2,1)S(1)} %get-tuple-element.67), channel_id=1, source_target_pairs={{1,4},{4,1},{3,6},{6,3},{5,8},{8,5},{7,10},{10,7},{9,12},{12,9},{1... | collective-permute-start | bytes 737288 | tf_op jit(solution)/shard_map/ppermute | solution.py:142
  9.6 12.1 %collective-permute-start.4 = (bf16[64,15,128]{2,1,0:T(8,128)(2,1)S(1)}, bf16[64,15,128]{2,1,0:T(8,128)(2,1)S(1)}, u32[]{:S(2)}, u32[]{:S(2)}) collective-permute-start(bf16[64,15,128]{2,1,0:T(8,128)(2,1)S(1)} %get-tuple-element.68), channel_id=1, source_target_pairs={{0,1},{1,0},{2,3},{3,2},{4,5},{5,4},{6,7},{7,6},{8,9},{9,8},{10,11... | collective-permute-start | bytes 737288 | tf_op jit(solution)/shard_map/ppermute | solution.py:23
  22.7 5.0 %collective-permute-start.5 = (bf16[2,15,16,128]{3,1,2,0:T(8,128)(2,1)S(1)}, bf16[2,15,16,128]{3,1,2,0:T(8,128)(2,1)S(1)}, u32[]{:S(2)}, u32[]{:S(2)}) collective-permute-start(bf16[2,15,16,128]{3,1,2,0:T(8,128)(2,1)S(1)} %constant_dynamic-slice_fusion.3), channel_id=1, source_target_pairs={{0,2},{2,0},{1,3},{3,1},{4,6},{6,4},{5,7},{7,5},{8,10},{10,8},{9,1... | collective-permute-start | bytes 368648 | tf_op jit(solution)/shard_map/ppermute | solution.py:118
  29.1 4.1 %collective-permute-start.8 = (bf16[2,64,15,128]{3,2,1,0:T(8,128)(2,1)S(1)}, bf16[2,64,15,128]{3,2,1,0:T(8,128)(2,1)S(1)}, u32[]{:S(2)}, u32[]{:S(2)}) collective-permute-start(bf16[2,64,15,128]{3,2,1,0:T(8,128)(2,1)S(1)} %get-tuple-element.58), channel_id=1, source_target_pairs={{0,1},{1,0},{2,3},{3,2},{4,5},{5,4},{6,7},{7,6},{8,9},{9,8},{10,11... | collective-permute-start | bytes 1474568 | tf_op jit(solution)/shard_map/ppermute | solution.py:23
  31.7 1.5 %collective-permute-start.6 = (bf16[64,15,128]{2,1,0:T(8,128)(2,1)S(1)}, bf16[64,15,128]{2,1,0:T(8,128)(2,1)S(1)}, u32[]{:S(2)}, u32[]{:S(2)}) collective-permute-start(bf16[64,15,128]{2,1,0:T(8,128)(2,1)S(1)} %get-tuple-element.55), channel_id=1, source_target_pairs={{1,4},{4,1},{3,6},{6,3},{5,8},{8,5},{7,10},{10,7},{9,12},{12,9},{1... | collective-permute-start | bytes 737288 | tf_op jit(solution)/shard_map/ppermute | solution.py:140
  32.4 0.8 collective-permute-start.7
  34.4 5.0 %collective-permute-start.9 = (bf16[2,15,16,128]{3,1,2,0:T(8,128)(2,1)S(1)}, bf16[2,15,16,128]{3,1,2,0:T(8,128)(2,1)S(1)}, u32[]{:S(2)}, u32[]{:S(2)}) collective-permute-start(bf16[2,15,16,128]{3,1,2,0:T(8,128)(2,1)S(1)} %constant_dynamic-slice_fusion.2), channel_id=1, source_target_pairs={{0,2},{2,0},{1,3},{3,1},{4,6},{6,4},{5,7},{7,5},{8,10},{10,8},{9,1... | collective-permute-start | bytes 368648 | tf_op jit(solution)/shard_map/ppermute | solution.py:118
  40.8 15.5 %collective-permute-start.10 = (bf16[64,15,128]{2,1,0:T(8,128)(2,1)S(1)}, bf16[64,15,128]{2,1,0:T(8,128)(2,1)S(1)}, u32[]{:S(2)}, u32[]{:S(2)}) collective-permute-start(bf16[64,15,128]{2,1,0:T(8,128)(2,1)S(1)} %get-tuple-element.65), channel_id=1, source_target_pairs={{1,4},{4,1},{3,6},{6,3},{5,8},{8,5},{7,10},{10,7},{9,12},{12,9},{1... | collective-permute-start | bytes 737288 | tf_op jit(solution)/shard_map/ppermute | solution.py:142
  41.5 16.0 %collective-permute-start.11 = (bf16[64,15,128]{2,1,0:T(8,128)(2,1)S(1)}, bf16[64,15,128]{2,1,0:T(8,128)(2,1)S(1)}, u32[]{:S(2)}, u32[]{:S(2)}) collective-permute-start(bf16[64,15,128]{2,1,0:T(8,128)(2,1)S(1)} %get-tuple-element.66), channel_id=1, source_target_pairs={{0,1},{1,0},{2,3},{3,2},{4,5},{5,4},{6,7},{7,6},{8,9},{9,8},{10,11... | collective-permute-start | bytes 737288 | tf_op jit(solution)/shard_map/ppermute | solution.py:23
  58.4 5.0 %collective-permute-start.12 = (bf16[2,15,16,128]{3,1,2,0:T(8,128)(2,1)S(1)}, bf16[2,15,16,128]{3,1,2,0:T(8,128)(2,1)S(1)}, u32[]{:S(2)}, u32[]{:S(2)}) collective-permute-start(bf16[2,15,16,128]{3,1,2,0:T(8,128)(2,1)S(1)} %constant_dynamic-slice_fusion.1), channel_id=1, source_target_pairs={{0,2},{2,0},{1,3},{3,1},{4,6},{6,4},{5,7},{7,5},{8,10},{10,8},{9,1... | collective-permute-start | bytes 368648 | tf_op jit(solution)/shard_map/ppermute | solution.py:118
  64.8 3.3 %collective-permute-start.15 = (bf16[2,64,15,128]{3,2,1,0:T(8,128)(2,1)S(1)}, bf16[2,64,15,128]{3,2,1,0:T(8,128)(2,1)S(1)}, u32[]{:S(2)}, u32[]{:S(2)}) collective-permute-start(bf16[2,64,15,128]{3,2,1,0:T(8,128)(2,1)S(1)} %get-tuple-element.52), channel_id=1, source_target_pairs={{0,1},{1,0},{2,3},{3,2},{4,5},{5,4},{6,7},{7,6},{8,9},{9,8},{10,11... | collective-permute-start | bytes 1474568 | tf_op jit(solution)/shard_map/ppermute | solution.py:23
  66.6 1.6 %collective-permute-start.13 = (bf16[64,15,128]{2,1,0:T(8,128)(2,1)S(1)}, bf16[64,15,128]{2,1,0:T(8,128)(2,1)S(1)}, u32[]{:S(2)}, u32[]{:S(2)}) collective-permute-start(bf16[64,15,128]{2,1,0:T(8,128)(2,1)S(1)} %get-tuple-element.49), channel_id=1, source_target_pairs={{1,4},{4,1},{3,6},{6,3},{5,8},{8,5},{7,10},{10,7},{9,12},{12,9},{1... | collective-permute-start | bytes 737288 | tf_op jit(solution)/shard_map/ppermute | solution.py:140
  67.2 0.9 collective-permute-start.14
  69.4 5.0 %collective-permute-start.16 = (bf16[2,15,16,128]{3,1,2,0:T(8,128)(2,1)S(1)}, bf16[2,15,16,128]{3,1,2,0:T(8,128)(2,1)S(1)}, u32[]{:S(2)}, u32[]{:S(2)}) collective-permute-start(bf16[2,15,16,128]{3,1,2,0:T(8,128)(2,1)S(1)} %constant_dynamic-slice_fusion), channel_id=1, source_target_pairs={{0,2},{2,0},{1,3},{3,1},{4,6},{6,4},{5,7},{7,5},{8,10},{10,8},{9,1... | collective-permute-start | bytes 368648 | tf_op jit(solution)/shard_map/ppermute | solution.py:118
  75.6 11.6 %collective-permute-start.17 = (f32[32,16,128]{2,1,0:T(8,128)S(1)}, f32[32,16,128]{2,1,0:T(8,128)S(1)}, u32[]{:S(2)}, u32[]{:S(2)}) collective-permute-start(f32[32,16,128]{2,1,0:T(8,128)S(1)} %dynamic-slice_bitcast_fusion), channel_id=1, source_target_pairs={{0,1},{1,0},{2,3},{3,2},{4,5},{5,4},{6,7},{7,6},{8,9},{9,8},{10,11... | collective-permute-start | bytes 786440 | tf_op jit(solution)/shard_map/ppermute | solution.py:23

commit v21 on v16

--- a/solution.py
+++ b/solution.py
@@ -113,8 +113,9 @@
         if not route:
             continue
         is_lower = slab % 2 == phase
-        start = jnp.where(is_lower, planes - reach, 0)
-        payload = lax.dynamic_slice_in_dim(volume, start, reach, axis)
+        top = lax.slice_in_dim(volume, planes - reach, planes, axis=axis)
+        bottom = lax.slice_in_dim(volume, 0, reach, axis=axis)
+        payload = jnp.where(is_lower, top, bottom)
         got = lax.ppermute(payload, "view", route)
         below = jnp.where(is_lower, below, got)
         above = jnp.where(is_lower, got, above)

time: 85.8 us -> 85.8 us (level)
  no operation moved by 1% of the time
where the time goes in v21:
time: 85.8 us; the launch traced here: 85.4 us
  starting transfers between devices  47.6 us (55%)
  waiting for transfers between devices  21.7 us (25%)
  other arithmetic  7.2 us (8%)
  matrix products  5.1 us (6%)
  local copies, waits for them, and re-layouts  3.24 us (4%)
    ppermute x6, starting transfers between devices, from_partner(): return lax.ppermute(block, axis, route)  37.8 us
    ppermute x4, waiting for transfers between devices, z_rims(): got = lax.ppermute(payload, 'view', route)  13.9 us
    ppermute x6, waiting for transfers between devices, from_partner(): return lax.ppermute(block, axis, route)  7.8 us
    ppermute x4, starting transfers between devices, z_rims(): got = lax.ppermute(payload, 'view', route)  6.22 us
    ppermute x4, starting transfers between devices, x_rims(): across = lax.ppermute(outward, ('tile', 'view'), route)  2.92 us
  transfers between devices with their start and end apart: 15, of which 10 were waited for; matrix products, arithmetic and copies ran while one was open for 3% of the time, Pallas kernels for 0%

profile of v21, /device:TPU:0, one launch (start us, length us, event | category | flops | bytes accessed | tf_op | source)
XLA Modules:
  0.0 85.4 jit_solution(12777063787171232840)
XLA Ops:
  0.0 0.9 %fusion.70 = (s32[4]{0:T(128)S(1)}, s32[4]{0:T(128)S(1)}, s32[4]{0:T(128)S(1)}, s32[4]{0:T(128)S(1)}) fusion(s32[1,32]{1,0:T(1,128)} %param.5, s32[]{:T(128)S(6)} %select_n.348, s32[]{:T(128)S(6)} %select_n.349, s32[]{:T(128)S(6)} %select_n.351, s32[]{:T(128)S(6)} %select_n.350), kind=kLoop, calls=%fused_computation.180 | loop fusion | bytes 144 | tf_op jit(solution)/shard_map/dynamic_slice | solution.py:165
  1.0 0.8 gather_fusion
  3.0 1.5 %collective-permute-done = bf16[2,64,16,128]{3,2,1,0:T(8,128)(2,1)S(1)} collective-permute-done((bf16[2,64,16,128]{3,2,1,0:T(8,128)(2,1)S(1)}, bf16[2,64,16,128]{3,2,1,0:T(8,128)(2,1)S(1)}, u32[]{:S(2)}, u32[]{:S(2)}) %collective-permute-start) | collective-permute-done | bytes 524320 | tf_op jit(solution)/shard_map/ppermute | solution.py:23
  6.9 1.0 %select_reduce_fusion.1 = (bf16[128,128]{1,0:T(8,128)(2,1)S(1)}, bf16[128,128]{1,0:T(8,128)(2,1)S(1)}, bf16[128,128]{1,0:T(8,128)(2,1)S(1)}, bf16[128,128]{1,0:T(8,128)(2,1)S(1)}) fusion(f32[31]{0:T(128)S(1)} %get-tuple-element.74, s32[128,128]{1,0:T(8,128)S(1)} %subtract_add_fusion, f32[31]{0:T(128)S(1)} %get-tuple-element.75, f32[31]{0:T(128)S(1)} %get-tuple-element.89, ...), kind=kLoop, calls=%fused_computation.2 | loop fusion | flops 4505600 | bytes 197104 | tf_op jit(solution)/shard_map/reduce_sum | solution.py:45
  8.8 11.7 %collective-permute-start.3 = (bf16[64,15,128]{2,1,0:T(8,128)(2,1)S(1)}, bf16[64,15,128]{2,1,0:T(8,128)(2,1)S(1)}, u32[]{:S(2)}, u32[]{:S(2)}) collective-permute-start(bf16[64,15,128]{2,1,0:T(8,128)(2,1)S(1)} %get-tuple-element.62), channel_id=1, source_target_pairs={{0,1},{1,0},{2,3},{3,2},{4,5},{5,4},{6,7},{7,6},{8,9},{9,8},{10,11... | collective-permute-start | bytes 737288 | tf_op jit(solution)/shard_map/ppermute | solution.py:23
  20.6 1.0 %collective-permute-done.3 = bf16[64,15,128]{2,1,0:T(8,128)(2,1)S(1)} collective-permute-done((bf16[64,15,128]{2,1,0:T(8,128)(2,1)S(1)}, bf16[64,15,128]{2,1,0:T(8,128)(2,1)S(1)}, u32[]{:S(2)}, u32[]{:S(2)}) %collective-permute-start.3) | collective-permute-done | bytes 245792 | tf_op jit(solution)/shard_map/ppermute | solution.py:23
  22.6 1.6 %collective-permute-start.4 = (bf16[2,15,16,128]{3,1,2,0:T(8,128)(2,1)S(1)}, bf16[2,15,16,128]{3,1,2,0:T(8,128)(2,1)S(1)}, u32[]{:S(2)}, u32[]{:S(2)}) collective-permute-start(bf16[2,15,16,128]{3,1,2,0:T(8,128)(2,1)S(1)} %slice_select_fusion.3), channel_id=1, source_target_pairs={{0,2},{2,0},{1,3},{3,1},{4,6},{6,4},{5,7},{7,5},{8,10},{10,8},{9,1... | collective-permute-start | bytes 368648 | tf_op jit(solution)/shard_map/ppermute | solution.py:119
  24.1 3.5 %collective-permute-done.4 = bf16[2,15,16,128]{3,1,2,0:T(8,128)(2,1)S(1)} collective-permute-done((bf16[2,15,16,128]{3,1,2,0:T(8,128)(2,1)S(1)}, bf16[2,15,16,128]{3,1,2,0:T(8,128)(2,1)S(1)}, u32[]{:S(2)}, u32[]{:S(2)}) %collective-permute-start.4) | collective-permute-done | bytes 122912 | tf_op jit(solution)/shard_map/ppermute | solution.py:119
  29.7 6.4 %collective-permute-start.6 = (bf16[2,64,15,128]{3,2,1,0:T(8,128)(2,1)S(1)}, bf16[2,64,15,128]{3,2,1,0:T(8,128)(2,1)S(1)}, u32[]{:S(2)}, u32[]{:S(2)}) collective-permute-start(bf16[2,64,15,128]{3,2,1,0:T(8,128)(2,1)S(1)} %get-tuple-element.54), channel_id=1, source_target_pairs={{0,1},{1,0},{2,3},{3,2},{4,5},{5,4},{6,7},{7,6},{8,9},{9,8},{10,11... | collective-permute-start | bytes 1474568 | tf_op jit(solution)/shard_map/ppermute | solution.py:23
  36.2 1.4 %collective-permute-done.6 = bf16[2,64,15,128]{3,2,1,0:T(8,128)(2,1)S(1)} collective-permute-done((bf16[2,64,15,128]{3,2,1,0:T(8,128)(2,1)S(1)}, bf16[2,64,15,128]{3,2,1,0:T(8,128)(2,1)S(1)}, u32[]{:S(2)}, u32[]{:S(2)}) %collective-permute-start.6) | collective-permute-done | bytes 491552 | tf_op jit(solution)/shard_map/ppermute | solution.py:23
  38.8 1.6 %collective-permute-start.7 = (bf16[2,15,16,128]{3,1,2,0:T(8,128)(2,1)S(1)}, bf16[2,15,16,128]{3,1,2,0:T(8,128)(2,1)S(1)}, u32[]{:S(2)}, u32[]{:S(2)}) collective-permute-start(bf16[2,15,16,128]{3,1,2,0:T(8,128)(2,1)S(1)} %slice_select_fusion.2), channel_id=1, source_target_pairs={{0,2},{2,0},{1,3},{3,1},{4,6},{6,4},{5,7},{7,5},{8,10},{10,8},{9,1... | collective-permute-start | bytes 368648 | tf_op jit(solution)/shard_map/ppermute | solution.py:119
  40.3 3.5 %collective-permute-done.7 = bf16[2,15,16,128]{3,1,2,0:T(8,128)(2,1)S(1)} collective-permute-done((bf16[2,15,16,128]{3,1,2,0:T(8,128)(2,1)S(1)}, bf16[2,15,16,128]{3,1,2,0:T(8,128)(2,1)S(1)}, u32[]{:S(2)}, u32[]{:S(2)}) %collective-permute-start.7) | collective-permute-done | bytes 122912 | tf_op jit(solution)/shard_map/ppermute | solution.py:119
  45.8 8.8 %collective-permute-start.9 = (bf16[64,15,128]{2,1,0:T(8,128)(2,1)S(1)}, bf16[64,15,128]{2,1,0:T(8,128)(2,1)S(1)}, u32[]{:S(2)}, u32[]{:S(2)}) collective-permute-start(bf16[64,15,128]{2,1,0:T(8,128)(2,1)S(1)} %get-tuple-element.60), channel_id=1, source_target_pairs={{0,1},{1,0},{2,3},{3,2},{4,5},{5,4},{6,7},{7,6},{8,9},{9,8},{10,11... | collective-permute-start | bytes 737288 | tf_op jit(solution)/shard_map/ppermute | solution.py:23
  54.6 1.2 %collective-permute-done.9 = bf16[64,15,128]{2,1,0:T(8,128)(2,1)S(1)} collective-permute-done((bf16[64,15,128]{2,1,0:T(8,128)(2,1)S(1)}, bf16[64,15,128]{2,1,0:T(8,128)(2,1)S(1)}, u32[]{:S(2)}, u32[]{:S(2)}) %collective-permute-start.9) | collective-permute-done | bytes 245792 | tf_op jit(solution)/shard_map/ppermute | solution.py:23
  56.8 1.6 %collective-permute-start.10 = (bf16[2,15,16,128]{3,1,2,0:T(8,128)(2,1)S(1)}, bf16[2,15,16,128]{3,1,2,0:T(8,128)(2,1)S(1)}, u32[]{:S(2)}, u32[]{:S(2)}) collective-permute-start(bf16[2,15,16,128]{3,1,2,0:T(8,128)(2,1)S(1)} %slice_select_fusion.1), channel_id=1, source_target_pairs={{0,2},{2,0},{1,3},{3,1},{4,6},{6,4},{5,7},{7,5},{8,10},{10,8},{9,1... | collective-permute-start | bytes 368648 | tf_op jit(solution)/shard_map/ppermute | solution.py:119
  58.3 3.5 %collective-permute-done.10 = bf16[2,15,16,128]{3,1,2,0:T(8,128)(2,1)S(1)} collective-permute-done((bf16[2,15,16,128]{3,1,2,0:T(8,128)(2,1)S(1)}, bf16[2,15,16,128]{3,1,2,0:T(8,128)(2,1)S(1)}, u32[]{:S(2)}, u32[]{:S(2)}) %collective-permute-start.10) | collective-permute-done | bytes 122912 | tf_op jit(solution)/shard_map/ppermute | solution.py:119
  63.1 0.9 %collective-permute-start.11 = (bf16[2,64,15,128]{3,2,1,0:T(8,128)(2,1)S(1)}, bf16[2,64,15,128]{3,2,1,0:T(8,128)(2,1)S(1)}, u32[]{:S(2)}, u32[]{:S(2)}) collective-permute-start(bf16[2,64,15,128]{3,2,1,0:T(8,128)(2,1)S(1)} %get-tuple-element.49), channel_id=1, source_target_pairs={{1,4},{4,1},{3,6},{6,3},{5,8},{8,5},{7,10},{10,7},{9,12},{12,9},{1... | collective-permute-start | bytes 1474568 | tf_op jit(solution)/shard_map/ppermute | solution.py:140
  64.0 6.1 %collective-permute-start.12 = (bf16[2,64,15,128]{3,2,1,0:T(8,128)(2,1)S(1)}, bf16[2,64,15,128]{3,2,1,0:T(8,128)(2,1)S(1)}, u32[]{:S(2)}, u32[]{:S(2)}) collective-permute-start(bf16[2,64,15,128]{3,2,1,0:T(8,128)(2,1)S(1)} %get-tuple-element.50), channel_id=1, source_target_pairs={{0,1},{1,0},{2,3},{3,2},{4,5},{5,4},{6,7},{7,6},{8,9},{9,8},{10,11... | collective-permute-start | bytes 1474568 | tf_op jit(solution)/shard_map/ppermute | solution.py:23
  70.1 1.5 %collective-permute-done.12 = bf16[2,64,15,128]{3,2,1,0:T(8,128)(2,1)S(1)} collective-permute-done((bf16[2,64,15,128]{3,2,1,0:T(8,128)(2,1)S(1)}, bf16[2,64,15,128]{3,2,1,0:T(8,128)(2,1)S(1)}, u32[]{:S(2)}, u32[]{:S(2)}) %collective-permute-start.12) | collective-permute-done | bytes 491552 | tf_op jit(solution)/shard_map/ppermute | solution.py:23
  72.8 1.6 %collective-permute-start.13 = (bf16[2,15,16,128]{3,1,2,0:T(8,128)(2,1)S(1)}, bf16[2,15,16,128]{3,1,2,0:T(8,128)(2,1)S(1)}, u32[]{:S(2)}, u32[]{:S(2)}) collective-permute-start(bf16[2,15,16,128]{3,1,2,0:T(8,128)(2,1)S(1)} %slice_select_fusion), channel_id=1, source_target_pairs={{0,2},{2,0},{1,3},{3,1},{4,6},{6,4},{5,7},{7,5},{8,10},{10,8},{9,1... | collective-permute-start | bytes 368648 | tf_op jit(solution)/shard_map/ppermute | solution.py:119
  74.4 3.5 %collective-permute-done.13 = bf16[2,15,16,128]{3,1,2,0:T(8,128)(2,1)S(1)} collective-permute-done((bf16[2,15,16,128]{3,1,2,0:T(8,128)(2,1)S(1)}, bf16[2,15,16,128]{3,1,2,0:T(8,128)(2,1)S(1)}, u32[]{:S(2)}, u32[]{:S(2)}) %collective-permute-start.13) | collective-permute-done | bytes 122912 | tf_op jit(solution)/shard_map/ppermute | solution.py:119
  79.1 4.3 %collective-permute-start.14 = (f32[32,16,128]{2,1,0:T(8,128)S(1)}, f32[32,16,128]{2,1,0:T(8,128)S(1)}, u32[]{:S(2)}, u32[]{:S(2)}) collective-permute-start(f32[32,16,128]{2,1,0:T(8,128)S(1)} %dynamic-slice_bitcast_fusion), channel_id=1, source_target_pairs={{0,1},{1,0},{2,3},{3,2},{4,5},{5,4},{6,7},{7,6},{8,9},{9,8},{10,11... | collective-permute-start | bytes 786440 | tf_op jit(solution)/shard_map/ppermute | solution.py:23
  83.3 1.2 %collective-permute-done.14 = f32[32,16,128]{2,1,0:T(8,128)S(1)} collective-permute-done((f32[32,16,128]{2,1,0:T(8,128)S(1)}, f32[32,16,128]{2,1,0:T(8,128)S(1)}, u32[]{:S(2)}, u32[]{:S(2)}) %collective-permute-start.14) | collective-permute-done | bytes 262176 | tf_op jit(solution)/shard_map/ppermute | solution.py:23
  84.5 0.9 pad_maximum_fusion.1
  (94 shorter events, 15.3 us)
Async XLA Ops:
  0.0 1.8 %copy-start = (bf16[64,32,128]{2,1,0:T(8,128)(2,1)S(1)}, bf16[64,32,128]{2,1,0:T(8,128)(2,1)}, u32[]{:S(2)}) copy-start(bf16[64,32,128]{2,1,0:T(8,128)(2,1)} %param.3) | copy-start | bytes 1572868
  2.5 2.1 %collective-permute-start = (bf16[2,64,16,128]{3,2,1,0:T(8,128)(2,1)S(1)}, bf16[2,64,16,128]{3,2,1,0:T(8,128)(2,1)S(1)}, u32[]{:S(2)}, u32[]{:S(2)}) collective-permute-start(bf16[2,64,16,128]{3,2,1,0:T(8,128)(2,1)S(1)} %pad_maximum_fusion), channel_id=1, source_target_pairs={{0,1},{1,0},{2,3},{3,2},{4,5},{5,4},{6,7},{7,6},{8,9},{9,8},{10,11... | collective-permute-start | bytes 1572872 | tf_op jit(solution)/shard_map/ppermute | solution.py:23
  3.0 2.3 %copy-start.1 = (f32[2,3,31]{2,0,1:T(2,128)S(1)}, f32[2,3,31]{2,0,1:T(2,128)}, u32[]{:S(2)}) copy-start(f32[2,3,31]{2,0,1:T(2,128)} %param.4) | copy-start | bytes 2236
  4.7 3.2 %collective-permute-start.1 = (bf16[2,64,16,128]{3,2,1,0:T(8,128)(2,1)S(1)}, bf16[2,64,16,128]{3,2,1,0:T(8,128)(2,1)S(1)}, u32[]{:S(2)}, u32[]{:S(2)}) collective-permute-start(bf16[2,64,16,128]{3,2,1,0:T(8,128)(2,1)S(1)} %maximum_select_fusion.1), channel_id=1, source_target_pairs={{1,4},{4,1},{3,6},{6,3},{5,8},{8,5},{7,10},{10,7},{9,12},{12,9},{1... | collective-permute-start | bytes 1572872 | tf_op jit(solution)/shard_map/ppermute | solution.py:192
  8.1 12.5 %collective-permute-start.2 = (bf16[64,15,128]{2,1,0:T(8,128)(2,1)S(1)}, bf16[64,15,128]{2,1,0:T(8,128)(2,1)S(1)}, u32[]{:S(2)}, u32[]{:S(2)}) collective-permute-start(bf16[64,15,128]{2,1,0:T(8,128)(2,1)S(1)} %get-tuple-element.61), channel_id=1, source_target_pairs={{1,4},{4,1},{3,6},{6,3},{5,8},{8,5},{7,10},{10,7},{9,12},{12,9},{1... | collective-permute-start | bytes 737288 | tf_op jit(solution)/shard_map/ppermute | solution.py:140
  8.8 12.8 %collective-permute-start.3 = (bf16[64,15,128]{2,1,0:T(8,128)(2,1)S(1)}, bf16[64,15,128]{2,1,0:T(8,128)(2,1)S(1)}, u32[]{:S(2)}, u32[]{:S(2)}) collective-permute-start(bf16[64,15,128]{2,1,0:T(8,128)(2,1)S(1)} %get-tuple-element.62), channel_id=1, source_target_pairs={{0,1},{1,0},{2,3},{3,2},{4,5},{5,4},{6,7},{7,6},{8,9},{9,8},{10,11... | collective-permute-start | bytes 737288 | tf_op jit(solution)/shard_map/ppermute | solution.py:23
  22.6 5.0 %collective-permute-start.4 = (bf16[2,15,16,128]{3,1,2,0:T(8,128)(2,1)S(1)}, bf16[2,15,16,128]{3,1,2,0:T(8,128)(2,1)S(1)}, u32[]{:S(2)}, u32[]{:S(2)}) collective-permute-start(bf16[2,15,16,128]{3,1,2,0:T(8,128)(2,1)S(1)} %slice_select_fusion.3), channel_id=1, source_target_pairs={{0,2},{2,0},{1,3},{3,1},{4,6},{6,4},{5,7},{7,5},{8,10},{10,8},{9,1... | collective-permute-start | bytes 368648 | tf_op jit(solution)/shard_map/ppermute | solution.py:119
  29.0 7.2 %collective-permute-start.5 = (bf16[2,64,15,128]{3,2,1,0:T(8,128)(2,1)S(1)}, bf16[2,64,15,128]{3,2,1,0:T(8,128)(2,1)S(1)}, u32[]{:S(2)}, u32[]{:S(2)}) collective-permute-start(bf16[2,64,15,128]{3,2,1,0:T(8,128)(2,1)S(1)} %get-tuple-element.53), channel_id=1, source_target_pairs={{1,4},{4,1},{3,6},{6,3},{5,8},{8,5},{7,10},{10,7},{9,12},{12,9},{1... | collective-permute-start | bytes 1474568 | tf_op jit(solution)/shard_map/ppermute | solution.py:140
  29.7 7.9 %collective-permute-start.6 = (bf16[2,64,15,128]{3,2,1,0:T(8,128)(2,1)S(1)}, bf16[2,64,15,128]{3,2,1,0:T(8,128)(2,1)S(1)}, u32[]{:S(2)}, u32[]{:S(2)}) collective-permute-start(bf16[2,64,15,128]{3,2,1,0:T(8,128)(2,1)S(1)} %get-tuple-element.54), channel_id=1, source_target_pairs={{0,1},{1,0},{2,3},{3,2},{4,5},{5,4},{6,7},{7,6},{8,9},{9,8},{10,11... | collective-permute-start | bytes 1474568 | tf_op jit(solution)/shard_map/ppermute | solution.py:23
  38.8 5.0 %collective-permute-start.7 = (bf16[2,15,16,128]{3,1,2,0:T(8,128)(2,1)S(1)}, bf16[2,15,16,128]{3,1,2,0:T(8,128)(2,1)S(1)}, u32[]{:S(2)}, u32[]{:S(2)}) collective-permute-start(bf16[2,15,16,128]{3,1,2,0:T(8,128)(2,1)S(1)} %slice_select_fusion.2), channel_id=1, source_target_pairs={{0,2},{2,0},{1,3},{3,1},{4,6},{6,4},{5,7},{7,5},{8,10},{10,8},{9,1... | collective-permute-start | bytes 368648 | tf_op jit(solution)/shard_map/ppermute | solution.py:119
  45.1 9.5 %collective-permute-start.8 = (bf16[64,15,128]{2,1,0:T(8,128)(2,1)S(1)}, bf16[64,15,128]{2,1,0:T(8,128)(2,1)S(1)}, u32[]{:S(2)}, u32[]{:S(2)}) collective-permute-start(bf16[64,15,128]{2,1,0:T(8,128)(2,1)S(1)} %get-tuple-element.59), channel_id=1, source_target_pairs={{1,4},{4,1},{3,6},{6,3},{5,8},{8,5},{7,10},{10,7},{9,12},{12,9},{1... | collective-permute-start | bytes 737288 | tf_op jit(solution)/shard_map/ppermute | solution.py:140
  45.8 10.0 %collective-permute-start.9 = (bf16[64,15,128]{2,1,0:T(8,128)(2,1)S(1)}, bf16[64,15,128]{2,1,0:T(8,128)(2,1)S(1)}, u32[]{:S(2)}, u32[]{:S(2)}) collective-permute-start(bf16[64,15,128]{2,1,0:T(8,128)(2,1)S(1)} %get-tuple-element.60), channel_id=1, source_target_pairs={{0,1},{1,0},{2,3},{3,2},{4,5},{5,4},{6,7},{7,6},{8,9},{9,8},{10,11... | collective-permute-start | bytes 737288 | tf_op jit(solution)/shard_map/ppermute | solution.py:23
  56.8 5.0 %collective-permute-start.10 = (bf16[2,15,16,128]{3,1,2,0:T(8,128)(2,1)S(1)}, bf16[2,15,16,128]{3,1,2,0:T(8,128)(2,1)S(1)}, u32[]{:S(2)}, u32[]{:S(2)}) collective-permute-start(bf16[2,15,16,128]{3,1,2,0:T(8,128)(2,1)S(1)} %slice_select_fusion.1), channel_id=1, source_target_pairs={{0,2},{2,0},{1,3},{3,1},{4,6},{6,4},{5,7},{7,5},{8,10},{10,8},{9,1... | collective-permute-start | bytes 368648 | tf_op jit(solution)/shard_map/ppermute | solution.py:119
  63.1 7.0 %collective-permute-start.11 = (bf16[2,64,15,128]{3,2,1,0:T(8,128)(2,1)S(1)}, bf16[2,64,15,128]{3,2,1,0:T(8,128)(2,1)S(1)}, u32[]{:S(2)}, u32[]{:S(2)}) collective-permute-start(bf16[2,64,15,128]{3,2,1,0:T(8,128)(2,1)S(1)} %get-tuple-element.49), channel_id=1, source_target_pairs={{1,4},{4,1},{3,6},{6,3},{5,8},{8,5},{7,10},{10,7},{9,12},{12,9},{1... | collective-permute-start | bytes 1474568 | tf_op jit(solution)/shard_map/ppermute | solution.py:140
  64.0 7.6 %collective-permute-start.12 = (bf16[2,64,15,128]{3,2,1,0:T(8,128)(2,1)S(1)}, bf16[2,64,15,128]{3,2,1,0:T(8,128)(2,1)S(1)}, u32[]{:S(2)}, u32[]{:S(2)}) collective-permute-start(bf16[2,64,15,128]{3,2,1,0:T(8,128)(2,1)S(1)} %get-tuple-element.50), channel_id=1, source_target_pairs={{0,1},{1,0},{2,3},{3,2},{4,5},{5,4},{6,7},{7,6},{8,9},{9,8},{10,11... | collective-permute-start | bytes 1474568 | tf_op jit(solution)/shard_map/ppermute | solution.py:23
  72.8 5.0 %collective-permute-start.13 = (bf16[2,15,16,128]{3,1,2,0:T(8,128)(2,1)S(1)}, bf16[2,15,16,128]{3,1,2,0:T(8,128)(2,1)S(1)}, u32[]{:S(2)}, u32[]{:S(2)}) collective-permute-start(bf16[2,15,16,128]{3,1,2,0:T(8,128)(2,1)S(1)} %slice_select_fusion), channel_id=1, source_target_pairs={{0,2},{2,0},{1,3},{3,1},{4,6},{6,4},{5,7},{7,5},{8,10},{10,8},{9,1... | collective-permute-start | bytes 368648 | tf_op jit(solution)/shard_map/ppermute | solution.py:119
  79.1 5.4 %collective-permute-start.14 = (f32[32,16,128]{2,1,0:T(8,128)S(1)}, f32[32,16,128]{2,1,0:T(8,128)S(1)}, u32[]{:S(2)}, u32[]{:S(2)}) collective-permute-start(f32[32,16,128]{2,1,0:T(8,128)S(1)} %dynamic-slice_bitcast_fusion), channel_id=1, source_target_pairs={{0,1},{1,0},{2,3},{3,2},{4,5},{5,4},{6,7},{7,6},{8,9},{9,8},{10,11... | collective-permute-start | bytes 786440 | tf_op jit(solution)/shard_map/ppermute | solution.py:23

commit v22 on v17

--- a/solution.py
+++ b/solution.py
@@ -113,8 +113,9 @@
         if not route:
             continue
         is_lower = slab % 2 == phase
-        start = jnp.where(is_lower, planes - reach, 0)
-        payload = lax.dynamic_slice_in_dim(volume, start, reach, axis)
+        top = lax.slice_in_dim(volume, planes - reach, planes, axis=axis)
+        bottom = lax.slice_in_dim(volume, 0, reach, axis=axis)
+        payload = jnp.where(is_lower, top, bottom)
         got = lax.ppermute(payload, "view", route)
         below = jnp.where(is_lower, below, got)
         above = jnp.where(is_lower, got, above)
@@ -161,7 +162,7 @@
     near = lax.dynamic_slice_in_dim(table, tile_index, 3, 0)
     slots = jnp.concatenate([near[1], near[2, :half_blocks], near[0, half_blocks:]])
     row_ids = jnp.arange(slots.shape[0] * BX, dtype=jnp.int32)
-    row_slots = jnp.repeat(slots, BX)
+    row_slots = slots[row_ids // BX]
     source_x = (row_slots % block_count) * BX + row_ids % BX
     chosen_rows = (row_slots // block_count == tile_index)[:, None] & (
         source_x[:, None] == jnp.arange(width_x, dtype=jnp.int32)[None, :]

time: 86.3 us -> 86.9 us (level)
  no operation moved by 1% of the time
where the time goes in v22:
time: 86.9 us; the launch traced here: 86.5 us
  starting transfers between devices  47.6 us (55%)
  waiting for transfers between devices  21.7 us (25%)
  other arithmetic  8.52 us (10%)
  matrix products  5.1 us (6%)
  local copies, waits for them, and re-layouts  3.03 us (3%)
    ppermute x6, starting transfers between devices, from_partner(): return lax.ppermute(block, axis, route)  37.8 us
    ppermute x4, waiting for transfers between devices, z_rims(): got = lax.ppermute(payload, 'view', route)  13.9 us
    ppermute x6, waiting for transfers between devices, from_partner(): return lax.ppermute(block, axis, route)  7.8 us
    ppermute x4, starting transfers between devices, z_rims(): got = lax.ppermute(payload, 'view', route)  6.22 us
    ppermute x4, starting transfers between devices, x_rims(): across = lax.ppermute(outward, ('tile', 'view'), route)  2.92 us
  transfers between devices with their start and end apart: 15, of which 10 were waited for; matrix products, arithmetic and copies ran while one was open for 3% of the time, Pallas kernels for 0%

profile of v22, /device:TPU:0, one launch (start us, length us, event | category | flops | bytes accessed | tf_op | source)
XLA Modules:
  0.0 86.5 jit_solution(308938521364584354)
XLA Ops:
  0.5 1.3 %reduce.3 = s32[32]{0:T(128)S(1)} reduce(s32[1,32]{1,0:T(1,128)} %param.5, s32[]{:T(128)} %broadcast.249), dimensions={0}, to_apply=%param.5.reduce_sub_computation.3 | reduce | bytes 260 | tf_op args[2]
  2.1 0.8 gather_fusion
  4.1 1.5 %collective-permute-done = bf16[2,64,16,128]{3,2,1,0:T(8,128)(2,1)S(1)} collective-permute-done((bf16[2,64,16,128]{3,2,1,0:T(8,128)(2,1)S(1)}, bf16[2,64,16,128]{3,2,1,0:T(8,128)(2,1)S(1)}, u32[]{:S(2)}, u32[]{:S(2)}) %collective-permute-start) | collective-permute-done | bytes 524320 | tf_op jit(solution)/shard_map/ppermute | solution.py:23
  8.0 1.0 %select_reduce_fusion.1 = (bf16[128,128]{1,0:T(8,128)(2,1)S(1)}, bf16[128,128]{1,0:T(8,128)(2,1)S(1)}, bf16[128,128]{1,0:T(8,128)(2,1)S(1)}, bf16[128,128]{1,0:T(8,128)(2,1)S(1)}) fusion(f32[31]{0:T(128)S(1)} %get-tuple-element.76, s32[128,128]{1,0:T(8,128)S(1)} %subtract_add_fusion, f32[31]{0:T(128)S(1)} %get-tuple-element.77, f32[31]{0:T(128)S(1)} %get-tuple-element.87, ...), kind=kLoop, calls=%fused_computation.2 | loop fusion | flops 4505600 | bytes 197104 | tf_op jit(solution)/shard_map/reduce_sum | solution.py:45
  9.9 11.7 %collective-permute-start.3 = (bf16[64,15,128]{2,1,0:T(8,128)(2,1)S(1)}, bf16[64,15,128]{2,1,0:T(8,128)(2,1)S(1)}, u32[]{:S(2)}, u32[]{:S(2)}) collective-permute-start(bf16[64,15,128]{2,1,0:T(8,128)(2,1)S(1)} %get-tuple-element.62), channel_id=1, source_target_pairs={{0,1},{1,0},{2,3},{3,2},{4,5},{5,4},{6,7},{7,6},{8,9},{9,8},{10,11... | collective-permute-start | bytes 737288 | tf_op jit(solution)/shard_map/ppermute | solution.py:23
  21.7 1.0 %collective-permute-done.3 = bf16[64,15,128]{2,1,0:T(8,128)(2,1)S(1)} collective-permute-done((bf16[64,15,128]{2,1,0:T(8,128)(2,1)S(1)}, bf16[64,15,128]{2,1,0:T(8,128)(2,1)S(1)}, u32[]{:S(2)}, u32[]{:S(2)}) %collective-permute-start.3) | collective-permute-done | bytes 245792 | tf_op jit(solution)/shard_map/ppermute | solution.py:23
  23.7 1.6 %collective-permute-start.4 = (bf16[2,15,16,128]{3,1,2,0:T(8,128)(2,1)S(1)}, bf16[2,15,16,128]{3,1,2,0:T(8,128)(2,1)S(1)}, u32[]{:S(2)}, u32[]{:S(2)}) collective-permute-start(bf16[2,15,16,128]{3,1,2,0:T(8,128)(2,1)S(1)} %slice_select_fusion.3), channel_id=1, source_target_pairs={{0,2},{2,0},{1,3},{3,1},{4,6},{6,4},{5,7},{7,5},{8,10},{10,8},{9,1... | collective-permute-start | bytes 368648 | tf_op jit(solution)/shard_map/ppermute | solution.py:119
  25.3 3.5 %collective-permute-done.4 = bf16[2,15,16,128]{3,1,2,0:T(8,128)(2,1)S(1)} collective-permute-done((bf16[2,15,16,128]{3,1,2,0:T(8,128)(2,1)S(1)}, bf16[2,15,16,128]{3,1,2,0:T(8,128)(2,1)S(1)}, u32[]{:S(2)}, u32[]{:S(2)}) %collective-permute-start.4) | collective-permute-done | bytes 122912 | tf_op jit(solution)/shard_map/ppermute | solution.py:119
  30.8 6.4 %collective-permute-start.6 = (bf16[2,64,15,128]{3,2,1,0:T(8,128)(2,1)S(1)}, bf16[2,64,15,128]{3,2,1,0:T(8,128)(2,1)S(1)}, u32[]{:S(2)}, u32[]{:S(2)}) collective-permute-start(bf16[2,64,15,128]{3,2,1,0:T(8,128)(2,1)S(1)} %get-tuple-element.54), channel_id=1, source_target_pairs={{0,1},{1,0},{2,3},{3,2},{4,5},{5,4},{6,7},{7,6},{8,9},{9,8},{10,11... | collective-permute-start | bytes 1474568 | tf_op jit(solution)/shard_map/ppermute | solution.py:23
  37.3 1.4 %collective-permute-done.6 = bf16[2,64,15,128]{3,2,1,0:T(8,128)(2,1)S(1)} collective-permute-done((bf16[2,64,15,128]{3,2,1,0:T(8,128)(2,1)S(1)}, bf16[2,64,15,128]{3,2,1,0:T(8,128)(2,1)S(1)}, u32[]{:S(2)}, u32[]{:S(2)}) %collective-permute-start.6) | collective-permute-done | bytes 491552 | tf_op jit(solution)/shard_map/ppermute | solution.py:23
  39.9 1.6 %collective-permute-start.7 = (bf16[2,15,16,128]{3,1,2,0:T(8,128)(2,1)S(1)}, bf16[2,15,16,128]{3,1,2,0:T(8,128)(2,1)S(1)}, u32[]{:S(2)}, u32[]{:S(2)}) collective-permute-start(bf16[2,15,16,128]{3,1,2,0:T(8,128)(2,1)S(1)} %slice_select_fusion.2), channel_id=1, source_target_pairs={{0,2},{2,0},{1,3},{3,1},{4,6},{6,4},{5,7},{7,5},{8,10},{10,8},{9,1... | collective-permute-start | bytes 368648 | tf_op jit(solution)/shard_map/ppermute | solution.py:119
  41.5 3.5 %collective-permute-done.7 = bf16[2,15,16,128]{3,1,2,0:T(8,128)(2,1)S(1)} collective-permute-done((bf16[2,15,16,128]{3,1,2,0:T(8,128)(2,1)S(1)}, bf16[2,15,16,128]{3,1,2,0:T(8,128)(2,1)S(1)}, u32[]{:S(2)}, u32[]{:S(2)}) %collective-permute-start.7) | collective-permute-done | bytes 122912 | tf_op jit(solution)/shard_map/ppermute | solution.py:119
  46.9 8.8 %collective-permute-start.9 = (bf16[64,15,128]{2,1,0:T(8,128)(2,1)S(1)}, bf16[64,15,128]{2,1,0:T(8,128)(2,1)S(1)}, u32[]{:S(2)}, u32[]{:S(2)}) collective-permute-start(bf16[64,15,128]{2,1,0:T(8,128)(2,1)S(1)} %get-tuple-element.60), channel_id=1, source_target_pairs={{0,1},{1,0},{2,3},{3,2},{4,5},{5,4},{6,7},{7,6},{8,9},{9,8},{10,11... | collective-permute-start | bytes 737288 | tf_op jit(solution)/shard_map/ppermute | solution.py:23
  55.8 1.2 %collective-permute-done.9 = bf16[64,15,128]{2,1,0:T(8,128)(2,1)S(1)} collective-permute-done((bf16[64,15,128]{2,1,0:T(8,128)(2,1)S(1)}, bf16[64,15,128]{2,1,0:T(8,128)(2,1)S(1)}, u32[]{:S(2)}, u32[]{:S(2)}) %collective-permute-start.9) | collective-permute-done | bytes 245792 | tf_op jit(solution)/shard_map/ppermute | solution.py:23
  57.9 1.6 %collective-permute-start.10 = (bf16[2,15,16,128]{3,1,2,0:T(8,128)(2,1)S(1)}, bf16[2,15,16,128]{3,1,2,0:T(8,128)(2,1)S(1)}, u32[]{:S(2)}, u32[]{:S(2)}) collective-permute-start(bf16[2,15,16,128]{3,1,2,0:T(8,128)(2,1)S(1)} %slice_select_fusion.1), channel_id=1, source_target_pairs={{0,2},{2,0},{1,3},{3,1},{4,6},{6,4},{5,7},{7,5},{8,10},{10,8},{9,1... | collective-permute-start | bytes 368648 | tf_op jit(solution)/shard_map/ppermute | solution.py:119
  59.4 3.5 %collective-permute-done.10 = bf16[2,15,16,128]{3,1,2,0:T(8,128)(2,1)S(1)} collective-permute-done((bf16[2,15,16,128]{3,1,2,0:T(8,128)(2,1)S(1)}, bf16[2,15,16,128]{3,1,2,0:T(8,128)(2,1)S(1)}, u32[]{:S(2)}, u32[]{:S(2)}) %collective-permute-start.10) | collective-permute-done | bytes 122912 | tf_op jit(solution)/shard_map/ppermute | solution.py:119
  64.2 0.9 %collective-permute-start.11 = (bf16[2,64,15,128]{3,2,1,0:T(8,128)(2,1)S(1)}, bf16[2,64,15,128]{3,2,1,0:T(8,128)(2,1)S(1)}, u32[]{:S(2)}, u32[]{:S(2)}) collective-permute-start(bf16[2,64,15,128]{3,2,1,0:T(8,128)(2,1)S(1)} %get-tuple-element.49), channel_id=1, source_target_pairs={{1,4},{4,1},{3,6},{6,3},{5,8},{8,5},{7,10},{10,7},{9,12},{12,9},{1... | collective-permute-start | bytes 1474568 | tf_op jit(solution)/shard_map/ppermute | solution.py:140
  65.1 6.1 %collective-permute-start.12 = (bf16[2,64,15,128]{3,2,1,0:T(8,128)(2,1)S(1)}, bf16[2,64,15,128]{3,2,1,0:T(8,128)(2,1)S(1)}, u32[]{:S(2)}, u32[]{:S(2)}) collective-permute-start(bf16[2,64,15,128]{3,2,1,0:T(8,128)(2,1)S(1)} %get-tuple-element.50), channel_id=1, source_target_pairs={{0,1},{1,0},{2,3},{3,2},{4,5},{5,4},{6,7},{7,6},{8,9},{9,8},{10,11... | collective-permute-start | bytes 1474568 | tf_op jit(solution)/shard_map/ppermute | solution.py:23
  71.2 1.5 %collective-permute-done.12 = bf16[2,64,15,128]{3,2,1,0:T(8,128)(2,1)S(1)} collective-permute-done((bf16[2,64,15,128]{3,2,1,0:T(8,128)(2,1)S(1)}, bf16[2,64,15,128]{3,2,1,0:T(8,128)(2,1)S(1)}, u32[]{:S(2)}, u32[]{:S(2)}) %collective-permute-start.12) | collective-permute-done | bytes 491552 | tf_op jit(solution)/shard_map/ppermute | solution.py:23
  73.9 1.6 %collective-permute-start.13 = (bf16[2,15,16,128]{3,1,2,0:T(8,128)(2,1)S(1)}, bf16[2,15,16,128]{3,1,2,0:T(8,128)(2,1)S(1)}, u32[]{:S(2)}, u32[]{:S(2)}) collective-permute-start(bf16[2,15,16,128]{3,1,2,0:T(8,128)(2,1)S(1)} %slice_select_fusion), channel_id=1, source_target_pairs={{0,2},{2,0},{1,3},{3,1},{4,6},{6,4},{5,7},{7,5},{8,10},{10,8},{9,1... | collective-permute-start | bytes 368648 | tf_op jit(solution)/shard_map/ppermute | solution.py:119
  75.5 3.5 %collective-permute-done.13 = bf16[2,15,16,128]{3,1,2,0:T(8,128)(2,1)S(1)} collective-permute-done((bf16[2,15,16,128]{3,1,2,0:T(8,128)(2,1)S(1)}, bf16[2,15,16,128]{3,1,2,0:T(8,128)(2,1)S(1)}, u32[]{:S(2)}, u32[]{:S(2)}) %collective-permute-start.13) | collective-permute-done | bytes 122912 | tf_op jit(solution)/shard_map/ppermute | solution.py:119
  80.2 4.3 %collective-permute-start.14 = (f32[32,16,128]{2,1,0:T(8,128)S(1)}, f32[32,16,128]{2,1,0:T(8,128)S(1)}, u32[]{:S(2)}, u32[]{:S(2)}) collective-permute-start(f32[32,16,128]{2,1,0:T(8,128)S(1)} %dynamic-slice_bitcast_fusion), channel_id=1, source_target_pairs={{0,1},{1,0},{2,3},{3,2},{4,5},{5,4},{6,7},{7,6},{8,9},{9,8},{10,11... | collective-permute-start | bytes 786440 | tf_op jit(solution)/shard_map/ppermute | solution.py:23
  84.5 1.2 %collective-permute-done.14 = f32[32,16,128]{2,1,0:T(8,128)S(1)} collective-permute-done((f32[32,16,128]{2,1,0:T(8,128)S(1)}, f32[32,16,128]{2,1,0:T(8,128)S(1)}, u32[]{:S(2)}, u32[]{:S(2)}) %collective-permute-start.14) | collective-permute-done | bytes 262176 | tf_op jit(solution)/shard_map/ppermute | solution.py:23
  85.7 0.9 pad_maximum_fusion.1
  (99 shorter events, 16.0 us)
Async XLA Ops:
  0.0 3.0 %copy-start = (bf16[64,32,128]{2,1,0:T(8,128)(2,1)S(1)}, bf16[64,32,128]{2,1,0:T(8,128)(2,1)}, u32[]{:S(2)}) copy-start(bf16[64,32,128]{2,1,0:T(8,128)(2,1)} %param.3) | copy-start | bytes 1572868
  3.6 2.1 %collective-permute-start = (bf16[2,64,16,128]{3,2,1,0:T(8,128)(2,1)S(1)}, bf16[2,64,16,128]{3,2,1,0:T(8,128)(2,1)S(1)}, u32[]{:S(2)}, u32[]{:S(2)}) collective-permute-start(bf16[2,64,16,128]{3,2,1,0:T(8,128)(2,1)S(1)} %pad_maximum_fusion), channel_id=1, source_target_pairs={{0,1},{1,0},{2,3},{3,2},{4,5},{5,4},{6,7},{7,6},{8,9},{9,8},{10,11... | collective-permute-start | bytes 1572872 | tf_op jit(solution)/shard_map/ppermute | solution.py:23
  4.1 2.3 %copy-start.1 = (f32[2,3,31]{2,0,1:T(2,128)S(1)}, f32[2,3,31]{2,0,1:T(2,128)}, u32[]{:S(2)}) copy-start(f32[2,3,31]{2,0,1:T(2,128)} %param.4) | copy-start | bytes 2236
  5.8 3.2 %collective-permute-start.1 = (bf16[2,64,16,128]{3,2,1,0:T(8,128)(2,1)S(1)}, bf16[2,64,16,128]{3,2,1,0:T(8,128)(2,1)S(1)}, u32[]{:S(2)}, u32[]{:S(2)}) collective-permute-start(bf16[2,64,16,128]{3,2,1,0:T(8,128)(2,1)S(1)} %maximum_select_fusion.1), channel_id=1, source_target_pairs={{1,4},{4,1},{3,6},{6,3},{5,8},{8,5},{7,10},{10,7},{9,12},{12,9},{1... | collective-permute-start | bytes 1572872 | tf_op jit(solution)/shard_map/ppermute | solution.py:190
  9.2 12.5 %collective-permute-start.2 = (bf16[64,15,128]{2,1,0:T(8,128)(2,1)S(1)}, bf16[64,15,128]{2,1,0:T(8,128)(2,1)S(1)}, u32[]{:S(2)}, u32[]{:S(2)}) collective-permute-start(bf16[64,15,128]{2,1,0:T(8,128)(2,1)S(1)} %get-tuple-element.61), channel_id=1, source_target_pairs={{1,4},{4,1},{3,6},{6,3},{5,8},{8,5},{7,10},{10,7},{9,12},{12,9},{1... | collective-permute-start | bytes 737288 | tf_op jit(solution)/shard_map/ppermute | solution.py:140
  9.9 12.8 %collective-permute-start.3 = (bf16[64,15,128]{2,1,0:T(8,128)(2,1)S(1)}, bf16[64,15,128]{2,1,0:T(8,128)(2,1)S(1)}, u32[]{:S(2)}, u32[]{:S(2)}) collective-permute-start(bf16[64,15,128]{2,1,0:T(8,128)(2,1)S(1)} %get-tuple-element.62), channel_id=1, source_target_pairs={{0,1},{1,0},{2,3},{3,2},{4,5},{5,4},{6,7},{7,6},{8,9},{9,8},{10,11... | collective-permute-start | bytes 737288 | tf_op jit(solution)/shard_map/ppermute | solution.py:23
  23.7 5.0 %collective-permute-start.4 = (bf16[2,15,16,128]{3,1,2,0:T(8,128)(2,1)S(1)}, bf16[2,15,16,128]{3,1,2,0:T(8,128)(2,1)S(1)}, u32[]{:S(2)}, u32[]{:S(2)}) collective-permute-start(bf16[2,15,16,128]{3,1,2,0:T(8,128)(2,1)S(1)} %slice_select_fusion.3), channel_id=1, source_target_pairs={{0,2},{2,0},{1,3},{3,1},{4,6},{6,4},{5,7},{7,5},{8,10},{10,8},{9,1... | collective-permute-start | bytes 368648 | tf_op jit(solution)/shard_map/ppermute | solution.py:119
  30.1 7.2 %collective-permute-start.5 = (bf16[2,64,15,128]{3,2,1,0:T(8,128)(2,1)S(1)}, bf16[2,64,15,128]{3,2,1,0:T(8,128)(2,1)S(1)}, u32[]{:S(2)}, u32[]{:S(2)}) collective-permute-start(bf16[2,64,15,128]{3,2,1,0:T(8,128)(2,1)S(1)} %get-tuple-element.53), channel_id=1, source_target_pairs={{1,4},{4,1},{3,6},{6,3},{5,8},{8,5},{7,10},{10,7},{9,12},{12,9},{1... | collective-permute-start | bytes 1474568 | tf_op jit(solution)/shard_map/ppermute | solution.py:140
  30.8 7.9 %collective-permute-start.6 = (bf16[2,64,15,128]{3,2,1,0:T(8,128)(2,1)S(1)}, bf16[2,64,15,128]{3,2,1,0:T(8,128)(2,1)S(1)}, u32[]{:S(2)}, u32[]{:S(2)}) collective-permute-start(bf16[2,64,15,128]{3,2,1,0:T(8,128)(2,1)S(1)} %get-tuple-element.54), channel_id=1, source_target_pairs={{0,1},{1,0},{2,3},{3,2},{4,5},{5,4},{6,7},{7,6},{8,9},{9,8},{10,11... | collective-permute-start | bytes 1474568 | tf_op jit(solution)/shard_map/ppermute | solution.py:23
  39.9 5.0 %collective-permute-start.7 = (bf16[2,15,16,128]{3,1,2,0:T(8,128)(2,1)S(1)}, bf16[2,15,16,128]{3,1,2,0:T(8,128)(2,1)S(1)}, u32[]{:S(2)}, u32[]{:S(2)}) collective-permute-start(bf16[2,15,16,128]{3,1,2,0:T(8,128)(2,1)S(1)} %slice_select_fusion.2), channel_id=1, source_target_pairs={{0,2},{2,0},{1,3},{3,1},{4,6},{6,4},{5,7},{7,5},{8,10},{10,8},{9,1... | collective-permute-start | bytes 368648 | tf_op jit(solution)/shard_map/ppermute | solution.py:119
  46.2 9.5 %collective-permute-start.8 = (bf16[64,15,128]{2,1,0:T(8,128)(2,1)S(1)}, bf16[64,15,128]{2,1,0:T(8,128)(2,1)S(1)}, u32[]{:S(2)}, u32[]{:S(2)}) collective-permute-start(bf16[64,15,128]{2,1,0:T(8,128)(2,1)S(1)} %get-tuple-element.59), channel_id=1, source_target_pairs={{1,4},{4,1},{3,6},{6,3},{5,8},{8,5},{7,10},{10,7},{9,12},{12,9},{1... | collective-permute-start | bytes 737288 | tf_op jit(solution)/shard_map/ppermute | solution.py:140
  46.9 10.0 %collective-permute-start.9 = (bf16[64,15,128]{2,1,0:T(8,128)(2,1)S(1)}, bf16[64,15,128]{2,1,0:T(8,128)(2,1)S(1)}, u32[]{:S(2)}, u32[]{:S(2)}) collective-permute-start(bf16[64,15,128]{2,1,0:T(8,128)(2,1)S(1)} %get-tuple-element.60), channel_id=1, source_target_pairs={{0,1},{1,0},{2,3},{3,2},{4,5},{5,4},{6,7},{7,6},{8,9},{9,8},{10,11... | collective-permute-start | bytes 737288 | tf_op jit(solution)/shard_map/ppermute | solution.py:23
  57.9 5.0 %collective-permute-start.10 = (bf16[2,15,16,128]{3,1,2,0:T(8,128)(2,1)S(1)}, bf16[2,15,16,128]{3,1,2,0:T(8,128)(2,1)S(1)}, u32[]{:S(2)}, u32[]{:S(2)}) collective-permute-start(bf16[2,15,16,128]{3,1,2,0:T(8,128)(2,1)S(1)} %slice_select_fusion.1), channel_id=1, source_target_pairs={{0,2},{2,0},{1,3},{3,1},{4,6},{6,4},{5,7},{7,5},{8,10},{10,8},{9,1... | collective-permute-start | bytes 368648 | tf_op jit(solution)/shard_map/ppermute | solution.py:119
  64.2 7.0 %collective-permute-start.11 = (bf16[2,64,15,128]{3,2,1,0:T(8,128)(2,1)S(1)}, bf16[2,64,15,128]{3,2,1,0:T(8,128)(2,1)S(1)}, u32[]{:S(2)}, u32[]{:S(2)}) collective-permute-start(bf16[2,64,15,128]{3,2,1,0:T(8,128)(2,1)S(1)} %get-tuple-element.49), channel_id=1, source_target_pairs={{1,4},{4,1},{3,6},{6,3},{5,8},{8,5},{7,10},{10,7},{9,12},{12,9},{1... | collective-permute-start | bytes 1474568 | tf_op jit(solution)/shard_map/ppermute | solution.py:140
  65.1 7.6 %collective-permute-start.12 = (bf16[2,64,15,128]{3,2,1,0:T(8,128)(2,1)S(1)}, bf16[2,64,15,128]{3,2,1,0:T(8,128)(2,1)S(1)}, u32[]{:S(2)}, u32[]{:S(2)}) collective-permute-start(bf16[2,64,15,128]{3,2,1,0:T(8,128)(2,1)S(1)} %get-tuple-element.50), channel_id=1, source_target_pairs={{0,1},{1,0},{2,3},{3,2},{4,5},{5,4},{6,7},{7,6},{8,9},{9,8},{10,11... | collective-permute-start | bytes 1474568 | tf_op jit(solution)/shard_map/ppermute | solution.py:23
  73.9 5.0 %collective-permute-start.13 = (bf16[2,15,16,128]{3,1,2,0:T(8,128)(2,1)S(1)}, bf16[2,15,16,128]{3,1,2,0:T(8,128)(2,1)S(1)}, u32[]{:S(2)}, u32[]{:S(2)}) collective-permute-start(bf16[2,15,16,128]{3,1,2,0:T(8,128)(2,1)S(1)} %slice_select_fusion), channel_id=1, source_target_pairs={{0,2},{2,0},{1,3},{3,1},{4,6},{6,4},{5,7},{7,5},{8,10},{10,8},{9,1... | collective-permute-start | bytes 368648 | tf_op jit(solution)/shard_map/ppermute | solution.py:119
  80.2 5.4 %collective-permute-start.14 = (f32[32,16,128]{2,1,0:T(8,128)S(1)}, f32[32,16,128]{2,1,0:T(8,128)S(1)}, u32[]{:S(2)}, u32[]{:S(2)}) collective-permute-start(f32[32,16,128]{2,1,0:T(8,128)S(1)} %dynamic-slice_bitcast_fusion), channel_id=1, source_target_pairs={{0,1},{1,0},{2,3},{3,2},{4,5},{5,4},{6,7},{7,6},{8,9},{9,8},{10,11... | collective-permute-start | bytes 786440 | tf_op jit(solution)/shard_map/ppermute | solution.py:23

commit v23 on v21

--- a/solution.py
+++ b/solution.py
@@ -217,9 +217,8 @@
     keep = lax.dynamic_slice_in_dim(estimate, view_bit * half_rows, half_rows, 0)
     give = lax.dynamic_slice_in_dim(estimate, (1 - view_bit) * half_rows, half_rows, 0)
     got = from_partner(give, "view", 0)
-    first_half = jnp.where(view_bit == 0, keep, got)
-    second_half = jnp.where(view_bit == 0, got, keep)
-    return jnp.concatenate([first_half, second_half], axis=1)
+    both = jnp.concatenate([keep, got, keep], axis=1)
+    return lax.dynamic_slice_in_dim(both, view_bit * half_x, width_x, 1)
 
 
 def solution(mesh):

time: 85.8 us -> 85.8 us (level)
  no operation moved by 1% of the time
where the time goes in v23:
time: 85.8 us; the launch traced here: 85.4 us
  starting transfers between devices  47.6 us (55%)
  waiting for transfers between devices  21.7 us (25%)
  other arithmetic  7.2 us (8%)
  matrix products  5.1 us (6%)
  local copies, waits for them, and re-layouts  3.24 us (4%)
    ppermute x6, starting transfers between devices, from_partner(): return lax.ppermute(block, axis, route)  37.8 us
    ppermute x4, waiting for transfers between devices, z_rims(): got = lax.ppermute(payload, 'view', route)  13.9 us
    ppermute x6, waiting for transfers between devices, from_partner(): return lax.ppermute(block, axis, route)  7.8 us
    ppermute x4, starting transfers between devices, z_rims(): got = lax.ppermute(payload, 'view', route)  6.22 us
    ppermute x4, starting transfers between devices, x_rims(): across = lax.ppermute(outward, ('tile', 'view'), route)  2.92 us
  transfers between devices with their start and end apart: 15, of which 10 were waited for; matrix products, arithmetic and copies ran while one was open for 3% of the time, Pallas kernels for 0%

profile of v23, /device:TPU:0, one launch (start us, length us, event | category | flops | bytes accessed | tf_op | source)
XLA Modules:
  0.0 85.4 jit_solution(4093594166854345670)
XLA Ops:
  0.0 0.9 %fusion.73 = (s32[4]{0:T(128)S(1)}, s32[4]{0:T(128)S(1)}, s32[4]{0:T(128)S(1)}, s32[4]{0:T(128)S(1)}) fusion(s32[1,32]{1,0:T(1,128)} %param.5, s32[]{:T(128)S(6)} %select_n.338, s32[]{:T(128)S(6)} %select_n.339, s32[]{:T(128)S(6)} %select_n.341, s32[]{:T(128)S(6)} %select_n.340), kind=kLoop, calls=%fused_computation.184 | loop fusion | bytes 144 | tf_op jit(solution)/shard_map/dynamic_slice | solution.py:165
  1.0 0.8 gather_fusion
  3.0 1.5 %collective-permute-done = bf16[2,64,16,128]{3,2,1,0:T(8,128)(2,1)S(1)} collective-permute-done((bf16[2,64,16,128]{3,2,1,0:T(8,128)(2,1)S(1)}, bf16[2,64,16,128]{3,2,1,0:T(8,128)(2,1)S(1)}, u32[]{:S(2)}, u32[]{:S(2)}) %collective-permute-start) | collective-permute-done | bytes 524320 | tf_op jit(solution)/shard_map/ppermute | solution.py:23
  6.9 1.0 %select_reduce_fusion.1 = (bf16[128,128]{1,0:T(8,128)(2,1)S(1)}, bf16[128,128]{1,0:T(8,128)(2,1)S(1)}, bf16[128,128]{1,0:T(8,128)(2,1)S(1)}, bf16[128,128]{1,0:T(8,128)(2,1)S(1)}) fusion(f32[31]{0:T(128)S(1)} %get-tuple-element.74, s32[128,128]{1,0:T(8,128)S(1)} %subtract_add_fusion, f32[31]{0:T(128)S(1)} %get-tuple-element.75, f32[31]{0:T(128)S(1)} %get-tuple-element.89, ...), kind=kLoop, calls=%fused_computation.2 | loop fusion | flops 4505600 | bytes 197104 | tf_op jit(solution)/shard_map/reduce_sum | solution.py:45
  8.8 11.7 %collective-permute-start.3 = (bf16[64,15,128]{2,1,0:T(8,128)(2,1)S(1)}, bf16[64,15,128]{2,1,0:T(8,128)(2,1)S(1)}, u32[]{:S(2)}, u32[]{:S(2)}) collective-permute-start(bf16[64,15,128]{2,1,0:T(8,128)(2,1)S(1)} %get-tuple-element.62), channel_id=1, source_target_pairs={{0,1},{1,0},{2,3},{3,2},{4,5},{5,4},{6,7},{7,6},{8,9},{9,8},{10,11... | collective-permute-start | bytes 737288 | tf_op jit(solution)/shard_map/ppermute | solution.py:23
  20.6 1.0 %collective-permute-done.3 = bf16[64,15,128]{2,1,0:T(8,128)(2,1)S(1)} collective-permute-done((bf16[64,15,128]{2,1,0:T(8,128)(2,1)S(1)}, bf16[64,15,128]{2,1,0:T(8,128)(2,1)S(1)}, u32[]{:S(2)}, u32[]{:S(2)}) %collective-permute-start.3) | collective-permute-done | bytes 245792 | tf_op jit(solution)/shard_map/ppermute | solution.py:23
  22.6 1.6 %collective-permute-start.4 = (bf16[2,15,16,128]{3,1,2,0:T(8,128)(2,1)S(1)}, bf16[2,15,16,128]{3,1,2,0:T(8,128)(2,1)S(1)}, u32[]{:S(2)}, u32[]{:S(2)}) collective-permute-start(bf16[2,15,16,128]{3,1,2,0:T(8,128)(2,1)S(1)} %slice_select_fusion.3), channel_id=1, source_target_pairs={{0,2},{2,0},{1,3},{3,1},{4,6},{6,4},{5,7},{7,5},{8,10},{10,8},{9,1... | collective-permute-start | bytes 368648 | tf_op jit(solution)/shard_map/ppermute | solution.py:119
  24.1 3.5 %collective-permute-done.4 = bf16[2,15,16,128]{3,1,2,0:T(8,128)(2,1)S(1)} collective-permute-done((bf16[2,15,16,128]{3,1,2,0:T(8,128)(2,1)S(1)}, bf16[2,15,16,128]{3,1,2,0:T(8,128)(2,1)S(1)}, u32[]{:S(2)}, u32[]{:S(2)}) %collective-permute-start.4) | collective-permute-done | bytes 122912 | tf_op jit(solution)/shard_map/ppermute | solution.py:119
  29.7 6.4 %collective-permute-start.6 = (bf16[2,64,15,128]{3,2,1,0:T(8,128)(2,1)S(1)}, bf16[2,64,15,128]{3,2,1,0:T(8,128)(2,1)S(1)}, u32[]{:S(2)}, u32[]{:S(2)}) collective-permute-start(bf16[2,64,15,128]{3,2,1,0:T(8,128)(2,1)S(1)} %get-tuple-element.54), channel_id=1, source_target_pairs={{0,1},{1,0},{2,3},{3,2},{4,5},{5,4},{6,7},{7,6},{8,9},{9,8},{10,11... | collective-permute-start | bytes 1474568 | tf_op jit(solution)/shard_map/ppermute | solution.py:23
  36.2 1.4 %collective-permute-done.6 = bf16[2,64,15,128]{3,2,1,0:T(8,128)(2,1)S(1)} collective-permute-done((bf16[2,64,15,128]{3,2,1,0:T(8,128)(2,1)S(1)}, bf16[2,64,15,128]{3,2,1,0:T(8,128)(2,1)S(1)}, u32[]{:S(2)}, u32[]{:S(2)}) %collective-permute-start.6) | collective-permute-done | bytes 491552 | tf_op jit(solution)/shard_map/ppermute | solution.py:23
  38.8 1.6 %collective-permute-start.7 = (bf16[2,15,16,128]{3,1,2,0:T(8,128)(2,1)S(1)}, bf16[2,15,16,128]{3,1,2,0:T(8,128)(2,1)S(1)}, u32[]{:S(2)}, u32[]{:S(2)}) collective-permute-start(bf16[2,15,16,128]{3,1,2,0:T(8,128)(2,1)S(1)} %slice_select_fusion.2), channel_id=1, source_target_pairs={{0,2},{2,0},{1,3},{3,1},{4,6},{6,4},{5,7},{7,5},{8,10},{10,8},{9,1... | collective-permute-start | bytes 368648 | tf_op jit(solution)/shard_map/ppermute | solution.py:119
  40.3 3.5 %collective-permute-done.7 = bf16[2,15,16,128]{3,1,2,0:T(8,128)(2,1)S(1)} collective-permute-done((bf16[2,15,16,128]{3,1,2,0:T(8,128)(2,1)S(1)}, bf16[2,15,16,128]{3,1,2,0:T(8,128)(2,1)S(1)}, u32[]{:S(2)}, u32[]{:S(2)}) %collective-permute-start.7) | collective-permute-done | bytes 122912 | tf_op jit(solution)/shard_map/ppermute | solution.py:119
  45.8 8.8 %collective-permute-start.9 = (bf16[64,15,128]{2,1,0:T(8,128)(2,1)S(1)}, bf16[64,15,128]{2,1,0:T(8,128)(2,1)S(1)}, u32[]{:S(2)}, u32[]{:S(2)}) collective-permute-start(bf16[64,15,128]{2,1,0:T(8,128)(2,1)S(1)} %get-tuple-element.60), channel_id=1, source_target_pairs={{0,1},{1,0},{2,3},{3,2},{4,5},{5,4},{6,7},{7,6},{8,9},{9,8},{10,11... | collective-permute-start | bytes 737288 | tf_op jit(solution)/shard_map/ppermute | solution.py:23
  54.6 1.2 %collective-permute-done.9 = bf16[64,15,128]{2,1,0:T(8,128)(2,1)S(1)} collective-permute-done((bf16[64,15,128]{2,1,0:T(8,128)(2,1)S(1)}, bf16[64,15,128]{2,1,0:T(8,128)(2,1)S(1)}, u32[]{:S(2)}, u32[]{:S(2)}) %collective-permute-start.9) | collective-permute-done | bytes 245792 | tf_op jit(solution)/shard_map/ppermute | solution.py:23
  56.8 1.6 %collective-permute-start.10 = (bf16[2,15,16,128]{3,1,2,0:T(8,128)(2,1)S(1)}, bf16[2,15,16,128]{3,1,2,0:T(8,128)(2,1)S(1)}, u32[]{:S(2)}, u32[]{:S(2)}) collective-permute-start(bf16[2,15,16,128]{3,1,2,0:T(8,128)(2,1)S(1)} %slice_select_fusion.1), channel_id=1, source_target_pairs={{0,2},{2,0},{1,3},{3,1},{4,6},{6,4},{5,7},{7,5},{8,10},{10,8},{9,1... | collective-permute-start | bytes 368648 | tf_op jit(solution)/shard_map/ppermute | solution.py:119
  58.3 3.5 %collective-permute-done.10 = bf16[2,15,16,128]{3,1,2,0:T(8,128)(2,1)S(1)} collective-permute-done((bf16[2,15,16,128]{3,1,2,0:T(8,128)(2,1)S(1)}, bf16[2,15,16,128]{3,1,2,0:T(8,128)(2,1)S(1)}, u32[]{:S(2)}, u32[]{:S(2)}) %collective-permute-start.10) | collective-permute-done | bytes 122912 | tf_op jit(solution)/shard_map/ppermute | solution.py:119
  63.1 0.9 %collective-permute-start.11 = (bf16[2,64,15,128]{3,2,1,0:T(8,128)(2,1)S(1)}, bf16[2,64,15,128]{3,2,1,0:T(8,128)(2,1)S(1)}, u32[]{:S(2)}, u32[]{:S(2)}) collective-permute-start(bf16[2,64,15,128]{3,2,1,0:T(8,128)(2,1)S(1)} %get-tuple-element.49), channel_id=1, source_target_pairs={{1,4},{4,1},{3,6},{6,3},{5,8},{8,5},{7,10},{10,7},{9,12},{12,9},{1... | collective-permute-start | bytes 1474568 | tf_op jit(solution)/shard_map/ppermute | solution.py:140
  64.0 6.1 %collective-permute-start.12 = (bf16[2,64,15,128]{3,2,1,0:T(8,128)(2,1)S(1)}, bf16[2,64,15,128]{3,2,1,0:T(8,128)(2,1)S(1)}, u32[]{:S(2)}, u32[]{:S(2)}) collective-permute-start(bf16[2,64,15,128]{3,2,1,0:T(8,128)(2,1)S(1)} %get-tuple-element.50), channel_id=1, source_target_pairs={{0,1},{1,0},{2,3},{3,2},{4,5},{5,4},{6,7},{7,6},{8,9},{9,8},{10,11... | collective-permute-start | bytes 1474568 | tf_op jit(solution)/shard_map/ppermute | solution.py:23
  70.1 1.5 %collective-permute-done.12 = bf16[2,64,15,128]{3,2,1,0:T(8,128)(2,1)S(1)} collective-permute-done((bf16[2,64,15,128]{3,2,1,0:T(8,128)(2,1)S(1)}, bf16[2,64,15,128]{3,2,1,0:T(8,128)(2,1)S(1)}, u32[]{:S(2)}, u32[]{:S(2)}) %collective-permute-start.12) | collective-permute-done | bytes 491552 | tf_op jit(solution)/shard_map/ppermute | solution.py:23
  72.8 1.6 %collective-permute-start.13 = (bf16[2,15,16,128]{3,1,2,0:T(8,128)(2,1)S(1)}, bf16[2,15,16,128]{3,1,2,0:T(8,128)(2,1)S(1)}, u32[]{:S(2)}, u32[]{:S(2)}) collective-permute-start(bf16[2,15,16,128]{3,1,2,0:T(8,128)(2,1)S(1)} %slice_select_fusion), channel_id=1, source_target_pairs={{0,2},{2,0},{1,3},{3,1},{4,6},{6,4},{5,7},{7,5},{8,10},{10,8},{9,1... | collective-permute-start | bytes 368648 | tf_op jit(solution)/shard_map/ppermute | solution.py:119
  74.4 3.5 %collective-permute-done.13 = bf16[2,15,16,128]{3,1,2,0:T(8,128)(2,1)S(1)} collective-permute-done((bf16[2,15,16,128]{3,1,2,0:T(8,128)(2,1)S(1)}, bf16[2,15,16,128]{3,1,2,0:T(8,128)(2,1)S(1)}, u32[]{:S(2)}, u32[]{:S(2)}) %collective-permute-start.13) | collective-permute-done | bytes 122912 | tf_op jit(solution)/shard_map/ppermute | solution.py:119
  79.1 4.3 %collective-permute-start.14 = (f32[32,16,128]{2,1,0:T(8,128)S(1)}, f32[32,16,128]{2,1,0:T(8,128)S(1)}, u32[]{:S(2)}, u32[]{:S(2)}) collective-permute-start(f32[32,16,128]{2,1,0:T(8,128)S(1)} %get-tuple-element.47), channel_id=1, source_target_pairs={{0,1},{1,0},{2,3},{3,2},{4,5},{5,4},{6,7},{7,6},{8,9},{9,8},{10,11... | collective-permute-start | bytes 786440 | tf_op jit(solution)/shard_map/ppermute | solution.py:23
  83.3 1.2 %collective-permute-done.14 = f32[32,16,128]{2,1,0:T(8,128)S(1)} collective-permute-done((f32[32,16,128]{2,1,0:T(8,128)S(1)}, f32[32,16,128]{2,1,0:T(8,128)S(1)}, u32[]{:S(2)}, u32[]{:S(2)}) %collective-permute-start.14) | collective-permute-done | bytes 262176 | tf_op jit(solution)/shard_map/ppermute | solution.py:23
  84.5 0.9 %fusion.55 = f32[32,32,128]{2,1,0:T(8,128)} fusion(s32[]{:T(128)S(6)} %select_n.404, f32[32,16,128]{2,1,0:T(8,128)S(1)} %get-tuple-element.48, f32[32,16,128]{2,1,0:T(8,128)S(1)} %collective-permute-done.14), kind=kLoop, calls=%fused_computation.76 | loop fusion | flops 262144 | bytes 1048580 | tf_op jit(solution)/shard_map/concatenate | solution.py:220
  (93 shorter events, 15.3 us)
Async XLA Ops:
  0.0 1.8 %copy-start = (bf16[64,32,128]{2,1,0:T(8,128)(2,1)S(1)}, bf16[64,32,128]{2,1,0:T(8,128)(2,1)}, u32[]{:S(2)}) copy-start(bf16[64,32,128]{2,1,0:T(8,128)(2,1)} %param.3) | copy-start | bytes 1572868
  2.5 2.1 %collective-permute-start = (bf16[2,64,16,128]{3,2,1,0:T(8,128)(2,1)S(1)}, bf16[2,64,16,128]{3,2,1,0:T(8,128)(2,1)S(1)}, u32[]{:S(2)}, u32[]{:S(2)}) collective-permute-start(bf16[2,64,16,128]{3,2,1,0:T(8,128)(2,1)S(1)} %pad_maximum_fusion), channel_id=1, source_target_pairs={{0,1},{1,0},{2,3},{3,2},{4,5},{5,4},{6,7},{7,6},{8,9},{9,8},{10,11... | collective-permute-start | bytes 1572872 | tf_op jit(solution)/shard_map/ppermute | solution.py:23
  3.0 2.3 %copy-start.1 = (f32[2,3,31]{2,0,1:T(2,128)S(1)}, f32[2,3,31]{2,0,1:T(2,128)}, u32[]{:S(2)}) copy-start(f32[2,3,31]{2,0,1:T(2,128)} %param.4) | copy-start | bytes 2236
  4.7 3.2 %collective-permute-start.1 = (bf16[2,64,16,128]{3,2,1,0:T(8,128)(2,1)S(1)}, bf16[2,64,16,128]{3,2,1,0:T(8,128)(2,1)S(1)}, u32[]{:S(2)}, u32[]{:S(2)}) collective-permute-start(bf16[2,64,16,128]{3,2,1,0:T(8,128)(2,1)S(1)} %maximum_select_fusion.1), channel_id=1, source_target_pairs={{1,4},{4,1},{3,6},{6,3},{5,8},{8,5},{7,10},{10,7},{9,12},{12,9},{1... | collective-permute-start | bytes 1572872 | tf_op jit(solution)/shard_map/ppermute | solution.py:192
  8.1 12.5 %collective-permute-start.2 = (bf16[64,15,128]{2,1,0:T(8,128)(2,1)S(1)}, bf16[64,15,128]{2,1,0:T(8,128)(2,1)S(1)}, u32[]{:S(2)}, u32[]{:S(2)}) collective-permute-start(bf16[64,15,128]{2,1,0:T(8,128)(2,1)S(1)} %get-tuple-element.61), channel_id=1, source_target_pairs={{1,4},{4,1},{3,6},{6,3},{5,8},{8,5},{7,10},{10,7},{9,12},{12,9},{1... | collective-permute-start | bytes 737288 | tf_op jit(solution)/shard_map/ppermute | solution.py:140
  8.8 12.8 %collective-permute-start.3 = (bf16[64,15,128]{2,1,0:T(8,128)(2,1)S(1)}, bf16[64,15,128]{2,1,0:T(8,128)(2,1)S(1)}, u32[]{:S(2)}, u32[]{:S(2)}) collective-permute-start(bf16[64,15,128]{2,1,0:T(8,128)(2,1)S(1)} %get-tuple-element.62), channel_id=1, source_target_pairs={{0,1},{1,0},{2,3},{3,2},{4,5},{5,4},{6,7},{7,6},{8,9},{9,8},{10,11... | collective-permute-start | bytes 737288 | tf_op jit(solution)/shard_map/ppermute | solution.py:23
  22.6 5.0 %collective-permute-start.4 = (bf16[2,15,16,128]{3,1,2,0:T(8,128)(2,1)S(1)}, bf16[2,15,16,128]{3,1,2,0:T(8,128)(2,1)S(1)}, u32[]{:S(2)}, u32[]{:S(2)}) collective-permute-start(bf16[2,15,16,128]{3,1,2,0:T(8,128)(2,1)S(1)} %slice_select_fusion.3), channel_id=1, source_target_pairs={{0,2},{2,0},{1,3},{3,1},{4,6},{6,4},{5,7},{7,5},{8,10},{10,8},{9,1... | collective-permute-start | bytes 368648 | tf_op jit(solution)/shard_map/ppermute | solution.py:119
  29.0 7.2 %collective-permute-start.5 = (bf16[2,64,15,128]{3,2,1,0:T(8,128)(2,1)S(1)}, bf16[2,64,15,128]{3,2,1,0:T(8,128)(2,1)S(1)}, u32[]{:S(2)}, u32[]{:S(2)}) collective-permute-start(bf16[2,64,15,128]{3,2,1,0:T(8,128)(2,1)S(1)} %get-tuple-element.53), channel_id=1, source_target_pairs={{1,4},{4,1},{3,6},{6,3},{5,8},{8,5},{7,10},{10,7},{9,12},{12,9},{1... | collective-permute-start | bytes 1474568 | tf_op jit(solution)/shard_map/ppermute | solution.py:140
  29.7 7.9 %collective-permute-start.6 = (bf16[2,64,15,128]{3,2,1,0:T(8,128)(2,1)S(1)}, bf16[2,64,15,128]{3,2,1,0:T(8,128)(2,1)S(1)}, u32[]{:S(2)}, u32[]{:S(2)}) collective-permute-start(bf16[2,64,15,128]{3,2,1,0:T(8,128)(2,1)S(1)} %get-tuple-element.54), channel_id=1, source_target_pairs={{0,1},{1,0},{2,3},{3,2},{4,5},{5,4},{6,7},{7,6},{8,9},{9,8},{10,11... | collective-permute-start | bytes 1474568 | tf_op jit(solution)/shard_map/ppermute | solution.py:23
  38.8 5.0 %collective-permute-start.7 = (bf16[2,15,16,128]{3,1,2,0:T(8,128)(2,1)S(1)}, bf16[2,15,16,128]{3,1,2,0:T(8,128)(2,1)S(1)}, u32[]{:S(2)}, u32[]{:S(2)}) collective-permute-start(bf16[2,15,16,128]{3,1,2,0:T(8,128)(2,1)S(1)} %slice_select_fusion.2), channel_id=1, source_target_pairs={{0,2},{2,0},{1,3},{3,1},{4,6},{6,4},{5,7},{7,5},{8,10},{10,8},{9,1... | collective-permute-start | bytes 368648 | tf_op jit(solution)/shard_map/ppermute | solution.py:119
  45.1 9.5 %collective-permute-start.8 = (bf16[64,15,128]{2,1,0:T(8,128)(2,1)S(1)}, bf16[64,15,128]{2,1,0:T(8,128)(2,1)S(1)}, u32[]{:S(2)}, u32[]{:S(2)}) collective-permute-start(bf16[64,15,128]{2,1,0:T(8,128)(2,1)S(1)} %get-tuple-element.59), channel_id=1, source_target_pairs={{1,4},{4,1},{3,6},{6,3},{5,8},{8,5},{7,10},{10,7},{9,12},{12,9},{1... | collective-permute-start | bytes 737288 | tf_op jit(solution)/shard_map/ppermute | solution.py:140
  45.8 10.0 %collective-permute-start.9 = (bf16[64,15,128]{2,1,0:T(8,128)(2,1)S(1)}, bf16[64,15,128]{2,1,0:T(8,128)(2,1)S(1)}, u32[]{:S(2)}, u32[]{:S(2)}) collective-permute-start(bf16[64,15,128]{2,1,0:T(8,128)(2,1)S(1)} %get-tuple-element.60), channel_id=1, source_target_pairs={{0,1},{1,0},{2,3},{3,2},{4,5},{5,4},{6,7},{7,6},{8,9},{9,8},{10,11... | collective-permute-start | bytes 737288 | tf_op jit(solution)/shard_map/ppermute | solution.py:23
  56.8 5.0 %collective-permute-start.10 = (bf16[2,15,16,128]{3,1,2,0:T(8,128)(2,1)S(1)}, bf16[2,15,16,128]{3,1,2,0:T(8,128)(2,1)S(1)}, u32[]{:S(2)}, u32[]{:S(2)}) collective-permute-start(bf16[2,15,16,128]{3,1,2,0:T(8,128)(2,1)S(1)} %slice_select_fusion.1), channel_id=1, source_target_pairs={{0,2},{2,0},{1,3},{3,1},{4,6},{6,4},{5,7},{7,5},{8,10},{10,8},{9,1... | collective-permute-start | bytes 368648 | tf_op jit(solution)/shard_map/ppermute | solution.py:119
  63.1 7.0 %collective-permute-start.11 = (bf16[2,64,15,128]{3,2,1,0:T(8,128)(2,1)S(1)}, bf16[2,64,15,128]{3,2,1,0:T(8,128)(2,1)S(1)}, u32[]{:S(2)}, u32[]{:S(2)}) collective-permute-start(bf16[2,64,15,128]{3,2,1,0:T(8,128)(2,1)S(1)} %get-tuple-element.49), channel_id=1, source_target_pairs={{1,4},{4,1},{3,6},{6,3},{5,8},{8,5},{7,10},{10,7},{9,12},{12,9},{1... | collective-permute-start | bytes 1474568 | tf_op jit(solution)/shard_map/ppermute | solution.py:140
  64.0 7.6 %collective-permute-start.12 = (bf16[2,64,15,128]{3,2,1,0:T(8,128)(2,1)S(1)}, bf16[2,64,15,128]{3,2,1,0:T(8,128)(2,1)S(1)}, u32[]{:S(2)}, u32[]{:S(2)}) collective-permute-start(bf16[2,64,15,128]{3,2,1,0:T(8,128)(2,1)S(1)} %get-tuple-element.50), channel_id=1, source_target_pairs={{0,1},{1,0},{2,3},{3,2},{4,5},{5,4},{6,7},{7,6},{8,9},{9,8},{10,11... | collective-permute-start | bytes 1474568 | tf_op jit(solution)/shard_map/ppermute | solution.py:23
  72.8 5.0 %collective-permute-start.13 = (bf16[2,15,16,128]{3,1,2,0:T(8,128)(2,1)S(1)}, bf16[2,15,16,128]{3,1,2,0:T(8,128)(2,1)S(1)}, u32[]{:S(2)}, u32[]{:S(2)}) collective-permute-start(bf16[2,15,16,128]{3,1,2,0:T(8,128)(2,1)S(1)} %slice_select_fusion), channel_id=1, source_target_pairs={{0,2},{2,0},{1,3},{3,1},{4,6},{6,4},{5,7},{7,5},{8,10},{10,8},{9,1... | collective-permute-start | bytes 368648 | tf_op jit(solution)/shard_map/ppermute | solution.py:119
  79.1 5.4 %collective-permute-start.14 = (f32[32,16,128]{2,1,0:T(8,128)S(1)}, f32[32,16,128]{2,1,0:T(8,128)S(1)}, u32[]{:S(2)}, u32[]{:S(2)}) collective-permute-start(f32[32,16,128]{2,1,0:T(8,128)S(1)} %get-tuple-element.47), channel_id=1, source_target_pairs={{0,1},{1,0},{2,3},{3,2},{4,5},{5,4},{6,7},{7,6},{8,9},{9,8},{10,11... | collective-permute-start | bytes 786440 | tf_op jit(solution)/shard_map/ppermute | solution.py:23

commit v24 on v21

--- a/solution.py
+++ b/solution.py
@@ -93,8 +93,15 @@
 
 def pass_z_views(after_y, matrices, reach):
     below, above = z_rims(after_y, reach, 1)
-    widened = jnp.concatenate([below, after_y, above], axis=1)
-    return jnp.einsum("vpa,vaxy->vpxy", matrices, widened, preferred_element_type=jnp.float32)
+    planes = after_y.shape[1]
+    inner = jnp.einsum(
+        "vpa,vaxy->vpxy", matrices[:, :, reach : reach + planes], after_y, preferred_element_type=jnp.float32
+    )
+    lower = jnp.einsum("vpa,vaxy->vpxy", matrices[:, :, :reach], below, preferred_element_type=jnp.float32)
+    upper = jnp.einsum(
+        "vpa,vaxy->vpxy", matrices[:, :, reach + planes :], above, preferred_element_type=jnp.float32
+    )
+    return inner + lower + upper
 
 
 def z_rims(volume, reach, axis):

time: 85.8 us -> 91.7 us (1.069)
  other arithmetic: 7.2 us -> 12.3 us
  matrix products: 5.1 us -> 7.28 us
  waiting for transfers between devices: 21.7 us -> 20.3 us
    add x0 -> x2, other arithmetic: none -> 3.39 us  [pass_z_views(): return inner + lower + upper]
    convert_element_type x2, other arithmetic: 1.47 us -> 3.66 us  [local(): quotients = (observed / blurred).astype(jnp.bfloat16)]
    dot_general x4 -> x12, matrix products: 1.61 us -> 3.79 us  [the longest x4 1.37 us: pass_z_views(): jnp.einsum('vpa,vaxy->vpxy', matrices[:, :, reach:reach + planes], after_...]
    ppermute x4, waiting for transfers between devices: 13.9 us -> 12.5 us  [z_rims(): got = lax.ppermute(payload, 'view', route)]
  transfers between devices with their start and end apart: 15 -> 15, of which waited for: 10 -> 10; matrix products, arithmetic and copies ran while one was open for 3% -> 4% of each run, Pallas kernels for 0% -> 0%
where the time goes in v24:
time: 91.7 us; the launch traced here: 91.4 us
  starting transfers between devices  47.8 us (52%)
  waiting for transfers between devices  20.3 us (22%)
  other arithmetic  12.3 us (13%)
  matrix products  7.28 us (8%)
  local copies, waits for them, and re-layouts  3.09 us (3%)
    ppermute x6, starting transfers between devices, from_partner(): return lax.ppermute(block, axis, route)  38 us
    ppermute x4, waiting for transfers between devices, z_rims(): got = lax.ppermute(payload, 'view', route)  12.5 us
    ppermute x6, waiting for transfers between devices, from_partner(): return lax.ppermute(block, axis, route)  7.78 us
    ppermute x4, starting transfers between devices, z_rims(): got = lax.ppermute(payload, 'view', route)  6.25 us
    convert_element_type x2, other arithmetic, local(): quotients = (observed / blurred).astype(jnp.bfloat16)  3.66 us
    add x2, other arithmetic, pass_z_views(): return inner + lower + upper  3.39 us
    ppermute x4, starting transfers between devices, x_rims(): across = lax.ppermute(outward, ('tile', 'view'), route)  2.91 us
  transfers between devices with their start and end apart: 15, of which 10 were waited for; matrix products, arithmetic and copies ran while one was open for 4% of the time, Pallas kernels for 0%

profile of v24, /device:TPU:0, one launch (start us, length us, event | category | flops | bytes accessed | tf_op | source)
XLA Modules:
  0.0 91.4 jit_solution(8880995565228562960)
XLA Ops:
  3.0 1.5 %collective-permute-done = bf16[2,64,16,128]{3,2,1,0:T(8,128)(2,1)S(1)} collective-permute-done((bf16[2,64,16,128]{3,2,1,0:T(8,128)(2,1)S(1)}, bf16[2,64,16,128]{3,2,1,0:T(8,128)(2,1)S(1)}, u32[]{:S(2)}, u32[]{:S(2)}) %collective-permute-start) | collective-permute-done | bytes 524320 | tf_op jit(solution)/shard_map/ppermute | solution.py:23
  6.8 1.0 %select_reduce_fusion.1 = (bf16[128,128]{1,0:T(8,128)(2,1)S(1)}, bf16[128,128]{1,0:T(8,128)(2,1)S(1)}, bf16[128,128]{1,0:T(8,128)(2,1)S(1)}, bf16[128,128]{1,0:T(8,128)(2,1)S(1)}) fusion(f32[31]{0:T(128)S(1)} %get-tuple-element.62, s32[128,128]{1,0:T(8,128)S(1)} %subtract_add_fusion, f32[31]{0:T(128)S(1)} %get-tuple-element.63, f32[31]{0:T(128)S(1)} %get-tuple-element.77, ...), kind=kLoop, calls=%fused_computation.2 | loop fusion | flops 4505600 | bytes 197104 | tf_op jit(solution)/shard_map/reduce_sum | solution.py:45
  8.8 11.7 %collective-permute-start.3 = (bf16[64,15,128]{2,1,0:T(8,128)(2,1)S(1)}, bf16[64,15,128]{2,1,0:T(8,128)(2,1)S(1)}, u32[]{:S(2)}, u32[]{:S(2)}) collective-permute-start(bf16[64,15,128]{2,1,0:T(8,128)(2,1)S(1)} %get-tuple-element.58), channel_id=1, source_target_pairs={{0,1},{1,0},{2,3},{3,2},{4,5},{5,4},{6,7},{7,6},{8,9},{9,8},{10,11... | collective-permute-start | bytes 737288 | tf_op jit(solution)/shard_map/ppermute | solution.py:23
  20.6 1.0 %collective-permute-done.3 = bf16[64,15,128]{2,1,0:T(8,128)(2,1)S(1)} collective-permute-done((bf16[64,15,128]{2,1,0:T(8,128)(2,1)S(1)}, bf16[64,15,128]{2,1,0:T(8,128)(2,1)S(1)}, u32[]{:S(2)}, u32[]{:S(2)}) %collective-permute-start.3) | collective-permute-done | bytes 245792 | tf_op jit(solution)/shard_map/ppermute | solution.py:23
  22.6 1.6 %collective-permute-start.4 = (bf16[2,15,16,128]{3,1,2,0:T(8,128)(2,1)S(1)}, bf16[2,15,16,128]{3,1,2,0:T(8,128)(2,1)S(1)}, u32[]{:S(2)}, u32[]{:S(2)}) collective-permute-start(bf16[2,15,16,128]{3,1,2,0:T(8,128)(2,1)S(1)} %slice_select_fusion.3), channel_id=1, source_target_pairs={{0,2},{2,0},{1,3},{3,1},{4,6},{6,4},{5,7},{7,5},{8,10},{10,8},{9,1... | collective-permute-start | bytes 368648 | tf_op jit(solution)/shard_map/ppermute | solution.py:126
  24.5 3.1 %collective-permute-done.4 = bf16[2,15,16,128]{3,1,2,0:T(8,128)(2,1)S(1)} collective-permute-done((bf16[2,15,16,128]{3,1,2,0:T(8,128)(2,1)S(1)}, bf16[2,15,16,128]{3,1,2,0:T(8,128)(2,1)S(1)}, u32[]{:S(2)}, u32[]{:S(2)}) %collective-permute-start.4) | collective-permute-done | bytes 122912 | tf_op jit(solution)/shard_map/ppermute | solution.py:126
  28.2 1.8 %fusion.23 = bf16[2,64,16,128]{3,2,1,0:T(8,128)(2,1)S(1)} fusion(f32[2,64,16,128]{3,1,2,0:T(8,128)S(1)} %fusion.52, f32[2,64,16,128]{3,1,2,0:T(8,128)S(1)} %fusion.54, f32[2,64,16,128]{3,1,2,0:T(8,128)S(1)} %fusion.82, bf16[2,64,16,128]{3,2,1,0:T(8,128)(2,1)S(1)} %collective-permute-done.1, bf16[1,64,16,128]{3,2,1,0:T(8,128)(2,1)S(1)} %get-tuple-element.39, ...), kind=kLoop, calls=%fused_computation.39 | loop fusion | flops 2359296 | bytes 4718593 | tf_op jit(solution)/shard_map/convert_element_type | solution.py:216
  30.9 6.4 %collective-permute-start.6 = (bf16[2,64,15,128]{3,2,1,0:T(8,128)(2,1)S(1)}, bf16[2,64,15,128]{3,2,1,0:T(8,128)(2,1)S(1)}, u32[]{:S(2)}, u32[]{:S(2)}) collective-permute-start(bf16[2,64,15,128]{3,2,1,0:T(8,128)(2,1)S(1)} %get-tuple-element.50), channel_id=1, source_target_pairs={{0,1},{1,0},{2,3},{3,2},{4,5},{5,4},{6,7},{7,6},{8,9},{9,8},{10,11... | collective-permute-start | bytes 1474568 | tf_op jit(solution)/shard_map/ppermute | solution.py:23
  37.5 1.4 %collective-permute-done.6 = bf16[2,64,15,128]{3,2,1,0:T(8,128)(2,1)S(1)} collective-permute-done((bf16[2,64,15,128]{3,2,1,0:T(8,128)(2,1)S(1)}, bf16[2,64,15,128]{3,2,1,0:T(8,128)(2,1)S(1)}, u32[]{:S(2)}, u32[]{:S(2)}) %collective-permute-start.6) | collective-permute-done | bytes 491552 | tf_op jit(solution)/shard_map/ppermute | solution.py:23
  40.0 1.6 %collective-permute-start.7 = (bf16[2,15,16,128]{3,1,2,0:T(8,128)(2,1)S(1)}, bf16[2,15,16,128]{3,1,2,0:T(8,128)(2,1)S(1)}, u32[]{:S(2)}, u32[]{:S(2)}) collective-permute-start(bf16[2,15,16,128]{3,1,2,0:T(8,128)(2,1)S(1)} %slice_select_fusion.2), channel_id=1, source_target_pairs={{0,2},{2,0},{1,3},{3,1},{4,6},{6,4},{5,7},{7,5},{8,10},{10,8},{9,1... | collective-permute-start | bytes 368648 | tf_op jit(solution)/shard_map/ppermute | solution.py:126
  41.9 3.1 %collective-permute-done.7 = bf16[2,15,16,128]{3,1,2,0:T(8,128)(2,1)S(1)} collective-permute-done((bf16[2,15,16,128]{3,1,2,0:T(8,128)(2,1)S(1)}, bf16[2,15,16,128]{3,1,2,0:T(8,128)(2,1)S(1)}, u32[]{:S(2)}, u32[]{:S(2)}) %collective-permute-start.7) | collective-permute-done | bytes 122912 | tf_op jit(solution)/shard_map/ppermute | solution.py:126
  45.7 1.7 %copy_add_fusion.4 = f32[2,64,16,128]{3,2,1,0:T(8,128)S(1)} fusion(f32[2,64,16,128]{3,1,2,0:T(8,128)S(1)} %fusion.48, f32[2,64,16,128]{3,1,2,0:T(8,128)S(1)} %fusion.50, f32[2,64,16,128]{3,1,2,0:T(8,128)S(1)} %fusion.86), kind=kLoop, calls=%fused_computation.35 | loop fusion | flops 524288 | bytes 4194304 | tf_op jit(solution)/shard_map/add | solution.py:104
  48.5 8.8 %collective-permute-start.9 = (bf16[64,15,128]{2,1,0:T(8,128)(2,1)S(1)}, bf16[64,15,128]{2,1,0:T(8,128)(2,1)S(1)}, u32[]{:S(2)}, u32[]{:S(2)}) collective-permute-start(bf16[64,15,128]{2,1,0:T(8,128)(2,1)S(1)} %get-tuple-element.56), channel_id=1, source_target_pairs={{0,1},{1,0},{2,3},{3,2},{4,5},{5,4},{6,7},{7,6},{8,9},{9,8},{10,11... | collective-permute-start | bytes 737288 | tf_op jit(solution)/shard_map/ppermute | solution.py:23
  57.3 1.2 %collective-permute-done.9 = bf16[64,15,128]{2,1,0:T(8,128)(2,1)S(1)} collective-permute-done((bf16[64,15,128]{2,1,0:T(8,128)(2,1)S(1)}, bf16[64,15,128]{2,1,0:T(8,128)(2,1)S(1)}, u32[]{:S(2)}, u32[]{:S(2)}) %collective-permute-start.9) | collective-permute-done | bytes 245792 | tf_op jit(solution)/shard_map/ppermute | solution.py:23
  59.4 1.6 %collective-permute-start.10 = (bf16[2,15,16,128]{3,1,2,0:T(8,128)(2,1)S(1)}, bf16[2,15,16,128]{3,1,2,0:T(8,128)(2,1)S(1)}, u32[]{:S(2)}, u32[]{:S(2)}) collective-permute-start(bf16[2,15,16,128]{3,1,2,0:T(8,128)(2,1)S(1)} %slice_select_fusion.1), channel_id=1, source_target_pairs={{0,2},{2,0},{1,3},{3,1},{4,6},{6,4},{5,7},{7,5},{8,10},{10,8},{9,1... | collective-permute-start | bytes 368648 | tf_op jit(solution)/shard_map/ppermute | solution.py:126
  61.4 3.1 %collective-permute-done.10 = bf16[2,15,16,128]{3,1,2,0:T(8,128)(2,1)S(1)} collective-permute-done((bf16[2,15,16,128]{3,1,2,0:T(8,128)(2,1)S(1)}, bf16[2,15,16,128]{3,1,2,0:T(8,128)(2,1)S(1)}, u32[]{:S(2)}, u32[]{:S(2)}) %collective-permute-start.10) | collective-permute-done | bytes 122912 | tf_op jit(solution)/shard_map/ppermute | solution.py:126
  65.1 1.8 %fusion.21 = bf16[2,64,16,128]{3,2,1,0:T(8,128)(2,1)S(1)} fusion(f32[2,64,16,128]{3,1,2,0:T(8,128)S(1)} %fusion.44, f32[2,64,16,128]{3,1,2,0:T(8,128)S(1)} %fusion.46, f32[2,64,16,128]{3,1,2,0:T(8,128)S(1)} %fusion.80, bf16[2,64,16,128]{3,2,1,0:T(8,128)(2,1)S(1)} %collective-permute-done.1, bf16[1,64,16,128]{3,2,1,0:T(8,128)(2,1)S(1)} %get-tuple-element.39, ...), kind=kLoop, calls=%fused_computation.33 | loop fusion | flops 2359296 | bytes 4718593 | tf_op jit(solution)/shard_map/convert_element_type | solution.py:216
  68.6 5.9 %collective-permute-start.12 = (bf16[2,64,15,128]{3,2,1,0:T(8,128)(2,1)S(1)}, bf16[2,64,15,128]{3,2,1,0:T(8,128)(2,1)S(1)}, u32[]{:S(2)}, u32[]{:S(2)}) collective-permute-start(bf16[2,64,15,128]{3,2,1,0:T(8,128)(2,1)S(1)} %get-tuple-element.46), channel_id=1, source_target_pairs={{0,1},{1,0},{2,3},{3,2},{4,5},{5,4},{6,7},{7,6},{8,9},{9,8},{10,11... | collective-permute-start | bytes 1474568 | tf_op jit(solution)/shard_map/ppermute | solution.py:23
  74.5 1.5 %collective-permute-done.12 = bf16[2,64,15,128]{3,2,1,0:T(8,128)(2,1)S(1)} collective-permute-done((bf16[2,64,15,128]{3,2,1,0:T(8,128)(2,1)S(1)}, bf16[2,64,15,128]{3,2,1,0:T(8,128)(2,1)S(1)}, u32[]{:S(2)}, u32[]{:S(2)}) %collective-permute-start.12) | collective-permute-done | bytes 491552 | tf_op jit(solution)/shard_map/ppermute | solution.py:23
  77.1 1.6 %collective-permute-start.13 = (bf16[2,15,16,128]{3,1,2,0:T(8,128)(2,1)S(1)}, bf16[2,15,16,128]{3,1,2,0:T(8,128)(2,1)S(1)}, u32[]{:S(2)}, u32[]{:S(2)}) collective-permute-start(bf16[2,15,16,128]{3,1,2,0:T(8,128)(2,1)S(1)} %slice_select_fusion), channel_id=1, source_target_pairs={{0,2},{2,0},{1,3},{3,1},{4,6},{6,4},{5,7},{7,5},{8,10},{10,8},{9,1... | collective-permute-start | bytes 368648 | tf_op jit(solution)/shard_map/ppermute | solution.py:126
  79.0 3.1 %collective-permute-done.13 = bf16[2,15,16,128]{3,1,2,0:T(8,128)(2,1)S(1)} collective-permute-done((bf16[2,15,16,128]{3,1,2,0:T(8,128)(2,1)S(1)}, bf16[2,15,16,128]{3,1,2,0:T(8,128)(2,1)S(1)}, u32[]{:S(2)}, u32[]{:S(2)}) %collective-permute-start.13) | collective-permute-done | bytes 122912 | tf_op jit(solution)/shard_map/ppermute | solution.py:126
  82.8 1.7 %copy_add_fusion = f32[2,64,16,128]{3,2,1,0:T(8,128)S(1)} fusion(f32[2,64,16,128]{3,1,2,0:T(8,128)S(1)} %fusion.40, f32[2,64,16,128]{3,1,2,0:T(8,128)S(1)} %fusion.42, f32[2,64,16,128]{3,1,2,0:T(8,128)S(1)} %fusion.84), kind=kLoop, calls=%fused_computation.29 | loop fusion | flops 524288 | bytes 4194304 | tf_op jit(solution)/shard_map/add | solution.py:104
  84.6 4.7 %collective-permute-start.14 = (f32[32,16,128]{2,1,0:T(8,128)S(1)}, f32[32,16,128]{2,1,0:T(8,128)S(1)}, u32[]{:S(2)}, u32[]{:S(2)}) collective-permute-start(f32[32,16,128]{2,1,0:T(8,128)S(1)} %dynamic-slice_bitcast_fusion), channel_id=1, source_target_pairs={{0,1},{1,0},{2,3},{3,2},{4,5},{5,4},{6,7},{7,6},{8,9},{9,8},{10,11... | collective-permute-start | bytes 786440 | tf_op jit(solution)/shard_map/ppermute | solution.py:23
  89.3 1.2 %collective-permute-done.14 = f32[32,16,128]{2,1,0:T(8,128)S(1)} collective-permute-done((f32[32,16,128]{2,1,0:T(8,128)S(1)}, f32[32,16,128]{2,1,0:T(8,128)S(1)}, u32[]{:S(2)}, u32[]{:S(2)}) %collective-permute-start.14) | collective-permute-done | bytes 262176 | tf_op jit(solution)/shard_map/ppermute | solution.py:23
  (102 shorter events, 18.8 us)
Async XLA Ops:
  0.0 1.8 %copy-start = (bf16[64,32,128]{2,1,0:T(8,128)(2,1)S(1)}, bf16[64,32,128]{2,1,0:T(8,128)(2,1)}, u32[]{:S(2)}) copy-start(bf16[64,32,128]{2,1,0:T(8,128)(2,1)} %param.3) | copy-start | bytes 1572868
  2.5 2.1 %collective-permute-start = (bf16[2,64,16,128]{3,2,1,0:T(8,128)(2,1)S(1)}, bf16[2,64,16,128]{3,2,1,0:T(8,128)(2,1)S(1)}, u32[]{:S(2)}, u32[]{:S(2)}) collective-permute-start(bf16[2,64,16,128]{3,2,1,0:T(8,128)(2,1)S(1)} %pad_maximum_fusion), channel_id=1, source_target_pairs={{0,1},{1,0},{2,3},{3,2},{4,5},{5,4},{6,7},{7,6},{8,9},{9,8},{10,11... | collective-permute-start | bytes 1572872 | tf_op jit(solution)/shard_map/ppermute | solution.py:23
  3.0 2.3 %copy-start.3 = (f32[2,3,31]{2,0,1:T(2,128)S(1)}, f32[2,3,31]{2,0,1:T(2,128)}, u32[]{:S(2)}) copy-start(f32[2,3,31]{2,0,1:T(2,128)} %param.4) | copy-start | bytes 2236
  4.7 3.2 %collective-permute-start.1 = (bf16[2,64,16,128]{3,2,1,0:T(8,128)(2,1)S(1)}, bf16[2,64,16,128]{3,2,1,0:T(8,128)(2,1)S(1)}, u32[]{:S(2)}, u32[]{:S(2)}) collective-permute-start(bf16[2,64,16,128]{3,2,1,0:T(8,128)(2,1)S(1)} %maximum_select_fusion.1), channel_id=1, source_target_pairs={{1,4},{4,1},{3,6},{6,3},{5,8},{8,5},{7,10},{10,7},{9,12},{12,9},{1... | collective-permute-start | bytes 1572872 | tf_op jit(solution)/shard_map/ppermute | solution.py:199
  8.1 12.5 %collective-permute-start.2 = (bf16[64,15,128]{2,1,0:T(8,128)(2,1)S(1)}, bf16[64,15,128]{2,1,0:T(8,128)(2,1)S(1)}, u32[]{:S(2)}, u32[]{:S(2)}) collective-permute-start(bf16[64,15,128]{2,1,0:T(8,128)(2,1)S(1)} %get-tuple-element.57), channel_id=1, source_target_pairs={{1,4},{4,1},{3,6},{6,3},{5,8},{8,5},{7,10},{10,7},{9,12},{12,9},{1... | collective-permute-start | bytes 737288 | tf_op jit(solution)/shard_map/ppermute | solution.py:147
  8.8 12.8 %collective-permute-start.3 = (bf16[64,15,128]{2,1,0:T(8,128)(2,1)S(1)}, bf16[64,15,128]{2,1,0:T(8,128)(2,1)S(1)}, u32[]{:S(2)}, u32[]{:S(2)}) collective-permute-start(bf16[64,15,128]{2,1,0:T(8,128)(2,1)S(1)} %get-tuple-element.58), channel_id=1, source_target_pairs={{0,1},{1,0},{2,3},{3,2},{4,5},{5,4},{6,7},{7,6},{8,9},{9,8},{10,11... | collective-permute-start | bytes 737288 | tf_op jit(solution)/shard_map/ppermute | solution.py:23
  22.6 5.0 %collective-permute-start.4 = (bf16[2,15,16,128]{3,1,2,0:T(8,128)(2,1)S(1)}, bf16[2,15,16,128]{3,1,2,0:T(8,128)(2,1)S(1)}, u32[]{:S(2)}, u32[]{:S(2)}) collective-permute-start(bf16[2,15,16,128]{3,1,2,0:T(8,128)(2,1)S(1)} %slice_select_fusion.3), channel_id=1, source_target_pairs={{0,2},{2,0},{1,3},{3,1},{4,6},{6,4},{5,7},{7,5},{8,10},{10,8},{9,1... | collective-permute-start | bytes 368648 | tf_op jit(solution)/shard_map/ppermute | solution.py:126
  30.2 7.2 %collective-permute-start.5 = (bf16[2,64,15,128]{3,2,1,0:T(8,128)(2,1)S(1)}, bf16[2,64,15,128]{3,2,1,0:T(8,128)(2,1)S(1)}, u32[]{:S(2)}, u32[]{:S(2)}) collective-permute-start(bf16[2,64,15,128]{3,2,1,0:T(8,128)(2,1)S(1)} %get-tuple-element.49), channel_id=1, source_target_pairs={{1,4},{4,1},{3,6},{6,3},{5,8},{8,5},{7,10},{10,7},{9,12},{12,9},{1... | collective-permute-start | bytes 1474568 | tf_op jit(solution)/shard_map/ppermute | solution.py:147
  30.9 7.9 %collective-permute-start.6 = (bf16[2,64,15,128]{3,2,1,0:T(8,128)(2,1)S(1)}, bf16[2,64,15,128]{3,2,1,0:T(8,128)(2,1)S(1)}, u32[]{:S(2)}, u32[]{:S(2)}) collective-permute-start(bf16[2,64,15,128]{3,2,1,0:T(8,128)(2,1)S(1)} %get-tuple-element.50), channel_id=1, source_target_pairs={{0,1},{1,0},{2,3},{3,2},{4,5},{5,4},{6,7},{7,6},{8,9},{9,8},{10,11... | collective-permute-start | bytes 1474568 | tf_op jit(solution)/shard_map/ppermute | solution.py:23
  37.5 1.5 %copy-start.1 = (bf16[2,64,16,46]{3,2,1,0:T(8,128)(2,1)}, bf16[2,64,16,46]{3,2,1,0:T(8,128)(2,1)S(1)}, u32[]{:S(2)}) copy-start(bf16[2,64,16,46]{3,2,1,0:T(8,128)(2,1)S(1)} %broadcast_in_dim.193) | copy-start | bytes 565252
  40.0 5.0 %collective-permute-start.7 = (bf16[2,15,16,128]{3,1,2,0:T(8,128)(2,1)S(1)}, bf16[2,15,16,128]{3,1,2,0:T(8,128)(2,1)S(1)}, u32[]{:S(2)}, u32[]{:S(2)}) collective-permute-start(bf16[2,15,16,128]{3,1,2,0:T(8,128)(2,1)S(1)} %slice_select_fusion.2), channel_id=1, source_target_pairs={{0,2},{2,0},{1,3},{3,1},{4,6},{6,4},{5,7},{7,5},{8,10},{10,8},{9,1... | collective-permute-start | bytes 368648 | tf_op jit(solution)/shard_map/ppermute | solution.py:126
  47.6 9.7 %collective-permute-start.8 = (bf16[64,15,128]{2,1,0:T(8,128)(2,1)S(1)}, bf16[64,15,128]{2,1,0:T(8,128)(2,1)S(1)}, u32[]{:S(2)}, u32[]{:S(2)}) collective-permute-start(bf16[64,15,128]{2,1,0:T(8,128)(2,1)S(1)} %get-tuple-element.55), channel_id=1, source_target_pairs={{1,4},{4,1},{3,6},{6,3},{5,8},{8,5},{7,10},{10,7},{9,12},{12,9},{1... | collective-permute-start | bytes 737288 | tf_op jit(solution)/shard_map/ppermute | solution.py:147
  48.5 10.0 %collective-permute-start.9 = (bf16[64,15,128]{2,1,0:T(8,128)(2,1)S(1)}, bf16[64,15,128]{2,1,0:T(8,128)(2,1)S(1)}, u32[]{:S(2)}, u32[]{:S(2)}) collective-permute-start(bf16[64,15,128]{2,1,0:T(8,128)(2,1)S(1)} %get-tuple-element.56), channel_id=1, source_target_pairs={{0,1},{1,0},{2,3},{3,2},{4,5},{5,4},{6,7},{7,6},{8,9},{9,8},{10,11... | collective-permute-start | bytes 737288 | tf_op jit(solution)/shard_map/ppermute | solution.py:23
  59.4 5.0 %collective-permute-start.10 = (bf16[2,15,16,128]{3,1,2,0:T(8,128)(2,1)S(1)}, bf16[2,15,16,128]{3,1,2,0:T(8,128)(2,1)S(1)}, u32[]{:S(2)}, u32[]{:S(2)}) collective-permute-start(bf16[2,15,16,128]{3,1,2,0:T(8,128)(2,1)S(1)} %slice_select_fusion.1), channel_id=1, source_target_pairs={{0,2},{2,0},{1,3},{3,1},{4,6},{6,4},{5,7},{7,5},{8,10},{10,8},{9,1... | collective-permute-start | bytes 368648 | tf_op jit(solution)/shard_map/ppermute | solution.py:126
  67.9 6.6 %collective-permute-start.11 = (bf16[2,64,15,128]{3,2,1,0:T(8,128)(2,1)}, bf16[2,64,15,128]{3,2,1,0:T(8,128)(2,1)S(1)}, u32[]{:S(2)}, u32[]{:S(2)}) collective-permute-start(bf16[2,64,15,128]{3,2,1,0:T(8,128)(2,1)} %get-tuple-element.45), channel_id=1, source_target_pairs={{1,4},{4,1},{3,6},{6,3},{5,8},{8,5},{7,10},{10,7},{9,12},{12,9},{1... | collective-permute-start | bytes 1474568 | tf_op jit(solution)/shard_map/ppermute | solution.py:147
  68.6 7.4 %collective-permute-start.12 = (bf16[2,64,15,128]{3,2,1,0:T(8,128)(2,1)S(1)}, bf16[2,64,15,128]{3,2,1,0:T(8,128)(2,1)S(1)}, u32[]{:S(2)}, u32[]{:S(2)}) collective-permute-start(bf16[2,64,15,128]{3,2,1,0:T(8,128)(2,1)S(1)} %get-tuple-element.46), channel_id=1, source_target_pairs={{0,1},{1,0},{2,3},{3,2},{4,5},{5,4},{6,7},{7,6},{8,9},{9,8},{10,11... | collective-permute-start | bytes 1474568 | tf_op jit(solution)/shard_map/ppermute | solution.py:23
  74.5 1.6 %copy-start.2 = (bf16[2,64,16,46]{3,2,1,0:T(8,128)(2,1)S(1)}, bf16[2,64,16,46]{3,2,1,0:T(8,128)(2,1)}, u32[]{:S(2)}) copy-start(bf16[2,64,16,46]{3,2,1,0:T(8,128)(2,1)} %copy-done.1) | copy-start | bytes 565252
  77.1 5.0 %collective-permute-start.13 = (bf16[2,15,16,128]{3,1,2,0:T(8,128)(2,1)S(1)}, bf16[2,15,16,128]{3,1,2,0:T(8,128)(2,1)S(1)}, u32[]{:S(2)}, u32[]{:S(2)}) collective-permute-start(bf16[2,15,16,128]{3,1,2,0:T(8,128)(2,1)S(1)} %slice_select_fusion), channel_id=1, source_target_pairs={{0,2},{2,0},{1,3},{3,1},{4,6},{6,4},{5,7},{7,5},{8,10},{10,8},{9,1... | collective-permute-start | bytes 368648 | tf_op jit(solution)/shard_map/ppermute | solution.py:126
  84.6 5.8 %collective-permute-start.14 = (f32[32,16,128]{2,1,0:T(8,128)S(1)}, f32[32,16,128]{2,1,0:T(8,128)S(1)}, u32[]{:S(2)}, u32[]{:S(2)}) collective-permute-start(f32[32,16,128]{2,1,0:T(8,128)S(1)} %dynamic-slice_bitcast_fusion), channel_id=1, source_target_pairs={{0,1},{1,0},{2,3},{3,2},{4,5},{5,4},{6,7},{7,6},{8,9},{9,8},{10,11... | collective-permute-start | bytes 786440 | tf_op jit(solution)/shard_map/ppermute | solution.py:23

commit v25 on v21

--- a/solution.py
+++ b/solution.py
@@ -136,11 +136,12 @@
     front = lax.slice_in_dim(block, 0, reach, axis=axis)
     back = lax.slice_in_dim(block, width - reach, width, axis=axis)
     outward = jnp.where(first, front, back)
-    inward = jnp.where(first, back, front)
     across = lax.ppermute(outward, ("tile", "view"), route)
-    beside = from_partner(inward, "view", 0)
-    low = jnp.where(first, across, beside)
-    high = jnp.where(first, beside, across)
+    whole = from_partner(block, "view", 0)
+    beside_low = lax.slice_in_dim(whole, width - reach, width, axis=axis)
+    beside_high = lax.slice_in_dim(whole, 0, reach, axis=axis)
+    low = jnp.where(first, across, beside_low)
+    high = jnp.where(first, beside_high, across)
     return low, high
 
 

time: 85.8 us -> 88.5 us (1.031); the launches traced: 85.4 us -> 86.9 us
  starting transfers between devices: 47.6 us -> 52.6 us
  waiting for transfers between devices: 21.7 us -> 18.1 us
    ppermute x6, starting transfers between devices: 37.8 us -> 42.5 us  [from_partner(): return lax.ppermute(block, axis, route)]
    ppermute x6, waiting for transfers between devices: 7.8 us -> 4.46 us  [from_partner(): return lax.ppermute(block, axis, route)]
where the time goes in v25:
time: 88.5 us; the launch traced here: 86.9 us
  starting transfers between devices  52.6 us (59%)
  waiting for transfers between devices  18.1 us (20%)
  other arithmetic  7.3 us (8%)
  matrix products  5.1 us (6%)
  local copies, waits for them, and re-layouts  3.24 us (4%)
    ppermute x6, starting transfers between devices, from_partner(): return lax.ppermute(block, axis, route)  42.5 us
    ppermute x4, waiting for transfers between devices, z_rims(): got = lax.ppermute(payload, 'view', route)  13.7 us
    ppermute x4, starting transfers between devices, z_rims(): got = lax.ppermute(payload, 'view', route)  6.47 us
    ppermute x6, waiting for transfers between devices, from_partner(): return lax.ppermute(block, axis, route)  4.46 us
    ppermute x4, starting transfers between devices, x_rims(): across = lax.ppermute(outward, ('tile', 'view'), route)  2.91 us
  transfers between devices with their start and end apart: 15, of which 10 were waited for; matrix products, arithmetic and copies ran while one was open for 3% of the time, Pallas kernels for 0%

profile of v25, /device:TPU:0, one launch (start us, length us, event | category | flops | bytes accessed | tf_op | source)
XLA Modules:
  0.0 86.9 jit_solution(3651419134243547859)
XLA Ops:
  0.0 0.9 %fusion.70 = (s32[4]{0:T(128)S(1)}, s32[4]{0:T(128)S(1)}, s32[4]{0:T(128)S(1)}, s32[4]{0:T(128)S(1)}) fusion(s32[1,32]{1,0:T(1,128)} %param.5, s32[]{:T(128)S(6)} %select_n.332, s32[]{:T(128)S(6)} %select_n.333, s32[]{:T(128)S(6)} %select_n.335, s32[]{:T(128)S(6)} %select_n.334), kind=kLoop, calls=%fused_computation.176 | loop fusion | bytes 144 | tf_op jit(solution)/shard_map/dynamic_slice | solution.py:166
  1.0 0.8 gather_fusion
  3.0 1.5 %collective-permute-done = bf16[2,64,16,128]{3,2,1,0:T(8,128)(2,1)S(1)} collective-permute-done((bf16[2,64,16,128]{3,2,1,0:T(8,128)(2,1)S(1)}, bf16[2,64,16,128]{3,2,1,0:T(8,128)(2,1)S(1)}, u32[]{:S(2)}, u32[]{:S(2)}) %collective-permute-start) | collective-permute-done | bytes 524320 | tf_op jit(solution)/shard_map/ppermute | solution.py:23
  4.7 0.7 collective-permute-start.1
  6.9 1.0 %select_reduce_fusion.1 = (bf16[128,128]{1,0:T(8,128)(2,1)S(1)}, bf16[128,128]{1,0:T(8,128)(2,1)S(1)}, bf16[128,128]{1,0:T(8,128)(2,1)S(1)}, bf16[128,128]{1,0:T(8,128)(2,1)S(1)}) fusion(f32[31]{0:T(128)S(1)} %get-tuple-element.66, s32[128,128]{1,0:T(8,128)S(1)} %subtract_add_fusion, f32[31]{0:T(128)S(1)} %get-tuple-element.67, f32[31]{0:T(128)S(1)} %get-tuple-element.81, ...), kind=kLoop, calls=%fused_computation.2 | loop fusion | flops 4505600 | bytes 197104 | tf_op jit(solution)/shard_map/reduce_sum | solution.py:45
  8.1 8.7 %collective-permute-start.3 = (bf16[64,16,128]{2,1,0:T(8,128)(2,1)S(1)}, bf16[64,16,128]{2,1,0:T(8,128)(2,1)S(1)}, u32[]{:S(2)}, u32[]{:S(2)}) collective-permute-start(bf16[64,16,128]{2,1,0:T(8,128)(2,1)S(1)} %convert_bitcast_fusion.1), channel_id=1, source_target_pairs={{0,1},{1,0},{2,3},{3,2},{4,5},{5,4},{6,7},{7,6},{8,9},{9,8},{10,11... | collective-permute-start | bytes 786440 | tf_op jit(solution)/shard_map/ppermute | solution.py:23
  19.0 1.7 %collective-permute-start.4 = (bf16[2,15,16,128]{3,1,2,0:T(8,128)(2,1)S(1)}, bf16[2,15,16,128]{3,1,2,0:T(8,128)(2,1)S(1)}, u32[]{:S(2)}, u32[]{:S(2)}) collective-permute-start(bf16[2,15,16,128]{3,1,2,0:T(8,128)(2,1)S(1)} %slice_select_fusion.15), channel_id=1, source_target_pairs={{0,2},{2,0},{1,3},{3,1},{4,6},{6,4},{5,7},{7,5},{8,10},{10,8},{9,1... | collective-permute-start | bytes 368648 | tf_op jit(solution)/shard_map/ppermute | solution.py:119
  20.7 3.3 %collective-permute-done.4 = bf16[2,15,16,128]{3,1,2,0:T(8,128)(2,1)S(1)} collective-permute-done((bf16[2,15,16,128]{3,1,2,0:T(8,128)(2,1)S(1)}, bf16[2,15,16,128]{3,1,2,0:T(8,128)(2,1)S(1)}, u32[]{:S(2)}, u32[]{:S(2)}) %collective-permute-start.4) | collective-permute-done | bytes 122912 | tf_op jit(solution)/shard_map/ppermute | solution.py:119
  24.4 0.7 fusion.21
  25.2 5.6 %collective-permute-start.6 = (bf16[2,64,16,128]{3,2,1,0:T(8,128)(2,1)S(1)}, bf16[2,64,16,128]{3,2,1,0:T(8,128)(2,1)S(1)}, u32[]{:S(2)}, u32[]{:S(2)}) collective-permute-start(bf16[2,64,16,128]{3,2,1,0:T(8,128)(2,1)S(1)} %fusion.21), channel_id=1, source_target_pairs={{0,1},{1,0},{2,3},{3,2},{4,5},{5,4},{6,7},{7,6},{8,9},{9,8},{10,11... | collective-permute-start | bytes 1572872 | tf_op jit(solution)/shard_map/ppermute | solution.py:23
  33.5 1.6 %collective-permute-start.7 = (bf16[2,15,16,128]{3,1,2,0:T(8,128)(2,1)S(1)}, bf16[2,15,16,128]{3,1,2,0:T(8,128)(2,1)S(1)}, u32[]{:S(2)}, u32[]{:S(2)}) collective-permute-start(bf16[2,15,16,128]{3,1,2,0:T(8,128)(2,1)S(1)} %slice_select_fusion.14), channel_id=1, source_target_pairs={{0,2},{2,0},{1,3},{3,1},{4,6},{6,4},{5,7},{7,5},{8,10},{10,8},{9,1... | collective-permute-start | bytes 368648 | tf_op jit(solution)/shard_map/ppermute | solution.py:119
  35.1 3.4 %collective-permute-done.7 = bf16[2,15,16,128]{3,1,2,0:T(8,128)(2,1)S(1)} collective-permute-done((bf16[2,15,16,128]{3,1,2,0:T(8,128)(2,1)S(1)}, bf16[2,15,16,128]{3,1,2,0:T(8,128)(2,1)S(1)}, u32[]{:S(2)}, u32[]{:S(2)}) %collective-permute-start.7) | collective-permute-done | bytes 122912 | tf_op jit(solution)/shard_map/ppermute | solution.py:119
  39.1 0.7 convert_bitcast_fusion
  39.8 10.0 %collective-permute-start.9 = (bf16[64,16,128]{2,1,0:T(8,128)(2,1)S(1)}, bf16[64,16,128]{2,1,0:T(8,128)(2,1)S(1)}, u32[]{:S(2)}, u32[]{:S(2)}) collective-permute-start(bf16[64,16,128]{2,1,0:T(8,128)(2,1)S(1)} %get-tuple-element.33), channel_id=1, source_target_pairs={{0,1},{1,0},{2,3},{3,2},{4,5},{5,4},{6,7},{7,6},{8,9},{9,8},{10,11... | collective-permute-start | bytes 786440 | tf_op jit(solution)/shard_map/ppermute | solution.py:23
  51.9 1.6 %collective-permute-start.10 = (bf16[2,15,16,128]{3,1,2,0:T(8,128)(2,1)S(1)}, bf16[2,15,16,128]{3,1,2,0:T(8,128)(2,1)S(1)}, u32[]{:S(2)}, u32[]{:S(2)}) collective-permute-start(bf16[2,15,16,128]{3,1,2,0:T(8,128)(2,1)S(1)} %slice_select_fusion.13), channel_id=1, source_target_pairs={{0,2},{2,0},{1,3},{3,1},{4,6},{6,4},{5,7},{7,5},{8,10},{10,8},{9,1... | collective-permute-start | bytes 368648 | tf_op jit(solution)/shard_map/ppermute | solution.py:119
  53.5 3.5 %collective-permute-done.10 = bf16[2,15,16,128]{3,1,2,0:T(8,128)(2,1)S(1)} collective-permute-done((bf16[2,15,16,128]{3,1,2,0:T(8,128)(2,1)S(1)}, bf16[2,15,16,128]{3,1,2,0:T(8,128)(2,1)S(1)}, u32[]{:S(2)}, u32[]{:S(2)}) %collective-permute-start.10) | collective-permute-done | bytes 122912 | tf_op jit(solution)/shard_map/ppermute | solution.py:119
  57.4 0.7 fusion.20
  58.1 7.6 %collective-permute-start.12 = (bf16[2,64,16,128]{3,2,1,0:T(8,128)(2,1)S(1)}, bf16[2,64,16,128]{3,2,1,0:T(8,128)(2,1)S(1)}, u32[]{:S(2)}, u32[]{:S(2)}) collective-permute-start(bf16[2,64,16,128]{3,2,1,0:T(8,128)(2,1)S(1)} %fusion.20), channel_id=1, source_target_pairs={{0,1},{1,0},{2,3},{3,2},{4,5},{5,4},{6,7},{7,6},{8,9},{9,8},{10,11... | collective-permute-start | bytes 1572872 | tf_op jit(solution)/shard_map/ppermute | solution.py:23
  65.9 0.9 %collective-permute-start.11 = (bf16[2,64,15,128]{3,2,1,0:T(8,128)(2,1)S(1)}, bf16[2,64,15,128]{3,2,1,0:T(8,128)(2,1)S(1)}, u32[]{:S(2)}, u32[]{:S(2)}) collective-permute-start(bf16[2,64,15,128]{3,2,1,0:T(8,128)(2,1)S(1)} %slice_select_fusion.2), channel_id=1, source_target_pairs={{1,4},{4,1},{3,6},{6,3},{5,8},{8,5},{7,10},{10,7},{9,12},{12,9},{1... | collective-permute-start | bytes 1474568 | tf_op jit(solution)/shard_map/ppermute | solution.py:139
  68.5 1.6 %collective-permute-start.13 = (bf16[2,15,16,128]{3,1,2,0:T(8,128)(2,1)S(1)}, bf16[2,15,16,128]{3,1,2,0:T(8,128)(2,1)S(1)}, u32[]{:S(2)}, u32[]{:S(2)}) collective-permute-start(bf16[2,15,16,128]{3,1,2,0:T(8,128)(2,1)S(1)} %slice_select_fusion.12), channel_id=1, source_target_pairs={{0,2},{2,0},{1,3},{3,1},{4,6},{6,4},{5,7},{7,5},{8,10},{10,8},{9,1... | collective-permute-start | bytes 368648 | tf_op jit(solution)/shard_map/ppermute | solution.py:119
  70.1 3.5 %collective-permute-done.13 = bf16[2,15,16,128]{3,1,2,0:T(8,128)(2,1)S(1)} collective-permute-done((bf16[2,15,16,128]{3,1,2,0:T(8,128)(2,1)S(1)}, bf16[2,15,16,128]{3,1,2,0:T(8,128)(2,1)S(1)}, u32[]{:S(2)}, u32[]{:S(2)}) %collective-permute-start.13) | collective-permute-done | bytes 122912 | tf_op jit(solution)/shard_map/ppermute | solution.py:119
  74.7 10.1 %collective-permute-start.14 = (f32[32,16,128]{2,1,0:T(8,128)S(1)}, f32[32,16,128]{2,1,0:T(8,128)S(1)}, u32[]{:S(2)}, u32[]{:S(2)}) collective-permute-start(f32[32,16,128]{2,1,0:T(8,128)S(1)} %dynamic-slice_bitcast_fusion), channel_id=1, source_target_pairs={{0,1},{1,0},{2,3},{3,2},{4,5},{5,4},{6,7},{7,6},{8,9},{9,8},{10,11... | collective-permute-start | bytes 786440 | tf_op jit(solution)/shard_map/ppermute | solution.py:23
  84.8 1.2 %collective-permute-done.14 = f32[32,16,128]{2,1,0:T(8,128)S(1)} collective-permute-done((f32[32,16,128]{2,1,0:T(8,128)S(1)}, f32[32,16,128]{2,1,0:T(8,128)S(1)}, u32[]{:S(2)}, u32[]{:S(2)}) %collective-permute-start.14) | collective-permute-done | bytes 262176 | tf_op jit(solution)/shard_map/ppermute | solution.py:23
  86.1 0.9 pad_maximum_fusion.1
  (94 shorter events, 14.3 us)
Async XLA Ops:
  0.0 1.8 %copy-start = (bf16[64,32,128]{2,1,0:T(8,128)(2,1)S(1)}, bf16[64,32,128]{2,1,0:T(8,128)(2,1)}, u32[]{:S(2)}) copy-start(bf16[64,32,128]{2,1,0:T(8,128)(2,1)} %param.3) | copy-start | bytes 1572868
  2.5 2.1 %collective-permute-start = (bf16[2,64,16,128]{3,2,1,0:T(8,128)(2,1)S(1)}, bf16[2,64,16,128]{3,2,1,0:T(8,128)(2,1)S(1)}, u32[]{:S(2)}, u32[]{:S(2)}) collective-permute-start(bf16[2,64,16,128]{3,2,1,0:T(8,128)(2,1)S(1)} %pad_maximum_fusion), channel_id=1, source_target_pairs={{0,1},{1,0},{2,3},{3,2},{4,5},{5,4},{6,7},{7,6},{8,9},{9,8},{10,11... | collective-permute-start | bytes 1572872 | tf_op jit(solution)/shard_map/ppermute | solution.py:23
  3.0 2.3 %copy-start.1 = (f32[2,3,31]{2,0,1:T(2,128)S(1)}, f32[2,3,31]{2,0,1:T(2,128)}, u32[]{:S(2)}) copy-start(f32[2,3,31]{2,0,1:T(2,128)} %param.4) | copy-start | bytes 2236
  4.7 3.2 %collective-permute-start.1 = (bf16[2,64,16,128]{3,2,1,0:T(8,128)(2,1)S(1)}, bf16[2,64,16,128]{3,2,1,0:T(8,128)(2,1)S(1)}, u32[]{:S(2)}, u32[]{:S(2)}) collective-permute-start(bf16[2,64,16,128]{3,2,1,0:T(8,128)(2,1)S(1)} %maximum_select_fusion.1), channel_id=1, source_target_pairs={{1,4},{4,1},{3,6},{6,3},{5,8},{8,5},{7,10},{10,7},{9,12},{12,9},{1... | collective-permute-start | bytes 1572872 | tf_op jit(solution)/shard_map/ppermute | solution.py:193
  8.1 9.9 %collective-permute-start.3 = (bf16[64,16,128]{2,1,0:T(8,128)(2,1)S(1)}, bf16[64,16,128]{2,1,0:T(8,128)(2,1)S(1)}, u32[]{:S(2)}, u32[]{:S(2)}) collective-permute-start(bf16[64,16,128]{2,1,0:T(8,128)(2,1)S(1)} %convert_bitcast_fusion.1), channel_id=1, source_target_pairs={{0,1},{1,0},{2,3},{3,2},{4,5},{5,4},{6,7},{7,6},{8,9},{9,8},{10,11... | collective-permute-start | bytes 786440 | tf_op jit(solution)/shard_map/ppermute | solution.py:23
  16.8 0.8 collective-permute-start.2
  19.0 5.0 %collective-permute-start.4 = (bf16[2,15,16,128]{3,1,2,0:T(8,128)(2,1)S(1)}, bf16[2,15,16,128]{3,1,2,0:T(8,128)(2,1)S(1)}, u32[]{:S(2)}, u32[]{:S(2)}) collective-permute-start(bf16[2,15,16,128]{3,1,2,0:T(8,128)(2,1)S(1)} %slice_select_fusion.15), channel_id=1, source_target_pairs={{0,2},{2,0},{1,3},{3,1},{4,6},{6,4},{5,7},{7,5},{8,10},{10,8},{9,1... | collective-permute-start | bytes 368648 | tf_op jit(solution)/shard_map/ppermute | solution.py:119
  25.2 7.1 %collective-permute-start.6 = (bf16[2,64,16,128]{3,2,1,0:T(8,128)(2,1)S(1)}, bf16[2,64,16,128]{3,2,1,0:T(8,128)(2,1)S(1)}, u32[]{:S(2)}, u32[]{:S(2)}) collective-permute-start(bf16[2,64,16,128]{3,2,1,0:T(8,128)(2,1)S(1)} %fusion.21), channel_id=1, source_target_pairs={{0,1},{1,0},{2,3},{3,2},{4,5},{5,4},{6,7},{7,6},{8,9},{9,8},{10,11... | collective-permute-start | bytes 1572872 | tf_op jit(solution)/shard_map/ppermute | solution.py:23
  30.9 0.8 collective-permute-start.5
  33.5 5.0 %collective-permute-start.7 = (bf16[2,15,16,128]{3,1,2,0:T(8,128)(2,1)S(1)}, bf16[2,15,16,128]{3,1,2,0:T(8,128)(2,1)S(1)}, u32[]{:S(2)}, u32[]{:S(2)}) collective-permute-start(bf16[2,15,16,128]{3,1,2,0:T(8,128)(2,1)S(1)} %slice_select_fusion.14), channel_id=1, source_target_pairs={{0,2},{2,0},{1,3},{3,1},{4,6},{6,4},{5,7},{7,5},{8,10},{10,8},{9,1... | collective-permute-start | bytes 368648 | tf_op jit(solution)/shard_map/ppermute | solution.py:119
  39.8 11.2 %collective-permute-start.9 = (bf16[64,16,128]{2,1,0:T(8,128)(2,1)S(1)}, bf16[64,16,128]{2,1,0:T(8,128)(2,1)S(1)}, u32[]{:S(2)}, u32[]{:S(2)}) collective-permute-start(bf16[64,16,128]{2,1,0:T(8,128)(2,1)S(1)} %get-tuple-element.33), channel_id=1, source_target_pairs={{0,1},{1,0},{2,3},{3,2},{4,5},{5,4},{6,7},{7,6},{8,9},{9,8},{10,11... | collective-permute-start | bytes 786440 | tf_op jit(solution)/shard_map/ppermute | solution.py:23
  49.8 0.7 collective-permute-start.8
  51.9 5.0 %collective-permute-start.10 = (bf16[2,15,16,128]{3,1,2,0:T(8,128)(2,1)S(1)}, bf16[2,15,16,128]{3,1,2,0:T(8,128)(2,1)S(1)}, u32[]{:S(2)}, u32[]{:S(2)}) collective-permute-start(bf16[2,15,16,128]{3,1,2,0:T(8,128)(2,1)S(1)} %slice_select_fusion.13), channel_id=1, source_target_pairs={{0,2},{2,0},{1,3},{3,1},{4,6},{6,4},{5,7},{7,5},{8,10},{10,8},{9,1... | collective-permute-start | bytes 368648 | tf_op jit(solution)/shard_map/ppermute | solution.py:119
  58.1 9.2 %collective-permute-start.12 = (bf16[2,64,16,128]{3,2,1,0:T(8,128)(2,1)S(1)}, bf16[2,64,16,128]{3,2,1,0:T(8,128)(2,1)S(1)}, u32[]{:S(2)}, u32[]{:S(2)}) collective-permute-start(bf16[2,64,16,128]{3,2,1,0:T(8,128)(2,1)S(1)} %fusion.20), channel_id=1, source_target_pairs={{0,1},{1,0},{2,3},{3,2},{4,5},{5,4},{6,7},{7,6},{8,9},{9,8},{10,11... | collective-permute-start | bytes 1572872 | tf_op jit(solution)/shard_map/ppermute | solution.py:23
  65.9 0.9 %collective-permute-start.11 = (bf16[2,64,15,128]{3,2,1,0:T(8,128)(2,1)S(1)}, bf16[2,64,15,128]{3,2,1,0:T(8,128)(2,1)S(1)}, u32[]{:S(2)}, u32[]{:S(2)}) collective-permute-start(bf16[2,64,15,128]{3,2,1,0:T(8,128)(2,1)S(1)} %slice_select_fusion.2), channel_id=1, source_target_pairs={{1,4},{4,1},{3,6},{6,3},{5,8},{8,5},{7,10},{10,7},{9,12},{12,9},{1... | collective-permute-start | bytes 1474568 | tf_op jit(solution)/shard_map/ppermute | solution.py:139
  68.5 5.0 %collective-permute-start.13 = (bf16[2,15,16,128]{3,1,2,0:T(8,128)(2,1)S(1)}, bf16[2,15,16,128]{3,1,2,0:T(8,128)(2,1)S(1)}, u32[]{:S(2)}, u32[]{:S(2)}) collective-permute-start(bf16[2,15,16,128]{3,1,2,0:T(8,128)(2,1)S(1)} %slice_select_fusion.12), channel_id=1, source_target_pairs={{0,2},{2,0},{1,3},{3,1},{4,6},{6,4},{5,7},{7,5},{8,10},{10,8},{9,1... | collective-permute-start | bytes 368648 | tf_op jit(solution)/shard_map/ppermute | solution.py:119
  74.7 11.3 %collective-permute-start.14 = (f32[32,16,128]{2,1,0:T(8,128)S(1)}, f32[32,16,128]{2,1,0:T(8,128)S(1)}, u32[]{:S(2)}, u32[]{:S(2)}) collective-permute-start(f32[32,16,128]{2,1,0:T(8,128)S(1)} %dynamic-slice_bitcast_fusion), channel_id=1, source_target_pairs={{0,1},{1,0},{2,3},{3,2},{4,5},{5,4},{6,7},{7,6},{8,9},{9,8},{10,11... | collective-permute-start | bytes 786440 | tf_op jit(solution)/shard_map/ppermute | solution.py:23

commit v26 on v21

--- a/solution.py
+++ b/solution.py
@@ -187,11 +187,11 @@
             right_core = tile * views + 2 * slab + 1
             left_core = (tile + 1) * views + 2 * slab
             route += [(right_core, left_core), (left_core, right_core)]
-    outgoing = jnp.where(first, jnp.stack([cross_keep, got[1]]), jnp.stack([got[1], cross_keep]))
+    outgoing = jnp.stack([cross_keep, got[1]])
     outgoing, psf_taps = lax.optimization_barrier((outgoing, psf_taps))
-    incoming = lax.ppermute(outgoing, ("tile", "view"), route)
-    own_parts = jnp.where(first, jnp.stack([own_keep, got[0]]), jnp.stack([got[0], own_keep]))
-    views_measured = own_parts + incoming
+    arrived = lax.ppermute(outgoing, ("tile", "view"), route)
+    local = jnp.stack([own_keep, got[0]]) + arrived[::-1]
+    views_measured = jnp.where(first, local, local[::-1])
     observed = views_measured.astype(jnp.float32)
     estimate = 0.5 * (observed[0] + observed[1])
     kernels = (psf_taps / jnp.sum(psf_taps, axis=2, keepdims=True)).astype(jnp.bfloat16)

time: 85.8 us -> 85.6 us (level)
  no operation moved by 1% of the time
where the time goes in v26:
time: 85.6 us; the launch traced here: 85.3 us
  starting transfers between devices  47.6 us (56%)
  waiting for transfers between devices  21.7 us (25%)
  other arithmetic  7.04 us (8%)
  matrix products  5.09 us (6%)
  local copies, waits for them, and re-layouts  3.28 us (4%)
    ppermute x6, starting transfers between devices, from_partner(): return lax.ppermute(block, axis, route)  37.8 us
    ppermute x4, waiting for transfers between devices, z_rims(): got = lax.ppermute(payload, 'view', route)  13.9 us
    ppermute x6, waiting for transfers between devices, from_partner(): return lax.ppermute(block, axis, route)  7.8 us
    ppermute x4, starting transfers between devices, z_rims(): got = lax.ppermute(payload, 'view', route)  6.21 us
    ppermute x4, starting transfers between devices, x_rims(): across = lax.ppermute(outward, ('tile', 'view'), route)  2.92 us
  transfers between devices with their start and end apart: 15, of which 10 were waited for; matrix products, arithmetic and copies ran while one was open for 3% of the time, Pallas kernels for 0%

profile of v26, /device:TPU:0, one launch (start us, length us, event | category | flops | bytes accessed | tf_op | source)
XLA Modules:
  0.0 85.3 jit_solution(5108898790155132861)
XLA Ops:
  0.0 0.9 %fusion.69 = (s32[4]{0:T(128)S(1)}, s32[4]{0:T(128)S(1)}, s32[4]{0:T(128)S(1)}, s32[4]{0:T(128)S(1)}) fusion(s32[1,32]{1,0:T(1,128)} %param.5, s32[]{:T(128)S(6)} %select_n.344, s32[]{:T(128)S(6)} %select_n.345, s32[]{:T(128)S(6)} %select_n.347, s32[]{:T(128)S(6)} %select_n.346), kind=kLoop, calls=%fused_computation.180 | loop fusion | bytes 144 | tf_op jit(solution)/shard_map/dynamic_slice | solution.py:165
  1.0 0.8 gather_fusion
  3.0 1.5 %collective-permute-done = bf16[2,64,16,128]{3,2,1,0:T(8,128)(2,1)S(1)} collective-permute-done((bf16[2,64,16,128]{3,2,1,0:T(8,128)(2,1)S(1)}, bf16[2,64,16,128]{3,2,1,0:T(8,128)(2,1)S(1)}, u32[]{:S(2)}, u32[]{:S(2)}) %collective-permute-start) | collective-permute-done | bytes 524320 | tf_op jit(solution)/shard_map/ppermute | solution.py:23
  6.8 1.0 %select_reduce_fusion.1 = (bf16[128,128]{1,0:T(8,128)(2,1)S(1)}, bf16[128,128]{1,0:T(8,128)(2,1)S(1)}, bf16[128,128]{1,0:T(8,128)(2,1)S(1)}, bf16[128,128]{1,0:T(8,128)(2,1)S(1)}) fusion(f32[31]{0:T(128)S(1)} %get-tuple-element.74, s32[128,128]{1,0:T(8,128)S(1)} %subtract_add_fusion, f32[31]{0:T(128)S(1)} %get-tuple-element.75, f32[31]{0:T(128)S(1)} %get-tuple-element.89, ...), kind=kLoop, calls=%fused_computation.2 | loop fusion | flops 4505600 | bytes 197104 | tf_op jit(solution)/shard_map/reduce_sum | solution.py:45
  8.9 11.7 %collective-permute-start.3 = (bf16[64,15,128]{2,1,0:T(8,128)(2,1)S(1)}, bf16[64,15,128]{2,1,0:T(8,128)(2,1)S(1)}, u32[]{:S(2)}, u32[]{:S(2)}) collective-permute-start(bf16[64,15,128]{2,1,0:T(8,128)(2,1)S(1)} %get-tuple-element.62), channel_id=1, source_target_pairs={{0,1},{1,0},{2,3},{3,2},{4,5},{5,4},{6,7},{7,6},{8,9},{9,8},{10,11... | collective-permute-start | bytes 737288 | tf_op jit(solution)/shard_map/ppermute | solution.py:23
  20.7 1.0 %collective-permute-done.3 = bf16[64,15,128]{2,1,0:T(8,128)(2,1)S(1)} collective-permute-done((bf16[64,15,128]{2,1,0:T(8,128)(2,1)S(1)}, bf16[64,15,128]{2,1,0:T(8,128)(2,1)S(1)}, u32[]{:S(2)}, u32[]{:S(2)}) %collective-permute-start.3) | collective-permute-done | bytes 245792 | tf_op jit(solution)/shard_map/ppermute | solution.py:23
  22.7 1.6 %collective-permute-start.4 = (bf16[2,15,16,128]{3,1,2,0:T(8,128)(2,1)S(1)}, bf16[2,15,16,128]{3,1,2,0:T(8,128)(2,1)S(1)}, u32[]{:S(2)}, u32[]{:S(2)}) collective-permute-start(bf16[2,15,16,128]{3,1,2,0:T(8,128)(2,1)S(1)} %slice_select_fusion.3), channel_id=1, source_target_pairs={{0,2},{2,0},{1,3},{3,1},{4,6},{6,4},{5,7},{7,5},{8,10},{10,8},{9,1... | collective-permute-start | bytes 368648 | tf_op jit(solution)/shard_map/ppermute | solution.py:119
  24.2 3.5 %collective-permute-done.4 = bf16[2,15,16,128]{3,1,2,0:T(8,128)(2,1)S(1)} collective-permute-done((bf16[2,15,16,128]{3,1,2,0:T(8,128)(2,1)S(1)}, bf16[2,15,16,128]{3,1,2,0:T(8,128)(2,1)S(1)}, u32[]{:S(2)}, u32[]{:S(2)}) %collective-permute-start.4) | collective-permute-done | bytes 122912 | tf_op jit(solution)/shard_map/ppermute | solution.py:119
  29.7 6.4 %collective-permute-start.6 = (bf16[2,64,15,128]{3,2,1,0:T(8,128)(2,1)S(1)}, bf16[2,64,15,128]{3,2,1,0:T(8,128)(2,1)S(1)}, u32[]{:S(2)}, u32[]{:S(2)}) collective-permute-start(bf16[2,64,15,128]{3,2,1,0:T(8,128)(2,1)S(1)} %get-tuple-element.54), channel_id=1, source_target_pairs={{0,1},{1,0},{2,3},{3,2},{4,5},{5,4},{6,7},{7,6},{8,9},{9,8},{10,11... | collective-permute-start | bytes 1474568 | tf_op jit(solution)/shard_map/ppermute | solution.py:23
  36.2 1.4 %collective-permute-done.6 = bf16[2,64,15,128]{3,2,1,0:T(8,128)(2,1)S(1)} collective-permute-done((bf16[2,64,15,128]{3,2,1,0:T(8,128)(2,1)S(1)}, bf16[2,64,15,128]{3,2,1,0:T(8,128)(2,1)S(1)}, u32[]{:S(2)}, u32[]{:S(2)}) %collective-permute-start.6) | collective-permute-done | bytes 491552 | tf_op jit(solution)/shard_map/ppermute | solution.py:23
  38.7 1.6 %collective-permute-start.7 = (bf16[2,15,16,128]{3,1,2,0:T(8,128)(2,1)S(1)}, bf16[2,15,16,128]{3,1,2,0:T(8,128)(2,1)S(1)}, u32[]{:S(2)}, u32[]{:S(2)}) collective-permute-start(bf16[2,15,16,128]{3,1,2,0:T(8,128)(2,1)S(1)} %slice_select_fusion.2), channel_id=1, source_target_pairs={{0,2},{2,0},{1,3},{3,1},{4,6},{6,4},{5,7},{7,5},{8,10},{10,8},{9,1... | collective-permute-start | bytes 368648 | tf_op jit(solution)/shard_map/ppermute | solution.py:119
  40.3 3.5 %collective-permute-done.7 = bf16[2,15,16,128]{3,1,2,0:T(8,128)(2,1)S(1)} collective-permute-done((bf16[2,15,16,128]{3,1,2,0:T(8,128)(2,1)S(1)}, bf16[2,15,16,128]{3,1,2,0:T(8,128)(2,1)S(1)}, u32[]{:S(2)}, u32[]{:S(2)}) %collective-permute-start.7) | collective-permute-done | bytes 122912 | tf_op jit(solution)/shard_map/ppermute | solution.py:119
  45.8 8.8 %collective-permute-start.9 = (bf16[64,15,128]{2,1,0:T(8,128)(2,1)S(1)}, bf16[64,15,128]{2,1,0:T(8,128)(2,1)S(1)}, u32[]{:S(2)}, u32[]{:S(2)}) collective-permute-start(bf16[64,15,128]{2,1,0:T(8,128)(2,1)S(1)} %get-tuple-element.60), channel_id=1, source_target_pairs={{0,1},{1,0},{2,3},{3,2},{4,5},{5,4},{6,7},{7,6},{8,9},{9,8},{10,11... | collective-permute-start | bytes 737288 | tf_op jit(solution)/shard_map/ppermute | solution.py:23
  54.6 1.2 %collective-permute-done.9 = bf16[64,15,128]{2,1,0:T(8,128)(2,1)S(1)} collective-permute-done((bf16[64,15,128]{2,1,0:T(8,128)(2,1)S(1)}, bf16[64,15,128]{2,1,0:T(8,128)(2,1)S(1)}, u32[]{:S(2)}, u32[]{:S(2)}) %collective-permute-start.9) | collective-permute-done | bytes 245792 | tf_op jit(solution)/shard_map/ppermute | solution.py:23
  56.8 1.6 %collective-permute-start.10 = (bf16[2,15,16,128]{3,1,2,0:T(8,128)(2,1)S(1)}, bf16[2,15,16,128]{3,1,2,0:T(8,128)(2,1)S(1)}, u32[]{:S(2)}, u32[]{:S(2)}) collective-permute-start(bf16[2,15,16,128]{3,1,2,0:T(8,128)(2,1)S(1)} %slice_select_fusion.1), channel_id=1, source_target_pairs={{0,2},{2,0},{1,3},{3,1},{4,6},{6,4},{5,7},{7,5},{8,10},{10,8},{9,1... | collective-permute-start | bytes 368648 | tf_op jit(solution)/shard_map/ppermute | solution.py:119
  58.3 3.5 %collective-permute-done.10 = bf16[2,15,16,128]{3,1,2,0:T(8,128)(2,1)S(1)} collective-permute-done((bf16[2,15,16,128]{3,1,2,0:T(8,128)(2,1)S(1)}, bf16[2,15,16,128]{3,1,2,0:T(8,128)(2,1)S(1)}, u32[]{:S(2)}, u32[]{:S(2)}) %collective-permute-start.10) | collective-permute-done | bytes 122912 | tf_op jit(solution)/shard_map/ppermute | solution.py:119
  63.1 0.9 %collective-permute-start.11 = (bf16[2,64,15,128]{3,2,1,0:T(8,128)(2,1)S(1)}, bf16[2,64,15,128]{3,2,1,0:T(8,128)(2,1)S(1)}, u32[]{:S(2)}, u32[]{:S(2)}) collective-permute-start(bf16[2,64,15,128]{3,2,1,0:T(8,128)(2,1)S(1)} %get-tuple-element.49), channel_id=1, source_target_pairs={{1,4},{4,1},{3,6},{6,3},{5,8},{8,5},{7,10},{10,7},{9,12},{12,9},{1... | collective-permute-start | bytes 1474568 | tf_op jit(solution)/shard_map/ppermute | solution.py:140
  64.0 6.1 %collective-permute-start.12 = (bf16[2,64,15,128]{3,2,1,0:T(8,128)(2,1)S(1)}, bf16[2,64,15,128]{3,2,1,0:T(8,128)(2,1)S(1)}, u32[]{:S(2)}, u32[]{:S(2)}) collective-permute-start(bf16[2,64,15,128]{3,2,1,0:T(8,128)(2,1)S(1)} %get-tuple-element.50), channel_id=1, source_target_pairs={{0,1},{1,0},{2,3},{3,2},{4,5},{5,4},{6,7},{7,6},{8,9},{9,8},{10,11... | collective-permute-start | bytes 1474568 | tf_op jit(solution)/shard_map/ppermute | solution.py:23
  70.0 1.5 %collective-permute-done.12 = bf16[2,64,15,128]{3,2,1,0:T(8,128)(2,1)S(1)} collective-permute-done((bf16[2,64,15,128]{3,2,1,0:T(8,128)(2,1)S(1)}, bf16[2,64,15,128]{3,2,1,0:T(8,128)(2,1)S(1)}, u32[]{:S(2)}, u32[]{:S(2)}) %collective-permute-start.12) | collective-permute-done | bytes 491552 | tf_op jit(solution)/shard_map/ppermute | solution.py:23
  72.7 1.6 %collective-permute-start.13 = (bf16[2,15,16,128]{3,1,2,0:T(8,128)(2,1)S(1)}, bf16[2,15,16,128]{3,1,2,0:T(8,128)(2,1)S(1)}, u32[]{:S(2)}, u32[]{:S(2)}) collective-permute-start(bf16[2,15,16,128]{3,1,2,0:T(8,128)(2,1)S(1)} %slice_select_fusion), channel_id=1, source_target_pairs={{0,2},{2,0},{1,3},{3,1},{4,6},{6,4},{5,7},{7,5},{8,10},{10,8},{9,1... | collective-permute-start | bytes 368648 | tf_op jit(solution)/shard_map/ppermute | solution.py:119
  74.2 3.5 %collective-permute-done.13 = bf16[2,15,16,128]{3,1,2,0:T(8,128)(2,1)S(1)} collective-permute-done((bf16[2,15,16,128]{3,1,2,0:T(8,128)(2,1)S(1)}, bf16[2,15,16,128]{3,1,2,0:T(8,128)(2,1)S(1)}, u32[]{:S(2)}, u32[]{:S(2)}) %collective-permute-start.13) | collective-permute-done | bytes 122912 | tf_op jit(solution)/shard_map/ppermute | solution.py:119
  78.9 4.3 %collective-permute-start.14 = (f32[32,16,128]{2,1,0:T(8,128)S(1)}, f32[32,16,128]{2,1,0:T(8,128)S(1)}, u32[]{:S(2)}, u32[]{:S(2)}) collective-permute-start(f32[32,16,128]{2,1,0:T(8,128)S(1)} %dynamic-slice_bitcast_fusion), channel_id=1, source_target_pairs={{0,1},{1,0},{2,3},{3,2},{4,5},{5,4},{6,7},{7,6},{8,9},{9,8},{10,11... | collective-permute-start | bytes 786440 | tf_op jit(solution)/shard_map/ppermute | solution.py:23
  83.2 1.2 %collective-permute-done.14 = f32[32,16,128]{2,1,0:T(8,128)S(1)} collective-permute-done((f32[32,16,128]{2,1,0:T(8,128)S(1)}, f32[32,16,128]{2,1,0:T(8,128)S(1)}, u32[]{:S(2)}, u32[]{:S(2)}) %collective-permute-start.14) | collective-permute-done | bytes 262176 | tf_op jit(solution)/shard_map/ppermute | solution.py:23
  84.4 0.9 %pad_maximum_fusion.2 = f32[32,32,128]{2,1,0:T(8,128)} fusion(f32[32,16,128]{2,1,0:T(8,128)S(1)} %get-tuple-element.48, f32[32,16,128]{2,1,0:T(8,128)S(1)} %get-tuple-element.47), kind=kLoop, calls=%fused_computation.79 | loop fusion | flops 131072 | bytes 1048576 | tf_op jit(solution)/shard_map/concatenate | solution.py:222
  (95 shorter events, 15.2 us)
Async XLA Ops:
  0.0 1.8 %copy-start = (bf16[64,32,128]{2,1,0:T(8,128)(2,1)S(1)}, bf16[64,32,128]{2,1,0:T(8,128)(2,1)}, u32[]{:S(2)}) copy-start(bf16[64,32,128]{2,1,0:T(8,128)(2,1)} %param.3) | copy-start | bytes 1572868
  2.5 2.1 %collective-permute-start = (bf16[2,64,16,128]{3,2,1,0:T(8,128)(2,1)S(1)}, bf16[2,64,16,128]{3,2,1,0:T(8,128)(2,1)S(1)}, u32[]{:S(2)}, u32[]{:S(2)}) collective-permute-start(bf16[2,64,16,128]{3,2,1,0:T(8,128)(2,1)S(1)} %pad_maximum_fusion), channel_id=1, source_target_pairs={{0,1},{1,0},{2,3},{3,2},{4,5},{5,4},{6,7},{7,6},{8,9},{9,8},{10,11... | collective-permute-start | bytes 1572872 | tf_op jit(solution)/shard_map/ppermute | solution.py:23
  3.0 2.3 %copy-start.1 = (f32[2,3,31]{2,0,1:T(2,128)S(1)}, f32[2,3,31]{2,0,1:T(2,128)}, u32[]{:S(2)}) copy-start(f32[2,3,31]{2,0,1:T(2,128)} %param.4) | copy-start | bytes 2236
  4.6 3.2 %collective-permute-start.1 = (bf16[2,64,16,128]{3,2,1,0:T(8,128)(2,1)S(1)}, bf16[2,64,16,128]{3,2,1,0:T(8,128)(2,1)S(1)}, u32[]{:S(2)}, u32[]{:S(2)}) collective-permute-start(bf16[2,64,16,128]{3,2,1,0:T(8,128)(2,1)S(1)} %pad_maximum_fusion.1), channel_id=1, source_target_pairs={{1,4},{4,1},{3,6},{6,3},{5,8},{8,5},{7,10},{10,7},{9,12},{12,9},{1... | collective-permute-start | bytes 1572872 | tf_op jit(solution)/shard_map/ppermute | solution.py:192
  8.2 12.5 %collective-permute-start.2 = (bf16[64,15,128]{2,1,0:T(8,128)(2,1)S(1)}, bf16[64,15,128]{2,1,0:T(8,128)(2,1)S(1)}, u32[]{:S(2)}, u32[]{:S(2)}) collective-permute-start(bf16[64,15,128]{2,1,0:T(8,128)(2,1)S(1)} %get-tuple-element.61), channel_id=1, source_target_pairs={{1,4},{4,1},{3,6},{6,3},{5,8},{8,5},{7,10},{10,7},{9,12},{12,9},{1... | collective-permute-start | bytes 737288 | tf_op jit(solution)/shard_map/ppermute | solution.py:140
  8.9 12.8 %collective-permute-start.3 = (bf16[64,15,128]{2,1,0:T(8,128)(2,1)S(1)}, bf16[64,15,128]{2,1,0:T(8,128)(2,1)S(1)}, u32[]{:S(2)}, u32[]{:S(2)}) collective-permute-start(bf16[64,15,128]{2,1,0:T(8,128)(2,1)S(1)} %get-tuple-element.62), channel_id=1, source_target_pairs={{0,1},{1,0},{2,3},{3,2},{4,5},{5,4},{6,7},{7,6},{8,9},{9,8},{10,11... | collective-permute-start | bytes 737288 | tf_op jit(solution)/shard_map/ppermute | solution.py:23
  22.7 5.0 %collective-permute-start.4 = (bf16[2,15,16,128]{3,1,2,0:T(8,128)(2,1)S(1)}, bf16[2,15,16,128]{3,1,2,0:T(8,128)(2,1)S(1)}, u32[]{:S(2)}, u32[]{:S(2)}) collective-permute-start(bf16[2,15,16,128]{3,1,2,0:T(8,128)(2,1)S(1)} %slice_select_fusion.3), channel_id=1, source_target_pairs={{0,2},{2,0},{1,3},{3,1},{4,6},{6,4},{5,7},{7,5},{8,10},{10,8},{9,1... | collective-permute-start | bytes 368648 | tf_op jit(solution)/shard_map/ppermute | solution.py:119
  29.0 7.2 %collective-permute-start.5 = (bf16[2,64,15,128]{3,2,1,0:T(8,128)(2,1)S(1)}, bf16[2,64,15,128]{3,2,1,0:T(8,128)(2,1)S(1)}, u32[]{:S(2)}, u32[]{:S(2)}) collective-permute-start(bf16[2,64,15,128]{3,2,1,0:T(8,128)(2,1)S(1)} %get-tuple-element.53), channel_id=1, source_target_pairs={{1,4},{4,1},{3,6},{6,3},{5,8},{8,5},{7,10},{10,7},{9,12},{12,9},{1... | collective-permute-start | bytes 1474568 | tf_op jit(solution)/shard_map/ppermute | solution.py:140
  29.7 7.9 %collective-permute-start.6 = (bf16[2,64,15,128]{3,2,1,0:T(8,128)(2,1)S(1)}, bf16[2,64,15,128]{3,2,1,0:T(8,128)(2,1)S(1)}, u32[]{:S(2)}, u32[]{:S(2)}) collective-permute-start(bf16[2,64,15,128]{3,2,1,0:T(8,128)(2,1)S(1)} %get-tuple-element.54), channel_id=1, source_target_pairs={{0,1},{1,0},{2,3},{3,2},{4,5},{5,4},{6,7},{7,6},{8,9},{9,8},{10,11... | collective-permute-start | bytes 1474568 | tf_op jit(solution)/shard_map/ppermute | solution.py:23
  38.7 5.0 %collective-permute-start.7 = (bf16[2,15,16,128]{3,1,2,0:T(8,128)(2,1)S(1)}, bf16[2,15,16,128]{3,1,2,0:T(8,128)(2,1)S(1)}, u32[]{:S(2)}, u32[]{:S(2)}) collective-permute-start(bf16[2,15,16,128]{3,1,2,0:T(8,128)(2,1)S(1)} %slice_select_fusion.2), channel_id=1, source_target_pairs={{0,2},{2,0},{1,3},{3,1},{4,6},{6,4},{5,7},{7,5},{8,10},{10,8},{9,1... | collective-permute-start | bytes 368648 | tf_op jit(solution)/shard_map/ppermute | solution.py:119
  45.1 9.5 %collective-permute-start.8 = (bf16[64,15,128]{2,1,0:T(8,128)(2,1)S(1)}, bf16[64,15,128]{2,1,0:T(8,128)(2,1)S(1)}, u32[]{:S(2)}, u32[]{:S(2)}) collective-permute-start(bf16[64,15,128]{2,1,0:T(8,128)(2,1)S(1)} %get-tuple-element.59), channel_id=1, source_target_pairs={{1,4},{4,1},{3,6},{6,3},{5,8},{8,5},{7,10},{10,7},{9,12},{12,9},{1... | collective-permute-start | bytes 737288 | tf_op jit(solution)/shard_map/ppermute | solution.py:140
  45.8 10.0 %collective-permute-start.9 = (bf16[64,15,128]{2,1,0:T(8,128)(2,1)S(1)}, bf16[64,15,128]{2,1,0:T(8,128)(2,1)S(1)}, u32[]{:S(2)}, u32[]{:S(2)}) collective-permute-start(bf16[64,15,128]{2,1,0:T(8,128)(2,1)S(1)} %get-tuple-element.60), channel_id=1, source_target_pairs={{0,1},{1,0},{2,3},{3,2},{4,5},{5,4},{6,7},{7,6},{8,9},{9,8},{10,11... | collective-permute-start | bytes 737288 | tf_op jit(solution)/shard_map/ppermute | solution.py:23
  56.8 5.0 %collective-permute-start.10 = (bf16[2,15,16,128]{3,1,2,0:T(8,128)(2,1)S(1)}, bf16[2,15,16,128]{3,1,2,0:T(8,128)(2,1)S(1)}, u32[]{:S(2)}, u32[]{:S(2)}) collective-permute-start(bf16[2,15,16,128]{3,1,2,0:T(8,128)(2,1)S(1)} %slice_select_fusion.1), channel_id=1, source_target_pairs={{0,2},{2,0},{1,3},{3,1},{4,6},{6,4},{5,7},{7,5},{8,10},{10,8},{9,1... | collective-permute-start | bytes 368648 | tf_op jit(solution)/shard_map/ppermute | solution.py:119
  63.1 7.0 %collective-permute-start.11 = (bf16[2,64,15,128]{3,2,1,0:T(8,128)(2,1)S(1)}, bf16[2,64,15,128]{3,2,1,0:T(8,128)(2,1)S(1)}, u32[]{:S(2)}, u32[]{:S(2)}) collective-permute-start(bf16[2,64,15,128]{3,2,1,0:T(8,128)(2,1)S(1)} %get-tuple-element.49), channel_id=1, source_target_pairs={{1,4},{4,1},{3,6},{6,3},{5,8},{8,5},{7,10},{10,7},{9,12},{12,9},{1... | collective-permute-start | bytes 1474568 | tf_op jit(solution)/shard_map/ppermute | solution.py:140
  64.0 7.6 %collective-permute-start.12 = (bf16[2,64,15,128]{3,2,1,0:T(8,128)(2,1)S(1)}, bf16[2,64,15,128]{3,2,1,0:T(8,128)(2,1)S(1)}, u32[]{:S(2)}, u32[]{:S(2)}) collective-permute-start(bf16[2,64,15,128]{3,2,1,0:T(8,128)(2,1)S(1)} %get-tuple-element.50), channel_id=1, source_target_pairs={{0,1},{1,0},{2,3},{3,2},{4,5},{5,4},{6,7},{7,6},{8,9},{9,8},{10,11... | collective-permute-start | bytes 1474568 | tf_op jit(solution)/shard_map/ppermute | solution.py:23
  72.7 5.0 %collective-permute-start.13 = (bf16[2,15,16,128]{3,1,2,0:T(8,128)(2,1)S(1)}, bf16[2,15,16,128]{3,1,2,0:T(8,128)(2,1)S(1)}, u32[]{:S(2)}, u32[]{:S(2)}) collective-permute-start(bf16[2,15,16,128]{3,1,2,0:T(8,128)(2,1)S(1)} %slice_select_fusion), channel_id=1, source_target_pairs={{0,2},{2,0},{1,3},{3,1},{4,6},{6,4},{5,7},{7,5},{8,10},{10,8},{9,1... | collective-permute-start | bytes 368648 | tf_op jit(solution)/shard_map/ppermute | solution.py:119
  78.9 5.4 %collective-permute-start.14 = (f32[32,16,128]{2,1,0:T(8,128)S(1)}, f32[32,16,128]{2,1,0:T(8,128)S(1)}, u32[]{:S(2)}, u32[]{:S(2)}) collective-permute-start(f32[32,16,128]{2,1,0:T(8,128)S(1)} %dynamic-slice_bitcast_fusion), channel_id=1, source_target_pairs={{0,1},{1,0},{2,3},{3,2},{4,5},{5,4},{6,7},{7,6},{8,9},{9,8},{10,11... | collective-permute-start | bytes 786440 | tf_op jit(solution)/shard_map/ppermute | solution.py:23

commit v27 on v26

--- a/solution.py
+++ b/solution.py
@@ -217,9 +217,8 @@
     keep = lax.dynamic_slice_in_dim(estimate, view_bit * half_rows, half_rows, 0)
     give = lax.dynamic_slice_in_dim(estimate, (1 - view_bit) * half_rows, half_rows, 0)
     got = from_partner(give, "view", 0)
-    first_half = jnp.where(view_bit == 0, keep, got)
-    second_half = jnp.where(view_bit == 0, got, keep)
-    return jnp.concatenate([first_half, second_half], axis=1)
+    both = jnp.concatenate([keep, got, keep], axis=1)
+    return lax.dynamic_slice_in_dim(both, view_bit * half_x, width_x, 1)
 
 
 def solution(mesh):

time: 85.6 us -> 85.6 us (level)
  no operation moved by 1% of the time
where the time goes in v27:
time: 85.6 us; the launch traced here: 85.2 us
  starting transfers between devices  47.6 us (56%)
  waiting for transfers between devices  21.7 us (25%)
  other arithmetic  7.01 us (8%)
  matrix products  5.08 us (6%)
  local copies, waits for them, and re-layouts  3.27 us (4%)
    ppermute x6, starting transfers between devices, from_partner(): return lax.ppermute(block, axis, route)  37.8 us
    ppermute x4, waiting for transfers between devices, z_rims(): got = lax.ppermute(payload, 'view', route)  13.9 us
    ppermute x6, waiting for transfers between devices, from_partner(): return lax.ppermute(block, axis, route)  7.8 us
    ppermute x4, starting transfers between devices, z_rims(): got = lax.ppermute(payload, 'view', route)  6.22 us
    ppermute x4, starting transfers between devices, x_rims(): across = lax.ppermute(outward, ('tile', 'view'), route)  2.92 us
  transfers between devices with their start and end apart: 15, of which 10 were waited for; matrix products, arithmetic and copies ran while one was open for 3% of the time, Pallas kernels for 0%

profile of v27, /device:TPU:0, one launch (start us, length us, event | category | flops | bytes accessed | tf_op | source)
XLA Modules:
  0.0 85.2 jit_solution(5503075761046255747)
XLA Ops:
  0.0 0.9 %fusion.72 = (s32[4]{0:T(128)S(1)}, s32[4]{0:T(128)S(1)}, s32[4]{0:T(128)S(1)}, s32[4]{0:T(128)S(1)}) fusion(s32[1,32]{1,0:T(1,128)} %param.5, s32[]{:T(128)S(6)} %select_n.334, s32[]{:T(128)S(6)} %select_n.335, s32[]{:T(128)S(6)} %select_n.337, s32[]{:T(128)S(6)} %select_n.336), kind=kLoop, calls=%fused_computation.184 | loop fusion | bytes 144 | tf_op jit(solution)/shard_map/dynamic_slice | solution.py:165
  1.0 0.8 gather_fusion
  3.0 1.5 %collective-permute-done = bf16[2,64,16,128]{3,2,1,0:T(8,128)(2,1)S(1)} collective-permute-done((bf16[2,64,16,128]{3,2,1,0:T(8,128)(2,1)S(1)}, bf16[2,64,16,128]{3,2,1,0:T(8,128)(2,1)S(1)}, u32[]{:S(2)}, u32[]{:S(2)}) %collective-permute-start) | collective-permute-done | bytes 524320 | tf_op jit(solution)/shard_map/ppermute | solution.py:23
  6.8 1.0 %select_reduce_fusion.1 = (bf16[128,128]{1,0:T(8,128)(2,1)S(1)}, bf16[128,128]{1,0:T(8,128)(2,1)S(1)}, bf16[128,128]{1,0:T(8,128)(2,1)S(1)}, bf16[128,128]{1,0:T(8,128)(2,1)S(1)}) fusion(f32[31]{0:T(128)S(1)} %get-tuple-element.74, s32[128,128]{1,0:T(8,128)S(1)} %subtract_add_fusion, f32[31]{0:T(128)S(1)} %get-tuple-element.75, f32[31]{0:T(128)S(1)} %get-tuple-element.89, ...), kind=kLoop, calls=%fused_computation.2 | loop fusion | flops 4505600 | bytes 197104 | tf_op jit(solution)/shard_map/reduce_sum | solution.py:45
  8.9 11.7 %collective-permute-start.3 = (bf16[64,15,128]{2,1,0:T(8,128)(2,1)S(1)}, bf16[64,15,128]{2,1,0:T(8,128)(2,1)S(1)}, u32[]{:S(2)}, u32[]{:S(2)}) collective-permute-start(bf16[64,15,128]{2,1,0:T(8,128)(2,1)S(1)} %get-tuple-element.62), channel_id=1, source_target_pairs={{0,1},{1,0},{2,3},{3,2},{4,5},{5,4},{6,7},{7,6},{8,9},{9,8},{10,11... | collective-permute-start | bytes 737288 | tf_op jit(solution)/shard_map/ppermute | solution.py:23
  20.7 1.0 %collective-permute-done.3 = bf16[64,15,128]{2,1,0:T(8,128)(2,1)S(1)} collective-permute-done((bf16[64,15,128]{2,1,0:T(8,128)(2,1)S(1)}, bf16[64,15,128]{2,1,0:T(8,128)(2,1)S(1)}, u32[]{:S(2)}, u32[]{:S(2)}) %collective-permute-start.3) | collective-permute-done | bytes 245792 | tf_op jit(solution)/shard_map/ppermute | solution.py:23
  22.7 1.6 %collective-permute-start.4 = (bf16[2,15,16,128]{3,1,2,0:T(8,128)(2,1)S(1)}, bf16[2,15,16,128]{3,1,2,0:T(8,128)(2,1)S(1)}, u32[]{:S(2)}, u32[]{:S(2)}) collective-permute-start(bf16[2,15,16,128]{3,1,2,0:T(8,128)(2,1)S(1)} %slice_select_fusion.3), channel_id=1, source_target_pairs={{0,2},{2,0},{1,3},{3,1},{4,6},{6,4},{5,7},{7,5},{8,10},{10,8},{9,1... | collective-permute-start | bytes 368648 | tf_op jit(solution)/shard_map/ppermute | solution.py:119
  24.2 3.5 %collective-permute-done.4 = bf16[2,15,16,128]{3,1,2,0:T(8,128)(2,1)S(1)} collective-permute-done((bf16[2,15,16,128]{3,1,2,0:T(8,128)(2,1)S(1)}, bf16[2,15,16,128]{3,1,2,0:T(8,128)(2,1)S(1)}, u32[]{:S(2)}, u32[]{:S(2)}) %collective-permute-start.4) | collective-permute-done | bytes 122912 | tf_op jit(solution)/shard_map/ppermute | solution.py:119
  29.7 6.4 %collective-permute-start.6 = (bf16[2,64,15,128]{3,2,1,0:T(8,128)(2,1)S(1)}, bf16[2,64,15,128]{3,2,1,0:T(8,128)(2,1)S(1)}, u32[]{:S(2)}, u32[]{:S(2)}) collective-permute-start(bf16[2,64,15,128]{3,2,1,0:T(8,128)(2,1)S(1)} %get-tuple-element.54), channel_id=1, source_target_pairs={{0,1},{1,0},{2,3},{3,2},{4,5},{5,4},{6,7},{7,6},{8,9},{9,8},{10,11... | collective-permute-start | bytes 1474568 | tf_op jit(solution)/shard_map/ppermute | solution.py:23
  36.2 1.4 %collective-permute-done.6 = bf16[2,64,15,128]{3,2,1,0:T(8,128)(2,1)S(1)} collective-permute-done((bf16[2,64,15,128]{3,2,1,0:T(8,128)(2,1)S(1)}, bf16[2,64,15,128]{3,2,1,0:T(8,128)(2,1)S(1)}, u32[]{:S(2)}, u32[]{:S(2)}) %collective-permute-start.6) | collective-permute-done | bytes 491552 | tf_op jit(solution)/shard_map/ppermute | solution.py:23
  38.7 1.6 %collective-permute-start.7 = (bf16[2,15,16,128]{3,1,2,0:T(8,128)(2,1)S(1)}, bf16[2,15,16,128]{3,1,2,0:T(8,128)(2,1)S(1)}, u32[]{:S(2)}, u32[]{:S(2)}) collective-permute-start(bf16[2,15,16,128]{3,1,2,0:T(8,128)(2,1)S(1)} %slice_select_fusion.2), channel_id=1, source_target_pairs={{0,2},{2,0},{1,3},{3,1},{4,6},{6,4},{5,7},{7,5},{8,10},{10,8},{9,1... | collective-permute-start | bytes 368648 | tf_op jit(solution)/shard_map/ppermute | solution.py:119
  40.3 3.5 %collective-permute-done.7 = bf16[2,15,16,128]{3,1,2,0:T(8,128)(2,1)S(1)} collective-permute-done((bf16[2,15,16,128]{3,1,2,0:T(8,128)(2,1)S(1)}, bf16[2,15,16,128]{3,1,2,0:T(8,128)(2,1)S(1)}, u32[]{:S(2)}, u32[]{:S(2)}) %collective-permute-start.7) | collective-permute-done | bytes 122912 | tf_op jit(solution)/shard_map/ppermute | solution.py:119
  45.8 8.8 %collective-permute-start.9 = (bf16[64,15,128]{2,1,0:T(8,128)(2,1)S(1)}, bf16[64,15,128]{2,1,0:T(8,128)(2,1)S(1)}, u32[]{:S(2)}, u32[]{:S(2)}) collective-permute-start(bf16[64,15,128]{2,1,0:T(8,128)(2,1)S(1)} %get-tuple-element.60), channel_id=1, source_target_pairs={{0,1},{1,0},{2,3},{3,2},{4,5},{5,4},{6,7},{7,6},{8,9},{9,8},{10,11... | collective-permute-start | bytes 737288 | tf_op jit(solution)/shard_map/ppermute | solution.py:23
  54.6 1.2 %collective-permute-done.9 = bf16[64,15,128]{2,1,0:T(8,128)(2,1)S(1)} collective-permute-done((bf16[64,15,128]{2,1,0:T(8,128)(2,1)S(1)}, bf16[64,15,128]{2,1,0:T(8,128)(2,1)S(1)}, u32[]{:S(2)}, u32[]{:S(2)}) %collective-permute-start.9) | collective-permute-done | bytes 245792 | tf_op jit(solution)/shard_map/ppermute | solution.py:23
  56.7 1.6 %collective-permute-start.10 = (bf16[2,15,16,128]{3,1,2,0:T(8,128)(2,1)S(1)}, bf16[2,15,16,128]{3,1,2,0:T(8,128)(2,1)S(1)}, u32[]{:S(2)}, u32[]{:S(2)}) collective-permute-start(bf16[2,15,16,128]{3,1,2,0:T(8,128)(2,1)S(1)} %slice_select_fusion.1), channel_id=1, source_target_pairs={{0,2},{2,0},{1,3},{3,1},{4,6},{6,4},{5,7},{7,5},{8,10},{10,8},{9,1... | collective-permute-start | bytes 368648 | tf_op jit(solution)/shard_map/ppermute | solution.py:119
  58.3 3.5 %collective-permute-done.10 = bf16[2,15,16,128]{3,1,2,0:T(8,128)(2,1)S(1)} collective-permute-done((bf16[2,15,16,128]{3,1,2,0:T(8,128)(2,1)S(1)}, bf16[2,15,16,128]{3,1,2,0:T(8,128)(2,1)S(1)}, u32[]{:S(2)}, u32[]{:S(2)}) %collective-permute-start.10) | collective-permute-done | bytes 122912 | tf_op jit(solution)/shard_map/ppermute | solution.py:119
  63.0 0.9 %collective-permute-start.11 = (bf16[2,64,15,128]{3,2,1,0:T(8,128)(2,1)S(1)}, bf16[2,64,15,128]{3,2,1,0:T(8,128)(2,1)S(1)}, u32[]{:S(2)}, u32[]{:S(2)}) collective-permute-start(bf16[2,64,15,128]{3,2,1,0:T(8,128)(2,1)S(1)} %get-tuple-element.49), channel_id=1, source_target_pairs={{1,4},{4,1},{3,6},{6,3},{5,8},{8,5},{7,10},{10,7},{9,12},{12,9},{1... | collective-permute-start | bytes 1474568 | tf_op jit(solution)/shard_map/ppermute | solution.py:140
  63.9 6.1 %collective-permute-start.12 = (bf16[2,64,15,128]{3,2,1,0:T(8,128)(2,1)S(1)}, bf16[2,64,15,128]{3,2,1,0:T(8,128)(2,1)S(1)}, u32[]{:S(2)}, u32[]{:S(2)}) collective-permute-start(bf16[2,64,15,128]{3,2,1,0:T(8,128)(2,1)S(1)} %get-tuple-element.50), channel_id=1, source_target_pairs={{0,1},{1,0},{2,3},{3,2},{4,5},{5,4},{6,7},{7,6},{8,9},{9,8},{10,11... | collective-permute-start | bytes 1474568 | tf_op jit(solution)/shard_map/ppermute | solution.py:23
  70.0 1.5 %collective-permute-done.12 = bf16[2,64,15,128]{3,2,1,0:T(8,128)(2,1)S(1)} collective-permute-done((bf16[2,64,15,128]{3,2,1,0:T(8,128)(2,1)S(1)}, bf16[2,64,15,128]{3,2,1,0:T(8,128)(2,1)S(1)}, u32[]{:S(2)}, u32[]{:S(2)}) %collective-permute-start.12) | collective-permute-done | bytes 491552 | tf_op jit(solution)/shard_map/ppermute | solution.py:23
  72.6 1.6 %collective-permute-start.13 = (bf16[2,15,16,128]{3,1,2,0:T(8,128)(2,1)S(1)}, bf16[2,15,16,128]{3,1,2,0:T(8,128)(2,1)S(1)}, u32[]{:S(2)}, u32[]{:S(2)}) collective-permute-start(bf16[2,15,16,128]{3,1,2,0:T(8,128)(2,1)S(1)} %slice_select_fusion), channel_id=1, source_target_pairs={{0,2},{2,0},{1,3},{3,1},{4,6},{6,4},{5,7},{7,5},{8,10},{10,8},{9,1... | collective-permute-start | bytes 368648 | tf_op jit(solution)/shard_map/ppermute | solution.py:119
  74.2 3.5 %collective-permute-done.13 = bf16[2,15,16,128]{3,1,2,0:T(8,128)(2,1)S(1)} collective-permute-done((bf16[2,15,16,128]{3,1,2,0:T(8,128)(2,1)S(1)}, bf16[2,15,16,128]{3,1,2,0:T(8,128)(2,1)S(1)}, u32[]{:S(2)}, u32[]{:S(2)}) %collective-permute-start.13) | collective-permute-done | bytes 122912 | tf_op jit(solution)/shard_map/ppermute | solution.py:119
  78.9 4.3 %collective-permute-start.14 = (f32[32,16,128]{2,1,0:T(8,128)S(1)}, f32[32,16,128]{2,1,0:T(8,128)S(1)}, u32[]{:S(2)}, u32[]{:S(2)}) collective-permute-start(f32[32,16,128]{2,1,0:T(8,128)S(1)} %get-tuple-element.47), channel_id=1, source_target_pairs={{0,1},{1,0},{2,3},{3,2},{4,5},{5,4},{6,7},{7,6},{8,9},{9,8},{10,11... | collective-permute-start | bytes 786440 | tf_op jit(solution)/shard_map/ppermute | solution.py:23
  83.2 1.2 %collective-permute-done.14 = f32[32,16,128]{2,1,0:T(8,128)S(1)} collective-permute-done((f32[32,16,128]{2,1,0:T(8,128)S(1)}, f32[32,16,128]{2,1,0:T(8,128)S(1)}, u32[]{:S(2)}, u32[]{:S(2)}) %collective-permute-start.14) | collective-permute-done | bytes 262176 | tf_op jit(solution)/shard_map/ppermute | solution.py:23
  84.3 0.9 %fusion.56 = f32[32,32,128]{2,1,0:T(8,128)} fusion(s32[]{:T(128)S(6)} %select_n.399, f32[32,16,128]{2,1,0:T(8,128)S(1)} %get-tuple-element.48, f32[32,16,128]{2,1,0:T(8,128)S(1)} %collective-permute-done.14), kind=kLoop, calls=%fused_computation.78 | loop fusion | flops 262144 | bytes 1048580 | tf_op jit(solution)/shard_map/concatenate | solution.py:220
  (94 shorter events, 15.1 us)
Async XLA Ops:
  0.0 1.8 %copy-start = (bf16[64,32,128]{2,1,0:T(8,128)(2,1)S(1)}, bf16[64,32,128]{2,1,0:T(8,128)(2,1)}, u32[]{:S(2)}) copy-start(bf16[64,32,128]{2,1,0:T(8,128)(2,1)} %param.3) | copy-start | bytes 1572868
  2.5 2.1 %collective-permute-start = (bf16[2,64,16,128]{3,2,1,0:T(8,128)(2,1)S(1)}, bf16[2,64,16,128]{3,2,1,0:T(8,128)(2,1)S(1)}, u32[]{:S(2)}, u32[]{:S(2)}) collective-permute-start(bf16[2,64,16,128]{3,2,1,0:T(8,128)(2,1)S(1)} %pad_maximum_fusion), channel_id=1, source_target_pairs={{0,1},{1,0},{2,3},{3,2},{4,5},{5,4},{6,7},{7,6},{8,9},{9,8},{10,11... | collective-permute-start | bytes 1572872 | tf_op jit(solution)/shard_map/ppermute | solution.py:23
  3.0 2.3 %copy-start.1 = (f32[2,3,31]{2,0,1:T(2,128)S(1)}, f32[2,3,31]{2,0,1:T(2,128)}, u32[]{:S(2)}) copy-start(f32[2,3,31]{2,0,1:T(2,128)} %param.4) | copy-start | bytes 2236
  4.6 3.2 %collective-permute-start.1 = (bf16[2,64,16,128]{3,2,1,0:T(8,128)(2,1)S(1)}, bf16[2,64,16,128]{3,2,1,0:T(8,128)(2,1)S(1)}, u32[]{:S(2)}, u32[]{:S(2)}) collective-permute-start(bf16[2,64,16,128]{3,2,1,0:T(8,128)(2,1)S(1)} %pad_maximum_fusion.1), channel_id=1, source_target_pairs={{1,4},{4,1},{3,6},{6,3},{5,8},{8,5},{7,10},{10,7},{9,12},{12,9},{1... | collective-permute-start | bytes 1572872 | tf_op jit(solution)/shard_map/ppermute | solution.py:192
  8.2 12.5 %collective-permute-start.2 = (bf16[64,15,128]{2,1,0:T(8,128)(2,1)S(1)}, bf16[64,15,128]{2,1,0:T(8,128)(2,1)S(1)}, u32[]{:S(2)}, u32[]{:S(2)}) collective-permute-start(bf16[64,15,128]{2,1,0:T(8,128)(2,1)S(1)} %get-tuple-element.61), channel_id=1, source_target_pairs={{1,4},{4,1},{3,6},{6,3},{5,8},{8,5},{7,10},{10,7},{9,12},{12,9},{1... | collective-permute-start | bytes 737288 | tf_op jit(solution)/shard_map/ppermute | solution.py:140
  8.9 12.8 %collective-permute-start.3 = (bf16[64,15,128]{2,1,0:T(8,128)(2,1)S(1)}, bf16[64,15,128]{2,1,0:T(8,128)(2,1)S(1)}, u32[]{:S(2)}, u32[]{:S(2)}) collective-permute-start(bf16[64,15,128]{2,1,0:T(8,128)(2,1)S(1)} %get-tuple-element.62), channel_id=1, source_target_pairs={{0,1},{1,0},{2,3},{3,2},{4,5},{5,4},{6,7},{7,6},{8,9},{9,8},{10,11... | collective-permute-start | bytes 737288 | tf_op jit(solution)/shard_map/ppermute | solution.py:23
  22.7 5.0 %collective-permute-start.4 = (bf16[2,15,16,128]{3,1,2,0:T(8,128)(2,1)S(1)}, bf16[2,15,16,128]{3,1,2,0:T(8,128)(2,1)S(1)}, u32[]{:S(2)}, u32[]{:S(2)}) collective-permute-start(bf16[2,15,16,128]{3,1,2,0:T(8,128)(2,1)S(1)} %slice_select_fusion.3), channel_id=1, source_target_pairs={{0,2},{2,0},{1,3},{3,1},{4,6},{6,4},{5,7},{7,5},{8,10},{10,8},{9,1... | collective-permute-start | bytes 368648 | tf_op jit(solution)/shard_map/ppermute | solution.py:119
  29.0 7.2 %collective-permute-start.5 = (bf16[2,64,15,128]{3,2,1,0:T(8,128)(2,1)S(1)}, bf16[2,64,15,128]{3,2,1,0:T(8,128)(2,1)S(1)}, u32[]{:S(2)}, u32[]{:S(2)}) collective-permute-start(bf16[2,64,15,128]{3,2,1,0:T(8,128)(2,1)S(1)} %get-tuple-element.53), channel_id=1, source_target_pairs={{1,4},{4,1},{3,6},{6,3},{5,8},{8,5},{7,10},{10,7},{9,12},{12,9},{1... | collective-permute-start | bytes 1474568 | tf_op jit(solution)/shard_map/ppermute | solution.py:140
  29.7 7.9 %collective-permute-start.6 = (bf16[2,64,15,128]{3,2,1,0:T(8,128)(2,1)S(1)}, bf16[2,64,15,128]{3,2,1,0:T(8,128)(2,1)S(1)}, u32[]{:S(2)}, u32[]{:S(2)}) collective-permute-start(bf16[2,64,15,128]{3,2,1,0:T(8,128)(2,1)S(1)} %get-tuple-element.54), channel_id=1, source_target_pairs={{0,1},{1,0},{2,3},{3,2},{4,5},{5,4},{6,7},{7,6},{8,9},{9,8},{10,11... | collective-permute-start | bytes 1474568 | tf_op jit(solution)/shard_map/ppermute | solution.py:23
  38.7 5.0 %collective-permute-start.7 = (bf16[2,15,16,128]{3,1,2,0:T(8,128)(2,1)S(1)}, bf16[2,15,16,128]{3,1,2,0:T(8,128)(2,1)S(1)}, u32[]{:S(2)}, u32[]{:S(2)}) collective-permute-start(bf16[2,15,16,128]{3,1,2,0:T(8,128)(2,1)S(1)} %slice_select_fusion.2), channel_id=1, source_target_pairs={{0,2},{2,0},{1,3},{3,1},{4,6},{6,4},{5,7},{7,5},{8,10},{10,8},{9,1... | collective-permute-start | bytes 368648 | tf_op jit(solution)/shard_map/ppermute | solution.py:119
  45.1 9.5 %collective-permute-start.8 = (bf16[64,15,128]{2,1,0:T(8,128)(2,1)S(1)}, bf16[64,15,128]{2,1,0:T(8,128)(2,1)S(1)}, u32[]{:S(2)}, u32[]{:S(2)}) collective-permute-start(bf16[64,15,128]{2,1,0:T(8,128)(2,1)S(1)} %get-tuple-element.59), channel_id=1, source_target_pairs={{1,4},{4,1},{3,6},{6,3},{5,8},{8,5},{7,10},{10,7},{9,12},{12,9},{1... | collective-permute-start | bytes 737288 | tf_op jit(solution)/shard_map/ppermute | solution.py:140
  45.8 10.0 %collective-permute-start.9 = (bf16[64,15,128]{2,1,0:T(8,128)(2,1)S(1)}, bf16[64,15,128]{2,1,0:T(8,128)(2,1)S(1)}, u32[]{:S(2)}, u32[]{:S(2)}) collective-permute-start(bf16[64,15,128]{2,1,0:T(8,128)(2,1)S(1)} %get-tuple-element.60), channel_id=1, source_target_pairs={{0,1},{1,0},{2,3},{3,2},{4,5},{5,4},{6,7},{7,6},{8,9},{9,8},{10,11... | collective-permute-start | bytes 737288 | tf_op jit(solution)/shard_map/ppermute | solution.py:23
  56.7 5.0 %collective-permute-start.10 = (bf16[2,15,16,128]{3,1,2,0:T(8,128)(2,1)S(1)}, bf16[2,15,16,128]{3,1,2,0:T(8,128)(2,1)S(1)}, u32[]{:S(2)}, u32[]{:S(2)}) collective-permute-start(bf16[2,15,16,128]{3,1,2,0:T(8,128)(2,1)S(1)} %slice_select_fusion.1), channel_id=1, source_target_pairs={{0,2},{2,0},{1,3},{3,1},{4,6},{6,4},{5,7},{7,5},{8,10},{10,8},{9,1... | collective-permute-start | bytes 368648 | tf_op jit(solution)/shard_map/ppermute | solution.py:119
  63.0 7.0 %collective-permute-start.11 = (bf16[2,64,15,128]{3,2,1,0:T(8,128)(2,1)S(1)}, bf16[2,64,15,128]{3,2,1,0:T(8,128)(2,1)S(1)}, u32[]{:S(2)}, u32[]{:S(2)}) collective-permute-start(bf16[2,64,15,128]{3,2,1,0:T(8,128)(2,1)S(1)} %get-tuple-element.49), channel_id=1, source_target_pairs={{1,4},{4,1},{3,6},{6,3},{5,8},{8,5},{7,10},{10,7},{9,12},{12,9},{1... | collective-permute-start | bytes 1474568 | tf_op jit(solution)/shard_map/ppermute | solution.py:140
  63.9 7.6 %collective-permute-start.12 = (bf16[2,64,15,128]{3,2,1,0:T(8,128)(2,1)S(1)}, bf16[2,64,15,128]{3,2,1,0:T(8,128)(2,1)S(1)}, u32[]{:S(2)}, u32[]{:S(2)}) collective-permute-start(bf16[2,64,15,128]{3,2,1,0:T(8,128)(2,1)S(1)} %get-tuple-element.50), channel_id=1, source_target_pairs={{0,1},{1,0},{2,3},{3,2},{4,5},{5,4},{6,7},{7,6},{8,9},{9,8},{10,11... | collective-permute-start | bytes 1474568 | tf_op jit(solution)/shard_map/ppermute | solution.py:23
  72.6 5.0 %collective-permute-start.13 = (bf16[2,15,16,128]{3,1,2,0:T(8,128)(2,1)S(1)}, bf16[2,15,16,128]{3,1,2,0:T(8,128)(2,1)S(1)}, u32[]{:S(2)}, u32[]{:S(2)}) collective-permute-start(bf16[2,15,16,128]{3,1,2,0:T(8,128)(2,1)S(1)} %slice_select_fusion), channel_id=1, source_target_pairs={{0,2},{2,0},{1,3},{3,1},{4,6},{6,4},{5,7},{7,5},{8,10},{10,8},{9,1... | collective-permute-start | bytes 368648 | tf_op jit(solution)/shard_map/ppermute | solution.py:119
  78.9 5.4 %collective-permute-start.14 = (f32[32,16,128]{2,1,0:T(8,128)S(1)}, f32[32,16,128]{2,1,0:T(8,128)S(1)}, u32[]{:S(2)}, u32[]{:S(2)}) collective-permute-start(f32[32,16,128]{2,1,0:T(8,128)S(1)} %get-tuple-element.47), channel_id=1, source_target_pairs={{0,1},{1,0},{2,3},{3,2},{4,5},{5,4},{6,7},{7,6},{8,9},{9,8},{10,11... | collective-permute-start | bytes 786440 | tf_op jit(solution)/shard_map/ppermute | solution.py:23

commit v28 on v27

--- a/solution.py
+++ b/solution.py
@@ -162,7 +162,13 @@
     for target, half in ((tile_index, 0), (tile_index, 1), (tile_index + 1, 0), (tile_index - 1, 1)):
         target = jnp.clip(target, 0, tile_total - 1)
         starts.append(target * block_count + half * half_blocks)
-    slots = jnp.concatenate([lax.dynamic_slice_in_dim(sources, st, half_blocks) for st in starts])
+    groups = [lax.dynamic_slice_in_dim(sources, st, half_blocks) for st in starts]
+    first = view_bit == 0
+    slots = jnp.where(
+        first,
+        jnp.concatenate([groups[0], groups[1], groups[3], groups[2]]),
+        jnp.concatenate([groups[1], groups[0], groups[2], groups[3]]),
+    )
     row_ids = jnp.arange(slots.shape[0] * BX, dtype=jnp.int32)
     row_slots = slots[row_ids // BX]
     source_x = (row_slots % block_count) * BX + row_ids % BX
@@ -174,10 +180,10 @@
         "zrx,zxy->zry", selection, acquired, preferred_element_type=jnp.float32
     ).astype(acquired.dtype)
     partials = partials.reshape(planes, 4, half_x, width_y)
-    own_keep = jnp.where(first, partials[:, 0], partials[:, 1])
-    own_give = jnp.where(first, partials[:, 1], partials[:, 0])
-    cross_keep = jnp.where(first, partials[:, 3], partials[:, 2])
-    cross_pass = jnp.where(first, partials[:, 2], partials[:, 3])
+    own_keep = partials[:, 0]
+    own_give = partials[:, 1]
+    cross_keep = partials[:, 2]
+    cross_pass = partials[:, 3]
     got = from_partner(jnp.stack([own_give, cross_pass]), "view", 0)
     tiles = lax.axis_size("tile")
     views = lax.axis_size("view")

time: 85.6 us -> 85.7 us (level)
  no operation moved by 1% of the time
where the time goes in v28:
time: 85.7 us; the launch traced here: 85.3 us
  starting transfers between devices  47.6 us (56%)
  waiting for transfers between devices  21.7 us (25%)
  other arithmetic  6.94 us (8%)
  matrix products  5.08 us (6%)
  local copies, waits for them, and re-layouts  3.45 us (4%)
    ppermute x6, starting transfers between devices, from_partner(): return lax.ppermute(block, axis, route)  37.8 us
    ppermute x4, waiting for transfers between devices, z_rims(): got = lax.ppermute(payload, 'view', route)  13.9 us
    ppermute x6, waiting for transfers between devices, from_partner(): return lax.ppermute(block, axis, route)  7.8 us
    ppermute x4, starting transfers between devices, z_rims(): got = lax.ppermute(payload, 'view', route)  6.22 us
    ppermute x4, starting transfers between devices, x_rims(): across = lax.ppermute(outward, ('tile', 'view'), route)  2.92 us
  transfers between devices with their start and end apart: 15, of which 10 were waited for; matrix products, arithmetic and copies ran while one was open for 3% of the time, Pallas kernels for 0%

profile of v28, /device:TPU:0, one launch (start us, length us, event | category | flops | bytes accessed | tf_op | source)
XLA Modules:
  0.0 85.3 jit_solution(9133886145833344414)
XLA Ops:
  0.0 0.9 %fusion.72 = (s32[4]{0:T(128)S(1)}, s32[4]{0:T(128)S(1)}, s32[4]{0:T(128)S(1)}, s32[4]{0:T(128)S(1)}) fusion(s32[1,32]{1,0:T(1,128)} %param.5, s32[]{:T(128)S(6)} %select_n.282, s32[]{:T(128)S(6)} %select_n.283, s32[]{:T(128)S(6)} %select_n.285, s32[]{:T(128)S(6)} %select_n.284), kind=kLoop, calls=%fused_computation.181 | loop fusion | bytes 144 | tf_op jit(solution)/shard_map/dynamic_slice | solution.py:165
  1.0 0.8 gather_fusion
  3.1 1.5 %collective-permute-done = bf16[2,64,16,128]{3,2,1,0:T(8,128)(2,1)S(1)} collective-permute-done((bf16[2,64,16,128]{3,2,1,0:T(8,128)(2,1)S(1)}, bf16[2,64,16,128]{3,2,1,0:T(8,128)(2,1)S(1)}, u32[]{:S(2)}, u32[]{:S(2)}) %collective-permute-start) | collective-permute-done | bytes 524320 | tf_op jit(solution)/shard_map/ppermute | solution.py:23
  6.9 1.0 %select_reduce_fusion.1 = (bf16[128,128]{1,0:T(8,128)(2,1)S(1)}, bf16[128,128]{1,0:T(8,128)(2,1)S(1)}, bf16[128,128]{1,0:T(8,128)(2,1)S(1)}, bf16[128,128]{1,0:T(8,128)(2,1)S(1)}) fusion(f32[31]{0:T(128)S(1)} %get-tuple-element.74, s32[128,128]{1,0:T(8,128)S(1)} %subtract_add_fusion, f32[31]{0:T(128)S(1)} %get-tuple-element.75, f32[31]{0:T(128)S(1)} %get-tuple-element.89, ...), kind=kLoop, calls=%fused_computation.2 | loop fusion | flops 4505600 | bytes 197104 | tf_op jit(solution)/shard_map/reduce_sum | solution.py:45
  9.0 11.7 %collective-permute-start.3 = (bf16[64,15,128]{2,1,0:T(8,128)(2,1)S(1)}, bf16[64,15,128]{2,1,0:T(8,128)(2,1)S(1)}, u32[]{:S(2)}, u32[]{:S(2)}) collective-permute-start(bf16[64,15,128]{2,1,0:T(8,128)(2,1)S(1)} %get-tuple-element.62), channel_id=1, source_target_pairs={{0,1},{1,0},{2,3},{3,2},{4,5},{5,4},{6,7},{7,6},{8,9},{9,8},{10,11... | collective-permute-start | bytes 737288 | tf_op jit(solution)/shard_map/ppermute | solution.py:23
  20.8 1.0 %collective-permute-done.3 = bf16[64,15,128]{2,1,0:T(8,128)(2,1)S(1)} collective-permute-done((bf16[64,15,128]{2,1,0:T(8,128)(2,1)S(1)}, bf16[64,15,128]{2,1,0:T(8,128)(2,1)S(1)}, u32[]{:S(2)}, u32[]{:S(2)}) %collective-permute-start.3) | collective-permute-done | bytes 245792 | tf_op jit(solution)/shard_map/ppermute | solution.py:23
  22.8 1.6 %collective-permute-start.4 = (bf16[2,15,16,128]{3,1,2,0:T(8,128)(2,1)S(1)}, bf16[2,15,16,128]{3,1,2,0:T(8,128)(2,1)S(1)}, u32[]{:S(2)}, u32[]{:S(2)}) collective-permute-start(bf16[2,15,16,128]{3,1,2,0:T(8,128)(2,1)S(1)} %slice_select_fusion.3), channel_id=1, source_target_pairs={{0,2},{2,0},{1,3},{3,1},{4,6},{6,4},{5,7},{7,5},{8,10},{10,8},{9,1... | collective-permute-start | bytes 368648 | tf_op jit(solution)/shard_map/ppermute | solution.py:119
  24.3 3.5 %collective-permute-done.4 = bf16[2,15,16,128]{3,1,2,0:T(8,128)(2,1)S(1)} collective-permute-done((bf16[2,15,16,128]{3,1,2,0:T(8,128)(2,1)S(1)}, bf16[2,15,16,128]{3,1,2,0:T(8,128)(2,1)S(1)}, u32[]{:S(2)}, u32[]{:S(2)}) %collective-permute-start.4) | collective-permute-done | bytes 122912 | tf_op jit(solution)/shard_map/ppermute | solution.py:119
  29.8 6.4 %collective-permute-start.6 = (bf16[2,64,15,128]{3,2,1,0:T(8,128)(2,1)S(1)}, bf16[2,64,15,128]{3,2,1,0:T(8,128)(2,1)S(1)}, u32[]{:S(2)}, u32[]{:S(2)}) collective-permute-start(bf16[2,64,15,128]{3,2,1,0:T(8,128)(2,1)S(1)} %get-tuple-element.54), channel_id=1, source_target_pairs={{0,1},{1,0},{2,3},{3,2},{4,5},{5,4},{6,7},{7,6},{8,9},{9,8},{10,11... | collective-permute-start | bytes 1474568 | tf_op jit(solution)/shard_map/ppermute | solution.py:23
  36.3 1.4 %collective-permute-done.6 = bf16[2,64,15,128]{3,2,1,0:T(8,128)(2,1)S(1)} collective-permute-done((bf16[2,64,15,128]{3,2,1,0:T(8,128)(2,1)S(1)}, bf16[2,64,15,128]{3,2,1,0:T(8,128)(2,1)S(1)}, u32[]{:S(2)}, u32[]{:S(2)}) %collective-permute-start.6) | collective-permute-done | bytes 491552 | tf_op jit(solution)/shard_map/ppermute | solution.py:23
  38.9 1.6 %collective-permute-start.7 = (bf16[2,15,16,128]{3,1,2,0:T(8,128)(2,1)S(1)}, bf16[2,15,16,128]{3,1,2,0:T(8,128)(2,1)S(1)}, u32[]{:S(2)}, u32[]{:S(2)}) collective-permute-start(bf16[2,15,16,128]{3,1,2,0:T(8,128)(2,1)S(1)} %slice_select_fusion.2), channel_id=1, source_target_pairs={{0,2},{2,0},{1,3},{3,1},{4,6},{6,4},{5,7},{7,5},{8,10},{10,8},{9,1... | collective-permute-start | bytes 368648 | tf_op jit(solution)/shard_map/ppermute | solution.py:119
  40.4 3.5 %collective-permute-done.7 = bf16[2,15,16,128]{3,1,2,0:T(8,128)(2,1)S(1)} collective-permute-done((bf16[2,15,16,128]{3,1,2,0:T(8,128)(2,1)S(1)}, bf16[2,15,16,128]{3,1,2,0:T(8,128)(2,1)S(1)}, u32[]{:S(2)}, u32[]{:S(2)}) %collective-permute-start.7) | collective-permute-done | bytes 122912 | tf_op jit(solution)/shard_map/ppermute | solution.py:119
  45.9 8.8 %collective-permute-start.9 = (bf16[64,15,128]{2,1,0:T(8,128)(2,1)S(1)}, bf16[64,15,128]{2,1,0:T(8,128)(2,1)S(1)}, u32[]{:S(2)}, u32[]{:S(2)}) collective-permute-start(bf16[64,15,128]{2,1,0:T(8,128)(2,1)S(1)} %get-tuple-element.60), channel_id=1, source_target_pairs={{0,1},{1,0},{2,3},{3,2},{4,5},{5,4},{6,7},{7,6},{8,9},{9,8},{10,11... | collective-permute-start | bytes 737288 | tf_op jit(solution)/shard_map/ppermute | solution.py:23
  54.7 1.2 %collective-permute-done.9 = bf16[64,15,128]{2,1,0:T(8,128)(2,1)S(1)} collective-permute-done((bf16[64,15,128]{2,1,0:T(8,128)(2,1)S(1)}, bf16[64,15,128]{2,1,0:T(8,128)(2,1)S(1)}, u32[]{:S(2)}, u32[]{:S(2)}) %collective-permute-start.9) | collective-permute-done | bytes 245792 | tf_op jit(solution)/shard_map/ppermute | solution.py:23
  56.8 1.6 %collective-permute-start.10 = (bf16[2,15,16,128]{3,1,2,0:T(8,128)(2,1)S(1)}, bf16[2,15,16,128]{3,1,2,0:T(8,128)(2,1)S(1)}, u32[]{:S(2)}, u32[]{:S(2)}) collective-permute-start(bf16[2,15,16,128]{3,1,2,0:T(8,128)(2,1)S(1)} %slice_select_fusion.1), channel_id=1, source_target_pairs={{0,2},{2,0},{1,3},{3,1},{4,6},{6,4},{5,7},{7,5},{8,10},{10,8},{9,1... | collective-permute-start | bytes 368648 | tf_op jit(solution)/shard_map/ppermute | solution.py:119
  58.4 3.5 %collective-permute-done.10 = bf16[2,15,16,128]{3,1,2,0:T(8,128)(2,1)S(1)} collective-permute-done((bf16[2,15,16,128]{3,1,2,0:T(8,128)(2,1)S(1)}, bf16[2,15,16,128]{3,1,2,0:T(8,128)(2,1)S(1)}, u32[]{:S(2)}, u32[]{:S(2)}) %collective-permute-start.10) | collective-permute-done | bytes 122912 | tf_op jit(solution)/shard_map/ppermute | solution.py:119
  63.1 0.9 %collective-permute-start.11 = (bf16[2,64,15,128]{3,2,1,0:T(8,128)(2,1)S(1)}, bf16[2,64,15,128]{3,2,1,0:T(8,128)(2,1)S(1)}, u32[]{:S(2)}, u32[]{:S(2)}) collective-permute-start(bf16[2,64,15,128]{3,2,1,0:T(8,128)(2,1)S(1)} %get-tuple-element.49), channel_id=1, source_target_pairs={{1,4},{4,1},{3,6},{6,3},{5,8},{8,5},{7,10},{10,7},{9,12},{12,9},{1... | collective-permute-start | bytes 1474568 | tf_op jit(solution)/shard_map/ppermute | solution.py:140
  64.0 6.1 %collective-permute-start.12 = (bf16[2,64,15,128]{3,2,1,0:T(8,128)(2,1)S(1)}, bf16[2,64,15,128]{3,2,1,0:T(8,128)(2,1)S(1)}, u32[]{:S(2)}, u32[]{:S(2)}) collective-permute-start(bf16[2,64,15,128]{3,2,1,0:T(8,128)(2,1)S(1)} %get-tuple-element.50), channel_id=1, source_target_pairs={{0,1},{1,0},{2,3},{3,2},{4,5},{5,4},{6,7},{7,6},{8,9},{9,8},{10,11... | collective-permute-start | bytes 1474568 | tf_op jit(solution)/shard_map/ppermute | solution.py:23
  70.1 1.5 %collective-permute-done.12 = bf16[2,64,15,128]{3,2,1,0:T(8,128)(2,1)S(1)} collective-permute-done((bf16[2,64,15,128]{3,2,1,0:T(8,128)(2,1)S(1)}, bf16[2,64,15,128]{3,2,1,0:T(8,128)(2,1)S(1)}, u32[]{:S(2)}, u32[]{:S(2)}) %collective-permute-start.12) | collective-permute-done | bytes 491552 | tf_op jit(solution)/shard_map/ppermute | solution.py:23
  72.7 1.6 %collective-permute-start.13 = (bf16[2,15,16,128]{3,1,2,0:T(8,128)(2,1)S(1)}, bf16[2,15,16,128]{3,1,2,0:T(8,128)(2,1)S(1)}, u32[]{:S(2)}, u32[]{:S(2)}) collective-permute-start(bf16[2,15,16,128]{3,1,2,0:T(8,128)(2,1)S(1)} %slice_select_fusion), channel_id=1, source_target_pairs={{0,2},{2,0},{1,3},{3,1},{4,6},{6,4},{5,7},{7,5},{8,10},{10,8},{9,1... | collective-permute-start | bytes 368648 | tf_op jit(solution)/shard_map/ppermute | solution.py:119
  74.3 3.5 %collective-permute-done.13 = bf16[2,15,16,128]{3,1,2,0:T(8,128)(2,1)S(1)} collective-permute-done((bf16[2,15,16,128]{3,1,2,0:T(8,128)(2,1)S(1)}, bf16[2,15,16,128]{3,1,2,0:T(8,128)(2,1)S(1)}, u32[]{:S(2)}, u32[]{:S(2)}) %collective-permute-start.13) | collective-permute-done | bytes 122912 | tf_op jit(solution)/shard_map/ppermute | solution.py:119
  79.0 4.3 %collective-permute-start.14 = (f32[32,16,128]{2,1,0:T(8,128)S(1)}, f32[32,16,128]{2,1,0:T(8,128)S(1)}, u32[]{:S(2)}, u32[]{:S(2)}) collective-permute-start(f32[32,16,128]{2,1,0:T(8,128)S(1)} %get-tuple-element.47), channel_id=1, source_target_pairs={{0,1},{1,0},{2,3},{3,2},{4,5},{5,4},{6,7},{7,6},{8,9},{9,8},{10,11... | collective-permute-start | bytes 786440 | tf_op jit(solution)/shard_map/ppermute | solution.py:23
  83.3 1.2 %collective-permute-done.14 = f32[32,16,128]{2,1,0:T(8,128)S(1)} collective-permute-done((f32[32,16,128]{2,1,0:T(8,128)S(1)}, f32[32,16,128]{2,1,0:T(8,128)S(1)}, u32[]{:S(2)}, u32[]{:S(2)}) %collective-permute-start.14) | collective-permute-done | bytes 262176 | tf_op jit(solution)/shard_map/ppermute | solution.py:23
  84.5 0.9 %fusion.56 = f32[32,32,128]{2,1,0:T(8,128)} fusion(s32[]{:T(128)S(6)} %select_n.340, f32[32,16,128]{2,1,0:T(8,128)S(1)} %get-tuple-element.48, f32[32,16,128]{2,1,0:T(8,128)S(1)} %collective-permute-done.14), kind=kLoop, calls=%fused_computation.78 | loop fusion | flops 262144 | bytes 1048580 | tf_op jit(solution)/shard_map/concatenate | solution.py:226
  (94 shorter events, 15.2 us)
Async XLA Ops:
  0.0 1.8 %copy-start = (bf16[64,32,128]{2,1,0:T(8,128)(2,1)S(1)}, bf16[64,32,128]{2,1,0:T(8,128)(2,1)}, u32[]{:S(2)}) copy-start(bf16[64,32,128]{2,1,0:T(8,128)(2,1)} %param.3) | copy-start | bytes 1572868
  2.6 2.1 %collective-permute-start = (bf16[2,64,16,128]{3,2,1,0:T(8,128)(2,1)S(1)}, bf16[2,64,16,128]{3,2,1,0:T(8,128)(2,1)S(1)}, u32[]{:S(2)}, u32[]{:S(2)}) collective-permute-start(bf16[2,64,16,128]{3,2,1,0:T(8,128)(2,1)S(1)} %pad_maximum_fusion), channel_id=1, source_target_pairs={{0,1},{1,0},{2,3},{3,2},{4,5},{5,4},{6,7},{7,6},{8,9},{9,8},{10,11... | collective-permute-start | bytes 1572872 | tf_op jit(solution)/shard_map/ppermute | solution.py:23
  3.1 2.3 %copy-start.1 = (f32[2,3,31]{2,0,1:T(2,128)S(1)}, f32[2,3,31]{2,0,1:T(2,128)}, u32[]{:S(2)}) copy-start(f32[2,3,31]{2,0,1:T(2,128)} %param.4) | copy-start | bytes 2236
  4.7 3.2 %collective-permute-start.1 = (bf16[2,64,16,128]{3,2,1,0:T(8,128)(2,1)S(1)}, bf16[2,64,16,128]{3,2,1,0:T(8,128)(2,1)S(1)}, u32[]{:S(2)}, u32[]{:S(2)}) collective-permute-start(bf16[2,64,16,128]{3,2,1,0:T(8,128)(2,1)S(1)} %pad_maximum_fusion.1), channel_id=1, source_target_pairs={{1,4},{4,1},{3,6},{6,3},{5,8},{8,5},{7,10},{10,7},{9,12},{12,9},{1... | collective-permute-start | bytes 1572872 | tf_op jit(solution)/shard_map/ppermute | solution.py:198
  8.3 12.5 %collective-permute-start.2 = (bf16[64,15,128]{2,1,0:T(8,128)(2,1)S(1)}, bf16[64,15,128]{2,1,0:T(8,128)(2,1)S(1)}, u32[]{:S(2)}, u32[]{:S(2)}) collective-permute-start(bf16[64,15,128]{2,1,0:T(8,128)(2,1)S(1)} %get-tuple-element.61), channel_id=1, source_target_pairs={{1,4},{4,1},{3,6},{6,3},{5,8},{8,5},{7,10},{10,7},{9,12},{12,9},{1... | collective-permute-start | bytes 737288 | tf_op jit(solution)/shard_map/ppermute | solution.py:140
  9.0 12.8 %collective-permute-start.3 = (bf16[64,15,128]{2,1,0:T(8,128)(2,1)S(1)}, bf16[64,15,128]{2,1,0:T(8,128)(2,1)S(1)}, u32[]{:S(2)}, u32[]{:S(2)}) collective-permute-start(bf16[64,15,128]{2,1,0:T(8,128)(2,1)S(1)} %get-tuple-element.62), channel_id=1, source_target_pairs={{0,1},{1,0},{2,3},{3,2},{4,5},{5,4},{6,7},{7,6},{8,9},{9,8},{10,11... | collective-permute-start | bytes 737288 | tf_op jit(solution)/shard_map/ppermute | solution.py:23
  22.8 5.0 %collective-permute-start.4 = (bf16[2,15,16,128]{3,1,2,0:T(8,128)(2,1)S(1)}, bf16[2,15,16,128]{3,1,2,0:T(8,128)(2,1)S(1)}, u32[]{:S(2)}, u32[]{:S(2)}) collective-permute-start(bf16[2,15,16,128]{3,1,2,0:T(8,128)(2,1)S(1)} %slice_select_fusion.3), channel_id=1, source_target_pairs={{0,2},{2,0},{1,3},{3,1},{4,6},{6,4},{5,7},{7,5},{8,10},{10,8},{9,1... | collective-permute-start | bytes 368648 | tf_op jit(solution)/shard_map/ppermute | solution.py:119
  29.1 7.2 %collective-permute-start.5 = (bf16[2,64,15,128]{3,2,1,0:T(8,128)(2,1)S(1)}, bf16[2,64,15,128]{3,2,1,0:T(8,128)(2,1)S(1)}, u32[]{:S(2)}, u32[]{:S(2)}) collective-permute-start(bf16[2,64,15,128]{3,2,1,0:T(8,128)(2,1)S(1)} %get-tuple-element.53), channel_id=1, source_target_pairs={{1,4},{4,1},{3,6},{6,3},{5,8},{8,5},{7,10},{10,7},{9,12},{12,9},{1... | collective-permute-start | bytes 1474568 | tf_op jit(solution)/shard_map/ppermute | solution.py:140
  29.8 7.9 %collective-permute-start.6 = (bf16[2,64,15,128]{3,2,1,0:T(8,128)(2,1)S(1)}, bf16[2,64,15,128]{3,2,1,0:T(8,128)(2,1)S(1)}, u32[]{:S(2)}, u32[]{:S(2)}) collective-permute-start(bf16[2,64,15,128]{3,2,1,0:T(8,128)(2,1)S(1)} %get-tuple-element.54), channel_id=1, source_target_pairs={{0,1},{1,0},{2,3},{3,2},{4,5},{5,4},{6,7},{7,6},{8,9},{9,8},{10,11... | collective-permute-start | bytes 1474568 | tf_op jit(solution)/shard_map/ppermute | solution.py:23
  38.9 5.0 %collective-permute-start.7 = (bf16[2,15,16,128]{3,1,2,0:T(8,128)(2,1)S(1)}, bf16[2,15,16,128]{3,1,2,0:T(8,128)(2,1)S(1)}, u32[]{:S(2)}, u32[]{:S(2)}) collective-permute-start(bf16[2,15,16,128]{3,1,2,0:T(8,128)(2,1)S(1)} %slice_select_fusion.2), channel_id=1, source_target_pairs={{0,2},{2,0},{1,3},{3,1},{4,6},{6,4},{5,7},{7,5},{8,10},{10,8},{9,1... | collective-permute-start | bytes 368648 | tf_op jit(solution)/shard_map/ppermute | solution.py:119
  45.2 9.5 %collective-permute-start.8 = (bf16[64,15,128]{2,1,0:T(8,128)(2,1)S(1)}, bf16[64,15,128]{2,1,0:T(8,128)(2,1)S(1)}, u32[]{:S(2)}, u32[]{:S(2)}) collective-permute-start(bf16[64,15,128]{2,1,0:T(8,128)(2,1)S(1)} %get-tuple-element.59), channel_id=1, source_target_pairs={{1,4},{4,1},{3,6},{6,3},{5,8},{8,5},{7,10},{10,7},{9,12},{12,9},{1... | collective-permute-start | bytes 737288 | tf_op jit(solution)/shard_map/ppermute | solution.py:140
  45.9 10.0 %collective-permute-start.9 = (bf16[64,15,128]{2,1,0:T(8,128)(2,1)S(1)}, bf16[64,15,128]{2,1,0:T(8,128)(2,1)S(1)}, u32[]{:S(2)}, u32[]{:S(2)}) collective-permute-start(bf16[64,15,128]{2,1,0:T(8,128)(2,1)S(1)} %get-tuple-element.60), channel_id=1, source_target_pairs={{0,1},{1,0},{2,3},{3,2},{4,5},{5,4},{6,7},{7,6},{8,9},{9,8},{10,11... | collective-permute-start | bytes 737288 | tf_op jit(solution)/shard_map/ppermute | solution.py:23
  56.8 5.0 %collective-permute-start.10 = (bf16[2,15,16,128]{3,1,2,0:T(8,128)(2,1)S(1)}, bf16[2,15,16,128]{3,1,2,0:T(8,128)(2,1)S(1)}, u32[]{:S(2)}, u32[]{:S(2)}) collective-permute-start(bf16[2,15,16,128]{3,1,2,0:T(8,128)(2,1)S(1)} %slice_select_fusion.1), channel_id=1, source_target_pairs={{0,2},{2,0},{1,3},{3,1},{4,6},{6,4},{5,7},{7,5},{8,10},{10,8},{9,1... | collective-permute-start | bytes 368648 | tf_op jit(solution)/shard_map/ppermute | solution.py:119
  63.1 7.0 %collective-permute-start.11 = (bf16[2,64,15,128]{3,2,1,0:T(8,128)(2,1)S(1)}, bf16[2,64,15,128]{3,2,1,0:T(8,128)(2,1)S(1)}, u32[]{:S(2)}, u32[]{:S(2)}) collective-permute-start(bf16[2,64,15,128]{3,2,1,0:T(8,128)(2,1)S(1)} %get-tuple-element.49), channel_id=1, source_target_pairs={{1,4},{4,1},{3,6},{6,3},{5,8},{8,5},{7,10},{10,7},{9,12},{12,9},{1... | collective-permute-start | bytes 1474568 | tf_op jit(solution)/shard_map/ppermute | solution.py:140
  64.0 7.6 %collective-permute-start.12 = (bf16[2,64,15,128]{3,2,1,0:T(8,128)(2,1)S(1)}, bf16[2,64,15,128]{3,2,1,0:T(8,128)(2,1)S(1)}, u32[]{:S(2)}, u32[]{:S(2)}) collective-permute-start(bf16[2,64,15,128]{3,2,1,0:T(8,128)(2,1)S(1)} %get-tuple-element.50), channel_id=1, source_target_pairs={{0,1},{1,0},{2,3},{3,2},{4,5},{5,4},{6,7},{7,6},{8,9},{9,8},{10,11... | collective-permute-start | bytes 1474568 | tf_op jit(solution)/shard_map/ppermute | solution.py:23
  72.7 5.0 %collective-permute-start.13 = (bf16[2,15,16,128]{3,1,2,0:T(8,128)(2,1)S(1)}, bf16[2,15,16,128]{3,1,2,0:T(8,128)(2,1)S(1)}, u32[]{:S(2)}, u32[]{:S(2)}) collective-permute-start(bf16[2,15,16,128]{3,1,2,0:T(8,128)(2,1)S(1)} %slice_select_fusion), channel_id=1, source_target_pairs={{0,2},{2,0},{1,3},{3,1},{4,6},{6,4},{5,7},{7,5},{8,10},{10,8},{9,1... | collective-permute-start | bytes 368648 | tf_op jit(solution)/shard_map/ppermute | solution.py:119
  79.0 5.4 %collective-permute-start.14 = (f32[32,16,128]{2,1,0:T(8,128)S(1)}, f32[32,16,128]{2,1,0:T(8,128)S(1)}, u32[]{:S(2)}, u32[]{:S(2)}) collective-permute-start(f32[32,16,128]{2,1,0:T(8,128)S(1)} %get-tuple-element.47), channel_id=1, source_target_pairs={{0,1},{1,0},{2,3},{3,2},{4,5},{5,4},{6,7},{7,6},{8,9},{9,8},{10,11... | collective-permute-start | bytes 786440 | tf_op jit(solution)/shard_map/ppermute | solution.py:23

commit v29 on v27

--- a/solution.py
+++ b/solution.py
@@ -76,7 +76,6 @@
     reach = kernels.shape[2] // 2
     views = range(kernels.shape[0])
     along_x = jnp.stack([band_matrix(kernels[v, 0], width_x + 2 * reach, width_x, 0).T for v in views])
-    along_x = jnp.broadcast_to(along_x[:, None], (along_x.shape[0], plane_count) + along_x.shape[1:])
     return lax.optimization_barrier((
         along_x,
         jnp.stack([band_matrix(kernels[v, 1], width_y, width_y, reach) for v in views]),
@@ -203,14 +202,14 @@
         low, high = x_rims(estimate_low, reach, 1)
         extended = jnp.concatenate([low, estimate_low, high], axis=1)
         after_x = jnp.einsum(
-            "vzpa,zay->vzpy", forward_ops[0], extended, preferred_element_type=jnp.float32
+            "vpa,zay->vzpy", forward_ops[0], extended, preferred_element_type=jnp.float32
         ).astype(jnp.bfloat16)
         blurred = pass_z_views(pass_y_views(after_x, forward_ops[1]), forward_ops[2], reach)
         quotients = (observed / blurred).astype(jnp.bfloat16)
         low, high = x_rims(quotients, reach, 2)
         widened = jnp.concatenate([low, quotients, high], axis=2)
         after_x = jnp.einsum(
-            "vzpa,vzay->vzpy", adjoint_ops[0], widened, preferred_element_type=jnp.float32
+            "vpa,vzay->vzpy", adjoint_ops[0], widened, preferred_element_type=jnp.float32
         ).astype(jnp.bfloat16)
         backs = pass_z_views(pass_y_views(after_x, adjoint_ops[1]), adjoint_ops[2], reach)
         estimate = estimate * (0.5 * (backs[0] + backs[1]))

time: 85.6 us -> 86.1 us (level)
  transfers between devices with their start and end apart: 15 -> 15, of which waited for: 10 -> 10; matrix products, arithmetic and copies ran while one was open for 3% -> 2% of each run, Pallas kernels for 0% -> 0%
where the time goes in v29:
time: 86.1 us; the launch traced here: 85.7 us
  starting transfers between devices  48.2 us (56%)
  waiting for transfers between devices  21.9 us (25%)
  other arithmetic  7.03 us (8%)
  matrix products  5.04 us (6%)
  local copies, waits for them, and re-layouts  3.13 us (4%)
    ppermute x6, starting transfers between devices, from_partner(): return lax.ppermute(block, axis, route)  38.3 us
    ppermute x4, waiting for transfers between devices, z_rims(): got = lax.ppermute(payload, 'view', route)  13.9 us
    ppermute x6, waiting for transfers between devices, from_partner(): return lax.ppermute(block, axis, route)  7.95 us
    ppermute x4, starting transfers between devices, z_rims(): got = lax.ppermute(payload, 'view', route)  6.23 us
    ppermute x4, starting transfers between devices, x_rims(): across = lax.ppermute(outward, ('tile', 'view'), route)  2.92 us
  transfers between devices with their start and end apart: 15, of which 10 were waited for; matrix products, arithmetic and copies ran while one was open for 2% of the time, Pallas kernels for 0%

profile of v29, /device:TPU:0, one launch (start us, length us, event | category | flops | bytes accessed | tf_op | source)
XLA Modules:
  0.0 85.7 jit_solution(47017559380690746)
XLA Ops:
  0.0 0.9 %fusion.76 = (s32[4]{0:T(128)S(1)}, s32[4]{0:T(128)S(1)}, s32[4]{0:T(128)S(1)}, s32[4]{0:T(128)S(1)}) fusion(s32[1,32]{1,0:T(1,128)} %param.5, s32[]{:T(128)S(6)} %select_n.334, s32[]{:T(128)S(6)} %select_n.335, s32[]{:T(128)S(6)} %select_n.337, s32[]{:T(128)S(6)} %select_n.336), kind=kLoop, calls=%fused_computation.188 | loop fusion | bytes 144 | tf_op jit(solution)/shard_map/dynamic_slice | solution.py:164
  1.0 0.8 gather_fusion
  3.0 1.5 %collective-permute-done = bf16[2,64,16,128]{3,2,1,0:T(8,128)(2,1)S(1)} collective-permute-done((bf16[2,64,16,128]{3,2,1,0:T(8,128)(2,1)S(1)}, bf16[2,64,16,128]{3,2,1,0:T(8,128)(2,1)S(1)}, u32[]{:S(2)}, u32[]{:S(2)}) %collective-permute-start) | collective-permute-done | bytes 524320 | tf_op jit(solution)/shard_map/ppermute | solution.py:23
  6.8 1.0 %select_reduce_fusion.3 = (bf16[128,128]{1,0:T(8,128)(2,1)S(1)}, bf16[128,128]{1,0:T(8,128)(2,1)S(1)}, bf16[128,128]{1,0:T(8,128)(2,1)S(1)}, bf16[128,128]{1,0:T(8,128)(2,1)S(1)}) fusion(f32[31]{0:T(128)S(1)} %get-tuple-element.90, s32[128,128]{1,0:T(8,128)S(1)} %subtract_add_fusion, f32[31]{0:T(128)S(1)} %get-tuple-element.75, f32[31]{0:T(128)S(1)} %get-tuple-element.74, ...), kind=kLoop, calls=%fused_computation.4 | loop fusion | flops 4505600 | bytes 197104 | tf_op jit(solution)/shard_map/reduce_sum | solution.py:45
  8.9 12.2 %collective-permute-start.3 = (bf16[64,15,128]{2,1,0:T(8,128)(2,1)S(1)}, bf16[64,15,128]{2,1,0:T(8,128)(2,1)S(1)}, u32[]{:S(2)}, u32[]{:S(2)}) collective-permute-start(bf16[64,15,128]{2,1,0:T(8,128)(2,1)S(1)} %get-tuple-element.62), channel_id=1, source_target_pairs={{0,1},{1,0},{2,3},{3,2},{4,5},{5,4},{6,7},{7,6},{8,9},{9,8},{10,11... | collective-permute-start | bytes 737288 | tf_op jit(solution)/shard_map/ppermute | solution.py:23
  21.2 1.1 %collective-permute-done.3 = bf16[64,15,128]{2,1,0:T(8,128)(2,1)S(1)} collective-permute-done((bf16[64,15,128]{2,1,0:T(8,128)(2,1)S(1)}, bf16[64,15,128]{2,1,0:T(8,128)(2,1)S(1)}, u32[]{:S(2)}, u32[]{:S(2)}) %collective-permute-start.3) | collective-permute-done | bytes 245792 | tf_op jit(solution)/shard_map/ppermute | solution.py:23
  23.2 1.6 %collective-permute-start.4 = (bf16[2,15,16,128]{3,1,2,0:T(8,128)(2,1)S(1)}, bf16[2,15,16,128]{3,1,2,0:T(8,128)(2,1)S(1)}, u32[]{:S(2)}, u32[]{:S(2)}) collective-permute-start(bf16[2,15,16,128]{3,1,2,0:T(8,128)(2,1)S(1)} %slice_select_fusion.3), channel_id=1, source_target_pairs={{0,2},{2,0},{1,3},{3,1},{4,6},{6,4},{5,7},{7,5},{8,10},{10,8},{9,1... | collective-permute-start | bytes 368648 | tf_op jit(solution)/shard_map/ppermute | solution.py:118
  24.8 3.5 %collective-permute-done.4 = bf16[2,15,16,128]{3,1,2,0:T(8,128)(2,1)S(1)} collective-permute-done((bf16[2,15,16,128]{3,1,2,0:T(8,128)(2,1)S(1)}, bf16[2,15,16,128]{3,1,2,0:T(8,128)(2,1)S(1)}, u32[]{:S(2)}, u32[]{:S(2)}) %collective-permute-start.4) | collective-permute-done | bytes 122912 | tf_op jit(solution)/shard_map/ppermute | solution.py:118
  30.2 6.4 %collective-permute-start.6 = (bf16[2,64,15,128]{3,2,1,0:T(8,128)(2,1)S(1)}, bf16[2,64,15,128]{3,2,1,0:T(8,128)(2,1)S(1)}, u32[]{:S(2)}, u32[]{:S(2)}) collective-permute-start(bf16[2,64,15,128]{3,2,1,0:T(8,128)(2,1)S(1)} %get-tuple-element.54), channel_id=1, source_target_pairs={{0,1},{1,0},{2,3},{3,2},{4,5},{5,4},{6,7},{7,6},{8,9},{9,8},{10,11... | collective-permute-start | bytes 1474568 | tf_op jit(solution)/shard_map/ppermute | solution.py:23
  36.7 1.5 %collective-permute-done.6 = bf16[2,64,15,128]{3,2,1,0:T(8,128)(2,1)S(1)} collective-permute-done((bf16[2,64,15,128]{3,2,1,0:T(8,128)(2,1)S(1)}, bf16[2,64,15,128]{3,2,1,0:T(8,128)(2,1)S(1)}, u32[]{:S(2)}, u32[]{:S(2)}) %collective-permute-start.6) | collective-permute-done | bytes 491552 | tf_op jit(solution)/shard_map/ppermute | solution.py:23
  39.3 1.6 %collective-permute-start.7 = (bf16[2,15,16,128]{3,1,2,0:T(8,128)(2,1)S(1)}, bf16[2,15,16,128]{3,1,2,0:T(8,128)(2,1)S(1)}, u32[]{:S(2)}, u32[]{:S(2)}) collective-permute-start(bf16[2,15,16,128]{3,1,2,0:T(8,128)(2,1)S(1)} %slice_select_fusion.2), channel_id=1, source_target_pairs={{0,2},{2,0},{1,3},{3,1},{4,6},{6,4},{5,7},{7,5},{8,10},{10,8},{9,1... | collective-permute-start | bytes 368648 | tf_op jit(solution)/shard_map/ppermute | solution.py:118
  40.8 3.5 %collective-permute-done.7 = bf16[2,15,16,128]{3,1,2,0:T(8,128)(2,1)S(1)} collective-permute-done((bf16[2,15,16,128]{3,1,2,0:T(8,128)(2,1)S(1)}, bf16[2,15,16,128]{3,1,2,0:T(8,128)(2,1)S(1)}, u32[]{:S(2)}, u32[]{:S(2)}) %collective-permute-start.7) | collective-permute-done | bytes 122912 | tf_op jit(solution)/shard_map/ppermute | solution.py:118
  46.3 8.8 %collective-permute-start.9 = (bf16[64,15,128]{2,1,0:T(8,128)(2,1)S(1)}, bf16[64,15,128]{2,1,0:T(8,128)(2,1)S(1)}, u32[]{:S(2)}, u32[]{:S(2)}) collective-permute-start(bf16[64,15,128]{2,1,0:T(8,128)(2,1)S(1)} %get-tuple-element.60), channel_id=1, source_target_pairs={{0,1},{1,0},{2,3},{3,2},{4,5},{5,4},{6,7},{7,6},{8,9},{9,8},{10,11... | collective-permute-start | bytes 737288 | tf_op jit(solution)/shard_map/ppermute | solution.py:23
  55.1 1.2 %collective-permute-done.9 = bf16[64,15,128]{2,1,0:T(8,128)(2,1)S(1)} collective-permute-done((bf16[64,15,128]{2,1,0:T(8,128)(2,1)S(1)}, bf16[64,15,128]{2,1,0:T(8,128)(2,1)S(1)}, u32[]{:S(2)}, u32[]{:S(2)}) %collective-permute-start.9) | collective-permute-done | bytes 245792 | tf_op jit(solution)/shard_map/ppermute | solution.py:23
  57.2 1.6 %collective-permute-start.10 = (bf16[2,15,16,128]{3,1,2,0:T(8,128)(2,1)S(1)}, bf16[2,15,16,128]{3,1,2,0:T(8,128)(2,1)S(1)}, u32[]{:S(2)}, u32[]{:S(2)}) collective-permute-start(bf16[2,15,16,128]{3,1,2,0:T(8,128)(2,1)S(1)} %slice_select_fusion.1), channel_id=1, source_target_pairs={{0,2},{2,0},{1,3},{3,1},{4,6},{6,4},{5,7},{7,5},{8,10},{10,8},{9,1... | collective-permute-start | bytes 368648 | tf_op jit(solution)/shard_map/ppermute | solution.py:118
  58.8 3.5 %collective-permute-done.10 = bf16[2,15,16,128]{3,1,2,0:T(8,128)(2,1)S(1)} collective-permute-done((bf16[2,15,16,128]{3,1,2,0:T(8,128)(2,1)S(1)}, bf16[2,15,16,128]{3,1,2,0:T(8,128)(2,1)S(1)}, u32[]{:S(2)}, u32[]{:S(2)}) %collective-permute-start.10) | collective-permute-done | bytes 122912 | tf_op jit(solution)/shard_map/ppermute | solution.py:118
  63.5 0.9 %collective-permute-start.11 = (bf16[2,64,15,128]{3,2,1,0:T(8,128)(2,1)S(1)}, bf16[2,64,15,128]{3,2,1,0:T(8,128)(2,1)S(1)}, u32[]{:S(2)}, u32[]{:S(2)}) collective-permute-start(bf16[2,64,15,128]{3,2,1,0:T(8,128)(2,1)S(1)} %get-tuple-element.49), channel_id=1, source_target_pairs={{1,4},{4,1},{3,6},{6,3},{5,8},{8,5},{7,10},{10,7},{9,12},{12,9},{1... | collective-permute-start | bytes 1474568 | tf_op jit(solution)/shard_map/ppermute | solution.py:139
  64.4 6.1 %collective-permute-start.12 = (bf16[2,64,15,128]{3,2,1,0:T(8,128)(2,1)S(1)}, bf16[2,64,15,128]{3,2,1,0:T(8,128)(2,1)S(1)}, u32[]{:S(2)}, u32[]{:S(2)}) collective-permute-start(bf16[2,64,15,128]{3,2,1,0:T(8,128)(2,1)S(1)} %get-tuple-element.50), channel_id=1, source_target_pairs={{0,1},{1,0},{2,3},{3,2},{4,5},{5,4},{6,7},{7,6},{8,9},{9,8},{10,11... | collective-permute-start | bytes 1474568 | tf_op jit(solution)/shard_map/ppermute | solution.py:23
  70.5 1.5 %collective-permute-done.12 = bf16[2,64,15,128]{3,2,1,0:T(8,128)(2,1)S(1)} collective-permute-done((bf16[2,64,15,128]{3,2,1,0:T(8,128)(2,1)S(1)}, bf16[2,64,15,128]{3,2,1,0:T(8,128)(2,1)S(1)}, u32[]{:S(2)}, u32[]{:S(2)}) %collective-permute-start.12) | collective-permute-done | bytes 491552 | tf_op jit(solution)/shard_map/ppermute | solution.py:23
  73.1 1.6 %collective-permute-start.13 = (bf16[2,15,16,128]{3,1,2,0:T(8,128)(2,1)S(1)}, bf16[2,15,16,128]{3,1,2,0:T(8,128)(2,1)S(1)}, u32[]{:S(2)}, u32[]{:S(2)}) collective-permute-start(bf16[2,15,16,128]{3,1,2,0:T(8,128)(2,1)S(1)} %slice_select_fusion), channel_id=1, source_target_pairs={{0,2},{2,0},{1,3},{3,1},{4,6},{6,4},{5,7},{7,5},{8,10},{10,8},{9,1... | collective-permute-start | bytes 368648 | tf_op jit(solution)/shard_map/ppermute | solution.py:118
  74.7 3.5 %collective-permute-done.13 = bf16[2,15,16,128]{3,1,2,0:T(8,128)(2,1)S(1)} collective-permute-done((bf16[2,15,16,128]{3,1,2,0:T(8,128)(2,1)S(1)}, bf16[2,15,16,128]{3,1,2,0:T(8,128)(2,1)S(1)}, u32[]{:S(2)}, u32[]{:S(2)}) %collective-permute-start.13) | collective-permute-done | bytes 122912 | tf_op jit(solution)/shard_map/ppermute | solution.py:118
  79.4 4.3 %collective-permute-start.14 = (f32[32,16,128]{2,1,0:T(8,128)S(1)}, f32[32,16,128]{2,1,0:T(8,128)S(1)}, u32[]{:S(2)}, u32[]{:S(2)}) collective-permute-start(f32[32,16,128]{2,1,0:T(8,128)S(1)} %get-tuple-element.47), channel_id=1, source_target_pairs={{0,1},{1,0},{2,3},{3,2},{4,5},{5,4},{6,7},{7,6},{8,9},{9,8},{10,11... | collective-permute-start | bytes 786440 | tf_op jit(solution)/shard_map/ppermute | solution.py:23
  83.7 1.2 %collective-permute-done.14 = f32[32,16,128]{2,1,0:T(8,128)S(1)} collective-permute-done((f32[32,16,128]{2,1,0:T(8,128)S(1)}, f32[32,16,128]{2,1,0:T(8,128)S(1)}, u32[]{:S(2)}, u32[]{:S(2)}) %collective-permute-start.14) | collective-permute-done | bytes 262176 | tf_op jit(solution)/shard_map/ppermute | solution.py:23
  84.8 0.9 %fusion.56 = f32[32,32,128]{2,1,0:T(8,128)} fusion(s32[]{:T(128)S(6)} %select_n.399, f32[32,16,128]{2,1,0:T(8,128)S(1)} %get-tuple-element.48, f32[32,16,128]{2,1,0:T(8,128)S(1)} %collective-permute-done.14), kind=kLoop, calls=%fused_computation.78 | loop fusion | flops 262144 | bytes 1048580 | tf_op jit(solution)/shard_map/concatenate | solution.py:219
  (92 shorter events, 14.9 us)
Async XLA Ops:
  0.0 1.8 %copy-start = (bf16[64,32,128]{2,1,0:T(8,128)(2,1)S(1)}, bf16[64,32,128]{2,1,0:T(8,128)(2,1)}, u32[]{:S(2)}) copy-start(bf16[64,32,128]{2,1,0:T(8,128)(2,1)} %param.3) | copy-start | bytes 1572868
  2.5 2.1 %collective-permute-start = (bf16[2,64,16,128]{3,2,1,0:T(8,128)(2,1)S(1)}, bf16[2,64,16,128]{3,2,1,0:T(8,128)(2,1)S(1)}, u32[]{:S(2)}, u32[]{:S(2)}) collective-permute-start(bf16[2,64,16,128]{3,2,1,0:T(8,128)(2,1)S(1)} %pad_maximum_fusion), channel_id=1, source_target_pairs={{0,1},{1,0},{2,3},{3,2},{4,5},{5,4},{6,7},{7,6},{8,9},{9,8},{10,11... | collective-permute-start | bytes 1572872 | tf_op jit(solution)/shard_map/ppermute | solution.py:23
  3.0 1.6 %copy-start.1 = (f32[2,3,31]{2,0,1:T(2,128)S(1)}, f32[2,3,31]{2,0,1:T(2,128)}, u32[]{:S(2)}) copy-start(f32[2,3,31]{2,0,1:T(2,128)} %param.4) | copy-start | bytes 2236
  5.2 2.6 %collective-permute-start.1 = (bf16[2,64,16,128]{3,2,1,0:T(8,128)(2,1)S(1)}, bf16[2,64,16,128]{3,2,1,0:T(8,128)(2,1)S(1)}, u32[]{:S(2)}, u32[]{:S(2)}) collective-permute-start(bf16[2,64,16,128]{3,2,1,0:T(8,128)(2,1)S(1)} %pad_maximum_fusion.1), channel_id=1, source_target_pairs={{1,4},{4,1},{3,6},{6,3},{5,8},{8,5},{7,10},{10,7},{9,12},{12,9},{1... | collective-permute-start | bytes 1572872 | tf_op jit(solution)/shard_map/ppermute | solution.py:191
  8.2 13.0 %collective-permute-start.2 = (bf16[64,15,128]{2,1,0:T(8,128)(2,1)S(1)}, bf16[64,15,128]{2,1,0:T(8,128)(2,1)S(1)}, u32[]{:S(2)}, u32[]{:S(2)}) collective-permute-start(bf16[64,15,128]{2,1,0:T(8,128)(2,1)S(1)} %get-tuple-element.61), channel_id=1, source_target_pairs={{1,4},{4,1},{3,6},{6,3},{5,8},{8,5},{7,10},{10,7},{9,12},{12,9},{1... | collective-permute-start | bytes 737288 | tf_op jit(solution)/shard_map/ppermute | solution.py:139
  8.9 13.4 %collective-permute-start.3 = (bf16[64,15,128]{2,1,0:T(8,128)(2,1)S(1)}, bf16[64,15,128]{2,1,0:T(8,128)(2,1)S(1)}, u32[]{:S(2)}, u32[]{:S(2)}) collective-permute-start(bf16[64,15,128]{2,1,0:T(8,128)(2,1)S(1)} %get-tuple-element.62), channel_id=1, source_target_pairs={{0,1},{1,0},{2,3},{3,2},{4,5},{5,4},{6,7},{7,6},{8,9},{9,8},{10,11... | collective-permute-start | bytes 737288 | tf_op jit(solution)/shard_map/ppermute | solution.py:23
  23.2 5.0 %collective-permute-start.4 = (bf16[2,15,16,128]{3,1,2,0:T(8,128)(2,1)S(1)}, bf16[2,15,16,128]{3,1,2,0:T(8,128)(2,1)S(1)}, u32[]{:S(2)}, u32[]{:S(2)}) collective-permute-start(bf16[2,15,16,128]{3,1,2,0:T(8,128)(2,1)S(1)} %slice_select_fusion.3), channel_id=1, source_target_pairs={{0,2},{2,0},{1,3},{3,1},{4,6},{6,4},{5,7},{7,5},{8,10},{10,8},{9,1... | collective-permute-start | bytes 368648 | tf_op jit(solution)/shard_map/ppermute | solution.py:118
  29.5 7.1 %collective-permute-start.5 = (bf16[2,64,15,128]{3,2,1,0:T(8,128)(2,1)S(1)}, bf16[2,64,15,128]{3,2,1,0:T(8,128)(2,1)S(1)}, u32[]{:S(2)}, u32[]{:S(2)}) collective-permute-start(bf16[2,64,15,128]{3,2,1,0:T(8,128)(2,1)S(1)} %get-tuple-element.53), channel_id=1, source_target_pairs={{1,4},{4,1},{3,6},{6,3},{5,8},{8,5},{7,10},{10,7},{9,12},{12,9},{1... | collective-permute-start | bytes 1474568 | tf_op jit(solution)/shard_map/ppermute | solution.py:139
  30.2 7.9 %collective-permute-start.6 = (bf16[2,64,15,128]{3,2,1,0:T(8,128)(2,1)S(1)}, bf16[2,64,15,128]{3,2,1,0:T(8,128)(2,1)S(1)}, u32[]{:S(2)}, u32[]{:S(2)}) collective-permute-start(bf16[2,64,15,128]{3,2,1,0:T(8,128)(2,1)S(1)} %get-tuple-element.54), channel_id=1, source_target_pairs={{0,1},{1,0},{2,3},{3,2},{4,5},{5,4},{6,7},{7,6},{8,9},{9,8},{10,11... | collective-permute-start | bytes 1474568 | tf_op jit(solution)/shard_map/ppermute | solution.py:23
  39.3 5.0 %collective-permute-start.7 = (bf16[2,15,16,128]{3,1,2,0:T(8,128)(2,1)S(1)}, bf16[2,15,16,128]{3,1,2,0:T(8,128)(2,1)S(1)}, u32[]{:S(2)}, u32[]{:S(2)}) collective-permute-start(bf16[2,15,16,128]{3,1,2,0:T(8,128)(2,1)S(1)} %slice_select_fusion.2), channel_id=1, source_target_pairs={{0,2},{2,0},{1,3},{3,1},{4,6},{6,4},{5,7},{7,5},{8,10},{10,8},{9,1... | collective-permute-start | bytes 368648 | tf_op jit(solution)/shard_map/ppermute | solution.py:118
  45.6 9.5 %collective-permute-start.8 = (bf16[64,15,128]{2,1,0:T(8,128)(2,1)S(1)}, bf16[64,15,128]{2,1,0:T(8,128)(2,1)S(1)}, u32[]{:S(2)}, u32[]{:S(2)}) collective-permute-start(bf16[64,15,128]{2,1,0:T(8,128)(2,1)S(1)} %get-tuple-element.59), channel_id=1, source_target_pairs={{1,4},{4,1},{3,6},{6,3},{5,8},{8,5},{7,10},{10,7},{9,12},{12,9},{1... | collective-permute-start | bytes 737288 | tf_op jit(solution)/shard_map/ppermute | solution.py:139
  46.3 10.0 %collective-permute-start.9 = (bf16[64,15,128]{2,1,0:T(8,128)(2,1)S(1)}, bf16[64,15,128]{2,1,0:T(8,128)(2,1)S(1)}, u32[]{:S(2)}, u32[]{:S(2)}) collective-permute-start(bf16[64,15,128]{2,1,0:T(8,128)(2,1)S(1)} %get-tuple-element.60), channel_id=1, source_target_pairs={{0,1},{1,0},{2,3},{3,2},{4,5},{5,4},{6,7},{7,6},{8,9},{9,8},{10,11... | collective-permute-start | bytes 737288 | tf_op jit(solution)/shard_map/ppermute | solution.py:23
  57.2 5.0 %collective-permute-start.10 = (bf16[2,15,16,128]{3,1,2,0:T(8,128)(2,1)S(1)}, bf16[2,15,16,128]{3,1,2,0:T(8,128)(2,1)S(1)}, u32[]{:S(2)}, u32[]{:S(2)}) collective-permute-start(bf16[2,15,16,128]{3,1,2,0:T(8,128)(2,1)S(1)} %slice_select_fusion.1), channel_id=1, source_target_pairs={{0,2},{2,0},{1,3},{3,1},{4,6},{6,4},{5,7},{7,5},{8,10},{10,8},{9,1... | collective-permute-start | bytes 368648 | tf_op jit(solution)/shard_map/ppermute | solution.py:118
  63.5 7.0 %collective-permute-start.11 = (bf16[2,64,15,128]{3,2,1,0:T(8,128)(2,1)S(1)}, bf16[2,64,15,128]{3,2,1,0:T(8,128)(2,1)S(1)}, u32[]{:S(2)}, u32[]{:S(2)}) collective-permute-start(bf16[2,64,15,128]{3,2,1,0:T(8,128)(2,1)S(1)} %get-tuple-element.49), channel_id=1, source_target_pairs={{1,4},{4,1},{3,6},{6,3},{5,8},{8,5},{7,10},{10,7},{9,12},{12,9},{1... | collective-permute-start | bytes 1474568 | tf_op jit(solution)/shard_map/ppermute | solution.py:139
  64.4 7.6 %collective-permute-start.12 = (bf16[2,64,15,128]{3,2,1,0:T(8,128)(2,1)S(1)}, bf16[2,64,15,128]{3,2,1,0:T(8,128)(2,1)S(1)}, u32[]{:S(2)}, u32[]{:S(2)}) collective-permute-start(bf16[2,64,15,128]{3,2,1,0:T(8,128)(2,1)S(1)} %get-tuple-element.50), channel_id=1, source_target_pairs={{0,1},{1,0},{2,3},{3,2},{4,5},{5,4},{6,7},{7,6},{8,9},{9,8},{10,11... | collective-permute-start | bytes 1474568 | tf_op jit(solution)/shard_map/ppermute | solution.py:23
  73.1 5.0 %collective-permute-start.13 = (bf16[2,15,16,128]{3,1,2,0:T(8,128)(2,1)S(1)}, bf16[2,15,16,128]{3,1,2,0:T(8,128)(2,1)S(1)}, u32[]{:S(2)}, u32[]{:S(2)}) collective-permute-start(bf16[2,15,16,128]{3,1,2,0:T(8,128)(2,1)S(1)} %slice_select_fusion), channel_id=1, source_target_pairs={{0,2},{2,0},{1,3},{3,1},{4,6},{6,4},{5,7},{7,5},{8,10},{10,8},{9,1... | collective-permute-start | bytes 368648 | tf_op jit(solution)/shard_map/ppermute | solution.py:118
  79.4 5.4 %collective-permute-start.14 = (f32[32,16,128]{2,1,0:T(8,128)S(1)}, f32[32,16,128]{2,1,0:T(8,128)S(1)}, u32[]{:S(2)}, u32[]{:S(2)}) collective-permute-start(f32[32,16,128]{2,1,0:T(8,128)S(1)} %get-tuple-element.47), channel_id=1, source_target_pairs={{0,1},{1,0},{2,3},{3,2},{4,5},{5,4},{6,7},{7,6},{8,9},{9,8},{10,11... | collective-permute-start | bytes 786440 | tf_op jit(solution)/shard_map/ppermute | solution.py:23

commit v30 on v27

--- a/solution.py
+++ b/solution.py
@@ -77,7 +77,7 @@
     views = range(kernels.shape[0])
     along_x = jnp.stack([band_matrix(kernels[v, 0], width_x + 2 * reach, width_x, 0).T for v in views])
     along_x = jnp.broadcast_to(along_x[:, None], (along_x.shape[0], plane_count) + along_x.shape[1:])
-    return lax.optimization_barrier((
+    return ((
         along_x,
         jnp.stack([band_matrix(kernels[v, 1], width_y, width_y, reach) for v in views]),
         jnp.stack([band_matrix(kernels[v, 2], plane_count + 2 * reach, plane_count, 0).T for v in views]),

time: 85.6 us -> 86.5 us (1.011)
  other arithmetic: 7.01 us -> 9.34 us
  starting transfers between devices: 47.6 us -> 45.4 us
  local copies, waits for them, and re-layouts: 3.27 us -> 5.43 us
  waiting for transfers between devices: 21.7 us -> 20.4 us
    slice x2, local copies, waits for them, and re-layouts: 0.19 us -> 2.51 us  [stacked_operators(): kernels[v, 2]]
    ppermute x6, starting transfers between devices: 37.8 us -> 35.6 us  [from_partner(): return lax.ppermute(block, axis, route)]
    ppermute x6, waiting for transfers between devices: 7.8 us -> 6.27 us  [from_partner(): return lax.ppermute(block, axis, route)]
  transfers between devices with their start and end apart: 15 -> 15, of which waited for: 10 -> 9; matrix products, arithmetic and copies ran while one was open for 3% -> 7% of each run, Pallas kernels for 0% -> 0%
where the time goes in v30:
time: 86.5 us; the launch traced here: 86.1 us
  starting transfers between devices  45.4 us (52%)
  waiting for transfers between devices  20.4 us (24%)
  other arithmetic  9.34 us (11%)
  local copies, waits for them, and re-layouts  5.43 us (6%)
  matrix products  4.97 us (6%)
    ppermute x6, starting transfers between devices, from_partner(): return lax.ppermute(block, axis, route)  35.6 us
    ppermute x4, waiting for transfers between devices, z_rims(): got = lax.ppermute(payload, 'view', route)  14.1 us
    ppermute x6, waiting for transfers between devices, from_partner(): return lax.ppermute(block, axis, route)  6.27 us
    ppermute x4, starting transfers between devices, z_rims(): got = lax.ppermute(payload, 'view', route)  6.22 us
    ppermute x4, starting transfers between devices, x_rims(): across = lax.ppermute(outward, ('tile', 'view'), route)  2.92 us
    slice x2, local copies, waits for them, and re-layouts, stacked_operators(): kernels[v, 2]  2.51 us
  transfers between devices with their start and end apart: 15, of which 9 were waited for; matrix products, arithmetic and copies ran while one was open for 7% of the time, Pallas kernels for 0%

profile of v30, /device:TPU:0, one launch (start us, length us, event | category | flops | bytes accessed | tf_op | source)
XLA Modules:
  0.0 86.1 jit_solution(13180697259744228563)
XLA Ops:
  0.0 0.9 %fusion.72 = (s32[4]{0:T(128)S(1)}, s32[4]{0:T(128)S(1)}, s32[4]{0:T(128)S(1)}, s32[4]{0:T(128)S(1)}) fusion(s32[1,32]{1,0:T(1,128)} %param.5, s32[]{:T(128)S(6)} %select_n.334, s32[]{:T(128)S(6)} %select_n.335, s32[]{:T(128)S(6)} %select_n.337, s32[]{:T(128)S(6)} %select_n.336), kind=kLoop, calls=%fused_computation.184 | loop fusion | bytes 144 | tf_op jit(solution)/shard_map/dynamic_slice | solution.py:165
  3.6 0.9 %collective-permute-done = bf16[2,64,16,128]{3,2,1,0:T(8,128)(2,1)S(1)} collective-permute-done((bf16[2,64,16,128]{3,2,1,0:T(8,128)(2,1)S(1)}, bf16[2,64,16,128]{3,2,1,0:T(8,128)(2,1)S(1)}, u32[]{:S(2)}, u32[]{:S(2)}) %collective-permute-start) | collective-permute-done | bytes 524320 | tf_op jit(solution)/shard_map/ppermute | solution.py:23
  6.7 1.0 %select_reduce_fusion.1 = (bf16[128,128]{1,0:T(8,128)(2,1)S(1)}, bf16[128,128]{1,0:T(8,128)(2,1)S(1)}, bf16[128,128]{1,0:T(8,128)(2,1)S(1)}, bf16[128,128]{1,0:T(8,128)(2,1)S(1)}) fusion(f32[31]{0:T(128)S(1)} %get-tuple-element.78, s32[128,128]{1,0:T(8,128)S(1)} %subtract_add_fusion, f32[31]{0:T(128)S(1)} %get-tuple-element.77, f32[31]{0:T(128)S(1)} %get-tuple-element.65, ...), kind=kLoop, calls=%fused_computation.2 | loop fusion | flops 4505600 | bytes 197104 | tf_op jit(solution)/shard_map/reduce_sum | solution.py:45
  8.8 12.7 %collective-permute-start.3 = (bf16[64,15,128]{2,1,0:T(8,128)(2,1)S(1)}, bf16[64,15,128]{2,1,0:T(8,128)(2,1)S(1)}, u32[]{:S(2)}, u32[]{:S(2)}) collective-permute-start(bf16[64,15,128]{2,1,0:T(8,128)(2,1)S(1)} %get-tuple-element.50), channel_id=1, source_target_pairs={{0,1},{1,0},{2,3},{3,2},{4,5},{5,4},{6,7},{7,6},{8,9},{9,8},{10,11... | collective-permute-start | bytes 737288 | tf_op jit(solution)/shard_map/ppermute | solution.py:23
  22.1 1.2 %slice.139 = bf16[1,1,31]{2,0,1:T(2,128)(2,1)} reverse(bf16[1,1,31]{2,0,1:T(2,128)(2,1)} %get-tuple-element.70), dimensions={2} | reverse | bytes 124 | tf_op jit(solution)/shard_map/slice | solution.py:83
  23.4 1.3 %slice.141 = bf16[1,1,31]{2,0,1:T(2,128)(2,1)} reverse(bf16[1,1,31]{2,0,1:T(2,128)(2,1)} %get-tuple-element.59), dimensions={2} | reverse | bytes 124 | tf_op jit(solution)/shard_map/slice | solution.py:83
  26.2 1.6 %collective-permute-start.4 = (bf16[2,15,16,128]{3,1,2,0:T(8,128)(2,1)S(1)}, bf16[2,15,16,128]{3,1,2,0:T(8,128)(2,1)S(1)}, u32[]{:S(2)}, u32[]{:S(2)}) collective-permute-start(bf16[2,15,16,128]{3,1,2,0:T(8,128)(2,1)S(1)} %slice_select_fusion.3), channel_id=1, source_target_pairs={{0,2},{2,0},{1,3},{3,1},{4,6},{6,4},{5,7},{7,5},{8,10},{10,8},{9,1... | collective-permute-start | bytes 368648 | tf_op jit(solution)/shard_map/ppermute | solution.py:119
  28.3 3.6 %collective-permute-done.4 = bf16[2,15,16,128]{3,1,2,0:T(8,128)(2,1)S(1)} collective-permute-done((bf16[2,15,16,128]{3,1,2,0:T(8,128)(2,1)S(1)}, bf16[2,15,16,128]{3,1,2,0:T(8,128)(2,1)S(1)}, u32[]{:S(2)}, u32[]{:S(2)}) %collective-permute-start.4) | collective-permute-done | bytes 122912 | tf_op jit(solution)/shard_map/ppermute | solution.py:119
  33.9 3.1 %collective-permute-start.6 = (bf16[2,64,15,128]{3,2,1,0:T(8,128)(2,1)S(1)}, bf16[2,64,15,128]{3,2,1,0:T(8,128)(2,1)S(1)}, u32[]{:S(2)}, u32[]{:S(2)}) collective-permute-start(bf16[2,64,15,128]{3,2,1,0:T(8,128)(2,1)S(1)} %get-tuple-element.42), channel_id=1, source_target_pairs={{0,1},{1,0},{2,3},{3,2},{4,5},{5,4},{6,7},{7,6},{8,9},{9,8},{10,11... | collective-permute-start | bytes 1474568 | tf_op jit(solution)/shard_map/ppermute | solution.py:23
  37.0 1.5 %collective-permute-done.6 = bf16[2,64,15,128]{3,2,1,0:T(8,128)(2,1)S(1)} collective-permute-done((bf16[2,64,15,128]{3,2,1,0:T(8,128)(2,1)S(1)}, bf16[2,64,15,128]{3,2,1,0:T(8,128)(2,1)S(1)}, u32[]{:S(2)}, u32[]{:S(2)}) %collective-permute-start.6) | collective-permute-done | bytes 491552 | tf_op jit(solution)/shard_map/ppermute | solution.py:23
  39.7 1.6 %collective-permute-start.7 = (bf16[2,15,16,128]{3,1,2,0:T(8,128)(2,1)S(1)}, bf16[2,15,16,128]{3,1,2,0:T(8,128)(2,1)S(1)}, u32[]{:S(2)}, u32[]{:S(2)}) collective-permute-start(bf16[2,15,16,128]{3,1,2,0:T(8,128)(2,1)S(1)} %slice_select_fusion.2), channel_id=1, source_target_pairs={{0,2},{2,0},{1,3},{3,1},{4,6},{6,4},{5,7},{7,5},{8,10},{10,8},{9,1... | collective-permute-start | bytes 368648 | tf_op jit(solution)/shard_map/ppermute | solution.py:119
  41.3 3.5 %collective-permute-done.7 = bf16[2,15,16,128]{3,1,2,0:T(8,128)(2,1)S(1)} collective-permute-done((bf16[2,15,16,128]{3,1,2,0:T(8,128)(2,1)S(1)}, bf16[2,15,16,128]{3,1,2,0:T(8,128)(2,1)S(1)}, u32[]{:S(2)}, u32[]{:S(2)}) %collective-permute-start.7) | collective-permute-done | bytes 122912 | tf_op jit(solution)/shard_map/ppermute | solution.py:119
  46.7 8.8 %collective-permute-start.9 = (bf16[64,15,128]{2,1,0:T(8,128)(2,1)S(1)}, bf16[64,15,128]{2,1,0:T(8,128)(2,1)S(1)}, u32[]{:S(2)}, u32[]{:S(2)}) collective-permute-start(bf16[64,15,128]{2,1,0:T(8,128)(2,1)S(1)} %get-tuple-element.48), channel_id=1, source_target_pairs={{0,1},{1,0},{2,3},{3,2},{4,5},{5,4},{6,7},{7,6},{8,9},{9,8},{10,11... | collective-permute-start | bytes 737288 | tf_op jit(solution)/shard_map/ppermute | solution.py:23
  55.5 1.2 %collective-permute-done.9 = bf16[64,15,128]{2,1,0:T(8,128)(2,1)S(1)} collective-permute-done((bf16[64,15,128]{2,1,0:T(8,128)(2,1)S(1)}, bf16[64,15,128]{2,1,0:T(8,128)(2,1)S(1)}, u32[]{:S(2)}, u32[]{:S(2)}) %collective-permute-start.9) | collective-permute-done | bytes 245792 | tf_op jit(solution)/shard_map/ppermute | solution.py:23
  57.6 1.6 %collective-permute-start.10 = (bf16[2,15,16,128]{3,1,2,0:T(8,128)(2,1)S(1)}, bf16[2,15,16,128]{3,1,2,0:T(8,128)(2,1)S(1)}, u32[]{:S(2)}, u32[]{:S(2)}) collective-permute-start(bf16[2,15,16,128]{3,1,2,0:T(8,128)(2,1)S(1)} %slice_select_fusion.1), channel_id=1, source_target_pairs={{0,2},{2,0},{1,3},{3,1},{4,6},{6,4},{5,7},{7,5},{8,10},{10,8},{9,1... | collective-permute-start | bytes 368648 | tf_op jit(solution)/shard_map/ppermute | solution.py:119
  59.1 3.5 %collective-permute-done.10 = bf16[2,15,16,128]{3,1,2,0:T(8,128)(2,1)S(1)} collective-permute-done((bf16[2,15,16,128]{3,1,2,0:T(8,128)(2,1)S(1)}, bf16[2,15,16,128]{3,1,2,0:T(8,128)(2,1)S(1)}, u32[]{:S(2)}, u32[]{:S(2)}) %collective-permute-start.10) | collective-permute-done | bytes 122912 | tf_op jit(solution)/shard_map/ppermute | solution.py:119
  63.9 0.9 %collective-permute-start.11 = (bf16[2,64,15,128]{3,2,1,0:T(8,128)(2,1)S(1)}, bf16[2,64,15,128]{3,2,1,0:T(8,128)(2,1)S(1)}, u32[]{:S(2)}, u32[]{:S(2)}) collective-permute-start(bf16[2,64,15,128]{3,2,1,0:T(8,128)(2,1)S(1)} %get-tuple-element.37), channel_id=1, source_target_pairs={{1,4},{4,1},{3,6},{6,3},{5,8},{8,5},{7,10},{10,7},{9,12},{12,9},{1... | collective-permute-start | bytes 1474568 | tf_op jit(solution)/shard_map/ppermute | solution.py:140
  64.7 6.1 %collective-permute-start.12 = (bf16[2,64,15,128]{3,2,1,0:T(8,128)(2,1)S(1)}, bf16[2,64,15,128]{3,2,1,0:T(8,128)(2,1)S(1)}, u32[]{:S(2)}, u32[]{:S(2)}) collective-permute-start(bf16[2,64,15,128]{3,2,1,0:T(8,128)(2,1)S(1)} %get-tuple-element.38), channel_id=1, source_target_pairs={{0,1},{1,0},{2,3},{3,2},{4,5},{5,4},{6,7},{7,6},{8,9},{9,8},{10,11... | collective-permute-start | bytes 1474568 | tf_op jit(solution)/shard_map/ppermute | solution.py:23
  70.8 1.5 %collective-permute-done.12 = bf16[2,64,15,128]{3,2,1,0:T(8,128)(2,1)S(1)} collective-permute-done((bf16[2,64,15,128]{3,2,1,0:T(8,128)(2,1)S(1)}, bf16[2,64,15,128]{3,2,1,0:T(8,128)(2,1)S(1)}, u32[]{:S(2)}, u32[]{:S(2)}) %collective-permute-start.12) | collective-permute-done | bytes 491552 | tf_op jit(solution)/shard_map/ppermute | solution.py:23
  73.5 1.6 %collective-permute-start.13 = (bf16[2,15,16,128]{3,1,2,0:T(8,128)(2,1)S(1)}, bf16[2,15,16,128]{3,1,2,0:T(8,128)(2,1)S(1)}, u32[]{:S(2)}, u32[]{:S(2)}) collective-permute-start(bf16[2,15,16,128]{3,1,2,0:T(8,128)(2,1)S(1)} %slice_select_fusion), channel_id=1, source_target_pairs={{0,2},{2,0},{1,3},{3,1},{4,6},{6,4},{5,7},{7,5},{8,10},{10,8},{9,1... | collective-permute-start | bytes 368648 | tf_op jit(solution)/shard_map/ppermute | solution.py:119
  75.1 3.5 %collective-permute-done.13 = bf16[2,15,16,128]{3,1,2,0:T(8,128)(2,1)S(1)} collective-permute-done((bf16[2,15,16,128]{3,1,2,0:T(8,128)(2,1)S(1)}, bf16[2,15,16,128]{3,1,2,0:T(8,128)(2,1)S(1)}, u32[]{:S(2)}, u32[]{:S(2)}) %collective-permute-start.13) | collective-permute-done | bytes 122912 | tf_op jit(solution)/shard_map/ppermute | solution.py:119
  79.7 4.3 %collective-permute-start.14 = (f32[32,16,128]{2,1,0:T(8,128)S(1)}, f32[32,16,128]{2,1,0:T(8,128)S(1)}, u32[]{:S(2)}, u32[]{:S(2)}) collective-permute-start(f32[32,16,128]{2,1,0:T(8,128)S(1)} %get-tuple-element.35), channel_id=1, source_target_pairs={{0,1},{1,0},{2,3},{3,2},{4,5},{5,4},{6,7},{7,6},{8,9},{9,8},{10,11... | collective-permute-start | bytes 786440 | tf_op jit(solution)/shard_map/ppermute | solution.py:23
  84.0 1.2 %collective-permute-done.14 = f32[32,16,128]{2,1,0:T(8,128)S(1)} collective-permute-done((f32[32,16,128]{2,1,0:T(8,128)S(1)}, f32[32,16,128]{2,1,0:T(8,128)S(1)}, u32[]{:S(2)}, u32[]{:S(2)}) %collective-permute-start.14) | collective-permute-done | bytes 262176 | tf_op jit(solution)/shard_map/ppermute | solution.py:23
  85.2 0.9 %fusion.56 = f32[32,32,128]{2,1,0:T(8,128)} fusion(s32[]{:T(128)S(6)} %select_n.399, f32[32,16,128]{2,1,0:T(8,128)S(1)} %get-tuple-element.36, f32[32,16,128]{2,1,0:T(8,128)S(1)} %collective-permute-done.14), kind=kLoop, calls=%fused_computation.78 | loop fusion | flops 262144 | bytes 1048580 | tf_op jit(solution)/shard_map/concatenate | solution.py:220
  (96 shorter events, 17.8 us)
Async XLA Ops:
  0.0 1.8 %copy-start = (bf16[64,32,128]{2,1,0:T(8,128)(2,1)S(1)}, bf16[64,32,128]{2,1,0:T(8,128)(2,1)}, u32[]{:S(2)}) copy-start(bf16[64,32,128]{2,1,0:T(8,128)(2,1)} %param.3) | copy-start | bytes 1572868
  2.5 2.1 %collective-permute-start = (bf16[2,64,16,128]{3,2,1,0:T(8,128)(2,1)S(1)}, bf16[2,64,16,128]{3,2,1,0:T(8,128)(2,1)S(1)}, u32[]{:S(2)}, u32[]{:S(2)}) collective-permute-start(bf16[2,64,16,128]{3,2,1,0:T(8,128)(2,1)S(1)} %pad_maximum_fusion), channel_id=1, source_target_pairs={{0,1},{1,0},{2,3},{3,2},{4,5},{5,4},{6,7},{7,6},{8,9},{9,8},{10,11... | collective-permute-start | bytes 1572872 | tf_op jit(solution)/shard_map/ppermute | solution.py:23
  3.6 1.0 %copy-start.2 = (f32[2,3,31]{2,0,1:T(2,128)S(1)}, f32[2,3,31]{2,0,1:T(2,128)}, u32[]{:S(2)}) copy-start(f32[2,3,31]{2,0,1:T(2,128)} %param.4) | copy-start | bytes 2236
  5.6 2.1 %collective-permute-start.1 = (bf16[2,64,16,128]{3,2,1,0:T(8,128)(2,1)S(1)}, bf16[2,64,16,128]{3,2,1,0:T(8,128)(2,1)S(1)}, u32[]{:S(2)}, u32[]{:S(2)}) collective-permute-start(bf16[2,64,16,128]{3,2,1,0:T(8,128)(2,1)S(1)} %pad_maximum_fusion.1), channel_id=1, source_target_pairs={{1,4},{4,1},{3,6},{6,3},{5,8},{8,5},{7,10},{10,7},{9,12},{12,9},{1... | collective-permute-start | bytes 1572872 | tf_op jit(solution)/shard_map/ppermute | solution.py:192
  8.1 17.2 %collective-permute-start.2 = (bf16[64,15,128]{2,1,0:T(8,128)(2,1)S(1)}, bf16[64,15,128]{2,1,0:T(8,128)(2,1)S(1)}, u32[]{:S(2)}, u32[]{:S(2)}) collective-permute-start(bf16[64,15,128]{2,1,0:T(8,128)(2,1)S(1)} %get-tuple-element.49), channel_id=1, source_target_pairs={{1,4},{4,1},{3,6},{6,3},{5,8},{8,5},{7,10},{10,7},{9,12},{12,9},{1... | collective-permute-start | bytes 737288 | tf_op jit(solution)/shard_map/ppermute | solution.py:140
  8.8 16.5 %collective-permute-start.3 = (bf16[64,15,128]{2,1,0:T(8,128)(2,1)S(1)}, bf16[64,15,128]{2,1,0:T(8,128)(2,1)S(1)}, u32[]{:S(2)}, u32[]{:S(2)}) collective-permute-start(bf16[64,15,128]{2,1,0:T(8,128)(2,1)S(1)} %get-tuple-element.50), channel_id=1, source_target_pairs={{0,1},{1,0},{2,3},{3,2},{4,5},{5,4},{6,7},{7,6},{8,9},{9,8},{10,11... | collective-permute-start | bytes 737288 | tf_op jit(solution)/shard_map/ppermute | solution.py:23
  22.1 3.2 %copy-start.3 = (bf16[2,16,46]{2,1,0:T(8,128)(2,1)S(1)}, bf16[2,16,46]{2,1,0:T(8,128)(2,1)}, u32[]{:S(2)}) copy-start(bf16[2,16,46]{2,1,0:T(8,128)(2,1)} %pad_maximum_fusion.9) | copy-start | bytes 8836
  25.7 2.1 %copy-start.1 = (s32[94,64]{0,1:T(8,128)S(1)}, s32[94,64]{0,1:T(8,128)}, u32[]{:S(2)}) copy-start(s32[94,64]{0,1:T(8,128)} %iota_subtract_fusion) | copy-start | bytes 72196
  25.7 2.1 %copy-start.4 = (f32[31]{0:T(128)S(1)}, f32[31]{0:T(128)}, u32[]{:S(2)}) copy-start(f32[31]{0:T(128)} %get-tuple-element.60) | copy-start | bytes 376
  25.7 2.1 %copy-start.5 = (f32[31]{0:T(128)S(1)}, f32[31]{0:T(128)}, u32[]{:S(2)}) copy-start(f32[31]{0:T(128)} %get-tuple-element.61) | copy-start | bytes 376
  26.2 5.7 %collective-permute-start.4 = (bf16[2,15,16,128]{3,1,2,0:T(8,128)(2,1)S(1)}, bf16[2,15,16,128]{3,1,2,0:T(8,128)(2,1)S(1)}, u32[]{:S(2)}, u32[]{:S(2)}) collective-permute-start(bf16[2,15,16,128]{3,1,2,0:T(8,128)(2,1)S(1)} %slice_select_fusion.3), channel_id=1, source_target_pairs={{0,2},{2,0},{1,3},{3,1},{4,6},{6,4},{5,7},{7,5},{8,10},{10,8},{9,1... | collective-permute-start | bytes 368648 | tf_op jit(solution)/shard_map/ppermute | solution.py:119
  33.2 3.9 %collective-permute-start.5 = (bf16[2,64,15,128]{3,2,1,0:T(8,128)(2,1)S(1)}, bf16[2,64,15,128]{3,2,1,0:T(8,128)(2,1)S(1)}, u32[]{:S(2)}, u32[]{:S(2)}) collective-permute-start(bf16[2,64,15,128]{3,2,1,0:T(8,128)(2,1)S(1)} %get-tuple-element.41), channel_id=1, source_target_pairs={{1,4},{4,1},{3,6},{6,3},{5,8},{8,5},{7,10},{10,7},{9,12},{12,9},{1... | collective-permute-start | bytes 1474568 | tf_op jit(solution)/shard_map/ppermute | solution.py:140
  33.9 4.7 %collective-permute-start.6 = (bf16[2,64,15,128]{3,2,1,0:T(8,128)(2,1)S(1)}, bf16[2,64,15,128]{3,2,1,0:T(8,128)(2,1)S(1)}, u32[]{:S(2)}, u32[]{:S(2)}) collective-permute-start(bf16[2,64,15,128]{3,2,1,0:T(8,128)(2,1)S(1)} %get-tuple-element.42), channel_id=1, source_target_pairs={{0,1},{1,0},{2,3},{3,2},{4,5},{5,4},{6,7},{7,6},{8,9},{9,8},{10,11... | collective-permute-start | bytes 1474568 | tf_op jit(solution)/shard_map/ppermute | solution.py:23
  39.7 5.0 %collective-permute-start.7 = (bf16[2,15,16,128]{3,1,2,0:T(8,128)(2,1)S(1)}, bf16[2,15,16,128]{3,1,2,0:T(8,128)(2,1)S(1)}, u32[]{:S(2)}, u32[]{:S(2)}) collective-permute-start(bf16[2,15,16,128]{3,1,2,0:T(8,128)(2,1)S(1)} %slice_select_fusion.2), channel_id=1, source_target_pairs={{0,2},{2,0},{1,3},{3,1},{4,6},{6,4},{5,7},{7,5},{8,10},{10,8},{9,1... | collective-permute-start | bytes 368648 | tf_op jit(solution)/shard_map/ppermute | solution.py:119
  46.0 9.5 %collective-permute-start.8 = (bf16[64,15,128]{2,1,0:T(8,128)(2,1)S(1)}, bf16[64,15,128]{2,1,0:T(8,128)(2,1)S(1)}, u32[]{:S(2)}, u32[]{:S(2)}) collective-permute-start(bf16[64,15,128]{2,1,0:T(8,128)(2,1)S(1)} %get-tuple-element.47), channel_id=1, source_target_pairs={{1,4},{4,1},{3,6},{6,3},{5,8},{8,5},{7,10},{10,7},{9,12},{12,9},{1... | collective-permute-start | bytes 737288 | tf_op jit(solution)/shard_map/ppermute | solution.py:140
  46.7 10.0 %collective-permute-start.9 = (bf16[64,15,128]{2,1,0:T(8,128)(2,1)S(1)}, bf16[64,15,128]{2,1,0:T(8,128)(2,1)S(1)}, u32[]{:S(2)}, u32[]{:S(2)}) collective-permute-start(bf16[64,15,128]{2,1,0:T(8,128)(2,1)S(1)} %get-tuple-element.48), channel_id=1, source_target_pairs={{0,1},{1,0},{2,3},{3,2},{4,5},{5,4},{6,7},{7,6},{8,9},{9,8},{10,11... | collective-permute-start | bytes 737288 | tf_op jit(solution)/shard_map/ppermute | solution.py:23
  57.6 5.0 %collective-permute-start.10 = (bf16[2,15,16,128]{3,1,2,0:T(8,128)(2,1)S(1)}, bf16[2,15,16,128]{3,1,2,0:T(8,128)(2,1)S(1)}, u32[]{:S(2)}, u32[]{:S(2)}) collective-permute-start(bf16[2,15,16,128]{3,1,2,0:T(8,128)(2,1)S(1)} %slice_select_fusion.1), channel_id=1, source_target_pairs={{0,2},{2,0},{1,3},{3,1},{4,6},{6,4},{5,7},{7,5},{8,10},{10,8},{9,1... | collective-permute-start | bytes 368648 | tf_op jit(solution)/shard_map/ppermute | solution.py:119
  63.9 7.0 %collective-permute-start.11 = (bf16[2,64,15,128]{3,2,1,0:T(8,128)(2,1)S(1)}, bf16[2,64,15,128]{3,2,1,0:T(8,128)(2,1)S(1)}, u32[]{:S(2)}, u32[]{:S(2)}) collective-permute-start(bf16[2,64,15,128]{3,2,1,0:T(8,128)(2,1)S(1)} %get-tuple-element.37), channel_id=1, source_target_pairs={{1,4},{4,1},{3,6},{6,3},{5,8},{8,5},{7,10},{10,7},{9,12},{12,9},{1... | collective-permute-start | bytes 1474568 | tf_op jit(solution)/shard_map/ppermute | solution.py:140
  64.7 7.6 %collective-permute-start.12 = (bf16[2,64,15,128]{3,2,1,0:T(8,128)(2,1)S(1)}, bf16[2,64,15,128]{3,2,1,0:T(8,128)(2,1)S(1)}, u32[]{:S(2)}, u32[]{:S(2)}) collective-permute-start(bf16[2,64,15,128]{3,2,1,0:T(8,128)(2,1)S(1)} %get-tuple-element.38), channel_id=1, source_target_pairs={{0,1},{1,0},{2,3},{3,2},{4,5},{5,4},{6,7},{7,6},{8,9},{9,8},{10,11... | collective-permute-start | bytes 1474568 | tf_op jit(solution)/shard_map/ppermute | solution.py:23
  73.5 5.0 %collective-permute-start.13 = (bf16[2,15,16,128]{3,1,2,0:T(8,128)(2,1)S(1)}, bf16[2,15,16,128]{3,1,2,0:T(8,128)(2,1)S(1)}, u32[]{:S(2)}, u32[]{:S(2)}) collective-permute-start(bf16[2,15,16,128]{3,1,2,0:T(8,128)(2,1)S(1)} %slice_select_fusion), channel_id=1, source_target_pairs={{0,2},{2,0},{1,3},{3,1},{4,6},{6,4},{5,7},{7,5},{8,10},{10,8},{9,1... | collective-permute-start | bytes 368648 | tf_op jit(solution)/shard_map/ppermute | solution.py:119
  79.7 5.4 %collective-permute-start.14 = (f32[32,16,128]{2,1,0:T(8,128)S(1)}, f32[32,16,128]{2,1,0:T(8,128)S(1)}, u32[]{:S(2)}, u32[]{:S(2)}) collective-permute-start(f32[32,16,128]{2,1,0:T(8,128)S(1)} %get-tuple-element.35), channel_id=1, source_target_pairs={{0,1},{1,0},{2,3},{3,2},{4,5},{5,4},{6,7},{7,6},{8,9},{9,8},{10,11... | collective-permute-start | bytes 786440 | tf_op jit(solution)/shard_map/ppermute | solution.py:23

commit v31 on v27

--- a/solution.py
+++ b/solution.py
@@ -135,12 +135,11 @@
     width = block.shape[axis]
     front = lax.slice_in_dim(block, 0, reach, axis=axis)
     back = lax.slice_in_dim(block, width - reach, width, axis=axis)
-    outward = jnp.where(first, front, back)
     inward = jnp.where(first, back, front)
-    across = lax.ppermute(outward, ("tile", "view"), route)
+    whole = lax.ppermute(block, ("tile", "view"), route)
     beside = from_partner(inward, "view", 0)
-    low = jnp.where(first, across, beside)
-    high = jnp.where(first, beside, across)
+    low = jnp.where(first, lax.slice_in_dim(whole, width - reach, width, axis=axis), beside)
+    high = jnp.where(first, beside, lax.slice_in_dim(whole, 0, reach, axis=axis))
     return low, high
 
 

time: 85.6 us -> 85.4 us (level)
  transfers between devices with their start and end apart: 15 -> 15, of which waited for: 10 -> 10; matrix products, arithmetic and copies ran while one was open for 3% -> 4% of each run, Pallas kernels for 0% -> 0%
where the time goes in v31:
time: 85.4 us; the launch traced here: 85.1 us
  starting transfers between devices  47.2 us (55%)
  waiting for transfers between devices  21.8 us (26%)
  other arithmetic  7.22 us (8%)
  matrix products  5.09 us (6%)
  local copies, waits for them, and re-layouts  3.27 us (4%)
    ppermute x6, starting transfers between devices, from_partner(): return lax.ppermute(block, axis, route)  37.4 us
    ppermute x4, waiting for transfers between devices, z_rims(): got = lax.ppermute(payload, 'view', route)  13.9 us
    ppermute x6, waiting for transfers between devices, from_partner(): return lax.ppermute(block, axis, route)  7.83 us
    ppermute x4, starting transfers between devices, z_rims(): got = lax.ppermute(payload, 'view', route)  6.21 us
    ppermute x4, starting transfers between devices, x_rims(): whole = lax.ppermute(block, ('tile', 'view'), route)  2.92 us
  transfers between devices with their start and end apart: 15, of which 10 were waited for; matrix products, arithmetic and copies ran while one was open for 4% of the time, Pallas kernels for 0%

profile of v31, /device:TPU:0, one launch (start us, length us, event | category | flops | bytes accessed | tf_op | source)
XLA Modules:
  0.0 85.1 jit_solution(11447409789870179303)
XLA Ops:
  0.0 0.9 %fusion.72 = (s32[4]{0:T(128)S(1)}, s32[4]{0:T(128)S(1)}, s32[4]{0:T(128)S(1)}, s32[4]{0:T(128)S(1)}) fusion(s32[1,32]{1,0:T(1,128)} %param.5, s32[]{:T(128)S(6)} %select_n.318, s32[]{:T(128)S(6)} %select_n.319, s32[]{:T(128)S(6)} %select_n.321, s32[]{:T(128)S(6)} %select_n.320), kind=kLoop, calls=%fused_computation.180 | loop fusion | bytes 144 | tf_op jit(solution)/shard_map/dynamic_slice | solution.py:164
  1.0 0.8 gather_fusion
  3.0 1.5 %collective-permute-done = bf16[2,64,16,128]{3,2,1,0:T(8,128)(2,1)S(1)} collective-permute-done((bf16[2,64,16,128]{3,2,1,0:T(8,128)(2,1)S(1)}, bf16[2,64,16,128]{3,2,1,0:T(8,128)(2,1)S(1)}, u32[]{:S(2)}, u32[]{:S(2)}) %collective-permute-start) | collective-permute-done | bytes 524320 | tf_op jit(solution)/shard_map/ppermute | solution.py:23
  6.8 1.0 %select_reduce_fusion.1 = (bf16[128,128]{1,0:T(8,128)(2,1)S(1)}, bf16[128,128]{1,0:T(8,128)(2,1)S(1)}, bf16[128,128]{1,0:T(8,128)(2,1)S(1)}, bf16[128,128]{1,0:T(8,128)(2,1)S(1)}) fusion(f32[31]{0:T(128)S(1)} %get-tuple-element.66, s32[128,128]{1,0:T(8,128)S(1)} %subtract_add_fusion, f32[31]{0:T(128)S(1)} %get-tuple-element.67, f32[31]{0:T(128)S(1)} %get-tuple-element.81, ...), kind=kLoop, calls=%fused_computation.2 | loop fusion | flops 4505600 | bytes 197104 | tf_op jit(solution)/shard_map/reduce_sum | solution.py:45
  8.9 11.7 %collective-permute-start.3 = (bf16[64,15,128]{2,1,0:T(8,128)(2,1)S(1)}, bf16[64,15,128]{2,1,0:T(8,128)(2,1)S(1)}, u32[]{:S(2)}, u32[]{:S(2)}) collective-permute-start(bf16[64,15,128]{2,1,0:T(8,128)(2,1)S(1)} %slice_select_fusion.10), channel_id=1, source_target_pairs={{0,1},{1,0},{2,3},{3,2},{4,5},{5,4},{6,7},{7,6},{8,9},{9,8},{10,11... | collective-permute-start | bytes 737288 | tf_op jit(solution)/shard_map/ppermute | solution.py:23
  20.7 1.0 %collective-permute-done.3 = bf16[64,15,128]{2,1,0:T(8,128)(2,1)S(1)} collective-permute-done((bf16[64,15,128]{2,1,0:T(8,128)(2,1)S(1)}, bf16[64,15,128]{2,1,0:T(8,128)(2,1)S(1)}, u32[]{:S(2)}, u32[]{:S(2)}) %collective-permute-start.3) | collective-permute-done | bytes 245792 | tf_op jit(solution)/shard_map/ppermute | solution.py:23
  22.7 1.6 %collective-permute-start.4 = (bf16[2,15,16,128]{3,1,2,0:T(8,128)(2,1)S(1)}, bf16[2,15,16,128]{3,1,2,0:T(8,128)(2,1)S(1)}, u32[]{:S(2)}, u32[]{:S(2)}) collective-permute-start(bf16[2,15,16,128]{3,1,2,0:T(8,128)(2,1)S(1)} %slice_select_fusion.15), channel_id=1, source_target_pairs={{0,2},{2,0},{1,3},{3,1},{4,6},{6,4},{5,7},{7,5},{8,10},{10,8},{9,1... | collective-permute-start | bytes 368648 | tf_op jit(solution)/shard_map/ppermute | solution.py:119
  24.3 3.5 %collective-permute-done.4 = bf16[2,15,16,128]{3,1,2,0:T(8,128)(2,1)S(1)} collective-permute-done((bf16[2,15,16,128]{3,1,2,0:T(8,128)(2,1)S(1)}, bf16[2,15,16,128]{3,1,2,0:T(8,128)(2,1)S(1)}, u32[]{:S(2)}, u32[]{:S(2)}) %collective-permute-start.4) | collective-permute-done | bytes 122912 | tf_op jit(solution)/shard_map/ppermute | solution.py:119
  29.7 6.4 %collective-permute-start.6 = (bf16[2,64,15,128]{3,2,1,0:T(8,128)(2,1)S(1)}, bf16[2,64,15,128]{3,2,1,0:T(8,128)(2,1)S(1)}, u32[]{:S(2)}, u32[]{:S(2)}) collective-permute-start(bf16[2,64,15,128]{3,2,1,0:T(8,128)(2,1)S(1)} %slice_select_fusion.4), channel_id=1, source_target_pairs={{0,1},{1,0},{2,3},{3,2},{4,5},{5,4},{6,7},{7,6},{8,9},{9,8},{10,11... | collective-permute-start | bytes 1474568 | tf_op jit(solution)/shard_map/ppermute | solution.py:23
  36.2 1.4 %collective-permute-done.6 = bf16[2,64,15,128]{3,2,1,0:T(8,128)(2,1)S(1)} collective-permute-done((bf16[2,64,15,128]{3,2,1,0:T(8,128)(2,1)S(1)}, bf16[2,64,15,128]{3,2,1,0:T(8,128)(2,1)S(1)}, u32[]{:S(2)}, u32[]{:S(2)}) %collective-permute-start.6) | collective-permute-done | bytes 491552 | tf_op jit(solution)/shard_map/ppermute | solution.py:23
  38.8 1.5 %collective-permute-start.7 = (bf16[2,15,16,128]{3,1,2,0:T(8,128)(2,1)S(1)}, bf16[2,15,16,128]{3,1,2,0:T(8,128)(2,1)S(1)}, u32[]{:S(2)}, u32[]{:S(2)}) collective-permute-start(bf16[2,15,16,128]{3,1,2,0:T(8,128)(2,1)S(1)} %slice_select_fusion.14), channel_id=1, source_target_pairs={{0,2},{2,0},{1,3},{3,1},{4,6},{6,4},{5,7},{7,5},{8,10},{10,8},{9,1... | collective-permute-start | bytes 368648 | tf_op jit(solution)/shard_map/ppermute | solution.py:119
  40.4 3.5 %collective-permute-done.7 = bf16[2,15,16,128]{3,1,2,0:T(8,128)(2,1)S(1)} collective-permute-done((bf16[2,15,16,128]{3,1,2,0:T(8,128)(2,1)S(1)}, bf16[2,15,16,128]{3,1,2,0:T(8,128)(2,1)S(1)}, u32[]{:S(2)}, u32[]{:S(2)}) %collective-permute-start.7) | collective-permute-done | bytes 122912 | tf_op jit(solution)/shard_map/ppermute | solution.py:119
  45.9 8.7 %collective-permute-start.9 = (bf16[64,15,128]{2,1,0:T(8,128)(2,1)S(1)}, bf16[64,15,128]{2,1,0:T(8,128)(2,1)S(1)}, u32[]{:S(2)}, u32[]{:S(2)}) collective-permute-start(bf16[64,15,128]{2,1,0:T(8,128)(2,1)S(1)} %slice_select_fusion.7), channel_id=1, source_target_pairs={{0,1},{1,0},{2,3},{3,2},{4,5},{5,4},{6,7},{7,6},{8,9},{9,8},{10,11... | collective-permute-start | bytes 737288 | tf_op jit(solution)/shard_map/ppermute | solution.py:23
  54.5 1.2 %collective-permute-done.9 = bf16[64,15,128]{2,1,0:T(8,128)(2,1)S(1)} collective-permute-done((bf16[64,15,128]{2,1,0:T(8,128)(2,1)S(1)}, bf16[64,15,128]{2,1,0:T(8,128)(2,1)S(1)}, u32[]{:S(2)}, u32[]{:S(2)}) %collective-permute-start.9) | collective-permute-done | bytes 245792 | tf_op jit(solution)/shard_map/ppermute | solution.py:23
  56.7 1.6 %collective-permute-start.10 = (bf16[2,15,16,128]{3,1,2,0:T(8,128)(2,1)S(1)}, bf16[2,15,16,128]{3,1,2,0:T(8,128)(2,1)S(1)}, u32[]{:S(2)}, u32[]{:S(2)}) collective-permute-start(bf16[2,15,16,128]{3,1,2,0:T(8,128)(2,1)S(1)} %slice_select_fusion.13), channel_id=1, source_target_pairs={{0,2},{2,0},{1,3},{3,1},{4,6},{6,4},{5,7},{7,5},{8,10},{10,8},{9,1... | collective-permute-start | bytes 368648 | tf_op jit(solution)/shard_map/ppermute | solution.py:119
  58.3 3.5 %collective-permute-done.10 = bf16[2,15,16,128]{3,1,2,0:T(8,128)(2,1)S(1)} collective-permute-done((bf16[2,15,16,128]{3,1,2,0:T(8,128)(2,1)S(1)}, bf16[2,15,16,128]{3,1,2,0:T(8,128)(2,1)S(1)}, u32[]{:S(2)}, u32[]{:S(2)}) %collective-permute-start.10) | collective-permute-done | bytes 122912 | tf_op jit(solution)/shard_map/ppermute | solution.py:119
  62.8 0.9 %collective-permute-start.11 = (bf16[2,64,16,128]{3,2,1,0:T(8,128)(2,1)S(1)}, bf16[2,64,16,128]{3,2,1,0:T(8,128)(2,1)S(1)}, u32[]{:S(2)}, u32[]{:S(2)}) collective-permute-start(bf16[2,64,16,128]{3,2,1,0:T(8,128)(2,1)S(1)} %fusion.20), channel_id=1, source_target_pairs={{1,4},{4,1},{3,6},{6,3},{5,8},{8,5},{7,10},{10,7},{9,12},{12,9},{1... | collective-permute-start | bytes 1572872 | tf_op jit(solution)/shard_map/ppermute | solution.py:139
  63.9 6.0 %collective-permute-start.12 = (bf16[2,64,15,128]{3,2,1,0:T(8,128)(2,1)S(1)}, bf16[2,64,15,128]{3,2,1,0:T(8,128)(2,1)S(1)}, u32[]{:S(2)}, u32[]{:S(2)}) collective-permute-start(bf16[2,64,15,128]{3,2,1,0:T(8,128)(2,1)S(1)} %slice_select_fusion.1), channel_id=1, source_target_pairs={{0,1},{1,0},{2,3},{3,2},{4,5},{5,4},{6,7},{7,6},{8,9},{9,8},{10,11... | collective-permute-start | bytes 1474568 | tf_op jit(solution)/shard_map/ppermute | solution.py:23
  69.9 1.5 %collective-permute-done.12 = bf16[2,64,15,128]{3,2,1,0:T(8,128)(2,1)S(1)} collective-permute-done((bf16[2,64,15,128]{3,2,1,0:T(8,128)(2,1)S(1)}, bf16[2,64,15,128]{3,2,1,0:T(8,128)(2,1)S(1)}, u32[]{:S(2)}, u32[]{:S(2)}) %collective-permute-start.12) | collective-permute-done | bytes 491552 | tf_op jit(solution)/shard_map/ppermute | solution.py:23
  72.6 1.6 %collective-permute-start.13 = (bf16[2,15,16,128]{3,1,2,0:T(8,128)(2,1)S(1)}, bf16[2,15,16,128]{3,1,2,0:T(8,128)(2,1)S(1)}, u32[]{:S(2)}, u32[]{:S(2)}) collective-permute-start(bf16[2,15,16,128]{3,1,2,0:T(8,128)(2,1)S(1)} %slice_select_fusion.12), channel_id=1, source_target_pairs={{0,2},{2,0},{1,3},{3,1},{4,6},{6,4},{5,7},{7,5},{8,10},{10,8},{9,1... | collective-permute-start | bytes 368648 | tf_op jit(solution)/shard_map/ppermute | solution.py:119
  74.2 3.5 %collective-permute-done.13 = bf16[2,15,16,128]{3,1,2,0:T(8,128)(2,1)S(1)} collective-permute-done((bf16[2,15,16,128]{3,1,2,0:T(8,128)(2,1)S(1)}, bf16[2,15,16,128]{3,1,2,0:T(8,128)(2,1)S(1)}, u32[]{:S(2)}, u32[]{:S(2)}) %collective-permute-start.13) | collective-permute-done | bytes 122912 | tf_op jit(solution)/shard_map/ppermute | solution.py:119
  78.9 4.1 %collective-permute-start.14 = (f32[32,16,128]{2,1,0:T(8,128)S(1)}, f32[32,16,128]{2,1,0:T(8,128)S(1)}, u32[]{:S(2)}, u32[]{:S(2)}) collective-permute-start(f32[32,16,128]{2,1,0:T(8,128)S(1)} %get-tuple-element.47), channel_id=1, source_target_pairs={{0,1},{1,0},{2,3},{3,2},{4,5},{5,4},{6,7},{7,6},{8,9},{9,8},{10,11... | collective-permute-start | bytes 786440 | tf_op jit(solution)/shard_map/ppermute | solution.py:23
  83.0 1.2 %collective-permute-done.14 = f32[32,16,128]{2,1,0:T(8,128)S(1)} collective-permute-done((f32[32,16,128]{2,1,0:T(8,128)S(1)}, f32[32,16,128]{2,1,0:T(8,128)S(1)}, u32[]{:S(2)}, u32[]{:S(2)}) %collective-permute-start.14) | collective-permute-done | bytes 262176 | tf_op jit(solution)/shard_map/ppermute | solution.py:23
  84.2 0.9 %fusion.56 = f32[32,32,128]{2,1,0:T(8,128)} fusion(s32[]{:T(128)S(6)} %select_n.379, f32[32,16,128]{2,1,0:T(8,128)S(1)} %get-tuple-element.48, f32[32,16,128]{2,1,0:T(8,128)S(1)} %collective-permute-done.14), kind=kLoop, calls=%fused_computation.78 | loop fusion | flops 262144 | bytes 1048580 | tf_op jit(solution)/shard_map/concatenate | solution.py:219
  (94 shorter events, 15.3 us)
Async XLA Ops:
  0.0 1.8 %copy-start = (bf16[64,32,128]{2,1,0:T(8,128)(2,1)S(1)}, bf16[64,32,128]{2,1,0:T(8,128)(2,1)}, u32[]{:S(2)}) copy-start(bf16[64,32,128]{2,1,0:T(8,128)(2,1)} %param.3) | copy-start | bytes 1572868
  2.5 2.1 %collective-permute-start = (bf16[2,64,16,128]{3,2,1,0:T(8,128)(2,1)S(1)}, bf16[2,64,16,128]{3,2,1,0:T(8,128)(2,1)S(1)}, u32[]{:S(2)}, u32[]{:S(2)}) collective-permute-start(bf16[2,64,16,128]{3,2,1,0:T(8,128)(2,1)S(1)} %pad_maximum_fusion), channel_id=1, source_target_pairs={{0,1},{1,0},{2,3},{3,2},{4,5},{5,4},{6,7},{7,6},{8,9},{9,8},{10,11... | collective-permute-start | bytes 1572872 | tf_op jit(solution)/shard_map/ppermute | solution.py:23
  3.0 2.3 %copy-start.1 = (f32[2,3,31]{2,0,1:T(2,128)S(1)}, f32[2,3,31]{2,0,1:T(2,128)}, u32[]{:S(2)}) copy-start(f32[2,3,31]{2,0,1:T(2,128)} %param.4) | copy-start | bytes 2236
  4.6 3.2 %collective-permute-start.1 = (bf16[2,64,16,128]{3,2,1,0:T(8,128)(2,1)S(1)}, bf16[2,64,16,128]{3,2,1,0:T(8,128)(2,1)S(1)}, u32[]{:S(2)}, u32[]{:S(2)}) collective-permute-start(bf16[2,64,16,128]{3,2,1,0:T(8,128)(2,1)S(1)} %pad_maximum_fusion.1), channel_id=1, source_target_pairs={{1,4},{4,1},{3,6},{6,3},{5,8},{8,5},{7,10},{10,7},{9,12},{12,9},{1... | collective-permute-start | bytes 1572872 | tf_op jit(solution)/shard_map/ppermute | solution.py:191
  8.2 13.5 %collective-permute-start.2 = (bf16[64,16,128]{2,1,0:T(8,128)(2,1)S(1)}, bf16[64,16,128]{2,1,0:T(8,128)(2,1)S(1)}, u32[]{:S(2)}, u32[]{:S(2)}) collective-permute-start(bf16[64,16,128]{2,1,0:T(8,128)(2,1)S(1)} %convert_bitcast_fusion.1), channel_id=1, source_target_pairs={{1,4},{4,1},{3,6},{6,3},{5,8},{8,5},{7,10},{10,7},{9,12},{12,9},{1... | collective-permute-start | bytes 786440 | tf_op jit(solution)/shard_map/ppermute | solution.py:139
  8.9 12.8 %collective-permute-start.3 = (bf16[64,15,128]{2,1,0:T(8,128)(2,1)S(1)}, bf16[64,15,128]{2,1,0:T(8,128)(2,1)S(1)}, u32[]{:S(2)}, u32[]{:S(2)}) collective-permute-start(bf16[64,15,128]{2,1,0:T(8,128)(2,1)S(1)} %slice_select_fusion.10), channel_id=1, source_target_pairs={{0,1},{1,0},{2,3},{3,2},{4,5},{5,4},{6,7},{7,6},{8,9},{9,8},{10,11... | collective-permute-start | bytes 737288 | tf_op jit(solution)/shard_map/ppermute | solution.py:23
  22.7 5.0 %collective-permute-start.4 = (bf16[2,15,16,128]{3,1,2,0:T(8,128)(2,1)S(1)}, bf16[2,15,16,128]{3,1,2,0:T(8,128)(2,1)S(1)}, u32[]{:S(2)}, u32[]{:S(2)}) collective-permute-start(bf16[2,15,16,128]{3,1,2,0:T(8,128)(2,1)S(1)} %slice_select_fusion.15), channel_id=1, source_target_pairs={{0,2},{2,0},{1,3},{3,1},{4,6},{6,4},{5,7},{7,5},{8,10},{10,8},{9,1... | collective-permute-start | bytes 368648 | tf_op jit(solution)/shard_map/ppermute | solution.py:119
  28.8 8.8 %collective-permute-start.5 = (bf16[2,64,16,128]{3,2,1,0:T(8,128)(2,1)S(1)}, bf16[2,64,16,128]{3,2,1,0:T(8,128)(2,1)S(1)}, u32[]{:S(2)}, u32[]{:S(2)}) collective-permute-start(bf16[2,64,16,128]{3,2,1,0:T(8,128)(2,1)S(1)} %fusion.21), channel_id=1, source_target_pairs={{1,4},{4,1},{3,6},{6,3},{5,8},{8,5},{7,10},{10,7},{9,12},{12,9},{1... | collective-permute-start | bytes 1572872 | tf_op jit(solution)/shard_map/ppermute | solution.py:139
  29.7 7.9 %collective-permute-start.6 = (bf16[2,64,15,128]{3,2,1,0:T(8,128)(2,1)S(1)}, bf16[2,64,15,128]{3,2,1,0:T(8,128)(2,1)S(1)}, u32[]{:S(2)}, u32[]{:S(2)}) collective-permute-start(bf16[2,64,15,128]{3,2,1,0:T(8,128)(2,1)S(1)} %slice_select_fusion.4), channel_id=1, source_target_pairs={{0,1},{1,0},{2,3},{3,2},{4,5},{5,4},{6,7},{7,6},{8,9},{9,8},{10,11... | collective-permute-start | bytes 1474568 | tf_op jit(solution)/shard_map/ppermute | solution.py:23
  38.8 5.0 %collective-permute-start.7 = (bf16[2,15,16,128]{3,1,2,0:T(8,128)(2,1)S(1)}, bf16[2,15,16,128]{3,1,2,0:T(8,128)(2,1)S(1)}, u32[]{:S(2)}, u32[]{:S(2)}) collective-permute-start(bf16[2,15,16,128]{3,1,2,0:T(8,128)(2,1)S(1)} %slice_select_fusion.14), channel_id=1, source_target_pairs={{0,2},{2,0},{1,3},{3,1},{4,6},{6,4},{5,7},{7,5},{8,10},{10,8},{9,1... | collective-permute-start | bytes 368648 | tf_op jit(solution)/shard_map/ppermute | solution.py:119
  45.1 10.6 %collective-permute-start.8 = (bf16[64,16,128]{2,1,0:T(8,128)(2,1)S(1)}, bf16[64,16,128]{2,1,0:T(8,128)(2,1)S(1)}, u32[]{:S(2)}, u32[]{:S(2)}) collective-permute-start(bf16[64,16,128]{2,1,0:T(8,128)(2,1)S(1)} %get-tuple-element.33), channel_id=1, source_target_pairs={{1,4},{4,1},{3,6},{6,3},{5,8},{8,5},{7,10},{10,7},{9,12},{12,9},{1... | collective-permute-start | bytes 786440 | tf_op jit(solution)/shard_map/ppermute | solution.py:139
  45.9 9.8 %collective-permute-start.9 = (bf16[64,15,128]{2,1,0:T(8,128)(2,1)S(1)}, bf16[64,15,128]{2,1,0:T(8,128)(2,1)S(1)}, u32[]{:S(2)}, u32[]{:S(2)}) collective-permute-start(bf16[64,15,128]{2,1,0:T(8,128)(2,1)S(1)} %slice_select_fusion.7), channel_id=1, source_target_pairs={{0,1},{1,0},{2,3},{3,2},{4,5},{5,4},{6,7},{7,6},{8,9},{9,8},{10,11... | collective-permute-start | bytes 737288 | tf_op jit(solution)/shard_map/ppermute | solution.py:23
  56.7 5.0 %collective-permute-start.10 = (bf16[2,15,16,128]{3,1,2,0:T(8,128)(2,1)S(1)}, bf16[2,15,16,128]{3,1,2,0:T(8,128)(2,1)S(1)}, u32[]{:S(2)}, u32[]{:S(2)}) collective-permute-start(bf16[2,15,16,128]{3,1,2,0:T(8,128)(2,1)S(1)} %slice_select_fusion.13), channel_id=1, source_target_pairs={{0,2},{2,0},{1,3},{3,1},{4,6},{6,4},{5,7},{7,5},{8,10},{10,8},{9,1... | collective-permute-start | bytes 368648 | tf_op jit(solution)/shard_map/ppermute | solution.py:119
  62.8 8.6 %collective-permute-start.11 = (bf16[2,64,16,128]{3,2,1,0:T(8,128)(2,1)S(1)}, bf16[2,64,16,128]{3,2,1,0:T(8,128)(2,1)S(1)}, u32[]{:S(2)}, u32[]{:S(2)}) collective-permute-start(bf16[2,64,16,128]{3,2,1,0:T(8,128)(2,1)S(1)} %fusion.20), channel_id=1, source_target_pairs={{1,4},{4,1},{3,6},{6,3},{5,8},{8,5},{7,10},{10,7},{9,12},{12,9},{1... | collective-permute-start | bytes 1572872 | tf_op jit(solution)/shard_map/ppermute | solution.py:139
  63.9 7.5 %collective-permute-start.12 = (bf16[2,64,15,128]{3,2,1,0:T(8,128)(2,1)S(1)}, bf16[2,64,15,128]{3,2,1,0:T(8,128)(2,1)S(1)}, u32[]{:S(2)}, u32[]{:S(2)}) collective-permute-start(bf16[2,64,15,128]{3,2,1,0:T(8,128)(2,1)S(1)} %slice_select_fusion.1), channel_id=1, source_target_pairs={{0,1},{1,0},{2,3},{3,2},{4,5},{5,4},{6,7},{7,6},{8,9},{9,8},{10,11... | collective-permute-start | bytes 1474568 | tf_op jit(solution)/shard_map/ppermute | solution.py:23
  72.6 5.0 %collective-permute-start.13 = (bf16[2,15,16,128]{3,1,2,0:T(8,128)(2,1)S(1)}, bf16[2,15,16,128]{3,1,2,0:T(8,128)(2,1)S(1)}, u32[]{:S(2)}, u32[]{:S(2)}) collective-permute-start(bf16[2,15,16,128]{3,1,2,0:T(8,128)(2,1)S(1)} %slice_select_fusion.12), channel_id=1, source_target_pairs={{0,2},{2,0},{1,3},{3,1},{4,6},{6,4},{5,7},{7,5},{8,10},{10,8},{9,1... | collective-permute-start | bytes 368648 | tf_op jit(solution)/shard_map/ppermute | solution.py:119
  78.9 5.3 %collective-permute-start.14 = (f32[32,16,128]{2,1,0:T(8,128)S(1)}, f32[32,16,128]{2,1,0:T(8,128)S(1)}, u32[]{:S(2)}, u32[]{:S(2)}) collective-permute-start(f32[32,16,128]{2,1,0:T(8,128)S(1)} %get-tuple-element.47), channel_id=1, source_target_pairs={{0,1},{1,0},{2,3},{3,2},{4,5},{5,4},{6,7},{7,6},{8,9},{9,8},{10,11... | collective-permute-start | bytes 786440 | tf_op jit(solution)/shard_map/ppermute | solution.py:23
